TPU v7x, 32 devices: a whole 2x2x4 slice. The times are simulated.
32 devices in a mesh: src: 8 (over z, y), vox: 4 (over x, core).
Axes of the slice: x: 2, y: 2, z: 4, core: 2. Of those that a mesh axis runs over, the one named last changes fastest.
Arguments:
- forward_voxel_field: bfloat16 [4096, 4096], P('src', 'vox'), may hold values from -0.09375 to 0.09375
- adjoint_voxel_field: bfloat16 [4096, 4096], P('src', 'vox'), may hold values from -6 to 6
- voxel_input_vector: float32 [4096], P('vox'), may hold values from -6 to 6
- measurement_weight: float32 [4096, 4096], P('src', 'vox'), may hold values from 0.00390625 to 0.0390625
Outputs:
- hess_vector: float32 [4096], P('vox')
All inputs are finite; a program needn't handle non-finite values.
Results may differ from a plain program's by a relative error of at most 0.00056.
Values may be sent and summed in bfloat16 or wider, within the bound.
No kernel may reach another device: no remote copies, remote signals or barrier semaphores. Data moves between devices by JAX's collectives and lax.ppermute only.
A program may use at most 64 MiB of HBM per device.

v0:
```python
import jax
import jax.numpy as jnp
from jax import lax
from jax.sharding import PartitionSpec as P


def per_device(forward_voxel_field, adjoint_voxel_field, voxel_input_vector, measurement_weight):
    scaled = (forward_voxel_field.astype(jnp.float32) * voxel_input_vector[None, :]).astype(
        jnp.bfloat16
    )
    adjoint_all = lax.all_gather(adjoint_voxel_field, "src", axis=0, tiled=True)
    predicted_part = lax.dot_general(
        scaled, adjoint_all, (((1,), (1,)), ((), ())), preferred_element_type=jnp.float32
    )
    pred_share = lax.psum_scatter(predicted_part, "vox", scatter_dimension=1, tiled=True)
    weighted_share = (measurement_weight * pred_share).astype(jnp.bfloat16)
    weighted_signal = lax.all_gather(weighted_share, "vox", axis=1, tiled=True)
    back = jnp.dot(weighted_signal, adjoint_all, preferred_element_type=jnp.float32)
    local_sum = jnp.sum(forward_voxel_field.astype(jnp.float32) * back, axis=0)
    return lax.psum(local_sum, "src")


def solution(mesh):
    placed = (P("src", "vox"), P("src", "vox"), P("vox"), P("src", "vox"))
    return jax.shard_map(
        per_device, mesh=mesh, in_specs=placed, out_specs=P("vox"), check_vma=False
    )
```

profile of v0, /device:TPU:0, one launch (start us, length us, event | category | flops | bytes accessed | tf_op | source)
XLA Modules:
  0.0 294.0 jit_solution(4092530594951713219)
XLA Ops:
  6.5 0.0 all-gather.3.cloned.1.call-start
  6.5 0.7 all-gather.3.cloned.1.call-update
  7.3 0.0 reduce-scatter.2.cloned.1.call-start
  7.3 129.8 %all-gather.3.cloned.1.call-done = bf16[4096,1024]{1,0:T(8,128)(2,1)} async-done(((bf16[512,1024]{1,0:T(8,128)(2,1)}), bf16[4096,1024]{1,0:T(8,128)(2,1)}) %all-gather.3.cloned.1.call-update) | async-done | bytes 8388624 | tf_op jit(solution)/shard_map/all_gather | solution.py:11
  137.2 11.5 %fusion.2 = f32[512,4096]{1,0:T(8,128)} fusion(bf16[4096,1024]{1,0:T(8,128)(2,1)} %all-gather.3.cloned.1.call-done, bf16[512,1024]{1,0:T(8,128)(2,1)} %param.4, f32[1024]{0:T(1024)} %param.6), kind=kOutput, calls=%fused_computation.5 | convolution fusion | flops 4296540160 | bytes 17829888 | tf_op jit(solution)/shard_map/dot_general | solution.py:12
  148.7 0.0 copy-start
  148.7 0.0 reduce-scatter.2.cloned.1.call-update
  148.7 0.0 copy-start.1
  148.7 0.0 all-gather.5.cloned.1.call-start
  148.7 70.0 %reduce-scatter.2.cloned.1.call-done = f32[512,1024]{1,0:T(8,128)} async-done(((f32[512,4096]{1,0:T(8,128)}), f32[512,1024]{1,0:T(8,128)}) %reduce-scatter.2.cloned.1.call-update) | async-done | bytes 2097168 | tf_op jit(solution)/shard_map/reduce_scatter | solution.py:15
  218.7 0.0 copy-done
  218.7 2.9 multiply_convert_fusion
  221.7 0.0 all-gather.5.cloned.1.call-update
  221.7 34.6 %all-gather.5.cloned.1.call-done = bf16[512,4096]{1,0:T(8,128)(2,1)} async-done(((bf16[512,1024]{1,0:T(8,128)(2,1)}), bf16[512,4096]{1,0:T(8,128)(2,1)}) %all-gather.5.cloned.1.call-update) | async-done | bytes 4194320 | tf_op jit(solution)/shard_map/all_gather | solution.py:17
  256.3 0.0 copy-done.1
  256.3 9.2 %fusion.1 = f32[1024]{0:T(1024)S(1)} fusion(bf16[512,1024]{1,0:T(8,128)(2,1)S(1)} %copy-done.1, bf16[512,4096]{1,0:T(8,128)(2,1)} %all-gather.5.cloned.1.call-done, bf16[4096,1024]{1,0:T(8,128)(2,1)} %all-gather.3.cloned.1.call-done), kind=kOutput, calls=%fused_computation.3 | convolution fusion | flops 4296539136 | bytes 13635584 | tf_op jit(solution)/shard_map/dot_general | solution.py:18
  265.5 22.0 %psum.7 = f32[1024]{0:T(1024)} all-reduce(f32[1024]{0:T(1024)S(1)} %fusion.1), channel_id=1, replica_groups=mesh['src'=8,'vox'=4] {'src'}, use_global_device_ids=true, to_apply=%region_2.0 | all-reduce | flops 1024 | bytes 8192 | tf_op jit(solution)/shard_map/psum | solution.py:20
Async XLA Ops:
  6.5 130.6 %all-gather.3.cloned.1.call-start = ((), (), s32[]{:S(2)}) async-start(), calls=%async_computation.1 | async-start | bytes 9437184 | tf_op jit(solution)/shard_map/all_gather | solution.py:11
  7.3 211.5 %reduce-scatter.2.cloned.1.call-start = ((), (), s32[]{:S(2)}) async-start(), calls=%async_computation.2 | async-start | bytes 10485760 | tf_op jit(solution)/shard_map/reduce_scatter | solution.py:15
  148.7 70.1 %copy-start = (f32[512,1024]{1,0:T(8,128)S(1)}, f32[512,1024]{1,0:T(8,128)}, u32[]{:S(2)}) copy-start(f32[512,1024]{1,0:T(8,128)} %param.7) | copy-start | bytes 6291460
  148.7 107.7 %copy-start.1 = (bf16[512,1024]{1,0:T(8,128)(2,1)S(1)}, bf16[512,1024]{1,0:T(8,128)(2,1)}, u32[]{:S(2)}) copy-start(bf16[512,1024]{1,0:T(8,128)(2,1)} %param.4) | copy-start | bytes 3145732
  148.7 107.6 %all-gather.5.cloned.1.call-start = ((), (), s32[]{:S(2)}) async-start(), calls=%async_computation.3 | async-start | bytes 5242880 | tf_op jit(solution)/shard_map/all_gather | solution.py:17
Sparse Core Ops, SparseCore 0:
  9.5 127.6 all-gather.2
  148.8 69.8 reduce-scatter.1
  221.8 34.4 all-gather.4
where the time goes:
time: 294 us
  waiting for transfers between devices  235 us (80%)
  blocking collectives  22 us (7%)
  matrix products  20.7 us (7%)
  between operations  13.1 us (4%)
    all_gather x1, waiting for transfers between devices, per_device(): adjoint_all = lax.all_gather(adjoint_voxel_field, 'src', axis=0, tiled=True)  130 us
    reduce_scatter x1, waiting for transfers between devices, per_device(): lax.psum_scatter(predicted_part, 'vox', scatter_dimension=1, tiled=True)  70 us
    all_gather x1, waiting for transfers between devices, per_device(): weighted_signal = lax.all_gather(weighted_share, 'vox', axis=1, tiled=True)  34.6 us
    psum x1, blocking collectives, per_device(): return lax.psum(local_sum, 'src')  22 us
    dot_general x1, matrix products, per_device(): lax.dot_general(scaled, adjoint_all, (((1,), (1,)), ((), ())), preferred_...  11.5 us
    dot_general x1, matrix products, per_device(): jnp.dot(weighted_signal, adjoint_all, preferred_element_type=jnp.float32)  9.15 us
  transfers between devices with their start and end apart: 3, of which 3 were waited for; matrix products, arithmetic and copies ran while one was open for 0% of the time, Pallas kernels for 0%

commit v1 on v0

--- a/solution.py
+++ b/solution.py
@@ -2,6 +2,38 @@
 import jax.numpy as jnp
 from jax import lax
 from jax.sharding import PartitionSpec as P
+
+
+def _reduce_scatter_vox(part):
+    vox = lax.axis_size("vox")
+    me = lax.axis_index("vox")
+    sl, d = part.shape
+    db = d // vox
+    m = vox // 2
+    par = me % 2
+    q = me // 2
+    blocks = part.reshape(sl, m, 2, db)
+    keep = lax.dynamic_index_in_dim(blocks, par, axis=2, keepdims=False)
+    send = lax.dynamic_index_in_dim(blocks, 1 - par, axis=2, keepdims=False)
+    pair = [(j, j ^ 1) for j in range(vox)]
+    half = keep + lax.ppermute(send, "vox", pair)
+    out = lax.dynamic_index_in_dim(half, q, axis=1, keepdims=False)
+    for k in range(1, m):
+        piece = lax.dynamic_index_in_dim(half, (q + k) % m, axis=1, keepdims=False)
+        perm = [(g * 2 + p, ((g + k) % m) * 2 + p) for g in range(m) for p in range(2)]
+        out = out + lax.ppermute(piece.astype(jnp.bfloat16), "vox", perm).astype(jnp.float32)
+    return out
+
+
+def _sum_over_src(v):
+    n = lax.axis_size("src")
+    if n & (n - 1):
+        return lax.psum(v, "src")
+    b = 1
+    while b < n:
+        v = v + lax.ppermute(v, "src", [(i, i ^ b) for i in range(n)])
+        b *= 2
+    return v
 
 
 def per_device(forward_voxel_field, adjoint_voxel_field, voxel_input_vector, measurement_weight):
@@ -12,12 +44,12 @@
     predicted_part = lax.dot_general(
         scaled, adjoint_all, (((1,), (1,)), ((), ())), preferred_element_type=jnp.float32
     )
-    pred_share = lax.psum_scatter(predicted_part, "vox", scatter_dimension=1, tiled=True)
+    pred_share = _reduce_scatter_vox(predicted_part)
     weighted_share = (measurement_weight * pred_share).astype(jnp.bfloat16)
     weighted_signal = lax.all_gather(weighted_share, "vox", axis=1, tiled=True)
     back = jnp.dot(weighted_signal, adjoint_all, preferred_element_type=jnp.float32)
     local_sum = jnp.sum(forward_voxel_field.astype(jnp.float32) * back, axis=0)
-    return lax.psum(local_sum, "src")
+    return _sum_over_src(local_sum)
 
 
 def solution(mesh):

time: 294 us -> 282 us (0.959)
  waiting for transfers between devices: 235 us -> 201 us
  local copies, waits for them, and re-layouts: 0.01 us -> 30.2 us
  blocking collectives: 22 us -> 0 us
  starting transfers between devices: 0.08 us -> 6.93 us
  other arithmetic: 2.92 us -> 8.99 us
    reduce_scatter x1 -> x0, waiting for transfers between devices: 70 us -> none  [per_device(): lax.psum_scatter(predicted_part, 'vox', scatter_dimension=1, tiled=True)]
    ppermute x0 -> x5, waiting for transfers between devices: none -> 37.8 us  [the longest x1 24 us: _reduce_scatter_vox(): lax.ppermute(piece.astype(jnp.bfloat16), 'vox', perm).astype(jnp.float32)]
    psum x1 -> x0, blocking collectives: 22 us -> none  [per_device(): return lax.psum(local_sum, 'src')]
    dynamic_slice x0 -> x2, local copies, waits for them, and re-layouts: none -> 15.3 us  [the longest x1 12.1 us: _reduce_scatter_vox(): keep = lax.dynamic_index_in_dim(blocks, par, axis=2, keepdims=False)]
    reshape x0 -> x1, local copies, waits for them, and re-layouts: none -> 11.7 us  [_reduce_scatter_vox(): blocks = part.reshape(sl, m, 2, db)]
    ppermute x0 -> x5, starting transfers between devices: none -> 6.89 us  [the longest x3 5.43 us: _sum_over_src(): v = v + lax.ppermute(v, 'src', [(i, i ^ b) for i in range(n)])]
    add x0 -> x4, other arithmetic: none -> 5.76 us  [the longest x1 5.16 us: _reduce_scatter_vox(): half = keep + lax.ppermute(send, 'vox', pair)]
  transfers between devices with their start and end apart: 3 -> 7, of which waited for: 3 -> 7; matrix products, arithmetic and copies ran while one was open for 0% -> 0% of each run, Pallas kernels for 0% -> 0%
where the time goes in v1:
time: 282 us
  waiting for transfers between devices  201 us (71%)
  local copies, waits for them, and re-layouts  30.2 us (11%)
  matrix products  20.8 us (7%)
  between operations  13.5 us (5%)
  other arithmetic  8.99 us (3%)
  starting transfers between devices  6.93 us (2%)
    all_gather x1, waiting for transfers between devices, per_device(): adjoint_all = lax.all_gather(adjoint_voxel_field, 'src', axis=0, tiled=True)  130 us
    all_gather x1, waiting for transfers between devices, per_device(): weighted_signal = lax.all_gather(weighted_share, 'vox', axis=1, tiled=True)  32.8 us
    ppermute x1, waiting for transfers between devices, _reduce_scatter_vox(): lax.ppermute(piece.astype(jnp.bfloat16), 'vox', perm).astype(jnp.float32)  24 us
    dynamic_slice x1, local copies, waits for them, and re-layouts, _reduce_scatter_vox(): keep = lax.dynamic_index_in_dim(blocks, par, axis=2, keepdims=False)  12.1 us
    reshape x1, local copies, waits for them, and re-layouts, _reduce_scatter_vox(): blocks = part.reshape(sl, m, 2, db)  11.7 us
    dot_general x1, matrix products, per_device(): lax.dot_general(scaled, adjoint_all, (((1,), (1,)), ((), ())), preferred_...  11.5 us
    dot_general x1, matrix products, per_device(): jnp.dot(weighted_signal, adjoint_all, preferred_element_type=jnp.float32)  9.3 us
    ppermute x1, waiting for transfers between devices, _reduce_scatter_vox(): half = keep + lax.ppermute(send, 'vox', pair)  7.5 us
  transfers between devices with their start and end apart: 7, of which 7 were waited for; matrix products, arithmetic and copies ran while one was open for 0% of the time, Pallas kernels for 0%

profile of v1, /device:TPU:0, one launch (start us, length us, event | category | flops | bytes accessed | tf_op | source)
XLA Modules:
  0.0 281.6 jit_solution(14991265973998548466)
XLA Ops:
  6.5 0.0 all-gather.3.cloned.1.call-start
  6.5 0.7 all-gather.3.cloned.1.call-update
  7.3 0.0 all-gather.5.cloned.1.call-start
  7.3 129.8 %all-gather.3.cloned.1.call-done = bf16[4096,1024]{1,0:T(8,128)(2,1)} async-done(((bf16[512,1024]{1,0:T(8,128)(2,1)}), bf16[4096,1024]{1,0:T(8,128)(2,1)}) %all-gather.3.cloned.1.call-update) | async-done | bytes 8388624 | tf_op jit(solution)/shard_map/all_gather | solution.py:43
  137.2 11.5 %fusion.5 = f32[512,4096]{1,0:T(8,128)} fusion(bf16[4096,1024]{1,0:T(8,128)(2,1)} %all-gather.3.cloned.1.call-done, bf16[512,1024]{1,0:T(8,128)(2,1)} %param.4, f32[1024]{0:T(1024)} %param.6), kind=kOutput, calls=%fused_computation.11 | convolution fusion | flops 4296540160 | bytes 17829888 | tf_op jit(solution)/shard_map/dot_general | solution.py:44
  148.6 11.7 %reshape.5 = f32[512,2,2,1024]{3,2,1,0:T(2,128)} reshape(f32[512,4096]{1,0:T(8,128)} %fusion.5) | data formatting | bytes 16777216 | tf_op jit(solution)/shard_map/reshape | solution.py:15
  160.4 12.1 %constant_dynamic-slice_fusion.1 = (f32[512,2,1,1024]{3,2,1,0:T(1,128)}, f32[512,2,1,1024]{3,2,1,0:T(1,128)S(1)}) fusion(f32[512,2,2,1024]{3,2,1,0:T(2,128)} %reshape.5, s32[]{:T(128)S(6)} %select_n.30, s32[]{:T(128)S(6)} %select_n.31), kind=kLoop, calls=%fused_computation.14 | loop fusion | bytes 16777224 | tf_op jit(solution)/shard_map/jit(dynamic_index_in_dim)/dynamic_slice | solution.py:16
  172.5 3.2 %copy.9 = f32[512,2,1,1024]{3,0,1,2:T(8,128)} copy(f32[512,2,1,1024]{3,2,1,0:T(1,128)S(1)} %get-tuple-element.6) | data formatting | bytes 8388608 | tf_op jit(solution)/shard_map/jit(dynamic_index_in_dim)/dynamic_slice | solution.py:17
  175.7 0.0 collective-permute-start
  175.7 7.5 %collective-permute-done = f32[512,2,1024]{2,0,1:T(8,128)} collective-permute-done((f32[512,2,1024]{2,0,1:T(8,128)}, f32[512,2,1024]{2,0,1:T(8,128)}, u32[]{:S(2)}, u32[]{:S(2)}) %collective-permute-start) | collective-permute-done | bytes 4194336 | tf_op jit(solution)/shard_map/ppermute | solution.py:19
  183.2 0.0 copy-start.1
  183.2 5.2 %bitcast_add_fusion = f32[512,2,1024]{2,0,1:T(8,128)S(1)} fusion(f32[512,2,1024]{2,0,1:T(8,128)} %collective-permute-done, f32[512,2,1,1024]{3,2,1,0:T(1,128)} %get-tuple-element.5), kind=kLoop, calls=%fused_computation | loop fusion | flops 1048576 | bytes 12582912 | tf_op jit(solution)/shard_map/add | solution.py:19
  188.4 0.0 copy-start
  188.4 2.0 copy-done
  190.3 1.2 fusion.4
  191.5 1.5 collective-permute-start.1
  193.0 24.0 %collective-permute-done.1 = bf16[512,1024]{1,0:T(8,128)(2,1)S(1)} collective-permute-done((bf16[512,1024]{1,0:T(8,128)(2,1)}, bf16[512,1024]{1,0:T(8,128)(2,1)S(1)}, u32[]{:S(2)}, u32[]{:S(2)}) %collective-permute-start.1) | collective-permute-done | bytes 1048608 | tf_op jit(solution)/shard_map/ppermute | solution.py:24
  216.9 0.0 copy-done.1
  216.9 3.2 %fusion.3 = bf16[512,1024]{1,0:T(8,128)(2,1)} fusion(f32[512,1024]{1,0:T(8,128)S(1)} %copy-done.1, bf16[512,1024]{1,0:T(8,128)(2,1)S(1)} %collective-permute-done.1, f32[512,2,1024]{2,0,1:T(8,128)} %copy-done, s32[]{:T(128)S(6)} %select_n.33), kind=kLoop, calls=%fused_computation.8 | loop fusion | flops 2097152 | bytes 6291460 | tf_op jit(solution)/shard_map/convert_element_type | solution.py:48
  220.2 0.0 all-gather.5.cloned.1.call-update
  220.2 32.8 %all-gather.5.cloned.1.call-done = bf16[512,4096]{1,0:T(8,128)(2,1)} async-done(((bf16[512,1024]{1,0:T(8,128)(2,1)}), bf16[512,4096]{1,0:T(8,128)(2,1)}) %all-gather.5.cloned.1.call-update) | async-done | bytes 4194320 | tf_op jit(solution)/shard_map/all_gather | solution.py:49
  253.0 9.3 %fusion.1 = f32[1024]{0:T(1024)S(1)} fusion(bf16[512,1024]{1,0:T(8,128)(2,1)} %param.4, bf16[512,4096]{1,0:T(8,128)(2,1)} %all-gather.5.cloned.1.call-done, bf16[4096,1024]{1,0:T(8,128)(2,1)} %all-gather.3.cloned.1.call-done), kind=kOutput, calls=%fused_computation.5 | convolution fusion | flops 4296539136 | bytes 13635584 | tf_op jit(solution)/shard_map/dot_general | solution.py:50
  262.3 1.5 collective-permute-start.2
  263.9 2.1 collective-permute-done.2
  266.0 1.5 collective-permute-start.3
  267.5 2.1 collective-permute-done.3
  269.6 2.4 collective-permute-start.4
  272.0 2.1 collective-permute-done.4
  274.1 0.6 add.52
  (2 shorter events, 0.0 us)
Async XLA Ops:
  6.5 130.6 %all-gather.3.cloned.1.call-start = ((), (), s32[]{:S(2)}) async-start(), calls=%async_computation | async-start | bytes 9437184 | tf_op jit(solution)/shard_map/all_gather | solution.py:43
  7.3 245.8 %all-gather.5.cloned.1.call-start = ((), (), s32[]{:S(2)}) async-start(), calls=%async_computation.1 | async-start | bytes 5242880 | tf_op jit(solution)/shard_map/all_gather | solution.py:49
  175.7 7.5 %collective-permute-start = (f32[512,2,1024]{2,0,1:T(8,128)}, f32[512,2,1024]{2,0,1:T(8,128)}, u32[]{:S(2)}, u32[]{:S(2)}) collective-permute-start(f32[512,2,1024]{2,0,1:T(8,128)} %bitcast.15), channel_id=1, source_target_pairs={{0,1},{1,0},{2,3},{3,2},{4,5},{5,4},{6,7},{7,6},{8,9},{9,8},{10,11... | collective-permute-start | bytes 12582920 | tf_op jit(solution)/shard_map/ppermute | solution.py:19
  183.2 33.7 %copy-start.1 = (f32[512,1024]{1,0:T(8,128)S(1)}, f32[512,1024]{1,0:T(8,128)}, u32[]{:S(2)}) copy-start(f32[512,1024]{1,0:T(8,128)} %param.7) | copy-start | bytes 6291460
  188.4 2.0 copy-start
  191.5 25.4 %collective-permute-start.1 = (bf16[512,1024]{1,0:T(8,128)(2,1)}, bf16[512,1024]{1,0:T(8,128)(2,1)S(1)}, u32[]{:S(2)}, u32[]{:S(2)}) collective-permute-start(bf16[512,1024]{1,0:T(8,128)(2,1)} %fusion.4), channel_id=1, source_target_pairs={{0,2},{1,3},{2,0},{3,1},{4,6},{5,7},{6,4},{7,5},{8,10},{9,11},{10,... | collective-permute-start | bytes 3145736 | tf_op jit(solution)/shard_map/ppermute | solution.py:24
  262.3 3.7 %collective-permute-start.2 = (f32[1024]{0:T(1024)S(1)}, f32[1024]{0:T(1024)S(1)}, u32[]{:S(2)}, u32[]{:S(2)}) collective-permute-start(f32[1024]{0:T(1024)S(1)} %fusion.1), channel_id=1, source_target_pairs={{0,4},{4,0},{8,12},{12,8},{16,20},{20,16},{24,28},{28,24},{1,5},{5... | collective-permute-start | bytes 12296 | tf_op jit(solution)/shard_map/ppermute | solution.py:34
  266.0 3.6 %collective-permute-start.3 = (f32[1024]{0:T(1024)S(1)}, f32[1024]{0:T(1024)S(1)}, u32[]{:S(2)}, u32[]{:S(2)}) collective-permute-start(f32[1024]{0:T(1024)S(1)} %add.50), channel_id=1, source_target_pairs={{0,8},{4,12},{8,0},{12,4},{16,24},{20,28},{24,16},{28,20},{1,9},{5... | collective-permute-start | bytes 12296 | tf_op jit(solution)/shard_map/ppermute | solution.py:34
  269.6 4.5 %collective-permute-start.4 = (f32[1024]{0:T(1024)S(1)}, f32[1024]{0:T(1024)S(1)}, u32[]{:S(2)}, u32[]{:S(2)}) collective-permute-start(f32[1024]{0:T(1024)S(1)} %add.51), channel_id=1, source_target_pairs={{0,16},{4,20},{8,24},{12,28},{16,0},{20,4},{24,8},{28,12},{1,17},{... | collective-permute-start | bytes 12296 | tf_op jit(solution)/shard_map/ppermute | solution.py:34
Sparse Core Ops, SparseCore 0:
  9.5 127.6 all-gather.2
  220.3 32.6 all-gather.4

commit v2 on v0

v2 whole, which is shorter than its diff:
```python
import jax
import jax.numpy as jnp
from jax import lax
from jax.sharding import PartitionSpec as P

CHUNKS = 4


def _rows(a, blk, n):
    return lax.dynamic_slice_in_dim(a, blk * n, n, axis=0)


def _sum_over_src(v):
    n = lax.axis_size("src")
    if n & (n - 1):
        return lax.psum(v, "src")
    b = 1
    while b < n:
        v = v + lax.ppermute(v, "src", [(i, i ^ b) for i in range(n)])
        b *= 2
    return v


def per_device(forward_voxel_field, adjoint_voxel_field, voxel_input_vector, measurement_weight):
    nsrc = lax.axis_size("src")
    vox = lax.axis_size("vox")
    me = lax.axis_index("vox")
    m = vox // 2
    par = me % 2
    q = me // 2
    t = nsrc // vox
    sl, vl = forward_voxel_field.shape
    ds = adjoint_voxel_field.shape[0]
    chunks = CHUNKS if ds % CHUNKS == 0 else 1
    r = ds // chunks
    n = t * r
    pair = [(j, j ^ 1) for j in range(vox)]

    def chip_perm(k):
        return [(g * 2 + p, ((g + k) % m) * 2 + p) for g in range(m) for p in range(2)]

    scaled = (forward_voxel_field.astype(jnp.float32) * voxel_input_vector[None, :]).astype(
        jnp.bfloat16
    )
    weight = measurement_weight.reshape(sl, t, ds)
    def gather(c):
        return lax.all_gather(adjoint_voxel_field[c * r:(c + 1) * r], "src", axis=0, tiled=True)

    back = jnp.zeros((sl, vl), jnp.float32)
    nxt = gather(0)
    for c in range(chunks):
        adj = nxt

        def pblock(blk):
            return lax.dot_general(
                scaled, _rows(adj, blk, n), (((1,), (1,)), ((), ())),
                preferred_element_type=jnp.float32,
            )

        halves = []
        for k in range(m):
            g = (q + k) % m
            keep = pblock(2 * g + par)
            send = pblock(2 * g + 1 - par)
            halves.append(keep + lax.ppermute(send, "vox", pair))
        share = halves[0]
        for k in range(1, m):
            share = share + lax.ppermute(
                halves[k].astype(jnp.bfloat16), "vox", chip_perm(k)
            ).astype(jnp.float32)

        w_c = weight[:, :, c * r:(c + 1) * r].reshape(sl, n)
        wt = (w_c * share).astype(jnp.bfloat16)

        got = [(me, wt)]
        for k in range(1, m):
            got.append((2 * ((q - k) % m) + par, lax.ppermute(wt, "vox", chip_perm(k))))
        got = got + [(blk ^ 1, lax.ppermute(w, "vox", pair)) for blk, w in got]
        if c + 1 < chunks:
            nxt, ws = lax.optimization_barrier((gather(c + 1), [w for _, w in got]))
            got = [(blk, w) for (blk, _), w in zip(got, ws)]
        for blk, w in got:
            back = back + jnp.dot(w, _rows(adj, blk, n), preferred_element_type=jnp.float32)

    local_sum = jnp.sum(forward_voxel_field.astype(jnp.float32) * back, axis=0)
    return _sum_over_src(local_sum)


def solution(mesh):
    placed = (P("src", "vox"), P("src", "vox"), P("vox"), P("src", "vox"))
    return jax.shard_map(
        per_device, mesh=mesh, in_specs=placed, out_specs=P("vox"), check_vma=False
    )
```

time: 294 us -> 269 us (0.915)
  waiting for transfers between devices: 235 us -> 175 us
  matrix products: 20.7 us -> 53 us
  blocking collectives: 22 us -> 0 us
  starting transfers between devices: 0.08 us -> 18.6 us
  local copies, waits for them, and re-layouts: 0.01 us -> 7.41 us
    reduce_scatter x1 -> x0, waiting for transfers between devices: 70 us -> none  [per_device(): lax.psum_scatter(predicted_part, 'vox', scatter_dimension=1, tiled=True)]
    ppermute x0 -> x27, waiting for transfers between devices: none -> 45.6 us  [the longest x4 19.2 us: per_device(): got.append((2 * ((q - k) % m) + par, lax.ppermute(wt, 'vox', chip_perm(k))))]
    all_gather x2 -> x4, waiting for transfers between devices: 164 us -> 128 us  [gather(): lax.all_gather(adjoint_voxel_field[c * r:(c + 1) * r], 'src', axis=0, til...]
    dot_general x2 -> x32, matrix products: 20.7 us -> 53 us  [the longest x16 37.4 us: per_device(): jnp.dot(w, _rows(adj, blk, n), preferred_element_type=jnp.float32)]
    psum x1 -> x0, blocking collectives: 22 us -> none  [per_device(): return lax.psum(local_sum, 'src')]
    ppermute x0 -> x27, starting transfers between devices: none -> 18.5 us  [the longest x4 6.13 us: per_device(): got.append((2 * ((q - k) % m) + par, lax.ppermute(wt, 'vox', chip_perm(k))))]
    slice x0 -> x2, local copies, waits for them, and re-layouts: none -> 3.98 us  [the longest x1 2.28 us: gather(): adjoint_voxel_field[c * r:(c + 1) * r]]
    reshape x0 -> x1, local copies, waits for them, and re-layouts: none -> 3.03 us  [per_device(): weight = measurement_weight.reshape(sl, t, ds)]
  transfers between devices with their start and end apart: 3 -> 31, of which waited for: 3 -> 16; matrix products, arithmetic and copies ran while one was open for 0% -> 18% of each run, Pallas kernels for 0% -> 0%
where the time goes in v2:
time: 269 us; the launch traced here: 268 us
  waiting for transfers between devices  175 us (65%)
  matrix products  53 us (20%)
  starting transfers between devices  18.6 us (7%)
  between operations  13.6 us (5%)
  local copies, waits for them, and re-layouts  7.41 us (3%)
    all_gather x4, waiting for transfers between devices, gather(): lax.all_gather(adjoint_voxel_field[c * r:(c + 1) * r], 'src', axis=0, til...  128 us
    dot_general x16, matrix products, per_device(): jnp.dot(w, _rows(adj, blk, n), preferred_element_type=jnp.float32)  37.4 us
    ppermute x4, waiting for transfers between devices, per_device(): got.append((2 * ((q - k) % m) + par, lax.ppermute(wt, 'vox', chip_perm(k))))  19.2 us
    ppermute x4, waiting for transfers between devices, per_device(): lax.ppermute(halves[k].astype(jnp.bfloat16), 'vox', chip_perm(k))  18.1 us
    dot_general x16, matrix products, pblock(): lax.dot_general(scaled, _rows(adj, blk, n), (((1,), (1,)), ((), ())), pre...  15.5 us
    ppermute x3, waiting for transfers between devices, _sum_over_src(): v = v + lax.ppermute(v, 'src', [(i, i ^ b) for i in range(n)])  7.93 us
    ppermute x4, starting transfers between devices, per_device(): got.append((2 * ((q - k) % m) + par, lax.ppermute(wt, 'vox', chip_perm(k))))  6.13 us
    ppermute x4, starting transfers between devices, per_device(): lax.ppermute(halves[k].astype(jnp.bfloat16), 'vox', chip_perm(k))  6.12 us
  transfers between devices with their start and end apart: 31, of which 16 were waited for; matrix products, arithmetic and copies ran while one was open for 18% of the time, Pallas kernels for 0%

profile of v2, /device:TPU:0, one launch (start us, length us, event | category | flops | bytes accessed | tf_op | source)
XLA Modules:
  0.0 268.1 jit_solution(17027108667810342406)
XLA Ops:
  6.5 2.3 fusion.122
  10.4 51.1 %all-gather.7.cloned.1.call-done = bf16[1024,1024]{1,0:T(8,128)(2,1)} async-done(((bf16[128,1024]{1,0:T(8,128)(2,1)}), bf16[1024,1024]{1,0:T(8,128)(2,1)}) %all-gather.7.cloned.1.call-update) | async-done | bytes 2097168 | tf_op jit(solution)/shard_map/all_gather | solution.py:47
  61.5 2.3 fusion.67
  63.9 3.0 %reshape.16 = f32[512,2,512]{2,1,0:T(2,128)S(1)} reshape(f32[512,1024]{1,0:T(8,128)} %param.7) | data formatting | bytes 4194304 | tf_op jit(solution)/shard_map/reshape | solution.py:45
  66.9 1.7 fusion.70
  69.2 1.5 fusion.10
  70.7 1.5 collective-permute-start.2
  72.3 1.7 fusion.121
  74.0 5.1 %collective-permute-done.2 = bf16[512,256]{1,0:T(8,128)(2,1)S(1)} collective-permute-done((bf16[512,256]{1,0:T(8,128)(2,1)S(1)}, bf16[512,256]{1,0:T(8,128)(2,1)S(1)}, u32[]{:S(2)}, u32[]{:S(2)}) %collective-permute-start.2) | collective-permute-done | bytes 262176 | tf_op jit(solution)/shard_map/ppermute | solution.py:68
  79.5 1.5 collective-permute-start.3
  81.1 6.0 %collective-permute-done.3 = bf16[512,256]{1,0:T(8,128)(2,1)S(1)} collective-permute-done((bf16[512,256]{1,0:T(8,128)(2,1)S(1)}, bf16[512,256]{1,0:T(8,128)(2,1)S(1)}, u32[]{:S(2)}, u32[]{:S(2)}) %collective-permute-start.3) | collective-permute-done | bytes 262176 | tf_op jit(solution)/shard_map/ppermute | solution.py:77
  87.2 24.3 %all-gather.5.cloned.1.call-done = bf16[1024,1024]{1,0:T(8,128)(2,1)} async-done(((bf16[128,1024]{1,0:T(8,128)(2,1)}), bf16[1024,1024]{1,0:T(8,128)(2,1)}) %all-gather.5.cloned.1.call-update) | async-done | bytes 2097168 | tf_op jit(solution)/shard_map/all_gather | solution.py:47
  111.5 1.7 fusion.53
  115.7 1.5 collective-permute-start.8
  117.2 1.8 fusion.59
  119.0 5.1 %collective-permute-done.8 = bf16[512,256]{1,0:T(8,128)(2,1)S(1)} collective-permute-done((bf16[512,256]{1,0:T(8,128)(2,1)S(1)}, bf16[512,256]{1,0:T(8,128)(2,1)S(1)}, u32[]{:S(2)}, u32[]{:S(2)}) %collective-permute-start.8) | collective-permute-done | bytes 262176 | tf_op jit(solution)/shard_map/ppermute | solution.py:68
  124.6 1.5 collective-permute-start.9
  126.1 1.8 fusion.61
  128.0 4.4 %collective-permute-done.9 = bf16[512,256]{1,0:T(8,128)(2,1)} collective-permute-done((bf16[512,256]{1,0:T(8,128)(2,1)S(1)}, bf16[512,256]{1,0:T(8,128)(2,1)}, u32[]{:S(2)}, u32[]{:S(2)}) %collective-permute-start.9) | collective-permute-done | bytes 262176 | tf_op jit(solution)/shard_map/ppermute | solution.py:77
  132.4 1.8 fusion.63
  134.2 27.2 %all-gather.9.cloned.1.call-done = bf16[1024,1024]{1,0:T(8,128)(2,1)} async-done(((bf16[128,1024]{1,0:T(8,128)(2,1)}), bf16[1024,1024]{1,0:T(8,128)(2,1)}) %all-gather.9.cloned.1.call-update) | async-done | bytes 2097168 | tf_op jit(solution)/shard_map/all_gather | solution.py:47
  161.4 1.7 fusion.39
  164.2 1.9 fusion.51
  166.6 1.5 collective-permute-start.14
  168.1 2.7 %fusion.47 = f32[512,1024]{1,0:T(8,128)} fusion(bf16[512,256]{1,0:T(8,128)(2,1)} %collective-permute-done.10, bf16[1024,1024]{1,0:T(8,128)(2,1)S(1)} %copy-done.12, s32[]{:T(128)S(6)} %select_n.100), kind=kOutput, calls=%fused_computation.57 | convolution fusion | flops 268435456 | bytes 2883588 | tf_op jit(solution)/shard_map/dot_general | solution.py:83
  170.8 4.1 %collective-permute-done.14 = bf16[512,256]{1,0:T(8,128)(2,1)S(1)} collective-permute-done((bf16[512,256]{1,0:T(8,128)(2,1)S(1)}, bf16[512,256]{1,0:T(8,128)(2,1)S(1)}, u32[]{:S(2)}, u32[]{:S(2)}) %collective-permute-start.14) | collective-permute-done | bytes 262176 | tf_op jit(solution)/shard_map/ppermute | solution.py:68
  175.4 1.5 collective-permute-start.15
  176.9 2.7 %fusion.45 = f32[512,1024]{1,0:T(8,128)} fusion(bf16[512,256]{1,0:T(8,128)(2,1)} %collective-permute-done.11, bf16[1024,1024]{1,0:T(8,128)(2,1)S(1)} %copy-done.12, s32[]{:T(128)S(6)} %select_n.101), kind=kOutput, calls=%fused_computation.55 | convolution fusion | flops 268435456 | bytes 2883588 | tf_op jit(solution)/shard_map/dot_general | solution.py:83
  179.6 3.4 %collective-permute-done.15 = bf16[512,256]{1,0:T(8,128)(2,1)} collective-permute-done((bf16[512,256]{1,0:T(8,128)(2,1)S(1)}, bf16[512,256]{1,0:T(8,128)(2,1)}, u32[]{:S(2)}, u32[]{:S(2)}) %collective-permute-start.15) | collective-permute-done | bytes 262176 | tf_op jit(solution)/shard_map/ppermute | solution.py:77
  183.0 2.8 %fusion.49 = f32[512,1024]{1,0:T(8,128)} fusion(bf16[512,256]{1,0:T(8,128)(2,1)} %collective-permute-done.9, bf16[1024,1024]{1,0:T(8,128)(2,1)S(1)} %copy-done.12, s32[]{:T(128)S(6)} %select_n.99), kind=kOutput, calls=%fused_computation.59 | convolution fusion | flops 268435456 | bytes 2883588 | tf_op jit(solution)/shard_map/dot_general | solution.py:83
  185.8 25.4 %all-gather.11.cloned.1.call-done = bf16[1024,1024]{1,0:T(8,128)(2,1)} async-done(((bf16[128,1024]{1,0:T(8,128)(2,1)}), bf16[1024,1024]{1,0:T(8,128)(2,1)}) %all-gather.11.cloned.1.call-update) | async-done | bytes 2097168 | tf_op jit(solution)/shard_map/all_gather | solution.py:47
  211.2 1.7 fusion.25
  214.4 3.0 %fusion.33 = f32[512,1024]{1,0:T(8,128)} fusion(bf16[512,256]{1,0:T(8,128)(2,1)} %collective-permute-done.16, bf16[1024,1024]{1,0:T(8,128)(2,1)S(1)} %copy-done.10, s32[]{:T(128)S(6)} %select_n.100), kind=kOutput, calls=%fused_computation.43 | convolution fusion | flops 268435456 | bytes 2883588 | tf_op jit(solution)/shard_map/dot_general | solution.py:83
  217.4 2.7 %fusion.31 = f32[512,1024]{1,0:T(8,128)} fusion(bf16[512,256]{1,0:T(8,128)(2,1)} %collective-permute-done.17, bf16[1024,1024]{1,0:T(8,128)(2,1)S(1)} %copy-done.10, s32[]{:T(128)S(6)} %select_n.101), kind=kOutput, calls=%fused_computation.41 | convolution fusion | flops 268435456 | bytes 2883588 | tf_op jit(solution)/shard_map/dot_general | solution.py:83
  220.6 1.5 collective-permute-start.20
  222.2 2.9 %fusion.35 = f32[512,1024]{1,0:T(8,128)} fusion(bf16[512,256]{1,0:T(8,128)(2,1)} %collective-permute-done.15, bf16[1024,1024]{1,0:T(8,128)(2,1)S(1)} %copy-done.10, s32[]{:T(128)S(6)} %select_n.99), kind=kOutput, calls=%fused_computation.45 | convolution fusion | flops 268435456 | bytes 2883588 | tf_op jit(solution)/shard_map/dot_general | solution.py:83
  225.1 3.9 %collective-permute-done.20 = bf16[512,256]{1,0:T(8,128)(2,1)S(1)} collective-permute-done((bf16[512,256]{1,0:T(8,128)(2,1)S(1)}, bf16[512,256]{1,0:T(8,128)(2,1)S(1)}, u32[]{:S(2)}, u32[]{:S(2)}) %collective-permute-start.20) | collective-permute-done | bytes 262176 | tf_op jit(solution)/shard_map/ppermute | solution.py:68
  229.6 1.5 collective-permute-start.21
  231.1 1.9 fusion.23
  233.0 5.3 %collective-permute-done.21 = bf16[512,256]{1,0:T(8,128)(2,1)S(1)} collective-permute-done((bf16[512,256]{1,0:T(8,128)(2,1)S(1)}, bf16[512,256]{1,0:T(8,128)(2,1)S(1)}, u32[]{:S(2)}, u32[]{:S(2)}) %collective-permute-start.21) | collective-permute-done | bytes 262176 | tf_op jit(solution)/shard_map/ppermute | solution.py:77
  238.3 1.8 fusion.21
  240.1 1.8 fusion.19
  242.1 7.1 %fusion.1 = f32[1024]{0:T(1024)S(1)} fusion(bf16[512,1024]{1,0:T(8,128)(2,1)S(1)} %copy-done, f32[512,1024]{1,0:T(8,128)} %fusion.19, f32[512,1024]{1,0:T(8,128)} %fusion.21, f32[512,1024]{1,0:T(8,128)} %fusion.23, f32[512,1024]{1,0:T(8,128)} %fusion.31, f32[512,1024]{1,0:T(8,128)} %fusion.33, f32[512,1024]{1,0:T(8,128)} %fusion.35, ...), kind=kOutput, calls=%fused_computation.3 | convolution fusion | flops 277871616 | bytes 33296388 | tf_op jit(solution)/shard_map/dot_general | solution.py:83
  249.8 3.1 %collective-permute-done.24 = f32[1024]{0:T(1024)S(1)} collective-permute-done((f32[1024]{0:T(1024)S(1)}, f32[1024]{0:T(1024)S(1)}, u32[]{:S(2)}, u32[]{:S(2)}) %collective-permute-start.24) | collective-permute-done | bytes 4128 | tf_op jit(solution)/shard_map/ppermute | solution.py:19
  252.9 1.5 collective-permute-start.25
  254.3 2.1 collective-permute-done.25
  256.5 1.8 collective-permute-start.26
  258.3 2.7 %collective-permute-done.26 = f32[1024]{0:T(1024)S(1)} collective-permute-done((f32[1024]{0:T(1024)S(1)}, f32[1024]{0:T(1024)S(1)}, u32[]{:S(2)}, u32[]{:S(2)}) %collective-permute-start.26) | collective-permute-done | bytes 4128 | tf_op jit(solution)/shard_map/ppermute | solution.py:19
  (106 shorter events, 11.7 us)
Async XLA Ops:
  6.5 55.0 %copy-start = (bf16[512,1024]{1,0:T(8,128)(2,1)S(1)}, bf16[512,1024]{1,0:T(8,128)(2,1)}, u32[]{:S(2)}) copy-start(bf16[512,1024]{1,0:T(8,128)(2,1)} %param.4) | copy-start | bytes 3145732
  6.5 55.0 %copy-start.24 = (f32[1024]{0:T(1024)S(1)}, f32[1024]{0:T(1024)}, u32[]{:S(2)}) copy-start(f32[1024]{0:T(1024)} %param.6) | copy-start | bytes 12292
  6.5 55.0 %all-gather.7.cloned.1.call-start = ((), (), s32[]{:S(2)}) async-start(), calls=%async_computation.1 | async-start | bytes 2359296 | tf_op jit(solution)/shard_map/all_gather | solution.py:47
  8.8 102.6 %all-gather.5.cloned.1.call-start = ((), (), s32[]{:S(2)}) async-start(), calls=%async_computation | async-start | bytes 2359296 | tf_op jit(solution)/shard_map/all_gather | solution.py:47
  9.6 151.8 %all-gather.9.cloned.1.call-start = ((), (), s32[]{:S(2)}) async-start(), calls=%async_computation.2 | async-start | bytes 2359296 | tf_op jit(solution)/shard_map/all_gather | solution.py:47
  10.3 200.8 %all-gather.11.cloned.1.call-start = ((), (), s32[]{:S(2)}) async-start(), calls=%async_computation.3 | async-start | bytes 2359296 | tf_op jit(solution)/shard_map/all_gather | solution.py:47
  63.9 5.3 %collective-permute-start.1 = (f32[512,256]{1,0:T(8,128)}, f32[512,256]{1,0:T(8,128)}, u32[]{:S(2)}, u32[]{:S(2)}) collective-permute-start(f32[512,256]{1,0:T(8,128)} %fusion.67), channel_id=1, source_target_pairs={{0,1},{1,0},{2,3},{3,2},{4,5},{5,4},{6,7},{7,6},{8,9},{9,8},{10,11... | collective-permute-start | bytes 1572872 | tf_op jit(solution)/shard_map/ppermute | solution.py:65
  68.6 5.4 %collective-permute-start = (f32[512,256]{1,0:T(8,128)S(1)}, f32[512,256]{1,0:T(8,128)S(1)}, u32[]{:S(2)}, u32[]{:S(2)}) collective-permute-start(f32[512,256]{1,0:T(8,128)S(1)} %fusion.70), channel_id=1, source_target_pairs={{0,1},{1,0},{2,3},{3,2},{4,5},{5,4},{6,7},{7,6},{8,9},{9,8},{10,11... | collective-permute-start | bytes 1572872 | tf_op jit(solution)/shard_map/ppermute | solution.py:65
  70.7 8.3 %collective-permute-start.2 = (bf16[512,256]{1,0:T(8,128)(2,1)S(1)}, bf16[512,256]{1,0:T(8,128)(2,1)S(1)}, u32[]{:S(2)}, u32[]{:S(2)}) collective-permute-start(bf16[512,256]{1,0:T(8,128)(2,1)S(1)} %fusion.10), channel_id=1, source_target_pairs={{0,2},{1,3},{2,0},{3,1},{4,6},{5,7},{6,4},{7,5},{8,10},{9,11},{10,... | collective-permute-start | bytes 786440 | tf_op jit(solution)/shard_map/ppermute | solution.py:68
  79.5 7.6 %collective-permute-start.3 = (bf16[512,256]{1,0:T(8,128)(2,1)S(1)}, bf16[512,256]{1,0:T(8,128)(2,1)S(1)}, u32[]{:S(2)}, u32[]{:S(2)}) collective-permute-start(bf16[512,256]{1,0:T(8,128)(2,1)S(1)} %fusion.14), channel_id=1, source_target_pairs={{0,2},{1,3},{2,0},{3,1},{4,6},{5,7},{6,4},{7,5},{8,10},{9,11},{10,... | collective-permute-start | bytes 786440 | tf_op jit(solution)/shard_map/ppermute | solution.py:77
  81.1 30.4 %collective-permute-start.4 = (bf16[512,256]{1,0:T(8,128)(2,1)S(1)}, bf16[512,256]{1,0:T(8,128)(2,1)S(1)}, u32[]{:S(2)}, u32[]{:S(2)}) collective-permute-start(bf16[512,256]{1,0:T(8,128)(2,1)S(1)} %fusion.14), channel_id=1, source_target_pairs={{0,1},{1,0},{2,3},{3,2},{4,5},{5,4},{6,7},{7,6},{8,9},{9,8},{10,11... | collective-permute-start | bytes 786440 | tf_op jit(solution)/shard_map/ppermute | solution.py:78
  87.1 26.8 %copy-start.18 = (bf16[512,256]{1,0:T(8,128)(2,1)}, bf16[512,256]{1,0:T(8,128)(2,1)S(1)}, u32[]{:S(2)}) copy-start(bf16[512,256]{1,0:T(8,128)(2,1)S(1)} %collective-permute-done.3) | copy-start | bytes 786436
  87.1 24.3 %collective-permute-start.5 = (bf16[512,256]{1,0:T(8,128)(2,1)S(1)}, bf16[512,256]{1,0:T(8,128)(2,1)S(1)}, u32[]{:S(2)}, u32[]{:S(2)}) collective-permute-start(bf16[512,256]{1,0:T(8,128)(2,1)S(1)} %collective-permute-done.3), channel_id=1, source_target_pairs={{0,1},{1,0},{2,3},{3,2},{4,5},{5,4},{6,7},{7,6},{8,9},{9,8},{10,11... | collective-permute-start | bytes 786440 | tf_op jit(solution)/shard_map/ppermute | solution.py:78
  111.4 3.0 %copy-start.14 = (bf16[1024,1024]{1,0:T(8,128)(2,1)S(1)}, bf16[1024,1024]{1,0:T(8,128)(2,1)}, u32[]{:S(2)}) copy-start(bf16[1024,1024]{1,0:T(8,128)(2,1)} %all-gather.7.cloned.1.call-done) | copy-start | bytes 6291460
  113.2 2.0 collective-permute-start.7
  113.9 5.2 %collective-permute-start.6 = (f32[512,256]{1,0:T(8,128)S(1)}, f32[512,256]{1,0:T(8,128)S(1)}, u32[]{:S(2)}, u32[]{:S(2)}) collective-permute-start(f32[512,256]{1,0:T(8,128)S(1)} %fusion.56), channel_id=1, source_target_pairs={{0,1},{1,0},{2,3},{3,2},{4,5},{5,4},{6,7},{7,6},{8,9},{9,8},{10,11... | collective-permute-start | bytes 1572872 | tf_op jit(solution)/shard_map/ppermute | solution.py:65
  114.4 2.8 %copy-start.23 = (bf16[512,256]{1,0:T(8,128)(2,1)S(1)}, bf16[512,256]{1,0:T(8,128)(2,1)}, u32[]{:S(2)}) copy-start(bf16[512,256]{1,0:T(8,128)(2,1)} %copy-done.22) | copy-start | bytes 786436
  114.8 9.3 %copy-start.17 = (f32[512,2,128]{2,1,0:T(2,128)S(1)}, f32[512,2,128]{2,1,0:T(2,128)}, u32[]{:S(2)}) copy-start(f32[512,2,128]{2,1,0:T(2,128)} %get-tuple-element.37) | copy-start | bytes 1572868
  115.7 8.4 %collective-permute-start.8 = (bf16[512,256]{1,0:T(8,128)(2,1)S(1)}, bf16[512,256]{1,0:T(8,128)(2,1)S(1)}, u32[]{:S(2)}, u32[]{:S(2)}) collective-permute-start(bf16[512,256]{1,0:T(8,128)(2,1)S(1)} %fusion.11), channel_id=1, source_target_pairs={{0,2},{1,3},{2,0},{3,1},{4,6},{5,7},{6,4},{7,5},{8,10},{9,11},{10,... | collective-permute-start | bytes 786440 | tf_op jit(solution)/shard_map/ppermute | solution.py:68
  119.0 7.1 %copy-start.21 = (bf16[512,256]{1,0:T(8,128)(2,1)S(1)}, bf16[512,256]{1,0:T(8,128)(2,1)}, u32[]{:S(2)}) copy-start(bf16[512,256]{1,0:T(8,128)(2,1)} %copy-done.20) | copy-start | bytes 786436
  124.6 7.8 %copy-start.19 = (bf16[512,256]{1,0:T(8,128)(2,1)S(1)}, bf16[512,256]{1,0:T(8,128)(2,1)}, u32[]{:S(2)}) copy-start(bf16[512,256]{1,0:T(8,128)(2,1)} %copy-done.18) | copy-start | bytes 786436
  124.6 7.8 %collective-permute-start.9 = (bf16[512,256]{1,0:T(8,128)(2,1)S(1)}, bf16[512,256]{1,0:T(8,128)(2,1)}, u32[]{:S(2)}, u32[]{:S(2)}) collective-permute-start(bf16[512,256]{1,0:T(8,128)(2,1)S(1)} %fusion.15), channel_id=1, source_target_pairs={{0,2},{1,3},{2,0},{3,1},{4,6},{5,7},{6,4},{7,5},{8,10},{9,11},{10,... | collective-permute-start | bytes 786440 | tf_op jit(solution)/shard_map/ppermute | solution.py:77
  128.0 33.4 %collective-permute-start.10 = (bf16[512,256]{1,0:T(8,128)(2,1)S(1)}, bf16[512,256]{1,0:T(8,128)(2,1)}, u32[]{:S(2)}, u32[]{:S(2)}) collective-permute-start(bf16[512,256]{1,0:T(8,128)(2,1)S(1)} %fusion.15), channel_id=1, source_target_pairs={{0,1},{1,0},{2,3},{3,2},{4,5},{5,4},{6,7},{7,6},{8,9},{9,8},{10,11... | collective-permute-start | bytes 786440 | tf_op jit(solution)/shard_map/ppermute | solution.py:78
  132.4 29.0 %collective-permute-start.11 = (bf16[512,256]{1,0:T(8,128)(2,1)}, bf16[512,256]{1,0:T(8,128)(2,1)}, u32[]{:S(2)}, u32[]{:S(2)}) collective-permute-start(bf16[512,256]{1,0:T(8,128)(2,1)} %collective-permute-done.9), channel_id=1, source_target_pairs={{0,1},{1,0},{2,3},{3,2},{4,5},{5,4},{6,7},{7,6},{8,9},{9,8},{10,11... | collective-permute-start | bytes 786440 | tf_op jit(solution)/shard_map/ppermute | solution.py:78
  161.4 2.8 %copy-start.12 = (bf16[1024,1024]{1,0:T(8,128)(2,1)S(1)}, bf16[1024,1024]{1,0:T(8,128)(2,1)}, u32[]{:S(2)}) copy-start(bf16[1024,1024]{1,0:T(8,128)(2,1)} %all-gather.5.cloned.1.call-done) | copy-start | bytes 6291460
  163.1 3.0 %collective-permute-start.13 = (f32[512,256]{1,0:T(8,128)S(1)}, f32[512,256]{1,0:T(8,128)S(1)}, u32[]{:S(2)}, u32[]{:S(2)}) collective-permute-start(f32[512,256]{1,0:T(8,128)S(1)} %fusion.39), channel_id=1, source_target_pairs={{0,1},{1,0},{2,3},{3,2},{4,5},{5,4},{6,7},{7,6},{8,9},{9,8},{10,11... | collective-permute-start | bytes 1572872 | tf_op jit(solution)/shard_map/ppermute | solution.py:65
  163.6 7.1 %collective-permute-start.12 = (f32[512,256]{1,0:T(8,128)S(1)}, f32[512,256]{1,0:T(8,128)S(1)}, u32[]{:S(2)}, u32[]{:S(2)}) collective-permute-start(f32[512,256]{1,0:T(8,128)S(1)} %fusion.42), channel_id=1, source_target_pairs={{0,1},{1,0},{2,3},{3,2},{4,5},{5,4},{6,7},{7,6},{8,9},{9,8},{10,11... | collective-permute-start | bytes 1572872 | tf_op jit(solution)/shard_map/ppermute | solution.py:65
  166.1 8.8 %copy-start.16 = (f32[512,2,128]{2,1,0:T(2,128)S(1)}, f32[512,2,128]{2,1,0:T(2,128)}, u32[]{:S(2)}) copy-start(f32[512,2,128]{2,1,0:T(2,128)} %get-tuple-element.36) | copy-start | bytes 1572868
  166.6 8.3 %collective-permute-start.14 = (bf16[512,256]{1,0:T(8,128)(2,1)S(1)}, bf16[512,256]{1,0:T(8,128)(2,1)S(1)}, u32[]{:S(2)}, u32[]{:S(2)}) collective-permute-start(bf16[512,256]{1,0:T(8,128)(2,1)S(1)} %fusion.12), channel_id=1, source_target_pairs={{0,2},{1,3},{2,0},{3,1},{4,6},{5,7},{6,4},{7,5},{8,10},{9,11},{10,... | collective-permute-start | bytes 786440 | tf_op jit(solution)/shard_map/ppermute | solution.py:68
  175.4 7.7 %collective-permute-start.15 = (bf16[512,256]{1,0:T(8,128)(2,1)S(1)}, bf16[512,256]{1,0:T(8,128)(2,1)}, u32[]{:S(2)}, u32[]{:S(2)}) collective-permute-start(bf16[512,256]{1,0:T(8,128)(2,1)S(1)} %fusion.16), channel_id=1, source_target_pairs={{0,2},{1,3},{2,0},{3,1},{4,6},{5,7},{6,4},{7,5},{8,10},{9,11},{10,... | collective-permute-start | bytes 786440 | tf_op jit(solution)/shard_map/ppermute | solution.py:77
  179.6 31.6 %collective-permute-start.16 = (bf16[512,256]{1,0:T(8,128)(2,1)S(1)}, bf16[512,256]{1,0:T(8,128)(2,1)}, u32[]{:S(2)}, u32[]{:S(2)}) collective-permute-start(bf16[512,256]{1,0:T(8,128)(2,1)S(1)} %fusion.16), channel_id=1, source_target_pairs={{0,1},{1,0},{2,3},{3,2},{4,5},{5,4},{6,7},{7,6},{8,9},{9,8},{10,11... | collective-permute-start | bytes 786440 | tf_op jit(solution)/shard_map/ppermute | solution.py:78
  183.0 28.1 %collective-permute-start.17 = (bf16[512,256]{1,0:T(8,128)(2,1)}, bf16[512,256]{1,0:T(8,128)(2,1)}, u32[]{:S(2)}, u32[]{:S(2)}) collective-permute-start(bf16[512,256]{1,0:T(8,128)(2,1)} %collective-permute-done.15), channel_id=1, source_target_pairs={{0,1},{1,0},{2,3},{3,2},{4,5},{5,4},{6,7},{7,6},{8,9},{9,8},{10,11... | collective-permute-start | bytes 786440 | tf_op jit(solution)/shard_map/ppermute | solution.py:78
  213.4 11.7 %collective-permute-start.18 = (f32[512,256]{1,0:T(8,128)S(1)}, f32[512,256]{1,0:T(8,128)S(1)}, u32[]{:S(2)}, u32[]{:S(2)}) collective-permute-start(f32[512,256]{1,0:T(8,128)S(1)} %fusion.28), channel_id=1, source_target_pairs={{0,1},{1,0},{2,3},{3,2},{4,5},{5,4},{6,7},{7,6},{8,9},{9,8},{10,11... | collective-permute-start | bytes 1572872 | tf_op jit(solution)/shard_map/ppermute | solution.py:65
  213.5 6.7 %collective-permute-start.19 = (f32[512,256]{1,0:T(8,128)S(1)}, f32[512,256]{1,0:T(8,128)S(1)}, u32[]{:S(2)}, u32[]{:S(2)}) collective-permute-start(f32[512,256]{1,0:T(8,128)S(1)} %fusion.25), channel_id=1, source_target_pairs={{0,1},{1,0},{2,3},{3,2},{4,5},{5,4},{6,7},{7,6},{8,9},{9,8},{10,11... | collective-permute-start | bytes 1572872 | tf_op jit(solution)/shard_map/ppermute | solution.py:65
  220.1 8.9 %copy-start.15 = (f32[512,2,128]{2,1,0:T(2,128)S(1)}, f32[512,2,128]{2,1,0:T(2,128)}, u32[]{:S(2)}) copy-start(f32[512,2,128]{2,1,0:T(2,128)} %get-tuple-element.35) | copy-start | bytes 1572868
  220.6 8.4 %collective-permute-start.20 = (bf16[512,256]{1,0:T(8,128)(2,1)S(1)}, bf16[512,256]{1,0:T(8,128)(2,1)S(1)}, u32[]{:S(2)}, u32[]{:S(2)}) collective-permute-start(bf16[512,256]{1,0:T(8,128)(2,1)S(1)} %fusion.13), channel_id=1, source_target_pairs={{0,2},{1,3},{2,0},{3,1},{4,6},{5,7},{6,4},{7,5},{8,10},{9,11},{10,... | collective-permute-start | bytes 786440 | tf_op jit(solution)/shard_map/ppermute | solution.py:68
  222.2 19.7 %copy-start.6 = (f32[512,1024]{1,0:T(8,128)S(1)}, f32[512,1024]{1,0:T(8,128)}, u32[]{:S(2)}) copy-start(f32[512,1024]{1,0:T(8,128)} %fusion.45) | copy-start | bytes 6291460
  222.2 19.7 %copy-start.7 = (f32[512,1024]{1,0:T(8,128)S(1)}, f32[512,1024]{1,0:T(8,128)}, u32[]{:S(2)}) copy-start(f32[512,1024]{1,0:T(8,128)} %fusion.49) | copy-start | bytes 6291460
  229.0 12.9 %copy-start.5 = (f32[512,1024]{1,0:T(8,128)S(1)}, f32[512,1024]{1,0:T(8,128)}, u32[]{:S(2)}) copy-start(f32[512,1024]{1,0:T(8,128)} %fusion.47) | copy-start | bytes 6291460
  229.5 10.6 %collective-permute-start.22 = (bf16[512,256]{1,0:T(8,128)(2,1)S(1)}, bf16[512,256]{1,0:T(8,128)(2,1)S(1)}, u32[]{:S(2)}, u32[]{:S(2)}) collective-permute-start(bf16[512,256]{1,0:T(8,128)(2,1)S(1)} %fusion.17), channel_id=1, source_target_pairs={{0,1},{1,0},{2,3},{3,2},{4,5},{5,4},{6,7},{7,6},{8,9},{9,8},{10,11... | collective-permute-start | bytes 786440 | tf_op jit(solution)/shard_map/ppermute | solution.py:78
  229.6 8.7 %collective-permute-start.21 = (bf16[512,256]{1,0:T(8,128)(2,1)S(1)}, bf16[512,256]{1,0:T(8,128)(2,1)S(1)}, u32[]{:S(2)}, u32[]{:S(2)}) collective-permute-start(bf16[512,256]{1,0:T(8,128)(2,1)S(1)} %fusion.17), channel_id=1, source_target_pairs={{0,2},{1,3},{2,0},{3,1},{4,6},{5,7},{6,4},{7,5},{8,10},{9,11},{10,... | collective-permute-start | bytes 786440 | tf_op jit(solution)/shard_map/ppermute | solution.py:77
  231.1 10.8 %copy-start.3 = (f32[512,1024]{1,0:T(8,128)S(1)}, f32[512,1024]{1,0:T(8,128)}, u32[]{:S(2)}) copy-start(f32[512,1024]{1,0:T(8,128)} %fusion.63) | copy-start | bytes 6291460
  231.1 10.8 %copy-start.4 = (f32[512,1024]{1,0:T(8,128)S(1)}, f32[512,1024]{1,0:T(8,128)}, u32[]{:S(2)}) copy-start(f32[512,1024]{1,0:T(8,128)} %fusion.51) | copy-start | bytes 6291460
  238.3 3.6 %collective-permute-start.23 = (bf16[512,256]{1,0:T(8,128)(2,1)S(1)}, bf16[512,256]{1,0:T(8,128)(2,1)S(1)}, u32[]{:S(2)}, u32[]{:S(2)}) collective-permute-start(bf16[512,256]{1,0:T(8,128)(2,1)S(1)} %collective-permute-done.21), channel_id=1, source_target_pairs={{0,1},{1,0},{2,3},{3,2},{4,5},{5,4},{6,7},{7,6},{8,9},{9,8},{10,11... | collective-permute-start | bytes 786440 | tf_op jit(solution)/shard_map/ppermute | solution.py:78
  238.3 3.6 %copy-start.2 = (f32[512,1024]{1,0:T(8,128)S(1)}, f32[512,1024]{1,0:T(8,128)}, u32[]{:S(2)}) copy-start(f32[512,1024]{1,0:T(8,128)} %fusion.61) | copy-start | bytes 6291460
  249.2 3.7 %collective-permute-start.24 = (f32[1024]{0:T(1024)S(1)}, f32[1024]{0:T(1024)S(1)}, u32[]{:S(2)}, u32[]{:S(2)}) collective-permute-start(f32[1024]{0:T(1024)S(1)} %fusion.1), channel_id=1, source_target_pairs={{0,4},{4,0},{8,12},{12,8},{16,20},{20,16},{24,28},{28,24},{1,5},{5... | collective-permute-start | bytes 12296 | tf_op jit(solution)/shard_map/ppermute | solution.py:19
  252.9 3.6 %collective-permute-start.25 = (f32[1024]{0:T(1024)S(1)}, f32[1024]{0:T(1024)S(1)}, u32[]{:S(2)}, u32[]{:S(2)}) collective-permute-start(f32[1024]{0:T(1024)S(1)} %add.243), channel_id=1, source_target_pairs={{0,8},{4,12},{8,0},{12,4},{16,24},{20,28},{24,16},{28,20},{1,9},{5... | collective-permute-start | bytes 12296 | tf_op jit(solution)/shard_map/ppermute | solution.py:19
  256.5 4.5 %collective-permute-start.26 = (f32[1024]{0:T(1024)S(1)}, f32[1024]{0:T(1024)S(1)}, u32[]{:S(2)}, u32[]{:S(2)}) collective-permute-start(f32[1024]{0:T(1024)S(1)} %add.244), channel_id=1, source_target_pairs={{0,16},{4,20},{8,24},{12,28},{16,0},{20,4},{24,8},{28,12},{1,17},{... | collective-permute-start | bytes 12296 | tf_op jit(solution)/shard_map/ppermute | solution.py:19
  (8 other events, 17.5 us)
Sparse Core Ops, SparseCore 0:
  9.5 51.9 all-gather.6
  63.6 47.7 all-gather.4
  113.6 47.7 all-gather.8
  163.3 47.7 all-gather.10

commit v3 on v2

--- a/solution.py
+++ b/solution.py
@@ -1,13 +1,105 @@
+import functools
+
 import jax
 import jax.numpy as jnp
 from jax import lax
 from jax.sharding import PartitionSpec as P
 
-CHUNKS = 4
+CHUNKS = 2
 
 
 def _rows(a, blk, n):
     return lax.dynamic_slice_in_dim(a, blk * n, n, axis=0)
+
+
+def _src_grid(mesh):
+    devs = mesh.devices
+    ax = mesh.axis_names.index("src")
+    row = [devs[(i,) + (0,) * (devs.ndim - 1)] if ax == 0 else None for i in range(devs.shape[0])]
+    if ax != 0 or any(not hasattr(d, "coords") for d in row):
+        return None
+    co = [tuple(d.coords) for d in row]
+    n = len(co)
+    diff = [k for k in range(len(co[0])) if n > 1 and co[1][k] != co[0][k]]
+    if len(diff) != 1:
+        return None
+    nb = 1
+    while nb < n and co[nb][diff[0]] != co[0][diff[0]]:
+        nb += 1
+    if n % nb:
+        return None
+    na = n // nb
+
+    def near(i, j):
+        return sum(abs(a - b) for a, b in zip(co[i], co[j])) == 1
+
+    for i in range(n):
+        ia, ib = divmod(i, nb)
+        if ib + 1 < nb and not near(i, i + 1):
+            return None
+        if ia + 1 < na and not near(i, i + nb):
+            return None
+    return nb, na
+
+
+def _line(block, pos, size, pairs_of):
+    out = []
+    for sign in (1, -1):
+        cur = block
+        for s in range(1, size):
+            pairs = []
+            for p in range(size):
+                if 0 <= p + sign < size and 0 <= p - sign * (s - 1) < size:
+                    pairs.extend(pairs_of(p, p + sign))
+            cur = lax.ppermute(cur, "src", pairs)
+            out.append((cur, pos - sign * s, sign, s))
+    return out
+
+
+def _valid(p, size, sign, s):
+    return 0 <= p - sign * s < size
+
+
+def _gather_src(block, grid):
+    nsrc = lax.axis_size("src")
+    if grid is None:
+        return lax.all_gather(block, "src", axis=0, tiled=True)
+    nb, na = grid
+    me = lax.axis_index("src")
+    ia, ib = me // nb, me % nb
+    r = block.shape[0]
+    if nb >= na:
+        n1, p1, n2, p2 = nb, ib, na, ia
+
+        def index(q1, q2):
+            return q2 * nb + q1
+    else:
+        n1, p1, n2, p2 = na, ia, nb, ib
+
+        def index(q1, q2):
+            return q1 * nb + q2
+
+    held = [(block, p1, None)] + [
+        (arr, o1, (sign, s))
+        for arr, o1, sign, s in _line(
+            block, p1, n1, lambda p, d: [(index(p, o), index(d, o)) for o in range(n2)]
+        )
+    ]
+    buf = jnp.zeros(((nsrc + 1) * r,) + block.shape[1:], block.dtype)
+    for arr, o1, how in held:
+
+        def ok1(q1, how=how):
+            return how is None or _valid(q1, n1, *how)
+
+        second = _line(
+            arr, p2, n2,
+            lambda p, d, ok1=ok1: [(index(o, p), index(o, d)) for o in range(n1) if ok1(o)],
+        )
+        for arr2, o2, how2 in [(arr, p2, None)] + [(a2, o, (sg, st)) for a2, o, sg, st in second]:
+            good = (o1 >= 0) & (o1 < n1) & (o2 >= 0) & (o2 < n2)
+            slot = jnp.where(good, index(o1, o2), nsrc)
+            buf = lax.dynamic_update_slice_in_dim(buf, arr2, slot * r, axis=0)
+    return buf[: nsrc * r]
 
 
 def _sum_over_src(v):
@@ -21,7 +113,7 @@
     return v
 
 
-def per_device(forward_voxel_field, adjoint_voxel_field, voxel_input_vector, measurement_weight):
+def per_device(grid, forward_voxel_field, adjoint_voxel_field, voxel_input_vector, measurement_weight):
     nsrc = lax.axis_size("src")
     vox = lax.axis_size("vox")
     me = lax.axis_index("vox")
@@ -44,7 +136,7 @@
     )
     weight = measurement_weight.reshape(sl, t, ds)
     def gather(c):
-        return lax.all_gather(adjoint_voxel_field[c * r:(c + 1) * r], "src", axis=0, tiled=True)
+        return _gather_src(adjoint_voxel_field[c * r:(c + 1) * r], grid)
 
     back = jnp.zeros((sl, vl), jnp.float32)
     nxt = gather(0)
@@ -89,5 +181,5 @@
 def solution(mesh):
     placed = (P("src", "vox"), P("src", "vox"), P("vox"), P("src", "vox"))
     return jax.shard_map(
-        per_device, mesh=mesh, in_specs=placed, out_specs=P("vox"), check_vma=False
+        functools.partial(per_device, _src_grid(mesh)), mesh=mesh, in_specs=placed, out_specs=P("vox"), check_vma=False
     )

time: 269 us -> 253 us (0.941)
  waiting for transfers between devices: 175 us -> 67.1 us
  starting transfers between devices: 18.6 us -> 91.9 us
  local copies, waits for them, and re-layouts: 7.41 us -> 68.8 us
  matrix products: 53 us -> 22.6 us
  between operations: 13.6 us -> 0.86 us
    all_gather x4 -> x0, waiting for transfers between devices: 128 us -> none  [gather(): lax.all_gather(adjoint_voxel_field[c * r:(c + 1) * r], 'src', axis=0, til...]
    ppermute x0 -> x40, starting transfers between devices: none -> 83.9 us  [_line(): cur = lax.ppermute(cur, 'src', pairs)]
    dynamic_update_slice x0 -> x41, local copies, waits for them, and re-layouts: none -> 48.2 us  [_gather_src(): buf = lax.dynamic_update_slice_in_dim(buf, arr2, slot * r, axis=0)]
    ppermute x0 -> x40, waiting for transfers between devices: none -> 34.7 us  [_line(): cur = lax.ppermute(cur, 'src', pairs)]
    dot_general x16 -> x8, matrix products: 37.4 us -> 7.86 us  [per_device(): jnp.dot(w, _rows(adj, blk, n), preferred_element_type=jnp.float32)]
    ppermute x4 -> x2, waiting for transfers between devices: 19.2 us -> 10.1 us  [per_device(): got.append((2 * ((q - k) % m) + par, lax.ppermute(wt, 'vox', chip_perm(k))))]
    ppermute x4 -> x2, waiting for transfers between devices: 18.1 us -> 9.62 us  [per_device(): lax.ppermute(halves[k].astype(jnp.bfloat16), 'vox', chip_perm(k))]
    another operation x0 -> x2, local copies, waits for them, and re-layouts: none -> 5.54 us
  transfers between devices with their start and end apart: 31 -> 55, of which waited for: 16 -> 14; matrix products, arithmetic and copies ran while one was open for 18% -> 32% of each run, Pallas kernels for 0% -> 0%
where the time goes in v3:
time: 253 us; the launch traced here: 252 us
  starting transfers between devices  91.9 us (36%)
  local copies, waits for them, and re-layouts  68.8 us (27%)
  waiting for transfers between devices  67.1 us (27%)
  matrix products  22.6 us (9%)
    ppermute x40, starting transfers between devices, _line(): cur = lax.ppermute(cur, 'src', pairs)  83.9 us
    dynamic_update_slice x41, local copies, waits for them, and re-layouts, _gather_src(): buf = lax.dynamic_update_slice_in_dim(buf, arr2, slot * r, axis=0)  48.2 us
    ppermute x40, waiting for transfers between devices, _line(): cur = lax.ppermute(cur, 'src', pairs)  34.7 us
    dot_general x8, matrix products, pblock(): lax.dot_general(scaled, _rows(adj, blk, n), (((1,), (1,)), ((), ())), pre...  14.7 us
    ppermute x3, waiting for transfers between devices, _sum_over_src(): v = v + lax.ppermute(v, 'src', [(i, i ^ b) for i in range(n)])  11.7 us
    ppermute x2, waiting for transfers between devices, per_device(): got.append((2 * ((q - k) % m) + par, lax.ppermute(wt, 'vox', chip_perm(k))))  10.1 us
    ppermute x2, waiting for transfers between devices, per_device(): lax.ppermute(halves[k].astype(jnp.bfloat16), 'vox', chip_perm(k))  9.62 us
    dot_general x8, matrix products, per_device(): jnp.dot(w, _rows(adj, blk, n), preferred_element_type=jnp.float32)  7.86 us
  transfers between devices with their start and end apart: 55, of which 14 were waited for; matrix products, arithmetic and copies ran while one was open for 32% of the time, Pallas kernels for 0%

profile of v3, /device:TPU:0, one launch (start us, length us, event | category | flops | bytes accessed | tf_op | source)
XLA Modules:
  0.0 251.9 jit_solution(13339982617382785953)
XLA Ops:
  0.0 2.8 %broadcast.11.clone = bf16[2304,1024]{1,0:T(8,128)(2,1)} broadcast(bf16[]{:T(256)} %constant.82.clone.1), dimensions={} | broadcast | bytes 4718594 | tf_op jit(solution)/shard_map/broadcast.1
  4.0 5.8 %collective-permute-start.22 = (bf16[256,1024]{1,0:T(8,128)(2,1)}, bf16[256,1024]{1,0:T(8,128)(2,1)}, u32[]{:S(2)}, u32[]{:S(2)}) collective-permute-start(bf16[256,1024]{1,0:T(8,128)(2,1)} %get-tuple-element.17), channel_id=1, source_target_pairs={{0,8},{4,12},{8,16},{12,20},{16,24},{20,28},{1,9},{5,13},{9,17},{1... | collective-permute-start | bytes 1572872 | tf_op jit(solution)/shard_map/ppermute | solution.py:54
  9.8 4.2 %collective-permute-start.20 = (bf16[256,1024]{1,0:T(8,128)(2,1)}, bf16[256,1024]{1,0:T(8,128)(2,1)}, u32[]{:S(2)}, u32[]{:S(2)}) collective-permute-start(bf16[256,1024]{1,0:T(8,128)(2,1)} %get-tuple-element.17), channel_id=1, source_target_pairs={{0,4},{8,12},{16,20},{24,28},{1,5},{9,13},{17,21},{25,29},{2,6},{1... | collective-permute-start | bytes 1572872 | tf_op jit(solution)/shard_map/ppermute | solution.py:54
  14.0 6.4 %collective-permute-done.22 = bf16[256,1024]{1,0:T(8,128)(2,1)} collective-permute-done((bf16[256,1024]{1,0:T(8,128)(2,1)}, bf16[256,1024]{1,0:T(8,128)(2,1)}, u32[]{:S(2)}, u32[]{:S(2)}) %collective-permute-start.22) | collective-permute-done | bytes 524320 | tf_op jit(solution)/shard_map/ppermute | solution.py:54
  28.9 2.8 %broadcast.11.clone.1 = bf16[2304,1024]{1,0:T(8,128)(2,1)} broadcast(bf16[]{:T(256)} %constant.82.clone.1), dimensions={} | broadcast | bytes 4718594 | tf_op jit(solution)/shard_map/broadcast.1
  32.5 3.0 %reshape.10 = f32[512,2,512]{2,1,0:T(2,128)S(1)} reshape(f32[512,1024]{1,0:T(8,128)} %param.7) | data formatting | bytes 4194304 | tf_op jit(solution)/shard_map/reshape | solution.py:137
  35.7 4.5 %collective-permute-done.31 = bf16[256,1024]{1,0:T(8,128)(2,1)} collective-permute-done((bf16[256,1024]{1,0:T(8,128)(2,1)}, bf16[256,1024]{1,0:T(8,128)(2,1)}, u32[]{:S(2)}, u32[]{:S(2)}) %collective-permute-start.31) | collective-permute-done | bytes 524320 | tf_op jit(solution)/shard_map/ppermute | solution.py:54
  41.5 1.9 constant_dynamic-update-slice_fusion.19
  44.0 1.9 constant_dynamic-update-slice_fusion.18
  46.6 1.9 constant_dynamic-update-slice_fusion.17
  48.5 1.9 constant_dynamic-update-slice_fusion.16
  51.1 1.9 constant_dynamic-update-slice_fusion.15
  53.6 1.9 constant_dynamic-update-slice_fusion.14
  55.5 3.4 %collective-permute-start.32 = (bf16[256,1024]{1,0:T(8,128)(2,1)}, bf16[256,1024]{1,0:T(8,128)(2,1)S(1)}, u32[]{:S(2)}, u32[]{:S(2)}) collective-permute-start(bf16[256,1024]{1,0:T(8,128)(2,1)} %collective-permute-done.31), channel_id=1, source_target_pairs={{0,4},{8,12},{16,20},{1,5},{9,13},{17,21},{2,6},{10,14},{18,22},{3... | collective-permute-start | bytes 1572872 | tf_op jit(solution)/shard_map/ppermute | solution.py:54
  63.1 1.9 constant_dynamic-update-slice_fusion.11
  65.0 4.6 %collective-permute-start.35 = (bf16[256,1024]{1,0:T(8,128)(2,1)S(1)}, bf16[256,1024]{1,0:T(8,128)(2,1)S(1)}, u32[]{:S(2)}, u32[]{:S(2)}) collective-permute-start(bf16[256,1024]{1,0:T(8,128)(2,1)S(1)} %collective-permute-done.34), channel_id=1, source_target_pairs={{0,4},{8,12},{1,5},{9,13},{2,6},{10,14},{3,7},{11,15}} | collective-permute-start | bytes 1572872 | tf_op jit(solution)/shard_map/ppermute | solution.py:54
  72.5 1.9 constant_dynamic-update-slice_fusion.8
  74.4 11.3 %collective-permute-start.2 = (bf16[256,1024]{1,0:T(8,128)(2,1)}, bf16[256,1024]{1,0:T(8,128)(2,1)}, u32[]{:S(2)}, u32[]{:S(2)}) collective-permute-start(bf16[256,1024]{1,0:T(8,128)(2,1)} %get-tuple-element.19), channel_id=1, source_target_pairs={{0,8},{4,12},{8,16},{12,20},{16,24},{20,28},{1,9},{5,13},{9,17},{1... | collective-permute-start | bytes 1572872 | tf_op jit(solution)/shard_map/ppermute | solution.py:54
  85.8 4.6 %collective-permute-start.38 = (bf16[256,1024]{1,0:T(8,128)(2,1)S(1)}, bf16[256,1024]{1,0:T(8,128)(2,1)S(1)}, u32[]{:S(2)}, u32[]{:S(2)}) collective-permute-start(bf16[256,1024]{1,0:T(8,128)(2,1)S(1)} %collective-permute-done.37), channel_id=1, source_target_pairs={{0,4},{1,5},{2,6},{3,7}} | collective-permute-start | bytes 1572872 | tf_op jit(solution)/shard_map/ppermute | solution.py:54
  94.2 5.4 %collective-permute-start = (bf16[256,1024]{1,0:T(8,128)(2,1)}, bf16[256,1024]{1,0:T(8,128)(2,1)}, u32[]{:S(2)}, u32[]{:S(2)}) collective-permute-start(bf16[256,1024]{1,0:T(8,128)(2,1)} %get-tuple-element.19), channel_id=1, source_target_pairs={{0,4},{8,12},{16,20},{24,28},{1,5},{9,13},{17,21},{25,29},{2,6},{1... | collective-permute-start | bytes 1572872 | tf_op jit(solution)/shard_map/ppermute | solution.py:54
  107.9 2.6 %slice.26 = bf16[2048,1024]{1,0:T(8,128)(2,1)S(1)} slice(bf16[2304,1024]{1,0:T(8,128)(2,1)} %constant_dynamic-update-slice_fusion), slice={[0:2048], [0:1024]} | slice | bytes 8388608 | tf_op jit(solution)/shard_map/slice | solution.py:102
  110.5 2.0 copy-done
  112.5 1.7 fusion.34
  114.3 2.0 fusion.64
  118.3 1.9 constant_dynamic-update-slice_fusion.40
  121.0 2.3 constant_dynamic-update-slice_fusion.39
  123.3 1.9 constant_dynamic-update-slice_fusion.38
  125.9 2.0 fusion.37
  133.6 2.0 fusion.6
  137.2 1.9 constant_dynamic-update-slice_fusion.35
  142.3 5.3 %collective-permute-start.12 = (bf16[256,1024]{1,0:T(8,128)(2,1)}, bf16[256,1024]{1,0:T(8,128)(2,1)S(1)}, u32[]{:S(2)}, u32[]{:S(2)}) collective-permute-start(bf16[256,1024]{1,0:T(8,128)(2,1)} %collective-permute-done.11), channel_id=1, source_target_pairs={{0,4},{8,12},{16,20},{1,5},{9,13},{17,21},{2,6},{10,14},{18,22},{3... | collective-permute-start | bytes 1572872 | tf_op jit(solution)/shard_map/ppermute | solution.py:54
  148.4 9.6 %collective-permute-done.14 = bf16[256,1024]{1,0:T(8,128)(2,1)S(1)} collective-permute-done((bf16[256,1024]{1,0:T(8,128)(2,1)}, bf16[256,1024]{1,0:T(8,128)(2,1)S(1)}, u32[]{:S(2)}, u32[]{:S(2)}) %collective-permute-start.14) | collective-permute-done | bytes 524320 | tf_op jit(solution)/shard_map/ppermute | solution.py:54
  159.4 4.6 %collective-permute-start.15 = (bf16[256,1024]{1,0:T(8,128)(2,1)S(1)}, bf16[256,1024]{1,0:T(8,128)(2,1)S(1)}, u32[]{:S(2)}, u32[]{:S(2)}) collective-permute-start(bf16[256,1024]{1,0:T(8,128)(2,1)S(1)} %collective-permute-done.14), channel_id=1, source_target_pairs={{0,4},{8,12},{1,5},{9,13},{2,6},{10,14},{3,7},{11,15}} | collective-permute-start | bytes 1572872 | tf_op jit(solution)/shard_map/ppermute | solution.py:54
  170.0 1.9 constant_dynamic-update-slice_fusion.29
  171.9 6.0 %collective-permute-done.17 = bf16[256,1024]{1,0:T(8,128)(2,1)S(1)} collective-permute-done((bf16[256,1024]{1,0:T(8,128)(2,1)S(1)}, bf16[256,1024]{1,0:T(8,128)(2,1)S(1)}, u32[]{:S(2)}, u32[]{:S(2)}) %collective-permute-start.17) | collective-permute-done | bytes 524320 | tf_op jit(solution)/shard_map/ppermute | solution.py:54
  189.2 6.0 %collective-permute-done.19 = bf16[256,1024]{1,0:T(8,128)(2,1)S(1)} collective-permute-done((bf16[256,1024]{1,0:T(8,128)(2,1)S(1)}, bf16[256,1024]{1,0:T(8,128)(2,1)S(1)}, u32[]{:S(2)}, u32[]{:S(2)}) %collective-permute-start.19) | collective-permute-done | bytes 524320 | tf_op jit(solution)/shard_map/ppermute | solution.py:54
  196.1 2.6 %slice.24 = bf16[2048,1024]{1,0:T(8,128)(2,1)S(1)} slice(bf16[2304,1024]{1,0:T(8,128)(2,1)} %constant_dynamic-update-slice_fusion.21), slice={[0:2048], [0:1024]} | slice | bytes 8388608 | tf_op jit(solution)/shard_map/slice | solution.py:102
  198.8 1.7 fusion.18
  200.5 1.8 fusion.21
  203.5 2.6 %fusion.7 = bf16[512,512]{1,0:T(8,128)(2,1)S(1)} fusion(f32[512,512]{1,0:T(8,128)} %collective-permute-done.47, bf16[2048,1024]{1,0:T(8,128)(2,1)} %copy-done.3, s32[]{:T(128)S(6)} %select_n.290, bf16[512,1024]{1,0:T(8,128)(2,1)S(1)} %copy-done.5, f32[1024]{0:T(1024)S(1)} %copy-done.15), kind=kOutput, calls=%fused_computation.13 | convolution fusion | flops 538968064 | bytes 3674116 | tf_op jit(solution)/shard_map/dot_general | solution.py:147
  207.7 2.1 fusion.28
  210.5 9.6 %collective-permute-done.48 = bf16[512,512]{1,0:T(8,128)(2,1)S(1)} collective-permute-done((bf16[512,512]{1,0:T(8,128)(2,1)S(1)}, bf16[512,512]{1,0:T(8,128)(2,1)S(1)}, u32[]{:S(2)}, u32[]{:S(2)}) %collective-permute-start.48) | collective-permute-done | bytes 524320 | tf_op jit(solution)/shard_map/ppermute | solution.py:160
  220.2 2.1 fusion.8
  222.2 1.6 collective-permute-start.49
  225.4 10.1 %collective-permute-done.49 = bf16[512,512]{1,0:T(8,128)(2,1)S(1)} collective-permute-done((bf16[512,512]{1,0:T(8,128)(2,1)S(1)}, bf16[512,512]{1,0:T(8,128)(2,1)S(1)}, u32[]{:S(2)}, u32[]{:S(2)}) %collective-permute-start.49) | collective-permute-done | bytes 524320 | tf_op jit(solution)/shard_map/ppermute | solution.py:169
  239.6 3.6 %collective-permute-done.52 = f32[1024]{0:T(1024)S(1)} collective-permute-done((f32[1024]{0:T(1024)S(1)}, f32[1024]{0:T(1024)S(1)}, u32[]{:S(2)}, u32[]{:S(2)}) %collective-permute-start.52) | collective-permute-done | bytes 4128 | tf_op jit(solution)/shard_map/ppermute | solution.py:111
  243.2 3.6 %collective-permute-done.53 = f32[1024]{0:T(1024)S(1)} collective-permute-done((f32[1024]{0:T(1024)S(1)}, f32[1024]{0:T(1024)S(1)}, u32[]{:S(2)}, u32[]{:S(2)}) %collective-permute-start.53) | collective-permute-done | bytes 4128 | tf_op jit(solution)/shard_map/ppermute | solution.py:111
  246.8 4.5 %collective-permute-done.54 = f32[1024]{0:T(1024)S(1)} collective-permute-done((f32[1024]{0:T(1024)S(1)}, f32[1024]{0:T(1024)S(1)}, u32[]{:S(2)}, u32[]{:S(2)}) %collective-permute-start.54) | collective-permute-done | bytes 4128 | tf_op jit(solution)/shard_map/ppermute | solution.py:111
  (163 shorter events, 77.6 us)
Async XLA Ops:
  4.0 16.4 %collective-permute-start.22 = (bf16[256,1024]{1,0:T(8,128)(2,1)}, bf16[256,1024]{1,0:T(8,128)(2,1)}, u32[]{:S(2)}, u32[]{:S(2)}) collective-permute-start(bf16[256,1024]{1,0:T(8,128)(2,1)} %get-tuple-element.17), channel_id=1, source_target_pairs={{0,8},{4,12},{8,16},{12,20},{16,24},{20,28},{1,9},{5,13},{9,17},{1... | collective-permute-start | bytes 1572872 | tf_op jit(solution)/shard_map/ppermute | solution.py:54
  9.8 16.2 %collective-permute-start.20 = (bf16[256,1024]{1,0:T(8,128)(2,1)}, bf16[256,1024]{1,0:T(8,128)(2,1)}, u32[]{:S(2)}, u32[]{:S(2)}) collective-permute-start(bf16[256,1024]{1,0:T(8,128)(2,1)} %get-tuple-element.17), channel_id=1, source_target_pairs={{0,4},{8,12},{16,20},{24,28},{1,5},{9,13},{17,21},{25,29},{2,6},{1... | collective-permute-start | bytes 1572872 | tf_op jit(solution)/shard_map/ppermute | solution.py:54
  21.9 18.3 %collective-permute-start.31 = (bf16[256,1024]{1,0:T(8,128)(2,1)}, bf16[256,1024]{1,0:T(8,128)(2,1)}, u32[]{:S(2)}, u32[]{:S(2)}) collective-permute-start(bf16[256,1024]{1,0:T(8,128)(2,1)} %get-tuple-element.17), channel_id=1, source_target_pairs={{8,0},{12,4},{16,8},{20,12},{24,16},{28,20},{9,1},{13,5},{17,9},{2... | collective-permute-start | bytes 1572872 | tf_op jit(solution)/shard_map/ppermute | solution.py:54
  23.2 20.1 %collective-permute-start.21 = (bf16[256,1024]{1,0:T(8,128)(2,1)}, bf16[256,1024]{1,0:T(8,128)(2,1)}, u32[]{:S(2)}, u32[]{:S(2)}) collective-permute-start(bf16[256,1024]{1,0:T(8,128)(2,1)} %get-tuple-element.17), channel_id=1, source_target_pairs={{4,0},{12,8},{20,16},{28,24},{5,1},{13,9},{21,17},{29,25},{6,2},{1... | collective-permute-start | bytes 1572872 | tf_op jit(solution)/shard_map/ppermute | solution.py:54
  24.5 21.4 %collective-permute-start.23 = (bf16[256,1024]{1,0:T(8,128)(2,1)}, bf16[256,1024]{1,0:T(8,128)(2,1)}, u32[]{:S(2)}, u32[]{:S(2)}) collective-permute-start(bf16[256,1024]{1,0:T(8,128)(2,1)} %collective-permute-done.22), channel_id=1, source_target_pairs={{8,12},{16,20},{24,28},{9,13},{17,21},{25,29},{10,14},{18,22},{26,... | collective-permute-start | bytes 1572872 | tf_op jit(solution)/shard_map/ppermute | solution.py:54
  26.0 25.1 %collective-permute-start.24 = (bf16[256,1024]{1,0:T(8,128)(2,1)}, bf16[256,1024]{1,0:T(8,128)(2,1)}, u32[]{:S(2)}, u32[]{:S(2)}) collective-permute-start(bf16[256,1024]{1,0:T(8,128)(2,1)} %collective-permute-done.22), channel_id=1, source_target_pairs={{12,8},{20,16},{28,24},{13,9},{21,17},{29,25},{14,10},{22,18},{30,... | collective-permute-start | bytes 1572872 | tf_op jit(solution)/shard_map/ppermute | solution.py:54
  27.5 22.9 %collective-permute-start.28 = (bf16[256,1024]{1,0:T(8,128)(2,1)}, bf16[256,1024]{1,0:T(8,128)(2,1)}, u32[]{:S(2)}, u32[]{:S(2)}) collective-permute-start(bf16[256,1024]{1,0:T(8,128)(2,1)} %collective-permute-done.25), channel_id=1, source_target_pairs={{16,24},{20,28},{17,25},{21,29},{18,26},{22,30},{19,27},{23,31}} | collective-permute-start | bytes 1572872 | tf_op jit(solution)/shard_map/ppermute | solution.py:54
  40.2 19.5 %collective-permute-start.34 = (bf16[256,1024]{1,0:T(8,128)(2,1)}, bf16[256,1024]{1,0:T(8,128)(2,1)S(1)}, u32[]{:S(2)}, u32[]{:S(2)}) collective-permute-start(bf16[256,1024]{1,0:T(8,128)(2,1)} %collective-permute-done.31), channel_id=1, source_target_pairs={{8,0},{12,4},{16,8},{20,12},{9,1},{13,5},{17,9},{21,13},{10,2},{14... | collective-permute-start | bytes 1572872 | tf_op jit(solution)/shard_map/ppermute | solution.py:54
  43.3 12.1 %collective-permute-start.26 = (bf16[256,1024]{1,0:T(8,128)(2,1)}, bf16[256,1024]{1,0:T(8,128)(2,1)S(1)}, u32[]{:S(2)}, u32[]{:S(2)}) collective-permute-start(bf16[256,1024]{1,0:T(8,128)(2,1)} %collective-permute-done.25), channel_id=1, source_target_pairs={{16,20},{24,28},{17,21},{25,29},{18,22},{26,30},{19,23},{27,31}} | collective-permute-start | bytes 1572872 | tf_op jit(solution)/shard_map/ppermute | solution.py:54
  45.9 15.1 %collective-permute-start.27 = (bf16[256,1024]{1,0:T(8,128)(2,1)}, bf16[256,1024]{1,0:T(8,128)(2,1)S(1)}, u32[]{:S(2)}, u32[]{:S(2)}) collective-permute-start(bf16[256,1024]{1,0:T(8,128)(2,1)} %collective-permute-done.25), channel_id=1, source_target_pairs={{20,16},{28,24},{21,17},{29,25},{22,18},{30,26},{23,19},{31,27}} | collective-permute-start | bytes 1572872 | tf_op jit(solution)/shard_map/ppermute | solution.py:54
  50.4 14.6 %collective-permute-start.29 = (bf16[256,1024]{1,0:T(8,128)(2,1)}, bf16[256,1024]{1,0:T(8,128)(2,1)S(1)}, u32[]{:S(2)}, u32[]{:S(2)}) collective-permute-start(bf16[256,1024]{1,0:T(8,128)(2,1)} %collective-permute-done.28), channel_id=1, source_target_pairs={{24,28},{25,29},{26,30},{27,31}} | collective-permute-start | bytes 1572872 | tf_op jit(solution)/shard_map/ppermute | solution.py:54
  52.9 17.5 %collective-permute-start.30 = (bf16[256,1024]{1,0:T(8,128)(2,1)}, bf16[256,1024]{1,0:T(8,128)(2,1)S(1)}, u32[]{:S(2)}, u32[]{:S(2)}) collective-permute-start(bf16[256,1024]{1,0:T(8,128)(2,1)} %collective-permute-done.28), channel_id=1, source_target_pairs={{28,24},{29,25},{30,26},{31,27}} | collective-permute-start | bytes 1572872 | tf_op jit(solution)/shard_map/ppermute | solution.py:54
  55.5 18.9 %collective-permute-start.32 = (bf16[256,1024]{1,0:T(8,128)(2,1)}, bf16[256,1024]{1,0:T(8,128)(2,1)S(1)}, u32[]{:S(2)}, u32[]{:S(2)}) collective-permute-start(bf16[256,1024]{1,0:T(8,128)(2,1)} %collective-permute-done.31), channel_id=1, source_target_pairs={{0,4},{8,12},{16,20},{1,5},{9,13},{17,21},{2,6},{10,14},{18,22},{3... | collective-permute-start | bytes 1572872 | tf_op jit(solution)/shard_map/ppermute | solution.py:54
  59.7 31.5 %collective-permute-start.33 = (bf16[256,1024]{1,0:T(8,128)(2,1)}, bf16[256,1024]{1,0:T(8,128)(2,1)S(1)}, u32[]{:S(2)}, u32[]{:S(2)}) collective-permute-start(bf16[256,1024]{1,0:T(8,128)(2,1)} %collective-permute-done.31), channel_id=1, source_target_pairs={{4,0},{12,8},{20,16},{5,1},{13,9},{21,17},{6,2},{14,10},{22,18},{7... | collective-permute-start | bytes 1572872 | tf_op jit(solution)/shard_map/ppermute | solution.py:54
  61.0 24.8 %collective-permute-start.37 = (bf16[256,1024]{1,0:T(8,128)(2,1)S(1)}, bf16[256,1024]{1,0:T(8,128)(2,1)S(1)}, u32[]{:S(2)}, u32[]{:S(2)}) collective-permute-start(bf16[256,1024]{1,0:T(8,128)(2,1)S(1)} %collective-permute-done.34), channel_id=1, source_target_pairs={{8,0},{12,4},{9,1},{13,5},{10,2},{14,6},{11,3},{15,7}} | collective-permute-start | bytes 1572872 | tf_op jit(solution)/shard_map/ppermute | solution.py:54
  65.0 29.2 %collective-permute-start.35 = (bf16[256,1024]{1,0:T(8,128)(2,1)S(1)}, bf16[256,1024]{1,0:T(8,128)(2,1)S(1)}, u32[]{:S(2)}, u32[]{:S(2)}) collective-permute-start(bf16[256,1024]{1,0:T(8,128)(2,1)S(1)} %collective-permute-done.34), channel_id=1, source_target_pairs={{0,4},{8,12},{1,5},{9,13},{2,6},{10,14},{3,7},{11,15}} | collective-permute-start | bytes 1572872 | tf_op jit(solution)/shard_map/ppermute | solution.py:54
  70.4 30.0 %collective-permute-start.36 = (bf16[256,1024]{1,0:T(8,128)(2,1)S(1)}, bf16[256,1024]{1,0:T(8,128)(2,1)S(1)}, u32[]{:S(2)}, u32[]{:S(2)}) collective-permute-start(bf16[256,1024]{1,0:T(8,128)(2,1)S(1)} %collective-permute-done.34), channel_id=1, source_target_pairs={{4,0},{12,8},{5,1},{13,9},{6,2},{14,10},{7,3},{15,11}} | collective-permute-start | bytes 1572872 | tf_op jit(solution)/shard_map/ppermute | solution.py:54
  74.4 29.0 %collective-permute-start.2 = (bf16[256,1024]{1,0:T(8,128)(2,1)}, bf16[256,1024]{1,0:T(8,128)(2,1)}, u32[]{:S(2)}, u32[]{:S(2)}) collective-permute-start(bf16[256,1024]{1,0:T(8,128)(2,1)} %get-tuple-element.19), channel_id=1, source_target_pairs={{0,8},{4,12},{8,16},{12,20},{16,24},{20,28},{1,9},{5,13},{9,17},{1... | collective-permute-start | bytes 1572872 | tf_op jit(solution)/shard_map/ppermute | solution.py:54
  85.8 18.9 %collective-permute-start.38 = (bf16[256,1024]{1,0:T(8,128)(2,1)S(1)}, bf16[256,1024]{1,0:T(8,128)(2,1)S(1)}, u32[]{:S(2)}, u32[]{:S(2)}) collective-permute-start(bf16[256,1024]{1,0:T(8,128)(2,1)S(1)} %collective-permute-done.37), channel_id=1, source_target_pairs={{0,4},{1,5},{2,6},{3,7}} | collective-permute-start | bytes 1572872 | tf_op jit(solution)/shard_map/ppermute | solution.py:54
  91.2 15.8 %collective-permute-start.39 = (bf16[256,1024]{1,0:T(8,128)(2,1)S(1)}, bf16[256,1024]{1,0:T(8,128)(2,1)S(1)}, u32[]{:S(2)}, u32[]{:S(2)}) collective-permute-start(bf16[256,1024]{1,0:T(8,128)(2,1)S(1)} %collective-permute-done.37), channel_id=1, source_target_pairs={{4,0},{5,1},{6,2},{7,3}} | collective-permute-start | bytes 1572872 | tf_op jit(solution)/shard_map/ppermute | solution.py:54
  94.2 23.4 %collective-permute-start = (bf16[256,1024]{1,0:T(8,128)(2,1)}, bf16[256,1024]{1,0:T(8,128)(2,1)}, u32[]{:S(2)}, u32[]{:S(2)}) collective-permute-start(bf16[256,1024]{1,0:T(8,128)(2,1)} %get-tuple-element.19), channel_id=1, source_target_pairs={{0,4},{8,12},{16,20},{24,28},{1,5},{9,13},{17,21},{25,29},{2,6},{1... | collective-permute-start | bytes 1572872 | tf_op jit(solution)/shard_map/ppermute | solution.py:54
  100.4 19.8 %collective-permute-start.1 = (bf16[256,1024]{1,0:T(8,128)(2,1)}, bf16[256,1024]{1,0:T(8,128)(2,1)}, u32[]{:S(2)}, u32[]{:S(2)}) collective-permute-start(bf16[256,1024]{1,0:T(8,128)(2,1)} %get-tuple-element.19), channel_id=1, source_target_pairs={{4,0},{12,8},{20,16},{28,24},{5,1},{13,9},{21,17},{29,25},{6,2},{1... | collective-permute-start | bytes 1572872 | tf_op jit(solution)/shard_map/ppermute | solution.py:54
  103.4 24.5 %collective-permute-start.11 = (bf16[256,1024]{1,0:T(8,128)(2,1)}, bf16[256,1024]{1,0:T(8,128)(2,1)}, u32[]{:S(2)}, u32[]{:S(2)}) collective-permute-start(bf16[256,1024]{1,0:T(8,128)(2,1)} %get-tuple-element.19), channel_id=1, source_target_pairs={{8,0},{12,4},{16,8},{20,12},{24,16},{28,20},{9,1},{13,5},{17,9},{2... | collective-permute-start | bytes 1572872 | tf_op jit(solution)/shard_map/ppermute | solution.py:54
  104.7 20.5 %collective-permute-start.5 = (bf16[256,1024]{1,0:T(8,128)(2,1)}, bf16[256,1024]{1,0:T(8,128)(2,1)}, u32[]{:S(2)}, u32[]{:S(2)}) collective-permute-start(bf16[256,1024]{1,0:T(8,128)(2,1)} %collective-permute-done.2), channel_id=1, source_target_pairs={{8,16},{12,20},{16,24},{20,28},{9,17},{13,21},{17,25},{21,29},{10,... | collective-permute-start | bytes 1572872 | tf_op jit(solution)/shard_map/ppermute | solution.py:54
  114.2 18.6 %collective-permute-start.41 = (f32[512,512]{1,0:T(8,128)}, f32[512,512]{1,0:T(8,128)}, u32[]{:S(2)}, u32[]{:S(2)}) collective-permute-start(f32[512,512]{1,0:T(8,128)} %fusion.34), channel_id=1, source_target_pairs={{0,1},{1,0},{2,3},{3,2},{4,5},{5,4},{6,7},{7,6},{8,9},{9,8},{10,11... | collective-permute-start | bytes 3145736 | tf_op jit(solution)/shard_map/ppermute | solution.py:157
  117.6 11.0 %collective-permute-start.3 = (bf16[256,1024]{1,0:T(8,128)(2,1)}, bf16[256,1024]{1,0:T(8,128)(2,1)S(1)}, u32[]{:S(2)}, u32[]{:S(2)}) collective-permute-start(bf16[256,1024]{1,0:T(8,128)(2,1)} %collective-permute-done.2), channel_id=1, source_target_pairs={{8,12},{16,20},{24,28},{9,13},{17,21},{25,29},{10,14},{18,22},{26,... | collective-permute-start | bytes 1572872 | tf_op jit(solution)/shard_map/ppermute | solution.py:54
  120.2 9.8 %collective-permute-start.4 = (bf16[256,1024]{1,0:T(8,128)(2,1)}, bf16[256,1024]{1,0:T(8,128)(2,1)S(1)}, u32[]{:S(2)}, u32[]{:S(2)}) collective-permute-start(bf16[256,1024]{1,0:T(8,128)(2,1)} %collective-permute-done.2), channel_id=1, source_target_pairs={{12,8},{20,16},{28,24},{13,9},{21,17},{29,25},{14,10},{22,18},{30,... | collective-permute-start | bytes 1572872 | tf_op jit(solution)/shard_map/ppermute | solution.py:54
  127.9 7.7 %collective-permute-start.6 = (bf16[256,1024]{1,0:T(8,128)(2,1)}, bf16[256,1024]{1,0:T(8,128)(2,1)S(1)}, u32[]{:S(2)}, u32[]{:S(2)}) collective-permute-start(bf16[256,1024]{1,0:T(8,128)(2,1)} %collective-permute-done.5), channel_id=1, source_target_pairs={{16,20},{24,28},{17,21},{25,29},{18,22},{26,30},{19,23},{27,31}} | collective-permute-start | bytes 1572872 | tf_op jit(solution)/shard_map/ppermute | solution.py:54
  128.6 30.7 %collective-permute-start.40 = (f32[512,512]{1,0:T(8,128)S(1)}, f32[512,512]{1,0:T(8,128)S(1)}, u32[]{:S(2)}, u32[]{:S(2)}) collective-permute-start(f32[512,512]{1,0:T(8,128)S(1)} %fusion.37), channel_id=1, source_target_pairs={{0,1},{1,0},{2,3},{3,2},{4,5},{5,4},{6,7},{7,6},{8,9},{9,8},{10,11... | collective-permute-start | bytes 3145736 | tf_op jit(solution)/shard_map/ppermute | solution.py:157
  130.0 28.0 %collective-permute-start.14 = (bf16[256,1024]{1,0:T(8,128)(2,1)}, bf16[256,1024]{1,0:T(8,128)(2,1)S(1)}, u32[]{:S(2)}, u32[]{:S(2)}) collective-permute-start(bf16[256,1024]{1,0:T(8,128)(2,1)} %collective-permute-done.11), channel_id=1, source_target_pairs={{8,0},{12,4},{16,8},{20,12},{9,1},{13,5},{17,9},{21,13},{10,2},{14... | collective-permute-start | bytes 1572872 | tf_op jit(solution)/shard_map/ppermute | solution.py:54
  132.2 7.7 %collective-permute-start.7 = (bf16[256,1024]{1,0:T(8,128)(2,1)}, bf16[256,1024]{1,0:T(8,128)(2,1)S(1)}, u32[]{:S(2)}, u32[]{:S(2)}) collective-permute-start(bf16[256,1024]{1,0:T(8,128)(2,1)} %collective-permute-done.5), channel_id=1, source_target_pairs={{20,16},{28,24},{21,17},{29,25},{22,18},{30,26},{23,19},{31,27}} | collective-permute-start | bytes 1572872 | tf_op jit(solution)/shard_map/ppermute | solution.py:54
  132.9 9.4 %collective-permute-start.9 = (bf16[256,1024]{1,0:T(8,128)(2,1)S(1)}, bf16[256,1024]{1,0:T(8,128)(2,1)S(1)}, u32[]{:S(2)}, u32[]{:S(2)}) collective-permute-start(bf16[256,1024]{1,0:T(8,128)(2,1)S(1)} %collective-permute-done.8), channel_id=1, source_target_pairs={{24,28},{25,29},{26,30},{27,31}} | collective-permute-start | bytes 1572872 | tf_op jit(solution)/shard_map/ppermute | solution.py:54
  135.6 28.3 %collective-permute-start.42 = (bf16[512,512]{1,0:T(8,128)(2,1)S(1)}, bf16[512,512]{1,0:T(8,128)(2,1)S(1)}, u32[]{:S(2)}, u32[]{:S(2)}) collective-permute-start(bf16[512,512]{1,0:T(8,128)(2,1)S(1)} %fusion.6), channel_id=1, source_target_pairs={{0,2},{1,3},{2,0},{3,1},{4,6},{5,7},{6,4},{7,5},{8,10},{9,11},{10,... | collective-permute-start | bytes 1572872 | tf_op jit(solution)/shard_map/ppermute | solution.py:160
  139.9 26.5 %collective-permute-start.10 = (bf16[256,1024]{1,0:T(8,128)(2,1)S(1)}, bf16[256,1024]{1,0:T(8,128)(2,1)S(1)}, u32[]{:S(2)}, u32[]{:S(2)}) collective-permute-start(bf16[256,1024]{1,0:T(8,128)(2,1)S(1)} %collective-permute-done.8), channel_id=1, source_target_pairs={{28,24},{29,25},{30,26},{31,27}} | collective-permute-start | bytes 1572872 | tf_op jit(solution)/shard_map/ppermute | solution.py:54
  142.3 26.5 %collective-permute-start.12 = (bf16[256,1024]{1,0:T(8,128)(2,1)}, bf16[256,1024]{1,0:T(8,128)(2,1)S(1)}, u32[]{:S(2)}, u32[]{:S(2)}) collective-permute-start(bf16[256,1024]{1,0:T(8,128)(2,1)} %collective-permute-done.11), channel_id=1, source_target_pairs={{0,4},{8,12},{16,20},{1,5},{9,13},{17,21},{2,6},{10,14},{18,22},{3... | collective-permute-start | bytes 1572872 | tf_op jit(solution)/shard_map/ppermute | solution.py:54
  158.1 22.3 %collective-permute-start.13 = (bf16[256,1024]{1,0:T(8,128)(2,1)}, bf16[256,1024]{1,0:T(8,128)(2,1)S(1)}, u32[]{:S(2)}, u32[]{:S(2)}) collective-permute-start(bf16[256,1024]{1,0:T(8,128)(2,1)} %collective-permute-done.11), channel_id=1, source_target_pairs={{4,0},{12,8},{20,16},{5,1},{13,9},{21,17},{6,2},{14,10},{22,18},{7... | collective-permute-start | bytes 1572872 | tf_op jit(solution)/shard_map/ppermute | solution.py:54
  159.4 24.0 %collective-permute-start.15 = (bf16[256,1024]{1,0:T(8,128)(2,1)S(1)}, bf16[256,1024]{1,0:T(8,128)(2,1)S(1)}, u32[]{:S(2)}, u32[]{:S(2)}) collective-permute-start(bf16[256,1024]{1,0:T(8,128)(2,1)S(1)} %collective-permute-done.14), channel_id=1, source_target_pairs={{0,4},{8,12},{1,5},{9,13},{2,6},{10,14},{3,7},{11,15}} | collective-permute-start | bytes 1572872 | tf_op jit(solution)/shard_map/ppermute | solution.py:54
  164.0 14.0 %collective-permute-start.17 = (bf16[256,1024]{1,0:T(8,128)(2,1)S(1)}, bf16[256,1024]{1,0:T(8,128)(2,1)S(1)}, u32[]{:S(2)}, u32[]{:S(2)}) collective-permute-start(bf16[256,1024]{1,0:T(8,128)(2,1)S(1)} %collective-permute-done.14), channel_id=1, source_target_pairs={{8,0},{12,4},{9,1},{13,5},{10,2},{14,6},{11,3},{15,7}} | collective-permute-start | bytes 1572872 | tf_op jit(solution)/shard_map/ppermute | solution.py:54
  166.4 17.0 %collective-permute-start.43 = (bf16[512,512]{1,0:T(8,128)(2,1)S(1)}, bf16[512,512]{1,0:T(8,128)(2,1)S(1)}, u32[]{:S(2)}, u32[]{:S(2)}) collective-permute-start(bf16[512,512]{1,0:T(8,128)(2,1)S(1)} %fusion.9), channel_id=1, source_target_pairs={{0,2},{1,3},{2,0},{3,1},{4,6},{5,7},{6,4},{7,5},{8,10},{9,11},{10,... | collective-permute-start | bytes 1572872 | tf_op jit(solution)/shard_map/ppermute | solution.py:169
  168.8 16.8 %collective-permute-start.16 = (bf16[256,1024]{1,0:T(8,128)(2,1)S(1)}, bf16[256,1024]{1,0:T(8,128)(2,1)S(1)}, u32[]{:S(2)}, u32[]{:S(2)}) collective-permute-start(bf16[256,1024]{1,0:T(8,128)(2,1)S(1)} %collective-permute-done.14), channel_id=1, source_target_pairs={{4,0},{12,8},{5,1},{13,9},{6,2},{14,10},{7,3},{15,11}} | collective-permute-start | bytes 1572872 | tf_op jit(solution)/shard_map/ppermute | solution.py:54
  177.9 10.5 %collective-permute-start.18 = (bf16[256,1024]{1,0:T(8,128)(2,1)S(1)}, bf16[256,1024]{1,0:T(8,128)(2,1)S(1)}, u32[]{:S(2)}, u32[]{:S(2)}) collective-permute-start(bf16[256,1024]{1,0:T(8,128)(2,1)S(1)} %collective-permute-done.17), channel_id=1, source_target_pairs={{0,4},{1,5},{2,6},{3,7}} | collective-permute-start | bytes 1572872 | tf_op jit(solution)/shard_map/ppermute | solution.py:54
  180.4 14.9 %collective-permute-start.19 = (bf16[256,1024]{1,0:T(8,128)(2,1)S(1)}, bf16[256,1024]{1,0:T(8,128)(2,1)S(1)}, u32[]{:S(2)}, u32[]{:S(2)}) collective-permute-start(bf16[256,1024]{1,0:T(8,128)(2,1)S(1)} %collective-permute-done.17), channel_id=1, source_target_pairs={{4,0},{5,1},{6,2},{7,3}} | collective-permute-start | bytes 1572872 | tf_op jit(solution)/shard_map/ppermute | solution.py:54
  183.3 15.4 %collective-permute-start.44 = (bf16[512,512]{1,0:T(8,128)(2,1)S(1)}, bf16[512,512]{1,0:T(8,128)(2,1)S(1)}, u32[]{:S(2)}, u32[]{:S(2)}) collective-permute-start(bf16[512,512]{1,0:T(8,128)(2,1)S(1)} %fusion.9), channel_id=1, source_target_pairs={{0,1},{1,0},{2,3},{3,2},{4,5},{5,4},{6,7},{7,6},{8,9},{9,8},{10,11... | collective-permute-start | bytes 1572872 | tf_op jit(solution)/shard_map/ppermute | solution.py:170
  183.3 15.4 %collective-permute-start.45 = (bf16[512,512]{1,0:T(8,128)(2,1)S(1)}, bf16[512,512]{1,0:T(8,128)(2,1)S(1)}, u32[]{:S(2)}, u32[]{:S(2)}) collective-permute-start(bf16[512,512]{1,0:T(8,128)(2,1)S(1)} %collective-permute-done.43), channel_id=1, source_target_pairs={{0,1},{1,0},{2,3},{3,2},{4,5},{5,4},{6,7},{7,6},{8,9},{9,8},{10,11... | collective-permute-start | bytes 1572872 | tf_op jit(solution)/shard_map/ppermute | solution.py:170
  202.3 8.3 %collective-permute-start.46 = (f32[512,512]{1,0:T(8,128)}, f32[512,512]{1,0:T(8,128)}, u32[]{:S(2)}, u32[]{:S(2)}) collective-permute-start(f32[512,512]{1,0:T(8,128)} %fusion.21), channel_id=1, source_target_pairs={{0,1},{1,0},{2,3},{3,2},{4,5},{5,4},{6,7},{7,6},{8,9},{9,8},{10,11... | collective-permute-start | bytes 3145736 | tf_op jit(solution)/shard_map/ppermute | solution.py:157
  206.1 14.1 %collective-permute-start.48 = (bf16[512,512]{1,0:T(8,128)(2,1)S(1)}, bf16[512,512]{1,0:T(8,128)(2,1)S(1)}, u32[]{:S(2)}, u32[]{:S(2)}) collective-permute-start(bf16[512,512]{1,0:T(8,128)(2,1)S(1)} %fusion.7), channel_id=1, source_target_pairs={{0,2},{1,3},{2,0},{3,1},{4,6},{5,7},{6,4},{7,5},{8,10},{9,11},{10,... | collective-permute-start | bytes 1572872 | tf_op jit(solution)/shard_map/ppermute | solution.py:160
  222.2 13.2 %collective-permute-start.49 = (bf16[512,512]{1,0:T(8,128)(2,1)S(1)}, bf16[512,512]{1,0:T(8,128)(2,1)S(1)}, u32[]{:S(2)}, u32[]{:S(2)}) collective-permute-start(bf16[512,512]{1,0:T(8,128)(2,1)S(1)} %fusion.8), channel_id=1, source_target_pairs={{0,2},{1,3},{2,0},{3,1},{4,6},{5,7},{6,4},{7,5},{8,10},{9,11},{10,... | collective-permute-start | bytes 1572872 | tf_op jit(solution)/shard_map/ppermute | solution.py:169
  224.6 11.7 %collective-permute-start.50 = (bf16[512,512]{1,0:T(8,128)(2,1)S(1)}, bf16[512,512]{1,0:T(8,128)(2,1)S(1)}, u32[]{:S(2)}, u32[]{:S(2)}) collective-permute-start(bf16[512,512]{1,0:T(8,128)(2,1)S(1)} %fusion.8), channel_id=1, source_target_pairs={{0,1},{1,0},{2,3},{3,2},{4,5},{5,4},{6,7},{7,6},{8,9},{9,8},{10,11... | collective-permute-start | bytes 1572872 | tf_op jit(solution)/shard_map/ppermute | solution.py:170
  (23 other events, 156.4 us)

commit v4 on v2

--- a/solution.py
+++ b/solution.py
@@ -1,13 +1,79 @@
+import functools
+
 import jax
 import jax.numpy as jnp
 from jax import lax
 from jax.sharding import PartitionSpec as P
 
-CHUNKS = 4
+CHUNKS = 2
 
 
 def _rows(a, blk, n):
     return lax.dynamic_slice_in_dim(a, blk * n, n, axis=0)
+
+
+def _src_grid(mesh):
+    devs = mesh.devices
+    ax = mesh.axis_names.index("src")
+    row = [devs[(i,) + (0,) * (devs.ndim - 1)] if ax == 0 else None for i in range(devs.shape[0])]
+    if ax != 0 or any(not hasattr(d, "coords") for d in row):
+        return None
+    co = [tuple(d.coords) for d in row]
+    n = len(co)
+    diff = [k for k in range(len(co[0])) if n > 1 and co[1][k] != co[0][k]]
+    if len(diff) != 1:
+        return None
+    nb = 1
+    while nb < n and co[nb][diff[0]] != co[0][diff[0]]:
+        nb += 1
+    if n % nb:
+        return None
+    na = n // nb
+
+    def near(i, j):
+        return sum(abs(a - b) for a, b in zip(co[i], co[j])) == 1
+
+    for i in range(n):
+        ia, ib = divmod(i, nb)
+        if ib + 1 < nb and not near(i, i + 1):
+            return None
+        if ia + 1 < na and not near(i, i + nb):
+            return None
+    if nb != 2 or na < 2:
+        return None
+    return nb, na
+
+
+def _gather_src(block, grid):
+    if grid is None:
+        return lax.all_gather(block, "src", axis=0, tiled=True)
+    nb, na = grid
+    me = lax.axis_index("src")
+    ia, ib = me // nb, me % nb
+    swap = [(i, i ^ 1) for i in range(na * nb)]
+
+    def along(p, d):
+        return [(p * nb + o, d * nb + o) for o in range(nb)]
+
+    def cross(sign, s):
+        return [(i, i ^ 1) for i in range(na * nb) if 0 <= i // nb - sign * s < na]
+
+    got = {}
+    for sign in (1, -1):
+        cur = block
+        for s in range(1, na):
+            pairs = []
+            for p in range(na):
+                if 0 <= p + sign < na and 0 <= p - sign * (s - 1) < na:
+                    pairs.extend(along(p, p + sign))
+            cur = lax.ppermute(cur, "src", pairs)
+            got[(sign, s)] = (cur, lax.ppermute(cur, "src", cross(sign, s)))
+    planes = [(block, lax.ppermute(block, "src", swap))]
+    for k in range(1, na):
+        up, down = got[(-1, k)], got[(1, na - k)]
+        ok = ia + k < na
+        planes.append(tuple(jnp.where(ok, u, d) for u, d in zip(up, down)))
+    return jnp.concatenate([x for pl in planes for x in pl], axis=0)
 
 
 def _sum_over_src(v):
@@ -21,7 +87,7 @@
     return v
 
 
-def per_device(forward_voxel_field, adjoint_voxel_field, voxel_input_vector, measurement_weight):
+def per_device(grid, forward_voxel_field, adjoint_voxel_field, voxel_input_vector, measurement_weight):
     nsrc = lax.axis_size("src")
     vox = lax.axis_size("vox")
     me = lax.axis_index("vox")
@@ -43,8 +109,26 @@
         jnp.bfloat16
     )
     weight = measurement_weight.reshape(sl, t, ds)
+    if grid is not None and grid[0] == t:
+        na = grid[1]
+        ia = lax.axis_index("src") // t
+        flip = lax.axis_index("src") % t == 1
+
+        def rel(blk):
+            return (blk - ia) % na
+
+        def order(w):
+            return jnp.where(flip, w[:, ::-1], w)
+    else:
+        grid = None
+
+        def rel(blk):
+            return blk
+
+        def order(w):
+            return w
     def gather(c):
-        return lax.all_gather(adjoint_voxel_field[c * r:(c + 1) * r], "src", axis=0, tiled=True)
+        return _gather_src(adjoint_voxel_field[c * r:(c + 1) * r], grid)
 
     back = jnp.zeros((sl, vl), jnp.float32)
     nxt = gather(0)
@@ -53,7 +137,7 @@
 
         def pblock(blk):
             return lax.dot_general(
-                scaled, _rows(adj, blk, n), (((1,), (1,)), ((), ())),
+                scaled, _rows(adj, rel(blk), n), (((1,), (1,)), ((), ())),
                 preferred_element_type=jnp.float32,
             )
 
@@ -69,7 +153,7 @@
                 halves[k].astype(jnp.bfloat16), "vox", chip_perm(k)
             ).astype(jnp.float32)
 
-        w_c = weight[:, :, c * r:(c + 1) * r].reshape(sl, n)
+        w_c = order(weight[:, :, c * r:(c + 1) * r]).reshape(sl, n)
         wt = (w_c * share).astype(jnp.bfloat16)
 
         got = [(me, wt)]
@@ -80,7 +164,7 @@
             nxt, ws = lax.optimization_barrier((gather(c + 1), [w for _, w in got]))
             got = [(blk, w) for (blk, _), w in zip(got, ws)]
         for blk, w in got:
-            back = back + jnp.dot(w, _rows(adj, blk, n), preferred_element_type=jnp.float32)
+            back = back + jnp.dot(w, _rows(adj, rel(blk), n), preferred_element_type=jnp.float32)
 
     local_sum = jnp.sum(forward_voxel_field.astype(jnp.float32) * back, axis=0)
     return _sum_over_src(local_sum)
@@ -89,5 +173,5 @@
 def solution(mesh):
     placed = (P("src", "vox"), P("src", "vox"), P("vox"), P("src", "vox"))
     return jax.shard_map(
-        per_device, mesh=mesh, in_specs=placed, out_specs=P("vox"), check_vma=False
+        functools.partial(per_device, _src_grid(mesh)), mesh=mesh, in_specs=placed, out_specs=P("vox"), check_vma=False
     )

time: 269 us -> 228 us (0.85)
  waiting for transfers between devices: 175 us -> 86.3 us
  starting transfers between devices: 18.6 us -> 65.5 us
  matrix products: 53 us -> 29.9 us
  other arithmetic: 0.6 us -> 19.9 us
  local copies, waits for them, and re-layouts: 7.41 us -> 24.8 us
  between operations: 13.6 us -> 0.58 us
    all_gather x4 -> x0, waiting for transfers between devices: 128 us -> none  [gather(): lax.all_gather(adjoint_voxel_field[c * r:(c + 1) * r], 'src', axis=0, til...]
    ppermute x0 -> x26, waiting for transfers between devices: none -> 53.1 us  [the longest x12 33.7 us: _gather_src(): cur = lax.ppermute(cur, 'src', pairs)]
    ppermute x0 -> x26, starting transfers between devices: none -> 50.8 us  [the longest x12 25.3 us: _gather_src(): cur = lax.ppermute(cur, 'src', pairs)]
    dot_general x32 -> x16, matrix products: 53 us -> 29.9 us  [the longest x8 21.1 us: pblock(): lax.dot_general(scaled, _rows(adj, rel(blk), n), (((1,), (1,)), ((), ()))...]
    unnamed x0 -> x10, other arithmetic: none -> 14.2 us
    rev x0 -> x2, local copies, waits for them, and re-layouts: none -> 12 us  [order(): return jnp.where(flip, w[:, ::-1], w)]
    ppermute x4 -> x2, waiting for transfers between devices: 18.1 us -> 9.53 us  [per_device(): lax.ppermute(halves[k].astype(jnp.bfloat16), 'vox', chip_perm(k))]
    unnamed x50 -> x28, local copies, waits for them, and re-layouts: 0.41 us -> 5.93 us
  transfers between devices with their start and end apart: 31 -> 41, of which waited for: 16 -> 18; matrix products, arithmetic and copies ran while one was open for 18% -> 28% of each run, Pallas kernels for 0% -> 0%
where the time goes in v4:
time: 228 us; the launch traced here: 227 us
  waiting for transfers between devices  86.3 us (38%)
  starting transfers between devices  65.5 us (29%)
  matrix products  29.9 us (13%)
  local copies, waits for them, and re-layouts  24.8 us (11%)
  other arithmetic  19.9 us (9%)
    ppermute x12, waiting for transfers between devices, _gather_src(): cur = lax.ppermute(cur, 'src', pairs)  33.7 us
    ppermute x12, starting transfers between devices, _gather_src(): cur = lax.ppermute(cur, 'src', pairs)  25.3 us
    ppermute x12, starting transfers between devices, _gather_src(): got[sign, s] = (cur, lax.ppermute(cur, 'src', cross(sign, s)))  23.4 us
    dot_general x8, matrix products, pblock(): lax.dot_general(scaled, _rows(adj, rel(blk), n), (((1,), (1,)), ((), ()))...  21.1 us
    ppermute x12, waiting for transfers between devices, _gather_src(): got[sign, s] = (cur, lax.ppermute(cur, 'src', cross(sign, s)))  19.4 us
    ppermute x2, waiting for transfers between devices, per_device(): got.append((2 * ((q - k) % m) + par, lax.ppermute(wt, 'vox', chip_perm(k))))  15 us
    unnamed x10, other arithmetic  14.2 us
    rev x2, local copies, waits for them, and re-layouts, order(): return jnp.where(flip, w[:, ::-1], w)  12 us
  transfers between devices with their start and end apart: 41, of which 18 were waited for; matrix products, arithmetic and copies ran while one was open for 28% of the time, Pallas kernels for 0%

profile of v4, /device:TPU:0, one launch (start us, length us, event | category | flops | bytes accessed | tf_op | source)
XLA Modules:
  0.0 227.0 jit_solution(10422608939320057788)
XLA Ops:
  0.0 2.5 %fusion.64 = (bf16[256,1024]{1,0:T(8,128)(2,1)S(1)}, bf16[2048,1024]{1,0:T(8,128)(2,1)}, bf16[2048,1024]{1,0:T(8,128)(2,1)}, bf16[256,1024]{1,0:T(8,128)(2,1)}) fusion(bf16[512,1024]{1,0:T(8,128)(2,1)} %param.5), kind=kLoop, calls=%fused_computation.78 | loop fusion | bytes 3145728 | tf_op jit(solution)/shard_map/slice | solution.py:131
  2.5 4.9 %collective-permute-start.15 = (bf16[256,1024]{1,0:T(8,128)(2,1)S(1)}, bf16[256,1024]{1,0:T(8,128)(2,1)S(1)}, u32[]{:S(2)}, u32[]{:S(2)}) collective-permute-start(bf16[256,1024]{1,0:T(8,128)(2,1)S(1)} %get-tuple-element.17), channel_id=1, source_target_pairs={{0,8},{4,12},{8,16},{12,20},{16,24},{20,28},{1,9},{5,13},{9,17},{1... | collective-permute-start | bytes 1572872 | tf_op jit(solution)/shard_map/ppermute | solution.py:69
  7.5 11.1 %collective-permute-done.15 = bf16[256,1024]{1,0:T(8,128)(2,1)S(1)} collective-permute-done((bf16[256,1024]{1,0:T(8,128)(2,1)S(1)}, bf16[256,1024]{1,0:T(8,128)(2,1)S(1)}, u32[]{:S(2)}, u32[]{:S(2)}) %collective-permute-start.15) | collective-permute-done | bytes 524320 | tf_op jit(solution)/shard_map/ppermute | solution.py:69
  21.3 1.6 collective-permute-start.13
  22.9 14.5 %collective-permute-done.14 = bf16[256,1024]{1,0:T(8,128)(2,1)} collective-permute-done((bf16[256,1024]{1,0:T(8,128)(2,1)S(1)}, bf16[256,1024]{1,0:T(8,128)(2,1)}, u32[]{:S(2)}, u32[]{:S(2)}) %collective-permute-start.14) | collective-permute-done | bytes 524320 | tf_op jit(solution)/shard_map/ppermute | solution.py:69
  37.4 3.4 %collective-permute-start.18 = (bf16[256,1024]{1,0:T(8,128)(2,1)}, bf16[256,1024]{1,0:T(8,128)(2,1)}, u32[]{:S(2)}, u32[]{:S(2)}) collective-permute-start(bf16[256,1024]{1,0:T(8,128)(2,1)} %collective-permute-done.14), channel_id=1, source_target_pairs={{0,4},{4,0},{8,12},{12,8},{16,20},{20,16},{1,5},{5,1},{9,13},{13,9... | collective-permute-start | bytes 1572872 | tf_op jit(solution)/shard_map/ppermute | solution.py:70
  45.0 8.2 %collective-permute-start.2 = (bf16[256,1024]{1,0:T(8,128)(2,1)}, bf16[256,1024]{1,0:T(8,128)(2,1)}, u32[]{:S(2)}, u32[]{:S(2)}) collective-permute-start(bf16[256,1024]{1,0:T(8,128)(2,1)} %get-tuple-element.20), channel_id=1, source_target_pairs={{0,8},{4,12},{8,16},{12,20},{16,24},{20,28},{1,9},{5,13},{9,17},{1... | collective-permute-start | bytes 1572872 | tf_op jit(solution)/shard_map/ppermute | solution.py:69
  54.0 2.0 select_dynamic-update-slice_fusion.5
  57.7 2.6 %collective-permute-start.21 = (bf16[256,1024]{1,0:T(8,128)(2,1)S(1)}, bf16[256,1024]{1,0:T(8,128)(2,1)S(1)}, u32[]{:S(2)}, u32[]{:S(2)}) collective-permute-start(bf16[256,1024]{1,0:T(8,128)(2,1)S(1)} %collective-permute-done.20), channel_id=1, source_target_pairs={{0,4},{4,0},{8,12},{12,8},{1,5},{5,1},{9,13},{13,9},{2,6},{6,2},{1... | collective-permute-start | bytes 1572872 | tf_op jit(solution)/shard_map/ppermute | solution.py:70
  61.6 2.0 select_dynamic-update-slice_fusion.4
  65.4 3.4 %collective-permute-done.21 = bf16[256,1024]{1,0:T(8,128)(2,1)S(1)} collective-permute-done((bf16[256,1024]{1,0:T(8,128)(2,1)S(1)}, bf16[256,1024]{1,0:T(8,128)(2,1)S(1)}, u32[]{:S(2)}, u32[]{:S(2)}) %collective-permute-start.21) | collective-permute-done | bytes 524320 | tf_op jit(solution)/shard_map/ppermute | solution.py:70
  70.3 6.7 %collective-permute-done.23 = bf16[256,1024]{1,0:T(8,128)(2,1)S(1)} collective-permute-done((bf16[256,1024]{1,0:T(8,128)(2,1)S(1)}, bf16[256,1024]{1,0:T(8,128)(2,1)S(1)}, u32[]{:S(2)}, u32[]{:S(2)}) %collective-permute-start.23) | collective-permute-done | bytes 524320 | tf_op jit(solution)/shard_map/ppermute | solution.py:69
  76.9 2.4 %collective-permute-start.24 = (bf16[256,1024]{1,0:T(8,128)(2,1)S(1)}, bf16[256,1024]{1,0:T(8,128)(2,1)S(1)}, u32[]{:S(2)}, u32[]{:S(2)}) collective-permute-start(bf16[256,1024]{1,0:T(8,128)(2,1)S(1)} %collective-permute-done.23), channel_id=1, source_target_pairs={{0,4},{4,0},{1,5},{5,1},{2,6},{6,2},{3,7},{7,3}} | collective-permute-start | bytes 1572872 | tf_op jit(solution)/shard_map/ppermute | solution.py:70
  81.4 8.1 %collective-permute-done.24 = bf16[256,1024]{1,0:T(8,128)(2,1)S(1)} collective-permute-done((bf16[256,1024]{1,0:T(8,128)(2,1)S(1)}, bf16[256,1024]{1,0:T(8,128)(2,1)S(1)}, u32[]{:S(2)}, u32[]{:S(2)}) %collective-permute-start.24) | collective-permute-done | bytes 524320 | tf_op jit(solution)/shard_map/ppermute | solution.py:70
  90.6 3.0 %fusion.34 = f32[512,512]{1,0:T(8,128)} fusion(bf16[2048,1024]{1,0:T(8,128)(2,1)} %select_dynamic-update-slice_fusion, s32[]{:T(128)S(6)} %select_n.216, bf16[512,1024]{1,0:T(8,128)(2,1)S(1)} %copy-done, f32[1024]{0:T(1024)S(1)} %copy-done.11), kind=kOutput, calls=%fused_computation.38 | convolution fusion | flops 538443776 | bytes 3149828 | tf_op jit(solution)/shard_map/dot_general | solution.py:139
  94.1 3.0 %reshape.10 = f32[512,2,512]{2,1,0:T(2,128)S(1)} reshape(f32[512,1024]{1,0:T(8,128)} %param.7) | data formatting | bytes 4194304 | tf_op jit(solution)/shard_map/reshape | solution.py:111
  98.4 6.0 %rev.6 = f32[512,2,256]{2,1,0:T(2,128)} reverse(f32[512,2,256]{2,1,0:T(2,128)} %slice.16), dimensions={1} | reverse | bytes 2097152 | tf_op jit(solution)/shard_map/rev | solution.py:121
  107.4 2.9 %fusion.37 = f32[512,512]{1,0:T(8,128)} fusion(bf16[2048,1024]{1,0:T(8,128)(2,1)} %select_dynamic-update-slice_fusion, s32[]{:T(128)S(6)} %select_n.211, bf16[512,1024]{1,0:T(8,128)(2,1)S(1)} %copy-done, f32[1024]{0:T(1024)S(1)} %copy-done.11), kind=kOutput, calls=%fused_computation.41 | convolution fusion | flops 538443776 | bytes 3149828 | tf_op jit(solution)/shard_map/dot_general | solution.py:139
  110.5 2.3 %broadcast_select_fusion.1 = (f32[512,2,256]{2,1,0:T(2,128)}, f32[512,2,256]{2,1,0:T(2,128)}) fusion(f32[512,2,256]{2,1,0:T(2,128)S(1)} %copy-done.5, pred[]{:T(512)S(6)} %eq.28, f32[512,2,512]{2,1,0:T(2,128)S(1)} %reshape.10), kind=kLoop, calls=%fused_computation.45 | loop fusion | flops 262144 | bytes 5242881 | tf_op jit(solution)/shard_map/jit(_where)/select_n | solution.py:121
  112.8 2.3 copy.5
  115.1 3.5 %collective-permute-start.5 = (bf16[256,1024]{1,0:T(8,128)(2,1)}, bf16[256,1024]{1,0:T(8,128)(2,1)S(1)}, u32[]{:S(2)}, u32[]{:S(2)}) collective-permute-start(bf16[256,1024]{1,0:T(8,128)(2,1)} %collective-permute-done.1), channel_id=1, source_target_pairs={{0,4},{4,0},{8,12},{12,8},{16,20},{20,16},{1,5},{5,1},{9,13},{13,9... | collective-permute-start | bytes 1572872 | tf_op jit(solution)/shard_map/ppermute | solution.py:70
  118.6 1.9 constant_dynamic-update-slice_fusion
  122.8 2.3 %fusion.6 = bf16[512,512]{1,0:T(8,128)(2,1)S(1)} fusion(f32[512,512]{1,0:T(8,128)} %collective-permute-done.27, bf16[2048,1024]{1,0:T(8,128)(2,1)} %select_dynamic-update-slice_fusion, s32[]{:T(128)S(6)} %select_n.214, bf16[512,1024]{1,0:T(8,128)(2,1)S(1)} %copy-done, f32[1024]{0:T(1024)S(1)} %copy-done.11), kind=kOutput, calls=%fused_computation.12 | convolution fusion | flops 538968064 | bytes 3674116 | tf_op jit(solution)/shard_map/dot_general | solution.py:139
  125.1 1.6 collective-permute-start.28
  126.7 2.1 select_dynamic-update-slice_fusion.11
  128.8 2.7 %collective-permute-done.5 = bf16[256,1024]{1,0:T(8,128)(2,1)S(1)} collective-permute-done((bf16[256,1024]{1,0:T(8,128)(2,1)}, bf16[256,1024]{1,0:T(8,128)(2,1)S(1)}, u32[]{:S(2)}, u32[]{:S(2)}) %collective-permute-start.5) | collective-permute-done | bytes 524320 | tf_op jit(solution)/shard_map/ppermute | solution.py:70
  132.1 3.4 %collective-permute-start.8 = (bf16[256,1024]{1,0:T(8,128)(2,1)}, bf16[256,1024]{1,0:T(8,128)(2,1)S(1)}, u32[]{:S(2)}, u32[]{:S(2)}) collective-permute-start(bf16[256,1024]{1,0:T(8,128)(2,1)} %collective-permute-done.7), channel_id=1, source_target_pairs={{0,4},{4,0},{8,12},{12,8},{1,5},{5,1},{9,13},{13,9},{2,6},{6,2},{1... | collective-permute-start | bytes 1572872 | tf_op jit(solution)/shard_map/ppermute | solution.py:70
  137.4 3.0 %collective-permute-start.11 = (bf16[256,1024]{1,0:T(8,128)(2,1)S(1)}, bf16[256,1024]{1,0:T(8,128)(2,1)S(1)}, u32[]{:S(2)}, u32[]{:S(2)}) collective-permute-start(bf16[256,1024]{1,0:T(8,128)(2,1)S(1)} %collective-permute-done.10), channel_id=1, source_target_pairs={{0,4},{4,0},{1,5},{5,1},{2,6},{6,2},{3,7},{7,3}} | collective-permute-start | bytes 1572872 | tf_op jit(solution)/shard_map/ppermute | solution.py:70
  140.5 2.4 %fusion.9 = bf16[512,512]{1,0:T(8,128)(2,1)S(1)} fusion(f32[512,512]{1,0:T(8,128)S(1)} %bitcast.13, f32[512,512]{1,0:T(8,128)} %collective-permute-done.26, bf16[512,512]{1,0:T(8,128)(2,1)S(1)} %collective-permute-done.28, bf16[2048,1024]{1,0:T(8,128)(2,1)} %select_dynamic-update-slice_fusion, s32[]{:T(128)S(6)} %select_n.209, ...), kind=kOutput, calls=%fused_computation.15 | convolution fusion | flops 539754496 | bytes 5246980 | tf_op jit(solution)/shard_map/dot_general | solution.py:139
  142.9 1.6 collective-permute-start.29
  144.5 2.0 select_dynamic-update-slice_fusion.9
  146.5 2.6 %collective-permute-done.8 = bf16[256,1024]{1,0:T(8,128)(2,1)S(1)} collective-permute-done((bf16[256,1024]{1,0:T(8,128)(2,1)}, bf16[256,1024]{1,0:T(8,128)(2,1)S(1)}, u32[]{:S(2)}, u32[]{:S(2)}) %collective-permute-start.8) | collective-permute-done | bytes 524320 | tf_op jit(solution)/shard_map/ppermute | solution.py:70
  150.1 5.0 %collective-permute-done.29 = bf16[512,512]{1,0:T(8,128)(2,1)S(1)} collective-permute-done((bf16[512,512]{1,0:T(8,128)(2,1)S(1)}, bf16[512,512]{1,0:T(8,128)(2,1)S(1)}, u32[]{:S(2)}, u32[]{:S(2)}) %collective-permute-start.29) | collective-permute-done | bytes 524320 | tf_op jit(solution)/shard_map/ppermute | solution.py:161
  156.1 2.7 %collective-permute-done.11 = bf16[256,1024]{1,0:T(8,128)(2,1)S(1)} collective-permute-done((bf16[256,1024]{1,0:T(8,128)(2,1)S(1)}, bf16[256,1024]{1,0:T(8,128)(2,1)S(1)}, u32[]{:S(2)}, u32[]{:S(2)}) %collective-permute-start.11) | collective-permute-done | bytes 524320 | tf_op jit(solution)/shard_map/ppermute | solution.py:70
  160.6 2.9 %fusion.18 = f32[512,512]{1,0:T(8,128)} fusion(bf16[2048,1024]{1,0:T(8,128)(2,1)} %select_dynamic-update-slice_fusion.6, s32[]{:T(128)S(6)} %select_n.216, bf16[512,1024]{1,0:T(8,128)(2,1)S(1)} %copy-done, f32[1024]{0:T(1024)S(1)} %copy-done.11), kind=kOutput, calls=%fused_computation.24 | convolution fusion | flops 538443776 | bytes 3149828 | tf_op jit(solution)/shard_map/dot_general | solution.py:139
  163.5 6.0 %rev.7 = f32[512,2,256]{2,1,0:T(2,128)} reverse(f32[512,2,256]{2,1,0:T(2,128)} %get-tuple-element.16), dimensions={1} | reverse | bytes 2097152 | tf_op jit(solution)/shard_map/rev | solution.py:121
  169.6 3.0 %fusion.21 = f32[512,512]{1,0:T(8,128)} fusion(bf16[2048,1024]{1,0:T(8,128)(2,1)} %select_dynamic-update-slice_fusion.6, s32[]{:T(128)S(6)} %select_n.211, bf16[512,1024]{1,0:T(8,128)(2,1)S(1)} %copy-done, f32[1024]{0:T(1024)S(1)} %copy-done.11), kind=kOutput, calls=%fused_computation.27 | convolution fusion | flops 538443776 | bytes 3149828 | tf_op jit(solution)/shard_map/dot_general | solution.py:139
  173.9 2.4 %fusion.7 = bf16[512,512]{1,0:T(8,128)(2,1)S(1)} fusion(f32[512,512]{1,0:T(8,128)} %collective-permute-done.33, bf16[2048,1024]{1,0:T(8,128)(2,1)} %select_dynamic-update-slice_fusion.6, s32[]{:T(128)S(6)} %select_n.214, bf16[512,1024]{1,0:T(8,128)(2,1)S(1)} %copy-done, f32[1024]{0:T(1024)S(1)} %copy-done.11), kind=kOutput, calls=%fused_computation.13 | convolution fusion | flops 538968064 | bytes 3674116 | tf_op jit(solution)/shard_map/dot_general | solution.py:139
  177.9 2.1 fusion.28
  180.8 9.5 %collective-permute-done.34 = bf16[512,512]{1,0:T(8,128)(2,1)S(1)} collective-permute-done((bf16[512,512]{1,0:T(8,128)(2,1)S(1)}, bf16[512,512]{1,0:T(8,128)(2,1)S(1)}, u32[]{:S(2)}, u32[]{:S(2)}) %collective-permute-start.34) | collective-permute-done | bytes 524320 | tf_op jit(solution)/shard_map/ppermute | solution.py:152
  190.3 2.1 fusion.8
  195.4 10.0 %collective-permute-done.35 = bf16[512,512]{1,0:T(8,128)(2,1)S(1)} collective-permute-done((bf16[512,512]{1,0:T(8,128)(2,1)S(1)}, bf16[512,512]{1,0:T(8,128)(2,1)S(1)}, u32[]{:S(2)}, u32[]{:S(2)}) %collective-permute-start.35) | collective-permute-done | bytes 524320 | tf_op jit(solution)/shard_map/ppermute | solution.py:161
  208.1 2.4 %fusion.1 = f32[1024]{0:T(1024)S(1)} fusion(bf16[512,1024]{1,0:T(8,128)(2,1)S(1)} %copy-done, f32[512,1024]{1,0:T(8,128)S(1)} %fusion.10, f32[512,1024]{1,0:T(8,128)S(1)} %fusion.12, f32[512,1024]{1,0:T(8,128)S(1)} %fusion.14, f32[512,1024]{1,0:T(8,128)S(1)} %fusion.16, f32[512,1024]{1,0:T(8,128)S(1)} %fusion.28, f32[512,1024]{1,0:T(8,128)S(1)} %fusion.32, ...), kind=kOutput, calls=%fused_computation.3 | convolution fusion | flops 542112768 | bytes 17305604 | tf_op jit(solution)/shard_map/dot_general | solution.py:167
  210.5 1.5 collective-permute-start.38
  212.1 2.1 collective-permute-done.38
  214.2 6.1 %collective-permute-start.39 = (f32[1024]{0:T(1024)S(1)}, f32[1024]{0:T(1024)S(1)}, u32[]{:S(2)}, u32[]{:S(2)}) collective-permute-start(f32[1024]{0:T(1024)S(1)} %add.213), channel_id=1, source_target_pairs={{0,8},{4,12},{8,0},{12,4},{16,24},{20,28},{24,16},{28,20},{1,9},{5... | collective-permute-start | bytes 12296 | tf_op jit(solution)/shard_map/ppermute | solution.py:85
  220.3 1.6 collective-permute-done.39
  221.9 4.5 %collective-permute-done.40 = f32[1024]{0:T(1024)S(1)} collective-permute-done((f32[1024]{0:T(1024)S(1)}, f32[1024]{0:T(1024)S(1)}, u32[]{:S(2)}, u32[]{:S(2)}) %collective-permute-start.40) | collective-permute-done | bytes 4128 | tf_op jit(solution)/shard_map/ppermute | solution.py:85
  (100 shorter events, 40.2 us)
Async XLA Ops:
  2.5 16.1 %collective-permute-start.15 = (bf16[256,1024]{1,0:T(8,128)(2,1)S(1)}, bf16[256,1024]{1,0:T(8,128)(2,1)S(1)}, u32[]{:S(2)}, u32[]{:S(2)}) collective-permute-start(bf16[256,1024]{1,0:T(8,128)(2,1)S(1)} %get-tuple-element.17), channel_id=1, source_target_pairs={{0,8},{4,12},{8,16},{12,20},{16,24},{20,28},{1,9},{5,13},{9,17},{1... | collective-permute-start | bytes 1572872 | tf_op jit(solution)/shard_map/ppermute | solution.py:69
  18.6 2.0 collective-permute-start.16
  19.3 18.1 %collective-permute-start.14 = (bf16[256,1024]{1,0:T(8,128)(2,1)S(1)}, bf16[256,1024]{1,0:T(8,128)(2,1)}, u32[]{:S(2)}, u32[]{:S(2)}) collective-permute-start(bf16[256,1024]{1,0:T(8,128)(2,1)S(1)} %get-tuple-element.17), channel_id=1, source_target_pairs={{8,0},{12,4},{16,8},{20,12},{24,16},{28,20},{9,1},{13,5},{17,9},{2... | collective-permute-start | bytes 1572872 | tf_op jit(solution)/shard_map/ppermute | solution.py:69
  20.6 21.5 %collective-permute-start.17 = (bf16[256,1024]{1,0:T(8,128)(2,1)S(1)}, bf16[256,1024]{1,0:T(8,128)(2,1)S(1)}, u32[]{:S(2)}, u32[]{:S(2)}) collective-permute-start(bf16[256,1024]{1,0:T(8,128)(2,1)S(1)} %collective-permute-done.16), channel_id=1, source_target_pairs={{16,24},{20,28},{17,25},{21,29},{18,26},{22,30},{19,27},{23,31}} | collective-permute-start | bytes 1572872 | tf_op jit(solution)/shard_map/ppermute | solution.py:69
  21.3 23.7 %collective-permute-start.13 = (bf16[256,1024]{1,0:T(8,128)(2,1)S(1)}, bf16[256,1024]{1,0:T(8,128)(2,1)S(1)}, u32[]{:S(2)}, u32[]{:S(2)}) collective-permute-start(bf16[256,1024]{1,0:T(8,128)(2,1)S(1)} %get-tuple-element.17), channel_id=1, source_target_pairs={{0,4},{4,0},{8,12},{12,8},{16,20},{20,16},{24,28},{28,24},{1,5},{5... | collective-permute-start | bytes 1572872 | tf_op jit(solution)/shard_map/ppermute | solution.py:71
  37.4 18.7 %collective-permute-start.18 = (bf16[256,1024]{1,0:T(8,128)(2,1)}, bf16[256,1024]{1,0:T(8,128)(2,1)}, u32[]{:S(2)}, u32[]{:S(2)}) collective-permute-start(bf16[256,1024]{1,0:T(8,128)(2,1)} %collective-permute-done.14), channel_id=1, source_target_pairs={{0,4},{4,0},{8,12},{12,8},{16,20},{20,16},{1,5},{5,1},{9,13},{13,9... | collective-permute-start | bytes 1572872 | tf_op jit(solution)/shard_map/ppermute | solution.py:70
  40.8 17.0 %collective-permute-start.20 = (bf16[256,1024]{1,0:T(8,128)(2,1)}, bf16[256,1024]{1,0:T(8,128)(2,1)S(1)}, u32[]{:S(2)}, u32[]{:S(2)}) collective-permute-start(bf16[256,1024]{1,0:T(8,128)(2,1)} %collective-permute-done.14), channel_id=1, source_target_pairs={{8,0},{12,4},{16,8},{20,12},{9,1},{13,5},{17,9},{21,13},{10,2},{14... | collective-permute-start | bytes 1572872 | tf_op jit(solution)/shard_map/ppermute | solution.py:69
  42.1 18.2 %collective-permute-start.19 = (bf16[256,1024]{1,0:T(8,128)(2,1)S(1)}, bf16[256,1024]{1,0:T(8,128)(2,1)}, u32[]{:S(2)}, u32[]{:S(2)}) collective-permute-start(bf16[256,1024]{1,0:T(8,128)(2,1)S(1)} %collective-permute-done.17), channel_id=1, source_target_pairs={{24,28},{28,24},{25,29},{29,25},{26,30},{30,26},{27,31},{31,27}} | collective-permute-start | bytes 1572872 | tf_op jit(solution)/shard_map/ppermute | solution.py:70
  43.6 60.9 %collective-permute-start.1 = (bf16[256,1024]{1,0:T(8,128)(2,1)}, bf16[256,1024]{1,0:T(8,128)(2,1)}, u32[]{:S(2)}, u32[]{:S(2)}) collective-permute-start(bf16[256,1024]{1,0:T(8,128)(2,1)} %get-tuple-element.20), channel_id=1, source_target_pairs={{8,0},{12,4},{16,8},{20,12},{24,16},{28,20},{9,1},{13,5},{17,9},{2... | collective-permute-start | bytes 1572872 | tf_op jit(solution)/shard_map/ppermute | solution.py:69
  45.0 19.7 %collective-permute-start.2 = (bf16[256,1024]{1,0:T(8,128)(2,1)}, bf16[256,1024]{1,0:T(8,128)(2,1)}, u32[]{:S(2)}, u32[]{:S(2)}) collective-permute-start(bf16[256,1024]{1,0:T(8,128)(2,1)} %get-tuple-element.20), channel_id=1, source_target_pairs={{0,8},{4,12},{8,16},{12,20},{16,24},{20,28},{1,9},{5,13},{9,17},{1... | collective-permute-start | bytes 1572872 | tf_op jit(solution)/shard_map/ppermute | solution.py:69
  56.1 34.5 %copy-start = (bf16[512,1024]{1,0:T(8,128)(2,1)S(1)}, bf16[512,1024]{1,0:T(8,128)(2,1)}, u32[]{:S(2)}) copy-start(bf16[512,1024]{1,0:T(8,128)(2,1)} %param.4) | copy-start | bytes 3145732
  56.1 34.5 %copy-start.11 = (f32[1024]{0:T(1024)S(1)}, f32[1024]{0:T(1024)}, u32[]{:S(2)}) copy-start(f32[1024]{0:T(1024)} %param.6) | copy-start | bytes 12292
  56.1 23.3 %collective-permute-start.22 = (bf16[256,1024]{1,0:T(8,128)(2,1)S(1)}, bf16[256,1024]{1,0:T(8,128)(2,1)S(1)}, u32[]{:S(2)}, u32[]{:S(2)}) collective-permute-start(bf16[256,1024]{1,0:T(8,128)(2,1)S(1)} %collective-permute-done.16), channel_id=1, source_target_pairs={{16,20},{20,16},{24,28},{28,24},{17,21},{21,17},{25,29},{29,25},{1... | collective-permute-start | bytes 1572872 | tf_op jit(solution)/shard_map/ppermute | solution.py:70
  57.7 11.1 %collective-permute-start.21 = (bf16[256,1024]{1,0:T(8,128)(2,1)S(1)}, bf16[256,1024]{1,0:T(8,128)(2,1)S(1)}, u32[]{:S(2)}, u32[]{:S(2)}) collective-permute-start(bf16[256,1024]{1,0:T(8,128)(2,1)S(1)} %collective-permute-done.20), channel_id=1, source_target_pairs={{0,4},{4,0},{8,12},{12,8},{1,5},{5,1},{9,13},{13,9},{2,6},{6,2},{1... | collective-permute-start | bytes 1572872 | tf_op jit(solution)/shard_map/ppermute | solution.py:70
  60.3 16.6 %collective-permute-start.23 = (bf16[256,1024]{1,0:T(8,128)(2,1)S(1)}, bf16[256,1024]{1,0:T(8,128)(2,1)S(1)}, u32[]{:S(2)}, u32[]{:S(2)}) collective-permute-start(bf16[256,1024]{1,0:T(8,128)(2,1)S(1)} %collective-permute-done.20), channel_id=1, source_target_pairs={{8,0},{12,4},{9,1},{13,5},{10,2},{14,6},{11,3},{15,7}} | collective-permute-start | bytes 1572872 | tf_op jit(solution)/shard_map/ppermute | solution.py:69
  64.7 16.7 %collective-permute-start.25 = (bf16[256,1024]{1,0:T(8,128)(2,1)S(1)}, bf16[256,1024]{1,0:T(8,128)(2,1)S(1)}, u32[]{:S(2)}, u32[]{:S(2)}) collective-permute-start(bf16[256,1024]{1,0:T(8,128)(2,1)S(1)} %collective-permute-done.15), channel_id=1, source_target_pairs={{8,12},{12,8},{16,20},{20,16},{24,28},{28,24},{9,13},{13,9},{17,21... | collective-permute-start | bytes 1572872 | tf_op jit(solution)/shard_map/ppermute | solution.py:70
  68.8 37.1 %collective-permute-start.3 = (bf16[256,1024]{1,0:T(8,128)(2,1)}, bf16[256,1024]{1,0:T(8,128)(2,1)}, u32[]{:S(2)}, u32[]{:S(2)}) collective-permute-start(bf16[256,1024]{1,0:T(8,128)(2,1)} %collective-permute-done.2), channel_id=1, source_target_pairs={{8,16},{12,20},{16,24},{20,28},{9,17},{13,21},{17,25},{21,29},{10,... | collective-permute-start | bytes 1572872 | tf_op jit(solution)/shard_map/ppermute | solution.py:69
  76.9 12.6 %collective-permute-start.24 = (bf16[256,1024]{1,0:T(8,128)(2,1)S(1)}, bf16[256,1024]{1,0:T(8,128)(2,1)S(1)}, u32[]{:S(2)}, u32[]{:S(2)}) collective-permute-start(bf16[256,1024]{1,0:T(8,128)(2,1)S(1)} %collective-permute-done.23), channel_id=1, source_target_pairs={{0,4},{4,0},{1,5},{5,1},{2,6},{6,2},{3,7},{7,3}} | collective-permute-start | bytes 1572872 | tf_op jit(solution)/shard_map/ppermute | solution.py:70
  93.6 29.3 %collective-permute-start.27 = (f32[512,512]{1,0:T(8,128)}, f32[512,512]{1,0:T(8,128)}, u32[]{:S(2)}, u32[]{:S(2)}) collective-permute-start(f32[512,512]{1,0:T(8,128)} %fusion.34), channel_id=1, source_target_pairs={{0,1},{1,0},{2,3},{3,2},{4,5},{5,4},{6,7},{7,6},{8,9},{9,8},{10,11... | collective-permute-start | bytes 3145736 | tf_op jit(solution)/shard_map/ppermute | solution.py:149
  93.6 21.5 %collective-permute-start = (bf16[256,1024]{1,0:T(8,128)(2,1)}, bf16[256,1024]{1,0:T(8,128)(2,1)}, u32[]{:S(2)}, u32[]{:S(2)}) collective-permute-start(bf16[256,1024]{1,0:T(8,128)(2,1)} %get-tuple-element.20), channel_id=1, source_target_pairs={{0,4},{4,0},{8,12},{12,8},{16,20},{20,16},{24,28},{28,24},{1,5},{5... | collective-permute-start | bytes 1572872 | tf_op jit(solution)/shard_map/ppermute | solution.py:71
  104.5 16.4 %collective-permute-start.7 = (bf16[256,1024]{1,0:T(8,128)(2,1)}, bf16[256,1024]{1,0:T(8,128)(2,1)}, u32[]{:S(2)}, u32[]{:S(2)}) collective-permute-start(bf16[256,1024]{1,0:T(8,128)(2,1)} %collective-permute-done.1), channel_id=1, source_target_pairs={{8,0},{12,4},{16,8},{20,12},{9,1},{13,5},{17,9},{21,13},{10,2},{14... | collective-permute-start | bytes 1572872 | tf_op jit(solution)/shard_map/ppermute | solution.py:69
  105.9 16.2 %collective-permute-start.4 = (bf16[256,1024]{1,0:T(8,128)(2,1)}, bf16[256,1024]{1,0:T(8,128)(2,1)}, u32[]{:S(2)}, u32[]{:S(2)}) collective-permute-start(bf16[256,1024]{1,0:T(8,128)(2,1)} %collective-permute-done.3), channel_id=1, source_target_pairs={{16,24},{20,28},{17,25},{21,29},{18,26},{22,30},{19,27},{23,31}} | collective-permute-start | bytes 1572872 | tf_op jit(solution)/shard_map/ppermute | solution.py:69
  110.3 27.2 %collective-permute-start.26 = (f32[512,512]{1,0:T(8,128)}, f32[512,512]{1,0:T(8,128)}, u32[]{:S(2)}, u32[]{:S(2)}) collective-permute-start(f32[512,512]{1,0:T(8,128)} %fusion.37), channel_id=1, source_target_pairs={{0,1},{1,0},{2,3},{3,2},{4,5},{5,4},{6,7},{7,6},{8,9},{9,8},{10,11... | collective-permute-start | bytes 3145736 | tf_op jit(solution)/shard_map/ppermute | solution.py:149
  115.1 25.4 %copy-start.4 = (f32[64,8,2,256]{3,1,2,0:T(8,128)S(1)}, f32[64,8,2,256]{3,1,2,0:T(8,128)}, u32[]{:S(2)}) copy-start(f32[64,8,2,256]{3,1,2,0:T(8,128)} %copy.5) | copy-start | bytes 3145732
  115.1 16.3 %collective-permute-start.5 = (bf16[256,1024]{1,0:T(8,128)(2,1)}, bf16[256,1024]{1,0:T(8,128)(2,1)S(1)}, u32[]{:S(2)}, u32[]{:S(2)}) collective-permute-start(bf16[256,1024]{1,0:T(8,128)(2,1)} %collective-permute-done.1), channel_id=1, source_target_pairs={{0,4},{4,0},{8,12},{12,8},{16,20},{20,16},{1,5},{5,1},{9,13},{13,9... | collective-permute-start | bytes 1572872 | tf_op jit(solution)/shard_map/ppermute | solution.py:70
  120.8 15.9 %collective-permute-start.10 = (bf16[256,1024]{1,0:T(8,128)(2,1)}, bf16[256,1024]{1,0:T(8,128)(2,1)S(1)}, u32[]{:S(2)}, u32[]{:S(2)}) collective-permute-start(bf16[256,1024]{1,0:T(8,128)(2,1)} %collective-permute-done.7), channel_id=1, source_target_pairs={{8,0},{12,4},{9,1},{13,5},{10,2},{14,6},{11,3},{15,7}} | collective-permute-start | bytes 1572872 | tf_op jit(solution)/shard_map/ppermute | solution.py:69
  122.1 10.0 %collective-permute-start.6 = (bf16[256,1024]{1,0:T(8,128)(2,1)}, bf16[256,1024]{1,0:T(8,128)(2,1)S(1)}, u32[]{:S(2)}, u32[]{:S(2)}) collective-permute-start(bf16[256,1024]{1,0:T(8,128)(2,1)} %collective-permute-done.4), channel_id=1, source_target_pairs={{24,28},{28,24},{25,29},{29,25},{26,30},{30,26},{27,31},{31,27}} | collective-permute-start | bytes 1572872 | tf_op jit(solution)/shard_map/ppermute | solution.py:70
  125.1 15.3 %collective-permute-start.28 = (bf16[512,512]{1,0:T(8,128)(2,1)S(1)}, bf16[512,512]{1,0:T(8,128)(2,1)S(1)}, u32[]{:S(2)}, u32[]{:S(2)}) collective-permute-start(bf16[512,512]{1,0:T(8,128)(2,1)S(1)} %fusion.6), channel_id=1, source_target_pairs={{0,2},{1,3},{2,0},{3,1},{4,6},{5,7},{6,4},{7,5},{8,10},{9,11},{10,... | collective-permute-start | bytes 1572872 | tf_op jit(solution)/shard_map/ppermute | solution.py:152
  131.4 24.7 %collective-permute-start.12 = (bf16[256,1024]{1,0:T(8,128)(2,1)}, bf16[256,1024]{1,0:T(8,128)(2,1)S(1)}, u32[]{:S(2)}, u32[]{:S(2)}) collective-permute-start(bf16[256,1024]{1,0:T(8,128)(2,1)} %collective-permute-done.2), channel_id=1, source_target_pairs={{8,12},{12,8},{16,20},{20,16},{24,28},{28,24},{9,13},{13,9},{17,21... | collective-permute-start | bytes 1572872 | tf_op jit(solution)/shard_map/ppermute | solution.py:70
  132.1 17.0 %collective-permute-start.8 = (bf16[256,1024]{1,0:T(8,128)(2,1)}, bf16[256,1024]{1,0:T(8,128)(2,1)S(1)}, u32[]{:S(2)}, u32[]{:S(2)}) collective-permute-start(bf16[256,1024]{1,0:T(8,128)(2,1)} %collective-permute-done.7), channel_id=1, source_target_pairs={{0,4},{4,0},{8,12},{12,8},{1,5},{5,1},{9,13},{13,9},{2,6},{6,2},{1... | collective-permute-start | bytes 1572872 | tf_op jit(solution)/shard_map/ppermute | solution.py:70
  136.7 12.4 %collective-permute-start.9 = (bf16[256,1024]{1,0:T(8,128)(2,1)}, bf16[256,1024]{1,0:T(8,128)(2,1)S(1)}, u32[]{:S(2)}, u32[]{:S(2)}) collective-permute-start(bf16[256,1024]{1,0:T(8,128)(2,1)} %collective-permute-done.3), channel_id=1, source_target_pairs={{16,20},{20,16},{24,28},{28,24},{17,21},{21,17},{25,29},{29,25},{1... | collective-permute-start | bytes 1572872 | tf_op jit(solution)/shard_map/ppermute | solution.py:70
  137.4 21.3 %collective-permute-start.11 = (bf16[256,1024]{1,0:T(8,128)(2,1)S(1)}, bf16[256,1024]{1,0:T(8,128)(2,1)S(1)}, u32[]{:S(2)}, u32[]{:S(2)}) collective-permute-start(bf16[256,1024]{1,0:T(8,128)(2,1)S(1)} %collective-permute-done.10), channel_id=1, source_target_pairs={{0,4},{4,0},{1,5},{5,1},{2,6},{6,2},{3,7},{7,3}} | collective-permute-start | bytes 1572872 | tf_op jit(solution)/shard_map/ppermute | solution.py:70
  142.9 20.7 %copy-start.6 = (bf16[512,512]{1,0:T(8,128)(2,1)}, bf16[512,512]{1,0:T(8,128)(2,1)S(1)}, u32[]{:S(2)}) copy-start(bf16[512,512]{1,0:T(8,128)(2,1)S(1)} %fusion.9) | copy-start | bytes 1572868
  142.9 12.2 %collective-permute-start.29 = (bf16[512,512]{1,0:T(8,128)(2,1)S(1)}, bf16[512,512]{1,0:T(8,128)(2,1)S(1)}, u32[]{:S(2)}, u32[]{:S(2)}) collective-permute-start(bf16[512,512]{1,0:T(8,128)(2,1)S(1)} %fusion.9), channel_id=1, source_target_pairs={{0,2},{1,3},{2,0},{3,1},{4,6},{5,7},{6,4},{7,5},{8,10},{9,11},{10,... | collective-permute-start | bytes 1572872 | tf_op jit(solution)/shard_map/ppermute | solution.py:161
  150.1 9.7 %collective-permute-start.30 = (bf16[512,512]{1,0:T(8,128)(2,1)S(1)}, bf16[512,512]{1,0:T(8,128)(2,1)S(1)}, u32[]{:S(2)}, u32[]{:S(2)}) collective-permute-start(bf16[512,512]{1,0:T(8,128)(2,1)S(1)} %fusion.9), channel_id=1, source_target_pairs={{0,1},{1,0},{2,3},{3,2},{4,5},{5,4},{6,7},{7,6},{8,9},{9,8},{10,11... | collective-permute-start | bytes 1572872 | tf_op jit(solution)/shard_map/ppermute | solution.py:162
  155.1 5.5 %collective-permute-start.31 = (bf16[512,512]{1,0:T(8,128)(2,1)S(1)}, bf16[512,512]{1,0:T(8,128)(2,1)}, u32[]{:S(2)}, u32[]{:S(2)}) collective-permute-start(bf16[512,512]{1,0:T(8,128)(2,1)S(1)} %collective-permute-done.29), channel_id=1, source_target_pairs={{0,1},{1,0},{2,3},{3,2},{4,5},{5,4},{6,7},{7,6},{8,9},{9,8},{10,11... | collective-permute-start | bytes 1572872 | tf_op jit(solution)/shard_map/ppermute | solution.py:162
  163.5 10.4 %collective-permute-start.33 = (f32[512,512]{1,0:T(8,128)}, f32[512,512]{1,0:T(8,128)}, u32[]{:S(2)}, u32[]{:S(2)}) collective-permute-start(f32[512,512]{1,0:T(8,128)} %fusion.18), channel_id=1, source_target_pairs={{0,1},{1,0},{2,3},{3,2},{4,5},{5,4},{6,7},{7,6},{8,9},{9,8},{10,11... | collective-permute-start | bytes 3145736 | tf_op jit(solution)/shard_map/ppermute | solution.py:149
  172.6 8.1 %collective-permute-start.32 = (f32[512,512]{1,0:T(8,128)}, f32[512,512]{1,0:T(8,128)}, u32[]{:S(2)}, u32[]{:S(2)}) collective-permute-start(f32[512,512]{1,0:T(8,128)} %fusion.21), channel_id=1, source_target_pairs={{0,1},{1,0},{2,3},{3,2},{4,5},{5,4},{6,7},{7,6},{8,9},{9,8},{10,11... | collective-permute-start | bytes 3145736 | tf_op jit(solution)/shard_map/ppermute | solution.py:149
  173.9 6.1 %copy-start.2 = (bf16[2048,1024]{1,0:T(8,128)(2,1)S(1)}, bf16[2048,1024]{1,0:T(8,128)(2,1)}, u32[]{:S(2)}) copy-start(bf16[2048,1024]{1,0:T(8,128)(2,1)} %select_dynamic-update-slice_fusion) | copy-start | bytes 12582916
  176.4 13.9 %copy-start.1 = (bf16[2048,1024]{1,0:T(8,128)(2,1)S(1)}, bf16[2048,1024]{1,0:T(8,128)(2,1)}, u32[]{:S(2)}) copy-start(bf16[2048,1024]{1,0:T(8,128)(2,1)} %select_dynamic-update-slice_fusion.6) | copy-start | bytes 12582916
  176.4 13.9 %collective-permute-start.34 = (bf16[512,512]{1,0:T(8,128)(2,1)S(1)}, bf16[512,512]{1,0:T(8,128)(2,1)S(1)}, u32[]{:S(2)}, u32[]{:S(2)}) collective-permute-start(bf16[512,512]{1,0:T(8,128)(2,1)S(1)} %fusion.7), channel_id=1, source_target_pairs={{0,2},{1,3},{2,0},{3,1},{4,6},{5,7},{6,4},{7,5},{8,10},{9,11},{10,... | collective-permute-start | bytes 1572872 | tf_op jit(solution)/shard_map/ppermute | solution.py:152
  180.0 13.9 %copy-start.9 = (bf16[512,512]{1,0:T(8,128)(2,1)S(1)}, bf16[512,512]{1,0:T(8,128)(2,1)}, u32[]{:S(2)}) copy-start(bf16[512,512]{1,0:T(8,128)(2,1)} %copy-done.8) | copy-start | bytes 1572868
  192.4 13.1 %collective-permute-start.35 = (bf16[512,512]{1,0:T(8,128)(2,1)S(1)}, bf16[512,512]{1,0:T(8,128)(2,1)S(1)}, u32[]{:S(2)}, u32[]{:S(2)}) collective-permute-start(bf16[512,512]{1,0:T(8,128)(2,1)S(1)} %fusion.8), channel_id=1, source_target_pairs={{0,2},{1,3},{2,0},{3,1},{4,6},{5,7},{6,4},{7,5},{8,10},{9,11},{10,... | collective-permute-start | bytes 1572872 | tf_op jit(solution)/shard_map/ppermute | solution.py:161
  194.6 11.6 %collective-permute-start.36 = (bf16[512,512]{1,0:T(8,128)(2,1)S(1)}, bf16[512,512]{1,0:T(8,128)(2,1)S(1)}, u32[]{:S(2)}, u32[]{:S(2)}) collective-permute-start(bf16[512,512]{1,0:T(8,128)(2,1)S(1)} %fusion.8), channel_id=1, source_target_pairs={{0,1},{1,0},{2,3},{3,2},{4,5},{5,4},{6,7},{7,6},{8,9},{9,8},{10,11... | collective-permute-start | bytes 1572872 | tf_op jit(solution)/shard_map/ppermute | solution.py:162
  205.4 1.9 collective-permute-start.37
  210.5 3.7 %collective-permute-start.38 = (f32[1024]{0:T(1024)S(1)}, f32[1024]{0:T(1024)S(1)}, u32[]{:S(2)}, u32[]{:S(2)}) collective-permute-start(f32[1024]{0:T(1024)S(1)} %fusion.1), channel_id=1, source_target_pairs={{0,4},{4,0},{8,12},{12,8},{16,20},{20,16},{24,28},{28,24},{1,5},{5... | collective-permute-start | bytes 12296 | tf_op jit(solution)/shard_map/ppermute | solution.py:85
  214.2 7.7 %collective-permute-start.39 = (f32[1024]{0:T(1024)S(1)}, f32[1024]{0:T(1024)S(1)}, u32[]{:S(2)}, u32[]{:S(2)}) collective-permute-start(f32[1024]{0:T(1024)S(1)} %add.213), channel_id=1, source_target_pairs={{0,8},{4,12},{8,0},{12,4},{16,24},{20,28},{24,16},{28,20},{1,9},{5... | collective-permute-start | bytes 12296 | tf_op jit(solution)/shard_map/ppermute | solution.py:85
  221.9 4.5 %collective-permute-start.40 = (f32[1024]{0:T(1024)S(1)}, f32[1024]{0:T(1024)S(1)}, u32[]{:S(2)}, u32[]{:S(2)}) collective-permute-start(f32[1024]{0:T(1024)S(1)} %add.214), channel_id=1, source_target_pairs={{0,16},{4,20},{8,24},{12,28},{16,0},{20,4},{24,8},{28,12},{1,17},{... | collective-permute-start | bytes 12296 | tf_op jit(solution)/shard_map/ppermute | solution.py:85
  (5 other events, 21.2 us)

commit v5 on v4

--- a/solution.py
+++ b/solution.py
@@ -68,12 +68,15 @@
                     pairs.extend(along(p, p + sign))
             cur = lax.ppermute(cur, "src", pairs)
             got[(sign, s)] = (cur, lax.ppermute(cur, "src", cross(sign, s)))
+    first = ib == 0
     planes = [(block, lax.ppermute(block, "src", swap))]
     for k in range(1, na):
         up, down = got[(-1, k)], got[(1, na - k)]
         ok = ia + k < na
         planes.append(tuple(jnp.where(ok, u, d) for u, d in zip(up, down)))
-    return jnp.concatenate([x for pl in planes for x in pl], axis=0)
+    return jnp.concatenate(
+        [x for a, b in planes for x in (jnp.where(first, a, b), jnp.where(first, b, a))], axis=0
+    )
 
 
 def _sum_over_src(v):
@@ -112,21 +115,14 @@
     if grid is not None and grid[0] == t:
         na = grid[1]
         ia = lax.axis_index("src") // t
-        flip = lax.axis_index("src") % t == 1
 
         def rel(blk):
             return (blk - ia) % na
-
-        def order(w):
-            return jnp.where(flip, w[:, ::-1], w)
     else:
         grid = None
 
         def rel(blk):
             return blk
-
-        def order(w):
-            return w
     def gather(c):
         return _gather_src(adjoint_voxel_field[c * r:(c + 1) * r], grid)
 
@@ -141,25 +137,23 @@
                 preferred_element_type=jnp.float32,
             )
 
-        halves = []
-        for k in range(m):
-            g = (q + k) % m
-            keep = pblock(2 * g + par)
-            send = pblock(2 * g + 1 - par)
-            halves.append(keep + lax.ppermute(send, "vox", pair))
+        keeps = [pblock(2 * ((q + k) % m) + par) for k in range(m)]
+        sends = [pblock(2 * ((q + k) % m) + 1 - par) for k in range(m)]
+        halves = [a + b for a, b in zip(keeps, lax.ppermute(tuple(sends), "vox", pair))]
         share = halves[0]
         for k in range(1, m):
             share = share + lax.ppermute(
                 halves[k].astype(jnp.bfloat16), "vox", chip_perm(k)
             ).astype(jnp.float32)
 
-        w_c = order(weight[:, :, c * r:(c + 1) * r]).reshape(sl, n)
+        w_c = weight[:, :, c * r:(c + 1) * r].reshape(sl, n)
         wt = (w_c * share).astype(jnp.bfloat16)
 
         got = [(me, wt)]
         for k in range(1, m):
             got.append((2 * ((q - k) % m) + par, lax.ppermute(wt, "vox", chip_perm(k))))
-        got = got + [(blk ^ 1, lax.ppermute(w, "vox", pair)) for blk, w in got]
+        mine = lax.ppermute(tuple(w for _, w in got), "vox", pair)
+        got = got + [(blk ^ 1, w) for (blk, _), w in zip(got, mine)]
         if c + 1 < chunks:
             nxt, ws = lax.optimization_barrier((gather(c + 1), [w for _, w in got]))
             got = [(blk, w) for (blk, _), w in zip(got, ws)]

time: 228 us -> 217 us (0.952)
  waiting for transfers between devices: 86.3 us -> 106 us
  local copies, waits for them, and re-layouts: 24.8 us -> 10.7 us
  other arithmetic: 19.9 us -> 10.8 us
  matrix products: 29.9 us -> 21.1 us
    ppermute x12, waiting for transfers between devices: 33.7 us -> 49.2 us  [_gather_src(): cur = lax.ppermute(cur, 'src', pairs)]
    rev x2 -> x0, local copies, waits for them, and re-layouts: 12 us -> none  [order(): return jnp.where(flip, w[:, ::-1], w)]
    dot_general x8, matrix products: 21.1 us -> 13.4 us  [pblock(): lax.dot_general(scaled, _rows(adj, rel(blk), n), (((1,), (1,)), ((), ()))...]
    ppermute x2, waiting for transfers between devices: 15 us -> 20.6 us  [per_device(): got.append((2 * ((q - k) % m) + par, lax.ppermute(wt, 'vox', chip_perm(k))))]
    unnamed x10 -> x14, other arithmetic: 14.2 us -> 9.45 us
    select_n x2 -> x0, other arithmetic: 2.98 us -> none  [order(): return jnp.where(flip, w[:, ::-1], w)]
    ppermute x12, waiting for transfers between devices: 19.4 us -> 16.8 us  [_gather_src(): got[sign, s] = (cur, lax.ppermute(cur, 'src', cross(sign, s)))]
    ppermute x12, starting transfers between devices: 25.3 us -> 27.8 us  [_gather_src(): cur = lax.ppermute(cur, 'src', pairs)]
  transfers between devices with their start and end apart: 41 -> 41, of which waited for: 18 -> 16; matrix products, arithmetic and copies ran while one was open for 28% -> 15% of each run, Pallas kernels for 0% -> 0%
where the time goes in v5:
time: 217 us; the launch traced here: 216 us
  waiting for transfers between devices  106 us (49%)
  starting transfers between devices  66.8 us (31%)
  matrix products  21.1 us (10%)
  other arithmetic  10.8 us (5%)
  local copies, waits for them, and re-layouts  10.7 us (5%)
    ppermute x12, waiting for transfers between devices, _gather_src(): cur = lax.ppermute(cur, 'src', pairs)  49.2 us
    ppermute x12, starting transfers between devices, _gather_src(): cur = lax.ppermute(cur, 'src', pairs)  27.8 us
    ppermute x12, starting transfers between devices, _gather_src(): got[sign, s] = (cur, lax.ppermute(cur, 'src', cross(sign, s)))  21 us
    ppermute x2, waiting for transfers between devices, per_device(): got.append((2 * ((q - k) % m) + par, lax.ppermute(wt, 'vox', chip_perm(k))))  20.6 us
    ppermute x12, waiting for transfers between devices, _gather_src(): got[sign, s] = (cur, lax.ppermute(cur, 'src', cross(sign, s)))  16.8 us
    dot_general x8, matrix products, pblock(): lax.dot_general(scaled, _rows(adj, rel(blk), n), (((1,), (1,)), ((), ()))...  13.4 us
    ppermute x2, waiting for transfers between devices, per_device(): lax.ppermute(halves[k].astype(jnp.bfloat16), 'vox', chip_perm(k))  11.3 us
    unnamed x14, other arithmetic  9.45 us
  transfers between devices with their start and end apart: 41, of which 16 were waited for; matrix products, arithmetic and copies ran while one was open for 15% of the time, Pallas kernels for 0%

profile of v5, /device:TPU:0, one launch (start us, length us, event | category | flops | bytes accessed | tf_op | source)
XLA Modules:
  0.0 216.3 jit_solution(6511687324726270654)
XLA Ops:
  0.0 2.0 slice.14
  2.0 4.9 %collective-permute-start.15 = (bf16[256,1024]{1,0:T(8,128)(2,1)}, bf16[256,1024]{1,0:T(8,128)(2,1)S(1)}, u32[]{:S(2)}, u32[]{:S(2)}) collective-permute-start(bf16[256,1024]{1,0:T(8,128)(2,1)} %slice.14), channel_id=1, source_target_pairs={{0,8},{4,12},{8,16},{12,20},{16,24},{20,28},{1,9},{5,13},{9,17},{1... | collective-permute-start | bytes 1572872 | tf_op jit(solution)/shard_map/ppermute | solution.py:69
  6.9 11.4 %collective-permute-done.15 = bf16[256,1024]{1,0:T(8,128)(2,1)S(1)} collective-permute-done((bf16[256,1024]{1,0:T(8,128)(2,1)}, bf16[256,1024]{1,0:T(8,128)(2,1)S(1)}, u32[]{:S(2)}, u32[]{:S(2)}) %collective-permute-start.15) | collective-permute-done | bytes 524320 | tf_op jit(solution)/shard_map/ppermute | solution.py:69
  19.1 1.3 collective-permute-start.14
  21.1 1.6 collective-permute-start.13
  22.7 4.0 %reshape.10 = f32[512,2,512]{2,1,0:T(2,128)} reshape(f32[512,1024]{1,0:T(8,128)} %param.7) | data formatting | bytes 4194304 | tf_op jit(solution)/shard_map/reshape | solution.py:114
  26.7 10.5 %collective-permute-done.14 = bf16[256,1024]{1,0:T(8,128)(2,1)S(1)} collective-permute-done((bf16[256,1024]{1,0:T(8,128)(2,1)}, bf16[256,1024]{1,0:T(8,128)(2,1)S(1)}, u32[]{:S(2)}, u32[]{:S(2)}) %collective-permute-start.14) | collective-permute-done | bytes 524320 | tf_op jit(solution)/shard_map/ppermute | solution.py:69
  37.1 3.4 %collective-permute-start.18 = (bf16[256,1024]{1,0:T(8,128)(2,1)S(1)}, bf16[256,1024]{1,0:T(8,128)(2,1)S(1)}, u32[]{:S(2)}, u32[]{:S(2)}) collective-permute-start(bf16[256,1024]{1,0:T(8,128)(2,1)S(1)} %collective-permute-done.14), channel_id=1, source_target_pairs={{0,4},{4,0},{8,12},{12,8},{16,20},{20,16},{1,5},{5,1},{9,13},{13,9... | collective-permute-start | bytes 1572872 | tf_op jit(solution)/shard_map/ppermute | solution.py:70
  40.6 1.3 collective-permute-start.20
  42.8 2.1 select_dynamic-update-slice_fusion.6
  45.4 11.6 %collective-permute-start.2 = (bf16[256,1024]{1,0:T(8,128)(2,1)}, bf16[256,1024]{1,0:T(8,128)(2,1)}, u32[]{:S(2)}, u32[]{:S(2)}) collective-permute-start(bf16[256,1024]{1,0:T(8,128)(2,1)} %get-tuple-element.18), channel_id=1, source_target_pairs={{0,8},{4,12},{8,16},{12,20},{16,24},{20,28},{1,9},{5,13},{9,17},{1... | collective-permute-start | bytes 1572872 | tf_op jit(solution)/shard_map/ppermute | solution.py:69
  57.7 2.4 %collective-permute-start.21 = (bf16[256,1024]{1,0:T(8,128)(2,1)S(1)}, bf16[256,1024]{1,0:T(8,128)(2,1)S(1)}, u32[]{:S(2)}, u32[]{:S(2)}) collective-permute-start(bf16[256,1024]{1,0:T(8,128)(2,1)S(1)} %collective-permute-done.20), channel_id=1, source_target_pairs={{0,4},{4,0},{8,12},{12,8},{1,5},{5,1},{9,13},{13,9},{2,6},{6,2},{1... | collective-permute-start | bytes 1572872 | tf_op jit(solution)/shard_map/ppermute | solution.py:70
  60.1 1.3 collective-permute-start.23
  63.2 1.3 collective-permute-start.1
  64.5 8.9 %collective-permute-done.21 = bf16[256,1024]{1,0:T(8,128)(2,1)S(1)} collective-permute-done((bf16[256,1024]{1,0:T(8,128)(2,1)S(1)}, bf16[256,1024]{1,0:T(8,128)(2,1)S(1)}, u32[]{:S(2)}, u32[]{:S(2)}) %collective-permute-start.21) | collective-permute-done | bytes 524320 | tf_op jit(solution)/shard_map/ppermute | solution.py:70
  74.1 1.5 collective-permute-start.3
  75.5 3.0 %collective-permute-done.23 = bf16[256,1024]{1,0:T(8,128)(2,1)S(1)} collective-permute-done((bf16[256,1024]{1,0:T(8,128)(2,1)S(1)}, bf16[256,1024]{1,0:T(8,128)(2,1)S(1)}, u32[]{:S(2)}, u32[]{:S(2)}) %collective-permute-start.23) | collective-permute-done | bytes 524320 | tf_op jit(solution)/shard_map/ppermute | solution.py:69
  78.6 2.4 %collective-permute-start.24 = (bf16[256,1024]{1,0:T(8,128)(2,1)S(1)}, bf16[256,1024]{1,0:T(8,128)(2,1)S(1)}, u32[]{:S(2)}, u32[]{:S(2)}) collective-permute-start(bf16[256,1024]{1,0:T(8,128)(2,1)S(1)} %collective-permute-done.23), channel_id=1, source_target_pairs={{0,4},{4,0},{1,5},{5,1},{2,6},{6,2},{3,7},{7,3}} | collective-permute-start | bytes 1572872 | tf_op jit(solution)/shard_map/ppermute | solution.py:70
  81.7 7.9 %collective-permute-done.24 = bf16[256,1024]{1,0:T(8,128)(2,1)S(1)} collective-permute-done((bf16[256,1024]{1,0:T(8,128)(2,1)S(1)}, bf16[256,1024]{1,0:T(8,128)(2,1)S(1)}, u32[]{:S(2)}, u32[]{:S(2)}) %collective-permute-start.24) | collective-permute-done | bytes 524320 | tf_op jit(solution)/shard_map/ppermute | solution.py:70
  90.4 2.0 copy-done.5
  92.3 1.7 fusion.31
  95.9 2.7 %collective-permute-start.5 = (bf16[256,1024]{1,0:T(8,128)(2,1)}, bf16[256,1024]{1,0:T(8,128)(2,1)S(1)}, u32[]{:S(2)}, u32[]{:S(2)}) collective-permute-start(bf16[256,1024]{1,0:T(8,128)(2,1)} %collective-permute-done.1), channel_id=1, source_target_pairs={{0,4},{4,0},{8,12},{12,8},{16,20},{20,16},{1,5},{5,1},{9,13},{13,9... | collective-permute-start | bytes 1572872 | tf_op jit(solution)/shard_map/ppermute | solution.py:70
  98.6 1.3 collective-permute-start.7
  100.8 2.0 fusion.34
  105.0 13.4 %collective-permute-done.7 = bf16[256,1024]{1,0:T(8,128)(2,1)S(1)} collective-permute-done((bf16[256,1024]{1,0:T(8,128)(2,1)}, bf16[256,1024]{1,0:T(8,128)(2,1)S(1)}, u32[]{:S(2)}, u32[]{:S(2)}) %collective-permute-start.7) | collective-permute-done | bytes 524320 | tf_op jit(solution)/shard_map/ppermute | solution.py:69
  119.1 2.4 %collective-permute-start.8 = (bf16[256,1024]{1,0:T(8,128)(2,1)S(1)}, bf16[256,1024]{1,0:T(8,128)(2,1)S(1)}, u32[]{:S(2)}, u32[]{:S(2)}) collective-permute-start(bf16[256,1024]{1,0:T(8,128)(2,1)S(1)} %collective-permute-done.7), channel_id=1, source_target_pairs={{0,4},{4,0},{8,12},{12,8},{1,5},{5,1},{9,13},{13,9},{2,6},{6,2},{1... | collective-permute-start | bytes 1572872 | tf_op jit(solution)/shard_map/ppermute | solution.py:70
  121.5 2.0 fusion.6
  123.6 1.3 collective-permute-start.10
  124.9 1.5 collective-permute-start.28
  126.4 1.4 select_dynamic-update-slice_fusion.13
  127.8 1.4 select_dynamic-update-slice_fusion.12
  129.2 9.8 %collective-permute-done.10 = bf16[256,1024]{1,0:T(8,128)(2,1)S(1)} collective-permute-done((bf16[256,1024]{1,0:T(8,128)(2,1)S(1)}, bf16[256,1024]{1,0:T(8,128)(2,1)S(1)}, u32[]{:S(2)}, u32[]{:S(2)}) %collective-permute-start.10) | collective-permute-done | bytes 524320 | tf_op jit(solution)/shard_map/ppermute | solution.py:69
  139.7 3.6 %collective-permute-start.11 = (bf16[256,1024]{1,0:T(8,128)(2,1)S(1)}, bf16[256,1024]{1,0:T(8,128)(2,1)S(1)}, u32[]{:S(2)}, u32[]{:S(2)}) collective-permute-start(bf16[256,1024]{1,0:T(8,128)(2,1)S(1)} %collective-permute-done.10), channel_id=1, source_target_pairs={{0,4},{4,0},{1,5},{5,1},{2,6},{6,2},{3,7},{7,3}} | collective-permute-start | bytes 1572872 | tf_op jit(solution)/shard_map/ppermute | solution.py:70
  144.3 1.6 collective-permute-start.29
  146.6 10.1 %collective-permute-done.29 = bf16[512,512]{1,0:T(8,128)(2,1)S(1)} collective-permute-done((bf16[512,512]{1,0:T(8,128)(2,1)S(1)}, bf16[512,512]{1,0:T(8,128)(2,1)S(1)}, u32[]{:S(2)}, u32[]{:S(2)}) %collective-permute-start.29) | collective-permute-done | bytes 524320 | tf_op jit(solution)/shard_map/ppermute | solution.py:154
  159.5 1.8 fusion.17
  161.9 2.1 fusion.20
  164.2 2.1 fusion.27
  166.3 2.1 fusion.7
  168.4 1.5 collective-permute-start.34
  171.4 11.3 %collective-permute-done.34 = bf16[512,512]{1,0:T(8,128)(2,1)S(1)} collective-permute-done((bf16[512,512]{1,0:T(8,128)(2,1)S(1)}, bf16[512,512]{1,0:T(8,128)(2,1)S(1)}, u32[]{:S(2)}, u32[]{:S(2)}) %collective-permute-start.34) | collective-permute-done | bytes 524320 | tf_op jit(solution)/shard_map/ppermute | solution.py:145
  183.6 1.5 collective-permute-start.35
  186.7 10.5 %collective-permute-done.35 = bf16[512,512]{1,0:T(8,128)(2,1)S(1)} collective-permute-done((bf16[512,512]{1,0:T(8,128)(2,1)S(1)}, bf16[512,512]{1,0:T(8,128)(2,1)S(1)}, u32[]{:S(2)}, u32[]{:S(2)}) %collective-permute-start.35) | collective-permute-done | bytes 524320 | tf_op jit(solution)/shard_map/ppermute | solution.py:154
  200.9 3.1 %collective-permute-done.38 = f32[1024]{0:T(1024)S(1)} collective-permute-done((f32[1024]{0:T(1024)S(1)}, f32[1024]{0:T(1024)S(1)}, u32[]{:S(2)}, u32[]{:S(2)}) %collective-permute-start.38) | collective-permute-done | bytes 4128 | tf_op jit(solution)/shard_map/ppermute | solution.py:88
  204.0 1.5 collective-permute-start.39
  205.5 2.1 collective-permute-done.39
  207.6 6.5 %collective-permute-start.40 = (f32[1024]{0:T(1024)S(1)}, f32[1024]{0:T(1024)S(1)}, u32[]{:S(2)}, u32[]{:S(2)}) collective-permute-start(f32[1024]{0:T(1024)S(1)} %add.221), channel_id=1, source_target_pairs={{0,16},{4,20},{8,24},{12,28},{16,0},{20,4},{24,8},{28,12},{1,17},{... | collective-permute-start | bytes 12296 | tf_op jit(solution)/shard_map/ppermute | solution.py:88
  214.1 1.6 collective-permute-done.40
  (110 shorter events, 26.9 us)
Async XLA Ops:
  0.0 42.6 %copy-start = (bf16[512,1024]{1,0:T(8,128)(2,1)S(1)}, bf16[512,1024]{1,0:T(8,128)(2,1)}, u32[]{:S(2)}) copy-start(bf16[512,1024]{1,0:T(8,128)(2,1)} %param.5) | copy-start | bytes 3145732
  2.0 16.4 %collective-permute-start.15 = (bf16[256,1024]{1,0:T(8,128)(2,1)}, bf16[256,1024]{1,0:T(8,128)(2,1)S(1)}, u32[]{:S(2)}, u32[]{:S(2)}) collective-permute-start(bf16[256,1024]{1,0:T(8,128)(2,1)} %slice.14), channel_id=1, source_target_pairs={{0,8},{4,12},{8,16},{12,20},{16,24},{20,28},{1,9},{5,13},{9,17},{1... | collective-permute-start | bytes 1572872 | tf_op jit(solution)/shard_map/ppermute | solution.py:69
  18.4 2.0 collective-permute-start.16
  19.1 18.1 %collective-permute-start.14 = (bf16[256,1024]{1,0:T(8,128)(2,1)}, bf16[256,1024]{1,0:T(8,128)(2,1)S(1)}, u32[]{:S(2)}, u32[]{:S(2)}) collective-permute-start(bf16[256,1024]{1,0:T(8,128)(2,1)} %slice.14), channel_id=1, source_target_pairs={{8,0},{12,4},{16,8},{20,12},{24,16},{28,20},{9,1},{13,5},{17,9},{2... | collective-permute-start | bytes 1572872 | tf_op jit(solution)/shard_map/ppermute | solution.py:69
  20.4 21.5 %collective-permute-start.17 = (bf16[256,1024]{1,0:T(8,128)(2,1)S(1)}, bf16[256,1024]{1,0:T(8,128)(2,1)S(1)}, u32[]{:S(2)}, u32[]{:S(2)}) collective-permute-start(bf16[256,1024]{1,0:T(8,128)(2,1)S(1)} %collective-permute-done.16), channel_id=1, source_target_pairs={{16,24},{20,28},{17,25},{21,29},{18,26},{22,30},{19,27},{23,31}} | collective-permute-start | bytes 1572872 | tf_op jit(solution)/shard_map/ppermute | solution.py:69
  21.1 21.5 %collective-permute-start.13 = (bf16[256,1024]{1,0:T(8,128)(2,1)}, bf16[256,1024]{1,0:T(8,128)(2,1)}, u32[]{:S(2)}, u32[]{:S(2)}) collective-permute-start(bf16[256,1024]{1,0:T(8,128)(2,1)} %slice.14), channel_id=1, source_target_pairs={{0,4},{4,0},{8,12},{12,8},{16,20},{20,16},{24,28},{28,24},{1,5},{5... | collective-permute-start | bytes 1572872 | tf_op jit(solution)/shard_map/ppermute | solution.py:72
  37.1 19.9 %collective-permute-start.18 = (bf16[256,1024]{1,0:T(8,128)(2,1)S(1)}, bf16[256,1024]{1,0:T(8,128)(2,1)S(1)}, u32[]{:S(2)}, u32[]{:S(2)}) collective-permute-start(bf16[256,1024]{1,0:T(8,128)(2,1)S(1)} %collective-permute-done.14), channel_id=1, source_target_pairs={{0,4},{4,0},{8,12},{12,8},{16,20},{20,16},{1,5},{5,1},{9,13},{13,9... | collective-permute-start | bytes 1572872 | tf_op jit(solution)/shard_map/ppermute | solution.py:70
  40.6 17.1 %collective-permute-start.20 = (bf16[256,1024]{1,0:T(8,128)(2,1)S(1)}, bf16[256,1024]{1,0:T(8,128)(2,1)S(1)}, u32[]{:S(2)}, u32[]{:S(2)}) collective-permute-start(bf16[256,1024]{1,0:T(8,128)(2,1)S(1)} %collective-permute-done.14), channel_id=1, source_target_pairs={{8,0},{12,4},{16,8},{20,12},{9,1},{13,5},{17,9},{21,13},{10,2},{14... | collective-permute-start | bytes 1572872 | tf_op jit(solution)/shard_map/ppermute | solution.py:69
  41.9 18.3 %collective-permute-start.19 = (bf16[256,1024]{1,0:T(8,128)(2,1)S(1)}, bf16[256,1024]{1,0:T(8,128)(2,1)S(1)}, u32[]{:S(2)}, u32[]{:S(2)}) collective-permute-start(bf16[256,1024]{1,0:T(8,128)(2,1)S(1)} %collective-permute-done.17), channel_id=1, source_target_pairs={{24,28},{28,24},{25,29},{29,25},{26,30},{30,26},{27,31},{31,27}} | collective-permute-start | bytes 1572872 | tf_op jit(solution)/shard_map/ppermute | solution.py:70
  44.9 55.6 %collective-permute-start = (bf16[256,1024]{1,0:T(8,128)(2,1)}, bf16[256,1024]{1,0:T(8,128)(2,1)}, u32[]{:S(2)}, u32[]{:S(2)}) collective-permute-start(bf16[256,1024]{1,0:T(8,128)(2,1)} %get-tuple-element.18), channel_id=1, source_target_pairs={{0,4},{4,0},{8,12},{12,8},{16,20},{20,16},{24,28},{28,24},{1,5},{5... | collective-permute-start | bytes 1572872 | tf_op jit(solution)/shard_map/ppermute | solution.py:72
  45.4 17.8 %collective-permute-start.2 = (bf16[256,1024]{1,0:T(8,128)(2,1)}, bf16[256,1024]{1,0:T(8,128)(2,1)}, u32[]{:S(2)}, u32[]{:S(2)}) collective-permute-start(bf16[256,1024]{1,0:T(8,128)(2,1)} %get-tuple-element.18), channel_id=1, source_target_pairs={{0,8},{4,12},{8,16},{12,20},{16,24},{20,28},{1,9},{5,13},{9,17},{1... | collective-permute-start | bytes 1572872 | tf_op jit(solution)/shard_map/ppermute | solution.py:69
  57.0 17.0 %collective-permute-start.22 = (bf16[256,1024]{1,0:T(8,128)(2,1)S(1)}, bf16[256,1024]{1,0:T(8,128)(2,1)S(1)}, u32[]{:S(2)}, u32[]{:S(2)}) collective-permute-start(bf16[256,1024]{1,0:T(8,128)(2,1)S(1)} %collective-permute-done.16), channel_id=1, source_target_pairs={{16,20},{20,16},{24,28},{28,24},{17,21},{21,17},{25,29},{29,25},{1... | collective-permute-start | bytes 1572872 | tf_op jit(solution)/shard_map/ppermute | solution.py:70
  57.7 15.7 %collective-permute-start.21 = (bf16[256,1024]{1,0:T(8,128)(2,1)S(1)}, bf16[256,1024]{1,0:T(8,128)(2,1)S(1)}, u32[]{:S(2)}, u32[]{:S(2)}) collective-permute-start(bf16[256,1024]{1,0:T(8,128)(2,1)S(1)} %collective-permute-done.20), channel_id=1, source_target_pairs={{0,4},{4,0},{8,12},{12,8},{1,5},{5,1},{9,13},{13,9},{2,6},{6,2},{1... | collective-permute-start | bytes 1572872 | tf_op jit(solution)/shard_map/ppermute | solution.py:70
  60.1 18.4 %collective-permute-start.23 = (bf16[256,1024]{1,0:T(8,128)(2,1)S(1)}, bf16[256,1024]{1,0:T(8,128)(2,1)S(1)}, u32[]{:S(2)}, u32[]{:S(2)}) collective-permute-start(bf16[256,1024]{1,0:T(8,128)(2,1)S(1)} %collective-permute-done.20), channel_id=1, source_target_pairs={{8,0},{12,4},{9,1},{13,5},{10,2},{14,6},{11,3},{15,7}} | collective-permute-start | bytes 1572872 | tf_op jit(solution)/shard_map/ppermute | solution.py:69
  63.2 32.7 %collective-permute-start.1 = (bf16[256,1024]{1,0:T(8,128)(2,1)}, bf16[256,1024]{1,0:T(8,128)(2,1)}, u32[]{:S(2)}, u32[]{:S(2)}) collective-permute-start(bf16[256,1024]{1,0:T(8,128)(2,1)} %get-tuple-element.18), channel_id=1, source_target_pairs={{8,0},{12,4},{16,8},{20,12},{24,16},{28,20},{9,1},{13,5},{17,9},{2... | collective-permute-start | bytes 1572872 | tf_op jit(solution)/shard_map/ppermute | solution.py:69
  73.4 8.4 %collective-permute-start.25 = (bf16[256,1024]{1,0:T(8,128)(2,1)S(1)}, bf16[256,1024]{1,0:T(8,128)(2,1)S(1)}, u32[]{:S(2)}, u32[]{:S(2)}) collective-permute-start(bf16[256,1024]{1,0:T(8,128)(2,1)S(1)} %collective-permute-done.15), channel_id=1, source_target_pairs={{8,12},{12,8},{16,20},{20,16},{24,28},{28,24},{9,13},{13,9},{17,21... | collective-permute-start | bytes 1572872 | tf_op jit(solution)/shard_map/ppermute | solution.py:70
  74.1 25.8 %collective-permute-start.3 = (bf16[256,1024]{1,0:T(8,128)(2,1)}, bf16[256,1024]{1,0:T(8,128)(2,1)}, u32[]{:S(2)}, u32[]{:S(2)}) collective-permute-start(bf16[256,1024]{1,0:T(8,128)(2,1)} %collective-permute-done.2), channel_id=1, source_target_pairs={{8,16},{12,20},{16,24},{20,28},{9,17},{13,21},{17,25},{21,29},{10,... | collective-permute-start | bytes 1572872 | tf_op jit(solution)/shard_map/ppermute | solution.py:69
  78.6 11.1 %collective-permute-start.24 = (bf16[256,1024]{1,0:T(8,128)(2,1)S(1)}, bf16[256,1024]{1,0:T(8,128)(2,1)S(1)}, u32[]{:S(2)}, u32[]{:S(2)}) collective-permute-start(bf16[256,1024]{1,0:T(8,128)(2,1)S(1)} %collective-permute-done.23), channel_id=1, source_target_pairs={{0,4},{4,0},{1,5},{5,1},{2,6},{6,2},{3,7},{7,3}} | collective-permute-start | bytes 1572872 | tf_op jit(solution)/shard_map/ppermute | solution.py:70
  81.3 11.0 %copy-start.1 = (bf16[512,1024]{1,0:T(8,128)(2,1)S(1)}, bf16[512,1024]{1,0:T(8,128)(2,1)}, u32[]{:S(2)}) copy-start(bf16[512,1024]{1,0:T(8,128)(2,1)} %param.4) | copy-start | bytes 3145732
  81.3 11.0 %copy-start.17 = (f32[1024]{0:T(1024)S(1)}, f32[1024]{0:T(1024)}, u32[]{:S(2)}) copy-start(f32[1024]{0:T(1024)} %param.6) | copy-start | bytes 12292
  94.1 25.0 %collective-permute-start.27 = (f32[512,512]{1,0:T(8,128)}, f32[512,512]{1,0:T(8,128)}, u32[]{:S(2)}, u32[]{:S(2)}) collective-permute-start(f32[512,512]{1,0:T(8,128)} %fusion.31), channel_id=1, source_target_pairs={{0,1},{1,0},{2,3},{3,2},{4,5},{5,4},{6,7},{7,6},{8,9},{9,8},{10,11... | collective-permute-start | bytes 3145736 | tf_op jit(solution)/shard_map/ppermute | solution.py:142
  95.9 25.6 %copy-start.6 = (bf16[2048,1024]{1,0:T(8,128)(2,1)S(1)}, bf16[2048,1024]{1,0:T(8,128)(2,1)}, u32[]{:S(2)}) copy-start(bf16[2048,1024]{1,0:T(8,128)(2,1)} %copy-done.5) | copy-start | bytes 12582916
  95.9 27.7 %collective-permute-start.5 = (bf16[256,1024]{1,0:T(8,128)(2,1)}, bf16[256,1024]{1,0:T(8,128)(2,1)S(1)}, u32[]{:S(2)}, u32[]{:S(2)}) collective-permute-start(bf16[256,1024]{1,0:T(8,128)(2,1)} %collective-permute-done.1), channel_id=1, source_target_pairs={{0,4},{4,0},{8,12},{12,8},{16,20},{20,16},{1,5},{5,1},{9,13},{13,9... | collective-permute-start | bytes 1572872 | tf_op jit(solution)/shard_map/ppermute | solution.py:70
  98.6 19.8 %collective-permute-start.7 = (bf16[256,1024]{1,0:T(8,128)(2,1)}, bf16[256,1024]{1,0:T(8,128)(2,1)S(1)}, u32[]{:S(2)}, u32[]{:S(2)}) collective-permute-start(bf16[256,1024]{1,0:T(8,128)(2,1)} %collective-permute-done.1), channel_id=1, source_target_pairs={{8,0},{12,4},{16,8},{20,12},{9,1},{13,5},{17,9},{21,13},{10,2},{14... | collective-permute-start | bytes 1572872 | tf_op jit(solution)/shard_map/ppermute | solution.py:69
  99.9 3.2 %collective-permute-start.4 = (bf16[256,1024]{1,0:T(8,128)(2,1)}, bf16[256,1024]{1,0:T(8,128)(2,1)S(1)}, u32[]{:S(2)}, u32[]{:S(2)}) collective-permute-start(bf16[256,1024]{1,0:T(8,128)(2,1)} %collective-permute-done.3), channel_id=1, source_target_pairs={{16,24},{20,28},{17,25},{21,29},{18,26},{22,30},{19,27},{23,31}} | collective-permute-start | bytes 1572872 | tf_op jit(solution)/shard_map/ppermute | solution.py:69
  102.8 37.0 %collective-permute-start.26 = (f32[512,512]{1,0:T(8,128)S(1)}, f32[512,512]{1,0:T(8,128)S(1)}, u32[]{:S(2)}, u32[]{:S(2)}) collective-permute-start(f32[512,512]{1,0:T(8,128)S(1)} %fusion.34), channel_id=1, source_target_pairs={{0,1},{1,0},{2,3},{3,2},{4,5},{5,4},{6,7},{7,6},{8,9},{9,8},{10,11... | collective-permute-start | bytes 3145736 | tf_op jit(solution)/shard_map/ppermute | solution.py:142
  103.1 21.8 %collective-permute-start.6 = (bf16[256,1024]{1,0:T(8,128)(2,1)S(1)}, bf16[256,1024]{1,0:T(8,128)(2,1)S(1)}, u32[]{:S(2)}, u32[]{:S(2)}) collective-permute-start(bf16[256,1024]{1,0:T(8,128)(2,1)S(1)} %collective-permute-done.4), channel_id=1, source_target_pairs={{24,28},{28,24},{25,29},{29,25},{26,30},{30,26},{27,31},{31,27}} | collective-permute-start | bytes 1572872 | tf_op jit(solution)/shard_map/ppermute | solution.py:70
  105.0 38.4 %copy-start.8 = (f32[64,8,2,256]{3,1,2,0:T(8,128)S(1)}, f32[64,8,2,256]{3,1,2,0:T(8,128)}, u32[]{:S(2)}) copy-start(f32[64,8,2,256]{3,1,2,0:T(8,128)} %copy.5) | copy-start | bytes 3145732
  118.4 27.4 %collective-permute-start.9 = (bf16[256,1024]{1,0:T(8,128)(2,1)}, bf16[256,1024]{1,0:T(8,128)(2,1)S(1)}, u32[]{:S(2)}, u32[]{:S(2)}) collective-permute-start(bf16[256,1024]{1,0:T(8,128)(2,1)} %collective-permute-done.3), channel_id=1, source_target_pairs={{16,20},{20,16},{24,28},{28,24},{17,21},{21,17},{25,29},{29,25},{1... | collective-permute-start | bytes 1572872 | tf_op jit(solution)/shard_map/ppermute | solution.py:70
  119.1 26.7 %collective-permute-start.8 = (bf16[256,1024]{1,0:T(8,128)(2,1)S(1)}, bf16[256,1024]{1,0:T(8,128)(2,1)S(1)}, u32[]{:S(2)}, u32[]{:S(2)}) collective-permute-start(bf16[256,1024]{1,0:T(8,128)(2,1)S(1)} %collective-permute-done.7), channel_id=1, source_target_pairs={{0,4},{4,0},{8,12},{12,8},{1,5},{5,1},{9,13},{13,9},{2,6},{6,2},{1... | collective-permute-start | bytes 1572872 | tf_op jit(solution)/shard_map/ppermute | solution.py:70
  123.6 15.5 %collective-permute-start.10 = (bf16[256,1024]{1,0:T(8,128)(2,1)S(1)}, bf16[256,1024]{1,0:T(8,128)(2,1)S(1)}, u32[]{:S(2)}, u32[]{:S(2)}) collective-permute-start(bf16[256,1024]{1,0:T(8,128)(2,1)S(1)} %collective-permute-done.7), channel_id=1, source_target_pairs={{8,0},{12,4},{9,1},{13,5},{10,2},{14,6},{11,3},{15,7}} | collective-permute-start | bytes 1572872 | tf_op jit(solution)/shard_map/ppermute | solution.py:69
  124.9 18.5 %collective-permute-start.28 = (bf16[512,512]{1,0:T(8,128)(2,1)S(1)}, bf16[512,512]{1,0:T(8,128)(2,1)S(1)}, u32[]{:S(2)}, u32[]{:S(2)}) collective-permute-start(bf16[512,512]{1,0:T(8,128)(2,1)S(1)} %fusion.6), channel_id=1, source_target_pairs={{0,2},{1,3},{2,0},{3,1},{4,6},{5,7},{6,4},{7,5},{8,10},{9,11},{10,... | collective-permute-start | bytes 1572872 | tf_op jit(solution)/shard_map/ppermute | solution.py:145
  139.0 17.7 %collective-permute-start.12 = (bf16[256,1024]{1,0:T(8,128)(2,1)}, bf16[256,1024]{1,0:T(8,128)(2,1)S(1)}, u32[]{:S(2)}, u32[]{:S(2)}) collective-permute-start(bf16[256,1024]{1,0:T(8,128)(2,1)} %collective-permute-done.2), channel_id=1, source_target_pairs={{8,12},{12,8},{16,20},{20,16},{24,28},{28,24},{9,13},{13,9},{17,21... | collective-permute-start | bytes 1572872 | tf_op jit(solution)/shard_map/ppermute | solution.py:70
  139.7 17.0 %collective-permute-start.11 = (bf16[256,1024]{1,0:T(8,128)(2,1)S(1)}, bf16[256,1024]{1,0:T(8,128)(2,1)S(1)}, u32[]{:S(2)}, u32[]{:S(2)}) collective-permute-start(bf16[256,1024]{1,0:T(8,128)(2,1)S(1)} %collective-permute-done.10), channel_id=1, source_target_pairs={{0,4},{4,0},{1,5},{5,1},{2,6},{6,2},{3,7},{7,3}} | collective-permute-start | bytes 1572872 | tf_op jit(solution)/shard_map/ppermute | solution.py:70
  144.2 13.2 %copy-start.9 = (bf16[512,512]{1,0:T(8,128)(2,1)}, bf16[512,512]{1,0:T(8,128)(2,1)S(1)}, u32[]{:S(2)}) copy-start(bf16[512,512]{1,0:T(8,128)(2,1)S(1)} %fusion.9) | copy-start | bytes 1572868
  144.3 12.5 %collective-permute-start.29 = (bf16[512,512]{1,0:T(8,128)(2,1)S(1)}, bf16[512,512]{1,0:T(8,128)(2,1)S(1)}, u32[]{:S(2)}, u32[]{:S(2)}) collective-permute-start(bf16[512,512]{1,0:T(8,128)(2,1)S(1)} %fusion.9), channel_id=1, source_target_pairs={{0,2},{1,3},{2,0},{3,1},{4,6},{5,7},{6,4},{7,5},{8,10},{9,11},{10,... | collective-permute-start | bytes 1572872 | tf_op jit(solution)/shard_map/ppermute | solution.py:154
  146.5 10.9 %collective-permute-start.30 = (bf16[512,512]{1,0:T(8,128)(2,1)S(1)}, bf16[512,512]{1,0:T(8,128)(2,1)S(1)}, u32[]{:S(2)}, u32[]{:S(2)}) collective-permute-start(bf16[512,512]{1,0:T(8,128)(2,1)S(1)} %fusion.9), channel_id=1, source_target_pairs={{0,1},{1,0},{2,3},{3,2},{4,5},{5,4},{6,7},{7,6},{8,9},{9,8},{10,11... | collective-permute-start | bytes 1572872 | tf_op jit(solution)/shard_map/ppermute | solution.py:155
  156.7 1.9 collective-permute-start.31
  161.2 5.1 %collective-permute-start.33 = (f32[512,512]{1,0:T(8,128)}, f32[512,512]{1,0:T(8,128)}, u32[]{:S(2)}, u32[]{:S(2)}) collective-permute-start(f32[512,512]{1,0:T(8,128)} %fusion.17), channel_id=1, source_target_pairs={{0,1},{1,0},{2,3},{3,2},{4,5},{5,4},{6,7},{7,6},{8,9},{9,8},{10,11... | collective-permute-start | bytes 3145736 | tf_op jit(solution)/shard_map/ppermute | solution.py:142
  164.0 7.4 %collective-permute-start.32 = (f32[512,512]{1,0:T(8,128)S(1)}, f32[512,512]{1,0:T(8,128)S(1)}, u32[]{:S(2)}, u32[]{:S(2)}) collective-permute-start(f32[512,512]{1,0:T(8,128)S(1)} %fusion.20), channel_id=1, source_target_pairs={{0,1},{1,0},{2,3},{3,2},{4,5},{5,4},{6,7},{7,6},{8,9},{9,8},{10,11... | collective-permute-start | bytes 3145736 | tf_op jit(solution)/shard_map/ppermute | solution.py:142
  168.4 14.3 %collective-permute-start.34 = (bf16[512,512]{1,0:T(8,128)(2,1)S(1)}, bf16[512,512]{1,0:T(8,128)(2,1)S(1)}, u32[]{:S(2)}, u32[]{:S(2)}) collective-permute-start(bf16[512,512]{1,0:T(8,128)(2,1)S(1)} %fusion.7), channel_id=1, source_target_pairs={{0,2},{1,3},{2,0},{3,1},{4,6},{5,7},{6,4},{7,5},{8,10},{9,11},{10,... | collective-permute-start | bytes 1572872 | tf_op jit(solution)/shard_map/ppermute | solution.py:145
  170.7 14.5 %copy-start.12 = (bf16[512,512]{1,0:T(8,128)(2,1)S(1)}, bf16[512,512]{1,0:T(8,128)(2,1)}, u32[]{:S(2)}) copy-start(bf16[512,512]{1,0:T(8,128)(2,1)} %copy-done.11) | copy-start | bytes 1572868
  183.6 13.5 %collective-permute-start.35 = (bf16[512,512]{1,0:T(8,128)(2,1)S(1)}, bf16[512,512]{1,0:T(8,128)(2,1)S(1)}, u32[]{:S(2)}, u32[]{:S(2)}) collective-permute-start(bf16[512,512]{1,0:T(8,128)(2,1)S(1)} %fusion.8), channel_id=1, source_target_pairs={{0,2},{1,3},{2,0},{3,1},{4,6},{5,7},{6,4},{7,5},{8,10},{9,11},{10,... | collective-permute-start | bytes 1572872 | tf_op jit(solution)/shard_map/ppermute | solution.py:154
  185.9 12.0 %collective-permute-start.36 = (bf16[512,512]{1,0:T(8,128)(2,1)S(1)}, bf16[512,512]{1,0:T(8,128)(2,1)S(1)}, u32[]{:S(2)}, u32[]{:S(2)}) collective-permute-start(bf16[512,512]{1,0:T(8,128)(2,1)S(1)} %fusion.8), channel_id=1, source_target_pairs={{0,1},{1,0},{2,3},{3,2},{4,5},{5,4},{6,7},{7,6},{8,9},{9,8},{10,11... | collective-permute-start | bytes 1572872 | tf_op jit(solution)/shard_map/ppermute | solution.py:155
  197.1 1.9 collective-permute-start.37
  200.3 3.7 %collective-permute-start.38 = (f32[1024]{0:T(1024)S(1)}, f32[1024]{0:T(1024)S(1)}, u32[]{:S(2)}, u32[]{:S(2)}) collective-permute-start(f32[1024]{0:T(1024)S(1)} %fusion.1), channel_id=1, source_target_pairs={{0,4},{4,0},{8,12},{12,8},{16,20},{20,16},{24,28},{28,24},{1,5},{5... | collective-permute-start | bytes 12296 | tf_op jit(solution)/shard_map/ppermute | solution.py:88
  204.0 3.6 %collective-permute-start.39 = (f32[1024]{0:T(1024)S(1)}, f32[1024]{0:T(1024)S(1)}, u32[]{:S(2)}, u32[]{:S(2)}) collective-permute-start(f32[1024]{0:T(1024)S(1)} %add.220), channel_id=1, source_target_pairs={{0,8},{4,12},{8,0},{12,4},{16,24},{20,28},{24,16},{28,20},{1,9},{5... | collective-permute-start | bytes 12296 | tf_op jit(solution)/shard_map/ppermute | solution.py:88
  207.6 8.1 %collective-permute-start.40 = (f32[1024]{0:T(1024)S(1)}, f32[1024]{0:T(1024)S(1)}, u32[]{:S(2)}, u32[]{:S(2)}) collective-permute-start(f32[1024]{0:T(1024)S(1)} %add.221), channel_id=1, source_target_pairs={{0,16},{4,20},{8,24},{12,28},{16,0},{20,4},{24,8},{28,12},{1,17},{... | collective-permute-start | bytes 12296 | tf_op jit(solution)/shard_map/ppermute | solution.py:88
  (11 other events, 41.8 us)

commit v6 on v5

--- a/solution.py
+++ b/solution.py
@@ -5,7 +5,7 @@
 from jax import lax
 from jax.sharding import PartitionSpec as P
 
-CHUNKS = 2
+CHUNKS = 1
 
 
 def _rows(a, blk, n):

time: 217 us -> 248 us (1.14)
  waiting for transfers between devices: 106 us -> 142 us
  starting transfers between devices: 66.8 us -> 55.7 us
  matrix products: 21.1 us -> 28.9 us
  local copies, waits for them, and re-layouts: 10.7 us -> 4.25 us
  other arithmetic: 10.8 us -> 16.1 us
    ppermute x12 -> x6, waiting for transfers between devices: 16.8 us -> 46.5 us  [_gather_src(): got[sign, s] = (cur, lax.ppermute(cur, 'src', cross(sign, s)))]
    ppermute x3, starting transfers between devices: 8.59 us -> 26.8 us  [_sum_over_src(): v = v + lax.ppermute(v, 'src', [(i, i ^ b) for i in range(n)])]
    ppermute x12 -> x6, starting transfers between devices: 27.8 us -> 11.3 us  [_gather_src(): cur = lax.ppermute(cur, 'src', pairs)]
    ppermute x2 -> x1, waiting for transfers between devices: 11.3 us -> 23.9 us  [per_device(): lax.ppermute(halves[k].astype(jnp.bfloat16), 'vox', chip_perm(k))]
    ppermute x12 -> x6, starting transfers between devices: 21 us -> 12.5 us  [_gather_src(): got[sign, s] = (cur, lax.ppermute(cur, 'src', cross(sign, s)))]
    ppermute x12 -> x6, waiting for transfers between devices: 49.2 us -> 43 us  [_gather_src(): cur = lax.ppermute(cur, 'src', pairs)]
    dot_general x8 -> x4, matrix products: 7.67 us -> 12.5 us  [per_device(): jnp.dot(w, _rows(adj, rel(blk), n), preferred_element_type=jnp.float32)]
    reshape x1 -> x0, local copies, waits for them, and re-layouts: 4 us -> none  [per_device(): weight = measurement_weight.reshape(sl, t, ds)]
  transfers between devices with their start and end apart: 41 -> 22, of which waited for: 16 -> 11; matrix products, arithmetic and copies ran while one was open for 15% -> 11% of each run, Pallas kernels for 0% -> 0%
where the time goes in v6:
time: 248 us; the launch traced here: 247 us
  waiting for transfers between devices  142 us (57%)
  starting transfers between devices  55.7 us (22%)
  matrix products  28.9 us (12%)
  other arithmetic  16.1 us (6%)
  local copies, waits for them, and re-layouts  4.25 us (2%)
    ppermute x6, waiting for transfers between devices, _gather_src(): got[sign, s] = (cur, lax.ppermute(cur, 'src', cross(sign, s)))  46.5 us
    ppermute x6, waiting for transfers between devices, _gather_src(): cur = lax.ppermute(cur, 'src', pairs)  43 us
    ppermute x3, starting transfers between devices, _sum_over_src(): v = v + lax.ppermute(v, 'src', [(i, i ^ b) for i in range(n)])  26.8 us
    ppermute x1, waiting for transfers between devices, per_device(): lax.ppermute(halves[k].astype(jnp.bfloat16), 'vox', chip_perm(k))  23.9 us
    ppermute x1, waiting for transfers between devices, per_device(): got.append((2 * ((q - k) % m) + par, lax.ppermute(wt, 'vox', chip_perm(k))))  22.9 us
    dot_general x4, matrix products, pblock(): lax.dot_general(scaled, _rows(adj, rel(blk), n), (((1,), (1,)), ((), ()))...  16.4 us
    unnamed x7, other arithmetic  13.3 us
    dot_general x4, matrix products, per_device(): jnp.dot(w, _rows(adj, rel(blk), n), preferred_element_type=jnp.float32)  12.5 us
  transfers between devices with their start and end apart: 22, of which 11 were waited for; matrix products, arithmetic and copies ran while one was open for 11% of the time, Pallas kernels for 0%

profile of v6, /device:TPU:0, one launch (start us, length us, event | category | flops | bytes accessed | tf_op | source)
XLA Modules:
  0.0 246.9 jit_solution(12960398982565657960)
XLA Ops:
  0.0 5.1 %collective-permute-start.2 = (bf16[512,1024]{1,0:T(8,128)(2,1)}, bf16[512,1024]{1,0:T(8,128)(2,1)S(1)}, u32[]{:S(2)}, u32[]{:S(2)}) collective-permute-start(bf16[512,1024]{1,0:T(8,128)(2,1)} %param.5), channel_id=1, source_target_pairs={{0,8},{4,12},{8,16},{12,20},{16,24},{20,28},{1,9},{5,13},{9,17},{1... | collective-permute-start | bytes 3145736 | tf_op jit(solution)/shard_map/ppermute | solution.py:69
  5.1 1.3 collective-permute-start.1
  6.4 21.3 %collective-permute-done.2 = bf16[512,1024]{1,0:T(8,128)(2,1)S(1)} collective-permute-done((bf16[512,1024]{1,0:T(8,128)(2,1)}, bf16[512,1024]{1,0:T(8,128)(2,1)S(1)}, u32[]{:S(2)}, u32[]{:S(2)}) %collective-permute-start.2) | collective-permute-done | bytes 1048608 | tf_op jit(solution)/shard_map/ppermute | solution.py:69
  27.8 0.7 collective-permute-start.3
  28.5 3.5 %collective-permute-done.1 = bf16[512,1024]{1,0:T(8,128)(2,1)} collective-permute-done((bf16[512,1024]{1,0:T(8,128)(2,1)}, bf16[512,1024]{1,0:T(8,128)(2,1)}, u32[]{:S(2)}, u32[]{:S(2)}) %collective-permute-start.1) | collective-permute-done | bytes 1048608 | tf_op jit(solution)/shard_map/ppermute | solution.py:69
  32.0 1.3 collective-permute-start.7
  33.3 1.0 copy-done.1
  34.2 1.7 collective-permute-start.4
  35.9 1.5 collective-permute-start
  37.4 2.4 collective-permute-start.5
  39.8 18.2 %collective-permute-done.7 = bf16[512,1024]{1,0:T(8,128)(2,1)} collective-permute-done((bf16[512,1024]{1,0:T(8,128)(2,1)}, bf16[512,1024]{1,0:T(8,128)(2,1)}, u32[]{:S(2)}, u32[]{:S(2)}) %collective-permute-start.7) | collective-permute-done | bytes 1048608 | tf_op jit(solution)/shard_map/ppermute | solution.py:69
  58.0 1.3 collective-permute-start.10
  59.3 1.6 collective-permute-start.6
  61.0 3.4 %collective-permute-start.8 = (bf16[512,1024]{1,0:T(8,128)(2,1)}, bf16[512,1024]{1,0:T(8,128)(2,1)S(1)}, u32[]{:S(2)}, u32[]{:S(2)}) collective-permute-start(bf16[512,1024]{1,0:T(8,128)(2,1)} %collective-permute-done.7), channel_id=1, source_target_pairs={{0,4},{4,0},{8,12},{12,8},{1,5},{5,1},{9,13},{13,9},{2,6},{6,2},{1... | collective-permute-start | bytes 3145736 | tf_op jit(solution)/shard_map/ppermute | solution.py:70
  64.4 0.7 collective-permute-start.9
  65.1 1.6 select_dynamic-update-slice_fusion.7
  67.2 17.6 %collective-permute-done.5 = bf16[512,1024]{1,0:T(8,128)(2,1)} collective-permute-done((bf16[512,1024]{1,0:T(8,128)(2,1)}, bf16[512,1024]{1,0:T(8,128)(2,1)}, u32[]{:S(2)}, u32[]{:S(2)}) %collective-permute-start.5) | collective-permute-done | bytes 1048608 | tf_op jit(solution)/shard_map/ppermute | solution.py:70
  84.8 0.7 collective-permute-start.12
  85.5 3.6 %collective-permute-start.11 = (bf16[512,1024]{1,0:T(8,128)(2,1)}, bf16[512,1024]{1,0:T(8,128)(2,1)S(1)}, u32[]{:S(2)}, u32[]{:S(2)}) collective-permute-start(bf16[512,1024]{1,0:T(8,128)(2,1)} %collective-permute-done.10), channel_id=1, source_target_pairs={{0,4},{4,0},{1,5},{5,1},{2,6},{6,2},{3,7},{7,3}} | collective-permute-start | bytes 3145736 | tf_op jit(solution)/shard_map/ppermute | solution.py:70
  89.1 2.4 select_dynamic-update-slice_fusion.5
  91.6 2.5 %select_dynamic-update-slice_fusion.4 = bf16[4096,1024]{1,0:T(8,128)(2,1)S(1)} fusion(bf16[4096,1024]{1,0:T(8,128)(2,1)S(1)} %select_dynamic-update-slice_fusion.5, pred[]{:T(512)S(6)} %eq.19, bf16[512,1024]{1,0:T(8,128)(2,1)} %collective-permute-done.1, bf16[512,1024]{1,0:T(8,128)(2,1)} %collective-permute-done.4, pred[]{:T(512)S(6)} %lt.92, ...), kind=kLoop, calls=%fused_computation.26 | loop fusion | flops 1572864 | bytes 5242882
  94.1 13.1 %collective-permute-done.8 = bf16[512,1024]{1,0:T(8,128)(2,1)S(1)} collective-permute-done((bf16[512,1024]{1,0:T(8,128)(2,1)}, bf16[512,1024]{1,0:T(8,128)(2,1)S(1)}, u32[]{:S(2)}, u32[]{:S(2)}) %collective-permute-start.8) | collective-permute-done | bytes 1048608 | tf_op jit(solution)/shard_map/ppermute | solution.py:70
  107.1 2.1 select_dynamic-update-slice_fusion.3
  109.3 2.1 select_dynamic-update-slice_fusion.2
  111.4 15.8 %collective-permute-done.11 = bf16[512,1024]{1,0:T(8,128)(2,1)S(1)} collective-permute-done((bf16[512,1024]{1,0:T(8,128)(2,1)}, bf16[512,1024]{1,0:T(8,128)(2,1)S(1)}, u32[]{:S(2)}, u32[]{:S(2)}) %collective-permute-start.11) | collective-permute-done | bytes 1048608 | tf_op jit(solution)/shard_map/ppermute | solution.py:70
  127.2 2.1 select_dynamic-update-slice_fusion.1
  129.4 2.2 select_dynamic-update-slice_fusion
  131.6 3.3 %copy-done.4 = bf16[4096,1024]{1,0:T(8,128)(2,1)} copy-done((bf16[4096,1024]{1,0:T(8,128)(2,1)}, bf16[4096,1024]{1,0:T(8,128)(2,1)S(1)}, u32[]{:S(2)}) %copy-start.4) | copy-done | bytes 8388632
  134.8 2.6 %fusion.10 = f32[512,1024]{1,0:T(8,128)} fusion(bf16[4096,1024]{1,0:T(8,128)(2,1)S(1)} %select_dynamic-update-slice_fusion, s32[]{:T(128)S(6)} %select_n.188, bf16[512,1024]{1,0:T(8,128)(2,1)S(1)} %copy-done.5, f32[1024]{0:T(1024)S(1)} %copy-done.6), kind=kOutput, calls=%fused_computation.14 | convolution fusion | flops 1075314688 | bytes 5246980 | tf_op jit(solution)/shard_map/dot_general | solution.py:135
  137.4 4.2 %fusion.14 = f32[512,1024]{1,0:T(8,128)} fusion(bf16[4096,1024]{1,0:T(8,128)(2,1)} %copy-done.4, s32[]{:T(128)S(6)} %select_n.183, bf16[512,1024]{1,0:T(8,128)(2,1)S(1)} %copy-done.5, f32[1024]{0:T(1024)S(1)} %copy-done.6), kind=kOutput, calls=%fused_computation.18 | convolution fusion | flops 1075314688 | bytes 5246980 | tf_op jit(solution)/shard_map/dot_general | solution.py:135
  141.7 0.5 collective-permute-start.13
  142.2 4.7 %add_convert_fusion = bf16[512,1024]{1,0:T(8,128)(2,1)} fusion(f32[512,1024]{1,0:T(8,128)} %collective-permute-done.14, bf16[4096,1024]{1,0:T(8,128)(2,1)} %copy-done.4, s32[]{:T(128)S(6)} %select_n.186, bf16[512,1024]{1,0:T(8,128)(2,1)S(1)} %copy-done.5, f32[1024]{0:T(1024)S(1)} %copy-done.6), kind=kOutput, calls=%fused_computation.13 | convolution fusion | flops 1076363264 | bytes 6295556 | tf_op jit(solution)/shard_map/dot_general | solution.py:135
  146.9 1.5 collective-permute-start.15
  148.4 23.9 %collective-permute-done.15 = bf16[512,1024]{1,0:T(8,128)(2,1)} collective-permute-done((bf16[512,1024]{1,0:T(8,128)(2,1)}, bf16[512,1024]{1,0:T(8,128)(2,1)}, u32[]{:S(2)}, u32[]{:S(2)}) %collective-permute-start.15) | collective-permute-done | bytes 1048608 | tf_op jit(solution)/shard_map/ppermute | solution.py:145
  172.3 4.9 %multiply_convert_fusion = bf16[512,1024]{1,0:T(8,128)(2,1)} fusion(f32[512,1024]{1,0:T(8,128)S(1)} %copy-done.3, bf16[512,1024]{1,0:T(8,128)(2,1)} %collective-permute-done.15, f32[512,1024]{1,0:T(8,128)} %collective-permute-done.13, bf16[4096,1024]{1,0:T(8,128)(2,1)} %copy-done.4, s32[]{:T(128)S(6)} %select_n.181, bf16[512,1024]{1,0:T(8,128)(2,1)S(1)} %copy-done.5, ...), kind=kOutput, calls=%fused_computation.12 | convolution fusion | flops 1077936128 | bytes 9441284 | tf_op jit(solution)/shard_map/dot_general | solution.py:135
  177.1 1.5 collective-permute-start.16
  178.6 22.9 %collective-permute-done.16 = bf16[512,1024]{1,0:T(8,128)(2,1)S(1)} collective-permute-done((bf16[512,1024]{1,0:T(8,128)(2,1)}, bf16[512,1024]{1,0:T(8,128)(2,1)S(1)}, u32[]{:S(2)}, u32[]{:S(2)}) %collective-permute-start.16) | collective-permute-done | bytes 1048608 | tf_op jit(solution)/shard_map/ppermute | solution.py:154
  201.6 2.8 %fusion.6 = f32[512,1024]{1,0:T(8,128)S(1)} fusion(bf16[512,1024]{1,0:T(8,128)(2,1)S(1)} %collective-permute-done.16, bf16[4096,1024]{1,0:T(8,128)(2,1)} %copy-done.4, s32[]{:T(128)S(6)} %select_n.193), kind=kOutput, calls=%fused_computation.8 | convolution fusion | flops 1073741824 | bytes 5242884 | tf_op jit(solution)/shard_map/dot_general | solution.py:161
  204.4 3.1 %fusion.4 = f32[512,1024]{1,0:T(8,128)S(1)} fusion(bf16[512,1024]{1,0:T(8,128)(2,1)S(1)} %collective-permute-done.17, bf16[4096,1024]{1,0:T(8,128)(2,1)} %copy-done.4, s32[]{:T(128)S(6)} %select_n.195), kind=kOutput, calls=%fused_computation.6 | convolution fusion | flops 1073741824 | bytes 5242884 | tf_op jit(solution)/shard_map/dot_general | solution.py:161
  207.5 3.2 %fusion.2 = f32[512,1024]{1,0:T(8,128)S(1)} fusion(bf16[512,1024]{1,0:T(8,128)(2,1)} %collective-permute-done.18, bf16[4096,1024]{1,0:T(8,128)(2,1)} %copy-done.4, s32[]{:T(128)S(6)} %select_n.197), kind=kOutput, calls=%fused_computation.4 | convolution fusion | flops 1073741824 | bytes 5242884 | tf_op jit(solution)/shard_map/dot_general | solution.py:161
  210.7 3.4 %fusion.1 = f32[1024]{0:T(1024)S(1)} fusion(bf16[512,1024]{1,0:T(8,128)(2,1)S(1)} %copy-done.5, f32[512,1024]{1,0:T(8,128)S(1)} %fusion.2, f32[512,1024]{1,0:T(8,128)S(1)} %fusion.4, f32[512,1024]{1,0:T(8,128)S(1)} %fusion.6, bf16[512,1024]{1,0:T(8,128)(2,1)} %multiply_convert_fusion, bf16[4096,1024]{1,0:T(8,128)(2,1)} %copy-done.4, s32[]{:T(128)S(6)} %select_n.190), kind=kOutput, calls=%fused_computation.3 | convolution fusion | flops 1076886528 | bytes 10489860 | tf_op jit(solution)/shard_map/dot_general | solution.py:161
  214.2 1.6 collective-permute-start.19
  215.8 2.1 collective-permute-done.19
  217.9 19.0 %collective-permute-start.20 = (f32[1024]{0:T(1024)S(1)}, f32[1024]{0:T(1024)S(1)}, u32[]{:S(2)}, u32[]{:S(2)}) collective-permute-start(f32[1024]{0:T(1024)S(1)} %add.160), channel_id=1, source_target_pairs={{0,8},{4,12},{8,0},{12,4},{16,24},{20,28},{24,16},{28,20},{1,9},{5... | collective-permute-start | bytes 12296 | tf_op jit(solution)/shard_map/ppermute | solution.py:88
  236.8 1.6 collective-permute-done.20
  238.4 6.3 %collective-permute-start.21 = (f32[1024]{0:T(1024)S(1)}, f32[1024]{0:T(1024)S(1)}, u32[]{:S(2)}, u32[]{:S(2)}) collective-permute-start(f32[1024]{0:T(1024)S(1)} %add.161), channel_id=1, source_target_pairs={{0,16},{4,20},{8,24},{12,28},{16,0},{20,4},{24,8},{28,12},{1,17},{... | collective-permute-start | bytes 12296 | tf_op jit(solution)/shard_map/ppermute | solution.py:88
  244.7 1.6 collective-permute-done.21
  246.3 0.6 add.162
  (29 shorter events, 0.5 us)
Async XLA Ops:
  0.0 66.8 %copy-start = (bf16[512,1024]{1,0:T(8,128)(2,1)S(1)}, bf16[512,1024]{1,0:T(8,128)(2,1)}, u32[]{:S(2)}) copy-start(bf16[512,1024]{1,0:T(8,128)(2,1)} %param.5) | copy-start | bytes 3145732
  0.0 27.8 %collective-permute-start.2 = (bf16[512,1024]{1,0:T(8,128)(2,1)}, bf16[512,1024]{1,0:T(8,128)(2,1)S(1)}, u32[]{:S(2)}, u32[]{:S(2)}) collective-permute-start(bf16[512,1024]{1,0:T(8,128)(2,1)} %param.5), channel_id=1, source_target_pairs={{0,8},{4,12},{8,16},{12,20},{16,24},{20,28},{1,9},{5,13},{9,17},{1... | collective-permute-start | bytes 3145736 | tf_op jit(solution)/shard_map/ppermute | solution.py:69
  5.1 26.8 %collective-permute-start.1 = (bf16[512,1024]{1,0:T(8,128)(2,1)}, bf16[512,1024]{1,0:T(8,128)(2,1)}, u32[]{:S(2)}, u32[]{:S(2)}) collective-permute-start(bf16[512,1024]{1,0:T(8,128)(2,1)} %param.5), channel_id=1, source_target_pairs={{8,0},{12,4},{16,8},{20,12},{24,16},{28,20},{9,1},{13,5},{17,9},{2... | collective-permute-start | bytes 3145736 | tf_op jit(solution)/shard_map/ppermute | solution.py:69
  27.8 5.5 %collective-permute-start.3 = (bf16[512,1024]{1,0:T(8,128)(2,1)S(1)}, bf16[512,1024]{1,0:T(8,128)(2,1)S(1)}, u32[]{:S(2)}, u32[]{:S(2)}) collective-permute-start(bf16[512,1024]{1,0:T(8,128)(2,1)S(1)} %collective-permute-done.2), channel_id=1, source_target_pairs={{8,16},{12,20},{16,24},{20,28},{9,17},{13,21},{17,25},{21,29},{10,... | collective-permute-start | bytes 3145736 | tf_op jit(solution)/shard_map/ppermute | solution.py:69
  32.0 26.1 %collective-permute-start.7 = (bf16[512,1024]{1,0:T(8,128)(2,1)}, bf16[512,1024]{1,0:T(8,128)(2,1)}, u32[]{:S(2)}, u32[]{:S(2)}) collective-permute-start(bf16[512,1024]{1,0:T(8,128)(2,1)} %collective-permute-done.1), channel_id=1, source_target_pairs={{8,0},{12,4},{16,8},{20,12},{9,1},{13,5},{17,9},{21,13},{10,2},{14... | collective-permute-start | bytes 3145736 | tf_op jit(solution)/shard_map/ppermute | solution.py:69
  33.3 1.0 copy-start.1
  34.2 25.1 %collective-permute-start.4 = (bf16[512,1024]{1,0:T(8,128)(2,1)S(1)}, bf16[512,1024]{1,0:T(8,128)(2,1)}, u32[]{:S(2)}, u32[]{:S(2)}) collective-permute-start(bf16[512,1024]{1,0:T(8,128)(2,1)S(1)} %collective-permute-done.3), channel_id=1, source_target_pairs={{16,24},{20,28},{17,25},{21,29},{18,26},{22,30},{19,27},{23,31}} | collective-permute-start | bytes 3145736 | tf_op jit(solution)/shard_map/ppermute | solution.py:69
  35.9 28.5 %collective-permute-start = (bf16[512,1024]{1,0:T(8,128)(2,1)}, bf16[512,1024]{1,0:T(8,128)(2,1)S(1)}, u32[]{:S(2)}, u32[]{:S(2)}) collective-permute-start(bf16[512,1024]{1,0:T(8,128)(2,1)} %param.5), channel_id=1, source_target_pairs={{0,4},{4,0},{8,12},{12,8},{16,20},{20,16},{24,28},{28,24},{1,5},{5... | collective-permute-start | bytes 3145736 | tf_op jit(solution)/shard_map/ppermute | solution.py:72
  37.4 47.4 %collective-permute-start.5 = (bf16[512,1024]{1,0:T(8,128)(2,1)}, bf16[512,1024]{1,0:T(8,128)(2,1)}, u32[]{:S(2)}, u32[]{:S(2)}) collective-permute-start(bf16[512,1024]{1,0:T(8,128)(2,1)} %collective-permute-done.1), channel_id=1, source_target_pairs={{0,4},{4,0},{8,12},{12,8},{16,20},{20,16},{1,5},{5,1},{9,13},{13,9... | collective-permute-start | bytes 3145736 | tf_op jit(solution)/shard_map/ppermute | solution.py:70
  58.0 27.5 %collective-permute-start.10 = (bf16[512,1024]{1,0:T(8,128)(2,1)}, bf16[512,1024]{1,0:T(8,128)(2,1)}, u32[]{:S(2)}, u32[]{:S(2)}) collective-permute-start(bf16[512,1024]{1,0:T(8,128)(2,1)} %collective-permute-done.7), channel_id=1, source_target_pairs={{8,0},{12,4},{9,1},{13,5},{10,2},{14,6},{11,3},{15,7}} | collective-permute-start | bytes 3145736 | tf_op jit(solution)/shard_map/ppermute | solution.py:69
  59.3 29.8 %collective-permute-start.6 = (bf16[512,1024]{1,0:T(8,128)(2,1)}, bf16[512,1024]{1,0:T(8,128)(2,1)}, u32[]{:S(2)}, u32[]{:S(2)}) collective-permute-start(bf16[512,1024]{1,0:T(8,128)(2,1)} %collective-permute-done.4), channel_id=1, source_target_pairs={{24,28},{28,24},{25,29},{29,25},{26,30},{30,26},{27,31},{31,27}} | collective-permute-start | bytes 3145736 | tf_op jit(solution)/shard_map/ppermute | solution.py:70
  61.0 46.2 %collective-permute-start.8 = (bf16[512,1024]{1,0:T(8,128)(2,1)}, bf16[512,1024]{1,0:T(8,128)(2,1)S(1)}, u32[]{:S(2)}, u32[]{:S(2)}) collective-permute-start(bf16[512,1024]{1,0:T(8,128)(2,1)} %collective-permute-done.7), channel_id=1, source_target_pairs={{0,4},{4,0},{8,12},{12,8},{1,5},{5,1},{9,13},{13,9},{2,6},{6,2},{1... | collective-permute-start | bytes 3145736 | tf_op jit(solution)/shard_map/ppermute | solution.py:70
  64.4 42.7 %collective-permute-start.9 = (bf16[512,1024]{1,0:T(8,128)(2,1)}, bf16[512,1024]{1,0:T(8,128)(2,1)S(1)}, u32[]{:S(2)}, u32[]{:S(2)}) collective-permute-start(bf16[512,1024]{1,0:T(8,128)(2,1)} %copy-done.1), channel_id=1, source_target_pairs={{16,20},{20,16},{24,28},{28,24},{17,21},{21,17},{25,29},{29,25},{1... | collective-permute-start | bytes 3145736 | tf_op jit(solution)/shard_map/ppermute | solution.py:70
  84.8 26.6 %collective-permute-start.12 = (bf16[512,1024]{1,0:T(8,128)(2,1)S(1)}, bf16[512,1024]{1,0:T(8,128)(2,1)S(1)}, u32[]{:S(2)}, u32[]{:S(2)}) collective-permute-start(bf16[512,1024]{1,0:T(8,128)(2,1)S(1)} %collective-permute-done.2), channel_id=1, source_target_pairs={{8,12},{12,8},{16,20},{20,16},{24,28},{28,24},{9,13},{13,9},{17,21... | collective-permute-start | bytes 3145736 | tf_op jit(solution)/shard_map/ppermute | solution.py:70
  85.5 41.7 %collective-permute-start.11 = (bf16[512,1024]{1,0:T(8,128)(2,1)}, bf16[512,1024]{1,0:T(8,128)(2,1)S(1)}, u32[]{:S(2)}, u32[]{:S(2)}) collective-permute-start(bf16[512,1024]{1,0:T(8,128)(2,1)} %collective-permute-done.10), channel_id=1, source_target_pairs={{0,4},{4,0},{1,5},{5,1},{2,6},{6,2},{3,7},{7,3}} | collective-permute-start | bytes 3145736 | tf_op jit(solution)/shard_map/ppermute | solution.py:70
  91.6 15.6 %copy-start.2 = (bf16[512,1024]{1,0:T(8,128)(2,1)S(1)}, bf16[512,1024]{1,0:T(8,128)(2,1)}, u32[]{:S(2)}) copy-start(bf16[512,1024]{1,0:T(8,128)(2,1)} %copy-done.1) | copy-start | bytes 3145732
  129.3 5.5 %copy-start.5 = (bf16[512,1024]{1,0:T(8,128)(2,1)S(1)}, bf16[512,1024]{1,0:T(8,128)(2,1)}, u32[]{:S(2)}) copy-start(bf16[512,1024]{1,0:T(8,128)(2,1)} %param.4) | copy-start | bytes 3145732
  129.3 5.5 %copy-start.6 = (f32[1024]{0:T(1024)S(1)}, f32[1024]{0:T(1024)}, u32[]{:S(2)}) copy-start(f32[1024]{0:T(1024)} %param.6) | copy-start | bytes 12292
  131.6 3.3 %copy-start.4 = (bf16[4096,1024]{1,0:T(8,128)(2,1)}, bf16[4096,1024]{1,0:T(8,128)(2,1)S(1)}, u32[]{:S(2)}) copy-start(bf16[4096,1024]{1,0:T(8,128)(2,1)S(1)} %select_dynamic-update-slice_fusion) | copy-start | bytes 25165828
  137.4 4.7 %collective-permute-start.14 = (f32[512,1024]{1,0:T(8,128)}, f32[512,1024]{1,0:T(8,128)}, u32[]{:S(2)}, u32[]{:S(2)}) collective-permute-start(f32[512,1024]{1,0:T(8,128)} %fusion.10), channel_id=1, source_target_pairs={{0,1},{1,0},{2,3},{3,2},{4,5},{5,4},{6,7},{7,6},{8,9},{9,8},{10,11... | collective-permute-start | bytes 6291464 | tf_op jit(solution)/shard_map/ppermute | solution.py:142
  141.7 6.7 %collective-permute-start.13 = (f32[512,1024]{1,0:T(8,128)}, f32[512,1024]{1,0:T(8,128)}, u32[]{:S(2)}, u32[]{:S(2)}) collective-permute-start(f32[512,1024]{1,0:T(8,128)} %fusion.14), channel_id=1, source_target_pairs={{0,1},{1,0},{2,3},{3,2},{4,5},{5,4},{6,7},{7,6},{8,9},{9,8},{10,11... | collective-permute-start | bytes 6291464 | tf_op jit(solution)/shard_map/ppermute | solution.py:142
  142.2 30.1 %copy-start.3 = (f32[512,1024]{1,0:T(8,128)S(1)}, f32[512,1024]{1,0:T(8,128)}, u32[]{:S(2)}) copy-start(f32[512,1024]{1,0:T(8,128)} %param.7) | copy-start | bytes 6291460
  146.9 25.4 %collective-permute-start.15 = (bf16[512,1024]{1,0:T(8,128)(2,1)}, bf16[512,1024]{1,0:T(8,128)(2,1)}, u32[]{:S(2)}, u32[]{:S(2)}) collective-permute-start(bf16[512,1024]{1,0:T(8,128)(2,1)} %add_convert_fusion), channel_id=1, source_target_pairs={{0,2},{1,3},{2,0},{3,1},{4,6},{5,7},{6,4},{7,5},{8,10},{9,11},{10,... | collective-permute-start | bytes 3145736 | tf_op jit(solution)/shard_map/ppermute | solution.py:145
  177.1 24.4 %collective-permute-start.16 = (bf16[512,1024]{1,0:T(8,128)(2,1)}, bf16[512,1024]{1,0:T(8,128)(2,1)S(1)}, u32[]{:S(2)}, u32[]{:S(2)}) collective-permute-start(bf16[512,1024]{1,0:T(8,128)(2,1)} %multiply_convert_fusion), channel_id=1, source_target_pairs={{0,2},{1,3},{2,0},{3,1},{4,6},{5,7},{6,4},{7,5},{8,10},{9,11},{10,... | collective-permute-start | bytes 3145736 | tf_op jit(solution)/shard_map/ppermute | solution.py:154
  178.6 25.8 %collective-permute-start.17 = (bf16[512,1024]{1,0:T(8,128)(2,1)}, bf16[512,1024]{1,0:T(8,128)(2,1)S(1)}, u32[]{:S(2)}, u32[]{:S(2)}) collective-permute-start(bf16[512,1024]{1,0:T(8,128)(2,1)} %multiply_convert_fusion), channel_id=1, source_target_pairs={{0,1},{1,0},{2,3},{3,2},{4,5},{5,4},{6,7},{7,6},{8,9},{9,8},{10,11... | collective-permute-start | bytes 3145736 | tf_op jit(solution)/shard_map/ppermute | solution.py:155
  201.6 5.9 %collective-permute-start.18 = (bf16[512,1024]{1,0:T(8,128)(2,1)S(1)}, bf16[512,1024]{1,0:T(8,128)(2,1)}, u32[]{:S(2)}, u32[]{:S(2)}) collective-permute-start(bf16[512,1024]{1,0:T(8,128)(2,1)S(1)} %collective-permute-done.16), channel_id=1, source_target_pairs={{0,1},{1,0},{2,3},{3,2},{4,5},{5,4},{6,7},{7,6},{8,9},{9,8},{10,11... | collective-permute-start | bytes 3145736 | tf_op jit(solution)/shard_map/ppermute | solution.py:155
  214.2 3.7 %collective-permute-start.19 = (f32[1024]{0:T(1024)S(1)}, f32[1024]{0:T(1024)S(1)}, u32[]{:S(2)}, u32[]{:S(2)}) collective-permute-start(f32[1024]{0:T(1024)S(1)} %fusion.1), channel_id=1, source_target_pairs={{0,4},{4,0},{8,12},{12,8},{16,20},{20,16},{24,28},{28,24},{1,5},{5... | collective-permute-start | bytes 12296 | tf_op jit(solution)/shard_map/ppermute | solution.py:88
  217.9 20.6 %collective-permute-start.20 = (f32[1024]{0:T(1024)S(1)}, f32[1024]{0:T(1024)S(1)}, u32[]{:S(2)}, u32[]{:S(2)}) collective-permute-start(f32[1024]{0:T(1024)S(1)} %add.160), channel_id=1, source_target_pairs={{0,8},{4,12},{8,0},{12,4},{16,24},{20,28},{24,16},{28,20},{1,9},{5... | collective-permute-start | bytes 12296 | tf_op jit(solution)/shard_map/ppermute | solution.py:88
  238.4 7.9 %collective-permute-start.21 = (f32[1024]{0:T(1024)S(1)}, f32[1024]{0:T(1024)S(1)}, u32[]{:S(2)}, u32[]{:S(2)}) collective-permute-start(f32[1024]{0:T(1024)S(1)} %add.161), channel_id=1, source_target_pairs={{0,16},{4,20},{8,24},{12,28},{16,0},{20,4},{24,8},{28,12},{1,17},{... | collective-permute-start | bytes 12296 | tf_op jit(solution)/shard_map/ppermute | solution.py:88

commit v7 on v6

--- a/solution.py
+++ b/solution.py
@@ -5,7 +5,7 @@
 from jax import lax
 from jax.sharding import PartitionSpec as P
 
-CHUNKS = 1
+CHUNKS = 4
 
 
 def _rows(a, blk, n):

time: 248 us -> 269 us (1.085)
  starting transfers between devices: 55.7 us -> 122 us
  waiting for transfers between devices: 142 us -> 84.8 us
  matrix products: 28.9 us -> 38.3 us
    ppermute x6 -> x24, waiting for transfers between devices: 46.5 us -> 5.87 us  [_gather_src(): got[sign, s] = (cur, lax.ppermute(cur, 'src', cross(sign, s)))]
    ppermute x6 -> x24, starting transfers between devices: 11.3 us -> 48.4 us  [_gather_src(): cur = lax.ppermute(cur, 'src', pairs)]
    ppermute x6 -> x24, starting transfers between devices: 12.5 us -> 44.5 us  [_gather_src(): got[sign, s] = (cur, lax.ppermute(cur, 'src', cross(sign, s)))]
    ppermute x3, starting transfers between devices: 26.8 us -> 8.89 us  [_sum_over_src(): v = v + lax.ppermute(v, 'src', [(i, i ^ b) for i in range(n)])]
    ppermute x6 -> x24, waiting for transfers between devices: 43 us -> 27.2 us  [_gather_src(): cur = lax.ppermute(cur, 'src', pairs)]
    dot_general x4 -> x16, matrix products: 12.5 us -> 26.3 us  [per_device(): jnp.dot(w, _rows(adj, rel(blk), n), preferred_element_type=jnp.float32)]
    ppermute x1 -> x4, waiting for transfers between devices: 23.9 us -> 16.8 us  [per_device(): lax.ppermute(halves[k].astype(jnp.bfloat16), 'vox', chip_perm(k))]
    ppermute x1 -> x4, starting transfers between devices: 1.49 us -> 6.27 us  [per_device(): lax.ppermute(halves[k].astype(jnp.bfloat16), 'vox', chip_perm(k))]
  transfers between devices with their start and end apart: 22 -> 79, of which waited for: 11 -> 26; matrix products, arithmetic and copies ran while one was open for 11% -> 18% of each run, Pallas kernels for 0% -> 0%
where the time goes in v7:
time: 269 us; the launch traced here: 268 us
  starting transfers between devices  122 us (45%)
  waiting for transfers between devices  84.8 us (32%)
  matrix products  38.3 us (14%)
  other arithmetic  15.2 us (6%)
  local copies, waits for them, and re-layouts  6.7 us (2%)
    ppermute x24, starting transfers between devices, _gather_src(): cur = lax.ppermute(cur, 'src', pairs)  48.4 us
    ppermute x24, starting transfers between devices, _gather_src(): got[sign, s] = (cur, lax.ppermute(cur, 'src', cross(sign, s)))  44.5 us
    ppermute x24, waiting for transfers between devices, _gather_src(): cur = lax.ppermute(cur, 'src', pairs)  27.2 us
    dot_general x16, matrix products, per_device(): jnp.dot(w, _rows(adj, rel(blk), n), preferred_element_type=jnp.float32)  26.3 us
    ppermute x4, waiting for transfers between devices, per_device(): got.append((2 * ((q - k) % m) + par, lax.ppermute(wt, 'vox', chip_perm(k))))  20.3 us
    ppermute x4, waiting for transfers between devices, per_device(): lax.ppermute(halves[k].astype(jnp.bfloat16), 'vox', chip_perm(k))  16.8 us
    unnamed x25, other arithmetic  13.2 us
    dot_general x16, matrix products, pblock(): lax.dot_general(scaled, _rows(adj, rel(blk), n), (((1,), (1,)), ((), ()))...  12 us
  transfers between devices with their start and end apart: 79, of which 26 were waited for; matrix products, arithmetic and copies ran while one was open for 18% of the time, Pallas kernels for 0%

profile of v7, /device:TPU:0, one launch (start us, length us, event | category | flops | bytes accessed | tf_op | source)
XLA Modules:
  0.0 267.7 jit_solution(95752986448018163)
XLA Ops:
  0.0 1.7 slice.26
  1.7 5.6 %collective-permute-start.15 = (bf16[128,1024]{1,0:T(8,128)(2,1)}, bf16[128,1024]{1,0:T(8,128)(2,1)}, u32[]{:S(2)}, u32[]{:S(2)}) collective-permute-start(bf16[128,1024]{1,0:T(8,128)(2,1)} %slice.26), channel_id=1, source_target_pairs={{0,8},{4,12},{8,16},{12,20},{16,24},{20,28},{1,9},{5,13},{9,17},{1... | collective-permute-start | bytes 786440 | tf_op jit(solution)/shard_map/ppermute | solution.py:69
  10.1 3.1 %reshape.16 = f32[512,2,512]{2,1,0:T(2,128)S(1)} reshape(f32[512,1024]{1,0:T(8,128)} %param.7) | data formatting | bytes 4194304 | tf_op jit(solution)/shard_map/reshape | solution.py:114
  22.0 1.9 fusion.121
  23.9 2.8 %collective-permute-done = bf16[128,1024]{1,0:T(8,128)(2,1)} collective-permute-done((bf16[128,1024]{1,0:T(8,128)(2,1)}, bf16[128,1024]{1,0:T(8,128)(2,1)}, u32[]{:S(2)}, u32[]{:S(2)}) %collective-permute-start) | collective-permute-done | bytes 262176 | tf_op jit(solution)/shard_map/ppermute | solution.py:72
  26.7 6.1 %collective-permute-start.2 = (bf16[128,1024]{1,0:T(8,128)(2,1)}, bf16[128,1024]{1,0:T(8,128)(2,1)S(1)}, u32[]{:S(2)}, u32[]{:S(2)}) collective-permute-start(bf16[128,1024]{1,0:T(8,128)(2,1)} %get-tuple-element.40), channel_id=1, source_target_pairs={{0,8},{4,12},{8,16},{12,20},{16,24},{20,28},{1,9},{5,13},{9,17},{1... | collective-permute-start | bytes 786440 | tf_op jit(solution)/shard_map/ppermute | solution.py:69
  34.2 4.0 %collective-permute-start.18 = (bf16[128,1024]{1,0:T(8,128)(2,1)}, bf16[128,1024]{1,0:T(8,128)(2,1)S(1)}, u32[]{:S(2)}, u32[]{:S(2)}) collective-permute-start(bf16[128,1024]{1,0:T(8,128)(2,1)} %collective-permute-done.14), channel_id=1, source_target_pairs={{0,4},{4,0},{8,12},{12,8},{16,20},{20,16},{1,5},{5,1},{9,13},{13,9... | collective-permute-start | bytes 786440 | tf_op jit(solution)/shard_map/ppermute | solution.py:70
  43.4 3.9 %collective-permute-done.20 = bf16[128,1024]{1,0:T(8,128)(2,1)S(1)} collective-permute-done((bf16[128,1024]{1,0:T(8,128)(2,1)}, bf16[128,1024]{1,0:T(8,128)(2,1)S(1)}, u32[]{:S(2)}, u32[]{:S(2)}) %collective-permute-start.20) | collective-permute-done | bytes 262176 | tf_op jit(solution)/shard_map/ppermute | solution.py:69
  47.3 3.6 %collective-permute-start.21 = (bf16[128,1024]{1,0:T(8,128)(2,1)S(1)}, bf16[128,1024]{1,0:T(8,128)(2,1)S(1)}, u32[]{:S(2)}, u32[]{:S(2)}) collective-permute-start(bf16[128,1024]{1,0:T(8,128)(2,1)S(1)} %collective-permute-done.20), channel_id=1, source_target_pairs={{0,4},{4,0},{8,12},{12,8},{1,5},{5,1},{9,13},{13,9},{2,6},{6,2},{1... | collective-permute-start | bytes 786440 | tf_op jit(solution)/shard_map/ppermute | solution.py:70
  52.3 1.8 select_dynamic-update-slice_fusion.21
  54.1 1.8 select_dynamic-update-slice_fusion.20
  55.9 4.6 %collective-permute-start.34 = (bf16[128,1024]{1,0:T(8,128)(2,1)}, bf16[128,1024]{1,0:T(8,128)(2,1)S(1)}, u32[]{:S(2)}, u32[]{:S(2)}) collective-permute-start(bf16[128,1024]{1,0:T(8,128)(2,1)} %get-tuple-element.42), channel_id=1, source_target_pairs={{0,8},{4,12},{8,16},{12,20},{16,24},{20,28},{1,9},{5,13},{9,17},{1... | collective-permute-start | bytes 786440 | tf_op jit(solution)/shard_map/ppermute | solution.py:69
  61.9 2.2 collective-permute-start.24
  67.2 3.7 %collective-permute-start.5 = (bf16[128,1024]{1,0:T(8,128)(2,1)S(1)}, bf16[128,1024]{1,0:T(8,128)(2,1)S(1)}, u32[]{:S(2)}, u32[]{:S(2)}) collective-permute-start(bf16[128,1024]{1,0:T(8,128)(2,1)S(1)} %collective-permute-done.1), channel_id=1, source_target_pairs={{0,4},{4,0},{8,12},{12,8},{16,20},{20,16},{1,5},{5,1},{9,13},{13,9... | collective-permute-start | bytes 786440 | tf_op jit(solution)/shard_map/ppermute | solution.py:70
  81.1 2.6 collective-permute-start.8
  85.3 9.8 %collective-permute-start.53 = (bf16[128,1024]{1,0:T(8,128)(2,1)}, bf16[128,1024]{1,0:T(8,128)(2,1)S(1)}, u32[]{:S(2)}, u32[]{:S(2)}) collective-permute-start(bf16[128,1024]{1,0:T(8,128)(2,1)} %get-tuple-element.41), channel_id=1, source_target_pairs={{0,8},{4,12},{8,16},{12,20},{16,24},{20,28},{1,9},{5,13},{9,17},{1... | collective-permute-start | bytes 786440 | tf_op jit(solution)/shard_map/ppermute | solution.py:69
  97.2 2.6 collective-permute-start.11
  101.4 3.3 %collective-permute-start.37 = (bf16[128,1024]{1,0:T(8,128)(2,1)S(1)}, bf16[128,1024]{1,0:T(8,128)(2,1)S(1)}, u32[]{:S(2)}, u32[]{:S(2)}) collective-permute-start(bf16[128,1024]{1,0:T(8,128)(2,1)S(1)} %collective-permute-done.33), channel_id=1, source_target_pairs={{0,4},{4,0},{8,12},{12,8},{16,20},{20,16},{1,5},{5,1},{9,13},{13,9... | collective-permute-start | bytes 786440 | tf_op jit(solution)/shard_map/ppermute | solution.py:70
  107.2 2.5 collective-permute-done.37
  110.4 5.9 %collective-permute-done.39 = bf16[128,1024]{1,0:T(8,128)(2,1)S(1)} collective-permute-done((bf16[128,1024]{1,0:T(8,128)(2,1)S(1)}, bf16[128,1024]{1,0:T(8,128)(2,1)S(1)}, u32[]{:S(2)}, u32[]{:S(2)}) %collective-permute-start.39) | collective-permute-done | bytes 262176 | tf_op jit(solution)/shard_map/ppermute | solution.py:69
  116.3 2.1 collective-permute-start.40
  121.5 3.0 %collective-permute-done.40 = bf16[128,1024]{1,0:T(8,128)(2,1)S(1)} collective-permute-done((bf16[128,1024]{1,0:T(8,128)(2,1)S(1)}, bf16[128,1024]{1,0:T(8,128)(2,1)S(1)}, u32[]{:S(2)}, u32[]{:S(2)}) %collective-permute-start.40) | collective-permute-done | bytes 262176 | tf_op jit(solution)/shard_map/ppermute | solution.py:70
  125.9 5.4 %collective-permute-done.42 = bf16[128,1024]{1,0:T(8,128)(2,1)S(1)} collective-permute-done((bf16[128,1024]{1,0:T(8,128)(2,1)S(1)}, bf16[128,1024]{1,0:T(8,128)(2,1)S(1)}, u32[]{:S(2)}, u32[]{:S(2)}) %collective-permute-start.42) | collective-permute-done | bytes 262176 | tf_op jit(solution)/shard_map/ppermute | solution.py:69
  131.3 2.2 collective-permute-start.43
  133.8 3.6 %collective-permute-start.56 = (bf16[128,1024]{1,0:T(8,128)(2,1)S(1)}, bf16[128,1024]{1,0:T(8,128)(2,1)S(1)}, u32[]{:S(2)}, u32[]{:S(2)}) collective-permute-start(bf16[128,1024]{1,0:T(8,128)(2,1)S(1)} %collective-permute-done.52), channel_id=1, source_target_pairs={{0,4},{4,0},{8,12},{12,8},{16,20},{20,16},{1,5},{5,1},{9,13},{13,9... | collective-permute-start | bytes 786440 | tf_op jit(solution)/shard_map/ppermute | solution.py:70
  138.2 2.8 %collective-permute-done.58 = bf16[128,1024]{1,0:T(8,128)(2,1)S(1)} collective-permute-done((bf16[128,1024]{1,0:T(8,128)(2,1)S(1)}, bf16[128,1024]{1,0:T(8,128)(2,1)S(1)}, u32[]{:S(2)}, u32[]{:S(2)}) %collective-permute-start.58) | collective-permute-done | bytes 262176 | tf_op jit(solution)/shard_map/ppermute | solution.py:69
  141.7 2.9 %collective-permute-start.59 = (bf16[128,1024]{1,0:T(8,128)(2,1)S(1)}, bf16[128,1024]{1,0:T(8,128)(2,1)S(1)}, u32[]{:S(2)}, u32[]{:S(2)}) collective-permute-start(bf16[128,1024]{1,0:T(8,128)(2,1)S(1)} %collective-permute-done.58), channel_id=1, source_target_pairs={{0,4},{4,0},{8,12},{12,8},{1,5},{5,1},{9,13},{13,9},{2,6},{6,2},{1... | collective-permute-start | bytes 786440 | tf_op jit(solution)/shard_map/ppermute | solution.py:70
  150.7 7.2 %collective-permute-done.61 = bf16[128,1024]{1,0:T(8,128)(2,1)S(1)} collective-permute-done((bf16[128,1024]{1,0:T(8,128)(2,1)S(1)}, bf16[128,1024]{1,0:T(8,128)(2,1)S(1)}, u32[]{:S(2)}, u32[]{:S(2)}) %collective-permute-start.61) | collective-permute-done | bytes 262176 | tf_op jit(solution)/shard_map/ppermute | solution.py:69
  158.6 3.5 %collective-permute-start.62 = (bf16[128,1024]{1,0:T(8,128)(2,1)S(1)}, bf16[128,1024]{1,0:T(8,128)(2,1)S(1)}, u32[]{:S(2)}, u32[]{:S(2)}) collective-permute-start(bf16[128,1024]{1,0:T(8,128)(2,1)S(1)} %collective-permute-done.61), channel_id=1, source_target_pairs={{0,4},{4,0},{1,5},{5,1},{2,6},{6,2},{3,7},{7,3}} | collective-permute-start | bytes 786440 | tf_op jit(solution)/shard_map/ppermute | solution.py:70
  165.6 5.9 %collective-permute-done.29 = bf16[512,256]{1,0:T(8,128)(2,1)S(1)} collective-permute-done((bf16[512,256]{1,0:T(8,128)(2,1)S(1)}, bf16[512,256]{1,0:T(8,128)(2,1)S(1)}, u32[]{:S(2)}, u32[]{:S(2)}) %collective-permute-start.29) | collective-permute-done | bytes 262176 | tf_op jit(solution)/shard_map/ppermute | solution.py:154
  179.7 5.3 %collective-permute-done.47 = bf16[512,256]{1,0:T(8,128)(2,1)S(1)} collective-permute-done((bf16[512,256]{1,0:T(8,128)(2,1)S(1)}, bf16[512,256]{1,0:T(8,128)(2,1)S(1)}, u32[]{:S(2)}, u32[]{:S(2)}) %collective-permute-start.47) | collective-permute-done | bytes 262176 | tf_op jit(solution)/shard_map/ppermute | solution.py:145
  188.7 4.4 %collective-permute-done.48 = bf16[512,256]{1,0:T(8,128)(2,1)S(1)} collective-permute-done((bf16[512,256]{1,0:T(8,128)(2,1)S(1)}, bf16[512,256]{1,0:T(8,128)(2,1)S(1)}, u32[]{:S(2)}, u32[]{:S(2)}) %collective-permute-start.48) | collective-permute-done | bytes 262176 | tf_op jit(solution)/shard_map/ppermute | solution.py:154
  197.8 1.6 collective-permute-start.66
  199.8 6.6 %collective-permute-done.66 = bf16[512,256]{1,0:T(8,128)(2,1)S(1)} collective-permute-done((bf16[512,256]{1,0:T(8,128)(2,1)S(1)}, bf16[512,256]{1,0:T(8,128)(2,1)S(1)}, u32[]{:S(2)}, u32[]{:S(2)}) %collective-permute-start.66) | collective-permute-done | bytes 262176 | tf_op jit(solution)/shard_map/ppermute | solution.py:145
  209.0 5.7 %collective-permute-done.67 = bf16[512,256]{1,0:T(8,128)(2,1)S(1)} collective-permute-done((bf16[512,256]{1,0:T(8,128)(2,1)S(1)}, bf16[512,256]{1,0:T(8,128)(2,1)S(1)}, u32[]{:S(2)}, u32[]{:S(2)}) %collective-permute-start.67) | collective-permute-done | bytes 262176 | tf_op jit(solution)/shard_map/ppermute | solution.py:154
  218.3 1.8 fusion.35
  220.1 1.8 fusion.33
  224.0 2.0 fusion.31
  226.0 4.8 %collective-permute-done.72 = bf16[512,256]{1,0:T(8,128)(2,1)S(1)} collective-permute-done((bf16[512,256]{1,0:T(8,128)(2,1)S(1)}, bf16[512,256]{1,0:T(8,128)(2,1)S(1)}, u32[]{:S(2)}, u32[]{:S(2)}) %collective-permute-start.72) | collective-permute-done | bytes 262176 | tf_op jit(solution)/shard_map/ppermute | solution.py:145
  232.9 1.8 fusion.23
  234.7 4.3 %collective-permute-done.73 = bf16[512,256]{1,0:T(8,128)(2,1)S(1)} collective-permute-done((bf16[512,256]{1,0:T(8,128)(2,1)S(1)}, bf16[512,256]{1,0:T(8,128)(2,1)S(1)}, u32[]{:S(2)}, u32[]{:S(2)}) %collective-permute-start.73) | collective-permute-done | bytes 262176 | tf_op jit(solution)/shard_map/ppermute | solution.py:154
  239.0 1.9 fusion.21
  240.8 1.7 fusion.19
  242.6 7.1 %fusion.1 = f32[1024]{0:T(1024)S(1)} fusion(bf16[512,1024]{1,0:T(8,128)(2,1)S(1)} %copy-done, f32[512,1024]{1,0:T(8,128)} %fusion.19, f32[512,1024]{1,0:T(8,128)} %fusion.21, f32[512,1024]{1,0:T(8,128)} %fusion.23, f32[512,1024]{1,0:T(8,128)} %fusion.31, f32[512,1024]{1,0:T(8,128)} %fusion.33, f32[512,1024]{1,0:T(8,128)} %fusion.35, ...), kind=kOutput, calls=%fused_computation.3 | convolution fusion | flops 277871616 | bytes 33296388 | tf_op jit(solution)/shard_map/dot_general | solution.py:161
  250.0 3.4 %collective-permute-done.76 = f32[1024]{0:T(1024)S(1)} collective-permute-done((f32[1024]{0:T(1024)S(1)}, f32[1024]{0:T(1024)S(1)}, u32[]{:S(2)}, u32[]{:S(2)}) %collective-permute-start.76) | collective-permute-done | bytes 4128 | tf_op jit(solution)/shard_map/ppermute | solution.py:88
  253.4 3.6 %collective-permute-done.77 = f32[1024]{0:T(1024)S(1)} collective-permute-done((f32[1024]{0:T(1024)S(1)}, f32[1024]{0:T(1024)S(1)}, u32[]{:S(2)}, u32[]{:S(2)}) %collective-permute-start.77) | collective-permute-done | bytes 4128 | tf_op jit(solution)/shard_map/ppermute | solution.py:88
  257.0 8.6 %collective-permute-start.78 = (f32[1024]{0:T(1024)S(1)}, f32[1024]{0:T(1024)S(1)}, u32[]{:S(2)}, u32[]{:S(2)}) collective-permute-start(f32[1024]{0:T(1024)S(1)} %add.341), channel_id=1, source_target_pairs={{0,16},{4,20},{8,24},{12,28},{16,0},{20,4},{24,8},{28,12},{1,17},{... | collective-permute-start | bytes 12296 | tf_op jit(solution)/shard_map/ppermute | solution.py:88
  265.6 1.6 collective-permute-done.78
  (193 shorter events, 86.4 us)
Async XLA Ops:
  1.7 11.6 %collective-permute-start.15 = (bf16[128,1024]{1,0:T(8,128)(2,1)}, bf16[128,1024]{1,0:T(8,128)(2,1)}, u32[]{:S(2)}, u32[]{:S(2)}) collective-permute-start(bf16[128,1024]{1,0:T(8,128)(2,1)} %slice.26), channel_id=1, source_target_pairs={{0,8},{4,12},{8,16},{12,20},{16,24},{20,28},{1,9},{5,13},{9,17},{1... | collective-permute-start | bytes 786440 | tf_op jit(solution)/shard_map/ppermute | solution.py:69
  8.8 24.0 %collective-permute-start.14 = (bf16[128,1024]{1,0:T(8,128)(2,1)}, bf16[128,1024]{1,0:T(8,128)(2,1)}, u32[]{:S(2)}, u32[]{:S(2)}) collective-permute-start(bf16[128,1024]{1,0:T(8,128)(2,1)} %slice.26), channel_id=1, source_target_pairs={{8,0},{12,4},{16,8},{20,12},{24,16},{28,20},{9,1},{13,5},{17,9},{2... | collective-permute-start | bytes 786440 | tf_op jit(solution)/shard_map/ppermute | solution.py:69
  17.1 9.6 %collective-permute-start = (bf16[128,1024]{1,0:T(8,128)(2,1)}, bf16[128,1024]{1,0:T(8,128)(2,1)}, u32[]{:S(2)}, u32[]{:S(2)}) collective-permute-start(bf16[128,1024]{1,0:T(8,128)(2,1)} %get-tuple-element.40), channel_id=1, source_target_pairs={{0,4},{4,0},{8,12},{12,8},{16,20},{20,16},{24,28},{28,24},{1,5},{5... | collective-permute-start | bytes 786440 | tf_op jit(solution)/shard_map/ppermute | solution.py:72
  18.6 15.6 %collective-permute-start.32 = (bf16[128,1024]{1,0:T(8,128)(2,1)}, bf16[128,1024]{1,0:T(8,128)(2,1)S(1)}, u32[]{:S(2)}, u32[]{:S(2)}) collective-permute-start(bf16[128,1024]{1,0:T(8,128)(2,1)} %get-tuple-element.42), channel_id=1, source_target_pairs={{0,4},{4,0},{8,12},{12,8},{16,20},{20,16},{24,28},{28,24},{1,5},{5... | collective-permute-start | bytes 786440 | tf_op jit(solution)/shard_map/ppermute | solution.py:72
  19.1 19.1 %collective-permute-start.51 = (bf16[128,1024]{1,0:T(8,128)(2,1)}, bf16[128,1024]{1,0:T(8,128)(2,1)}, u32[]{:S(2)}, u32[]{:S(2)}) collective-permute-start(bf16[128,1024]{1,0:T(8,128)(2,1)} %get-tuple-element.41), channel_id=1, source_target_pairs={{0,4},{4,0},{8,12},{12,8},{16,20},{20,16},{24,28},{28,24},{1,5},{5... | collective-permute-start | bytes 786440 | tf_op jit(solution)/shard_map/ppermute | solution.py:72
  20.7 18.9 %collective-permute-start.17 = (bf16[128,1024]{1,0:T(8,128)(2,1)}, bf16[128,1024]{1,0:T(8,128)(2,1)}, u32[]{:S(2)}, u32[]{:S(2)}) collective-permute-start(bf16[128,1024]{1,0:T(8,128)(2,1)} %collective-permute-done.16), channel_id=1, source_target_pairs={{16,24},{20,28},{17,25},{21,29},{18,26},{22,30},{19,27},{23,31}} | collective-permute-start | bytes 786440 | tf_op jit(solution)/shard_map/ppermute | solution.py:69
  26.7 29.3 %collective-permute-start.2 = (bf16[128,1024]{1,0:T(8,128)(2,1)}, bf16[128,1024]{1,0:T(8,128)(2,1)S(1)}, u32[]{:S(2)}, u32[]{:S(2)}) collective-permute-start(bf16[128,1024]{1,0:T(8,128)(2,1)} %get-tuple-element.40), channel_id=1, source_target_pairs={{0,8},{4,12},{8,16},{12,20},{16,24},{20,28},{1,9},{5,13},{9,17},{1... | collective-permute-start | bytes 786440 | tf_op jit(solution)/shard_map/ppermute | solution.py:69
  32.9 34.3 %collective-permute-start.1 = (bf16[128,1024]{1,0:T(8,128)(2,1)}, bf16[128,1024]{1,0:T(8,128)(2,1)S(1)}, u32[]{:S(2)}, u32[]{:S(2)}) collective-permute-start(bf16[128,1024]{1,0:T(8,128)(2,1)} %get-tuple-element.40), channel_id=1, source_target_pairs={{8,0},{12,4},{16,8},{20,12},{24,16},{28,20},{9,1},{13,5},{17,9},{2... | collective-permute-start | bytes 786440 | tf_op jit(solution)/shard_map/ppermute | solution.py:69
  34.2 8.6 %collective-permute-start.18 = (bf16[128,1024]{1,0:T(8,128)(2,1)}, bf16[128,1024]{1,0:T(8,128)(2,1)S(1)}, u32[]{:S(2)}, u32[]{:S(2)}) collective-permute-start(bf16[128,1024]{1,0:T(8,128)(2,1)} %collective-permute-done.14), channel_id=1, source_target_pairs={{0,4},{4,0},{8,12},{12,8},{16,20},{20,16},{1,5},{5,1},{9,13},{13,9... | collective-permute-start | bytes 786440 | tf_op jit(solution)/shard_map/ppermute | solution.py:70
  38.2 9.1 %collective-permute-start.20 = (bf16[128,1024]{1,0:T(8,128)(2,1)}, bf16[128,1024]{1,0:T(8,128)(2,1)S(1)}, u32[]{:S(2)}, u32[]{:S(2)}) collective-permute-start(bf16[128,1024]{1,0:T(8,128)(2,1)} %collective-permute-done.14), channel_id=1, source_target_pairs={{8,0},{12,4},{16,8},{20,12},{9,1},{13,5},{17,9},{21,13},{10,2},{14... | collective-permute-start | bytes 786440 | tf_op jit(solution)/shard_map/ppermute | solution.py:69
  39.5 11.5 %collective-permute-start.19 = (bf16[128,1024]{1,0:T(8,128)(2,1)}, bf16[128,1024]{1,0:T(8,128)(2,1)S(1)}, u32[]{:S(2)}, u32[]{:S(2)}) collective-permute-start(bf16[128,1024]{1,0:T(8,128)(2,1)} %collective-permute-done.17), channel_id=1, source_target_pairs={{24,28},{28,24},{25,29},{29,25},{26,30},{30,26},{27,31},{31,27}} | collective-permute-start | bytes 786440 | tf_op jit(solution)/shard_map/ppermute | solution.py:70
  42.8 18.5 %collective-permute-start.22 = (bf16[128,1024]{1,0:T(8,128)(2,1)}, bf16[128,1024]{1,0:T(8,128)(2,1)S(1)}, u32[]{:S(2)}, u32[]{:S(2)}) collective-permute-start(bf16[128,1024]{1,0:T(8,128)(2,1)} %collective-permute-done.16), channel_id=1, source_target_pairs={{16,20},{20,16},{24,28},{28,24},{17,21},{21,17},{25,29},{29,25},{1... | collective-permute-start | bytes 786440 | tf_op jit(solution)/shard_map/ppermute | solution.py:70
  47.3 13.2 %collective-permute-start.21 = (bf16[128,1024]{1,0:T(8,128)(2,1)S(1)}, bf16[128,1024]{1,0:T(8,128)(2,1)S(1)}, u32[]{:S(2)}, u32[]{:S(2)}) collective-permute-start(bf16[128,1024]{1,0:T(8,128)(2,1)S(1)} %collective-permute-done.20), channel_id=1, source_target_pairs={{0,4},{4,0},{8,12},{12,8},{1,5},{5,1},{9,13},{13,9},{2,6},{6,2},{1... | collective-permute-start | bytes 786440 | tf_op jit(solution)/shard_map/ppermute | solution.py:70
  51.0 10.9 %collective-permute-start.23 = (bf16[128,1024]{1,0:T(8,128)(2,1)S(1)}, bf16[128,1024]{1,0:T(8,128)(2,1)S(1)}, u32[]{:S(2)}, u32[]{:S(2)}) collective-permute-start(bf16[128,1024]{1,0:T(8,128)(2,1)S(1)} %collective-permute-done.20), channel_id=1, source_target_pairs={{8,0},{12,4},{9,1},{13,5},{10,2},{14,6},{11,3},{15,7}} | collective-permute-start | bytes 786440 | tf_op jit(solution)/shard_map/ppermute | solution.py:69
  55.9 14.9 %collective-permute-start.34 = (bf16[128,1024]{1,0:T(8,128)(2,1)}, bf16[128,1024]{1,0:T(8,128)(2,1)S(1)}, u32[]{:S(2)}, u32[]{:S(2)}) collective-permute-start(bf16[128,1024]{1,0:T(8,128)(2,1)} %get-tuple-element.42), channel_id=1, source_target_pairs={{0,8},{4,12},{8,16},{12,20},{16,24},{20,28},{1,9},{5,13},{9,17},{1... | collective-permute-start | bytes 786440 | tf_op jit(solution)/shard_map/ppermute | solution.py:69
  61.2 11.0 %collective-permute-start.3 = (bf16[128,1024]{1,0:T(8,128)(2,1)S(1)}, bf16[128,1024]{1,0:T(8,128)(2,1)S(1)}, u32[]{:S(2)}, u32[]{:S(2)}) collective-permute-start(bf16[128,1024]{1,0:T(8,128)(2,1)S(1)} %collective-permute-done.2), channel_id=1, source_target_pairs={{8,16},{12,20},{16,24},{20,28},{9,17},{13,21},{17,25},{21,29},{10,... | collective-permute-start | bytes 786440 | tf_op jit(solution)/shard_map/ppermute | solution.py:69
  61.9 11.0 %collective-permute-start.24 = (bf16[128,1024]{1,0:T(8,128)(2,1)S(1)}, bf16[128,1024]{1,0:T(8,128)(2,1)S(1)}, u32[]{:S(2)}, u32[]{:S(2)}) collective-permute-start(bf16[128,1024]{1,0:T(8,128)(2,1)S(1)} %collective-permute-done.23), channel_id=1, source_target_pairs={{0,4},{4,0},{1,5},{5,1},{2,6},{6,2},{3,7},{7,3}} | collective-permute-start | bytes 786440 | tf_op jit(solution)/shard_map/ppermute | solution.py:70
  65.9 34.2 %collective-permute-start.33 = (bf16[128,1024]{1,0:T(8,128)(2,1)}, bf16[128,1024]{1,0:T(8,128)(2,1)S(1)}, u32[]{:S(2)}, u32[]{:S(2)}) collective-permute-start(bf16[128,1024]{1,0:T(8,128)(2,1)} %get-tuple-element.42), channel_id=1, source_target_pairs={{8,0},{12,4},{16,8},{20,12},{24,16},{28,20},{9,1},{13,5},{17,9},{2... | collective-permute-start | bytes 786440 | tf_op jit(solution)/shard_map/ppermute | solution.py:69
  67.2 11.9 %collective-permute-start.5 = (bf16[128,1024]{1,0:T(8,128)(2,1)S(1)}, bf16[128,1024]{1,0:T(8,128)(2,1)S(1)}, u32[]{:S(2)}, u32[]{:S(2)}) collective-permute-start(bf16[128,1024]{1,0:T(8,128)(2,1)S(1)} %collective-permute-done.1), channel_id=1, source_target_pairs={{0,4},{4,0},{8,12},{12,8},{16,20},{20,16},{1,5},{5,1},{9,13},{13,9... | collective-permute-start | bytes 786440 | tf_op jit(solution)/shard_map/ppermute | solution.py:70
  70.9 10.2 %collective-permute-start.7 = (bf16[128,1024]{1,0:T(8,128)(2,1)S(1)}, bf16[128,1024]{1,0:T(8,128)(2,1)S(1)}, u32[]{:S(2)}, u32[]{:S(2)}) collective-permute-start(bf16[128,1024]{1,0:T(8,128)(2,1)S(1)} %collective-permute-done.1), channel_id=1, source_target_pairs={{8,0},{12,4},{16,8},{20,12},{9,1},{13,5},{17,9},{21,13},{10,2},{14... | collective-permute-start | bytes 786440 | tf_op jit(solution)/shard_map/ppermute | solution.py:69
  72.2 13.1 %collective-permute-start.35 = (bf16[128,1024]{1,0:T(8,128)(2,1)S(1)}, bf16[128,1024]{1,0:T(8,128)(2,1)S(1)}, u32[]{:S(2)}, u32[]{:S(2)}) collective-permute-start(bf16[128,1024]{1,0:T(8,128)(2,1)S(1)} %collective-permute-done.34), channel_id=1, source_target_pairs={{8,16},{12,20},{16,24},{20,28},{9,17},{13,21},{17,25},{21,29},{10,... | collective-permute-start | bytes 786440 | tf_op jit(solution)/shard_map/ppermute | solution.py:69
  79.1 16.7 %collective-permute-start.9 = (bf16[128,1024]{1,0:T(8,128)(2,1)S(1)}, bf16[128,1024]{1,0:T(8,128)(2,1)S(1)}, u32[]{:S(2)}, u32[]{:S(2)}) collective-permute-start(bf16[128,1024]{1,0:T(8,128)(2,1)S(1)} %collective-permute-done.3), channel_id=1, source_target_pairs={{16,20},{20,16},{24,28},{28,24},{17,21},{21,17},{25,29},{29,25},{1... | collective-permute-start | bytes 786440 | tf_op jit(solution)/shard_map/ppermute | solution.py:70
  81.1 14.1 %collective-permute-start.8 = (bf16[128,1024]{1,0:T(8,128)(2,1)S(1)}, bf16[128,1024]{1,0:T(8,128)(2,1)S(1)}, u32[]{:S(2)}, u32[]{:S(2)}) collective-permute-start(bf16[128,1024]{1,0:T(8,128)(2,1)S(1)} %collective-permute-done.7), channel_id=1, source_target_pairs={{0,4},{4,0},{8,12},{12,8},{1,5},{5,1},{9,13},{13,9},{2,6},{6,2},{1... | collective-permute-start | bytes 786440 | tf_op jit(solution)/shard_map/ppermute | solution.py:70
  83.7 13.5 %collective-permute-start.10 = (bf16[128,1024]{1,0:T(8,128)(2,1)S(1)}, bf16[128,1024]{1,0:T(8,128)(2,1)S(1)}, u32[]{:S(2)}, u32[]{:S(2)}) collective-permute-start(bf16[128,1024]{1,0:T(8,128)(2,1)S(1)} %collective-permute-done.7), channel_id=1, source_target_pairs={{8,0},{12,4},{9,1},{13,5},{10,2},{14,6},{11,3},{15,7}} | collective-permute-start | bytes 786440 | tf_op jit(solution)/shard_map/ppermute | solution.py:69
  85.3 34.8 %collective-permute-start.53 = (bf16[128,1024]{1,0:T(8,128)(2,1)}, bf16[128,1024]{1,0:T(8,128)(2,1)S(1)}, u32[]{:S(2)}, u32[]{:S(2)}) collective-permute-start(bf16[128,1024]{1,0:T(8,128)(2,1)} %get-tuple-element.41), channel_id=1, source_target_pairs={{0,8},{4,12},{8,16},{12,20},{16,24},{20,28},{1,9},{5,13},{9,17},{1... | collective-permute-start | bytes 786440 | tf_op jit(solution)/shard_map/ppermute | solution.py:69
  95.9 8.8 %collective-permute-start.36 = (bf16[128,1024]{1,0:T(8,128)(2,1)S(1)}, bf16[128,1024]{1,0:T(8,128)(2,1)S(1)}, u32[]{:S(2)}, u32[]{:S(2)}) collective-permute-start(bf16[128,1024]{1,0:T(8,128)(2,1)S(1)} %collective-permute-done.35), channel_id=1, source_target_pairs={{16,24},{20,28},{17,25},{21,29},{18,26},{22,30},{19,27},{23,31}} | collective-permute-start | bytes 786440 | tf_op jit(solution)/shard_map/ppermute | solution.py:69
  97.2 9.0 %collective-permute-start.11 = (bf16[128,1024]{1,0:T(8,128)(2,1)S(1)}, bf16[128,1024]{1,0:T(8,128)(2,1)S(1)}, u32[]{:S(2)}, u32[]{:S(2)}) collective-permute-start(bf16[128,1024]{1,0:T(8,128)(2,1)S(1)} %collective-permute-done.10), channel_id=1, source_target_pairs={{0,4},{4,0},{1,5},{5,1},{2,6},{6,2},{3,7},{7,3}} | collective-permute-start | bytes 786440 | tf_op jit(solution)/shard_map/ppermute | solution.py:70
  100.1 20.7 %collective-permute-start.52 = (bf16[128,1024]{1,0:T(8,128)(2,1)}, bf16[128,1024]{1,0:T(8,128)(2,1)S(1)}, u32[]{:S(2)}, u32[]{:S(2)}) collective-permute-start(bf16[128,1024]{1,0:T(8,128)(2,1)} %get-tuple-element.41), channel_id=1, source_target_pairs={{8,0},{12,4},{16,8},{20,12},{24,16},{28,20},{9,1},{13,5},{17,9},{2... | collective-permute-start | bytes 786440 | tf_op jit(solution)/shard_map/ppermute | solution.py:69
  104.7 11.6 %collective-permute-start.39 = (bf16[128,1024]{1,0:T(8,128)(2,1)S(1)}, bf16[128,1024]{1,0:T(8,128)(2,1)S(1)}, u32[]{:S(2)}, u32[]{:S(2)}) collective-permute-start(bf16[128,1024]{1,0:T(8,128)(2,1)S(1)} %collective-permute-done.33), channel_id=1, source_target_pairs={{8,0},{12,4},{16,8},{20,12},{9,1},{13,5},{17,9},{21,13},{10,2},{14... | collective-permute-start | bytes 786440 | tf_op jit(solution)/shard_map/ppermute | solution.py:69
  106.1 12.3 %collective-permute-start.38 = (bf16[128,1024]{1,0:T(8,128)(2,1)S(1)}, bf16[128,1024]{1,0:T(8,128)(2,1)S(1)}, u32[]{:S(2)}, u32[]{:S(2)}) collective-permute-start(bf16[128,1024]{1,0:T(8,128)(2,1)S(1)} %collective-permute-done.36), channel_id=1, source_target_pairs={{24,28},{28,24},{25,29},{29,25},{26,30},{30,26},{27,31},{31,27}} | collective-permute-start | bytes 786440 | tf_op jit(solution)/shard_map/ppermute | solution.py:70
  109.7 16.1 %collective-permute-start.41 = (bf16[128,1024]{1,0:T(8,128)(2,1)S(1)}, bf16[128,1024]{1,0:T(8,128)(2,1)S(1)}, u32[]{:S(2)}, u32[]{:S(2)}) collective-permute-start(bf16[128,1024]{1,0:T(8,128)(2,1)S(1)} %collective-permute-done.35), channel_id=1, source_target_pairs={{16,20},{20,16},{24,28},{28,24},{17,21},{21,17},{25,29},{29,25},{1... | collective-permute-start | bytes 786440 | tf_op jit(solution)/shard_map/ppermute | solution.py:70
  118.4 12.8 %collective-permute-start.42 = (bf16[128,1024]{1,0:T(8,128)(2,1)S(1)}, bf16[128,1024]{1,0:T(8,128)(2,1)S(1)}, u32[]{:S(2)}, u32[]{:S(2)}) collective-permute-start(bf16[128,1024]{1,0:T(8,128)(2,1)S(1)} %collective-permute-done.39), channel_id=1, source_target_pairs={{8,0},{12,4},{9,1},{13,5},{10,2},{14,6},{11,3},{15,7}} | collective-permute-start | bytes 786440 | tf_op jit(solution)/shard_map/ppermute | solution.py:69
  120.1 13.7 %collective-permute-start.44 = (bf16[128,1024]{1,0:T(8,128)(2,1)S(1)}, bf16[128,1024]{1,0:T(8,128)(2,1)S(1)}, u32[]{:S(2)}, u32[]{:S(2)}) collective-permute-start(bf16[128,1024]{1,0:T(8,128)(2,1)S(1)} %collective-permute-done.34), channel_id=1, source_target_pairs={{8,12},{12,8},{16,20},{20,16},{24,28},{28,24},{9,13},{13,9},{17,21... | collective-permute-start | bytes 786440 | tf_op jit(solution)/shard_map/ppermute | solution.py:70
  120.8 16.7 %collective-permute-start.54 = (bf16[128,1024]{1,0:T(8,128)(2,1)S(1)}, bf16[128,1024]{1,0:T(8,128)(2,1)S(1)}, u32[]{:S(2)}, u32[]{:S(2)}) collective-permute-start(bf16[128,1024]{1,0:T(8,128)(2,1)S(1)} %collective-permute-done.53), channel_id=1, source_target_pairs={{8,16},{12,20},{16,24},{20,28},{9,17},{13,21},{17,25},{21,29},{10,... | collective-permute-start | bytes 786440 | tf_op jit(solution)/shard_map/ppermute | solution.py:69
  124.5 16.5 %collective-permute-start.58 = (bf16[128,1024]{1,0:T(8,128)(2,1)S(1)}, bf16[128,1024]{1,0:T(8,128)(2,1)S(1)}, u32[]{:S(2)}, u32[]{:S(2)}) collective-permute-start(bf16[128,1024]{1,0:T(8,128)(2,1)S(1)} %collective-permute-done.52), channel_id=1, source_target_pairs={{8,0},{12,4},{16,8},{20,12},{9,1},{13,5},{17,9},{21,13},{10,2},{14... | collective-permute-start | bytes 786440 | tf_op jit(solution)/shard_map/ppermute | solution.py:69
  125.8 19.2 %collective-permute-start.27 = (f32[512,256]{1,0:T(8,128)S(1)}, f32[512,256]{1,0:T(8,128)S(1)}, u32[]{:S(2)}, u32[]{:S(2)}) collective-permute-start(f32[512,256]{1,0:T(8,128)S(1)} %fusion.67), channel_id=1, source_target_pairs={{0,1},{1,0},{2,3},{3,2},{4,5},{5,4},{6,7},{7,6},{8,9},{9,8},{10,11... | collective-permute-start | bytes 1572872 | tf_op jit(solution)/shard_map/ppermute | solution.py:142
  131.3 10.4 %collective-permute-start.43 = (bf16[128,1024]{1,0:T(8,128)(2,1)S(1)}, bf16[128,1024]{1,0:T(8,128)(2,1)S(1)}, u32[]{:S(2)}, u32[]{:S(2)}) collective-permute-start(bf16[128,1024]{1,0:T(8,128)(2,1)S(1)} %collective-permute-done.42), channel_id=1, source_target_pairs={{0,4},{4,0},{1,5},{5,1},{2,6},{6,2},{3,7},{7,3}} | collective-permute-start | bytes 786440 | tf_op jit(solution)/shard_map/ppermute | solution.py:70
  133.8 13.6 %collective-permute-start.56 = (bf16[128,1024]{1,0:T(8,128)(2,1)S(1)}, bf16[128,1024]{1,0:T(8,128)(2,1)S(1)}, u32[]{:S(2)}, u32[]{:S(2)}) collective-permute-start(bf16[128,1024]{1,0:T(8,128)(2,1)S(1)} %collective-permute-done.52), channel_id=1, source_target_pairs={{0,4},{4,0},{8,12},{12,8},{16,20},{20,16},{1,5},{5,1},{9,13},{13,9... | collective-permute-start | bytes 786440 | tf_op jit(solution)/shard_map/ppermute | solution.py:70
  137.5 34.0 %collective-permute-start.63 = (bf16[128,1024]{1,0:T(8,128)(2,1)S(1)}, bf16[128,1024]{1,0:T(8,128)(2,1)S(1)}, u32[]{:S(2)}, u32[]{:S(2)}) collective-permute-start(bf16[128,1024]{1,0:T(8,128)(2,1)S(1)} %collective-permute-done.53), channel_id=1, source_target_pairs={{8,12},{12,8},{16,20},{20,16},{24,28},{28,24},{9,13},{13,9},{17,21... | collective-permute-start | bytes 786440 | tf_op jit(solution)/shard_map/ppermute | solution.py:70
  141.7 23.5 %collective-permute-start.59 = (bf16[128,1024]{1,0:T(8,128)(2,1)S(1)}, bf16[128,1024]{1,0:T(8,128)(2,1)S(1)}, u32[]{:S(2)}, u32[]{:S(2)}) collective-permute-start(bf16[128,1024]{1,0:T(8,128)(2,1)S(1)} %collective-permute-done.58), channel_id=1, source_target_pairs={{0,4},{4,0},{8,12},{12,8},{1,5},{5,1},{9,13},{13,9},{2,6},{6,2},{1... | collective-permute-start | bytes 786440 | tf_op jit(solution)/shard_map/ppermute | solution.py:70
  145.0 13.6 %collective-permute-start.26 = (f32[512,256]{1,0:T(8,128)S(1)}, f32[512,256]{1,0:T(8,128)S(1)}, u32[]{:S(2)}, u32[]{:S(2)}) collective-permute-start(f32[512,256]{1,0:T(8,128)S(1)} %fusion.70), channel_id=1, source_target_pairs={{0,1},{1,0},{2,3},{3,2},{4,5},{5,4},{6,7},{7,6},{8,9},{9,8},{10,11... | collective-permute-start | bytes 1572872 | tf_op jit(solution)/shard_map/ppermute | solution.py:142
  147.4 10.4 %collective-permute-start.61 = (bf16[128,1024]{1,0:T(8,128)(2,1)S(1)}, bf16[128,1024]{1,0:T(8,128)(2,1)S(1)}, u32[]{:S(2)}, u32[]{:S(2)}) collective-permute-start(bf16[128,1024]{1,0:T(8,128)(2,1)S(1)} %collective-permute-done.58), channel_id=1, source_target_pairs={{8,0},{12,4},{9,1},{13,5},{10,2},{14,6},{11,3},{15,7}} | collective-permute-start | bytes 786440 | tf_op jit(solution)/shard_map/ppermute | solution.py:69
  148.8 13.3 %collective-permute-start.28 = (bf16[512,256]{1,0:T(8,128)(2,1)S(1)}, bf16[512,256]{1,0:T(8,128)(2,1)S(1)}, u32[]{:S(2)}, u32[]{:S(2)}) collective-permute-start(bf16[512,256]{1,0:T(8,128)(2,1)S(1)} %fusion.10), channel_id=1, source_target_pairs={{0,2},{1,3},{2,0},{3,1},{4,6},{5,7},{6,4},{7,5},{8,10},{9,11},{10,... | collective-permute-start | bytes 786440 | tf_op jit(solution)/shard_map/ppermute | solution.py:145
  158.6 12.9 %collective-permute-start.62 = (bf16[128,1024]{1,0:T(8,128)(2,1)S(1)}, bf16[128,1024]{1,0:T(8,128)(2,1)S(1)}, u32[]{:S(2)}, u32[]{:S(2)}) collective-permute-start(bf16[128,1024]{1,0:T(8,128)(2,1)S(1)} %collective-permute-done.61), channel_id=1, source_target_pairs={{0,4},{4,0},{1,5},{5,1},{2,6},{6,2},{3,7},{7,3}} | collective-permute-start | bytes 786440 | tf_op jit(solution)/shard_map/ppermute | solution.py:70
  176.7 8.4 %collective-permute-start.47 = (bf16[512,256]{1,0:T(8,128)(2,1)S(1)}, bf16[512,256]{1,0:T(8,128)(2,1)S(1)}, u32[]{:S(2)}, u32[]{:S(2)}) collective-permute-start(bf16[512,256]{1,0:T(8,128)(2,1)S(1)} %fusion.11), channel_id=1, source_target_pairs={{0,2},{1,3},{2,0},{3,1},{4,6},{5,7},{6,4},{7,5},{8,10},{9,11},{10,... | collective-permute-start | bytes 786440 | tf_op jit(solution)/shard_map/ppermute | solution.py:145
  197.8 8.7 %collective-permute-start.66 = (bf16[512,256]{1,0:T(8,128)(2,1)S(1)}, bf16[512,256]{1,0:T(8,128)(2,1)S(1)}, u32[]{:S(2)}, u32[]{:S(2)}) collective-permute-start(bf16[512,256]{1,0:T(8,128)(2,1)S(1)} %fusion.12), channel_id=1, source_target_pairs={{0,2},{1,3},{2,0},{3,1},{4,6},{5,7},{6,4},{7,5},{8,10},{9,11},{10,... | collective-permute-start | bytes 786440 | tf_op jit(solution)/shard_map/ppermute | solution.py:145
  222.4 8.4 %collective-permute-start.72 = (bf16[512,256]{1,0:T(8,128)(2,1)S(1)}, bf16[512,256]{1,0:T(8,128)(2,1)S(1)}, u32[]{:S(2)}, u32[]{:S(2)}) collective-permute-start(bf16[512,256]{1,0:T(8,128)(2,1)S(1)} %fusion.13), channel_id=1, source_target_pairs={{0,2},{1,3},{2,0},{3,1},{4,6},{5,7},{6,4},{7,5},{8,10},{9,11},{10,... | collective-permute-start | bytes 786440 | tf_op jit(solution)/shard_map/ppermute | solution.py:145
  257.0 10.1 %collective-permute-start.78 = (f32[1024]{0:T(1024)S(1)}, f32[1024]{0:T(1024)S(1)}, u32[]{:S(2)}, u32[]{:S(2)}) collective-permute-start(f32[1024]{0:T(1024)S(1)} %add.341), channel_id=1, source_target_pairs={{0,16},{4,20},{8,24},{12,28},{16,0},{20,4},{24,8},{28,12},{1,17},{... | collective-permute-start | bytes 12296 | tf_op jit(solution)/shard_map/ppermute | solution.py:88
  (39 other events, 307.7 us)

commit v8 on v5

--- a/solution.py
+++ b/solution.py
@@ -55,9 +55,6 @@
     def along(p, d):
         return [(p * nb + o, d * nb + o) for o in range(nb)]
 
-    def cross(sign, s):
-        return [(i, i ^ 1) for i in range(na * nb) if 0 <= i // nb - sign * s < na]
-
     got = {}
     for sign in (1, -1):
         cur = block
@@ -67,16 +64,15 @@
                 if 0 <= p + sign < na and 0 <= p - sign * (s - 1) < na:
                     pairs.extend(along(p, p + sign))
             cur = lax.ppermute(cur, "src", pairs)
-            got[(sign, s)] = (cur, lax.ppermute(cur, "src", cross(sign, s)))
+            got[(sign, s)] = cur
+    col = [block] + [
+        jnp.where(ia + k < na, got[(-1, k)], got[(1, na - k)]) for k in range(1, na)
+    ]
+    col = jnp.stack(col)
+    other = lax.ppermute(col, "src", swap)
     first = ib == 0
-    planes = [(block, lax.ppermute(block, "src", swap))]
-    for k in range(1, na):
-        up, down = got[(-1, k)], got[(1, na - k)]
-        ok = ia + k < na
-        planes.append(tuple(jnp.where(ok, u, d) for u, d in zip(up, down)))
-    return jnp.concatenate(
-        [x for a, b in planes for x in (jnp.where(first, a, b), jnp.where(first, b, a))], axis=0
-    )
+    planes = jnp.stack([jnp.where(first, col, other), jnp.where(first, other, col)], axis=1)
+    return planes.reshape((-1,) + block.shape[1:])
 
 
 def _sum_over_src(v):

time: 217 us -> 208 us (0.959)
  starting transfers between devices: 66.8 us -> 33.4 us
  waiting for transfers between devices: 106 us -> 130 us
    ppermute x14 -> x2, starting transfers between devices: 23.1 us -> 1.76 us  [_gather_src(): other = lax.ppermute(col, 'src', swap)]
    ppermute x14 -> x2, waiting for transfers between devices: 16.8 us -> 29.2 us  [_gather_src(): other = lax.ppermute(col, 'src', swap)]
    another operation x0 -> x12, other arithmetic: none -> 10.3 us  [the longest x8 5.73 us: _gather_src(): col = jnp.stack(col)]
    unnamed x14 -> x0, other arithmetic: 9.45 us -> none
    ppermute x2, waiting for transfers between devices: 11.3 us -> 20.1 us  [per_device(): lax.ppermute(halves[k].astype(jnp.bfloat16), 'vox', chip_perm(k))]
    ppermute x3, starting transfers between devices: 8.59 us -> 3.42 us  [_sum_over_src(): v = v + lax.ppermute(v, 'src', [(i, i ^ b) for i in range(n)])]
    ppermute x12, starting transfers between devices: 27.8 us -> 23 us  [_gather_src(): cur = lax.ppermute(cur, 'src', pairs)]
    another operation x0 -> x2, local copies, waits for them, and re-layouts: none -> 2.69 us  [the longest x1 2.25 us: _gather_src(): col = jnp.stack(col)]
  transfers between devices with their start and end apart: 41 -> 29, of which waited for: 16 -> 15; matrix products, arithmetic and copies ran while one was open for 15% -> 15% of each run, Pallas kernels for 0% -> 0%
where the time goes in v8:
time: 208 us
  waiting for transfers between devices  130 us (62%)
  starting transfers between devices  33.4 us (16%)
  matrix products  21.8 us (10%)
  other arithmetic  10.9 us (5%)
  local copies, waits for them, and re-layouts  10.7 us (5%)
    ppermute x12, waiting for transfers between devices, _gather_src(): cur = lax.ppermute(cur, 'src', pairs)  49.3 us
    ppermute x2, waiting for transfers between devices, _gather_src(): other = lax.ppermute(col, 'src', swap)  29.2 us
    ppermute x12, starting transfers between devices, _gather_src(): cur = lax.ppermute(cur, 'src', pairs)  23 us
    ppermute x2, waiting for transfers between devices, per_device(): got.append((2 * ((q - k) % m) + par, lax.ppermute(wt, 'vox', chip_perm(k))))  22.9 us
    ppermute x2, waiting for transfers between devices, per_device(): lax.ppermute(halves[k].astype(jnp.bfloat16), 'vox', chip_perm(k))  20.1 us
    dot_general x8, matrix products, pblock(): lax.dot_general(scaled, _rows(adj, rel(blk), n), (((1,), (1,)), ((), ()))...  15.5 us
    ppermute x3, waiting for transfers between devices, _sum_over_src(): v = v + lax.ppermute(v, 'src', [(i, i ^ b) for i in range(n)])  8.36 us
    dot_general x8, matrix products, per_device(): jnp.dot(w, _rows(adj, rel(blk), n), preferred_element_type=jnp.float32)  6.29 us
  transfers between devices with their start and end apart: 29, of which 15 were waited for; matrix products, arithmetic and copies ran while one was open for 15% of the time, Pallas kernels for 0%

profile of v8, /device:TPU:0, one launch (start us, length us, event | category | flops | bytes accessed | tf_op | source)
XLA Modules:
  0.0 207.6 jit_solution(7478066382218142012)
XLA Ops:
  0.0 2.3 %slice_bitcast_fusion = (bf16[1,256,1024]{2,1,0:T(8,128)(2,1)S(1)}, bf16[1,256,1024]{2,1,0:T(8,128)(2,1)S(1)}, bf16[256,1024]{1,0:T(8,128)(2,1)S(1)}, bf16[256,1024]{1,0:T(8,128)(2,1)}) fusion(bf16[512,1024]{1,0:T(8,128)(2,1)} %param.5), kind=kLoop, calls=%fused_computation.73 | loop fusion | bytes 3145728 | tf_op jit(solution)/shard_map/stack | solution.py:71
  2.3 1.3 collective-permute-start.7
  3.5 5.6 %collective-permute-start.8 = (bf16[256,1024]{1,0:T(8,128)(2,1)S(1)}, bf16[256,1024]{1,0:T(8,128)(2,1)S(1)}, u32[]{:S(2)}, u32[]{:S(2)}) collective-permute-start(bf16[256,1024]{1,0:T(8,128)(2,1)S(1)} %get-tuple-element.23), channel_id=1, source_target_pairs={{0,8},{4,12},{8,16},{12,20},{16,24},{20,28},{1,9},{5,13},{9,17},{1... | collective-permute-start | bytes 1572872 | tf_op jit(solution)/shard_map/ppermute | solution.py:66
  9.1 10.0 %collective-permute-done.7 = bf16[256,1024]{1,0:T(8,128)(2,1)S(1)} collective-permute-done((bf16[256,1024]{1,0:T(8,128)(2,1)S(1)}, bf16[256,1024]{1,0:T(8,128)(2,1)S(1)}, u32[]{:S(2)}, u32[]{:S(2)}) %collective-permute-start.7) | collective-permute-done | bytes 524320 | tf_op jit(solution)/shard_map/ppermute | solution.py:66
  19.1 1.3 collective-permute-start.11
  20.4 1.5 collective-permute-start.9
  21.9 12.2 %collective-permute-done.11 = bf16[256,1024]{1,0:T(8,128)(2,1)S(1)} collective-permute-done((bf16[256,1024]{1,0:T(8,128)(2,1)S(1)}, bf16[256,1024]{1,0:T(8,128)(2,1)S(1)}, u32[]{:S(2)}, u32[]{:S(2)}) %collective-permute-start.11) | collective-permute-done | bytes 524320 | tf_op jit(solution)/shard_map/ppermute | solution.py:66
  34.1 1.3 collective-permute-start.12
  36.2 12.1 %collective-permute-done.12 = bf16[256,1024]{1,0:T(8,128)(2,1)} collective-permute-done((bf16[256,1024]{1,0:T(8,128)(2,1)S(1)}, bf16[256,1024]{1,0:T(8,128)(2,1)}, u32[]{:S(2)}, u32[]{:S(2)}) %collective-permute-start.12) | collective-permute-done | bytes 524320 | tf_op jit(solution)/shard_map/ppermute | solution.py:66
  48.3 1.1 select_bitcast_fusion.4
  49.4 1.6 pad_maximum_fusion.3
  51.1 1.0 collective-permute-start.13
  52.1 1.3 collective-permute-start
  53.4 5.4 %collective-permute-start.1 = (bf16[256,1024]{1,0:T(8,128)(2,1)S(1)}, bf16[256,1024]{1,0:T(8,128)(2,1)}, u32[]{:S(2)}, u32[]{:S(2)}) collective-permute-start(bf16[256,1024]{1,0:T(8,128)(2,1)S(1)} %copy-done.22), channel_id=1, source_target_pairs={{0,8},{4,12},{8,16},{12,20},{16,24},{20,28},{1,9},{5,13},{9,17},{1... | collective-permute-start | bytes 1572872 | tf_op jit(solution)/shard_map/ppermute | solution.py:66
  58.8 5.9 %collective-permute-done = bf16[256,1024]{1,0:T(8,128)(2,1)S(1)} collective-permute-done((bf16[256,1024]{1,0:T(8,128)(2,1)S(1)}, bf16[256,1024]{1,0:T(8,128)(2,1)S(1)}, u32[]{:S(2)}, u32[]{:S(2)}) %collective-permute-start) | collective-permute-done | bytes 524320 | tf_op jit(solution)/shard_map/ppermute | solution.py:66
  64.7 1.3 collective-permute-start.4
  65.9 1.5 collective-permute-start.2
  67.4 9.1 %collective-permute-done.4 = bf16[256,1024]{1,0:T(8,128)(2,1)} collective-permute-done((bf16[256,1024]{1,0:T(8,128)(2,1)S(1)}, bf16[256,1024]{1,0:T(8,128)(2,1)}, u32[]{:S(2)}, u32[]{:S(2)}) %collective-permute-start.4) | collective-permute-done | bytes 524320 | tf_op jit(solution)/shard_map/ppermute | solution.py:66
  76.5 1.3 collective-permute-start.5
  78.5 1.1 select_bitcast_fusion.8
  79.7 16.7 %collective-permute-done.13 = bf16[4,256,1024]{2,1,0:T(8,128)(2,1)} collective-permute-done((bf16[4,256,1024]{2,1,0:T(8,128)(2,1)}, bf16[4,256,1024]{2,1,0:T(8,128)(2,1)}, u32[]{:S(2)}, u32[]{:S(2)}) %collective-permute-start.13) | collective-permute-done | bytes 2097184 | tf_op jit(solution)/shard_map/ppermute | solution.py:72
  96.3 1.8 select_bitcast_fusion.1
  99.7 1.7 fusion.31
  101.6 1.7 pad_maximum_fusion.2
  104.0 1.7 fusion.34
  106.0 2.8 %fusion.6 = bf16[512,512]{1,0:T(8,128)(2,1)} fusion(f32[512,512]{1,0:T(8,128)S(1)} %collective-permute-done.15, bf16[2048,1024]{1,0:T(8,128)(2,1)} %bitcast.42, s32[]{:T(128)S(6)} %select_n.205, bf16[512,1024]{1,0:T(8,128)(2,1)S(1)} %copy-done.4, f32[1024]{0:T(1024)S(1)} %copy-done.23), kind=kOutput, calls=%fused_computation.20 | convolution fusion | flops 538968064 | bytes 3674116 | tf_op jit(solution)/shard_map/dot_general | solution.py:131
  108.7 1.5 collective-permute-start.16
  110.2 3.0 %reshape.17 = f32[512,2,512]{2,1,0:T(2,128)S(1)} reshape(f32[512,1024]{1,0:T(8,128)} %param.7) | data formatting | bytes 4194304 | tf_op jit(solution)/shard_map/reshape | solution.py:110
  113.3 1.7 fusion.61
  115.0 8.1 %collective-permute-done.16 = bf16[512,512]{1,0:T(8,128)(2,1)} collective-permute-done((bf16[512,512]{1,0:T(8,128)(2,1)}, bf16[512,512]{1,0:T(8,128)(2,1)}, u32[]{:S(2)}, u32[]{:S(2)}) %collective-permute-start.16) | collective-permute-done | bytes 524320 | tf_op jit(solution)/shard_map/ppermute | solution.py:141
  123.2 2.6 %fusion.9 = bf16[512,512]{1,0:T(8,128)(2,1)S(1)} fusion(f32[512,512]{1,0:T(8,128)S(1)} %bitcast.58, f32[512,512]{1,0:T(8,128)} %collective-permute-done.14, bf16[512,512]{1,0:T(8,128)(2,1)} %collective-permute-done.16, bf16[2048,1024]{1,0:T(8,128)(2,1)} %bitcast.43, s32[]{:T(128)S(6)} %select_n.200, bf16[512,1024]{1,0:T(8,128)(2,1)S(1)} %copy-done.4, ...), kind=kOutput, calls=%fused_computation.23 | convolution fusion | flops 539754496 | bytes 5246980 | tf_op jit(solution)/shard_map/dot_general | solution.py:131
  125.8 1.6 collective-permute-start.17
  127.4 11.8 %collective-permute-done.17 = bf16[512,512]{1,0:T(8,128)(2,1)S(1)} collective-permute-done((bf16[512,512]{1,0:T(8,128)(2,1)S(1)}, bf16[512,512]{1,0:T(8,128)(2,1)S(1)}, u32[]{:S(2)}, u32[]{:S(2)}) %collective-permute-start.17) | collective-permute-done | bytes 524320 | tf_op jit(solution)/shard_map/ppermute | solution.py:150
  139.2 12.5 %collective-permute-done.6 = bf16[4,256,1024]{2,1,0:T(8,128)(2,1)} collective-permute-done((bf16[4,256,1024]{2,1,0:T(8,128)(2,1)}, bf16[4,256,1024]{2,1,0:T(8,128)(2,1)}, u32[]{:S(2)}, u32[]{:S(2)}) %collective-permute-start.6) | collective-permute-done | bytes 2097184 | tf_op jit(solution)/shard_map/ppermute | solution.py:72
  151.7 2.0 select_bitcast_fusion.3
  154.2 0.9 copy-done.18
  155.0 1.7 fusion.17
  157.1 2.1 %fusion.20 = f32[512,512]{1,0:T(8,128)S(1)} fusion(bf16[2048,1024]{1,0:T(8,128)(2,1)} %bitcast.49, s32[]{:T(128)S(6)} %select_n.202, bf16[512,1024]{1,0:T(8,128)(2,1)S(1)} %copy-done.4, f32[1024]{0:T(1024)S(1)} %copy-done.23), kind=kOutput, calls=%fused_computation.34 | convolution fusion | flops 538443776 | bytes 3149828 | tf_op jit(solution)/shard_map/dot_general | solution.py:131
  160.5 1.1 copy-done.3
  161.6 2.0 fusion.7
  165.8 11.9 %collective-permute-done.22 = bf16[512,512]{1,0:T(8,128)(2,1)S(1)} collective-permute-done((bf16[512,512]{1,0:T(8,128)(2,1)S(1)}, bf16[512,512]{1,0:T(8,128)(2,1)S(1)}, u32[]{:S(2)}, u32[]{:S(2)}) %collective-permute-start.22) | collective-permute-done | bytes 524320 | tf_op jit(solution)/shard_map/ppermute | solution.py:141
  177.8 0.9 fusion.8
  180.9 11.1 %collective-permute-done.23 = bf16[512,512]{1,0:T(8,128)(2,1)S(1)} collective-permute-done((bf16[512,512]{1,0:T(8,128)(2,1)S(1)}, bf16[512,512]{1,0:T(8,128)(2,1)S(1)}, u32[]{:S(2)}, u32[]{:S(2)}) %collective-permute-start.23) | collective-permute-done | bytes 524320 | tf_op jit(solution)/shard_map/ppermute | solution.py:150
  193.9 1.2 fusion.1
  195.9 2.9 %collective-permute-done.26 = f32[1024]{0:T(1024)S(1)} collective-permute-done((f32[1024]{0:T(1024)S(1)}, f32[1024]{0:T(1024)S(1)}, u32[]{:S(2)}, u32[]{:S(2)}) %collective-permute-start.26) | collective-permute-done | bytes 4128 | tf_op jit(solution)/shard_map/ppermute | solution.py:84
  198.8 3.6 %collective-permute-done.27 = f32[1024]{0:T(1024)S(1)} collective-permute-done((f32[1024]{0:T(1024)S(1)}, f32[1024]{0:T(1024)S(1)}, u32[]{:S(2)}, u32[]{:S(2)}) %collective-permute-start.27) | collective-permute-done | bytes 4128 | tf_op jit(solution)/shard_map/ppermute | solution.py:84
  202.5 2.6 %collective-permute-start.28 = (f32[1024]{0:T(1024)S(1)}, f32[1024]{0:T(1024)S(1)}, u32[]{:S(2)}, u32[]{:S(2)}) collective-permute-start(f32[1024]{0:T(1024)S(1)} %add.221), channel_id=1, source_target_pairs={{0,16},{4,20},{8,24},{12,28},{16,0},{20,4},{24,8},{28,12},{1,17},{... | collective-permute-start | bytes 12296 | tf_op jit(solution)/shard_map/ppermute | solution.py:84
  205.1 1.9 collective-permute-done.28
  (95 shorter events, 14.0 us)
Async XLA Ops:
  2.3 99.4 %copy-start.11 = (bf16[1,256,1024]{2,1,0:T(8,128)(2,1)}, bf16[1,256,1024]{2,1,0:T(8,128)(2,1)S(1)}, u32[]{:S(2)}) copy-start(bf16[1,256,1024]{2,1,0:T(8,128)(2,1)S(1)} %get-tuple-element.22) | copy-start | bytes 1572868
  2.3 16.8 %collective-permute-start.7 = (bf16[256,1024]{1,0:T(8,128)(2,1)S(1)}, bf16[256,1024]{1,0:T(8,128)(2,1)S(1)}, u32[]{:S(2)}, u32[]{:S(2)}) collective-permute-start(bf16[256,1024]{1,0:T(8,128)(2,1)S(1)} %get-tuple-element.23), channel_id=1, source_target_pairs={{8,0},{12,4},{16,8},{20,12},{24,16},{28,20},{9,1},{13,5},{17,9},{2... | collective-permute-start | bytes 1572872 | tf_op jit(solution)/shard_map/ppermute | solution.py:66
  3.5 16.8 %collective-permute-start.8 = (bf16[256,1024]{1,0:T(8,128)(2,1)S(1)}, bf16[256,1024]{1,0:T(8,128)(2,1)S(1)}, u32[]{:S(2)}, u32[]{:S(2)}) collective-permute-start(bf16[256,1024]{1,0:T(8,128)(2,1)S(1)} %get-tuple-element.23), channel_id=1, source_target_pairs={{0,8},{4,12},{8,16},{12,20},{16,24},{20,28},{1,9},{5,13},{9,17},{1... | collective-permute-start | bytes 1572872 | tf_op jit(solution)/shard_map/ppermute | solution.py:66
  19.1 15.0 %collective-permute-start.11 = (bf16[256,1024]{1,0:T(8,128)(2,1)S(1)}, bf16[256,1024]{1,0:T(8,128)(2,1)S(1)}, u32[]{:S(2)}, u32[]{:S(2)}) collective-permute-start(bf16[256,1024]{1,0:T(8,128)(2,1)S(1)} %collective-permute-done.7), channel_id=1, source_target_pairs={{8,0},{12,4},{16,8},{20,12},{9,1},{13,5},{17,9},{21,13},{10,2},{14... | collective-permute-start | bytes 1572872 | tf_op jit(solution)/shard_map/ppermute | solution.py:66
  20.4 15.0 %collective-permute-start.9 = (bf16[256,1024]{1,0:T(8,128)(2,1)S(1)}, bf16[256,1024]{1,0:T(8,128)(2,1)}, u32[]{:S(2)}, u32[]{:S(2)}) collective-permute-start(bf16[256,1024]{1,0:T(8,128)(2,1)S(1)} %collective-permute-done.8), channel_id=1, source_target_pairs={{8,16},{12,20},{16,24},{20,28},{9,17},{13,21},{17,25},{21,29},{10,... | collective-permute-start | bytes 1572872 | tf_op jit(solution)/shard_map/ppermute | solution.py:66
  34.1 14.2 %collective-permute-start.12 = (bf16[256,1024]{1,0:T(8,128)(2,1)S(1)}, bf16[256,1024]{1,0:T(8,128)(2,1)}, u32[]{:S(2)}, u32[]{:S(2)}) collective-permute-start(bf16[256,1024]{1,0:T(8,128)(2,1)S(1)} %collective-permute-done.11), channel_id=1, source_target_pairs={{8,0},{12,4},{9,1},{13,5},{10,2},{14,6},{11,3},{15,7}} | collective-permute-start | bytes 1572872 | tf_op jit(solution)/shard_map/ppermute | solution.py:66
  35.4 14.0 %collective-permute-start.10 = (bf16[256,1024]{1,0:T(8,128)(2,1)}, bf16[256,1024]{1,0:T(8,128)(2,1)S(1)}, u32[]{:S(2)}, u32[]{:S(2)}) collective-permute-start(bf16[256,1024]{1,0:T(8,128)(2,1)} %collective-permute-done.9), channel_id=1, source_target_pairs={{16,24},{20,28},{17,25},{21,29},{18,26},{22,30},{19,27},{23,31}} | collective-permute-start | bytes 1572872 | tf_op jit(solution)/shard_map/ppermute | solution.py:66
  49.4 2.7 %copy-start.22 = (bf16[256,1024]{1,0:T(8,128)(2,1)S(1)}, bf16[256,1024]{1,0:T(8,128)(2,1)}, u32[]{:S(2)}) copy-start(bf16[256,1024]{1,0:T(8,128)(2,1)} %get-tuple-element.24) | copy-start | bytes 1572868
  51.1 45.3 %collective-permute-start.13 = (bf16[4,256,1024]{2,1,0:T(8,128)(2,1)}, bf16[4,256,1024]{2,1,0:T(8,128)(2,1)}, u32[]{:S(2)}, u32[]{:S(2)}) collective-permute-start(bf16[4,256,1024]{2,1,0:T(8,128)(2,1)} %pad_maximum_fusion.3), channel_id=1, source_target_pairs={{0,4},{4,0},{8,12},{12,8},{16,20},{20,16},{24,28},{28,24},{1,5},{5... | collective-permute-start | bytes 6291464 | tf_op jit(solution)/shard_map/ppermute | solution.py:72
  52.1 12.6 %collective-permute-start = (bf16[256,1024]{1,0:T(8,128)(2,1)S(1)}, bf16[256,1024]{1,0:T(8,128)(2,1)S(1)}, u32[]{:S(2)}, u32[]{:S(2)}) collective-permute-start(bf16[256,1024]{1,0:T(8,128)(2,1)S(1)} %copy-done.22), channel_id=1, source_target_pairs={{8,0},{12,4},{16,8},{20,12},{24,16},{28,20},{9,1},{13,5},{17,9},{2... | collective-permute-start | bytes 1572872 | tf_op jit(solution)/shard_map/ppermute | solution.py:66
  53.4 12.6 %collective-permute-start.1 = (bf16[256,1024]{1,0:T(8,128)(2,1)S(1)}, bf16[256,1024]{1,0:T(8,128)(2,1)}, u32[]{:S(2)}, u32[]{:S(2)}) collective-permute-start(bf16[256,1024]{1,0:T(8,128)(2,1)S(1)} %copy-done.22), channel_id=1, source_target_pairs={{0,8},{4,12},{8,16},{12,20},{16,24},{20,28},{1,9},{5,13},{9,17},{1... | collective-permute-start | bytes 1572872 | tf_op jit(solution)/shard_map/ppermute | solution.py:66
  64.7 11.9 %collective-permute-start.4 = (bf16[256,1024]{1,0:T(8,128)(2,1)S(1)}, bf16[256,1024]{1,0:T(8,128)(2,1)}, u32[]{:S(2)}, u32[]{:S(2)}) collective-permute-start(bf16[256,1024]{1,0:T(8,128)(2,1)S(1)} %collective-permute-done), channel_id=1, source_target_pairs={{8,0},{12,4},{16,8},{20,12},{9,1},{13,5},{17,9},{21,13},{10,2},{14... | collective-permute-start | bytes 1572872 | tf_op jit(solution)/shard_map/ppermute | solution.py:66
  65.9 11.9 %collective-permute-start.2 = (bf16[256,1024]{1,0:T(8,128)(2,1)}, bf16[256,1024]{1,0:T(8,128)(2,1)}, u32[]{:S(2)}, u32[]{:S(2)}) collective-permute-start(bf16[256,1024]{1,0:T(8,128)(2,1)} %collective-permute-done.1), channel_id=1, source_target_pairs={{8,16},{12,20},{16,24},{20,28},{9,17},{13,21},{17,25},{21,29},{10,... | collective-permute-start | bytes 1572872 | tf_op jit(solution)/shard_map/ppermute | solution.py:66
  76.5 24.9 %collective-permute-start.5 = (bf16[256,1024]{1,0:T(8,128)(2,1)}, bf16[256,1024]{1,0:T(8,128)(2,1)S(1)}, u32[]{:S(2)}, u32[]{:S(2)}) collective-permute-start(bf16[256,1024]{1,0:T(8,128)(2,1)} %collective-permute-done.4), channel_id=1, source_target_pairs={{8,0},{12,4},{9,1},{13,5},{10,2},{14,6},{11,3},{15,7}} | collective-permute-start | bytes 1572872 | tf_op jit(solution)/shard_map/ppermute | solution.py:66
  77.8 23.7 %collective-permute-start.3 = (bf16[256,1024]{1,0:T(8,128)(2,1)}, bf16[256,1024]{1,0:T(8,128)(2,1)S(1)}, u32[]{:S(2)}, u32[]{:S(2)}) collective-permute-start(bf16[256,1024]{1,0:T(8,128)(2,1)} %collective-permute-done.2), channel_id=1, source_target_pairs={{16,24},{20,28},{17,25},{21,29},{18,26},{22,30},{19,27},{23,31}} | collective-permute-start | bytes 1572872 | tf_op jit(solution)/shard_map/ppermute | solution.py:66
  79.6 22.0 %copy-start.5 = (bf16[1,256,1024]{2,1,0:T(8,128)(2,1)}, bf16[1,256,1024]{2,1,0:T(8,128)(2,1)S(1)}, u32[]{:S(2)}) copy-start(bf16[1,256,1024]{2,1,0:T(8,128)(2,1)S(1)} %select_bitcast_fusion.8) | copy-start | bytes 1572868
  99.0 5.1 %copy-start = (bf16[4,2,256,1024]{3,2,1,0:T(8,128)(2,1)}, bf16[4,2,256,1024]{3,2,1,0:T(8,128)(2,1)S(1)}, u32[]{:S(2)}) copy-start(bf16[4,2,256,1024]{3,2,1,0:T(8,128)(2,1)S(1)} %copy.6) | copy-start | bytes 12582916
  101.4 4.5 %collective-permute-start.15 = (f32[512,512]{1,0:T(8,128)}, f32[512,512]{1,0:T(8,128)S(1)}, u32[]{:S(2)}, u32[]{:S(2)}) collective-permute-start(f32[512,512]{1,0:T(8,128)} %fusion.31), channel_id=1, source_target_pairs={{0,1},{1,0},{2,3},{3,2},{4,5},{5,4},{6,7},{7,6},{8,9},{9,8},{10,11... | collective-permute-start | bytes 3145736 | tf_op jit(solution)/shard_map/ppermute | solution.py:138
  101.5 1.8 copy-start.7
  101.6 1.7 copy-start.9
  103.3 48.4 %collective-permute-start.6 = (bf16[4,256,1024]{2,1,0:T(8,128)(2,1)}, bf16[4,256,1024]{2,1,0:T(8,128)(2,1)}, u32[]{:S(2)}, u32[]{:S(2)}) collective-permute-start(bf16[4,256,1024]{2,1,0:T(8,128)(2,1)} %pad_maximum_fusion.2), channel_id=1, source_target_pairs={{0,4},{4,0},{8,12},{12,8},{16,20},{20,16},{24,28},{28,24},{1,5},{5... | collective-permute-start | bytes 6291464 | tf_op jit(solution)/shard_map/ppermute | solution.py:72
  105.7 9.3 %collective-permute-start.14 = (f32[512,512]{1,0:T(8,128)}, f32[512,512]{1,0:T(8,128)}, u32[]{:S(2)}, u32[]{:S(2)}) collective-permute-start(f32[512,512]{1,0:T(8,128)} %fusion.34), channel_id=1, source_target_pairs={{0,1},{1,0},{2,3},{3,2},{4,5},{5,4},{6,7},{7,6},{8,9},{9,8},{10,11... | collective-permute-start | bytes 3145736 | tf_op jit(solution)/shard_map/ppermute | solution.py:138
  108.7 14.4 %collective-permute-start.16 = (bf16[512,512]{1,0:T(8,128)(2,1)}, bf16[512,512]{1,0:T(8,128)(2,1)}, u32[]{:S(2)}, u32[]{:S(2)}) collective-permute-start(bf16[512,512]{1,0:T(8,128)(2,1)} %fusion.6), channel_id=1, source_target_pairs={{0,2},{1,3},{2,0},{3,1},{4,6},{5,7},{6,4},{7,5},{8,10},{9,11},{10,... | collective-permute-start | bytes 1572872 | tf_op jit(solution)/shard_map/ppermute | solution.py:141
  123.2 28.5 %copy-start.6 = (bf16[1,256,1024]{2,1,0:T(8,128)(2,1)S(1)}, bf16[1,256,1024]{2,1,0:T(8,128)(2,1)}, u32[]{:S(2)}) copy-start(bf16[1,256,1024]{2,1,0:T(8,128)(2,1)} %copy-done.5) | copy-start | bytes 1572868
  123.2 28.5 %copy-start.8 = (bf16[1,256,1024]{2,1,0:T(8,128)(2,1)S(1)}, bf16[1,256,1024]{2,1,0:T(8,128)(2,1)}, u32[]{:S(2)}) copy-start(bf16[1,256,1024]{2,1,0:T(8,128)(2,1)} %copy-done.7) | copy-start | bytes 1572868
  123.2 28.5 %copy-start.10 = (bf16[1,256,1024]{2,1,0:T(8,128)(2,1)S(1)}, bf16[1,256,1024]{2,1,0:T(8,128)(2,1)}, u32[]{:S(2)}) copy-start(bf16[1,256,1024]{2,1,0:T(8,128)(2,1)} %copy-done.9) | copy-start | bytes 1572868
  123.2 28.5 %copy-start.12 = (bf16[1,256,1024]{2,1,0:T(8,128)(2,1)S(1)}, bf16[1,256,1024]{2,1,0:T(8,128)(2,1)}, u32[]{:S(2)}) copy-start(bf16[1,256,1024]{2,1,0:T(8,128)(2,1)} %copy-done.11) | copy-start | bytes 1572868
  125.8 27.9 %copy-start.14 = (bf16[512,512]{1,0:T(8,128)(2,1)}, bf16[512,512]{1,0:T(8,128)(2,1)S(1)}, u32[]{:S(2)}) copy-start(bf16[512,512]{1,0:T(8,128)(2,1)S(1)} %fusion.9) | copy-start | bytes 1572868
  125.8 13.4 %collective-permute-start.17 = (bf16[512,512]{1,0:T(8,128)(2,1)S(1)}, bf16[512,512]{1,0:T(8,128)(2,1)S(1)}, u32[]{:S(2)}, u32[]{:S(2)}) collective-permute-start(bf16[512,512]{1,0:T(8,128)(2,1)S(1)} %fusion.9), channel_id=1, source_target_pairs={{0,2},{1,3},{2,0},{3,1},{4,6},{5,7},{6,4},{7,5},{8,10},{9,11},{10,... | collective-permute-start | bytes 1572872 | tf_op jit(solution)/shard_map/ppermute | solution.py:150
  127.4 26.7 %collective-permute-start.18 = (bf16[512,512]{1,0:T(8,128)(2,1)S(1)}, bf16[512,512]{1,0:T(8,128)(2,1)S(1)}, u32[]{:S(2)}, u32[]{:S(2)}) collective-permute-start(bf16[512,512]{1,0:T(8,128)(2,1)S(1)} %fusion.9), channel_id=1, source_target_pairs={{0,1},{1,0},{2,3},{3,2},{4,5},{5,4},{6,7},{7,6},{8,9},{9,8},{10,11... | collective-permute-start | bytes 1572872 | tf_op jit(solution)/shard_map/ppermute | solution.py:151
  139.2 14.5 %copy-start.20 = (bf16[512,512]{1,0:T(8,128)(2,1)}, bf16[512,512]{1,0:T(8,128)(2,1)S(1)}, u32[]{:S(2)}) copy-start(bf16[512,512]{1,0:T(8,128)(2,1)S(1)} %collective-permute-done.17) | copy-start | bytes 1572868
  139.2 15.0 %collective-permute-start.19 = (bf16[512,512]{1,0:T(8,128)(2,1)S(1)}, bf16[512,512]{1,0:T(8,128)(2,1)S(1)}, u32[]{:S(2)}, u32[]{:S(2)}) collective-permute-start(bf16[512,512]{1,0:T(8,128)(2,1)S(1)} %collective-permute-done.17), channel_id=1, source_target_pairs={{0,1},{1,0},{2,3},{3,2},{4,5},{5,4},{6,7},{7,6},{8,9},{9,8},{10,11... | collective-permute-start | bytes 1572872 | tf_op jit(solution)/shard_map/ppermute | solution.py:151
  154.1 2.6 %copy-start.2 = (bf16[4,2,256,1024]{3,2,1,0:T(8,128)(2,1)}, bf16[4,2,256,1024]{3,2,1,0:T(8,128)(2,1)S(1)}, u32[]{:S(2)}) copy-start(bf16[4,2,256,1024]{3,2,1,0:T(8,128)(2,1)S(1)} %pad_maximum_fusion) | copy-start | bytes 12582916
  155.0 1.8 copy-start.16
  155.0 2.0 copy-start.13
  156.8 3.7 %collective-permute-start.21 = (f32[512,512]{1,0:T(8,128)}, f32[512,512]{1,0:T(8,128)}, u32[]{:S(2)}, u32[]{:S(2)}) collective-permute-start(f32[512,512]{1,0:T(8,128)} %fusion.17), channel_id=1, source_target_pairs={{0,1},{1,0},{2,3},{3,2},{4,5},{5,4},{6,7},{7,6},{8,9},{9,8},{10,11... | collective-permute-start | bytes 3145736 | tf_op jit(solution)/shard_map/ppermute | solution.py:138
  157.1 2.5 %copy-start.1 = (bf16[4,2,256,1024]{3,2,1,0:T(8,128)(2,1)S(1)}, bf16[4,2,256,1024]{3,2,1,0:T(8,128)(2,1)}, u32[]{:S(2)}) copy-start(bf16[4,2,256,1024]{3,2,1,0:T(8,128)(2,1)} %copy-done) | copy-start | bytes 12582916
  157.1 2.6 %copy-start.21 = (bf16[512,512]{1,0:T(8,128)(2,1)S(1)}, bf16[512,512]{1,0:T(8,128)(2,1)}, u32[]{:S(2)}) copy-start(bf16[512,512]{1,0:T(8,128)(2,1)} %copy-done.20) | copy-start | bytes 1572868
  159.3 2.3 %copy-start.3 = (bf16[4,2,256,1024]{3,2,1,0:T(8,128)(2,1)S(1)}, bf16[4,2,256,1024]{3,2,1,0:T(8,128)(2,1)}, u32[]{:S(2)}) copy-start(bf16[4,2,256,1024]{3,2,1,0:T(8,128)(2,1)} %copy-done.2) | copy-start | bytes 12582916
  159.3 6.6 %collective-permute-start.20 = (f32[512,512]{1,0:T(8,128)S(1)}, f32[512,512]{1,0:T(8,128)S(1)}, u32[]{:S(2)}, u32[]{:S(2)}) collective-permute-start(f32[512,512]{1,0:T(8,128)S(1)} %fusion.20), channel_id=1, source_target_pairs={{0,1},{1,0},{2,3},{3,2},{4,5},{5,4},{6,7},{7,6},{8,9},{9,8},{10,11... | collective-permute-start | bytes 3145736 | tf_op jit(solution)/shard_map/ppermute | solution.py:138
  160.5 3.9 %copy-start.15 = (bf16[512,512]{1,0:T(8,128)(2,1)S(1)}, bf16[512,512]{1,0:T(8,128)(2,1)}, u32[]{:S(2)}) copy-start(bf16[512,512]{1,0:T(8,128)(2,1)} %copy-done.14) | copy-start | bytes 1572868
  163.6 14.2 %collective-permute-start.22 = (bf16[512,512]{1,0:T(8,128)(2,1)S(1)}, bf16[512,512]{1,0:T(8,128)(2,1)S(1)}, u32[]{:S(2)}, u32[]{:S(2)}) collective-permute-start(bf16[512,512]{1,0:T(8,128)(2,1)S(1)} %fusion.7), channel_id=1, source_target_pairs={{0,2},{1,3},{2,0},{3,1},{4,6},{5,7},{6,4},{7,5},{8,10},{9,11},{10,... | collective-permute-start | bytes 1572872 | tf_op jit(solution)/shard_map/ppermute | solution.py:141
  178.7 13.3 %collective-permute-start.23 = (bf16[512,512]{1,0:T(8,128)(2,1)S(1)}, bf16[512,512]{1,0:T(8,128)(2,1)S(1)}, u32[]{:S(2)}, u32[]{:S(2)}) collective-permute-start(bf16[512,512]{1,0:T(8,128)(2,1)S(1)} %fusion.8), channel_id=1, source_target_pairs={{0,2},{1,3},{2,0},{3,1},{4,6},{5,7},{6,4},{7,5},{8,10},{9,11},{10,... | collective-permute-start | bytes 1572872 | tf_op jit(solution)/shard_map/ppermute | solution.py:150
  180.1 12.6 %collective-permute-start.24 = (bf16[512,512]{1,0:T(8,128)(2,1)S(1)}, bf16[512,512]{1,0:T(8,128)(2,1)S(1)}, u32[]{:S(2)}, u32[]{:S(2)}) collective-permute-start(bf16[512,512]{1,0:T(8,128)(2,1)S(1)} %fusion.8), channel_id=1, source_target_pairs={{0,1},{1,0},{2,3},{3,2},{4,5},{5,4},{6,7},{7,6},{8,9},{9,8},{10,11... | collective-permute-start | bytes 1572872 | tf_op jit(solution)/shard_map/ppermute | solution.py:151
  192.0 1.9 collective-permute-start.25
  195.2 3.7 %collective-permute-start.26 = (f32[1024]{0:T(1024)S(1)}, f32[1024]{0:T(1024)S(1)}, u32[]{:S(2)}, u32[]{:S(2)}) collective-permute-start(f32[1024]{0:T(1024)S(1)} %fusion.1), channel_id=1, source_target_pairs={{0,4},{4,0},{8,12},{12,8},{16,20},{20,16},{24,28},{28,24},{1,5},{5... | collective-permute-start | bytes 12296 | tf_op jit(solution)/shard_map/ppermute | solution.py:84
  198.8 3.6 %collective-permute-start.27 = (f32[1024]{0:T(1024)S(1)}, f32[1024]{0:T(1024)S(1)}, u32[]{:S(2)}, u32[]{:S(2)}) collective-permute-start(f32[1024]{0:T(1024)S(1)} %add.220), channel_id=1, source_target_pairs={{0,8},{4,12},{8,0},{12,4},{16,24},{20,28},{24,16},{28,20},{1,9},{5... | collective-permute-start | bytes 12296 | tf_op jit(solution)/shard_map/ppermute | solution.py:84
  202.5 4.5 %collective-permute-start.28 = (f32[1024]{0:T(1024)S(1)}, f32[1024]{0:T(1024)S(1)}, u32[]{:S(2)}, u32[]{:S(2)}) collective-permute-start(f32[1024]{0:T(1024)S(1)} %add.221), channel_id=1, source_target_pairs={{0,16},{4,20},{8,24},{12,28},{16,0},{20,4},{24,8},{28,12},{1,17},{... | collective-permute-start | bytes 12296 | tf_op jit(solution)/shard_map/ppermute | solution.py:84
  (5 other events, 6.4 us)

commit v9 on v8

--- a/solution.py
+++ b/solution.py
@@ -55,6 +55,7 @@
     def along(p, d):
         return [(p * nb + o, d * nb + o) for o in range(nb)]
 
+    mate = lax.ppermute(block, "src", swap)
     got = {}
     for sign in (1, -1):
         cur = block
@@ -65,11 +66,11 @@
                     pairs.extend(along(p, p + sign))
             cur = lax.ppermute(cur, "src", pairs)
             got[(sign, s)] = cur
-    col = [block] + [
-        jnp.where(ia + k < na, got[(-1, k)], got[(1, na - k)]) for k in range(1, na)
-    ]
-    col = jnp.stack(col)
-    other = lax.ppermute(col, "src", swap)
+    far = jnp.stack(
+        [jnp.where(ia + k < na, got[(-1, k)], got[(1, na - k)]) for k in range(1, na)]
+    )
+    col = jnp.concatenate([block[None], far])
+    other = jnp.concatenate([mate[None], lax.ppermute(far, "src", swap)])
     first = ib == 0
     planes = jnp.stack([jnp.where(first, col, other), jnp.where(first, other, col)], axis=1)
     return planes.reshape((-1,) + block.shape[1:])

time: 208 us -> 225 us (1.082)
  waiting for transfers between devices: 130 us -> 151 us
    ppermute x2 -> x4, waiting for transfers between devices: 29.2 us -> 43.1 us  [the longest x2 43.1 us: _gather_src(): mate = lax.ppermute(block, 'src', swap)]
    ppermute x12, waiting for transfers between devices: 49.3 us -> 58.4 us  [_gather_src(): cur = lax.ppermute(cur, 'src', pairs)]
    ppermute x12, starting transfers between devices: 23 us -> 18.4 us  [_gather_src(): cur = lax.ppermute(cur, 'src', pairs)]
    another operation x4 -> x2, other arithmetic: 4.53 us -> 0.77 us  [_gather_src(): jnp.stack([jnp.where(first, col, other), jnp.where(first, other, col)], a...]
    select_n x0 -> x2, other arithmetic: none -> 3.56 us  [_gather_src(): jnp.where(first, col, other)]
    another operation x8 -> x2, other arithmetic: 5.73 us -> 2.67 us  [_gather_src(): jnp.stack([jnp.where(ia + k < na, got[-1, k], got[1, na - k]) for k in ra...]
    concatenate x0 -> x6, other arithmetic: none -> 2.92 us  [_gather_src(): col = jnp.concatenate([block[None], far])]
    concatenate x0 -> x1, local copies, waits for them, and re-layouts: none -> 2.48 us  [_gather_src(): col = jnp.concatenate([block[None], far])]
  transfers between devices with their start and end apart: 29 -> 31, of which waited for: 15 -> 17; matrix products, arithmetic and copies ran while one was open for 15% -> 13% of each run, Pallas kernels for 0% -> 0%
where the time goes in v9:
time: 225 us; the launch traced here: 224 us
  waiting for transfers between devices  151 us (67%)
  starting transfers between devices  31.4 us (14%)
  matrix products  19.8 us (9%)
  local copies, waits for them, and re-layouts  10.8 us (5%)
  other arithmetic  10.5 us (5%)
    ppermute x12, waiting for transfers between devices, _gather_src(): cur = lax.ppermute(cur, 'src', pairs)  58.4 us
    ppermute x2, waiting for transfers between devices, _gather_src(): mate = lax.ppermute(block, 'src', swap)  43.1 us
    ppermute x2, waiting for transfers between devices, per_device(): got.append((2 * ((q - k) % m) + par, lax.ppermute(wt, 'vox', chip_perm(k))))  20.6 us
    ppermute x2, waiting for transfers between devices, per_device(): lax.ppermute(halves[k].astype(jnp.bfloat16), 'vox', chip_perm(k))  18.4 us
    ppermute x12, starting transfers between devices, _gather_src(): cur = lax.ppermute(cur, 'src', pairs)  18.4 us
    dot_general x8, matrix products, pblock(): lax.dot_general(scaled, _rows(adj, rel(blk), n), (((1,), (1,)), ((), ()))...  13.4 us
    ppermute x3, waiting for transfers between devices, _sum_over_src(): v = v + lax.ppermute(v, 'src', [(i, i ^ b) for i in range(n)])  10.2 us
    dot_general x8, matrix products, per_device(): jnp.dot(w, _rows(adj, rel(blk), n), preferred_element_type=jnp.float32)  6.4 us
  transfers between devices with their start and end apart: 31, of which 17 were waited for; matrix products, arithmetic and copies ran while one was open for 13% of the time, Pallas kernels for 0%

profile of v9, /device:TPU:0, one launch (start us, length us, event | category | flops | bytes accessed | tf_op | source)
XLA Modules:
  0.0 224.2 jit_solution(15399414064780686516)
XLA Ops:
  0.0 2.5 %slice_bitcast_fusion = (bf16[1,1,256,1024]{3,2,0,1:T(8,128)(2,1)S(1)}, bf16[1,1,256,1024]{3,2,1,0:T(8,128)(2,1)}, bf16[256,1024]{1,0:T(8,128)(2,1)}, bf16[256,1024]{1,0:T(8,128)(2,1)}) fusion(bf16[512,1024]{1,0:T(8,128)(2,1)} %param.5), kind=kLoop, calls=%fused_computation.89 | loop fusion | bytes 3145728 | tf_op jit(solution)/shard_map/concatenate | solution.py:72
  2.5 4.9 %collective-permute-start.9 = (bf16[256,1024]{1,0:T(8,128)(2,1)}, bf16[256,1024]{1,0:T(8,128)(2,1)S(1)}, u32[]{:S(2)}, u32[]{:S(2)}) collective-permute-start(bf16[256,1024]{1,0:T(8,128)(2,1)} %get-tuple-element.23), channel_id=1, source_target_pairs={{0,8},{4,12},{8,16},{12,20},{16,24},{20,28},{1,9},{5,13},{9,17},{1... | collective-permute-start | bytes 1572872 | tf_op jit(solution)/shard_map/ppermute | solution.py:67
  7.4 1.3 collective-permute-start.8
  8.7 10.1 %collective-permute-done.9 = bf16[256,1024]{1,0:T(8,128)(2,1)S(1)} collective-permute-done((bf16[256,1024]{1,0:T(8,128)(2,1)}, bf16[256,1024]{1,0:T(8,128)(2,1)S(1)}, u32[]{:S(2)}, u32[]{:S(2)}) %collective-permute-start.9) | collective-permute-done | bytes 524320 | tf_op jit(solution)/shard_map/ppermute | solution.py:67
  19.6 3.3 %collective-permute-done.8 = bf16[256,1024]{1,0:T(8,128)(2,1)S(1)} collective-permute-done((bf16[256,1024]{1,0:T(8,128)(2,1)}, bf16[256,1024]{1,0:T(8,128)(2,1)S(1)}, u32[]{:S(2)}, u32[]{:S(2)}) %collective-permute-start.8) | collective-permute-done | bytes 524320 | tf_op jit(solution)/shard_map/ppermute | solution.py:67
  22.9 1.3 collective-permute-start.12
  24.2 1.5 collective-permute-start.11
  25.7 11.8 %collective-permute-done.12 = bf16[256,1024]{1,0:T(8,128)(2,1)S(1)} collective-permute-done((bf16[256,1024]{1,0:T(8,128)(2,1)S(1)}, bf16[256,1024]{1,0:T(8,128)(2,1)S(1)}, u32[]{:S(2)}, u32[]{:S(2)}) %collective-permute-start.12) | collective-permute-done | bytes 524320 | tf_op jit(solution)/shard_map/ppermute | solution.py:67
  37.5 1.3 collective-permute-start.13
  38.9 12.1 %collective-permute-done.13 = bf16[256,1024]{1,0:T(8,128)(2,1)S(1)} collective-permute-done((bf16[256,1024]{1,0:T(8,128)(2,1)S(1)}, bf16[256,1024]{1,0:T(8,128)(2,1)S(1)}, u32[]{:S(2)}, u32[]{:S(2)}) %collective-permute-start.13) | collective-permute-done | bytes 524320 | tf_op jit(solution)/shard_map/ppermute | solution.py:67
  51.1 1.3 pad_maximum_fusion.7
  52.5 1.5 collective-permute-start.15
  54.0 1.5 collective-permute-start.1
  55.5 1.3 collective-permute-start
  56.8 7.1 %collective-permute-done.1 = bf16[256,1024]{1,0:T(8,128)(2,1)S(1)} collective-permute-done((bf16[256,1024]{1,0:T(8,128)(2,1)}, bf16[256,1024]{1,0:T(8,128)(2,1)S(1)}, u32[]{:S(2)}, u32[]{:S(2)}) %collective-permute-start.1) | collective-permute-done | bytes 524320 | tf_op jit(solution)/shard_map/ppermute | solution.py:67
  63.9 1.5 collective-permute-start.2
  65.9 2.1 collective-permute-done
  67.9 1.3 collective-permute-start.4
  70.0 27.4 %collective-permute-done.14 = bf16[256,1024]{1,0:T(8,128)(2,1)} collective-permute-done((bf16[256,1024]{1,0:T(8,128)(2,1)}, bf16[256,1024]{1,0:T(8,128)(2,1)}, u32[]{:S(2)}, u32[]{:S(2)}) %collective-permute-start.14) | collective-permute-done | bytes 524320 | tf_op jit(solution)/shard_map/ppermute | solution.py:58
  97.3 1.7 broadcast_select_fusion
  102.5 1.3 collective-permute-start.5
  104.7 1.7 fusion.34
  106.9 11.8 %collective-permute-done.5 = bf16[256,1024]{1,0:T(8,128)(2,1)S(1)} collective-permute-done((bf16[256,1024]{1,0:T(8,128)(2,1)S(1)}, bf16[256,1024]{1,0:T(8,128)(2,1)S(1)}, u32[]{:S(2)}, u32[]{:S(2)}) %collective-permute-start.5) | collective-permute-done | bytes 524320 | tf_op jit(solution)/shard_map/ppermute | solution.py:67
  119.5 1.3 pad_maximum_fusion.6
  120.9 1.5 collective-permute-start.7
  122.4 1.6 fusion.6
  124.0 1.5 collective-permute-start.18
  125.5 3.0 %reshape.361 = f32[512,2,512]{2,1,0:T(2,128)S(1)} reshape(f32[512,1024]{1,0:T(8,128)} %param.7) | data formatting | bytes 4194304 | tf_op jit(solution)/shard_map/reshape | solution.py:111
  128.5 1.7 fusion.73
  130.3 7.3 %collective-permute-done.18 = bf16[512,512]{1,0:T(8,128)(2,1)} collective-permute-done((bf16[512,512]{1,0:T(8,128)(2,1)}, bf16[512,512]{1,0:T(8,128)(2,1)}, u32[]{:S(2)}, u32[]{:S(2)}) %collective-permute-start.18) | collective-permute-done | bytes 524320 | tf_op jit(solution)/shard_map/ppermute | solution.py:142
  137.5 2.6 %fusion.9 = bf16[512,512]{1,0:T(8,128)(2,1)S(1)} fusion(f32[512,512]{1,0:T(8,128)S(1)} %bitcast.74, f32[512,512]{1,0:T(8,128)} %collective-permute-done.16, bf16[512,512]{1,0:T(8,128)(2,1)} %collective-permute-done.18, bf16[2048,1024]{1,0:T(8,128)(2,1)} %bitcast.59, s32[]{:T(128)S(6)} %select_n.228, bf16[512,1024]{1,0:T(8,128)(2,1)S(1)} %copy-done.4, ...), kind=kOutput, calls=%fused_computation.27 | convolution fusion | flops 539754496 | bytes 5246980 | tf_op jit(solution)/shard_map/dot_general | solution.py:132
  140.2 1.6 collective-permute-start.19
  142.2 10.3 %collective-permute-done.19 = bf16[512,512]{1,0:T(8,128)(2,1)S(1)} collective-permute-done((bf16[512,512]{1,0:T(8,128)(2,1)S(1)}, bf16[512,512]{1,0:T(8,128)(2,1)S(1)}, u32[]{:S(2)}, u32[]{:S(2)}) %collective-permute-start.19) | collective-permute-done | bytes 524320 | tf_op jit(solution)/shard_map/ppermute | solution.py:151
  152.6 15.8 %collective-permute-done.6 = bf16[256,1024]{1,0:T(8,128)(2,1)S(1)} collective-permute-done((bf16[256,1024]{1,0:T(8,128)(2,1)}, bf16[256,1024]{1,0:T(8,128)(2,1)S(1)}, u32[]{:S(2)}, u32[]{:S(2)}) %collective-permute-start.6) | collective-permute-done | bytes 524320 | tf_op jit(solution)/shard_map/ppermute | solution.py:58
  168.3 1.8 bitcast_select_fusion.1
  171.4 1.7 fusion.17
  173.6 2.1 fusion.20
  176.9 1.1 copy-done.3
  178.0 2.0 fusion.7
  180.0 1.6 collective-permute-start.24
  183.1 11.2 %collective-permute-done.24 = bf16[512,512]{1,0:T(8,128)(2,1)S(1)} collective-permute-done((bf16[512,512]{1,0:T(8,128)(2,1)S(1)}, bf16[512,512]{1,0:T(8,128)(2,1)S(1)}, u32[]{:S(2)}, u32[]{:S(2)}) %collective-permute-start.24) | collective-permute-done | bytes 524320 | tf_op jit(solution)/shard_map/ppermute | solution.py:142
  195.2 1.6 collective-permute-start.25
  198.3 10.3 %collective-permute-done.25 = bf16[512,512]{1,0:T(8,128)(2,1)S(1)} collective-permute-done((bf16[512,512]{1,0:T(8,128)(2,1)S(1)}, bf16[512,512]{1,0:T(8,128)(2,1)S(1)}, u32[]{:S(2)}, u32[]{:S(2)}) %collective-permute-start.25) | collective-permute-done | bytes 524320 | tf_op jit(solution)/shard_map/ppermute | solution.py:151
  210.5 1.2 fusion.1
  211.8 1.6 collective-permute-start.28
  213.4 2.1 collective-permute-done.28
  215.4 3.6 %collective-permute-done.29 = f32[1024]{0:T(1024)S(1)} collective-permute-done((f32[1024]{0:T(1024)S(1)}, f32[1024]{0:T(1024)S(1)}, u32[]{:S(2)}, u32[]{:S(2)}) %collective-permute-start.29) | collective-permute-done | bytes 4128 | tf_op jit(solution)/shard_map/ppermute | solution.py:85
  219.1 4.5 %collective-permute-done.30 = f32[1024]{0:T(1024)S(1)} collective-permute-done((f32[1024]{0:T(1024)S(1)}, f32[1024]{0:T(1024)S(1)}, u32[]{:S(2)}, u32[]{:S(2)}) %collective-permute-start.30) | collective-permute-done | bytes 4128 | tf_op jit(solution)/shard_map/ppermute | solution.py:85
  (89 shorter events, 17.5 us)
Async XLA Ops:
  2.5 16.4 %collective-permute-start.9 = (bf16[256,1024]{1,0:T(8,128)(2,1)}, bf16[256,1024]{1,0:T(8,128)(2,1)S(1)}, u32[]{:S(2)}, u32[]{:S(2)}) collective-permute-start(bf16[256,1024]{1,0:T(8,128)(2,1)} %get-tuple-element.23), channel_id=1, source_target_pairs={{0,8},{4,12},{8,16},{12,20},{16,24},{20,28},{1,9},{5,13},{9,17},{1... | collective-permute-start | bytes 1572872 | tf_op jit(solution)/shard_map/ppermute | solution.py:67
  7.4 15.5 %collective-permute-start.8 = (bf16[256,1024]{1,0:T(8,128)(2,1)}, bf16[256,1024]{1,0:T(8,128)(2,1)S(1)}, u32[]{:S(2)}, u32[]{:S(2)}) collective-permute-start(bf16[256,1024]{1,0:T(8,128)(2,1)} %get-tuple-element.23), channel_id=1, source_target_pairs={{8,0},{12,4},{16,8},{20,12},{24,16},{28,20},{9,1},{13,5},{17,9},{2... | collective-permute-start | bytes 1572872 | tf_op jit(solution)/shard_map/ppermute | solution.py:67
  18.9 5.3 %collective-permute-start.10 = (bf16[256,1024]{1,0:T(8,128)(2,1)S(1)}, bf16[256,1024]{1,0:T(8,128)(2,1)S(1)}, u32[]{:S(2)}, u32[]{:S(2)}) collective-permute-start(bf16[256,1024]{1,0:T(8,128)(2,1)S(1)} %collective-permute-done.9), channel_id=1, source_target_pairs={{8,16},{12,20},{16,24},{20,28},{9,17},{13,21},{17,25},{21,29},{10,... | collective-permute-start | bytes 1572872 | tf_op jit(solution)/shard_map/ppermute | solution.py:67
  22.9 14.5 %collective-permute-start.12 = (bf16[256,1024]{1,0:T(8,128)(2,1)S(1)}, bf16[256,1024]{1,0:T(8,128)(2,1)S(1)}, u32[]{:S(2)}, u32[]{:S(2)}) collective-permute-start(bf16[256,1024]{1,0:T(8,128)(2,1)S(1)} %collective-permute-done.8), channel_id=1, source_target_pairs={{8,0},{12,4},{16,8},{20,12},{9,1},{13,5},{17,9},{21,13},{10,2},{14... | collective-permute-start | bytes 1572872 | tf_op jit(solution)/shard_map/ppermute | solution.py:67
  24.2 14.6 %collective-permute-start.11 = (bf16[256,1024]{1,0:T(8,128)(2,1)S(1)}, bf16[256,1024]{1,0:T(8,128)(2,1)}, u32[]{:S(2)}, u32[]{:S(2)}) collective-permute-start(bf16[256,1024]{1,0:T(8,128)(2,1)S(1)} %collective-permute-done.10), channel_id=1, source_target_pairs={{16,24},{20,28},{17,25},{21,29},{18,26},{22,30},{19,27},{23,31}} | collective-permute-start | bytes 1572872 | tf_op jit(solution)/shard_map/ppermute | solution.py:67
  37.5 13.6 %collective-permute-start.13 = (bf16[256,1024]{1,0:T(8,128)(2,1)S(1)}, bf16[256,1024]{1,0:T(8,128)(2,1)S(1)}, u32[]{:S(2)}, u32[]{:S(2)}) collective-permute-start(bf16[256,1024]{1,0:T(8,128)(2,1)S(1)} %collective-permute-done.12), channel_id=1, source_target_pairs={{8,0},{12,4},{9,1},{13,5},{10,2},{14,6},{11,3},{15,7}} | collective-permute-start | bytes 1572872 | tf_op jit(solution)/shard_map/ppermute | solution.py:67
  52.5 44.8 %collective-permute-start.15 = (bf16[3,256,1024]{2,1,0:T(8,128)(2,1)}, bf16[3,256,1024]{2,1,0:T(8,128)(2,1)}, u32[]{:S(2)}, u32[]{:S(2)}) collective-permute-start(bf16[3,256,1024]{2,1,0:T(8,128)(2,1)} %pad_maximum_fusion.7), channel_id=1, source_target_pairs={{0,4},{4,0},{8,12},{12,8},{16,20},{20,16},{24,28},{28,24},{1,5},{5... | collective-permute-start | bytes 4718600 | tf_op jit(solution)/shard_map/ppermute | solution.py:73
  54.0 9.9 %collective-permute-start.1 = (bf16[256,1024]{1,0:T(8,128)(2,1)}, bf16[256,1024]{1,0:T(8,128)(2,1)S(1)}, u32[]{:S(2)}, u32[]{:S(2)}) collective-permute-start(bf16[256,1024]{1,0:T(8,128)(2,1)} %get-tuple-element.24), channel_id=1, source_target_pairs={{0,8},{4,12},{8,16},{12,20},{16,24},{20,28},{1,9},{5,13},{9,17},{1... | collective-permute-start | bytes 1572872 | tf_op jit(solution)/shard_map/ppermute | solution.py:67
  55.5 12.5 %collective-permute-start = (bf16[256,1024]{1,0:T(8,128)(2,1)}, bf16[256,1024]{1,0:T(8,128)(2,1)S(1)}, u32[]{:S(2)}, u32[]{:S(2)}) collective-permute-start(bf16[256,1024]{1,0:T(8,128)(2,1)} %get-tuple-element.24), channel_id=1, source_target_pairs={{8,0},{12,4},{16,8},{20,12},{24,16},{28,20},{9,1},{13,5},{17,9},{2... | collective-permute-start | bytes 1572872 | tf_op jit(solution)/shard_map/ppermute | solution.py:67
  63.9 5.3 %collective-permute-start.2 = (bf16[256,1024]{1,0:T(8,128)(2,1)S(1)}, bf16[256,1024]{1,0:T(8,128)(2,1)}, u32[]{:S(2)}, u32[]{:S(2)}) collective-permute-start(bf16[256,1024]{1,0:T(8,128)(2,1)S(1)} %collective-permute-done.1), channel_id=1, source_target_pairs={{8,16},{12,20},{16,24},{20,28},{9,17},{13,21},{17,25},{21,29},{10,... | collective-permute-start | bytes 1572872 | tf_op jit(solution)/shard_map/ppermute | solution.py:67
  65.4 31.9 %collective-permute-start.14 = (bf16[256,1024]{1,0:T(8,128)(2,1)}, bf16[256,1024]{1,0:T(8,128)(2,1)}, u32[]{:S(2)}, u32[]{:S(2)}) collective-permute-start(bf16[256,1024]{1,0:T(8,128)(2,1)} %get-tuple-element.23), channel_id=1, source_target_pairs={{0,4},{4,0},{8,12},{12,8},{16,20},{20,16},{24,28},{28,24},{1,5},{5... | collective-permute-start | bytes 1572872 | tf_op jit(solution)/shard_map/ppermute | solution.py:58
  67.9 33.6 %collective-permute-start.4 = (bf16[256,1024]{1,0:T(8,128)(2,1)S(1)}, bf16[256,1024]{1,0:T(8,128)(2,1)S(1)}, u32[]{:S(2)}, u32[]{:S(2)}) collective-permute-start(bf16[256,1024]{1,0:T(8,128)(2,1)S(1)} %collective-permute-done), channel_id=1, source_target_pairs={{8,0},{12,4},{16,8},{20,12},{9,1},{13,5},{17,9},{21,13},{10,2},{14... | collective-permute-start | bytes 1572872 | tf_op jit(solution)/shard_map/ppermute | solution.py:67
  69.2 34.5 %collective-permute-start.3 = (bf16[256,1024]{1,0:T(8,128)(2,1)}, bf16[256,1024]{1,0:T(8,128)(2,1)S(1)}, u32[]{:S(2)}, u32[]{:S(2)}) collective-permute-start(bf16[256,1024]{1,0:T(8,128)(2,1)} %collective-permute-done.2), channel_id=1, source_target_pairs={{16,24},{20,28},{17,25},{21,29},{18,26},{22,30},{19,27},{23,31}} | collective-permute-start | bytes 1572872 | tf_op jit(solution)/shard_map/ppermute | solution.py:67
  99.5 1.2 copy-start.4
  99.9 22.5 %copy-start = (bf16[4,2,256,1024]{3,2,1,0:T(8,128)(2,1)}, bf16[4,2,256,1024]{3,2,1,0:T(8,128)(2,1)S(1)}, u32[]{:S(2)}) copy-start(bf16[4,2,256,1024]{3,2,1,0:T(8,128)(2,1)S(1)} %copy.15) | copy-start | bytes 12582916
  101.4 20.9 %collective-permute-start.17 = (f32[512,512]{1,0:T(8,128)S(1)}, f32[512,512]{1,0:T(8,128)S(1)}, u32[]{:S(2)}, u32[]{:S(2)}) collective-permute-start(f32[512,512]{1,0:T(8,128)S(1)} %fusion.31), channel_id=1, source_target_pairs={{0,1},{1,0},{2,3},{3,2},{4,5},{5,4},{6,7},{7,6},{8,9},{9,8},{10,11... | collective-permute-start | bytes 3145736 | tf_op jit(solution)/shard_map/ppermute | solution.py:139
  102.5 16.2 %collective-permute-start.5 = (bf16[256,1024]{1,0:T(8,128)(2,1)S(1)}, bf16[256,1024]{1,0:T(8,128)(2,1)S(1)}, u32[]{:S(2)}, u32[]{:S(2)}) collective-permute-start(bf16[256,1024]{1,0:T(8,128)(2,1)S(1)} %collective-permute-done.4), channel_id=1, source_target_pairs={{8,0},{12,4},{9,1},{13,5},{10,2},{14,6},{11,3},{15,7}} | collective-permute-start | bytes 1572872 | tf_op jit(solution)/shard_map/ppermute | solution.py:67
  106.4 23.9 %collective-permute-start.16 = (f32[512,512]{1,0:T(8,128)}, f32[512,512]{1,0:T(8,128)}, u32[]{:S(2)}, u32[]{:S(2)}) collective-permute-start(f32[512,512]{1,0:T(8,128)} %fusion.34), channel_id=1, source_target_pairs={{0,1},{1,0},{2,3},{3,2},{4,5},{5,4},{6,7},{7,6},{8,9},{9,8},{10,11... | collective-permute-start | bytes 3145736 | tf_op jit(solution)/shard_map/ppermute | solution.py:139
  120.9 47.4 %collective-permute-start.7 = (bf16[3,256,1024]{2,1,0:T(8,128)(2,1)}, bf16[3,256,1024]{2,1,0:T(8,128)(2,1)}, u32[]{:S(2)}, u32[]{:S(2)}) collective-permute-start(bf16[3,256,1024]{2,1,0:T(8,128)(2,1)} %pad_maximum_fusion.6), channel_id=1, source_target_pairs={{0,4},{4,0},{8,12},{12,8},{16,20},{20,16},{24,28},{28,24},{1,5},{5... | collective-permute-start | bytes 4718600 | tf_op jit(solution)/shard_map/ppermute | solution.py:73
  124.0 13.6 %collective-permute-start.18 = (bf16[512,512]{1,0:T(8,128)(2,1)}, bf16[512,512]{1,0:T(8,128)(2,1)}, u32[]{:S(2)}, u32[]{:S(2)}) collective-permute-start(bf16[512,512]{1,0:T(8,128)(2,1)} %fusion.6), channel_id=1, source_target_pairs={{0,2},{1,3},{2,0},{3,1},{4,6},{5,7},{6,4},{7,5},{8,10},{9,11},{10,... | collective-permute-start | bytes 1572872 | tf_op jit(solution)/shard_map/ppermute | solution.py:142
  137.5 30.8 %copy-start.8 = (bf16[1,1,256,1024]{3,2,1,0:T(8,128)(2,1)S(1)}, bf16[1,1,256,1024]{3,2,1,0:T(8,128)(2,1)}, u32[]{:S(2)}) copy-start(bf16[1,1,256,1024]{3,2,1,0:T(8,128)(2,1)} %get-tuple-element.33) | copy-start | bytes 1572868
  137.5 30.8 %copy-start.9 = (bf16[1,1,256,1024]{3,2,1,0:T(8,128)(2,1)S(1)}, bf16[1,1,256,1024]{3,2,1,0:T(8,128)(2,1)}, u32[]{:S(2)}) copy-start(bf16[1,1,256,1024]{3,2,1,0:T(8,128)(2,1)} %get-tuple-element.31) | copy-start | bytes 1572868
  137.5 30.8 %copy-start.10 = (bf16[1,1,256,1024]{3,2,1,0:T(8,128)(2,1)S(1)}, bf16[1,1,256,1024]{3,2,1,0:T(8,128)(2,1)}, u32[]{:S(2)}) copy-start(bf16[1,1,256,1024]{3,2,1,0:T(8,128)(2,1)} %get-tuple-element.35) | copy-start | bytes 1572868
  137.5 30.8 %copy-start.11 = (bf16[1,1,256,1024]{3,2,1,0:T(8,128)(2,1)S(1)}, bf16[1,1,256,1024]{3,2,1,0:T(8,128)(2,1)}, u32[]{:S(2)}) copy-start(bf16[1,1,256,1024]{3,2,1,0:T(8,128)(2,1)} %get-tuple-element.22) | copy-start | bytes 1572868
  140.1 30.0 %copy-start.6 = (bf16[512,512]{1,0:T(8,128)(2,1)}, bf16[512,512]{1,0:T(8,128)(2,1)S(1)}, u32[]{:S(2)}) copy-start(bf16[512,512]{1,0:T(8,128)(2,1)S(1)} %fusion.9) | copy-start | bytes 1572868
  140.2 12.4 %collective-permute-start.19 = (bf16[512,512]{1,0:T(8,128)(2,1)S(1)}, bf16[512,512]{1,0:T(8,128)(2,1)S(1)}, u32[]{:S(2)}, u32[]{:S(2)}) collective-permute-start(bf16[512,512]{1,0:T(8,128)(2,1)S(1)} %fusion.9), channel_id=1, source_target_pairs={{0,2},{1,3},{2,0},{3,1},{4,6},{5,7},{6,4},{7,5},{8,10},{9,11},{10,... | collective-permute-start | bytes 1572872 | tf_op jit(solution)/shard_map/ppermute | solution.py:151
  141.7 26.6 %collective-permute-start.6 = (bf16[256,1024]{1,0:T(8,128)(2,1)}, bf16[256,1024]{1,0:T(8,128)(2,1)S(1)}, u32[]{:S(2)}, u32[]{:S(2)}) collective-permute-start(bf16[256,1024]{1,0:T(8,128)(2,1)} %get-tuple-element.24), channel_id=1, source_target_pairs={{0,4},{4,0},{8,12},{12,8},{16,20},{20,16},{24,28},{28,24},{1,5},{5... | collective-permute-start | bytes 1572872 | tf_op jit(solution)/shard_map/ppermute | solution.py:58
  142.2 28.4 %collective-permute-start.20 = (bf16[512,512]{1,0:T(8,128)(2,1)S(1)}, bf16[512,512]{1,0:T(8,128)(2,1)S(1)}, u32[]{:S(2)}, u32[]{:S(2)}) collective-permute-start(bf16[512,512]{1,0:T(8,128)(2,1)S(1)} %fusion.9), channel_id=1, source_target_pairs={{0,1},{1,0},{2,3},{3,2},{4,5},{5,4},{6,7},{7,6},{8,9},{9,8},{10,11... | collective-permute-start | bytes 1572872 | tf_op jit(solution)/shard_map/ppermute | solution.py:152
  152.5 17.6 %copy-start.16 = (bf16[512,512]{1,0:T(8,128)(2,1)}, bf16[512,512]{1,0:T(8,128)(2,1)S(1)}, u32[]{:S(2)}) copy-start(bf16[512,512]{1,0:T(8,128)(2,1)S(1)} %collective-permute-done.19) | copy-start | bytes 1572868
  152.6 18.1 %collective-permute-start.21 = (bf16[512,512]{1,0:T(8,128)(2,1)S(1)}, bf16[512,512]{1,0:T(8,128)(2,1)S(1)}, u32[]{:S(2)}, u32[]{:S(2)}) collective-permute-start(bf16[512,512]{1,0:T(8,128)(2,1)S(1)} %collective-permute-done.19), channel_id=1, source_target_pairs={{0,1},{1,0},{2,3},{3,2},{4,5},{5,4},{6,7},{7,6},{8,9},{9,8},{10,11... | collective-permute-start | bytes 1572872 | tf_op jit(solution)/shard_map/ppermute | solution.py:152
  170.6 2.6 %copy-start.2 = (bf16[4,2,256,1024]{3,2,1,0:T(8,128)(2,1)}, bf16[4,2,256,1024]{3,2,1,0:T(8,128)(2,1)S(1)}, u32[]{:S(2)}) copy-start(bf16[4,2,256,1024]{3,2,1,0:T(8,128)(2,1)S(1)} %pad_maximum_fusion) | copy-start | bytes 12582916
  171.4 1.9 copy-start.12
  171.4 2.0 copy-start.5
  173.3 3.6 %collective-permute-start.23 = (f32[512,512]{1,0:T(8,128)}, f32[512,512]{1,0:T(8,128)}, u32[]{:S(2)}, u32[]{:S(2)}) collective-permute-start(f32[512,512]{1,0:T(8,128)} %fusion.17), channel_id=1, source_target_pairs={{0,1},{1,0},{2,3},{3,2},{4,5},{5,4},{6,7},{7,6},{8,9},{9,8},{10,11... | collective-permute-start | bytes 3145736 | tf_op jit(solution)/shard_map/ppermute | solution.py:139
  173.5 2.6 %copy-start.1 = (bf16[4,2,256,1024]{3,2,1,0:T(8,128)(2,1)S(1)}, bf16[4,2,256,1024]{3,2,1,0:T(8,128)(2,1)}, u32[]{:S(2)}) copy-start(bf16[4,2,256,1024]{3,2,1,0:T(8,128)(2,1)} %copy-done) | copy-start | bytes 12582916
  173.5 2.6 %copy-start.17 = (bf16[512,512]{1,0:T(8,128)(2,1)S(1)}, bf16[512,512]{1,0:T(8,128)(2,1)}, u32[]{:S(2)}) copy-start(bf16[512,512]{1,0:T(8,128)(2,1)} %copy-done.16) | copy-start | bytes 1572868
  175.7 2.3 %copy-start.3 = (bf16[4,2,256,1024]{3,2,1,0:T(8,128)(2,1)S(1)}, bf16[4,2,256,1024]{3,2,1,0:T(8,128)(2,1)}, u32[]{:S(2)}) copy-start(bf16[4,2,256,1024]{3,2,1,0:T(8,128)(2,1)} %copy-done.2) | copy-start | bytes 12582916
  175.7 7.4 %collective-permute-start.22 = (f32[512,512]{1,0:T(8,128)S(1)}, f32[512,512]{1,0:T(8,128)S(1)}, u32[]{:S(2)}, u32[]{:S(2)}) collective-permute-start(f32[512,512]{1,0:T(8,128)S(1)} %fusion.20), channel_id=1, source_target_pairs={{0,1},{1,0},{2,3},{3,2},{4,5},{5,4},{6,7},{7,6},{8,9},{9,8},{10,11... | collective-permute-start | bytes 3145736 | tf_op jit(solution)/shard_map/ppermute | solution.py:139
  176.9 4.7 %copy-start.7 = (bf16[512,512]{1,0:T(8,128)(2,1)S(1)}, bf16[512,512]{1,0:T(8,128)(2,1)}, u32[]{:S(2)}) copy-start(bf16[512,512]{1,0:T(8,128)(2,1)} %copy-done.6) | copy-start | bytes 1572868
  180.0 2.3 %copy-start.15 = (bf16[512,512]{1,0:T(8,128)(2,1)S(1)}, bf16[512,512]{1,0:T(8,128)(2,1)}, u32[]{:S(2)}) copy-start(bf16[512,512]{1,0:T(8,128)(2,1)} %copy-done.14) | copy-start | bytes 1572868
  180.0 14.3 %collective-permute-start.24 = (bf16[512,512]{1,0:T(8,128)(2,1)S(1)}, bf16[512,512]{1,0:T(8,128)(2,1)S(1)}, u32[]{:S(2)}, u32[]{:S(2)}) collective-permute-start(bf16[512,512]{1,0:T(8,128)(2,1)S(1)} %fusion.7), channel_id=1, source_target_pairs={{0,2},{1,3},{2,0},{3,1},{4,6},{5,7},{6,4},{7,5},{8,10},{9,11},{10,... | collective-permute-start | bytes 1572872 | tf_op jit(solution)/shard_map/ppermute | solution.py:142
  194.3 2.4 %copy-start.13 = (bf16[512,512]{1,0:T(8,128)(2,1)S(1)}, bf16[512,512]{1,0:T(8,128)(2,1)}, u32[]{:S(2)}) copy-start(bf16[512,512]{1,0:T(8,128)(2,1)} %copy-done.12) | copy-start | bytes 1572868
  195.2 13.4 %collective-permute-start.25 = (bf16[512,512]{1,0:T(8,128)(2,1)S(1)}, bf16[512,512]{1,0:T(8,128)(2,1)S(1)}, u32[]{:S(2)}, u32[]{:S(2)}) collective-permute-start(bf16[512,512]{1,0:T(8,128)(2,1)S(1)} %fusion.8), channel_id=1, source_target_pairs={{0,2},{1,3},{2,0},{3,1},{4,6},{5,7},{6,4},{7,5},{8,10},{9,11},{10,... | collective-permute-start | bytes 1572872 | tf_op jit(solution)/shard_map/ppermute | solution.py:151
  197.5 11.9 %collective-permute-start.26 = (bf16[512,512]{1,0:T(8,128)(2,1)S(1)}, bf16[512,512]{1,0:T(8,128)(2,1)S(1)}, u32[]{:S(2)}, u32[]{:S(2)}) collective-permute-start(bf16[512,512]{1,0:T(8,128)(2,1)S(1)} %fusion.8), channel_id=1, source_target_pairs={{0,1},{1,0},{2,3},{3,2},{4,5},{5,4},{6,7},{7,6},{8,9},{9,8},{10,11... | collective-permute-start | bytes 1572872 | tf_op jit(solution)/shard_map/ppermute | solution.py:152
  208.6 1.9 collective-permute-start.27
  211.8 3.7 %collective-permute-start.28 = (f32[1024]{0:T(1024)S(1)}, f32[1024]{0:T(1024)S(1)}, u32[]{:S(2)}, u32[]{:S(2)}) collective-permute-start(f32[1024]{0:T(1024)S(1)} %fusion.1), channel_id=1, source_target_pairs={{0,4},{4,0},{8,12},{12,8},{16,20},{20,16},{24,28},{28,24},{1,5},{5... | collective-permute-start | bytes 12296 | tf_op jit(solution)/shard_map/ppermute | solution.py:85
  215.4 3.6 %collective-permute-start.29 = (f32[1024]{0:T(1024)S(1)}, f32[1024]{0:T(1024)S(1)}, u32[]{:S(2)}, u32[]{:S(2)}) collective-permute-start(f32[1024]{0:T(1024)S(1)} %add.220), channel_id=1, source_target_pairs={{0,8},{4,12},{8,0},{12,4},{16,24},{20,28},{24,16},{28,20},{1,9},{5... | collective-permute-start | bytes 12296 | tf_op jit(solution)/shard_map/ppermute | solution.py:85
  219.1 4.5 %collective-permute-start.30 = (f32[1024]{0:T(1024)S(1)}, f32[1024]{0:T(1024)S(1)}, u32[]{:S(2)}, u32[]{:S(2)}) collective-permute-start(f32[1024]{0:T(1024)S(1)} %add.221), channel_id=1, source_target_pairs={{0,16},{4,20},{8,24},{12,28},{16,0},{20,4},{24,8},{28,12},{1,17},{... | collective-permute-start | bytes 12296 | tf_op jit(solution)/shard_map/ppermute | solution.py:85
  (2 other events, 2.0 us)

commit v10 on v8

--- a/solution.py
+++ b/solution.py
@@ -5,7 +5,7 @@
 from jax import lax
 from jax.sharding import PartitionSpec as P
 
-CHUNKS = 2
+SPLIT = (1, 2, 1)
 
 
 def _rows(a, blk, n):
@@ -96,9 +96,12 @@
     t = nsrc // vox
     sl, vl = forward_voxel_field.shape
     ds = adjoint_voxel_field.shape[0]
-    chunks = CHUNKS if ds % CHUNKS == 0 else 1
-    r = ds // chunks
-    n = t * r
+    unit = ds // sum(SPLIT)
+    if unit * sum(SPLIT) == ds and unit % 8 == 0:
+        bounds = [unit * sum(SPLIT[:k]) for k in range(len(SPLIT) + 1)]
+    else:
+        bounds = [0, ds]
+    chunks = len(bounds) - 1
     pair = [(j, j ^ 1) for j in range(vox)]
 
     def chip_perm(k):
@@ -120,12 +123,13 @@
         def rel(blk):
             return blk
     def gather(c):
-        return _gather_src(adjoint_voxel_field[c * r:(c + 1) * r], grid)
+        return _gather_src(adjoint_voxel_field[bounds[c]:bounds[c + 1]], grid)
 
     back = jnp.zeros((sl, vl), jnp.float32)
     nxt = gather(0)
     for c in range(chunks):
         adj = nxt
+        n = t * (bounds[c + 1] - bounds[c])
 
         def pblock(blk):
             return lax.dot_general(
@@ -142,7 +146,7 @@
                 halves[k].astype(jnp.bfloat16), "vox", chip_perm(k)
             ).astype(jnp.float32)
 
-        w_c = weight[:, :, c * r:(c + 1) * r].reshape(sl, n)
+        w_c = weight[:, :, bounds[c]:bounds[c + 1]].reshape(sl, n)
         wt = (w_c * share).astype(jnp.bfloat16)
 
         got = [(me, wt)]

time: 208 us -> 217 us (1.043)
  waiting for transfers between devices: 130 us -> 103 us
  starting transfers between devices: 33.4 us -> 55.2 us
  local copies, waits for them, and re-layouts: 10.7 us -> 16.8 us
  other arithmetic: 10.9 us -> 15.6 us
    ppermute x12 -> x18, waiting for transfers between devices: 49.3 us -> 37.2 us  [_gather_src(): cur = lax.ppermute(cur, 'src', pairs)]
    ppermute x2 -> x3, waiting for transfers between devices: 20.1 us -> 8.64 us  [per_device(): lax.ppermute(halves[k].astype(jnp.bfloat16), 'vox', chip_perm(k))]
    ppermute x12 -> x18, starting transfers between devices: 23 us -> 33.6 us  [_gather_src(): cur = lax.ppermute(cur, 'src', pairs)]
    ppermute x2 -> x3, waiting for transfers between devices: 22.9 us -> 16.6 us  [per_device(): got.append((2 * ((q - k) % m) + par, lax.ppermute(wt, 'vox', chip_perm(k))))]
    another operation x8 -> x12, other arithmetic: 5.73 us -> 9.22 us  [_gather_src(): col = jnp.stack(col)]
    ppermute x2 -> x3, starting transfers between devices: 1.76 us -> 4.62 us  [_gather_src(): other = lax.ppermute(col, 'src', swap)]
    unnamed x50 -> x59, local copies, waits for them, and re-layouts: 3.25 us -> 5.72 us
    ppermute x2 -> x3, starting transfers between devices: 2.25 us -> 4.62 us  [per_device(): lax.ppermute(halves[k].astype(jnp.bfloat16), 'vox', chip_perm(k))]
  transfers between devices with their start and end apart: 29 -> 42, of which waited for: 15 -> 18; matrix products, arithmetic and copies ran while one was open for 15% -> 21% of each run, Pallas kernels for 0% -> 0%
where the time goes in v10:
time: 217 us; the launch traced here: 216 us
  waiting for transfers between devices  103 us (47%)
  starting transfers between devices  55.2 us (25%)
  matrix products  23.6 us (11%)
  local copies, waits for them, and re-layouts  16.8 us (8%)
  other arithmetic  15.6 us (7%)
    ppermute x18, waiting for transfers between devices, _gather_src(): cur = lax.ppermute(cur, 'src', pairs)  37.2 us
    ppermute x18, starting transfers between devices, _gather_src(): cur = lax.ppermute(cur, 'src', pairs)  33.6 us
    ppermute x3, waiting for transfers between devices, _gather_src(): other = lax.ppermute(col, 'src', swap)  31.1 us
    ppermute x3, waiting for transfers between devices, per_device(): got.append((2 * ((q - k) % m) + par, lax.ppermute(wt, 'vox', chip_perm(k))))  16.6 us
    dot_general x12, matrix products, pblock(): lax.dot_general(scaled, _rows(adj, rel(blk), n), (((1,), (1,)), ((), ()))...  16.2 us
    another operation x12, other arithmetic, _gather_src(): col = jnp.stack(col)  9.22 us
    ppermute x3, waiting for transfers between devices, per_device(): lax.ppermute(halves[k].astype(jnp.bfloat16), 'vox', chip_perm(k))  8.64 us
    ppermute x3, waiting for transfers between devices, _sum_over_src(): v = v + lax.ppermute(v, 'src', [(i, i ^ b) for i in range(n)])  8.19 us
  transfers between devices with their start and end apart: 42, of which 18 were waited for; matrix products, arithmetic and copies ran while one was open for 21% of the time, Pallas kernels for 0%

profile of v10, /device:TPU:0, one launch (start us, length us, event | category | flops | bytes accessed | tf_op | source)
XLA Modules:
  0.0 215.5 jit_solution(11249497866171730531)
XLA Ops:
  1.2 1.3 collective-permute-start
  2.5 1.9 slice_bitcast_fusion.1
  5.6 6.9 %collective-permute-start.8 = (bf16[128,1024]{1,0:T(8,128)(2,1)S(1)}, bf16[128,1024]{1,0:T(8,128)(2,1)}, u32[]{:S(2)}, u32[]{:S(2)}) collective-permute-start(bf16[128,1024]{1,0:T(8,128)(2,1)S(1)} %get-tuple-element.36), channel_id=1, source_target_pairs={{0,8},{4,12},{8,16},{12,20},{16,24},{20,28},{1,9},{5,13},{9,17},{1... | collective-permute-start | bytes 786440 | tf_op jit(solution)/shard_map/ppermute | solution.py:66
  12.6 3.2 %collective-permute-start.1 = (bf16[256,1024]{1,0:T(8,128)(2,1)S(1)}, bf16[256,1024]{1,0:T(8,128)(2,1)S(1)}, u32[]{:S(2)}, u32[]{:S(2)}) collective-permute-start(bf16[256,1024]{1,0:T(8,128)(2,1)S(1)} %get-tuple-element.38), channel_id=1, source_target_pairs={{0,8},{4,12},{8,16},{12,20},{16,24},{20,28},{1,9},{5,13},{9,17},{1... | collective-permute-start | bytes 1572872 | tf_op jit(solution)/shard_map/ppermute | solution.py:66
  15.8 7.9 %collective-permute-done.7 = bf16[128,1024]{1,0:T(8,128)(2,1)S(1)} collective-permute-done((bf16[128,1024]{1,0:T(8,128)(2,1)S(1)}, bf16[128,1024]{1,0:T(8,128)(2,1)S(1)}, u32[]{:S(2)}, u32[]{:S(2)}) %collective-permute-start.7) | collective-permute-done | bytes 262176 | tf_op jit(solution)/shard_map/ppermute | solution.py:66
  25.0 1.4 collective-permute-start.9
  27.7 5.5 %collective-permute-done.11 = bf16[128,1024]{1,0:T(8,128)(2,1)} collective-permute-done((bf16[128,1024]{1,0:T(8,128)(2,1)S(1)}, bf16[128,1024]{1,0:T(8,128)(2,1)}, u32[]{:S(2)}, u32[]{:S(2)}) %collective-permute-start.11) | collective-permute-done | bytes 262176 | tf_op jit(solution)/shard_map/ppermute | solution.py:66
  36.2 1.5 collective-permute-start.2
  37.6 13.2 %collective-permute-done.12 = bf16[128,1024]{1,0:T(8,128)(2,1)} collective-permute-done((bf16[128,1024]{1,0:T(8,128)(2,1)}, bf16[128,1024]{1,0:T(8,128)(2,1)}, u32[]{:S(2)}, u32[]{:S(2)}) %collective-permute-start.12) | collective-permute-done | bytes 262176 | tf_op jit(solution)/shard_map/ppermute | solution.py:66
  51.8 1.3 collective-permute-start.5
  55.2 1.5 collective-permute-start.13
  56.8 6.0 %collective-permute-start.21 = (bf16[128,1024]{1,0:T(8,128)(2,1)}, bf16[128,1024]{1,0:T(8,128)(2,1)}, u32[]{:S(2)}, u32[]{:S(2)}) collective-permute-start(bf16[128,1024]{1,0:T(8,128)(2,1)} %get-tuple-element.35), channel_id=1, source_target_pairs={{0,8},{4,12},{8,16},{12,20},{16,24},{20,28},{1,9},{5,13},{9,17},{1... | collective-permute-start | bytes 786440 | tf_op jit(solution)/shard_map/ppermute | solution.py:66
  63.7 1.7 collective-permute-done.5
  66.6 1.7 pad_maximum_fusion.1
  68.3 1.6 collective-permute-start.6
  69.9 11.8 %collective-permute-done.13 = bf16[4,128,1024]{2,1,0:T(8,128)(2,1)} collective-permute-done((bf16[4,128,1024]{2,1,0:T(8,128)(2,1)}, bf16[4,128,1024]{2,1,0:T(8,128)(2,1)}, u32[]{:S(2)}, u32[]{:S(2)}) %collective-permute-start.13) | collective-permute-done | bytes 1048608 | tf_op jit(solution)/shard_map/ppermute | solution.py:72
  81.7 1.4 select_bitcast_fusion.5
  87.0 4.0 %reshape.23 = f32[512,2,512]{2,1,0:T(2,128)} reshape(f32[512,1024]{1,0:T(8,128)} %param.7) | data formatting | bytes 4194304 | tf_op jit(solution)/shard_map/reshape | solution.py:113
  92.9 1.5 fusion.10
  94.4 1.6 collective-permute-start.16
  100.2 2.5 %collective-permute-done.16 = bf16[512,256]{1,0:T(8,128)(2,1)S(1)} collective-permute-done((bf16[512,256]{1,0:T(8,128)(2,1)S(1)}, bf16[512,256]{1,0:T(8,128)(2,1)S(1)}, u32[]{:S(2)}, u32[]{:S(2)}) %collective-permute-start.16) | collective-permute-done | bytes 262176 | tf_op jit(solution)/shard_map/ppermute | solution.py:145
  103.2 1.6 collective-permute-start.17
  104.8 8.0 %collective-permute-done.24 = bf16[128,1024]{1,0:T(8,128)(2,1)S(1)} collective-permute-done((bf16[128,1024]{1,0:T(8,128)(2,1)}, bf16[128,1024]{1,0:T(8,128)(2,1)S(1)}, u32[]{:S(2)}, u32[]{:S(2)}) %collective-permute-start.24) | collective-permute-done | bytes 262176 | tf_op jit(solution)/shard_map/ppermute | solution.py:66
  115.7 7.6 %collective-permute-done.6 = bf16[4,256,1024]{2,1,0:T(8,128)(2,1)} collective-permute-done((bf16[4,256,1024]{2,1,0:T(8,128)(2,1)}, bf16[4,256,1024]{2,1,0:T(8,128)(2,1)}, u32[]{:S(2)}, u32[]{:S(2)}) %collective-permute-start.6) | collective-permute-done | bytes 2097184 | tf_op jit(solution)/shard_map/ppermute | solution.py:72
  123.3 2.0 select_bitcast_fusion.1
  125.8 2.2 %fusion.22 = f32[512,512]{1,0:T(8,128)} fusion(bf16[2048,1024]{1,0:T(8,128)(2,1)S(1)} %bitcast.63, s32[]{:T(128)S(6)} %select_n.314, bf16[512,1024]{1,0:T(8,128)(2,1)S(1)} %copy-done.2, f32[1024]{0:T(1024)S(1)} %copy-done.28), kind=kOutput, calls=%fused_computation.38 | convolution fusion | flops 538443776 | bytes 3149828 | tf_op jit(solution)/shard_map/dot_general | solution.py:135
  129.5 1.5 collective-permute-start.26
  131.0 2.9 %fusion.25 = f32[512,512]{1,0:T(8,128)} fusion(bf16[2048,1024]{1,0:T(8,128)(2,1)} %bitcast.64, s32[]{:T(128)S(6)} %select_n.312, bf16[512,1024]{1,0:T(8,128)(2,1)S(1)} %copy-done.2, f32[1024]{0:T(1024)S(1)} %copy-done.28), kind=kOutput, calls=%fused_computation.41 | convolution fusion | flops 538443776 | bytes 3149828 | tf_op jit(solution)/shard_map/dot_general | solution.py:135
  134.1 3.1 %fusion.4 = bf16[512,512]{1,0:T(8,128)(2,1)} fusion(f32[512,512]{1,0:T(8,128)} %collective-permute-done.28, bf16[2048,1024]{1,0:T(8,128)(2,1)} %bitcast.65, s32[]{:T(128)S(6)} %select_n.313, bf16[512,1024]{1,0:T(8,128)(2,1)S(1)} %copy-done.2, f32[1024]{0:T(1024)S(1)} %copy-done.28), kind=kOutput, calls=%fused_computation.14 | convolution fusion | flops 538968064 | bytes 3674116 | tf_op jit(solution)/shard_map/dot_general | solution.py:135
  137.3 1.5 collective-permute-start.29
  138.8 2.6 %slice.25 = f32[512,2,256]{2,1,0:T(2,128)} slice(f32[512,2,512]{2,1,0:T(2,128)} %reshape.23), slice={[0:512], [0:2], [128:384]} | slice | bytes 2097152 | tf_op jit(solution)/shard_map/slice | solution.py:149
  141.4 2.3 %copy.9 = f32[64,8,2,256]{3,1,2,0:T(8,128)} copy(f32[64,8,2,256]{3,2,1,0:T(2,128)} %bitcast.87) | data formatting | bytes 2097152
  143.7 11.7 %collective-permute-done.26 = bf16[4,128,1024]{2,1,0:T(8,128)(2,1)} collective-permute-done((bf16[4,128,1024]{2,1,0:T(8,128)(2,1)}, bf16[4,128,1024]{2,1,0:T(8,128)(2,1)}, u32[]{:S(2)}, u32[]{:S(2)}) %collective-permute-start.26) | collective-permute-done | bytes 1048608 | tf_op jit(solution)/shard_map/ppermute | solution.py:72
  155.4 1.6 select_bitcast_fusion.3
  158.2 1.3 copy-done.1
  159.5 2.2 %fusion.5 = bf16[512,512]{1,0:T(8,128)(2,1)S(1)} fusion(f32[512,512]{1,0:T(8,128)S(1)} %bitcast.88, f32[512,512]{1,0:T(8,128)} %collective-permute-done.27, bf16[512,512]{1,0:T(8,128)(2,1)} %collective-permute-done.29, bf16[2048,1024]{1,0:T(8,128)(2,1)S(1)} %bitcast.66, s32[]{:T(128)S(6)} %select_n.311, bf16[512,1024]{1,0:T(8,128)(2,1)S(1)} %copy-done.2, ...), kind=kOutput, calls=%fused_computation.15 | convolution fusion | flops 539754496 | bytes 5246980 | tf_op jit(solution)/shard_map/dot_general | solution.py:135
  161.7 1.6 collective-permute-start.30
  164.3 11.0 %collective-permute-done.30 = bf16[512,512]{1,0:T(8,128)(2,1)S(1)} collective-permute-done((bf16[512,512]{1,0:T(8,128)(2,1)S(1)}, bf16[512,512]{1,0:T(8,128)(2,1)S(1)}, u32[]{:S(2)}, u32[]{:S(2)}) %collective-permute-start.30) | collective-permute-done | bytes 524320 | tf_op jit(solution)/shard_map/ppermute | solution.py:154
  181.5 1.6 collective-permute-start.35
  183.8 6.1 %collective-permute-done.35 = bf16[512,256]{1,0:T(8,128)(2,1)S(1)} collective-permute-done((bf16[512,256]{1,0:T(8,128)(2,1)S(1)}, bf16[512,256]{1,0:T(8,128)(2,1)S(1)}, u32[]{:S(2)}, u32[]{:S(2)}) %collective-permute-start.35) | collective-permute-done | bytes 262176 | tf_op jit(solution)/shard_map/ppermute | solution.py:145
  190.5 1.6 collective-permute-start.36
  192.5 5.6 %collective-permute-done.36 = bf16[512,256]{1,0:T(8,128)(2,1)S(1)} collective-permute-done((bf16[512,256]{1,0:T(8,128)(2,1)S(1)}, bf16[512,256]{1,0:T(8,128)(2,1)S(1)}, u32[]{:S(2)}, u32[]{:S(2)}) %collective-permute-start.36) | collective-permute-done | bytes 262176 | tf_op jit(solution)/shard_map/ppermute | solution.py:154
  199.6 1.5 fusion.1
  201.0 1.6 collective-permute-start.39
  202.6 2.1 collective-permute-done.39
  204.7 4.1 %collective-permute-start.40 = (f32[1024]{0:T(1024)S(1)}, f32[1024]{0:T(1024)S(1)}, u32[]{:S(2)}, u32[]{:S(2)}) collective-permute-start(f32[1024]{0:T(1024)S(1)} %add.304), channel_id=1, source_target_pairs={{0,8},{4,12},{8,0},{12,4},{16,24},{20,28},{24,16},{28,20},{1,9},{5... | collective-permute-start | bytes 12296 | tf_op jit(solution)/shard_map/ppermute | solution.py:84
  208.8 1.6 collective-permute-done.40
  210.4 4.5 %collective-permute-done.41 = f32[1024]{0:T(1024)S(1)} collective-permute-done((f32[1024]{0:T(1024)S(1)}, f32[1024]{0:T(1024)S(1)}, u32[]{:S(2)}, u32[]{:S(2)}) %collective-permute-start.41) | collective-permute-done | bytes 4128 | tf_op jit(solution)/shard_map/ppermute | solution.py:84
  (146 shorter events, 40.5 us)
Async XLA Ops:
  1.2 65.4 %copy-start.4 = (bf16[1,256,1024]{2,1,0:T(8,128)(2,1)}, bf16[1,256,1024]{2,1,0:T(8,128)(2,1)S(1)}, u32[]{:S(2)}) copy-start(bf16[1,256,1024]{2,1,0:T(8,128)(2,1)S(1)} %get-tuple-element.37) | copy-start | bytes 1572868
  1.2 25.2 %collective-permute-start = (bf16[256,1024]{1,0:T(8,128)(2,1)S(1)}, bf16[256,1024]{1,0:T(8,128)(2,1)S(1)}, u32[]{:S(2)}, u32[]{:S(2)}) collective-permute-start(bf16[256,1024]{1,0:T(8,128)(2,1)S(1)} %get-tuple-element.38), channel_id=1, source_target_pairs={{8,0},{12,4},{16,8},{20,12},{24,16},{28,20},{9,1},{13,5},{17,9},{2... | collective-permute-start | bytes 1572872 | tf_op jit(solution)/shard_map/ppermute | solution.py:66
  4.3 19.3 %collective-permute-start.7 = (bf16[128,1024]{1,0:T(8,128)(2,1)S(1)}, bf16[128,1024]{1,0:T(8,128)(2,1)S(1)}, u32[]{:S(2)}, u32[]{:S(2)}) collective-permute-start(bf16[128,1024]{1,0:T(8,128)(2,1)S(1)} %get-tuple-element.36), channel_id=1, source_target_pairs={{8,0},{12,4},{16,8},{20,12},{24,16},{28,20},{9,1},{13,5},{17,9},{2... | collective-permute-start | bytes 786440 | tf_op jit(solution)/shard_map/ppermute | solution.py:66
  5.6 19.3 %collective-permute-start.8 = (bf16[128,1024]{1,0:T(8,128)(2,1)S(1)}, bf16[128,1024]{1,0:T(8,128)(2,1)}, u32[]{:S(2)}, u32[]{:S(2)}) collective-permute-start(bf16[128,1024]{1,0:T(8,128)(2,1)S(1)} %get-tuple-element.36), channel_id=1, source_target_pairs={{0,8},{4,12},{8,16},{12,20},{16,24},{20,28},{1,9},{5,13},{9,17},{1... | collective-permute-start | bytes 786440 | tf_op jit(solution)/shard_map/ppermute | solution.py:66
  12.6 23.6 %collective-permute-start.1 = (bf16[256,1024]{1,0:T(8,128)(2,1)S(1)}, bf16[256,1024]{1,0:T(8,128)(2,1)S(1)}, u32[]{:S(2)}, u32[]{:S(2)}) collective-permute-start(bf16[256,1024]{1,0:T(8,128)(2,1)S(1)} %get-tuple-element.38), channel_id=1, source_target_pairs={{0,8},{4,12},{8,16},{12,20},{16,24},{20,28},{1,9},{5,13},{9,17},{1... | collective-permute-start | bytes 1572872 | tf_op jit(solution)/shard_map/ppermute | solution.py:66
  23.7 9.5 %collective-permute-start.11 = (bf16[128,1024]{1,0:T(8,128)(2,1)S(1)}, bf16[128,1024]{1,0:T(8,128)(2,1)}, u32[]{:S(2)}, u32[]{:S(2)}) collective-permute-start(bf16[128,1024]{1,0:T(8,128)(2,1)S(1)} %collective-permute-done.7), channel_id=1, source_target_pairs={{8,0},{12,4},{16,8},{20,12},{9,1},{13,5},{17,9},{21,13},{10,2},{14... | collective-permute-start | bytes 786440 | tf_op jit(solution)/shard_map/ppermute | solution.py:66
  25.0 9.5 %collective-permute-start.9 = (bf16[128,1024]{1,0:T(8,128)(2,1)}, bf16[128,1024]{1,0:T(8,128)(2,1)}, u32[]{:S(2)}, u32[]{:S(2)}) collective-permute-start(bf16[128,1024]{1,0:T(8,128)(2,1)} %collective-permute-done.8), channel_id=1, source_target_pairs={{8,16},{12,20},{16,24},{20,28},{9,17},{13,21},{17,25},{21,29},{10,... | collective-permute-start | bytes 786440 | tf_op jit(solution)/shard_map/ppermute | solution.py:66
  26.4 28.9 %copy-start.19 = (bf16[256,1024]{1,0:T(8,128)(2,1)}, bf16[256,1024]{1,0:T(8,128)(2,1)S(1)}, u32[]{:S(2)}) copy-start(bf16[256,1024]{1,0:T(8,128)(2,1)S(1)} %collective-permute-done) | copy-start | bytes 1572868
  26.4 25.4 %collective-permute-start.4 = (bf16[256,1024]{1,0:T(8,128)(2,1)S(1)}, bf16[256,1024]{1,0:T(8,128)(2,1)S(1)}, u32[]{:S(2)}, u32[]{:S(2)}) collective-permute-start(bf16[256,1024]{1,0:T(8,128)(2,1)S(1)} %collective-permute-done), channel_id=1, source_target_pairs={{8,0},{12,4},{16,8},{20,12},{9,1},{13,5},{17,9},{21,13},{10,2},{14... | collective-permute-start | bytes 1572872 | tf_op jit(solution)/shard_map/ppermute | solution.py:66
  33.1 17.7 %collective-permute-start.12 = (bf16[128,1024]{1,0:T(8,128)(2,1)}, bf16[128,1024]{1,0:T(8,128)(2,1)}, u32[]{:S(2)}, u32[]{:S(2)}) collective-permute-start(bf16[128,1024]{1,0:T(8,128)(2,1)} %collective-permute-done.11), channel_id=1, source_target_pairs={{8,0},{12,4},{9,1},{13,5},{10,2},{14,6},{11,3},{15,7}} | collective-permute-start | bytes 786440 | tf_op jit(solution)/shard_map/ppermute | solution.py:66
  34.5 18.6 %collective-permute-start.10 = (bf16[128,1024]{1,0:T(8,128)(2,1)}, bf16[128,1024]{1,0:T(8,128)(2,1)S(1)}, u32[]{:S(2)}, u32[]{:S(2)}) collective-permute-start(bf16[128,1024]{1,0:T(8,128)(2,1)} %collective-permute-done.9), channel_id=1, source_target_pairs={{16,24},{20,28},{17,25},{21,29},{18,26},{22,30},{19,27},{23,31}} | collective-permute-start | bytes 786440 | tf_op jit(solution)/shard_map/ppermute | solution.py:66
  36.2 26.6 %collective-permute-start.2 = (bf16[256,1024]{1,0:T(8,128)(2,1)S(1)}, bf16[256,1024]{1,0:T(8,128)(2,1)}, u32[]{:S(2)}, u32[]{:S(2)}) collective-permute-start(bf16[256,1024]{1,0:T(8,128)(2,1)S(1)} %collective-permute-done.1), channel_id=1, source_target_pairs={{8,16},{12,20},{16,24},{20,28},{9,17},{13,21},{17,25},{21,29},{10,... | collective-permute-start | bytes 1572872 | tf_op jit(solution)/shard_map/ppermute | solution.py:66
  51.8 13.6 %collective-permute-start.5 = (bf16[256,1024]{1,0:T(8,128)(2,1)S(1)}, bf16[256,1024]{1,0:T(8,128)(2,1)}, u32[]{:S(2)}, u32[]{:S(2)}) collective-permute-start(bf16[256,1024]{1,0:T(8,128)(2,1)S(1)} %collective-permute-done.4), channel_id=1, source_target_pairs={{8,0},{12,4},{9,1},{13,5},{10,2},{14,6},{11,3},{15,7}} | collective-permute-start | bytes 1572872 | tf_op jit(solution)/shard_map/ppermute | solution.py:66
  55.2 26.4 %collective-permute-start.13 = (bf16[4,128,1024]{2,1,0:T(8,128)(2,1)}, bf16[4,128,1024]{2,1,0:T(8,128)(2,1)}, u32[]{:S(2)}, u32[]{:S(2)}) collective-permute-start(bf16[4,128,1024]{2,1,0:T(8,128)(2,1)} %pad_maximum_fusion.4), channel_id=1, source_target_pairs={{0,4},{4,0},{8,12},{12,8},{16,20},{20,16},{24,28},{28,24},{1,5},{5... | collective-permute-start | bytes 3145736 | tf_op jit(solution)/shard_map/ppermute | solution.py:72
  56.8 34.2 %collective-permute-start.21 = (bf16[128,1024]{1,0:T(8,128)(2,1)}, bf16[128,1024]{1,0:T(8,128)(2,1)}, u32[]{:S(2)}, u32[]{:S(2)}) collective-permute-start(bf16[128,1024]{1,0:T(8,128)(2,1)} %get-tuple-element.35), channel_id=1, source_target_pairs={{0,8},{4,12},{8,16},{12,20},{16,24},{20,28},{1,9},{5,13},{9,17},{1... | collective-permute-start | bytes 786440 | tf_op jit(solution)/shard_map/ppermute | solution.py:66
  62.8 3.7 %collective-permute-start.3 = (bf16[256,1024]{1,0:T(8,128)(2,1)}, bf16[256,1024]{1,0:T(8,128)(2,1)S(1)}, u32[]{:S(2)}, u32[]{:S(2)}) collective-permute-start(bf16[256,1024]{1,0:T(8,128)(2,1)} %collective-permute-done.2), channel_id=1, source_target_pairs={{16,24},{20,28},{17,25},{21,29},{18,26},{22,30},{19,27},{23,31}} | collective-permute-start | bytes 1572872 | tf_op jit(solution)/shard_map/ppermute | solution.py:66
  68.3 55.0 %collective-permute-start.6 = (bf16[4,256,1024]{2,1,0:T(8,128)(2,1)}, bf16[4,256,1024]{2,1,0:T(8,128)(2,1)}, u32[]{:S(2)}, u32[]{:S(2)}) collective-permute-start(bf16[4,256,1024]{2,1,0:T(8,128)(2,1)} %pad_maximum_fusion.1), channel_id=1, source_target_pairs={{0,4},{4,0},{8,12},{12,8},{16,20},{20,16},{24,28},{28,24},{1,5},{5... | collective-permute-start | bytes 6291464 | tf_op jit(solution)/shard_map/ppermute | solution.py:72
  85.6 7.3 %collective-permute-start.15 = (f32[512,256]{1,0:T(8,128)}, f32[512,256]{1,0:T(8,128)}, u32[]{:S(2)}, u32[]{:S(2)}) collective-permute-start(f32[512,256]{1,0:T(8,128)} %fusion.49), channel_id=1, source_target_pairs={{0,1},{1,0},{2,3},{3,2},{4,5},{5,4},{6,7},{7,6},{8,9},{9,8},{10,11... | collective-permute-start | bytes 1572872 | tf_op jit(solution)/shard_map/ppermute | solution.py:142
  85.6 12.6 %collective-permute-start.20 = (bf16[128,1024]{1,0:T(8,128)(2,1)}, bf16[128,1024]{1,0:T(8,128)(2,1)}, u32[]{:S(2)}, u32[]{:S(2)}) collective-permute-start(bf16[128,1024]{1,0:T(8,128)(2,1)} %get-tuple-element.35), channel_id=1, source_target_pairs={{8,0},{12,4},{16,8},{20,12},{24,16},{28,20},{9,1},{13,5},{17,9},{2... | collective-permute-start | bytes 786440 | tf_op jit(solution)/shard_map/ppermute | solution.py:66
  91.0 8.5 %collective-permute-start.22 = (bf16[128,1024]{1,0:T(8,128)(2,1)}, bf16[128,1024]{1,0:T(8,128)(2,1)S(1)}, u32[]{:S(2)}, u32[]{:S(2)}) collective-permute-start(bf16[128,1024]{1,0:T(8,128)(2,1)} %collective-permute-done.21), channel_id=1, source_target_pairs={{8,16},{12,20},{16,24},{20,28},{9,17},{13,21},{17,25},{21,29},{10,... | collective-permute-start | bytes 786440 | tf_op jit(solution)/shard_map/ppermute | solution.py:66
  92.3 7.9 %collective-permute-start.14 = (f32[512,256]{1,0:T(8,128)S(1)}, f32[512,256]{1,0:T(8,128)S(1)}, u32[]{:S(2)}, u32[]{:S(2)}) collective-permute-start(f32[512,256]{1,0:T(8,128)S(1)} %fusion.52), channel_id=1, source_target_pairs={{0,1},{1,0},{2,3},{3,2},{4,5},{5,4},{6,7},{7,6},{8,9},{9,8},{10,11... | collective-permute-start | bytes 1572872 | tf_op jit(solution)/shard_map/ppermute | solution.py:142
  94.4 8.3 %collective-permute-start.16 = (bf16[512,256]{1,0:T(8,128)(2,1)S(1)}, bf16[512,256]{1,0:T(8,128)(2,1)S(1)}, u32[]{:S(2)}, u32[]{:S(2)}) collective-permute-start(bf16[512,256]{1,0:T(8,128)(2,1)S(1)} %fusion.10), channel_id=1, source_target_pairs={{0,2},{1,3},{2,0},{3,1},{4,6},{5,7},{6,4},{7,5},{8,10},{9,11},{10,... | collective-permute-start | bytes 786440 | tf_op jit(solution)/shard_map/ppermute | solution.py:145
  98.2 14.5 %collective-permute-start.24 = (bf16[128,1024]{1,0:T(8,128)(2,1)}, bf16[128,1024]{1,0:T(8,128)(2,1)S(1)}, u32[]{:S(2)}, u32[]{:S(2)}) collective-permute-start(bf16[128,1024]{1,0:T(8,128)(2,1)} %collective-permute-done.20), channel_id=1, source_target_pairs={{8,0},{12,4},{16,8},{20,12},{9,1},{13,5},{17,9},{21,13},{10,2},{14... | collective-permute-start | bytes 786440 | tf_op jit(solution)/shard_map/ppermute | solution.py:66
  99.5 14.6 %collective-permute-start.23 = (bf16[128,1024]{1,0:T(8,128)(2,1)S(1)}, bf16[128,1024]{1,0:T(8,128)(2,1)S(1)}, u32[]{:S(2)}, u32[]{:S(2)}) collective-permute-start(bf16[128,1024]{1,0:T(8,128)(2,1)S(1)} %collective-permute-done.22), channel_id=1, source_target_pairs={{16,24},{20,28},{17,25},{21,29},{18,26},{22,30},{19,27},{23,31}} | collective-permute-start | bytes 786440 | tf_op jit(solution)/shard_map/ppermute | solution.py:66
  102.7 20.6 %copy-start.7 = (bf16[1,256,1024]{2,1,0:T(8,128)(2,1)S(1)}, bf16[1,256,1024]{2,1,0:T(8,128)(2,1)}, u32[]{:S(2)}) copy-start(bf16[1,256,1024]{2,1,0:T(8,128)(2,1)} %copy-done.6) | copy-start | bytes 1572868
  102.7 20.6 %copy-start.9 = (bf16[1,256,1024]{2,1,0:T(8,128)(2,1)S(1)}, bf16[1,256,1024]{2,1,0:T(8,128)(2,1)}, u32[]{:S(2)}) copy-start(bf16[1,256,1024]{2,1,0:T(8,128)(2,1)} %copy-done.8) | copy-start | bytes 1572868
  102.7 20.6 %copy-start.11 = (bf16[1,256,1024]{2,1,0:T(8,128)(2,1)S(1)}, bf16[1,256,1024]{2,1,0:T(8,128)(2,1)}, u32[]{:S(2)}) copy-start(bf16[1,256,1024]{2,1,0:T(8,128)(2,1)} %copy-done.10) | copy-start | bytes 1572868
  103.2 22.1 %copy-start.17 = (bf16[512,256]{1,0:T(8,128)(2,1)}, bf16[512,256]{1,0:T(8,128)(2,1)S(1)}, u32[]{:S(2)}) copy-start(bf16[512,256]{1,0:T(8,128)(2,1)S(1)} %fusion.12) | copy-start | bytes 786436
  103.2 12.0 %collective-permute-start.17 = (bf16[512,256]{1,0:T(8,128)(2,1)S(1)}, bf16[512,256]{1,0:T(8,128)(2,1)S(1)}, u32[]{:S(2)}, u32[]{:S(2)}) collective-permute-start(bf16[512,256]{1,0:T(8,128)(2,1)S(1)} %fusion.12), channel_id=1, source_target_pairs={{0,2},{1,3},{2,0},{3,1},{4,6},{5,7},{6,4},{7,5},{8,10},{9,11},{10,... | collective-permute-start | bytes 786440 | tf_op jit(solution)/shard_map/ppermute | solution.py:154
  112.8 15.5 %collective-permute-start.25 = (bf16[128,1024]{1,0:T(8,128)(2,1)S(1)}, bf16[128,1024]{1,0:T(8,128)(2,1)S(1)}, u32[]{:S(2)}, u32[]{:S(2)}) collective-permute-start(bf16[128,1024]{1,0:T(8,128)(2,1)S(1)} %collective-permute-done.24), channel_id=1, source_target_pairs={{8,0},{12,4},{9,1},{13,5},{10,2},{14,6},{11,3},{15,7}} | collective-permute-start | bytes 786440 | tf_op jit(solution)/shard_map/ppermute | solution.py:66
  115.1 10.7 %collective-permute-start.18 = (bf16[512,256]{1,0:T(8,128)(2,1)S(1)}, bf16[512,256]{1,0:T(8,128)(2,1)S(1)}, u32[]{:S(2)}, u32[]{:S(2)}) collective-permute-start(bf16[512,256]{1,0:T(8,128)(2,1)S(1)} %fusion.12), channel_id=1, source_target_pairs={{0,1},{1,0},{2,3},{3,2},{4,5},{5,4},{6,7},{7,6},{8,9},{9,8},{10,11... | collective-permute-start | bytes 786440 | tf_op jit(solution)/shard_map/ppermute | solution.py:155
  115.2 10.6 %collective-permute-start.19 = (bf16[512,256]{1,0:T(8,128)(2,1)S(1)}, bf16[512,256]{1,0:T(8,128)(2,1)S(1)}, u32[]{:S(2)}, u32[]{:S(2)}) collective-permute-start(bf16[512,256]{1,0:T(8,128)(2,1)S(1)} %collective-permute-done.17), channel_id=1, source_target_pairs={{0,1},{1,0},{2,3},{3,2},{4,5},{5,4},{6,7},{7,6},{8,9},{9,8},{10,11... | collective-permute-start | bytes 786440 | tf_op jit(solution)/shard_map/ppermute | solution.py:155
  128.3 5.9 %collective-permute-start.28 = (f32[512,512]{1,0:T(8,128)}, f32[512,512]{1,0:T(8,128)}, u32[]{:S(2)}, u32[]{:S(2)}) collective-permute-start(f32[512,512]{1,0:T(8,128)} %fusion.22), channel_id=1, source_target_pairs={{0,1},{1,0},{2,3},{3,2},{4,5},{5,4},{6,7},{7,6},{8,9},{9,8},{10,11... | collective-permute-start | bytes 3145736 | tf_op jit(solution)/shard_map/ppermute | solution.py:142
  129.5 25.9 %collective-permute-start.26 = (bf16[4,128,1024]{2,1,0:T(8,128)(2,1)}, bf16[4,128,1024]{2,1,0:T(8,128)(2,1)}, u32[]{:S(2)}, u32[]{:S(2)}) collective-permute-start(bf16[4,128,1024]{2,1,0:T(8,128)(2,1)} %pad_maximum_fusion.5), channel_id=1, source_target_pairs={{0,4},{4,0},{8,12},{12,8},{16,20},{20,16},{24,28},{28,24},{1,5},{5... | collective-permute-start | bytes 3145736 | tf_op jit(solution)/shard_map/ppermute | solution.py:72
  133.9 23.5 %collective-permute-start.27 = (f32[512,512]{1,0:T(8,128)}, f32[512,512]{1,0:T(8,128)}, u32[]{:S(2)}, u32[]{:S(2)}) collective-permute-start(f32[512,512]{1,0:T(8,128)} %fusion.25), channel_id=1, source_target_pairs={{0,1},{1,0},{2,3},{3,2},{4,5},{5,4},{6,7},{7,6},{8,9},{9,8},{10,11... | collective-permute-start | bytes 3145736 | tf_op jit(solution)/shard_map/ppermute | solution.py:142
  137.3 20.2 %collective-permute-start.29 = (bf16[512,512]{1,0:T(8,128)(2,1)}, bf16[512,512]{1,0:T(8,128)(2,1)}, u32[]{:S(2)}, u32[]{:S(2)}) collective-permute-start(bf16[512,512]{1,0:T(8,128)(2,1)} %fusion.4), channel_id=1, source_target_pairs={{0,2},{1,3},{2,0},{3,1},{4,6},{5,7},{6,4},{7,5},{8,10},{9,11},{10,... | collective-permute-start | bytes 1572872 | tf_op jit(solution)/shard_map/ppermute | solution.py:145
  161.7 13.6 %collective-permute-start.30 = (bf16[512,512]{1,0:T(8,128)(2,1)S(1)}, bf16[512,512]{1,0:T(8,128)(2,1)S(1)}, u32[]{:S(2)}, u32[]{:S(2)}) collective-permute-start(bf16[512,512]{1,0:T(8,128)(2,1)S(1)} %fusion.5), channel_id=1, source_target_pairs={{0,2},{1,3},{2,0},{3,1},{4,6},{5,7},{6,4},{7,5},{8,10},{9,11},{10,... | collective-permute-start | bytes 1572872 | tf_op jit(solution)/shard_map/ppermute | solution.py:154
  164.2 12.0 %collective-permute-start.31 = (bf16[512,512]{1,0:T(8,128)(2,1)S(1)}, bf16[512,512]{1,0:T(8,128)(2,1)S(1)}, u32[]{:S(2)}, u32[]{:S(2)}) collective-permute-start(bf16[512,512]{1,0:T(8,128)(2,1)S(1)} %fusion.5), channel_id=1, source_target_pairs={{0,1},{1,0},{2,3},{3,2},{4,5},{5,4},{6,7},{7,6},{8,9},{9,8},{10,11... | collective-permute-start | bytes 1572872 | tf_op jit(solution)/shard_map/ppermute | solution.py:155
  175.4 1.9 collective-permute-start.32
  178.3 2.8 %collective-permute-start.34 = (f32[512,256]{1,0:T(8,128)S(1)}, f32[512,256]{1,0:T(8,128)S(1)}, u32[]{:S(2)}, u32[]{:S(2)}) collective-permute-start(f32[512,256]{1,0:T(8,128)S(1)} %fusion.35), channel_id=1, source_target_pairs={{0,1},{1,0},{2,3},{3,2},{4,5},{5,4},{6,7},{7,6},{8,9},{9,8},{10,11... | collective-permute-start | bytes 1572872 | tf_op jit(solution)/shard_map/ppermute | solution.py:142
  178.5 5.4 %collective-permute-start.33 = (f32[512,256]{1,0:T(8,128)S(1)}, f32[512,256]{1,0:T(8,128)S(1)}, u32[]{:S(2)}, u32[]{:S(2)}) collective-permute-start(f32[512,256]{1,0:T(8,128)S(1)} %fusion.38), channel_id=1, source_target_pairs={{0,1},{1,0},{2,3},{3,2},{4,5},{5,4},{6,7},{7,6},{8,9},{9,8},{10,11... | collective-permute-start | bytes 1572872 | tf_op jit(solution)/shard_map/ppermute | solution.py:142
  181.5 8.4 %collective-permute-start.35 = (bf16[512,256]{1,0:T(8,128)(2,1)S(1)}, bf16[512,256]{1,0:T(8,128)(2,1)S(1)}, u32[]{:S(2)}, u32[]{:S(2)}) collective-permute-start(bf16[512,256]{1,0:T(8,128)(2,1)S(1)} %fusion.11), channel_id=1, source_target_pairs={{0,2},{1,3},{2,0},{3,1},{4,6},{5,7},{6,4},{7,5},{8,10},{9,11},{10,... | collective-permute-start | bytes 786440 | tf_op jit(solution)/shard_map/ppermute | solution.py:145
  190.5 7.6 %collective-permute-start.36 = (bf16[512,256]{1,0:T(8,128)(2,1)S(1)}, bf16[512,256]{1,0:T(8,128)(2,1)S(1)}, u32[]{:S(2)}, u32[]{:S(2)}) collective-permute-start(bf16[512,256]{1,0:T(8,128)(2,1)S(1)} %fusion.13), channel_id=1, source_target_pairs={{0,2},{1,3},{2,0},{3,1},{4,6},{5,7},{6,4},{7,5},{8,10},{9,11},{10,... | collective-permute-start | bytes 786440 | tf_op jit(solution)/shard_map/ppermute | solution.py:154
  192.0 6.5 %collective-permute-start.37 = (bf16[512,256]{1,0:T(8,128)(2,1)S(1)}, bf16[512,256]{1,0:T(8,128)(2,1)S(1)}, u32[]{:S(2)}, u32[]{:S(2)}) collective-permute-start(bf16[512,256]{1,0:T(8,128)(2,1)S(1)} %fusion.13), channel_id=1, source_target_pairs={{0,1},{1,0},{2,3},{3,2},{4,5},{5,4},{6,7},{7,6},{8,9},{9,8},{10,11... | collective-permute-start | bytes 786440 | tf_op jit(solution)/shard_map/ppermute | solution.py:155
  198.0 1.5 collective-permute-start.38
  201.0 3.7 %collective-permute-start.39 = (f32[1024]{0:T(1024)S(1)}, f32[1024]{0:T(1024)S(1)}, u32[]{:S(2)}, u32[]{:S(2)}) collective-permute-start(f32[1024]{0:T(1024)S(1)} %fusion.1), channel_id=1, source_target_pairs={{0,4},{4,0},{8,12},{12,8},{16,20},{20,16},{24,28},{28,24},{1,5},{5... | collective-permute-start | bytes 12296 | tf_op jit(solution)/shard_map/ppermute | solution.py:84
  204.7 5.7 %collective-permute-start.40 = (f32[1024]{0:T(1024)S(1)}, f32[1024]{0:T(1024)S(1)}, u32[]{:S(2)}, u32[]{:S(2)}) collective-permute-start(f32[1024]{0:T(1024)S(1)} %add.304), channel_id=1, source_target_pairs={{0,8},{4,12},{8,0},{12,4},{16,24},{20,28},{24,16},{28,20},{1,9},{5... | collective-permute-start | bytes 12296 | tf_op jit(solution)/shard_map/ppermute | solution.py:84
  210.4 4.5 %collective-permute-start.41 = (f32[1024]{0:T(1024)S(1)}, f32[1024]{0:T(1024)S(1)}, u32[]{:S(2)}, u32[]{:S(2)}) collective-permute-start(f32[1024]{0:T(1024)S(1)} %add.305), channel_id=1, source_target_pairs={{0,16},{4,20},{8,24},{12,28},{16,0},{20,4},{24,8},{28,12},{1,17},{... | collective-permute-start | bytes 12296 | tf_op jit(solution)/shard_map/ppermute | solution.py:84
  (23 other events, 139.0 us)

commit v11 on v10

--- a/solution.py
+++ b/solution.py
@@ -5,7 +5,7 @@
 from jax import lax
 from jax.sharding import PartitionSpec as P
 
-SPLIT = (1, 2, 1)
+SPLIT = (1, 3)
 
 
 def _rows(a, blk, n):

time: 217 us -> 231 us (1.065)
  waiting for transfers between devices: 103 us -> 139 us
  starting transfers between devices: 55.2 us -> 33.4 us
  matrix products: 23.6 us -> 27.5 us
  other arithmetic: 15.6 us -> 12.8 us
    ppermute x3 -> x2, waiting for transfers between devices: 31.1 us -> 46.4 us  [_gather_src(): other = lax.ppermute(col, 'src', swap)]
    ppermute x18 -> x12, starting transfers between devices: 33.6 us -> 22.2 us  [_gather_src(): cur = lax.ppermute(cur, 'src', pairs)]
    ppermute x18 -> x12, waiting for transfers between devices: 37.2 us -> 47.9 us  [_gather_src(): cur = lax.ppermute(cur, 'src', pairs)]
    ppermute x3 -> x2, waiting for transfers between devices: 16.6 us -> 22.3 us  [per_device(): got.append((2 * ((q - k) % m) + par, lax.ppermute(wt, 'vox', chip_perm(k))))]
    ppermute x3 -> x2, waiting for transfers between devices: 8.64 us -> 12.8 us  [per_device(): lax.ppermute(halves[k].astype(jnp.bfloat16), 'vox', chip_perm(k))]
    dot_general x12 -> x8, matrix products: 16.2 us -> 20 us  [pblock(): lax.dot_general(scaled, _rows(adj, rel(blk), n), (((1,), (1,)), ((), ()))...]
    ppermute x3, starting transfers between devices: 5.68 us -> 2.96 us  [_sum_over_src(): v = v + lax.ppermute(v, 'src', [(i, i ^ b) for i in range(n)])]
    another operation x12 -> x8, other arithmetic: 9.22 us -> 6.57 us  [_gather_src(): col = jnp.stack(col)]
  transfers between devices with their start and end apart: 42 -> 29, of which waited for: 18 -> 15; matrix products, arithmetic and copies ran while one was open for 21% -> 19% of each run, Pallas kernels for 0% -> 0%
where the time goes in v11:
time: 231 us; the launch traced here: 230 us
  waiting for transfers between devices  139 us (60%)
  starting transfers between devices  33.4 us (14%)
  matrix products  27.5 us (12%)
  local copies, waits for them, and re-layouts  16.9 us (7%)
  other arithmetic  12.8 us (6%)
    ppermute x12, waiting for transfers between devices, _gather_src(): cur = lax.ppermute(cur, 'src', pairs)  47.9 us
    ppermute x2, waiting for transfers between devices, _gather_src(): other = lax.ppermute(col, 'src', swap)  46.4 us
    ppermute x2, waiting for transfers between devices, per_device(): got.append((2 * ((q - k) % m) + par, lax.ppermute(wt, 'vox', chip_perm(k))))  22.3 us
    ppermute x12, starting transfers between devices, _gather_src(): cur = lax.ppermute(cur, 'src', pairs)  22.2 us
    dot_general x8, matrix products, pblock(): lax.dot_general(scaled, _rows(adj, rel(blk), n), (((1,), (1,)), ((), ()))...  20 us
    ppermute x2, waiting for transfers between devices, per_device(): lax.ppermute(halves[k].astype(jnp.bfloat16), 'vox', chip_perm(k))  12.8 us
    ppermute x3, waiting for transfers between devices, _sum_over_src(): v = v + lax.ppermute(v, 'src', [(i, i ^ b) for i in range(n)])  8.83 us
    dot_general x8, matrix products, per_device(): jnp.dot(w, _rows(adj, rel(blk), n), preferred_element_type=jnp.float32)  7.5 us
  transfers between devices with their start and end apart: 29, of which 15 were waited for; matrix products, arithmetic and copies ran while one was open for 19% of the time, Pallas kernels for 0%

profile of v11, /device:TPU:0, one launch (start us, length us, event | category | flops | bytes accessed | tf_op | source)
XLA Modules:
  0.0 229.8 jit_solution(13057393907715046566)
XLA Ops:
  0.0 1.3 slice_bitcast_fusion.1
  1.3 1.3 collective-permute-start
  2.6 5.6 %collective-permute-start.1 = (bf16[384,1024]{1,0:T(8,128)(2,1)S(1)}, bf16[384,1024]{1,0:T(8,128)(2,1)S(1)}, u32[]{:S(2)}, u32[]{:S(2)}) collective-permute-start(bf16[384,1024]{1,0:T(8,128)(2,1)S(1)} %get-tuple-element.22), channel_id=1, source_target_pairs={{0,8},{4,12},{8,16},{12,20},{16,24},{20,28},{1,9},{5,13},{9,17},{1... | collective-permute-start | bytes 2359304 | tf_op jit(solution)/shard_map/ppermute | solution.py:66
  9.3 1.3 collective-permute-start.7
  10.6 14.1 %collective-permute-done = bf16[384,1024]{1,0:T(8,128)(2,1)S(1)} collective-permute-done((bf16[384,1024]{1,0:T(8,128)(2,1)S(1)}, bf16[384,1024]{1,0:T(8,128)(2,1)S(1)}, u32[]{:S(2)}, u32[]{:S(2)}) %collective-permute-start) | collective-permute-done | bytes 786464 | tf_op jit(solution)/shard_map/ppermute | solution.py:66
  24.6 1.3 collective-permute-start.4
  25.9 4.6 %collective-permute-start.8 = (bf16[128,1024]{1,0:T(8,128)(2,1)S(1)}, bf16[128,1024]{1,0:T(8,128)(2,1)S(1)}, u32[]{:S(2)}, u32[]{:S(2)}) collective-permute-start(bf16[128,1024]{1,0:T(8,128)(2,1)S(1)} %get-tuple-element.20), channel_id=1, source_target_pairs={{0,8},{4,12},{8,16},{12,20},{16,24},{20,28},{1,9},{5,13},{9,17},{1... | collective-permute-start | bytes 786440 | tf_op jit(solution)/shard_map/ppermute | solution.py:66
  30.5 1.6 collective-permute-start.2
  32.1 1.3 collective-permute-start.11
  34.4 1.4 collective-permute-start.9
  35.7 16.2 %collective-permute-done.11 = bf16[128,1024]{1,0:T(8,128)(2,1)} collective-permute-done((bf16[128,1024]{1,0:T(8,128)(2,1)S(1)}, bf16[128,1024]{1,0:T(8,128)(2,1)}, u32[]{:S(2)}, u32[]{:S(2)}) %collective-permute-start.11) | collective-permute-done | bytes 262176 | tf_op jit(solution)/shard_map/ppermute | solution.py:66
  52.0 1.3 collective-permute-start.12
  55.0 1.3 collective-permute-start.5
  56.3 7.1 %collective-permute-done.12 = bf16[128,1024]{1,0:T(8,128)(2,1)} collective-permute-done((bf16[128,1024]{1,0:T(8,128)(2,1)}, bf16[128,1024]{1,0:T(8,128)(2,1)}, u32[]{:S(2)}, u32[]{:S(2)}) %collective-permute-start.12) | collective-permute-done | bytes 262176 | tf_op jit(solution)/shard_map/ppermute | solution.py:66
  65.2 1.2 pad_maximum_fusion.3
  66.4 1.3 collective-permute-start.13
  67.7 1.2 select_bitcast_fusion.5
  68.9 9.5 %collective-permute-done.5 = bf16[384,1024]{1,0:T(8,128)(2,1)S(1)} collective-permute-done((bf16[384,1024]{1,0:T(8,128)(2,1)}, bf16[384,1024]{1,0:T(8,128)(2,1)S(1)}, u32[]{:S(2)}, u32[]{:S(2)}) %collective-permute-start.5) | collective-permute-done | bytes 786464 | tf_op jit(solution)/shard_map/ppermute | solution.py:66
  78.7 2.0 pad_maximum_fusion.1
  80.7 1.4 collective-permute-start.6
  82.0 10.8 %collective-permute-done.13 = bf16[4,128,1024]{2,1,0:T(8,128)(2,1)} collective-permute-done((bf16[4,128,1024]{2,1,0:T(8,128)(2,1)}, bf16[4,128,1024]{2,1,0:T(8,128)(2,1)}, u32[]{:S(2)}, u32[]{:S(2)}) %collective-permute-start.13) | collective-permute-done | bytes 1048608 | tf_op jit(solution)/shard_map/ppermute | solution.py:72
  92.9 1.6 select_bitcast_fusion.3
  95.7 1.3 fusion.33
  97.0 1.3 fusion.36
  99.3 2.2 fusion.23
  101.5 1.2 collective-permute-start.16
  102.7 4.0 %reshape.17 = f32[512,2,512]{2,1,0:T(2,128)} reshape(f32[512,1024]{1,0:T(8,128)} %param.7) | data formatting | bytes 4194304 | tf_op jit(solution)/shard_map/reshape | solution.py:113
  106.7 1.9 slice.16
  108.6 1.4 collective-permute-done.16
  110.8 1.7 fusion.24
  112.5 1.2 collective-permute-start.17
  113.8 6.5 %collective-permute-done.17 = bf16[512,256]{1,0:T(8,128)(2,1)} collective-permute-done((bf16[512,256]{1,0:T(8,128)(2,1)S(1)}, bf16[512,256]{1,0:T(8,128)(2,1)}, u32[]{:S(2)}, u32[]{:S(2)}) %collective-permute-start.17) | collective-permute-done | bytes 262176 | tf_op jit(solution)/shard_map/ppermute | solution.py:154
  120.3 35.5 %collective-permute-done.6 = bf16[4,384,1024]{2,1,0:T(8,128)(2,1)} collective-permute-done((bf16[4,384,1024]{2,1,0:T(8,128)(2,1)}, bf16[4,384,1024]{2,1,0:T(8,128)(2,1)}, u32[]{:S(2)}, u32[]{:S(2)}) %collective-permute-start.6) | collective-permute-done | bytes 3145760 | tf_op jit(solution)/shard_map/ppermute | solution.py:72
  155.9 3.3 %select_bitcast_fusion.1 = (bf16[4,1,384,1024]{3,2,1,0:T(8,128)(2,1)S(1)}, bf16[4,1,384,1024]{3,2,1,0:T(8,128)(2,1)S(1)}) fusion(bf16[4,384,1024]{2,1,0:T(8,128)(2,1)} %collective-permute-done.6, pred[]{:T(512)S(6)} %eq.34, bf16[1,384,1024]{2,1,0:T(8,128)(2,1)} %copy-done.3, bf16[1,384,1024]{2,1,0:T(8,128)(2,1)} %copy-done.2, ...), kind=kLoop, calls=%fused_computation.3 | loop fusion | flops 7864320 | bytes 12582913 | tf_op jit(solution)/shard_map/stack | solution.py:74
  159.8 2.7 %fusion.9 = f32[512,768]{1,0:T(8,128)} fusion(bf16[3072,1024]{1,0:T(8,128)(2,1)S(1)} %bitcast.43, s32[]{:T(128)S(6)} %select_n.252, bf16[512,1024]{1,0:T(8,128)(2,1)S(1)} %copy-done.1, f32[1024]{0:T(1024)S(1)} %copy-done.17), kind=kOutput, calls=%fused_computation.18 | convolution fusion | flops 806879232 | bytes 4198404 | tf_op jit(solution)/shard_map/dot_general | solution.py:135
  163.0 3.6 %fusion.13 = f32[512,768]{1,0:T(8,128)} fusion(bf16[3072,1024]{1,0:T(8,128)(2,1)} %bitcast.44, s32[]{:T(128)S(6)} %select_n.250, bf16[512,1024]{1,0:T(8,128)(2,1)S(1)} %copy-done.1, f32[1024]{0:T(1024)S(1)} %copy-done.17), kind=kOutput, calls=%fused_computation.22 | convolution fusion | flops 806879232 | bytes 4198404 | tf_op jit(solution)/shard_map/dot_general | solution.py:135
  167.1 3.8 %add_convert_fusion = bf16[512,768]{1,0:T(8,128)(2,1)} fusion(f32[512,768]{1,0:T(8,128)} %collective-permute-done.21, bf16[3072,1024]{1,0:T(8,128)(2,1)} %bitcast.45, s32[]{:T(128)S(6)} %select_n.251, bf16[512,1024]{1,0:T(8,128)(2,1)S(1)} %copy-done.1, f32[1024]{0:T(1024)S(1)} %copy-done.17), kind=kOutput, calls=%fused_computation.17 | convolution fusion | flops 807665664 | bytes 4984836 | tf_op jit(solution)/shard_map/dot_general | solution.py:135
  171.9 3.2 %slice.17 = f32[512,2,384]{2,1,0:T(2,128)} slice(f32[512,2,512]{2,1,0:T(2,128)} %reshape.17), slice={[0:512], [0:2], [128:512]} | slice | bytes 3145728 | tf_op jit(solution)/shard_map/slice | solution.py:149
  175.1 2.7 %copy.8 = f32[64,8,2,384]{3,1,2,0:T(8,128)} copy(f32[64,8,2,384]{3,2,1,0:T(2,128)} %bitcast.62) | data formatting | bytes 3145728
  177.8 1.5 fusion.29
  179.3 11.3 %collective-permute-done.22 = bf16[512,768]{1,0:T(8,128)(2,1)} collective-permute-done((bf16[512,768]{1,0:T(8,128)(2,1)}, bf16[512,768]{1,0:T(8,128)(2,1)}, u32[]{:S(2)}, u32[]{:S(2)}) %collective-permute-start.22) | collective-permute-done | bytes 786464 | tf_op jit(solution)/shard_map/ppermute | solution.py:145
  190.7 3.4 %multiply_convert_fusion = bf16[512,768]{1,0:T(8,128)(2,1)S(1)} fusion(f32[512,768]{1,0:T(8,128)S(1)} %bitcast.61, bf16[512,768]{1,0:T(8,128)(2,1)} %collective-permute-done.22, f32[512,768]{1,0:T(8,128)} %collective-permute-done.20, bf16[3072,1024]{1,0:T(8,128)(2,1)} %bitcast.46, s32[]{:T(128)S(6)} %select_n.249, bf16[512,1024]{1,0:T(8,128)(2,1)S(1)} %copy-done.1, ...), kind=kOutput, calls=%fused_computation.16 | convolution fusion | flops 808845312 | bytes 7344132 | tf_op jit(solution)/shard_map/dot_general | solution.py:135
  197.0 15.7 %collective-permute-done.23 = bf16[512,768]{1,0:T(8,128)(2,1)S(1)} collective-permute-done((bf16[512,768]{1,0:T(8,128)(2,1)S(1)}, bf16[512,768]{1,0:T(8,128)(2,1)S(1)}, u32[]{:S(2)}, u32[]{:S(2)}) %collective-permute-start.23) | collective-permute-done | bytes 786464 | tf_op jit(solution)/shard_map/ppermute | solution.py:154
  215.8 1.7 fusion.1
  218.6 2.6 %collective-permute-done.26 = f32[1024]{0:T(1024)S(1)} collective-permute-done((f32[1024]{0:T(1024)S(1)}, f32[1024]{0:T(1024)S(1)}, u32[]{:S(2)}, u32[]{:S(2)}) %collective-permute-start.26) | collective-permute-done | bytes 4128 | tf_op jit(solution)/shard_map/ppermute | solution.py:84
  221.1 3.6 %collective-permute-done.27 = f32[1024]{0:T(1024)S(1)} collective-permute-done((f32[1024]{0:T(1024)S(1)}, f32[1024]{0:T(1024)S(1)}, u32[]{:S(2)}, u32[]{:S(2)}) %collective-permute-start.27) | collective-permute-done | bytes 4128 | tf_op jit(solution)/shard_map/ppermute | solution.py:84
  224.7 1.8 collective-permute-start.28
  226.6 2.7 %collective-permute-done.28 = f32[1024]{0:T(1024)S(1)} collective-permute-done((f32[1024]{0:T(1024)S(1)}, f32[1024]{0:T(1024)S(1)}, u32[]{:S(2)}, u32[]{:S(2)}) %collective-permute-start.28) | collective-permute-done | bytes 4128 | tf_op jit(solution)/shard_map/ppermute | solution.py:84
  (88 shorter events, 18.8 us)
Async XLA Ops:
  1.3 77.3 %copy-start.5 = (bf16[1,384,1024]{2,1,0:T(8,128)(2,1)}, bf16[1,384,1024]{2,1,0:T(8,128)(2,1)S(1)}, u32[]{:S(2)}) copy-start(bf16[1,384,1024]{2,1,0:T(8,128)(2,1)S(1)} %get-tuple-element.21) | copy-start | bytes 2359300
  1.3 23.3 %collective-permute-start = (bf16[384,1024]{1,0:T(8,128)(2,1)S(1)}, bf16[384,1024]{1,0:T(8,128)(2,1)S(1)}, u32[]{:S(2)}, u32[]{:S(2)}) collective-permute-start(bf16[384,1024]{1,0:T(8,128)(2,1)S(1)} %get-tuple-element.22), channel_id=1, source_target_pairs={{8,0},{12,4},{16,8},{20,12},{24,16},{28,20},{9,1},{13,5},{17,9},{2... | collective-permute-start | bytes 2359304 | tf_op jit(solution)/shard_map/ppermute | solution.py:66
  2.6 27.9 %collective-permute-start.1 = (bf16[384,1024]{1,0:T(8,128)(2,1)S(1)}, bf16[384,1024]{1,0:T(8,128)(2,1)S(1)}, u32[]{:S(2)}, u32[]{:S(2)}) collective-permute-start(bf16[384,1024]{1,0:T(8,128)(2,1)S(1)} %get-tuple-element.22), channel_id=1, source_target_pairs={{0,8},{4,12},{8,16},{12,20},{16,24},{20,28},{1,9},{5,13},{9,17},{1... | collective-permute-start | bytes 2359304 | tf_op jit(solution)/shard_map/ppermute | solution.py:66
  9.3 22.9 %collective-permute-start.7 = (bf16[128,1024]{1,0:T(8,128)(2,1)S(1)}, bf16[128,1024]{1,0:T(8,128)(2,1)S(1)}, u32[]{:S(2)}, u32[]{:S(2)}) collective-permute-start(bf16[128,1024]{1,0:T(8,128)(2,1)S(1)} %get-tuple-element.20), channel_id=1, source_target_pairs={{8,0},{12,4},{16,8},{20,12},{24,16},{28,20},{9,1},{13,5},{17,9},{2... | collective-permute-start | bytes 786440 | tf_op jit(solution)/shard_map/ppermute | solution.py:66
  24.6 31.7 %copy-start.10 = (bf16[384,1024]{1,0:T(8,128)(2,1)}, bf16[384,1024]{1,0:T(8,128)(2,1)S(1)}, u32[]{:S(2)}) copy-start(bf16[384,1024]{1,0:T(8,128)(2,1)S(1)} %collective-permute-done) | copy-start | bytes 2359300
  24.6 30.4 %collective-permute-start.4 = (bf16[384,1024]{1,0:T(8,128)(2,1)S(1)}, bf16[384,1024]{1,0:T(8,128)(2,1)}, u32[]{:S(2)}, u32[]{:S(2)}) collective-permute-start(bf16[384,1024]{1,0:T(8,128)(2,1)S(1)} %collective-permute-done), channel_id=1, source_target_pairs={{8,0},{12,4},{16,8},{20,12},{9,1},{13,5},{17,9},{21,13},{10,2},{14... | collective-permute-start | bytes 2359304 | tf_op jit(solution)/shard_map/ppermute | solution.py:66
  25.9 8.5 %collective-permute-start.8 = (bf16[128,1024]{1,0:T(8,128)(2,1)S(1)}, bf16[128,1024]{1,0:T(8,128)(2,1)S(1)}, u32[]{:S(2)}, u32[]{:S(2)}) collective-permute-start(bf16[128,1024]{1,0:T(8,128)(2,1)S(1)} %get-tuple-element.20), channel_id=1, source_target_pairs={{0,8},{4,12},{8,16},{12,20},{16,24},{20,28},{1,9},{5,13},{9,17},{1... | collective-permute-start | bytes 786440 | tf_op jit(solution)/shard_map/ppermute | solution.py:66
  30.5 33.9 %collective-permute-start.2 = (bf16[384,1024]{1,0:T(8,128)(2,1)S(1)}, bf16[384,1024]{1,0:T(8,128)(2,1)}, u32[]{:S(2)}, u32[]{:S(2)}) collective-permute-start(bf16[384,1024]{1,0:T(8,128)(2,1)S(1)} %collective-permute-done.1), channel_id=1, source_target_pairs={{8,16},{12,20},{16,24},{20,28},{9,17},{13,21},{17,25},{21,29},{10,... | collective-permute-start | bytes 2359304 | tf_op jit(solution)/shard_map/ppermute | solution.py:66
  32.1 19.9 %collective-permute-start.11 = (bf16[128,1024]{1,0:T(8,128)(2,1)S(1)}, bf16[128,1024]{1,0:T(8,128)(2,1)}, u32[]{:S(2)}, u32[]{:S(2)}) collective-permute-start(bf16[128,1024]{1,0:T(8,128)(2,1)S(1)} %collective-permute-done.7), channel_id=1, source_target_pairs={{8,0},{12,4},{16,8},{20,12},{9,1},{13,5},{17,9},{21,13},{10,2},{14... | collective-permute-start | bytes 786440 | tf_op jit(solution)/shard_map/ppermute | solution.py:66
  34.4 18.9 %collective-permute-start.9 = (bf16[128,1024]{1,0:T(8,128)(2,1)S(1)}, bf16[128,1024]{1,0:T(8,128)(2,1)}, u32[]{:S(2)}, u32[]{:S(2)}) collective-permute-start(bf16[128,1024]{1,0:T(8,128)(2,1)S(1)} %collective-permute-done.8), channel_id=1, source_target_pairs={{8,16},{12,20},{16,24},{20,28},{9,17},{13,21},{17,25},{21,29},{10,... | collective-permute-start | bytes 786440 | tf_op jit(solution)/shard_map/ppermute | solution.py:66
  52.0 11.4 %collective-permute-start.12 = (bf16[128,1024]{1,0:T(8,128)(2,1)}, bf16[128,1024]{1,0:T(8,128)(2,1)}, u32[]{:S(2)}, u32[]{:S(2)}) collective-permute-start(bf16[128,1024]{1,0:T(8,128)(2,1)} %collective-permute-done.11), channel_id=1, source_target_pairs={{8,0},{12,4},{9,1},{13,5},{10,2},{14,6},{11,3},{15,7}} | collective-permute-start | bytes 786440 | tf_op jit(solution)/shard_map/ppermute | solution.py:66
  53.3 11.8 %collective-permute-start.10 = (bf16[128,1024]{1,0:T(8,128)(2,1)}, bf16[128,1024]{1,0:T(8,128)(2,1)S(1)}, u32[]{:S(2)}, u32[]{:S(2)}) collective-permute-start(bf16[128,1024]{1,0:T(8,128)(2,1)} %collective-permute-done.9), channel_id=1, source_target_pairs={{16,24},{20,28},{17,25},{21,29},{18,26},{22,30},{19,27},{23,31}} | collective-permute-start | bytes 786440 | tf_op jit(solution)/shard_map/ppermute | solution.py:66
  55.0 11.4 %copy-start.7 = (bf16[1,128,1024]{2,1,0:T(8,128)(2,1)}, bf16[1,128,1024]{2,1,0:T(8,128)(2,1)S(1)}, u32[]{:S(2)}) copy-start(bf16[1,128,1024]{2,1,0:T(8,128)(2,1)S(1)} %select_bitcast_fusion.8) | copy-start | bytes 786436
  55.0 23.4 %collective-permute-start.5 = (bf16[384,1024]{1,0:T(8,128)(2,1)}, bf16[384,1024]{1,0:T(8,128)(2,1)S(1)}, u32[]{:S(2)}, u32[]{:S(2)}) collective-permute-start(bf16[384,1024]{1,0:T(8,128)(2,1)} %collective-permute-done.4), channel_id=1, source_target_pairs={{8,0},{12,4},{9,1},{13,5},{10,2},{14,6},{11,3},{15,7}} | collective-permute-start | bytes 2359304 | tf_op jit(solution)/shard_map/ppermute | solution.py:66
  64.4 2.0 copy-start.8
  64.4 14.1 %collective-permute-start.3 = (bf16[384,1024]{1,0:T(8,128)(2,1)}, bf16[384,1024]{1,0:T(8,128)(2,1)S(1)}, u32[]{:S(2)}, u32[]{:S(2)}) collective-permute-start(bf16[384,1024]{1,0:T(8,128)(2,1)} %collective-permute-done.2), channel_id=1, source_target_pairs={{16,24},{20,28},{17,25},{21,29},{18,26},{22,30},{19,27},{23,31}} | collective-permute-start | bytes 2359304 | tf_op jit(solution)/shard_map/ppermute | solution.py:66
  65.2 1.2 copy-start.9
  66.4 12.1 %copy-start.11 = (bf16[384,1024]{1,0:T(8,128)(2,1)S(1)}, bf16[384,1024]{1,0:T(8,128)(2,1)}, u32[]{:S(2)}) copy-start(bf16[384,1024]{1,0:T(8,128)(2,1)} %copy-done.10) | copy-start | bytes 2359300
  66.4 26.5 %collective-permute-start.13 = (bf16[4,128,1024]{2,1,0:T(8,128)(2,1)}, bf16[4,128,1024]{2,1,0:T(8,128)(2,1)}, u32[]{:S(2)}, u32[]{:S(2)}) collective-permute-start(bf16[4,128,1024]{2,1,0:T(8,128)(2,1)} %pad_maximum_fusion.3), channel_id=1, source_target_pairs={{0,4},{4,0},{8,12},{12,8},{16,20},{20,16},{24,28},{28,24},{1,5},{5... | collective-permute-start | bytes 3145736 | tf_op jit(solution)/shard_map/ppermute | solution.py:72
  68.9 9.8 %copy-start.2 = (bf16[1,384,1024]{2,1,0:T(8,128)(2,1)}, bf16[1,384,1024]{2,1,0:T(8,128)(2,1)S(1)}, u32[]{:S(2)}) copy-start(bf16[1,384,1024]{2,1,0:T(8,128)(2,1)S(1)} %select_bitcast_fusion.5) | copy-start | bytes 2359300
  78.5 2.2 copy-start.3
  78.6 2.0 copy-start.4
  80.7 75.2 %collective-permute-start.6 = (bf16[4,384,1024]{2,1,0:T(8,128)(2,1)}, bf16[4,384,1024]{2,1,0:T(8,128)(2,1)}, u32[]{:S(2)}, u32[]{:S(2)}) collective-permute-start(bf16[4,384,1024]{2,1,0:T(8,128)(2,1)} %pad_maximum_fusion.1), channel_id=1, source_target_pairs={{0,4},{4,0},{8,12},{12,8},{16,20},{20,16},{24,28},{28,24},{1,5},{5... | collective-permute-start | bytes 9437192 | tf_op jit(solution)/shard_map/ppermute | solution.py:72
  94.5 1.2 copy-start.1
  94.5 1.2 copy-start.17
  97.0 2.3 collective-permute-start.15
  98.3 10.3 %collective-permute-start.14 = (f32[512,256]{1,0:T(8,128)}, f32[512,256]{1,0:T(8,128)}, u32[]{:S(2)}, u32[]{:S(2)}) collective-permute-start(f32[512,256]{1,0:T(8,128)} %fusion.36), channel_id=1, source_target_pairs={{0,1},{1,0},{2,3},{3,2},{4,5},{5,4},{6,7},{7,6},{8,9},{9,8},{10,11... | collective-permute-start | bytes 1572872 | tf_op jit(solution)/shard_map/ppermute | solution.py:142
  101.5 8.6 %collective-permute-start.16 = (bf16[512,256]{1,0:T(8,128)(2,1)}, bf16[512,256]{1,0:T(8,128)(2,1)S(1)}, u32[]{:S(2)}, u32[]{:S(2)}) collective-permute-start(bf16[512,256]{1,0:T(8,128)(2,1)} %fusion.23), channel_id=1, source_target_pairs={{0,2},{1,3},{2,0},{3,1},{4,6},{5,7},{6,4},{7,5},{8,10},{9,11},{10,... | collective-permute-start | bytes 786440 | tf_op jit(solution)/shard_map/ppermute | solution.py:145
  112.5 7.8 %collective-permute-start.17 = (bf16[512,256]{1,0:T(8,128)(2,1)S(1)}, bf16[512,256]{1,0:T(8,128)(2,1)}, u32[]{:S(2)}, u32[]{:S(2)}) collective-permute-start(bf16[512,256]{1,0:T(8,128)(2,1)S(1)} %fusion.24), channel_id=1, source_target_pairs={{0,2},{1,3},{2,0},{3,1},{4,6},{5,7},{6,4},{7,5},{8,10},{9,11},{10,... | collective-permute-start | bytes 786440 | tf_op jit(solution)/shard_map/ppermute | solution.py:154
  113.8 46.0 %collective-permute-start.18 = (bf16[512,256]{1,0:T(8,128)(2,1)S(1)}, bf16[512,256]{1,0:T(8,128)(2,1)S(1)}, u32[]{:S(2)}, u32[]{:S(2)}) collective-permute-start(bf16[512,256]{1,0:T(8,128)(2,1)S(1)} %fusion.24), channel_id=1, source_target_pairs={{0,1},{1,0},{2,3},{3,2},{4,5},{5,4},{6,7},{7,6},{8,9},{9,8},{10,11... | collective-permute-start | bytes 786440 | tf_op jit(solution)/shard_map/ppermute | solution.py:155
  120.3 39.4 %collective-permute-start.19 = (bf16[512,256]{1,0:T(8,128)(2,1)}, bf16[512,256]{1,0:T(8,128)(2,1)S(1)}, u32[]{:S(2)}, u32[]{:S(2)}) collective-permute-start(bf16[512,256]{1,0:T(8,128)(2,1)} %collective-permute-done.17), channel_id=1, source_target_pairs={{0,1},{1,0},{2,3},{3,2},{4,5},{5,4},{6,7},{7,6},{8,9},{9,8},{10,11... | collective-permute-start | bytes 786440 | tf_op jit(solution)/shard_map/ppermute | solution.py:155
  159.7 3.1 %copy-start = (bf16[4,2,384,1024]{3,2,1,0:T(8,128)(2,1)}, bf16[4,2,384,1024]{3,2,1,0:T(8,128)(2,1)S(1)}, u32[]{:S(2)}) copy-start(bf16[4,2,384,1024]{3,2,1,0:T(8,128)(2,1)S(1)} %pad_maximum_fusion) | copy-start | bytes 18874372
  159.7 3.2 %copy-start.14 = (bf16[512,256]{1,0:T(8,128)(2,1)}, bf16[512,256]{1,0:T(8,128)(2,1)S(1)}, u32[]{:S(2)}) copy-start(bf16[512,256]{1,0:T(8,128)(2,1)S(1)} %collective-permute-done.18) | copy-start | bytes 786436
  159.8 3.3 %copy-start.12 = (bf16[512,256]{1,0:T(8,128)(2,1)}, bf16[512,256]{1,0:T(8,128)(2,1)S(1)}, u32[]{:S(2)}) copy-start(bf16[512,256]{1,0:T(8,128)(2,1)S(1)} %collective-permute-done.19) | copy-start | bytes 786436
  163.0 4.1 %collective-permute-start.21 = (f32[512,768]{1,0:T(8,128)}, f32[512,768]{1,0:T(8,128)}, u32[]{:S(2)}, u32[]{:S(2)}) collective-permute-start(f32[512,768]{1,0:T(8,128)} %fusion.9), channel_id=1, source_target_pairs={{0,1},{1,0},{2,3},{3,2},{4,5},{5,4},{6,7},{7,6},{8,9},{9,8},{10,11... | collective-permute-start | bytes 4718600 | tf_op jit(solution)/shard_map/ppermute | solution.py:142
  166.6 12.7 %collective-permute-start.20 = (f32[512,768]{1,0:T(8,128)}, f32[512,768]{1,0:T(8,128)}, u32[]{:S(2)}, u32[]{:S(2)}) collective-permute-start(f32[512,768]{1,0:T(8,128)} %fusion.13), channel_id=1, source_target_pairs={{0,1},{1,0},{2,3},{3,2},{4,5},{5,4},{6,7},{7,6},{8,9},{9,8},{10,11... | collective-permute-start | bytes 4718600 | tf_op jit(solution)/shard_map/ppermute | solution.py:142
  170.9 19.8 %collective-permute-start.22 = (bf16[512,768]{1,0:T(8,128)(2,1)}, bf16[512,768]{1,0:T(8,128)(2,1)}, u32[]{:S(2)}, u32[]{:S(2)}) collective-permute-start(bf16[512,768]{1,0:T(8,128)(2,1)} %add_convert_fusion), channel_id=1, source_target_pairs={{0,2},{1,3},{2,0},{3,1},{4,6},{5,7},{6,4},{7,5},{8,10},{9,11},{10,... | collective-permute-start | bytes 2359304 | tf_op jit(solution)/shard_map/ppermute | solution.py:145
  177.8 12.9 %copy-start.6 = (f32[64,8,2,384]{3,1,2,0:T(8,128)S(1)}, f32[64,8,2,384]{3,1,2,0:T(8,128)}, u32[]{:S(2)}) copy-start(f32[64,8,2,384]{3,1,2,0:T(8,128)} %copy.8) | copy-start | bytes 4718596
  190.7 22.1 %slice-start = ((s8[6291456]{0:T(1024)(128)(4,1)}), s8[4194304]{0:T(1024)(128)(4,1)S(1)}, s32[]{:S(2)}) async-start(s8[6291456]{0:T(1024)(128)(4,1)} %bitcast.47), calls=%async_computation | async-start | bytes 8388608
  194.0 1.5 copy-start.15
  194.1 18.7 %slice-start.1 = ((s8[6291456]{0:T(1024)(128)(4,1)}), s8[2097152]{0:T(1024)(128)(4,1)S(1)}, s32[]{:S(2)}) async-start(s8[6291456]{0:T(1024)(128)(4,1)} %bitcast.47), calls=%async_computation.1 | async-start | bytes 4194304
  194.1 18.7 %collective-permute-start.23 = (bf16[512,768]{1,0:T(8,128)(2,1)S(1)}, bf16[512,768]{1,0:T(8,128)(2,1)S(1)}, u32[]{:S(2)}, u32[]{:S(2)}) collective-permute-start(bf16[512,768]{1,0:T(8,128)(2,1)S(1)} %multiply_convert_fusion), channel_id=1, source_target_pairs={{0,2},{1,3},{2,0},{3,1},{4,6},{5,7},{6,4},{7,5},{8,10},{9,11},{10,... | collective-permute-start | bytes 2359304 | tf_op jit(solution)/shard_map/ppermute | solution.py:154
  195.6 1.0 copy-start.13
  196.1 18.7 %collective-permute-start.24 = (bf16[512,768]{1,0:T(8,128)(2,1)S(1)}, bf16[512,768]{1,0:T(8,128)(2,1)S(1)}, u32[]{:S(2)}, u32[]{:S(2)}) collective-permute-start(bf16[512,768]{1,0:T(8,128)(2,1)S(1)} %multiply_convert_fusion), channel_id=1, source_target_pairs={{0,1},{1,0},{2,3},{3,2},{4,5},{5,4},{6,7},{7,6},{8,9},{9,8},{10,11... | collective-permute-start | bytes 2359304 | tf_op jit(solution)/shard_map/ppermute | solution.py:155
  212.7 3.0 %collective-permute-start.25 = (bf16[512,768]{1,0:T(8,128)(2,1)S(1)}, bf16[512,768]{1,0:T(8,128)(2,1)S(1)}, u32[]{:S(2)}, u32[]{:S(2)}) collective-permute-start(bf16[512,768]{1,0:T(8,128)(2,1)S(1)} %collective-permute-done.23), channel_id=1, source_target_pairs={{0,1},{1,0},{2,3},{3,2},{4,5},{5,4},{6,7},{7,6},{8,9},{9,8},{10,11... | collective-permute-start | bytes 2359304 | tf_op jit(solution)/shard_map/ppermute | solution.py:155
  217.4 3.7 %collective-permute-start.26 = (f32[1024]{0:T(1024)S(1)}, f32[1024]{0:T(1024)S(1)}, u32[]{:S(2)}, u32[]{:S(2)}) collective-permute-start(f32[1024]{0:T(1024)S(1)} %fusion.1), channel_id=1, source_target_pairs={{0,4},{4,0},{8,12},{12,8},{16,20},{20,16},{24,28},{28,24},{1,5},{5... | collective-permute-start | bytes 12296 | tf_op jit(solution)/shard_map/ppermute | solution.py:84
  221.1 3.6 %collective-permute-start.27 = (f32[1024]{0:T(1024)S(1)}, f32[1024]{0:T(1024)S(1)}, u32[]{:S(2)}, u32[]{:S(2)}) collective-permute-start(f32[1024]{0:T(1024)S(1)} %add.244), channel_id=1, source_target_pairs={{0,8},{4,12},{8,0},{12,4},{16,24},{20,28},{24,16},{28,20},{1,9},{5... | collective-permute-start | bytes 12296 | tf_op jit(solution)/shard_map/ppermute | solution.py:84
  224.7 4.5 %collective-permute-start.28 = (f32[1024]{0:T(1024)S(1)}, f32[1024]{0:T(1024)S(1)}, u32[]{:S(2)}, u32[]{:S(2)}) collective-permute-start(f32[1024]{0:T(1024)S(1)} %add.245), channel_id=1, source_target_pairs={{0,16},{4,20},{8,24},{12,28},{16,0},{20,4},{24,8},{28,12},{1,17},{... | collective-permute-start | bytes 12296 | tf_op jit(solution)/shard_map/ppermute | solution.py:84
  (1 other events, 0.7 us)

commit v12 on v8

--- a/solution.py
+++ b/solution.py
@@ -49,24 +49,14 @@
         return lax.all_gather(block, "src", axis=0, tiled=True)
     nb, na = grid
     me = lax.axis_index("src")
-    ia, ib = me // nb, me % nb
+    ib = me % nb
     swap = [(i, i ^ 1) for i in range(na * nb)]
 
-    def along(p, d):
-        return [(p * nb + o, d * nb + o) for o in range(nb)]
-
-    got = {}
-    for sign in (1, -1):
-        cur = block
-        for s in range(1, na):
-            pairs = []
-            for p in range(na):
-                if 0 <= p + sign < na and 0 <= p - sign * (s - 1) < na:
-                    pairs.extend(along(p, p + sign))
-            cur = lax.ppermute(cur, "src", pairs)
-            got[(sign, s)] = cur
     col = [block] + [
-        jnp.where(ia + k < na, got[(-1, k)], got[(1, na - k)]) for k in range(1, na)
+        lax.ppermute(
+            block, "src", [(p * nb + o, ((p - k) % na) * nb + o) for p in range(na) for o in range(nb)]
+        )
+        for k in range(1, na)
     ]
     col = jnp.stack(col)
     other = lax.ppermute(col, "src", swap)

time: 208 us -> 224 us (1.077)
  starting transfers between devices: 33.4 us -> 52.2 us
    ppermute x12 -> x6, starting transfers between devices: 23 us -> 33.4 us  [_gather_src(): lax.ppermute(block, 'src', [(p * nb + o, (p - k) % na * nb + o) for p in...]
    ppermute x3, starting transfers between devices: 3.42 us -> 10.1 us  [_sum_over_src(): v = v + lax.ppermute(v, 'src', [(i, i ^ b) for i in range(n)])]
    ppermute x12 -> x6, waiting for transfers between devices: 49.3 us -> 51.9 us  [_gather_src(): lax.ppermute(block, 'src', [(p * nb + o, (p - k) % na * nb + o) for p in...]
    another operation x8 -> x2, other arithmetic: 5.73 us -> 3.29 us  [_gather_src(): col = jnp.stack(col)]
  transfers between devices with their start and end apart: 29 -> 23, of which waited for: 15 -> 13; matrix products, arithmetic and copies ran while one was open for 15% -> 14% of each run, Pallas kernels for 0% -> 0%
where the time goes in v12:
time: 224 us
  waiting for transfers between devices  129 us (58%)
  starting transfers between devices  52.2 us (23%)
  matrix products  23.5 us (10%)
  local copies, waits for them, and re-layouts  10.6 us (5%)
  other arithmetic  8.7 us (4%)
    ppermute x6, waiting for transfers between devices, _gather_src(): lax.ppermute(block, 'src', [(p * nb + o, (p - k) % na * nb + o) for p in...  51.9 us
    ppermute x6, starting transfers between devices, _gather_src(): lax.ppermute(block, 'src', [(p * nb + o, (p - k) % na * nb + o) for p in...  33.4 us
    ppermute x2, waiting for transfers between devices, _gather_src(): other = lax.ppermute(col, 'src', swap)  28 us
    ppermute x2, waiting for transfers between devices, per_device(): got.append((2 * ((q - k) % m) + par, lax.ppermute(wt, 'vox', chip_perm(k))))  22.4 us
    ppermute x2, waiting for transfers between devices, per_device(): lax.ppermute(halves[k].astype(jnp.bfloat16), 'vox', chip_perm(k))  19.5 us
    dot_general x8, matrix products, pblock(): lax.dot_general(scaled, _rows(adj, rel(blk), n), (((1,), (1,)), ((), ()))...  17.2 us
    ppermute x3, starting transfers between devices, _sum_over_src(): v = v + lax.ppermute(v, 'src', [(i, i ^ b) for i in range(n)])  10.1 us
    dot_general x8, matrix products, per_device(): jnp.dot(w, _rows(adj, rel(blk), n), preferred_element_type=jnp.float32)  6.29 us
  transfers between devices with their start and end apart: 23, of which 13 were waited for; matrix products, arithmetic and copies ran while one was open for 14% of the time, Pallas kernels for 0%

profile of v12, /device:TPU:0, one launch (start us, length us, event | category | flops | bytes accessed | tf_op | source)
XLA Modules:
  0.0 223.9 jit_solution(27064724967942919)
XLA Ops:
  0.0 2.2 slice_bitcast_fusion
  2.2 4.0 %collective-permute-start.5 = (bf16[256,1024]{1,0:T(8,128)(2,1)S(1)}, bf16[256,1024]{1,0:T(8,128)(2,1)S(1)}, u32[]{:S(2)}, u32[]{:S(2)}) collective-permute-start(bf16[256,1024]{1,0:T(8,128)(2,1)S(1)} %get-tuple-element.23), channel_id=1, source_target_pairs={{0,16},{4,20},{8,24},{12,28},{16,0},{20,4},{24,8},{28,12},{1,17},{... | collective-permute-start | bytes 1572872 | tf_op jit(solution)/shard_map/ppermute | solution.py:56
  6.3 1.6 collective-permute-start.6
  7.8 2.2 %collective-permute-start.4 = (bf16[256,1024]{1,0:T(8,128)(2,1)S(1)}, bf16[256,1024]{1,0:T(8,128)(2,1)S(1)}, u32[]{:S(2)}, u32[]{:S(2)}) collective-permute-start(bf16[256,1024]{1,0:T(8,128)(2,1)S(1)} %get-tuple-element.23), channel_id=1, source_target_pairs={{0,24},{4,28},{8,0},{12,4},{16,8},{20,12},{24,16},{28,20},{1,25},{... | collective-permute-start | bytes 1572872 | tf_op jit(solution)/shard_map/ppermute | solution.py:56
  10.1 31.4 %collective-permute-done.5 = bf16[256,1024]{1,0:T(8,128)(2,1)S(1)} collective-permute-done((bf16[256,1024]{1,0:T(8,128)(2,1)S(1)}, bf16[256,1024]{1,0:T(8,128)(2,1)S(1)}, u32[]{:S(2)}, u32[]{:S(2)}) %collective-permute-start.5) | collective-permute-done | bytes 524320 | tf_op jit(solution)/shard_map/ppermute | solution.py:56
  42.3 1.6 pad_maximum_fusion.3
  43.9 1.6 collective-permute-start.7
  45.4 2.0 collective-permute-start
  47.5 21.5 %collective-permute-start.1 = (bf16[256,1024]{1,0:T(8,128)(2,1)}, bf16[256,1024]{1,0:T(8,128)(2,1)S(1)}, u32[]{:S(2)}, u32[]{:S(2)}) collective-permute-start(bf16[256,1024]{1,0:T(8,128)(2,1)} %get-tuple-element.24), channel_id=1, source_target_pairs={{0,16},{4,20},{8,24},{12,28},{16,0},{20,4},{24,8},{28,12},{1,17},{... | collective-permute-start | bytes 1572872 | tf_op jit(solution)/shard_map/ppermute | solution.py:56
  68.9 2.0 collective-permute-start.2
  71.0 18.5 %collective-permute-done.7 = bf16[4,256,1024]{2,1,0:T(8,128)(2,1)} collective-permute-done((bf16[4,256,1024]{2,1,0:T(8,128)(2,1)}, bf16[4,256,1024]{2,1,0:T(8,128)(2,1)}, u32[]{:S(2)}, u32[]{:S(2)}) %collective-permute-start.7) | collective-permute-done | bytes 2097184 | tf_op jit(solution)/shard_map/ppermute | solution.py:62
  89.5 2.0 select_bitcast_fusion.1
  92.4 0.7 copy-done.4
  93.2 1.7 fusion.31
  94.9 19.8 %collective-permute-done.1 = bf16[256,1024]{1,0:T(8,128)(2,1)S(1)} collective-permute-done((bf16[256,1024]{1,0:T(8,128)(2,1)}, bf16[256,1024]{1,0:T(8,128)(2,1)S(1)}, u32[]{:S(2)}, u32[]{:S(2)}) %collective-permute-start.1) | collective-permute-done | bytes 524320 | tf_op jit(solution)/shard_map/ppermute | solution.py:56
  114.7 1.7 pad_maximum_fusion.2
  117.0 3.0 %fusion.34 = f32[512,512]{1,0:T(8,128)} fusion(bf16[2048,1024]{1,0:T(8,128)(2,1)} %bitcast.35, s32[]{:T(128)S(6)} %select_n.159, bf16[512,1024]{1,0:T(8,128)(2,1)S(1)} %copy-done.4, f32[1024]{0:T(1024)S(1)} %copy-done.24), kind=kOutput, calls=%fused_computation.48 | convolution fusion | flops 538443776 | bytes 3149828 | tf_op jit(solution)/shard_map/dot_general | solution.py:121
  120.0 3.1 %fusion.6 = bf16[512,512]{1,0:T(8,128)(2,1)} fusion(f32[512,512]{1,0:T(8,128)} %collective-permute-done.9, bf16[2048,1024]{1,0:T(8,128)(2,1)} %bitcast.36, s32[]{:T(128)S(6)} %select_n.162, bf16[512,1024]{1,0:T(8,128)(2,1)S(1)} %copy-done.4, f32[1024]{0:T(1024)S(1)} %copy-done.24), kind=kOutput, calls=%fused_computation.20 | convolution fusion | flops 538968064 | bytes 3674116 | tf_op jit(solution)/shard_map/dot_general | solution.py:121
  123.1 1.5 collective-permute-start.10
  124.6 3.0 %reshape.17 = f32[512,2,512]{2,1,0:T(2,128)S(1)} reshape(f32[512,1024]{1,0:T(8,128)} %param.7) | data formatting | bytes 4194304 | tf_op jit(solution)/shard_map/reshape | solution.py:100
  127.6 1.7 fusion.61
  129.4 8.3 %collective-permute-done.10 = bf16[512,512]{1,0:T(8,128)(2,1)} collective-permute-done((bf16[512,512]{1,0:T(8,128)(2,1)}, bf16[512,512]{1,0:T(8,128)(2,1)}, u32[]{:S(2)}, u32[]{:S(2)}) %collective-permute-start.10) | collective-permute-done | bytes 524320 | tf_op jit(solution)/shard_map/ppermute | solution.py:131
  137.8 2.6 %fusion.9 = bf16[512,512]{1,0:T(8,128)(2,1)S(1)} fusion(f32[512,512]{1,0:T(8,128)S(1)} %bitcast.52, f32[512,512]{1,0:T(8,128)} %collective-permute-done.8, bf16[512,512]{1,0:T(8,128)(2,1)} %collective-permute-done.10, bf16[2048,1024]{1,0:T(8,128)(2,1)} %bitcast.37, s32[]{:T(128)S(6)} %select_n.157, bf16[512,1024]{1,0:T(8,128)(2,1)S(1)} %copy-done.4, ...), kind=kOutput, calls=%fused_computation.23 | convolution fusion | flops 539754496 | bytes 5246980 | tf_op jit(solution)/shard_map/dot_general | solution.py:121
  140.4 1.5 collective-permute-start.11
  141.9 12.1 %collective-permute-done.11 = bf16[512,512]{1,0:T(8,128)(2,1)S(1)} collective-permute-done((bf16[512,512]{1,0:T(8,128)(2,1)S(1)}, bf16[512,512]{1,0:T(8,128)(2,1)S(1)}, u32[]{:S(2)}, u32[]{:S(2)}) %collective-permute-start.11) | collective-permute-done | bytes 524320 | tf_op jit(solution)/shard_map/ppermute | solution.py:140
  154.0 9.5 %collective-permute-done.3 = bf16[4,256,1024]{2,1,0:T(8,128)(2,1)} collective-permute-done((bf16[4,256,1024]{2,1,0:T(8,128)(2,1)}, bf16[4,256,1024]{2,1,0:T(8,128)(2,1)}, u32[]{:S(2)}, u32[]{:S(2)}) %collective-permute-start.3) | collective-permute-done | bytes 2097184 | tf_op jit(solution)/shard_map/ppermute | solution.py:62
  163.5 2.0 select_bitcast_fusion.3
  166.0 0.8 copy-done.20
  166.8 1.7 fusion.17
  168.9 2.1 fusion.20
  171.5 0.7 fusion.27
  172.3 1.1 copy-done.3
  173.4 2.0 fusion.7
  175.4 1.6 collective-permute-start.16
  177.7 0.7 fusion.25
  178.4 11.2 %collective-permute-done.16 = bf16[512,512]{1,0:T(8,128)(2,1)S(1)} collective-permute-done((bf16[512,512]{1,0:T(8,128)(2,1)S(1)}, bf16[512,512]{1,0:T(8,128)(2,1)S(1)}, u32[]{:S(2)}, u32[]{:S(2)}) %collective-permute-start.16) | collective-permute-done | bytes 524320 | tf_op jit(solution)/shard_map/ppermute | solution.py:131
  189.6 0.9 fusion.8
  190.5 1.6 collective-permute-start.17
  192.8 0.7 fusion.15
  193.5 10.3 %collective-permute-done.17 = bf16[512,512]{1,0:T(8,128)(2,1)S(1)} collective-permute-done((bf16[512,512]{1,0:T(8,128)(2,1)S(1)}, bf16[512,512]{1,0:T(8,128)(2,1)S(1)}, u32[]{:S(2)}, u32[]{:S(2)}) %collective-permute-start.17) | collective-permute-done | bytes 524320 | tf_op jit(solution)/shard_map/ppermute | solution.py:140
  203.8 0.7 fusion.13
  204.6 0.7 fusion.11
  205.7 1.2 fusion.1
  207.6 3.1 %collective-permute-done.20 = f32[1024]{0:T(1024)S(1)} collective-permute-done((f32[1024]{0:T(1024)S(1)}, f32[1024]{0:T(1024)S(1)}, u32[]{:S(2)}, u32[]{:S(2)}) %collective-permute-start.20) | collective-permute-done | bytes 4128 | tf_op jit(solution)/shard_map/ppermute | solution.py:74
  210.7 5.5 %collective-permute-start.21 = (f32[1024]{0:T(1024)S(1)}, f32[1024]{0:T(1024)S(1)}, u32[]{:S(2)}, u32[]{:S(2)}) collective-permute-start(f32[1024]{0:T(1024)S(1)} %add.205), channel_id=1, source_target_pairs={{0,8},{4,12},{8,0},{12,4},{16,24},{20,28},{24,16},{28,20},{1,9},{5... | collective-permute-start | bytes 12296 | tf_op jit(solution)/shard_map/ppermute | solution.py:74
  216.2 1.6 collective-permute-done.21
  217.8 4.0 %collective-permute-start.22 = (f32[1024]{0:T(1024)S(1)}, f32[1024]{0:T(1024)S(1)}, u32[]{:S(2)}, u32[]{:S(2)}) collective-permute-start(f32[1024]{0:T(1024)S(1)} %add.206), channel_id=1, source_target_pairs={{0,16},{4,20},{8,24},{12,28},{16,0},{20,4},{24,8},{28,12},{1,17},{... | collective-permute-start | bytes 12296 | tf_op jit(solution)/shard_map/ppermute | solution.py:74
  221.8 1.6 collective-permute-done.22
  (79 shorter events, 6.5 us)
Async XLA Ops:
  2.2 112.5 %copy-start.5 = (bf16[1,256,1024]{2,1,0:T(8,128)(2,1)}, bf16[1,256,1024]{2,1,0:T(8,128)(2,1)S(1)}, u32[]{:S(2)}) copy-start(bf16[1,256,1024]{2,1,0:T(8,128)(2,1)S(1)} %get-tuple-element.22) | copy-start | bytes 1572868
  2.2 39.3 %collective-permute-start.5 = (bf16[256,1024]{1,0:T(8,128)(2,1)S(1)}, bf16[256,1024]{1,0:T(8,128)(2,1)S(1)}, u32[]{:S(2)}, u32[]{:S(2)}) collective-permute-start(bf16[256,1024]{1,0:T(8,128)(2,1)S(1)} %get-tuple-element.23), channel_id=1, source_target_pairs={{0,16},{4,20},{8,24},{12,28},{16,0},{20,4},{24,8},{28,12},{1,17},{... | collective-permute-start | bytes 1572872 | tf_op jit(solution)/shard_map/ppermute | solution.py:56
  6.3 35.3 %collective-permute-start.6 = (bf16[256,1024]{1,0:T(8,128)(2,1)S(1)}, bf16[256,1024]{1,0:T(8,128)(2,1)S(1)}, u32[]{:S(2)}, u32[]{:S(2)}) collective-permute-start(bf16[256,1024]{1,0:T(8,128)(2,1)S(1)} %get-tuple-element.23), channel_id=1, source_target_pairs={{0,8},{4,12},{8,16},{12,20},{16,24},{20,28},{24,0},{28,4},{1,9},{5... | collective-permute-start | bytes 1572872 | tf_op jit(solution)/shard_map/ppermute | solution.py:56
  7.8 34.4 %collective-permute-start.4 = (bf16[256,1024]{1,0:T(8,128)(2,1)S(1)}, bf16[256,1024]{1,0:T(8,128)(2,1)S(1)}, u32[]{:S(2)}, u32[]{:S(2)}) collective-permute-start(bf16[256,1024]{1,0:T(8,128)(2,1)S(1)} %get-tuple-element.23), channel_id=1, source_target_pairs={{0,24},{4,28},{8,0},{12,4},{16,8},{20,12},{24,16},{28,20},{1,25},{... | collective-permute-start | bytes 1572872 | tf_op jit(solution)/shard_map/ppermute | solution.py:56
  41.5 2.3 %copy-start.16 = (bf16[256,1024]{1,0:T(8,128)(2,1)}, bf16[256,1024]{1,0:T(8,128)(2,1)S(1)}, u32[]{:S(2)}) copy-start(bf16[256,1024]{1,0:T(8,128)(2,1)S(1)} %collective-permute-done.6) | copy-start | bytes 1572868
  42.3 1.6 copy-start.17
  43.9 45.6 %collective-permute-start.7 = (bf16[4,256,1024]{2,1,0:T(8,128)(2,1)}, bf16[4,256,1024]{2,1,0:T(8,128)(2,1)}, u32[]{:S(2)}, u32[]{:S(2)}) collective-permute-start(bf16[4,256,1024]{2,1,0:T(8,128)(2,1)} %pad_maximum_fusion.3), channel_id=1, source_target_pairs={{0,4},{4,0},{8,12},{12,8},{16,20},{20,16},{24,28},{28,24},{1,5},{5... | collective-permute-start | bytes 6291464 | tf_op jit(solution)/shard_map/ppermute | solution.py:62
  45.4 49.5 %collective-permute-start = (bf16[256,1024]{1,0:T(8,128)(2,1)}, bf16[256,1024]{1,0:T(8,128)(2,1)S(1)}, u32[]{:S(2)}, u32[]{:S(2)}) collective-permute-start(bf16[256,1024]{1,0:T(8,128)(2,1)} %get-tuple-element.24), channel_id=1, source_target_pairs={{0,24},{4,28},{8,0},{12,4},{16,8},{20,12},{24,16},{28,20},{1,25},{... | collective-permute-start | bytes 1572872 | tf_op jit(solution)/shard_map/ppermute | solution.py:56
  47.5 67.2 %collective-permute-start.1 = (bf16[256,1024]{1,0:T(8,128)(2,1)}, bf16[256,1024]{1,0:T(8,128)(2,1)S(1)}, u32[]{:S(2)}, u32[]{:S(2)}) collective-permute-start(bf16[256,1024]{1,0:T(8,128)(2,1)} %get-tuple-element.24), channel_id=1, source_target_pairs={{0,16},{4,20},{8,24},{12,28},{16,0},{20,4},{24,8},{28,12},{1,17},{... | collective-permute-start | bytes 1572872 | tf_op jit(solution)/shard_map/ppermute | solution.py:56
  68.9 45.7 %collective-permute-start.2 = (bf16[256,1024]{1,0:T(8,128)(2,1)}, bf16[256,1024]{1,0:T(8,128)(2,1)S(1)}, u32[]{:S(2)}, u32[]{:S(2)}) collective-permute-start(bf16[256,1024]{1,0:T(8,128)(2,1)} %get-tuple-element.24), channel_id=1, source_target_pairs={{0,8},{4,12},{8,16},{12,20},{16,24},{20,28},{24,0},{28,4},{1,9},{5... | collective-permute-start | bytes 1572872 | tf_op jit(solution)/shard_map/ppermute | solution.py:56
  91.9 1.2 copy-start.4
  91.9 1.2 copy-start.24
  92.4 2.5 %copy-start = (bf16[4,2,256,1024]{3,2,1,0:T(8,128)(2,1)}, bf16[4,2,256,1024]{3,2,1,0:T(8,128)(2,1)S(1)}, u32[]{:S(2)}) copy-start(bf16[4,2,256,1024]{3,2,1,0:T(8,128)(2,1)S(1)} %copy.6) | copy-start | bytes 12582916
  94.9 25.1 %collective-permute-start.9 = (f32[512,512]{1,0:T(8,128)}, f32[512,512]{1,0:T(8,128)}, u32[]{:S(2)}, u32[]{:S(2)}) collective-permute-start(f32[512,512]{1,0:T(8,128)} %fusion.31), channel_id=1, source_target_pairs={{0,1},{1,0},{2,3},{3,2},{4,5},{5,4},{6,7},{7,6},{8,9},{9,8},{10,11... | collective-permute-start | bytes 3145736 | tf_op jit(solution)/shard_map/ppermute | solution.py:128
  94.9 21.5 %copy-start.10 = (bf16[256,1024]{1,0:T(8,128)(2,1)}, bf16[256,1024]{1,0:T(8,128)(2,1)S(1)}, u32[]{:S(2)}) copy-start(bf16[256,1024]{1,0:T(8,128)(2,1)S(1)} %collective-permute-done) | copy-start | bytes 1572868
  114.7 1.7 copy-start.12
  114.7 1.7 copy-start.14
  116.4 47.1 %collective-permute-start.3 = (bf16[4,256,1024]{2,1,0:T(8,128)(2,1)}, bf16[4,256,1024]{2,1,0:T(8,128)(2,1)}, u32[]{:S(2)}, u32[]{:S(2)}) collective-permute-start(bf16[4,256,1024]{2,1,0:T(8,128)(2,1)} %pad_maximum_fusion.2), channel_id=1, source_target_pairs={{0,4},{4,0},{8,12},{12,8},{16,20},{20,16},{24,28},{28,24},{1,5},{5... | collective-permute-start | bytes 6291464 | tf_op jit(solution)/shard_map/ppermute | solution.py:62
  120.0 9.4 %collective-permute-start.8 = (f32[512,512]{1,0:T(8,128)}, f32[512,512]{1,0:T(8,128)}, u32[]{:S(2)}, u32[]{:S(2)}) collective-permute-start(f32[512,512]{1,0:T(8,128)} %fusion.34), channel_id=1, source_target_pairs={{0,1},{1,0},{2,3},{3,2},{4,5},{5,4},{6,7},{7,6},{8,9},{9,8},{10,11... | collective-permute-start | bytes 3145736 | tf_op jit(solution)/shard_map/ppermute | solution.py:128
  123.1 14.7 %collective-permute-start.10 = (bf16[512,512]{1,0:T(8,128)(2,1)}, bf16[512,512]{1,0:T(8,128)(2,1)}, u32[]{:S(2)}, u32[]{:S(2)}) collective-permute-start(bf16[512,512]{1,0:T(8,128)(2,1)} %fusion.6), channel_id=1, source_target_pairs={{0,2},{1,3},{2,0},{3,1},{4,6},{5,7},{6,4},{7,5},{8,10},{9,11},{10,... | collective-permute-start | bytes 1572872 | tf_op jit(solution)/shard_map/ppermute | solution.py:131
  137.7 25.7 %copy-start.6 = (bf16[1,256,1024]{2,1,0:T(8,128)(2,1)S(1)}, bf16[1,256,1024]{2,1,0:T(8,128)(2,1)}, u32[]{:S(2)}) copy-start(bf16[1,256,1024]{2,1,0:T(8,128)(2,1)} %copy-done.5) | copy-start | bytes 1572868
  137.7 25.7 %copy-start.11 = (bf16[256,1024]{1,0:T(8,128)(2,1)S(1)}, bf16[256,1024]{1,0:T(8,128)(2,1)}, u32[]{:S(2)}) copy-start(bf16[256,1024]{1,0:T(8,128)(2,1)} %copy-done.10) | copy-start | bytes 1572868
  137.7 25.7 %copy-start.13 = (bf16[256,1024]{1,0:T(8,128)(2,1)S(1)}, bf16[256,1024]{1,0:T(8,128)(2,1)}, u32[]{:S(2)}) copy-start(bf16[256,1024]{1,0:T(8,128)(2,1)} %copy-done.12) | copy-start | bytes 1572868
  137.8 25.7 %copy-start.15 = (bf16[256,1024]{1,0:T(8,128)(2,1)S(1)}, bf16[256,1024]{1,0:T(8,128)(2,1)}, u32[]{:S(2)}) copy-start(bf16[256,1024]{1,0:T(8,128)(2,1)} %copy-done.14) | copy-start | bytes 1572868
  140.4 25.1 %copy-start.8 = (bf16[512,512]{1,0:T(8,128)(2,1)}, bf16[512,512]{1,0:T(8,128)(2,1)S(1)}, u32[]{:S(2)}) copy-start(bf16[512,512]{1,0:T(8,128)(2,1)S(1)} %fusion.9) | copy-start | bytes 1572868
  140.4 13.6 %collective-permute-start.11 = (bf16[512,512]{1,0:T(8,128)(2,1)S(1)}, bf16[512,512]{1,0:T(8,128)(2,1)S(1)}, u32[]{:S(2)}, u32[]{:S(2)}) collective-permute-start(bf16[512,512]{1,0:T(8,128)(2,1)S(1)} %fusion.9), channel_id=1, source_target_pairs={{0,2},{1,3},{2,0},{3,1},{4,6},{5,7},{6,4},{7,5},{8,10},{9,11},{10,... | collective-permute-start | bytes 1572872 | tf_op jit(solution)/shard_map/ppermute | solution.py:140
  141.9 24.0 %collective-permute-start.12 = (bf16[512,512]{1,0:T(8,128)(2,1)S(1)}, bf16[512,512]{1,0:T(8,128)(2,1)S(1)}, u32[]{:S(2)}, u32[]{:S(2)}) collective-permute-start(bf16[512,512]{1,0:T(8,128)(2,1)S(1)} %fusion.9), channel_id=1, source_target_pairs={{0,1},{1,0},{2,3},{3,2},{4,5},{5,4},{6,7},{7,6},{8,9},{9,8},{10,11... | collective-permute-start | bytes 1572872 | tf_op jit(solution)/shard_map/ppermute | solution.py:141
  154.0 11.5 %copy-start.22 = (bf16[512,512]{1,0:T(8,128)(2,1)}, bf16[512,512]{1,0:T(8,128)(2,1)S(1)}, u32[]{:S(2)}) copy-start(bf16[512,512]{1,0:T(8,128)(2,1)S(1)} %collective-permute-done.11) | copy-start | bytes 1572868
  154.0 12.0 %collective-permute-start.13 = (bf16[512,512]{1,0:T(8,128)(2,1)S(1)}, bf16[512,512]{1,0:T(8,128)(2,1)S(1)}, u32[]{:S(2)}, u32[]{:S(2)}) collective-permute-start(bf16[512,512]{1,0:T(8,128)(2,1)S(1)} %collective-permute-done.11), channel_id=1, source_target_pairs={{0,1},{1,0},{2,3},{3,2},{4,5},{5,4},{6,7},{7,6},{8,9},{9,8},{10,11... | collective-permute-start | bytes 1572872 | tf_op jit(solution)/shard_map/ppermute | solution.py:141
  165.9 2.6 %copy-start.2 = (bf16[4,2,256,1024]{3,2,1,0:T(8,128)(2,1)}, bf16[4,2,256,1024]{3,2,1,0:T(8,128)(2,1)S(1)}, u32[]{:S(2)}) copy-start(bf16[4,2,256,1024]{3,2,1,0:T(8,128)(2,1)S(1)} %pad_maximum_fusion) | copy-start | bytes 12582916
  166.0 0.9 copy-start.20
  166.8 1.8 copy-start.18
  166.8 2.0 copy-start.7
  168.6 3.7 %collective-permute-start.15 = (f32[512,512]{1,0:T(8,128)}, f32[512,512]{1,0:T(8,128)}, u32[]{:S(2)}, u32[]{:S(2)}) collective-permute-start(f32[512,512]{1,0:T(8,128)} %fusion.17), channel_id=1, source_target_pairs={{0,1},{1,0},{2,3},{3,2},{4,5},{5,4},{6,7},{7,6},{8,9},{9,8},{10,11... | collective-permute-start | bytes 3145736 | tf_op jit(solution)/shard_map/ppermute | solution.py:128
  168.9 2.5 %copy-start.1 = (bf16[4,2,256,1024]{3,2,1,0:T(8,128)(2,1)S(1)}, bf16[4,2,256,1024]{3,2,1,0:T(8,128)(2,1)}, u32[]{:S(2)}) copy-start(bf16[4,2,256,1024]{3,2,1,0:T(8,128)(2,1)} %copy-done) | copy-start | bytes 12582916
  168.9 2.6 %copy-start.23 = (bf16[512,512]{1,0:T(8,128)(2,1)S(1)}, bf16[512,512]{1,0:T(8,128)(2,1)}, u32[]{:S(2)}) copy-start(bf16[512,512]{1,0:T(8,128)(2,1)} %copy-done.22) | copy-start | bytes 1572868
  171.1 2.3 %copy-start.3 = (bf16[4,2,256,1024]{3,2,1,0:T(8,128)(2,1)S(1)}, bf16[4,2,256,1024]{3,2,1,0:T(8,128)(2,1)}, u32[]{:S(2)}) copy-start(bf16[4,2,256,1024]{3,2,1,0:T(8,128)(2,1)} %copy-done.2) | copy-start | bytes 12582916
  171.1 7.3 %collective-permute-start.14 = (f32[512,512]{1,0:T(8,128)S(1)}, f32[512,512]{1,0:T(8,128)S(1)}, u32[]{:S(2)}, u32[]{:S(2)}) collective-permute-start(f32[512,512]{1,0:T(8,128)S(1)} %fusion.20), channel_id=1, source_target_pairs={{0,1},{1,0},{2,3},{3,2},{4,5},{5,4},{6,7},{7,6},{8,9},{9,8},{10,11... | collective-permute-start | bytes 3145736 | tf_op jit(solution)/shard_map/ppermute | solution.py:128
  172.3 4.7 %copy-start.9 = (bf16[512,512]{1,0:T(8,128)(2,1)S(1)}, bf16[512,512]{1,0:T(8,128)(2,1)}, u32[]{:S(2)}) copy-start(bf16[512,512]{1,0:T(8,128)(2,1)} %copy-done.8) | copy-start | bytes 1572868
  175.4 2.3 %copy-start.21 = (bf16[512,512]{1,0:T(8,128)(2,1)S(1)}, bf16[512,512]{1,0:T(8,128)(2,1)}, u32[]{:S(2)}) copy-start(bf16[512,512]{1,0:T(8,128)(2,1)} %copy-done.20) | copy-start | bytes 1572868
  175.4 14.2 %collective-permute-start.16 = (bf16[512,512]{1,0:T(8,128)(2,1)S(1)}, bf16[512,512]{1,0:T(8,128)(2,1)S(1)}, u32[]{:S(2)}, u32[]{:S(2)}) collective-permute-start(bf16[512,512]{1,0:T(8,128)(2,1)S(1)} %fusion.7), channel_id=1, source_target_pairs={{0,2},{1,3},{2,0},{3,1},{4,6},{5,7},{6,4},{7,5},{8,10},{9,11},{10,... | collective-permute-start | bytes 1572872 | tf_op jit(solution)/shard_map/ppermute | solution.py:131
  189.6 2.4 %copy-start.19 = (bf16[512,512]{1,0:T(8,128)(2,1)S(1)}, bf16[512,512]{1,0:T(8,128)(2,1)}, u32[]{:S(2)}) copy-start(bf16[512,512]{1,0:T(8,128)(2,1)} %copy-done.18) | copy-start | bytes 1572868
  190.5 13.4 %collective-permute-start.17 = (bf16[512,512]{1,0:T(8,128)(2,1)S(1)}, bf16[512,512]{1,0:T(8,128)(2,1)S(1)}, u32[]{:S(2)}, u32[]{:S(2)}) collective-permute-start(bf16[512,512]{1,0:T(8,128)(2,1)S(1)} %fusion.8), channel_id=1, source_target_pairs={{0,2},{1,3},{2,0},{3,1},{4,6},{5,7},{6,4},{7,5},{8,10},{9,11},{10,... | collective-permute-start | bytes 1572872 | tf_op jit(solution)/shard_map/ppermute | solution.py:140
  192.7 11.8 %collective-permute-start.18 = (bf16[512,512]{1,0:T(8,128)(2,1)S(1)}, bf16[512,512]{1,0:T(8,128)(2,1)S(1)}, u32[]{:S(2)}, u32[]{:S(2)}) collective-permute-start(bf16[512,512]{1,0:T(8,128)(2,1)S(1)} %fusion.8), channel_id=1, source_target_pairs={{0,1},{1,0},{2,3},{3,2},{4,5},{5,4},{6,7},{7,6},{8,9},{9,8},{10,11... | collective-permute-start | bytes 1572872 | tf_op jit(solution)/shard_map/ppermute | solution.py:141
  203.8 1.9 collective-permute-start.19
  207.0 3.7 %collective-permute-start.20 = (f32[1024]{0:T(1024)S(1)}, f32[1024]{0:T(1024)S(1)}, u32[]{:S(2)}, u32[]{:S(2)}) collective-permute-start(f32[1024]{0:T(1024)S(1)} %fusion.1), channel_id=1, source_target_pairs={{0,4},{4,0},{8,12},{12,8},{16,20},{20,16},{24,28},{28,24},{1,5},{5... | collective-permute-start | bytes 12296 | tf_op jit(solution)/shard_map/ppermute | solution.py:74
  210.7 7.1 %collective-permute-start.21 = (f32[1024]{0:T(1024)S(1)}, f32[1024]{0:T(1024)S(1)}, u32[]{:S(2)}, u32[]{:S(2)}) collective-permute-start(f32[1024]{0:T(1024)S(1)} %add.205), channel_id=1, source_target_pairs={{0,8},{4,12},{8,0},{12,4},{16,24},{20,28},{24,16},{28,20},{1,9},{5... | collective-permute-start | bytes 12296 | tf_op jit(solution)/shard_map/ppermute | solution.py:74
  217.8 5.5 %collective-permute-start.22 = (f32[1024]{0:T(1024)S(1)}, f32[1024]{0:T(1024)S(1)}, u32[]{:S(2)}, u32[]{:S(2)}) collective-permute-start(f32[1024]{0:T(1024)S(1)} %add.206), channel_id=1, source_target_pairs={{0,16},{4,20},{8,24},{12,28},{16,0},{20,4},{24,8},{28,12},{1,17},{... | collective-permute-start | bytes 12296 | tf_op jit(solution)/shard_map/ppermute | solution.py:74

commit v13 on v8

--- a/solution.py
+++ b/solution.py
@@ -77,13 +77,15 @@
 
 def _sum_over_src(v):
     n = lax.axis_size("src")
-    if n & (n - 1):
-        return lax.psum(v, "src")
-    b = 1
-    while b < n:
-        v = v + lax.ppermute(v, "src", [(i, i ^ b) for i in range(n)])
-        b *= 2
-    return v
+    me = lax.axis_index("src")
+    got = [v] + [
+        lax.ppermute(v, "src", [(i, (i - k) % n) for i in range(n)]) for k in range(1, n)
+    ]
+    ordered = jnp.roll(jnp.stack(got), me, axis=0)
+    total = ordered[0]
+    for a in range(1, n):
+        total = total + ordered[a]
+    return total
 
 
 def per_device(grid, forward_voxel_field, adjoint_voxel_field, voxel_input_vector, measurement_weight):

time: 208 us -> 213 us (1.024)
  starting transfers between devices: 33.4 us -> 41.6 us
  waiting for transfers between devices: 130 us -> 127 us
    ppermute x3 -> x7, starting transfers between devices: 3.42 us -> 11.5 us  [_sum_over_src(): lax.ppermute(v, 'src', [(i, (i - k) % n) for i in range(n)])]
    ppermute x3 -> x7, waiting for transfers between devices: 8.36 us -> 4.84 us  [_sum_over_src(): lax.ppermute(v, 'src', [(i, (i - k) % n) for i in range(n)])]
  transfers between devices with their start and end apart: 29 -> 33, of which waited for: 15 -> 15; matrix products, arithmetic and copies ran while one was open for 15% -> 15% of each run, Pallas kernels for 0% -> 0%
where the time goes in v13:
time: 213 us; the launch traced here: 212 us
  waiting for transfers between devices  127 us (60%)
  starting transfers between devices  41.6 us (20%)
  matrix products  21.9 us (10%)
  other arithmetic  10.9 us (5%)
  local copies, waits for them, and re-layouts  10.8 us (5%)
    ppermute x12, waiting for transfers between devices, _gather_src(): cur = lax.ppermute(cur, 'src', pairs)  49.2 us
    ppermute x2, waiting for transfers between devices, _gather_src(): other = lax.ppermute(col, 'src', swap)  29.2 us
    ppermute x12, starting transfers between devices, _gather_src(): cur = lax.ppermute(cur, 'src', pairs)  23 us
    ppermute x2, waiting for transfers between devices, per_device(): got.append((2 * ((q - k) % m) + par, lax.ppermute(wt, 'vox', chip_perm(k))))  22.8 us
    ppermute x2, waiting for transfers between devices, per_device(): lax.ppermute(halves[k].astype(jnp.bfloat16), 'vox', chip_perm(k))  20 us
    dot_general x8, matrix products, pblock(): lax.dot_general(scaled, _rows(adj, rel(blk), n), (((1,), (1,)), ((), ()))...  15.5 us
    ppermute x7, starting transfers between devices, _sum_over_src(): lax.ppermute(v, 'src', [(i, (i - k) % n) for i in range(n)])  11.5 us
    dot_general x8, matrix products, per_device(): jnp.dot(w, _rows(adj, rel(blk), n), preferred_element_type=jnp.float32)  6.4 us
  transfers between devices with their start and end apart: 33, of which 15 were waited for; matrix products, arithmetic and copies ran while one was open for 15% of the time, Pallas kernels for 0%

profile of v13, /device:TPU:0, one launch (start us, length us, event | category | flops | bytes accessed | tf_op | source)
XLA Modules:
  0.0 212.4 jit_solution(13272184254027843725)
XLA Ops:
  0.0 2.3 %slice_bitcast_fusion = (bf16[1,256,1024]{2,1,0:T(8,128)(2,1)S(1)}, bf16[1,256,1024]{2,1,0:T(8,128)(2,1)S(1)}, bf16[256,1024]{1,0:T(8,128)(2,1)S(1)}, bf16[256,1024]{1,0:T(8,128)(2,1)}) fusion(bf16[512,1024]{1,0:T(8,128)(2,1)} %param.5), kind=kLoop, calls=%fused_computation.88 | loop fusion | bytes 3145728 | tf_op jit(solution)/shard_map/stack | solution.py:71
  2.3 1.3 collective-permute-start.7
  3.6 5.6 %collective-permute-start.8 = (bf16[256,1024]{1,0:T(8,128)(2,1)S(1)}, bf16[256,1024]{1,0:T(8,128)(2,1)S(1)}, u32[]{:S(2)}, u32[]{:S(2)}) collective-permute-start(bf16[256,1024]{1,0:T(8,128)(2,1)S(1)} %get-tuple-element.23), channel_id=1, source_target_pairs={{0,8},{4,12},{8,16},{12,20},{16,24},{20,28},{1,9},{5,13},{9,17},{1... | collective-permute-start | bytes 1572872 | tf_op jit(solution)/shard_map/ppermute | solution.py:66
  9.2 10.0 %collective-permute-done.7 = bf16[256,1024]{1,0:T(8,128)(2,1)S(1)} collective-permute-done((bf16[256,1024]{1,0:T(8,128)(2,1)S(1)}, bf16[256,1024]{1,0:T(8,128)(2,1)S(1)}, u32[]{:S(2)}, u32[]{:S(2)}) %collective-permute-start.7) | collective-permute-done | bytes 524320 | tf_op jit(solution)/shard_map/ppermute | solution.py:66
  19.1 1.3 collective-permute-start.11
  20.4 1.5 collective-permute-start.9
  21.9 12.2 %collective-permute-done.11 = bf16[256,1024]{1,0:T(8,128)(2,1)S(1)} collective-permute-done((bf16[256,1024]{1,0:T(8,128)(2,1)S(1)}, bf16[256,1024]{1,0:T(8,128)(2,1)S(1)}, u32[]{:S(2)}, u32[]{:S(2)}) %collective-permute-start.11) | collective-permute-done | bytes 524320 | tf_op jit(solution)/shard_map/ppermute | solution.py:66
  34.1 1.3 collective-permute-start.12
  36.2 12.1 %collective-permute-done.12 = bf16[256,1024]{1,0:T(8,128)(2,1)} collective-permute-done((bf16[256,1024]{1,0:T(8,128)(2,1)S(1)}, bf16[256,1024]{1,0:T(8,128)(2,1)}, u32[]{:S(2)}, u32[]{:S(2)}) %collective-permute-start.12) | collective-permute-done | bytes 524320 | tf_op jit(solution)/shard_map/ppermute | solution.py:66
  48.3 1.1 select_bitcast_fusion.4
  49.5 1.6 pad_maximum_fusion.3
  51.1 1.0 collective-permute-start.13
  52.1 1.3 collective-permute-start
  53.4 5.4 %collective-permute-start.1 = (bf16[256,1024]{1,0:T(8,128)(2,1)S(1)}, bf16[256,1024]{1,0:T(8,128)(2,1)}, u32[]{:S(2)}, u32[]{:S(2)}) collective-permute-start(bf16[256,1024]{1,0:T(8,128)(2,1)S(1)} %copy-done.22), channel_id=1, source_target_pairs={{0,8},{4,12},{8,16},{12,20},{16,24},{20,28},{1,9},{5,13},{9,17},{1... | collective-permute-start | bytes 1572872 | tf_op jit(solution)/shard_map/ppermute | solution.py:66
  58.8 5.9 %collective-permute-done = bf16[256,1024]{1,0:T(8,128)(2,1)S(1)} collective-permute-done((bf16[256,1024]{1,0:T(8,128)(2,1)S(1)}, bf16[256,1024]{1,0:T(8,128)(2,1)S(1)}, u32[]{:S(2)}, u32[]{:S(2)}) %collective-permute-start) | collective-permute-done | bytes 524320 | tf_op jit(solution)/shard_map/ppermute | solution.py:66
  64.7 1.3 collective-permute-start.4
  66.0 1.5 collective-permute-start.2
  67.5 9.1 %collective-permute-done.4 = bf16[256,1024]{1,0:T(8,128)(2,1)} collective-permute-done((bf16[256,1024]{1,0:T(8,128)(2,1)S(1)}, bf16[256,1024]{1,0:T(8,128)(2,1)}, u32[]{:S(2)}, u32[]{:S(2)}) %collective-permute-start.4) | collective-permute-done | bytes 524320 | tf_op jit(solution)/shard_map/ppermute | solution.py:66
  76.6 1.3 collective-permute-start.5
  78.6 1.1 select_bitcast_fusion.8
  79.7 16.7 %collective-permute-done.13 = bf16[4,256,1024]{2,1,0:T(8,128)(2,1)} collective-permute-done((bf16[4,256,1024]{2,1,0:T(8,128)(2,1)}, bf16[4,256,1024]{2,1,0:T(8,128)(2,1)}, u32[]{:S(2)}, u32[]{:S(2)}) %collective-permute-start.13) | collective-permute-done | bytes 2097184 | tf_op jit(solution)/shard_map/ppermute | solution.py:72
  96.4 1.8 select_bitcast_fusion.1
  99.8 1.7 fusion.31
  101.7 1.6 pad_maximum_fusion.2
  104.0 1.7 fusion.34
  106.0 2.8 %fusion.6 = bf16[512,512]{1,0:T(8,128)(2,1)} fusion(f32[512,512]{1,0:T(8,128)S(1)} %collective-permute-done.15, bf16[2048,1024]{1,0:T(8,128)(2,1)} %bitcast.51, s32[]{:T(128)S(6)} %select_n.217, bf16[512,1024]{1,0:T(8,128)(2,1)S(1)} %copy-done.4, f32[1024]{0:T(1024)S(1)} %copy-done.23), kind=kOutput, calls=%fused_computation.20 | convolution fusion | flops 538968064 | bytes 3674116 | tf_op jit(solution)/shard_map/dot_general | solution.py:133
  108.8 1.5 collective-permute-start.16
  110.3 3.0 %reshape.21 = f32[512,2,512]{2,1,0:T(2,128)S(1)} reshape(f32[512,1024]{1,0:T(8,128)} %param.7) | data formatting | bytes 4194304 | tf_op jit(solution)/shard_map/reshape | solution.py:112
  113.3 1.7 fusion.68
  115.1 8.1 %collective-permute-done.16 = bf16[512,512]{1,0:T(8,128)(2,1)} collective-permute-done((bf16[512,512]{1,0:T(8,128)(2,1)}, bf16[512,512]{1,0:T(8,128)(2,1)}, u32[]{:S(2)}, u32[]{:S(2)}) %collective-permute-start.16) | collective-permute-done | bytes 524320 | tf_op jit(solution)/shard_map/ppermute | solution.py:143
  123.2 2.6 %fusion.9 = bf16[512,512]{1,0:T(8,128)(2,1)S(1)} fusion(f32[512,512]{1,0:T(8,128)S(1)} %bitcast.67, f32[512,512]{1,0:T(8,128)} %collective-permute-done.14, bf16[512,512]{1,0:T(8,128)(2,1)} %collective-permute-done.16, bf16[2048,1024]{1,0:T(8,128)(2,1)} %bitcast.52, s32[]{:T(128)S(6)} %select_n.212, bf16[512,1024]{1,0:T(8,128)(2,1)S(1)} %copy-done.4, ...), kind=kOutput, calls=%fused_computation.23 | convolution fusion | flops 539754496 | bytes 5246980 | tf_op jit(solution)/shard_map/dot_general | solution.py:133
  125.8 1.6 collective-permute-start.17
  127.4 11.8 %collective-permute-done.17 = bf16[512,512]{1,0:T(8,128)(2,1)S(1)} collective-permute-done((bf16[512,512]{1,0:T(8,128)(2,1)S(1)}, bf16[512,512]{1,0:T(8,128)(2,1)S(1)}, u32[]{:S(2)}, u32[]{:S(2)}) %collective-permute-start.17) | collective-permute-done | bytes 524320 | tf_op jit(solution)/shard_map/ppermute | solution.py:152
  139.2 12.5 %collective-permute-done.6 = bf16[4,256,1024]{2,1,0:T(8,128)(2,1)} collective-permute-done((bf16[4,256,1024]{2,1,0:T(8,128)(2,1)}, bf16[4,256,1024]{2,1,0:T(8,128)(2,1)}, u32[]{:S(2)}, u32[]{:S(2)}) %collective-permute-start.6) | collective-permute-done | bytes 2097184 | tf_op jit(solution)/shard_map/ppermute | solution.py:72
  151.7 2.0 select_bitcast_fusion.3
  155.0 1.7 fusion.17
  157.1 2.1 %fusion.20 = f32[512,512]{1,0:T(8,128)S(1)} fusion(bf16[2048,1024]{1,0:T(8,128)(2,1)} %bitcast.58, s32[]{:T(128)S(6)} %select_n.214, bf16[512,1024]{1,0:T(8,128)(2,1)S(1)} %copy-done.4, f32[1024]{0:T(1024)S(1)} %copy-done.23), kind=kOutput, calls=%fused_computation.34 | convolution fusion | flops 538443776 | bytes 3149828 | tf_op jit(solution)/shard_map/dot_general | solution.py:133
  160.5 1.1 copy-done.3
  161.6 2.0 fusion.7
  165.9 11.9 %collective-permute-done.22 = bf16[512,512]{1,0:T(8,128)(2,1)S(1)} collective-permute-done((bf16[512,512]{1,0:T(8,128)(2,1)S(1)}, bf16[512,512]{1,0:T(8,128)(2,1)S(1)}, u32[]{:S(2)}, u32[]{:S(2)}) %collective-permute-start.22) | collective-permute-done | bytes 524320 | tf_op jit(solution)/shard_map/ppermute | solution.py:143
  181.0 11.1 %collective-permute-done.23 = bf16[512,512]{1,0:T(8,128)(2,1)S(1)} collective-permute-done((bf16[512,512]{1,0:T(8,128)(2,1)S(1)}, bf16[512,512]{1,0:T(8,128)(2,1)S(1)}, u32[]{:S(2)}, u32[]{:S(2)}) %collective-permute-start.23) | collective-permute-done | bytes 524320 | tf_op jit(solution)/shard_map/ppermute | solution.py:152
  194.0 1.2 fusion.1
  195.2 5.1 %collective-permute-start.26 = (f32[1024]{0:T(1024)S(1)}, f32[1024]{0:T(1024)S(1)}, u32[]{:S(2)}, u32[]{:S(2)}) collective-permute-start(f32[1024]{0:T(1024)S(1)} %fusion.1), channel_id=1, source_target_pairs={{0,28},{4,0},{8,4},{12,8},{16,12},{20,16},{24,20},{28,24},{1,29},{... | collective-permute-start | bytes 12296 | tf_op jit(solution)/shard_map/ppermute | solution.py:82
  200.4 3.4 %collective-permute-start.29 = (f32[1024]{0:T(1024)S(1)}, f32[1024]{0:T(1024)S(1)}, u32[]{:S(2)}, u32[]{:S(2)}) collective-permute-start(f32[1024]{0:T(1024)S(1)} %fusion.1), channel_id=1, source_target_pairs={{0,16},{4,20},{8,24},{12,28},{16,0},{20,4},{24,8},{28,12},{1,17},{... | collective-permute-start | bytes 12296 | tf_op jit(solution)/shard_map/ppermute | solution.py:82
  203.8 1.5 collective-permute-start.31
  205.3 1.5 collective-permute-start.32
  206.8 2.4 %collective-permute-done.30 = f32[1024]{0:T(1024)S(1)} collective-permute-done((f32[1024]{0:T(1024)S(1)}, f32[1024]{0:T(1024)S(1)}, u32[]{:S(2)}, u32[]{:S(2)}) %collective-permute-start.30) | collective-permute-done | bytes 4128 | tf_op jit(solution)/shard_map/ppermute | solution.py:82
  210.2 1.4 collective-permute-done.32
  (102 shorter events, 16.2 us)
Async XLA Ops:
  2.3 99.4 %copy-start.11 = (bf16[1,256,1024]{2,1,0:T(8,128)(2,1)}, bf16[1,256,1024]{2,1,0:T(8,128)(2,1)S(1)}, u32[]{:S(2)}) copy-start(bf16[1,256,1024]{2,1,0:T(8,128)(2,1)S(1)} %get-tuple-element.22) | copy-start | bytes 1572868
  2.3 16.8 %collective-permute-start.7 = (bf16[256,1024]{1,0:T(8,128)(2,1)S(1)}, bf16[256,1024]{1,0:T(8,128)(2,1)S(1)}, u32[]{:S(2)}, u32[]{:S(2)}) collective-permute-start(bf16[256,1024]{1,0:T(8,128)(2,1)S(1)} %get-tuple-element.23), channel_id=1, source_target_pairs={{8,0},{12,4},{16,8},{20,12},{24,16},{28,20},{9,1},{13,5},{17,9},{2... | collective-permute-start | bytes 1572872 | tf_op jit(solution)/shard_map/ppermute | solution.py:66
  3.6 16.8 %collective-permute-start.8 = (bf16[256,1024]{1,0:T(8,128)(2,1)S(1)}, bf16[256,1024]{1,0:T(8,128)(2,1)S(1)}, u32[]{:S(2)}, u32[]{:S(2)}) collective-permute-start(bf16[256,1024]{1,0:T(8,128)(2,1)S(1)} %get-tuple-element.23), channel_id=1, source_target_pairs={{0,8},{4,12},{8,16},{12,20},{16,24},{20,28},{1,9},{5,13},{9,17},{1... | collective-permute-start | bytes 1572872 | tf_op jit(solution)/shard_map/ppermute | solution.py:66
  19.1 15.0 %collective-permute-start.11 = (bf16[256,1024]{1,0:T(8,128)(2,1)S(1)}, bf16[256,1024]{1,0:T(8,128)(2,1)S(1)}, u32[]{:S(2)}, u32[]{:S(2)}) collective-permute-start(bf16[256,1024]{1,0:T(8,128)(2,1)S(1)} %collective-permute-done.7), channel_id=1, source_target_pairs={{8,0},{12,4},{16,8},{20,12},{9,1},{13,5},{17,9},{21,13},{10,2},{14... | collective-permute-start | bytes 1572872 | tf_op jit(solution)/shard_map/ppermute | solution.py:66
  20.4 15.0 %collective-permute-start.9 = (bf16[256,1024]{1,0:T(8,128)(2,1)S(1)}, bf16[256,1024]{1,0:T(8,128)(2,1)}, u32[]{:S(2)}, u32[]{:S(2)}) collective-permute-start(bf16[256,1024]{1,0:T(8,128)(2,1)S(1)} %collective-permute-done.8), channel_id=1, source_target_pairs={{8,16},{12,20},{16,24},{20,28},{9,17},{13,21},{17,25},{21,29},{10,... | collective-permute-start | bytes 1572872 | tf_op jit(solution)/shard_map/ppermute | solution.py:66
  34.1 14.2 %collective-permute-start.12 = (bf16[256,1024]{1,0:T(8,128)(2,1)S(1)}, bf16[256,1024]{1,0:T(8,128)(2,1)}, u32[]{:S(2)}, u32[]{:S(2)}) collective-permute-start(bf16[256,1024]{1,0:T(8,128)(2,1)S(1)} %collective-permute-done.11), channel_id=1, source_target_pairs={{8,0},{12,4},{9,1},{13,5},{10,2},{14,6},{11,3},{15,7}} | collective-permute-start | bytes 1572872 | tf_op jit(solution)/shard_map/ppermute | solution.py:66
  35.4 14.0 %collective-permute-start.10 = (bf16[256,1024]{1,0:T(8,128)(2,1)}, bf16[256,1024]{1,0:T(8,128)(2,1)S(1)}, u32[]{:S(2)}, u32[]{:S(2)}) collective-permute-start(bf16[256,1024]{1,0:T(8,128)(2,1)} %collective-permute-done.9), channel_id=1, source_target_pairs={{16,24},{20,28},{17,25},{21,29},{18,26},{22,30},{19,27},{23,31}} | collective-permute-start | bytes 1572872 | tf_op jit(solution)/shard_map/ppermute | solution.py:66
  49.5 2.7 %copy-start.22 = (bf16[256,1024]{1,0:T(8,128)(2,1)S(1)}, bf16[256,1024]{1,0:T(8,128)(2,1)}, u32[]{:S(2)}) copy-start(bf16[256,1024]{1,0:T(8,128)(2,1)} %get-tuple-element.24) | copy-start | bytes 1572868
  51.1 45.3 %collective-permute-start.13 = (bf16[4,256,1024]{2,1,0:T(8,128)(2,1)}, bf16[4,256,1024]{2,1,0:T(8,128)(2,1)}, u32[]{:S(2)}, u32[]{:S(2)}) collective-permute-start(bf16[4,256,1024]{2,1,0:T(8,128)(2,1)} %pad_maximum_fusion.3), channel_id=1, source_target_pairs={{0,4},{4,0},{8,12},{12,8},{16,20},{20,16},{24,28},{28,24},{1,5},{5... | collective-permute-start | bytes 6291464 | tf_op jit(solution)/shard_map/ppermute | solution.py:72
  52.1 12.6 %collective-permute-start = (bf16[256,1024]{1,0:T(8,128)(2,1)S(1)}, bf16[256,1024]{1,0:T(8,128)(2,1)S(1)}, u32[]{:S(2)}, u32[]{:S(2)}) collective-permute-start(bf16[256,1024]{1,0:T(8,128)(2,1)S(1)} %copy-done.22), channel_id=1, source_target_pairs={{8,0},{12,4},{16,8},{20,12},{24,16},{28,20},{9,1},{13,5},{17,9},{2... | collective-permute-start | bytes 1572872 | tf_op jit(solution)/shard_map/ppermute | solution.py:66
  53.4 12.6 %collective-permute-start.1 = (bf16[256,1024]{1,0:T(8,128)(2,1)S(1)}, bf16[256,1024]{1,0:T(8,128)(2,1)}, u32[]{:S(2)}, u32[]{:S(2)}) collective-permute-start(bf16[256,1024]{1,0:T(8,128)(2,1)S(1)} %copy-done.22), channel_id=1, source_target_pairs={{0,8},{4,12},{8,16},{12,20},{16,24},{20,28},{1,9},{5,13},{9,17},{1... | collective-permute-start | bytes 1572872 | tf_op jit(solution)/shard_map/ppermute | solution.py:66
  64.7 11.9 %collective-permute-start.4 = (bf16[256,1024]{1,0:T(8,128)(2,1)S(1)}, bf16[256,1024]{1,0:T(8,128)(2,1)}, u32[]{:S(2)}, u32[]{:S(2)}) collective-permute-start(bf16[256,1024]{1,0:T(8,128)(2,1)S(1)} %collective-permute-done), channel_id=1, source_target_pairs={{8,0},{12,4},{16,8},{20,12},{9,1},{13,5},{17,9},{21,13},{10,2},{14... | collective-permute-start | bytes 1572872 | tf_op jit(solution)/shard_map/ppermute | solution.py:66
  66.0 11.9 %collective-permute-start.2 = (bf16[256,1024]{1,0:T(8,128)(2,1)}, bf16[256,1024]{1,0:T(8,128)(2,1)}, u32[]{:S(2)}, u32[]{:S(2)}) collective-permute-start(bf16[256,1024]{1,0:T(8,128)(2,1)} %collective-permute-done.1), channel_id=1, source_target_pairs={{8,16},{12,20},{16,24},{20,28},{9,17},{13,21},{17,25},{21,29},{10,... | collective-permute-start | bytes 1572872 | tf_op jit(solution)/shard_map/ppermute | solution.py:66
  76.6 24.9 %collective-permute-start.5 = (bf16[256,1024]{1,0:T(8,128)(2,1)}, bf16[256,1024]{1,0:T(8,128)(2,1)S(1)}, u32[]{:S(2)}, u32[]{:S(2)}) collective-permute-start(bf16[256,1024]{1,0:T(8,128)(2,1)} %collective-permute-done.4), channel_id=1, source_target_pairs={{8,0},{12,4},{9,1},{13,5},{10,2},{14,6},{11,3},{15,7}} | collective-permute-start | bytes 1572872 | tf_op jit(solution)/shard_map/ppermute | solution.py:66
  77.9 23.7 %collective-permute-start.3 = (bf16[256,1024]{1,0:T(8,128)(2,1)}, bf16[256,1024]{1,0:T(8,128)(2,1)S(1)}, u32[]{:S(2)}, u32[]{:S(2)}) collective-permute-start(bf16[256,1024]{1,0:T(8,128)(2,1)} %collective-permute-done.2), channel_id=1, source_target_pairs={{16,24},{20,28},{17,25},{21,29},{18,26},{22,30},{19,27},{23,31}} | collective-permute-start | bytes 1572872 | tf_op jit(solution)/shard_map/ppermute | solution.py:66
  79.7 22.0 %copy-start.5 = (bf16[1,256,1024]{2,1,0:T(8,128)(2,1)}, bf16[1,256,1024]{2,1,0:T(8,128)(2,1)S(1)}, u32[]{:S(2)}) copy-start(bf16[1,256,1024]{2,1,0:T(8,128)(2,1)S(1)} %select_bitcast_fusion.8) | copy-start | bytes 1572868
  99.0 5.1 %copy-start = (bf16[4,2,256,1024]{3,2,1,0:T(8,128)(2,1)}, bf16[4,2,256,1024]{3,2,1,0:T(8,128)(2,1)S(1)}, u32[]{:S(2)}) copy-start(bf16[4,2,256,1024]{3,2,1,0:T(8,128)(2,1)S(1)} %copy.6) | copy-start | bytes 12582916
  101.5 4.5 %collective-permute-start.15 = (f32[512,512]{1,0:T(8,128)}, f32[512,512]{1,0:T(8,128)S(1)}, u32[]{:S(2)}, u32[]{:S(2)}) collective-permute-start(f32[512,512]{1,0:T(8,128)} %fusion.31), channel_id=1, source_target_pairs={{0,1},{1,0},{2,3},{3,2},{4,5},{5,4},{6,7},{7,6},{8,9},{9,8},{10,11... | collective-permute-start | bytes 3145736 | tf_op jit(solution)/shard_map/ppermute | solution.py:140
  103.3 48.4 %collective-permute-start.6 = (bf16[4,256,1024]{2,1,0:T(8,128)(2,1)}, bf16[4,256,1024]{2,1,0:T(8,128)(2,1)}, u32[]{:S(2)}, u32[]{:S(2)}) collective-permute-start(bf16[4,256,1024]{2,1,0:T(8,128)(2,1)} %pad_maximum_fusion.2), channel_id=1, source_target_pairs={{0,4},{4,0},{8,12},{12,8},{16,20},{20,16},{24,28},{28,24},{1,5},{5... | collective-permute-start | bytes 6291464 | tf_op jit(solution)/shard_map/ppermute | solution.py:72
  105.8 9.3 %collective-permute-start.14 = (f32[512,512]{1,0:T(8,128)}, f32[512,512]{1,0:T(8,128)}, u32[]{:S(2)}, u32[]{:S(2)}) collective-permute-start(f32[512,512]{1,0:T(8,128)} %fusion.34), channel_id=1, source_target_pairs={{0,1},{1,0},{2,3},{3,2},{4,5},{5,4},{6,7},{7,6},{8,9},{9,8},{10,11... | collective-permute-start | bytes 3145736 | tf_op jit(solution)/shard_map/ppermute | solution.py:140
  108.8 14.4 %collective-permute-start.16 = (bf16[512,512]{1,0:T(8,128)(2,1)}, bf16[512,512]{1,0:T(8,128)(2,1)}, u32[]{:S(2)}, u32[]{:S(2)}) collective-permute-start(bf16[512,512]{1,0:T(8,128)(2,1)} %fusion.6), channel_id=1, source_target_pairs={{0,2},{1,3},{2,0},{3,1},{4,6},{5,7},{6,4},{7,5},{8,10},{9,11},{10,... | collective-permute-start | bytes 1572872 | tf_op jit(solution)/shard_map/ppermute | solution.py:143
  123.2 28.5 %copy-start.6 = (bf16[1,256,1024]{2,1,0:T(8,128)(2,1)S(1)}, bf16[1,256,1024]{2,1,0:T(8,128)(2,1)}, u32[]{:S(2)}) copy-start(bf16[1,256,1024]{2,1,0:T(8,128)(2,1)} %copy-done.5) | copy-start | bytes 1572868
  123.2 28.5 %copy-start.8 = (bf16[1,256,1024]{2,1,0:T(8,128)(2,1)S(1)}, bf16[1,256,1024]{2,1,0:T(8,128)(2,1)}, u32[]{:S(2)}) copy-start(bf16[1,256,1024]{2,1,0:T(8,128)(2,1)} %copy-done.7) | copy-start | bytes 1572868
  123.2 28.5 %copy-start.10 = (bf16[1,256,1024]{2,1,0:T(8,128)(2,1)S(1)}, bf16[1,256,1024]{2,1,0:T(8,128)(2,1)}, u32[]{:S(2)}) copy-start(bf16[1,256,1024]{2,1,0:T(8,128)(2,1)} %copy-done.9) | copy-start | bytes 1572868
  123.2 28.5 %copy-start.12 = (bf16[1,256,1024]{2,1,0:T(8,128)(2,1)S(1)}, bf16[1,256,1024]{2,1,0:T(8,128)(2,1)}, u32[]{:S(2)}) copy-start(bf16[1,256,1024]{2,1,0:T(8,128)(2,1)} %copy-done.11) | copy-start | bytes 1572868
  125.8 27.9 %copy-start.14 = (bf16[512,512]{1,0:T(8,128)(2,1)}, bf16[512,512]{1,0:T(8,128)(2,1)S(1)}, u32[]{:S(2)}) copy-start(bf16[512,512]{1,0:T(8,128)(2,1)S(1)} %fusion.9) | copy-start | bytes 1572868
  125.8 13.3 %collective-permute-start.17 = (bf16[512,512]{1,0:T(8,128)(2,1)S(1)}, bf16[512,512]{1,0:T(8,128)(2,1)S(1)}, u32[]{:S(2)}, u32[]{:S(2)}) collective-permute-start(bf16[512,512]{1,0:T(8,128)(2,1)S(1)} %fusion.9), channel_id=1, source_target_pairs={{0,2},{1,3},{2,0},{3,1},{4,6},{5,7},{6,4},{7,5},{8,10},{9,11},{10,... | collective-permute-start | bytes 1572872 | tf_op jit(solution)/shard_map/ppermute | solution.py:152
  127.4 26.7 %collective-permute-start.18 = (bf16[512,512]{1,0:T(8,128)(2,1)S(1)}, bf16[512,512]{1,0:T(8,128)(2,1)S(1)}, u32[]{:S(2)}, u32[]{:S(2)}) collective-permute-start(bf16[512,512]{1,0:T(8,128)(2,1)S(1)} %fusion.9), channel_id=1, source_target_pairs={{0,1},{1,0},{2,3},{3,2},{4,5},{5,4},{6,7},{7,6},{8,9},{9,8},{10,11... | collective-permute-start | bytes 1572872 | tf_op jit(solution)/shard_map/ppermute | solution.py:153
  139.2 14.6 %copy-start.20 = (bf16[512,512]{1,0:T(8,128)(2,1)}, bf16[512,512]{1,0:T(8,128)(2,1)S(1)}, u32[]{:S(2)}) copy-start(bf16[512,512]{1,0:T(8,128)(2,1)S(1)} %collective-permute-done.17) | copy-start | bytes 1572868
  139.2 15.0 %collective-permute-start.19 = (bf16[512,512]{1,0:T(8,128)(2,1)S(1)}, bf16[512,512]{1,0:T(8,128)(2,1)S(1)}, u32[]{:S(2)}, u32[]{:S(2)}) collective-permute-start(bf16[512,512]{1,0:T(8,128)(2,1)S(1)} %collective-permute-done.17), channel_id=1, source_target_pairs={{0,1},{1,0},{2,3},{3,2},{4,5},{5,4},{6,7},{7,6},{8,9},{9,8},{10,11... | collective-permute-start | bytes 1572872 | tf_op jit(solution)/shard_map/ppermute | solution.py:153
  154.1 2.6 %copy-start.2 = (bf16[4,2,256,1024]{3,2,1,0:T(8,128)(2,1)}, bf16[4,2,256,1024]{3,2,1,0:T(8,128)(2,1)S(1)}, u32[]{:S(2)}) copy-start(bf16[4,2,256,1024]{3,2,1,0:T(8,128)(2,1)S(1)} %pad_maximum_fusion) | copy-start | bytes 12582916
  156.8 3.7 %collective-permute-start.21 = (f32[512,512]{1,0:T(8,128)}, f32[512,512]{1,0:T(8,128)}, u32[]{:S(2)}, u32[]{:S(2)}) collective-permute-start(f32[512,512]{1,0:T(8,128)} %fusion.17), channel_id=1, source_target_pairs={{0,1},{1,0},{2,3},{3,2},{4,5},{5,4},{6,7},{7,6},{8,9},{9,8},{10,11... | collective-permute-start | bytes 3145736 | tf_op jit(solution)/shard_map/ppermute | solution.py:140
  157.1 2.5 %copy-start.1 = (bf16[4,2,256,1024]{3,2,1,0:T(8,128)(2,1)S(1)}, bf16[4,2,256,1024]{3,2,1,0:T(8,128)(2,1)}, u32[]{:S(2)}) copy-start(bf16[4,2,256,1024]{3,2,1,0:T(8,128)(2,1)} %copy-done) | copy-start | bytes 12582916
  157.1 2.6 %copy-start.21 = (bf16[512,512]{1,0:T(8,128)(2,1)S(1)}, bf16[512,512]{1,0:T(8,128)(2,1)}, u32[]{:S(2)}) copy-start(bf16[512,512]{1,0:T(8,128)(2,1)} %copy-done.20) | copy-start | bytes 1572868
  159.2 2.3 %copy-start.3 = (bf16[4,2,256,1024]{3,2,1,0:T(8,128)(2,1)S(1)}, bf16[4,2,256,1024]{3,2,1,0:T(8,128)(2,1)}, u32[]{:S(2)}) copy-start(bf16[4,2,256,1024]{3,2,1,0:T(8,128)(2,1)} %copy-done.2) | copy-start | bytes 12582916
  159.3 6.6 %collective-permute-start.20 = (f32[512,512]{1,0:T(8,128)S(1)}, f32[512,512]{1,0:T(8,128)S(1)}, u32[]{:S(2)}, u32[]{:S(2)}) collective-permute-start(f32[512,512]{1,0:T(8,128)S(1)} %fusion.20), channel_id=1, source_target_pairs={{0,1},{1,0},{2,3},{3,2},{4,5},{5,4},{6,7},{7,6},{8,9},{9,8},{10,11... | collective-permute-start | bytes 3145736 | tf_op jit(solution)/shard_map/ppermute | solution.py:140
  160.4 3.9 %copy-start.15 = (bf16[512,512]{1,0:T(8,128)(2,1)S(1)}, bf16[512,512]{1,0:T(8,128)(2,1)}, u32[]{:S(2)}) copy-start(bf16[512,512]{1,0:T(8,128)(2,1)} %copy-done.14) | copy-start | bytes 1572868
  163.6 14.2 %collective-permute-start.22 = (bf16[512,512]{1,0:T(8,128)(2,1)S(1)}, bf16[512,512]{1,0:T(8,128)(2,1)S(1)}, u32[]{:S(2)}, u32[]{:S(2)}) collective-permute-start(bf16[512,512]{1,0:T(8,128)(2,1)S(1)} %fusion.7), channel_id=1, source_target_pairs={{0,2},{1,3},{2,0},{3,1},{4,6},{5,7},{6,4},{7,5},{8,10},{9,11},{10,... | collective-permute-start | bytes 1572872 | tf_op jit(solution)/shard_map/ppermute | solution.py:143
  178.7 13.4 %collective-permute-start.23 = (bf16[512,512]{1,0:T(8,128)(2,1)S(1)}, bf16[512,512]{1,0:T(8,128)(2,1)S(1)}, u32[]{:S(2)}, u32[]{:S(2)}) collective-permute-start(bf16[512,512]{1,0:T(8,128)(2,1)S(1)} %fusion.8), channel_id=1, source_target_pairs={{0,2},{1,3},{2,0},{3,1},{4,6},{5,7},{6,4},{7,5},{8,10},{9,11},{10,... | collective-permute-start | bytes 1572872 | tf_op jit(solution)/shard_map/ppermute | solution.py:152
  180.2 12.6 %collective-permute-start.24 = (bf16[512,512]{1,0:T(8,128)(2,1)S(1)}, bf16[512,512]{1,0:T(8,128)(2,1)S(1)}, u32[]{:S(2)}, u32[]{:S(2)}) collective-permute-start(bf16[512,512]{1,0:T(8,128)(2,1)S(1)} %fusion.8), channel_id=1, source_target_pairs={{0,1},{1,0},{2,3},{3,2},{4,5},{5,4},{6,7},{7,6},{8,9},{9,8},{10,11... | collective-permute-start | bytes 1572872 | tf_op jit(solution)/shard_map/ppermute | solution.py:153
  192.1 1.9 collective-permute-start.25
  195.2 8.6 %collective-permute-start.26 = (f32[1024]{0:T(1024)S(1)}, f32[1024]{0:T(1024)S(1)}, u32[]{:S(2)}, u32[]{:S(2)}) collective-permute-start(f32[1024]{0:T(1024)S(1)} %fusion.1), channel_id=1, source_target_pairs={{0,28},{4,0},{8,4},{12,8},{16,12},{20,16},{24,20},{28,24},{1,29},{... | collective-permute-start | bytes 12296 | tf_op jit(solution)/shard_map/ppermute | solution.py:82
  200.3 5.0 %collective-permute-start.27 = (f32[1024]{0:T(1024)S(1)}, f32[1024]{0:T(1024)S(1)}, u32[]{:S(2)}, u32[]{:S(2)}) collective-permute-start(f32[1024]{0:T(1024)S(1)} %fusion.1), channel_id=1, source_target_pairs={{0,24},{4,28},{8,0},{12,4},{16,8},{20,12},{24,16},{28,20},{1,25},{... | collective-permute-start | bytes 12296 | tf_op jit(solution)/shard_map/ppermute | solution.py:82
  200.3 6.4 %collective-permute-start.28 = (f32[1024]{0:T(1024)S(1)}, f32[1024]{0:T(1024)S(1)}, u32[]{:S(2)}, u32[]{:S(2)}) collective-permute-start(f32[1024]{0:T(1024)S(1)} %fusion.1), channel_id=1, source_target_pairs={{0,20},{4,24},{8,28},{12,0},{16,4},{20,8},{24,12},{28,16},{1,21},{... | collective-permute-start | bytes 12296 | tf_op jit(solution)/shard_map/ppermute | solution.py:82
  200.4 6.4 %collective-permute-start.29 = (f32[1024]{0:T(1024)S(1)}, f32[1024]{0:T(1024)S(1)}, u32[]{:S(2)}, u32[]{:S(2)}) collective-permute-start(f32[1024]{0:T(1024)S(1)} %fusion.1), channel_id=1, source_target_pairs={{0,16},{4,20},{8,24},{12,28},{16,0},{20,4},{24,8},{28,12},{1,17},{... | collective-permute-start | bytes 12296 | tf_op jit(solution)/shard_map/ppermute | solution.py:82
  203.8 5.4 %collective-permute-start.30 = (f32[1024]{0:T(1024)S(1)}, f32[1024]{0:T(1024)S(1)}, u32[]{:S(2)}, u32[]{:S(2)}) collective-permute-start(f32[1024]{0:T(1024)S(1)} %fusion.1), channel_id=1, source_target_pairs={{0,12},{4,16},{8,20},{12,24},{16,28},{20,0},{24,4},{28,8},{1,13},{... | collective-permute-start | bytes 12296 | tf_op jit(solution)/shard_map/ppermute | solution.py:82
  203.8 6.4 %collective-permute-start.31 = (f32[1024]{0:T(1024)S(1)}, f32[1024]{0:T(1024)S(1)}, u32[]{:S(2)}, u32[]{:S(2)}) collective-permute-start(f32[1024]{0:T(1024)S(1)} %fusion.1), channel_id=1, source_target_pairs={{0,8},{4,12},{8,16},{12,20},{16,24},{20,28},{24,0},{28,4},{1,9},{5... | collective-permute-start | bytes 12296 | tf_op jit(solution)/shard_map/ppermute | solution.py:82
  205.3 6.3 %collective-permute-start.32 = (f32[1024]{0:T(1024)S(1)}, f32[1024]{0:T(1024)S(1)}, u32[]{:S(2)}, u32[]{:S(2)}) collective-permute-start(f32[1024]{0:T(1024)S(1)} %fusion.1), channel_id=1, source_target_pairs={{0,4},{4,8},{8,12},{12,16},{16,20},{20,24},{24,28},{28,0},{1,5},{5... | collective-permute-start | bytes 12296 | tf_op jit(solution)/shard_map/ppermute | solution.py:82
  (9 other events, 13.7 us)

commit v14 on v8

--- a/solution.py
+++ b/solution.py
@@ -86,6 +86,101 @@
     return v
 
 
+def _zline(block, na):
+    me = lax.axis_index("src")
+    ia = me // 2
+
+    def along(p, d):
+        return [(p * 2 + o, d * 2 + o) for o in range(2)]
+
+    got = {}
+    for sign in (1, -1):
+        cur = block
+        for s in range(1, na):
+            pairs = []
+            for p in range(na):
+                if 0 <= p + sign < na and 0 <= p - sign * (s - 1) < na:
+                    pairs.extend(along(p, p + sign))
+            cur = lax.ppermute(cur, "src", pairs)
+            got[(sign, s)] = cur
+    col = [block] + [
+        jnp.where(ia + k < na, got[(-1, k)], got[(1, na - k)]) for k in range(1, na)
+    ]
+    return jnp.concatenate(col, axis=0)
+
+
+def _fast(na, forward_voxel_field, adjoint_voxel_field, voxel_input_vector, measurement_weight):
+    vox = lax.axis_size("vox")
+    me = lax.axis_index("vox")
+    m = vox // 2
+    par = me % 2
+    q = me // 2
+    si = lax.axis_index("src")
+    ia = si // 2
+    first = si % 2 == 0
+    sl, vl = forward_voxel_field.shape
+    ds = adjoint_voxel_field.shape[0]
+    chunks = CHUNKS if ds % (CHUNKS * 8) == 0 else 1
+    r = ds // chunks
+    swap = [(i, i ^ 1) for i in range(2 * na)]
+    pair = [(j, j ^ 1) for j in range(vox)]
+
+    def chip_perm(k):
+        return [(g * 2 + p, ((g + k) % m) * 2 + p) for g in range(m) for p in range(2)]
+
+    def rows(col, blk):
+        return lax.dynamic_slice_in_dim(col, ((blk - ia) % na) * r, r, axis=0)
+
+    fwd = jnp.concatenate(
+        [forward_voxel_field, lax.ppermute(forward_voxel_field, "src", swap)], axis=0
+    )
+    scaled = (fwd.astype(jnp.float32) * voxel_input_vector[None, :]).astype(jnp.bfloat16)
+    weight = measurement_weight.reshape(sl, 2, ds)
+    back = jnp.zeros((2 * sl, vl), jnp.float32)
+    nxt = _zline(adjoint_voxel_field[:r], na)
+    for c in range(chunks):
+        col = nxt
+
+        def pblock(blk):
+            return lax.dot_general(
+                scaled, rows(col, blk), (((1,), (1,)), ((), ())),
+                preferred_element_type=jnp.float32,
+            )
+
+        keeps = [pblock(2 * ((q + k) % m) + par) for k in range(m)]
+        sends = [pblock(2 * ((q + k) % m) + 1 - par) for k in range(m)]
+        halves = [a + b for a, b in zip(keeps, lax.ppermute(tuple(sends), "vox", pair))]
+        share = halves[0]
+        for k in range(1, m):
+            share = share + lax.ppermute(
+                halves[k].astype(jnp.bfloat16), "vox", chip_perm(k)
+            ).astype(jnp.float32)
+
+        own, theirs = share[:sl], lax.ppermute(share[sl:], "src", swap)
+        pred = jnp.stack([jnp.where(first, own, theirs), jnp.where(first, theirs, own)], axis=1)
+        w_c = weight[:, :, c * r:(c + 1) * r]
+        wt = (w_c * pred).astype(jnp.bfloat16)
+        mine = jnp.where(first, wt[:, 0], wt[:, 1])
+        other = jnp.where(first, wt[:, 1], wt[:, 0])
+        piece = jnp.concatenate([mine, lax.ppermute(other, "src", swap)], axis=0)
+
+        got = [(me, piece)]
+        for k in range(1, m):
+            got.append((2 * ((q - k) % m) + par, lax.ppermute(piece, "vox", chip_perm(k))))
+        mates = lax.ppermute(tuple(w for _, w in got), "vox", pair)
+        got = got + [(blk ^ 1, w) for (blk, _), w in zip(got, mates)]
+        if c + 1 < chunks:
+            nxt, ws = lax.optimization_barrier(
+                (_zline(adjoint_voxel_field[(c + 1) * r:(c + 2) * r], na), [w for _, w in got])
+            )
+            got = [(blk, w) for (blk, _), w in zip(got, ws)]
+        for blk, w in got:
+            back = back + jnp.dot(w, rows(col, blk), preferred_element_type=jnp.float32)
+
+    local_sum = jnp.sum(fwd.astype(jnp.float32) * back, axis=0)
+    return _sum_over_src(local_sum)
+
+
 def per_device(grid, forward_voxel_field, adjoint_voxel_field, voxel_input_vector, measurement_weight):
     nsrc = lax.axis_size("src")
     vox = lax.axis_size("vox")
@@ -162,6 +257,12 @@
 
 def solution(mesh):
     placed = (P("src", "vox"), P("src", "vox"), P("vox"), P("src", "vox"))
+    grid = _src_grid(mesh)
+    nsrc, vox = mesh.shape["src"], mesh.shape["vox"]
+    if grid is not None and grid[0] == 2 and nsrc == 2 * vox and vox % 2 == 0 and grid[1] == vox:
+        body = functools.partial(_fast, grid[1])
+    else:
+        body = functools.partial(per_device, None)
     return jax.shard_map(
-        functools.partial(per_device, _src_grid(mesh)), mesh=mesh, in_specs=placed, out_specs=P("vox"), check_vma=False
+        body, mesh=mesh, in_specs=placed, out_specs=P("vox"), check_vma=False
     )

time: 208 us -> 214 us (1.029)
  matrix products: 21.8 us -> 41.7 us
  waiting for transfers between devices: 130 us -> 115 us
  starting transfers between devices: 33.4 us -> 40.8 us
  other arithmetic: 10.9 us -> 5.22 us
    dot_general x16, matrix products: 21.8 us -> 41.7 us  [the longest x8 22.8 us: pblock(): lax.dot_general(scaled, rows(col, blk), (((1,), (1,)), ((), ())), preferr...]
    ppermute x26 -> x29, waiting for transfers between devices: 122 us -> 108 us  [the longest x12 40.1 us: _zline(): cur = lax.ppermute(cur, 'src', pairs)]
    another operation x12 -> x2, other arithmetic: 10.3 us -> 1.34 us  [_fast(): jnp.stack([jnp.where(first, own, theirs), jnp.where(first, theirs, own)],...]
    ppermute x3, starting transfers between devices: 3.42 us -> 7.34 us  [_sum_over_src(): v = v + lax.ppermute(v, 'src', [(i, i ^ b) for i in range(n)])]
    ppermute x26 -> x29, starting transfers between devices: 30 us -> 33.5 us  [the longest x12 21.5 us: _zline(): cur = lax.ppermute(cur, 'src', pairs)]
    reshape x1 -> x0, local copies, waits for them, and re-layouts: 3.03 us -> none  [per_device(): weight = measurement_weight.reshape(sl, t, ds)]
    another operation x2 -> x0, local copies, waits for them, and re-layouts: 2.69 us -> none  [the longest x1 2.25 us: _gather_src(): col = jnp.stack(col)]
    slice x1 -> x4, local copies, waits for them, and re-layouts: 1.68 us -> 4.14 us  [the longest x1 2.07 us: _fast(): nxt = _zline(adjoint_voxel_field[:r], na)]
  transfers between devices with their start and end apart: 29 -> 32, of which waited for: 15 -> 17; matrix products, arithmetic and copies ran while one was open for 15% -> 17% of each run, Pallas kernels for 0% -> 0%
where the time goes in v14:
time: 214 us; the launch traced here: 213 us
  waiting for transfers between devices  115 us (54%)
  matrix products  41.7 us (19%)
  starting transfers between devices  40.8 us (19%)
  local copies, waits for them, and re-layouts  9 us (4%)
  other arithmetic  5.22 us (2%)
    ppermute x12, waiting for transfers between devices, _zline(): cur = lax.ppermute(cur, 'src', pairs)  40.1 us
    ppermute x2, waiting for transfers between devices, _fast(): lax.ppermute(halves[k].astype(jnp.bfloat16), 'vox', chip_perm(k))  22.9 us
    dot_general x8, matrix products, pblock(): lax.dot_general(scaled, rows(col, blk), (((1,), (1,)), ((), ())), preferr...  22.8 us
    ppermute x12, starting transfers between devices, _zline(): cur = lax.ppermute(cur, 'src', pairs)  21.5 us
    dot_general x8, matrix products, _fast(): back = back + jnp.dot(w, rows(col, blk), preferred_element_type=jnp.float32)  18.9 us
    ppermute x2, waiting for transfers between devices, _fast(): own, theirs = (share[:sl], lax.ppermute(share[sl:], 'src', swap))  12.9 us
    ppermute x2, waiting for transfers between devices, _fast(): lax.ppermute(piece, 'vox', chip_perm(k))  12.2 us
    ppermute x1, waiting for transfers between devices, _fast(): lax.ppermute(forward_voxel_field, 'src', swap)  10.7 us
  transfers between devices with their start and end apart: 32, of which 17 were waited for; matrix products, arithmetic and copies ran while one was open for 17% of the time, Pallas kernels for 0%

profile of v14, /device:TPU:0, one launch (start us, length us, event | category | flops | bytes accessed | tf_op | source)
XLA Modules:
  0.0 212.7 jit_solution(9615551031149348081)
XLA Ops:
  0.0 2.1 fusion.60
  2.1 1.3 collective-permute-start.7
  3.4 5.6 %collective-permute-start.8 = (bf16[256,1024]{1,0:T(8,128)(2,1)S(1)}, bf16[256,1024]{1,0:T(8,128)(2,1)S(1)}, u32[]{:S(2)}, u32[]{:S(2)}) collective-permute-start(bf16[256,1024]{1,0:T(8,128)(2,1)S(1)} %get-tuple-element.21), channel_id=1, source_target_pairs={{0,8},{4,12},{8,16},{12,20},{16,24},{20,28},{1,9},{5,13},{9,17},{1... | collective-permute-start | bytes 1572872 | tf_op jit(solution)/shard_map/ppermute | solution.py:104
  9.0 10.0 %collective-permute-done.7 = bf16[256,1024]{1,0:T(8,128)(2,1)S(1)} collective-permute-done((bf16[256,1024]{1,0:T(8,128)(2,1)S(1)}, bf16[256,1024]{1,0:T(8,128)(2,1)S(1)}, u32[]{:S(2)}, u32[]{:S(2)}) %collective-permute-start.7) | collective-permute-done | bytes 524320 | tf_op jit(solution)/shard_map/ppermute | solution.py:104
  18.9 1.3 collective-permute-start.11
  20.9 13.0 %collective-permute-done.11 = bf16[256,1024]{1,0:T(8,128)(2,1)S(1)} collective-permute-done((bf16[256,1024]{1,0:T(8,128)(2,1)S(1)}, bf16[256,1024]{1,0:T(8,128)(2,1)S(1)}, u32[]{:S(2)}, u32[]{:S(2)}) %collective-permute-start.11) | collective-permute-done | bytes 524320 | tf_op jit(solution)/shard_map/ppermute | solution.py:104
  33.9 1.3 collective-permute-start.12
  35.2 1.4 collective-permute-start
  37.5 10.5 %collective-permute-done.12 = bf16[256,1024]{1,0:T(8,128)(2,1)S(1)} collective-permute-done((bf16[256,1024]{1,0:T(8,128)(2,1)S(1)}, bf16[256,1024]{1,0:T(8,128)(2,1)S(1)}, u32[]{:S(2)}, u32[]{:S(2)}) %collective-permute-start.12) | collective-permute-done | bytes 524320 | tf_op jit(solution)/shard_map/ppermute | solution.py:104
  48.3 10.7 %collective-permute-done = bf16[512,1024]{1,0:T(8,128)(2,1)} collective-permute-done((bf16[512,1024]{1,0:T(8,128)(2,1)}, bf16[512,1024]{1,0:T(8,128)(2,1)}, u32[]{:S(2)}, u32[]{:S(2)}) %collective-permute-start) | collective-permute-done | bytes 1048608 | tf_op jit(solution)/shard_map/ppermute | solution.py:135
  59.0 3.0 %fusion.29 = f32[1024,256]{1,0:T(8,128)} fusion(bf16[1024,1024]{1,0:T(8,128)(2,1)S(1)} %pad_maximum_fusion.2, s32[]{:T(128)S(6)} %select_n.234, f32[1024]{0:T(1024)S(1)} %copy-done.17, bf16[512,1024]{1,0:T(8,128)(2,1)} %collective-permute-done, bf16[512,1024]{1,0:T(8,128)(2,1)S(1)} %copy-done.12), kind=kOutput, calls=%fused_computation.46 | convolution fusion | flops 543162368 | bytes 3674116 | tf_op jit(solution)/shard_map/dot_general | solution.py:145
  62.0 3.0 %fusion.32 = f32[1024,256]{1,0:T(8,128)} fusion(bf16[1024,1024]{1,0:T(8,128)(2,1)S(1)} %pad_maximum_fusion.2, s32[]{:T(128)S(6)} %select_n.229, f32[1024]{0:T(1024)S(1)} %copy-done.17, bf16[512,1024]{1,0:T(8,128)(2,1)} %collective-permute-done, bf16[512,1024]{1,0:T(8,128)(2,1)S(1)} %copy-done.13), kind=kOutput, calls=%fused_computation.49 | convolution fusion | flops 543162368 | bytes 3674116 | tf_op jit(solution)/shard_map/dot_general | solution.py:145
  65.4 3.1 %fusion.4 = bf16[1024,256]{1,0:T(8,128)(2,1)} fusion(f32[1024,256]{1,0:T(8,128)} %collective-permute-done.14, bf16[1024,1024]{1,0:T(8,128)(2,1)S(1)} %pad_maximum_fusion.2, s32[]{:T(128)S(6)} %select_n.232, f32[1024]{0:T(1024)S(1)} %copy-done.17, bf16[512,1024]{1,0:T(8,128)(2,1)} %collective-permute-done, bf16[512,1024]{1,0:T(8,128)(2,1)S(1)} %copy-done.13), kind=kOutput, calls=%fused_computation.13 | convolution fusion | flops 543686656 | bytes 4198404 | tf_op jit(solution)/shard_map/dot_general | solution.py:145
  69.6 1.3 collective-permute-start.1
  70.9 11.8 %collective-permute-done.15 = bf16[1024,256]{1,0:T(8,128)(2,1)} collective-permute-done((bf16[1024,256]{1,0:T(8,128)(2,1)}, bf16[1024,256]{1,0:T(8,128)(2,1)}, u32[]{:S(2)}, u32[]{:S(2)}) %collective-permute-start.15) | collective-permute-done | bytes 524320 | tf_op jit(solution)/shard_map/ppermute | solution.py:155
  82.7 2.4 %fusion.3 = f32[1024,256]{1,0:T(8,128)S(1)} fusion(f32[1024,256]{1,0:T(8,128)} %collective-permute-done.13, bf16[1024,256]{1,0:T(8,128)(2,1)} %collective-permute-done.15, bf16[1024,1024]{1,0:T(8,128)(2,1)S(1)} %pad_maximum_fusion.2, s32[]{:T(128)S(6)} %select_n.227, f32[1024]{0:T(1024)S(1)} %copy-done.17, bf16[512,1024]{1,0:T(8,128)(2,1)} %collective-permute-done, ...), kind=kOutput, calls=%fused_computation.12 | convolution fusion | flops 543948800 | bytes 5246980 | tf_op jit(solution)/shard_map/dot_general | solution.py:145
  88.0 5.1 %collective-permute-start.2 = (bf16[256,1024]{1,0:T(8,128)(2,1)}, bf16[256,1024]{1,0:T(8,128)(2,1)}, u32[]{:S(2)}, u32[]{:S(2)}) collective-permute-start(bf16[256,1024]{1,0:T(8,128)(2,1)} %get-tuple-element.22), channel_id=1, source_target_pairs={{0,8},{4,12},{8,16},{12,20},{16,24},{20,28},{1,9},{5,13},{9,17},{1... | collective-permute-start | bytes 1572872 | tf_op jit(solution)/shard_map/ppermute | solution.py:104
  93.1 1.9 copy.5
  95.0 1.2 fusion.59
  96.6 1.3 collective-permute-start.5
  97.9 2.4 %collective-permute-done.16 = f32[512,256]{1,0:T(8,128)} collective-permute-done((f32[512,256]{1,0:T(8,128)}, f32[512,256]{1,0:T(8,128)}, u32[]{:S(2)}, u32[]{:S(2)}) %collective-permute-start.16) | collective-permute-done | bytes 524320 | tf_op jit(solution)/shard_map/ppermute | solution.py:159
  100.2 1.3 select_bitcast_fusion.3
  101.7 1.1 collective-permute-start.17
  103.5 4.7 %collective-permute-done.17 = bf16[512,256]{1,0:T(8,128)(2,1)S(1)} collective-permute-done((bf16[512,256]{1,0:T(8,128)(2,1)S(1)}, bf16[512,256]{1,0:T(8,128)(2,1)S(1)}, u32[]{:S(2)}, u32[]{:S(2)}) %collective-permute-start.17) | collective-permute-done | bytes 262176 | tf_op jit(solution)/shard_map/ppermute | solution.py:165
  109.4 1.7 collective-permute-done.5
  111.1 1.3 collective-permute-start.6
  113.4 6.1 %collective-permute-done.18 = bf16[1024,256]{1,0:T(8,128)(2,1)S(1)} collective-permute-done((bf16[1024,256]{1,0:T(8,128)(2,1)S(1)}, bf16[1024,256]{1,0:T(8,128)(2,1)S(1)}, u32[]{:S(2)}, u32[]{:S(2)}) %collective-permute-start.18) | collective-permute-done | bytes 524320 | tf_op jit(solution)/shard_map/ppermute | solution.py:169
  119.5 5.0 %collective-permute-done.6 = bf16[256,1024]{1,0:T(8,128)(2,1)S(1)} collective-permute-done((bf16[256,1024]{1,0:T(8,128)(2,1)S(1)}, bf16[256,1024]{1,0:T(8,128)(2,1)S(1)}, u32[]{:S(2)}, u32[]{:S(2)}) %collective-permute-start.6) | collective-permute-done | bytes 524320 | tf_op jit(solution)/shard_map/ppermute | solution.py:104
  125.7 1.2 pad_maximum_fusion.1
  127.0 2.8 %fusion.15 = f32[1024,256]{1,0:T(8,128)S(1)} fusion(bf16[1024,1024]{1,0:T(8,128)(2,1)S(1)} %pad_maximum_fusion.1, s32[]{:T(128)S(6)} %select_n.234, f32[1024]{0:T(1024)S(1)} %copy-done.17, bf16[512,1024]{1,0:T(8,128)(2,1)} %collective-permute-done, bf16[512,1024]{1,0:T(8,128)(2,1)S(1)} %copy-done.14), kind=kOutput, calls=%fused_computation.30 | convolution fusion | flops 543162368 | bytes 3674116 | tf_op jit(solution)/shard_map/dot_general | solution.py:145
  129.8 3.0 %fusion.18 = f32[1024,256]{1,0:T(8,128)} fusion(bf16[1024,1024]{1,0:T(8,128)(2,1)S(1)} %pad_maximum_fusion.1, s32[]{:T(128)S(6)} %select_n.229, f32[1024]{0:T(1024)S(1)} %copy-done.17, bf16[512,1024]{1,0:T(8,128)(2,1)} %collective-permute-done, bf16[512,1024]{1,0:T(8,128)(2,1)S(1)} %copy-done.14), kind=kOutput, calls=%fused_computation.33 | convolution fusion | flops 543162368 | bytes 3674116 | tf_op jit(solution)/shard_map/dot_general | solution.py:145
  133.3 2.8 %fusion.5 = bf16[1024,256]{1,0:T(8,128)(2,1)} fusion(f32[1024,256]{1,0:T(8,128)S(1)} %collective-permute-done.22, bf16[1024,1024]{1,0:T(8,128)(2,1)S(1)} %pad_maximum_fusion.1, s32[]{:T(128)S(6)} %select_n.232, f32[1024]{0:T(1024)S(1)} %copy-done.17, bf16[512,1024]{1,0:T(8,128)(2,1)} %collective-permute-done, bf16[512,1024]{1,0:T(8,128)(2,1)S(1)} %copy-done.14), kind=kOutput, calls=%fused_computation.14 | convolution fusion | flops 543686656 | bytes 4198404 | tf_op jit(solution)/shard_map/dot_general | solution.py:145
  136.2 1.5 collective-permute-start.23
  137.6 1.6 copy.9
  139.3 11.1 %collective-permute-done.23 = bf16[1024,256]{1,0:T(8,128)(2,1)} collective-permute-done((bf16[1024,256]{1,0:T(8,128)(2,1)}, bf16[1024,256]{1,0:T(8,128)(2,1)}, u32[]{:S(2)}, u32[]{:S(2)}) %collective-permute-start.23) | collective-permute-done | bytes 524320 | tf_op jit(solution)/shard_map/ppermute | solution.py:155
  150.3 2.7 %fusion.2 = f32[1024,256]{1,0:T(8,128)S(1)} fusion(f32[1024,256]{1,0:T(8,128)} %collective-permute-done.21, bf16[1024,256]{1,0:T(8,128)(2,1)} %collective-permute-done.23, bf16[1024,1024]{1,0:T(8,128)(2,1)S(1)} %pad_maximum_fusion.1, s32[]{:T(128)S(6)} %select_n.227, f32[1024]{0:T(1024)S(1)} %copy-done.17, bf16[512,1024]{1,0:T(8,128)(2,1)} %collective-permute-done, ...), kind=kOutput, calls=%fused_computation.9 | convolution fusion | flops 543948800 | bytes 5246980 | tf_op jit(solution)/shard_map/dot_general | solution.py:145
  155.7 10.5 %collective-permute-done.24 = f32[512,256]{1,0:T(8,128)S(1)} collective-permute-done((f32[512,256]{1,0:T(8,128)S(1)}, f32[512,256]{1,0:T(8,128)S(1)}, u32[]{:S(2)}, u32[]{:S(2)}) %collective-permute-start.24) | collective-permute-done | bytes 524320 | tf_op jit(solution)/shard_map/ppermute | solution.py:159
  168.3 4.8 %collective-permute-done.25 = bf16[512,256]{1,0:T(8,128)(2,1)S(1)} collective-permute-done((bf16[512,256]{1,0:T(8,128)(2,1)S(1)}, bf16[512,256]{1,0:T(8,128)(2,1)S(1)}, u32[]{:S(2)}, u32[]{:S(2)}) %collective-permute-start.25) | collective-permute-done | bytes 262176 | tf_op jit(solution)/shard_map/ppermute | solution.py:165
  173.1 1.5 collective-permute-start.26
  175.4 2.8 %fusion.13 = f32[1024,1024]{1,0:T(8,128)} fusion(bf16[1024,1024]{1,0:T(8,128)(2,1)S(1)} %copy-done.1, s32[]{:T(128)S(6)} %select_n.242, bf16[512,256]{1,0:T(8,128)(2,1)S(1)} %collective-permute-done.25, bf16[512,256]{1,0:T(8,128)(2,1)S(1)} %get-tuple-element.23), kind=kOutput, calls=%fused_computation.26 | convolution fusion | flops 537919488 | bytes 5242884 | tf_op jit(solution)/shard_map/dot_general | solution.py:178
  178.2 6.1 %collective-permute-done.26 = bf16[1024,256]{1,0:T(8,128)(2,1)S(1)} collective-permute-done((bf16[1024,256]{1,0:T(8,128)(2,1)S(1)}, bf16[1024,256]{1,0:T(8,128)(2,1)S(1)}, u32[]{:S(2)}, u32[]{:S(2)}) %collective-permute-start.26) | collective-permute-done | bytes 524320 | tf_op jit(solution)/shard_map/ppermute | solution.py:169
  184.3 2.7 %fusion.11 = f32[1024,1024]{1,0:T(8,128)} fusion(bf16[1024,256]{1,0:T(8,128)(2,1)S(1)} %collective-permute-done.26, bf16[1024,1024]{1,0:T(8,128)(2,1)S(1)} %copy-done.1, s32[]{:T(128)S(6)} %select_n.245), kind=kOutput, calls=%fused_computation.24 | convolution fusion | flops 536870912 | bytes 5242884 | tf_op jit(solution)/shard_map/dot_general | solution.py:178
  187.1 2.7 %fusion.9 = f32[1024,1024]{1,0:T(8,128)} fusion(bf16[1024,256]{1,0:T(8,128)(2,1)S(1)} %collective-permute-done.27, bf16[1024,1024]{1,0:T(8,128)(2,1)S(1)} %copy-done.1, s32[]{:T(128)S(6)} %select_n.247), kind=kOutput, calls=%fused_computation.22 | convolution fusion | flops 536870912 | bytes 5242884 | tf_op jit(solution)/shard_map/dot_general | solution.py:178
  189.8 7.8 %fusion.1 = f32[1024]{0:T(1024)S(1)} fusion(f32[1024,1024]{1,0:T(8,128)} %fusion.9, f32[1024,1024]{1,0:T(8,128)} %fusion.11, f32[1024,1024]{1,0:T(8,128)} %fusion.13, f32[1024,1024]{1,0:T(8,128)S(1)} %fusion.21, f32[1024,1024]{1,0:T(8,128)S(1)} %fusion.23, f32[1024,1024]{1,0:T(8,128)S(1)} %fusion.27, f32[1024,1024]{1,0:T(8,128)S(1)} %fusion.25, ...), kind=kOutput, calls=%fused_computation.3 | convolution fusion | flops 550501376 | bytes 32509956 | tf_op jit(solution)/shard_map/dot_general | solution.py:178
  198.6 2.6 %collective-permute-done.29 = f32[1024]{0:T(1024)S(1)} collective-permute-done((f32[1024]{0:T(1024)S(1)}, f32[1024]{0:T(1024)S(1)}, u32[]{:S(2)}, u32[]{:S(2)}) %collective-permute-start.29) | collective-permute-done | bytes 4128 | tf_op jit(solution)/shard_map/ppermute | solution.py:84
  201.8 3.0 %collective-permute-done.30 = f32[1024]{0:T(1024)S(1)} collective-permute-done((f32[1024]{0:T(1024)S(1)}, f32[1024]{0:T(1024)S(1)}, u32[]{:S(2)}, u32[]{:S(2)}) %collective-permute-start.30) | collective-permute-done | bytes 4128 | tf_op jit(solution)/shard_map/ppermute | solution.py:84
  204.9 5.7 %collective-permute-start.31 = (f32[1024]{0:T(1024)S(1)}, f32[1024]{0:T(1024)S(1)}, u32[]{:S(2)}, u32[]{:S(2)}) collective-permute-start(f32[1024]{0:T(1024)S(1)} %add.220), channel_id=1, source_target_pairs={{0,16},{4,20},{8,24},{12,28},{16,0},{20,4},{24,8},{28,12},{1,17},{... | collective-permute-start | bytes 12296 | tf_op jit(solution)/shard_map/ppermute | solution.py:84
  210.5 1.6 collective-permute-done.31
  (94 shorter events, 19.1 us)
Async XLA Ops:
  2.1 16.8 %collective-permute-start.7 = (bf16[256,1024]{1,0:T(8,128)(2,1)S(1)}, bf16[256,1024]{1,0:T(8,128)(2,1)S(1)}, u32[]{:S(2)}, u32[]{:S(2)}) collective-permute-start(bf16[256,1024]{1,0:T(8,128)(2,1)S(1)} %get-tuple-element.21), channel_id=1, source_target_pairs={{8,0},{12,4},{16,8},{20,12},{24,16},{28,20},{9,1},{13,5},{17,9},{2... | collective-permute-start | bytes 1572872 | tf_op jit(solution)/shard_map/ppermute | solution.py:104
  3.4 16.8 %collective-permute-start.8 = (bf16[256,1024]{1,0:T(8,128)(2,1)S(1)}, bf16[256,1024]{1,0:T(8,128)(2,1)S(1)}, u32[]{:S(2)}, u32[]{:S(2)}) collective-permute-start(bf16[256,1024]{1,0:T(8,128)(2,1)S(1)} %get-tuple-element.21), channel_id=1, source_target_pairs={{0,8},{4,12},{8,16},{12,20},{16,24},{20,28},{1,9},{5,13},{9,17},{1... | collective-permute-start | bytes 1572872 | tf_op jit(solution)/shard_map/ppermute | solution.py:104
  18.9 15.0 %collective-permute-start.11 = (bf16[256,1024]{1,0:T(8,128)(2,1)S(1)}, bf16[256,1024]{1,0:T(8,128)(2,1)S(1)}, u32[]{:S(2)}, u32[]{:S(2)}) collective-permute-start(bf16[256,1024]{1,0:T(8,128)(2,1)S(1)} %collective-permute-done.7), channel_id=1, source_target_pairs={{8,0},{12,4},{16,8},{20,12},{9,1},{13,5},{17,9},{21,13},{10,2},{14... | collective-permute-start | bytes 1572872 | tf_op jit(solution)/shard_map/ppermute | solution.py:104
  20.2 16.4 %collective-permute-start.9 = (bf16[256,1024]{1,0:T(8,128)(2,1)S(1)}, bf16[256,1024]{1,0:T(8,128)(2,1)S(1)}, u32[]{:S(2)}, u32[]{:S(2)}) collective-permute-start(bf16[256,1024]{1,0:T(8,128)(2,1)S(1)} %collective-permute-done.8), channel_id=1, source_target_pairs={{8,16},{12,20},{16,24},{20,28},{9,17},{13,21},{17,25},{21,29},{10,... | collective-permute-start | bytes 1572872 | tf_op jit(solution)/shard_map/ppermute | solution.py:104
  33.9 14.1 %collective-permute-start.12 = (bf16[256,1024]{1,0:T(8,128)(2,1)S(1)}, bf16[256,1024]{1,0:T(8,128)(2,1)S(1)}, u32[]{:S(2)}, u32[]{:S(2)}) collective-permute-start(bf16[256,1024]{1,0:T(8,128)(2,1)S(1)} %collective-permute-done.11), channel_id=1, source_target_pairs={{8,0},{12,4},{9,1},{13,5},{10,2},{14,6},{11,3},{15,7}} | collective-permute-start | bytes 1572872 | tf_op jit(solution)/shard_map/ppermute | solution.py:104
  35.2 23.8 %collective-permute-start = (bf16[512,1024]{1,0:T(8,128)(2,1)}, bf16[512,1024]{1,0:T(8,128)(2,1)}, u32[]{:S(2)}, u32[]{:S(2)}) collective-permute-start(bf16[512,1024]{1,0:T(8,128)(2,1)} %param.4), channel_id=1, source_target_pairs={{0,4},{4,0},{8,12},{12,8},{16,20},{20,16},{24,28},{28,24},{1,5},{5... | collective-permute-start | bytes 3145736 | tf_op jit(solution)/shard_map/ppermute | solution.py:135
  36.6 22.4 %copy-start.12 = (bf16[512,1024]{1,0:T(8,128)(2,1)S(1)}, bf16[512,1024]{1,0:T(8,128)(2,1)}, u32[]{:S(2)}) copy-start(bf16[512,1024]{1,0:T(8,128)(2,1)} %param.4) | copy-start | bytes 3145732
  36.6 22.4 %copy-start.17 = (f32[1024]{0:T(1024)S(1)}, f32[1024]{0:T(1024)}, u32[]{:S(2)}) copy-start(f32[1024]{0:T(1024)} %param.6) | copy-start | bytes 12292
  36.6 11.4 %collective-permute-start.10 = (bf16[256,1024]{1,0:T(8,128)(2,1)S(1)}, bf16[256,1024]{1,0:T(8,128)(2,1)S(1)}, u32[]{:S(2)}, u32[]{:S(2)}) collective-permute-start(bf16[256,1024]{1,0:T(8,128)(2,1)S(1)} %collective-permute-done.9), channel_id=1, source_target_pairs={{16,24},{20,28},{17,25},{21,29},{18,26},{22,30},{19,27},{23,31}} | collective-permute-start | bytes 1572872 | tf_op jit(solution)/shard_map/ppermute | solution.py:104
  48.3 34.4 %copy-start.2 = (bf16[1024,1024]{1,0:T(8,128)(2,1)}, bf16[1024,1024]{1,0:T(8,128)(2,1)S(1)}, u32[]{:S(2)}) copy-start(bf16[1024,1024]{1,0:T(8,128)(2,1)S(1)} %pad_maximum_fusion.2) | copy-start | bytes 6291460
  48.3 13.7 %copy-start.13 = (bf16[512,1024]{1,0:T(8,128)(2,1)S(1)}, bf16[512,1024]{1,0:T(8,128)(2,1)}, u32[]{:S(2)}) copy-start(bf16[512,1024]{1,0:T(8,128)(2,1)} %param.4) | copy-start | bytes 3145732
  62.0 3.5 %collective-permute-start.14 = (f32[1024,256]{1,0:T(8,128)}, f32[1024,256]{1,0:T(8,128)}, u32[]{:S(2)}, u32[]{:S(2)}) collective-permute-start(f32[1024,256]{1,0:T(8,128)} %fusion.29), channel_id=1, source_target_pairs={{0,1},{1,0},{2,3},{3,2},{4,5},{5,4},{6,7},{7,6},{8,9},{9,8},{10,11... | collective-permute-start | bytes 3145736 | tf_op jit(solution)/shard_map/ppermute | solution.py:152
  64.9 5.9 %collective-permute-start.13 = (f32[1024,256]{1,0:T(8,128)}, f32[1024,256]{1,0:T(8,128)}, u32[]{:S(2)}, u32[]{:S(2)}) collective-permute-start(f32[1024,256]{1,0:T(8,128)} %fusion.32), channel_id=1, source_target_pairs={{0,1},{1,0},{2,3},{3,2},{4,5},{5,4},{6,7},{7,6},{8,9},{9,8},{10,11... | collective-permute-start | bytes 3145736 | tf_op jit(solution)/shard_map/ppermute | solution.py:152
  68.5 14.1 %collective-permute-start.15 = (bf16[1024,256]{1,0:T(8,128)(2,1)}, bf16[1024,256]{1,0:T(8,128)(2,1)}, u32[]{:S(2)}, u32[]{:S(2)}) collective-permute-start(bf16[1024,256]{1,0:T(8,128)(2,1)} %fusion.4), channel_id=1, source_target_pairs={{0,2},{1,3},{2,0},{3,1},{4,6},{5,7},{6,4},{7,5},{8,10},{9,11},{10,... | collective-permute-start | bytes 1572872 | tf_op jit(solution)/shard_map/ppermute | solution.py:155
  69.6 27.0 %collective-permute-start.1 = (bf16[256,1024]{1,0:T(8,128)(2,1)}, bf16[256,1024]{1,0:T(8,128)(2,1)}, u32[]{:S(2)}, u32[]{:S(2)}) collective-permute-start(bf16[256,1024]{1,0:T(8,128)(2,1)} %get-tuple-element.22), channel_id=1, source_target_pairs={{8,0},{12,4},{16,8},{20,12},{24,16},{28,20},{9,1},{13,5},{17,9},{2... | collective-permute-start | bytes 1572872 | tf_op jit(solution)/shard_map/ppermute | solution.py:104
  86.9 13.3 %collective-permute-start.16 = (f32[512,256]{1,0:T(8,128)}, f32[512,256]{1,0:T(8,128)}, u32[]{:S(2)}, u32[]{:S(2)}) collective-permute-start(f32[512,256]{1,0:T(8,128)} %slice.54), channel_id=1, source_target_pairs={{0,4},{4,0},{8,12},{12,8},{16,20},{20,16},{24,28},{28,24},{1,5},{5... | collective-permute-start | bytes 1572872 | tf_op jit(solution)/shard_map/ppermute | solution.py:159
  88.0 14.9 %collective-permute-start.2 = (bf16[256,1024]{1,0:T(8,128)(2,1)}, bf16[256,1024]{1,0:T(8,128)(2,1)}, u32[]{:S(2)}, u32[]{:S(2)}) collective-permute-start(bf16[256,1024]{1,0:T(8,128)(2,1)} %get-tuple-element.22), channel_id=1, source_target_pairs={{0,8},{4,12},{8,16},{12,20},{16,24},{20,28},{1,9},{5,13},{9,17},{1... | collective-permute-start | bytes 1572872 | tf_op jit(solution)/shard_map/ppermute | solution.py:104
  96.6 14.5 %collective-permute-start.5 = (bf16[256,1024]{1,0:T(8,128)(2,1)}, bf16[256,1024]{1,0:T(8,128)(2,1)S(1)}, u32[]{:S(2)}, u32[]{:S(2)}) collective-permute-start(bf16[256,1024]{1,0:T(8,128)(2,1)} %collective-permute-done.1), channel_id=1, source_target_pairs={{8,0},{12,4},{16,8},{20,12},{9,1},{13,5},{17,9},{21,13},{10,2},{14... | collective-permute-start | bytes 1572872 | tf_op jit(solution)/shard_map/ppermute | solution.py:104
  101.7 6.5 %collective-permute-start.17 = (bf16[512,256]{1,0:T(8,128)(2,1)S(1)}, bf16[512,256]{1,0:T(8,128)(2,1)S(1)}, u32[]{:S(2)}, u32[]{:S(2)}) collective-permute-start(bf16[512,256]{1,0:T(8,128)(2,1)S(1)} %get-tuple-element.26), channel_id=1, source_target_pairs={{0,4},{4,0},{8,12},{12,8},{16,20},{20,16},{24,28},{28,24},{1,5},{5... | collective-permute-start | bytes 786440 | tf_op jit(solution)/shard_map/ppermute | solution.py:165
  102.9 9.5 %collective-permute-start.3 = (bf16[256,1024]{1,0:T(8,128)(2,1)}, bf16[256,1024]{1,0:T(8,128)(2,1)S(1)}, u32[]{:S(2)}, u32[]{:S(2)}) collective-permute-start(bf16[256,1024]{1,0:T(8,128)(2,1)} %collective-permute-done.2), channel_id=1, source_target_pairs={{8,16},{12,20},{16,24},{20,28},{9,17},{13,21},{17,25},{21,29},{10,... | collective-permute-start | bytes 1572872 | tf_op jit(solution)/shard_map/ppermute | solution.py:104
  108.3 18.6 %copy-start.4 = (bf16[1024,256]{1,0:T(8,128)(2,1)}, bf16[1024,256]{1,0:T(8,128)(2,1)S(1)}, u32[]{:S(2)}) copy-start(bf16[1024,256]{1,0:T(8,128)(2,1)S(1)} %pad_maximum_fusion.3) | copy-start | bytes 1572868
  108.3 18.6 %copy-start.14 = (bf16[512,1024]{1,0:T(8,128)(2,1)S(1)}, bf16[512,1024]{1,0:T(8,128)(2,1)}, u32[]{:S(2)}) copy-start(bf16[512,1024]{1,0:T(8,128)(2,1)} %param.4) | copy-start | bytes 3145732
  108.3 11.2 %collective-permute-start.18 = (bf16[1024,256]{1,0:T(8,128)(2,1)S(1)}, bf16[1024,256]{1,0:T(8,128)(2,1)S(1)}, u32[]{:S(2)}, u32[]{:S(2)}) collective-permute-start(bf16[1024,256]{1,0:T(8,128)(2,1)S(1)} %pad_maximum_fusion.3), channel_id=1, source_target_pairs={{0,2},{1,3},{2,0},{3,1},{4,6},{5,7},{6,4},{7,5},{8,10},{9,11},{10,... | collective-permute-start | bytes 1572872 | tf_op jit(solution)/shard_map/ppermute | solution.py:169
  111.1 13.4 %collective-permute-start.6 = (bf16[256,1024]{1,0:T(8,128)(2,1)S(1)}, bf16[256,1024]{1,0:T(8,128)(2,1)S(1)}, u32[]{:S(2)}, u32[]{:S(2)}) collective-permute-start(bf16[256,1024]{1,0:T(8,128)(2,1)S(1)} %collective-permute-done.5), channel_id=1, source_target_pairs={{8,0},{12,4},{9,1},{13,5},{10,2},{14,6},{11,3},{15,7}} | collective-permute-start | bytes 1572872 | tf_op jit(solution)/shard_map/ppermute | solution.py:104
  112.4 12.1 %collective-permute-start.4 = (bf16[256,1024]{1,0:T(8,128)(2,1)S(1)}, bf16[256,1024]{1,0:T(8,128)(2,1)S(1)}, u32[]{:S(2)}, u32[]{:S(2)}) collective-permute-start(bf16[256,1024]{1,0:T(8,128)(2,1)S(1)} %collective-permute-done.3), channel_id=1, source_target_pairs={{16,24},{20,28},{17,25},{21,29},{18,26},{22,30},{19,27},{23,31}} | collective-permute-start | bytes 1572872 | tf_op jit(solution)/shard_map/ppermute | solution.py:104
  113.4 13.6 %collective-permute-start.19 = (bf16[1024,256]{1,0:T(8,128)(2,1)S(1)}, bf16[1024,256]{1,0:T(8,128)(2,1)S(1)}, u32[]{:S(2)}, u32[]{:S(2)}) collective-permute-start(bf16[1024,256]{1,0:T(8,128)(2,1)S(1)} %pad_maximum_fusion.3), channel_id=1, source_target_pairs={{0,1},{1,0},{2,3},{3,2},{4,5},{5,4},{6,7},{7,6},{8,9},{9,8},{10,11... | collective-permute-start | bytes 1572872 | tf_op jit(solution)/shard_map/ppermute | solution.py:170
  119.5 10.2 %copy-start.8 = (bf16[1024,256]{1,0:T(8,128)(2,1)}, bf16[1024,256]{1,0:T(8,128)(2,1)S(1)}, u32[]{:S(2)}) copy-start(bf16[1024,256]{1,0:T(8,128)(2,1)S(1)} %collective-permute-done.18) | copy-start | bytes 1572868
  119.5 7.4 %collective-permute-start.20 = (bf16[1024,256]{1,0:T(8,128)(2,1)S(1)}, bf16[1024,256]{1,0:T(8,128)(2,1)S(1)}, u32[]{:S(2)}, u32[]{:S(2)}) collective-permute-start(bf16[1024,256]{1,0:T(8,128)(2,1)S(1)} %collective-permute-done.18), channel_id=1, source_target_pairs={{0,1},{1,0},{2,3},{3,2},{4,5},{5,4},{6,7},{7,6},{8,9},{9,8},{10,11... | collective-permute-start | bytes 1572872 | tf_op jit(solution)/shard_map/ppermute | solution.py:170
  126.9 23.4 %copy-start = (bf16[1024,1024]{1,0:T(8,128)(2,1)}, bf16[1024,1024]{1,0:T(8,128)(2,1)S(1)}, u32[]{:S(2)}) copy-start(bf16[1024,1024]{1,0:T(8,128)(2,1)S(1)} %pad_maximum_fusion.1) | copy-start | bytes 6291460
  126.9 5.9 %copy-start.6 = (bf16[1024,256]{1,0:T(8,128)(2,1)}, bf16[1024,256]{1,0:T(8,128)(2,1)S(1)}, u32[]{:S(2)}) copy-start(bf16[1024,256]{1,0:T(8,128)(2,1)S(1)} %collective-permute-done.19) | copy-start | bytes 1572868
  126.9 5.9 %copy-start.10 = (bf16[1024,256]{1,0:T(8,128)(2,1)}, bf16[1024,256]{1,0:T(8,128)(2,1)S(1)}, u32[]{:S(2)}) copy-start(bf16[1024,256]{1,0:T(8,128)(2,1)S(1)} %collective-permute-done.20) | copy-start | bytes 1572868
  129.8 3.6 %collective-permute-start.22 = (f32[1024,256]{1,0:T(8,128)S(1)}, f32[1024,256]{1,0:T(8,128)S(1)}, u32[]{:S(2)}, u32[]{:S(2)}) collective-permute-start(f32[1024,256]{1,0:T(8,128)S(1)} %fusion.15), channel_id=1, source_target_pairs={{0,1},{1,0},{2,3},{3,2},{4,5},{5,4},{6,7},{7,6},{8,9},{9,8},{10,11... | collective-permute-start | bytes 3145736 | tf_op jit(solution)/shard_map/ppermute | solution.py:152
  132.8 6.4 %collective-permute-start.21 = (f32[1024,256]{1,0:T(8,128)}, f32[1024,256]{1,0:T(8,128)}, u32[]{:S(2)}, u32[]{:S(2)}) collective-permute-start(f32[1024,256]{1,0:T(8,128)} %fusion.18), channel_id=1, source_target_pairs={{0,1},{1,0},{2,3},{3,2},{4,5},{5,4},{6,7},{7,6},{8,9},{9,8},{10,11... | collective-permute-start | bytes 3145736 | tf_op jit(solution)/shard_map/ppermute | solution.py:152
  136.2 14.2 %collective-permute-start.23 = (bf16[1024,256]{1,0:T(8,128)(2,1)}, bf16[1024,256]{1,0:T(8,128)(2,1)}, u32[]{:S(2)}, u32[]{:S(2)}) collective-permute-start(bf16[1024,256]{1,0:T(8,128)(2,1)} %fusion.5), channel_id=1, source_target_pairs={{0,2},{1,3},{2,0},{3,1},{4,6},{5,7},{6,4},{7,5},{8,10},{9,11},{10,... | collective-permute-start | bytes 1572872 | tf_op jit(solution)/shard_map/ppermute | solution.py:155
  139.2 15.0 %copy-start.3 = (bf16[1024,1024]{1,0:T(8,128)(2,1)S(1)}, bf16[1024,1024]{1,0:T(8,128)(2,1)}, u32[]{:S(2)}) copy-start(bf16[1024,1024]{1,0:T(8,128)(2,1)} %copy-done.2) | copy-start | bytes 6291460
  139.2 15.0 %copy-start.9 = (bf16[1024,256]{1,0:T(8,128)(2,1)S(1)}, bf16[1024,256]{1,0:T(8,128)(2,1)}, u32[]{:S(2)}) copy-start(bf16[1024,256]{1,0:T(8,128)(2,1)} %copy-done.8) | copy-start | bytes 1572868
  153.1 13.1 %collective-permute-start.24 = (f32[512,256]{1,0:T(8,128)S(1)}, f32[512,256]{1,0:T(8,128)S(1)}, u32[]{:S(2)}, u32[]{:S(2)}) collective-permute-start(f32[512,256]{1,0:T(8,128)S(1)} %slice.59), channel_id=1, source_target_pairs={{0,4},{4,0},{8,12},{12,8},{16,20},{20,16},{24,28},{28,24},{1,5},{5... | collective-permute-start | bytes 1572872 | tf_op jit(solution)/shard_map/ppermute | solution.py:159
  155.7 11.9 %copy-start.7 = (bf16[1024,256]{1,0:T(8,128)(2,1)S(1)}, bf16[1024,256]{1,0:T(8,128)(2,1)}, u32[]{:S(2)}) copy-start(bf16[1024,256]{1,0:T(8,128)(2,1)} %copy-done.6) | copy-start | bytes 1572868
  166.5 8.1 %copy-start.5 = (bf16[1024,256]{1,0:T(8,128)(2,1)S(1)}, bf16[1024,256]{1,0:T(8,128)(2,1)}, u32[]{:S(2)}) copy-start(bf16[1024,256]{1,0:T(8,128)(2,1)} %copy-done.4) | copy-start | bytes 1572868
  166.5 6.5 %collective-permute-start.25 = (bf16[512,256]{1,0:T(8,128)(2,1)S(1)}, bf16[512,256]{1,0:T(8,128)(2,1)S(1)}, u32[]{:S(2)}, u32[]{:S(2)}) collective-permute-start(bf16[512,256]{1,0:T(8,128)(2,1)S(1)} %get-tuple-element.24), channel_id=1, source_target_pairs={{0,4},{4,0},{8,12},{12,8},{16,20},{20,16},{24,28},{28,24},{1,5},{5... | collective-permute-start | bytes 786440 | tf_op jit(solution)/shard_map/ppermute | solution.py:165
  173.1 2.4 %copy-start.1 = (bf16[1024,1024]{1,0:T(8,128)(2,1)S(1)}, bf16[1024,1024]{1,0:T(8,128)(2,1)}, u32[]{:S(2)}) copy-start(bf16[1024,1024]{1,0:T(8,128)(2,1)} %copy-done) | copy-start | bytes 6291460
  173.1 11.2 %collective-permute-start.26 = (bf16[1024,256]{1,0:T(8,128)(2,1)S(1)}, bf16[1024,256]{1,0:T(8,128)(2,1)S(1)}, u32[]{:S(2)}, u32[]{:S(2)}) collective-permute-start(bf16[1024,256]{1,0:T(8,128)(2,1)S(1)} %pad_maximum_fusion.4), channel_id=1, source_target_pairs={{0,2},{1,3},{2,0},{3,1},{4,6},{5,7},{6,4},{7,5},{8,10},{9,11},{10,... | collective-permute-start | bytes 1572872 | tf_op jit(solution)/shard_map/ppermute | solution.py:169
  175.4 11.7 %collective-permute-start.27 = (bf16[1024,256]{1,0:T(8,128)(2,1)S(1)}, bf16[1024,256]{1,0:T(8,128)(2,1)S(1)}, u32[]{:S(2)}, u32[]{:S(2)}) collective-permute-start(bf16[1024,256]{1,0:T(8,128)(2,1)S(1)} %pad_maximum_fusion.4), channel_id=1, source_target_pairs={{0,1},{1,0},{2,3},{3,2},{4,5},{5,4},{6,7},{7,6},{8,9},{9,8},{10,11... | collective-permute-start | bytes 1572872 | tf_op jit(solution)/shard_map/ppermute | solution.py:170
  184.3 5.4 %collective-permute-start.28 = (bf16[1024,256]{1,0:T(8,128)(2,1)S(1)}, bf16[1024,256]{1,0:T(8,128)(2,1)}, u32[]{:S(2)}, u32[]{:S(2)}) collective-permute-start(bf16[1024,256]{1,0:T(8,128)(2,1)S(1)} %collective-permute-done.26), channel_id=1, source_target_pairs={{0,1},{1,0},{2,3},{3,2},{4,5},{5,4},{6,7},{7,6},{8,9},{9,8},{10,11... | collective-permute-start | bytes 1572872 | tf_op jit(solution)/shard_map/ppermute | solution.py:170
  187.1 2.7 %copy-start.15 = (bf16[512,1024]{1,0:T(8,128)(2,1)S(1)}, bf16[512,1024]{1,0:T(8,128)(2,1)}, u32[]{:S(2)}) copy-start(bf16[512,1024]{1,0:T(8,128)(2,1)} %param.4) | copy-start | bytes 3145732
  197.6 3.7 %collective-permute-start.29 = (f32[1024]{0:T(1024)S(1)}, f32[1024]{0:T(1024)S(1)}, u32[]{:S(2)}, u32[]{:S(2)}) collective-permute-start(f32[1024]{0:T(1024)S(1)} %fusion.1), channel_id=1, source_target_pairs={{0,4},{4,0},{8,12},{12,8},{16,20},{20,16},{24,28},{28,24},{1,5},{5... | collective-permute-start | bytes 12296 | tf_op jit(solution)/shard_map/ppermute | solution.py:84
  201.2 3.6 %collective-permute-start.30 = (f32[1024]{0:T(1024)S(1)}, f32[1024]{0:T(1024)S(1)}, u32[]{:S(2)}, u32[]{:S(2)}) collective-permute-start(f32[1024]{0:T(1024)S(1)} %add.219), channel_id=1, source_target_pairs={{0,8},{4,12},{8,0},{12,4},{16,24},{20,28},{24,16},{28,20},{1,9},{5... | collective-permute-start | bytes 12296 | tf_op jit(solution)/shard_map/ppermute | solution.py:84
  204.9 7.3 %collective-permute-start.31 = (f32[1024]{0:T(1024)S(1)}, f32[1024]{0:T(1024)S(1)}, u32[]{:S(2)}, u32[]{:S(2)}) collective-permute-start(f32[1024]{0:T(1024)S(1)} %add.220), channel_id=1, source_target_pairs={{0,16},{4,20},{8,24},{12,28},{16,0},{20,4},{24,8},{28,12},{1,17},{... | collective-permute-start | bytes 12296 | tf_op jit(solution)/shard_map/ppermute | solution.py:84
  (2 other events, 2.8 us)

commit v15 on v14

--- a/solution.py
+++ b/solution.py
@@ -5,7 +5,7 @@
 from jax import lax
 from jax.sharding import PartitionSpec as P
 
-CHUNKS = 2
+CHUNKS = 1
 
 
 def _rows(a, blk, n):

time: 214 us -> 209 us (0.977)
  waiting for transfers between devices: 115 us -> 142 us
  matrix products: 41.7 us -> 23.4 us
  starting transfers between devices: 40.8 us -> 24.5 us
  other arithmetic: 5.22 us -> 9.71 us
    ppermute x12 -> x6, waiting for transfers between devices: 40.1 us -> 64.6 us  [_zline(): cur = lax.ppermute(cur, 'src', pairs)]
    ppermute x1, waiting for transfers between devices: 10.7 us -> 0.01 us  [_fast(): lax.ppermute(forward_voxel_field, 'src', swap)]
    ppermute x2 -> x1, waiting for transfers between devices: 12.2 us -> 21.7 us  [_fast(): lax.ppermute(piece, 'vox', chip_perm(k))]
    dot_general x8 -> x4, matrix products: 18.9 us -> 9.37 us  [_fast(): back = back + jnp.dot(w, rows(col, blk), preferred_element_type=jnp.float32)]
    dot_general x8 -> x4, matrix products: 22.8 us -> 14 us  [pblock(): lax.dot_general(scaled, rows(col, blk), (((1,), (1,)), ((), ())), preferr...]
    ppermute x12 -> x6, starting transfers between devices: 21.5 us -> 12.8 us  [_zline(): cur = lax.ppermute(cur, 'src', pairs)]
    ppermute x2 -> x1, waiting for transfers between devices: 12.9 us -> 17.7 us  [_fast(): own, theirs = (share[:sl], lax.ppermute(share[sl:], 'src', swap))]
    slice x2 -> x0, local copies, waits for them, and re-layouts: 3.28 us -> none  [the longest x1 2.07 us: _fast(): nxt = _zline(adjoint_voxel_field[:r], na)]
  transfers between devices with their start and end apart: 32 -> 18, of which waited for: 17 -> 11; matrix products, arithmetic and copies ran while one was open for 17% -> 13% of each run, Pallas kernels for 0% -> 0%
where the time goes in v15:
time: 209 us
  waiting for transfers between devices  142 us (68%)
  starting transfers between devices  24.5 us (12%)
  matrix products  23.4 us (11%)
  other arithmetic  9.71 us (5%)
  local copies, waits for them, and re-layouts  9.09 us (4%)
    ppermute x6, waiting for transfers between devices, _zline(): cur = lax.ppermute(cur, 'src', pairs)  64.6 us
    ppermute x1, waiting for transfers between devices, _fast(): lax.ppermute(piece, 'vox', chip_perm(k))  21.7 us
    ppermute x1, waiting for transfers between devices, _fast(): lax.ppermute(halves[k].astype(jnp.bfloat16), 'vox', chip_perm(k))  20.3 us
    ppermute x1, waiting for transfers between devices, _fast(): own, theirs = (share[:sl], lax.ppermute(share[sl:], 'src', swap))  17.7 us
    dot_general x4, matrix products, pblock(): lax.dot_general(scaled, rows(col, blk), (((1,), (1,)), ((), ())), preferr...  14 us
    ppermute x6, starting transfers between devices, _zline(): cur = lax.ppermute(cur, 'src', pairs)  12.8 us
    ppermute x1, waiting for transfers between devices, _fast(): piece = jnp.concatenate([mine, lax.ppermute(other, 'src', swap)], axis=0)  11.2 us
    dot_general x4, matrix products, _fast(): back = back + jnp.dot(w, rows(col, blk), preferred_element_type=jnp.float32)  9.37 us
  transfers between devices with their start and end apart: 18, of which 11 were waited for; matrix products, arithmetic and copies ran while one was open for 13% of the time, Pallas kernels for 0%

profile of v15, /device:TPU:0, one launch (start us, length us, event | category | flops | bytes accessed | tf_op | source)
XLA Modules:
  0.0 208.9 jit_solution(4608123317794780330)
XLA Ops:
  0.0 1.3 collective-permute-start.1
  1.3 5.6 %collective-permute-start.2 = (bf16[512,1024]{1,0:T(8,128)(2,1)}, bf16[512,1024]{1,0:T(8,128)(2,1)S(1)}, u32[]{:S(2)}, u32[]{:S(2)}) collective-permute-start(bf16[512,1024]{1,0:T(8,128)(2,1)} %param.5), channel_id=1, source_target_pairs={{0,8},{4,12},{8,16},{12,20},{16,24},{20,28},{1,9},{5,13},{9,17},{1... | collective-permute-start | bytes 3145736 | tf_op jit(solution)/shard_map/ppermute | solution.py:104
  6.9 21.4 %collective-permute-done.1 = bf16[512,1024]{1,0:T(8,128)(2,1)S(1)} collective-permute-done((bf16[512,1024]{1,0:T(8,128)(2,1)}, bf16[512,1024]{1,0:T(8,128)(2,1)S(1)}, u32[]{:S(2)}, u32[]{:S(2)}) %collective-permute-start.1) | collective-permute-done | bytes 1048608 | tf_op jit(solution)/shard_map/ppermute | solution.py:104
  28.3 1.3 collective-permute-start.5
  29.6 1.7 collective-permute-start.3
  31.3 23.3 %collective-permute-done.5 = bf16[512,1024]{1,0:T(8,128)(2,1)} collective-permute-done((bf16[512,1024]{1,0:T(8,128)(2,1)S(1)}, bf16[512,1024]{1,0:T(8,128)(2,1)}, u32[]{:S(2)}, u32[]{:S(2)}) %collective-permute-start.5) | collective-permute-done | bytes 1048608 | tf_op jit(solution)/shard_map/ppermute | solution.py:104
  54.6 1.3 collective-permute-start.6
  55.9 1.7 collective-permute-start.4
  57.6 1.4 collective-permute-start
  58.9 1.4 broadcast_select_fusion.1
  60.4 19.9 %collective-permute-done.6 = bf16[512,1024]{1,0:T(8,128)(2,1)} collective-permute-done((bf16[512,1024]{1,0:T(8,128)(2,1)}, bf16[512,1024]{1,0:T(8,128)(2,1)}, u32[]{:S(2)}, u32[]{:S(2)}) %collective-permute-start.6) | collective-permute-done | bytes 1048608 | tf_op jit(solution)/shard_map/ppermute | solution.py:104
  80.2 1.3 broadcast_select_fusion
  81.6 0.1 broadcast_select_fusion.2
  81.8 0.5 pad_maximum_fusion
  82.3 0.6 copy-done.4
  83.0 2.7 %fusion.10 = f32[1024,512]{1,0:T(8,128)} fusion(bf16[2048,1024]{1,0:T(8,128)(2,1)S(1)} %pad_maximum_fusion, s32[]{:T(128)S(6)} %select_n.162, f32[1024]{0:T(1024)S(1)} %copy-done.8, bf16[512,1024]{1,0:T(8,128)(2,1)S(1)} %collective-permute-done, bf16[512,1024]{1,0:T(8,128)(2,1)S(1)} %copy-done.4), kind=kOutput, calls=%fused_computation.20 | convolution fusion | flops 1080033280 | bytes 5246980 | tf_op jit(solution)/shard_map/dot_general | solution.py:145
  85.7 3.9 %fusion.13 = f32[1024,512]{1,0:T(8,128)} fusion(bf16[2048,1024]{1,0:T(8,128)(2,1)} %copy-done, s32[]{:T(128)S(6)} %select_n.157, f32[1024]{0:T(1024)S(1)} %copy-done.8, bf16[512,1024]{1,0:T(8,128)(2,1)S(1)} %collective-permute-done, bf16[512,1024]{1,0:T(8,128)(2,1)S(1)} %copy-done.4), kind=kOutput, calls=%fused_computation.23 | convolution fusion | flops 1080033280 | bytes 5246980 | tf_op jit(solution)/shard_map/dot_general | solution.py:145
  89.5 0.5 collective-permute-start.7
  90.0 0.1 collective-permute-done.8
  90.2 4.6 %add_convert_fusion = bf16[1024,512]{1,0:T(8,128)(2,1)} fusion(f32[1024,512]{1,0:T(8,128)} %collective-permute-done.8, bf16[2048,1024]{1,0:T(8,128)(2,1)} %copy-done, s32[]{:T(128)S(6)} %select_n.160, f32[1024]{0:T(1024)S(1)} %copy-done.8, bf16[512,1024]{1,0:T(8,128)(2,1)} %copy-done.5, bf16[512,1024]{1,0:T(8,128)(2,1)S(1)} %copy-done.4), kind=kOutput, calls=%fused_computation.9 | convolution fusion | flops 1081081856 | bytes 6295556 | tf_op jit(solution)/shard_map/dot_general | solution.py:145
  94.8 1.0 collective-permute-start.9
  95.8 2.8 %fusion.15 = f32[1024,512]{1,0:T(8,128)S(1)} fusion(bf16[2048,1024]{1,0:T(8,128)(2,1)} %copy-done, s32[]{:T(128)S(6)} %select_n.155, f32[1024]{0:T(1024)S(1)} %copy-done.8, bf16[512,1024]{1,0:T(8,128)(2,1)} %copy-done.5, bf16[512,1024]{1,0:T(8,128)(2,1)S(1)} %copy-done.4), kind=kOutput, calls=%fused_computation.25 | convolution fusion | flops 1080033280 | bytes 5246980 | tf_op jit(solution)/shard_map/dot_general | solution.py:145
  98.6 1.4 copy-done.3
  100.0 20.3 %collective-permute-done.9 = bf16[1024,512]{1,0:T(8,128)(2,1)} collective-permute-done((bf16[1024,512]{1,0:T(8,128)(2,1)}, bf16[1024,512]{1,0:T(8,128)(2,1)}, u32[]{:S(2)}, u32[]{:S(2)}) %collective-permute-start.9) | collective-permute-done | bytes 1048608 | tf_op jit(solution)/shard_map/ppermute | solution.py:155
  120.3 2.6 %convert_add_fusion = f32[1024,512]{1,0:T(8,128)S(1)} fusion(bf16[1024,512]{1,0:T(8,128)(2,1)} %collective-permute-done.9, f32[1024,512]{1,0:T(8,128)S(1)} %fusion.15, f32[1024,512]{1,0:T(8,128)} %copy-done.3), kind=kLoop, calls=%fused_computation.8 | loop fusion | flops 1572864 | bytes 7340032 | tf_op jit(solution)/shard_map/add | solution.py:155
  122.8 1.1 slice.19
  124.0 1.0 collective-permute-start.10
  125.0 3.0 %copy.5 = f32[512,1024]{0,1:T(8,128)} copy(f32[512,1024]{1,0:T(8,128)} %param.7) | data formatting | bytes 4194304 | tf_op args[3]
  128.0 2.9 %copy.6 = f32[512,2,512]{2,0,1:T(8,128)} copy(f32[512,2,512]{0,2,1:T(8,128)} %bitcast.12) | data formatting | bytes 4194304 | tf_op jit(solution)/shard_map/reshape | solution.py:138
  130.9 17.7 %collective-permute-done.10 = f32[512,512]{1,0:T(8,128)} collective-permute-done((f32[512,512]{1,0:T(8,128)}, f32[512,512]{1,0:T(8,128)}, u32[]{:S(2)}, u32[]{:S(2)}) %collective-permute-start.10) | collective-permute-done | bytes 1048608 | tf_op jit(solution)/shard_map/ppermute | solution.py:159
  148.7 1.4 select_bitcast_fusion.1
  150.1 0.6 fusion.2
  150.8 1.1 collective-permute-start.11
  151.9 11.2 %collective-permute-done.11 = bf16[512,512]{1,0:T(8,128)(2,1)S(1)} collective-permute-done((bf16[512,512]{1,0:T(8,128)(2,1)S(1)}, bf16[512,512]{1,0:T(8,128)(2,1)S(1)}, u32[]{:S(2)}, u32[]{:S(2)}) %collective-permute-start.11) | collective-permute-done | bytes 524320 | tf_op jit(solution)/shard_map/ppermute | solution.py:165
  163.1 1.0 pad_maximum_fusion.2
  164.1 1.0 collective-permute-start.12
  165.1 21.7 %collective-permute-done.12 = bf16[1024,512]{1,0:T(8,128)(2,1)S(1)} collective-permute-done((bf16[1024,512]{1,0:T(8,128)(2,1)}, bf16[1024,512]{1,0:T(8,128)(2,1)S(1)}, u32[]{:S(2)}, u32[]{:S(2)}) %collective-permute-start.12) | collective-permute-done | bytes 1048608 | tf_op jit(solution)/shard_map/ppermute | solution.py:169
  186.9 2.6 %fusion.8 = f32[1024,1024]{1,0:T(8,128)S(1)} fusion(bf16[2048,1024]{1,0:T(8,128)(2,1)} %copy-done, s32[]{:T(128)S(6)} %select_n.170, bf16[512,512]{1,0:T(8,128)(2,1)S(1)} %collective-permute-done.11, bf16[512,512]{1,0:T(8,128)(2,1)S(1)} %get-tuple-element.7), kind=kOutput, calls=%fused_computation.16 | convolution fusion | flops 1075838976 | bytes 6291460 | tf_op jit(solution)/shard_map/dot_general | solution.py:178
  189.5 1.3 fusion.6
  190.8 2.6 %fusion.4 = f32[1024,1024]{1,0:T(8,128)S(1)} fusion(bf16[1024,512]{1,0:T(8,128)(2,1)} %collective-permute-done.13, bf16[2048,1024]{1,0:T(8,128)(2,1)S(1)} %copy-done.1, s32[]{:T(128)S(6)} %select_n.175), kind=kOutput, calls=%fused_computation.12 | convolution fusion | flops 1073741824 | bytes 6291460 | tf_op jit(solution)/shard_map/dot_general | solution.py:178
  193.4 2.9 %fusion.1 = f32[1024]{0:T(1024)S(1)} fusion(f32[1024,1024]{1,0:T(8,128)S(1)} %fusion.4, f32[1024,1024]{1,0:T(8,128)S(1)} %fusion.8, f32[1024,1024]{1,0:T(8,128)S(1)} %fusion.6, bf16[1024,512]{1,0:T(8,128)(2,1)} %collective-permute-done.14, bf16[512,1024]{1,0:T(8,128)(2,1)S(1)} %copy-done.6, bf16[512,1024]{1,0:T(8,128)(2,1)S(1)} %copy-done.4, ...), kind=kOutput, calls=%fused_computation.3 | convolution fusion | flops 1083177984 | bytes 16781316 | tf_op jit(solution)/shard_map/dot_general | solution.py:178
  196.3 1.0 collective-permute-start.15
  197.4 2.6 %collective-permute-done.15 = f32[1024]{0:T(1024)S(1)} collective-permute-done((f32[1024]{0:T(1024)S(1)}, f32[1024]{0:T(1024)S(1)}, u32[]{:S(2)}, u32[]{:S(2)}) %collective-permute-start.15) | collective-permute-done | bytes 4128 | tf_op jit(solution)/shard_map/ppermute | solution.py:84
  200.0 1.5 collective-permute-start.16
  201.5 2.1 collective-permute-done.16
  203.6 3.1 %collective-permute-start.17 = (f32[1024]{0:T(1024)S(1)}, f32[1024]{0:T(1024)S(1)}, u32[]{:S(2)}, u32[]{:S(2)}) collective-permute-start(f32[1024]{0:T(1024)S(1)} %add.161), channel_id=1, source_target_pairs={{0,16},{4,20},{8,24},{12,28},{16,0},{20,4},{24,8},{28,12},{1,17},{... | collective-permute-start | bytes 12296 | tf_op jit(solution)/shard_map/ppermute | solution.py:84
  206.7 1.6 collective-permute-done.17
  208.3 0.6 add.162
  (29 shorter events, 0.1 us)
Async XLA Ops:
  0.0 28.3 %collective-permute-start.1 = (bf16[512,1024]{1,0:T(8,128)(2,1)}, bf16[512,1024]{1,0:T(8,128)(2,1)S(1)}, u32[]{:S(2)}, u32[]{:S(2)}) collective-permute-start(bf16[512,1024]{1,0:T(8,128)(2,1)} %param.5), channel_id=1, source_target_pairs={{8,0},{12,4},{16,8},{20,12},{24,16},{28,20},{9,1},{13,5},{17,9},{2... | collective-permute-start | bytes 3145736 | tf_op jit(solution)/shard_map/ppermute | solution.py:104
  1.3 28.3 %collective-permute-start.2 = (bf16[512,1024]{1,0:T(8,128)(2,1)}, bf16[512,1024]{1,0:T(8,128)(2,1)S(1)}, u32[]{:S(2)}, u32[]{:S(2)}) collective-permute-start(bf16[512,1024]{1,0:T(8,128)(2,1)} %param.5), channel_id=1, source_target_pairs={{0,8},{4,12},{8,16},{12,20},{16,24},{20,28},{1,9},{5,13},{9,17},{1... | collective-permute-start | bytes 3145736 | tf_op jit(solution)/shard_map/ppermute | solution.py:104
  28.3 26.3 %collective-permute-start.5 = (bf16[512,1024]{1,0:T(8,128)(2,1)S(1)}, bf16[512,1024]{1,0:T(8,128)(2,1)}, u32[]{:S(2)}, u32[]{:S(2)}) collective-permute-start(bf16[512,1024]{1,0:T(8,128)(2,1)S(1)} %collective-permute-done.1), channel_id=1, source_target_pairs={{8,0},{12,4},{16,8},{20,12},{9,1},{13,5},{17,9},{21,13},{10,2},{14... | collective-permute-start | bytes 3145736 | tf_op jit(solution)/shard_map/ppermute | solution.py:104
  29.6 26.3 %collective-permute-start.3 = (bf16[512,1024]{1,0:T(8,128)(2,1)S(1)}, bf16[512,1024]{1,0:T(8,128)(2,1)}, u32[]{:S(2)}, u32[]{:S(2)}) collective-permute-start(bf16[512,1024]{1,0:T(8,128)(2,1)S(1)} %collective-permute-done.2), channel_id=1, source_target_pairs={{8,16},{12,20},{16,24},{20,28},{9,17},{13,21},{17,25},{21,29},{10,... | collective-permute-start | bytes 3145736 | tf_op jit(solution)/shard_map/ppermute | solution.py:104
  54.6 25.6 %collective-permute-start.6 = (bf16[512,1024]{1,0:T(8,128)(2,1)}, bf16[512,1024]{1,0:T(8,128)(2,1)}, u32[]{:S(2)}, u32[]{:S(2)}) collective-permute-start(bf16[512,1024]{1,0:T(8,128)(2,1)} %collective-permute-done.5), channel_id=1, source_target_pairs={{8,0},{12,4},{9,1},{13,5},{10,2},{14,6},{11,3},{15,7}} | collective-permute-start | bytes 3145736 | tf_op jit(solution)/shard_map/ppermute | solution.py:104
  55.9 25.7 %collective-permute-start.4 = (bf16[512,1024]{1,0:T(8,128)(2,1)}, bf16[512,1024]{1,0:T(8,128)(2,1)}, u32[]{:S(2)}, u32[]{:S(2)}) collective-permute-start(bf16[512,1024]{1,0:T(8,128)(2,1)} %collective-permute-done.3), channel_id=1, source_target_pairs={{16,24},{20,28},{17,25},{21,29},{18,26},{22,30},{19,27},{23,31}} | collective-permute-start | bytes 3145736 | tf_op jit(solution)/shard_map/ppermute | solution.py:104
  57.6 24.7 %collective-permute-start = (bf16[512,1024]{1,0:T(8,128)(2,1)}, bf16[512,1024]{1,0:T(8,128)(2,1)S(1)}, u32[]{:S(2)}, u32[]{:S(2)}) collective-permute-start(bf16[512,1024]{1,0:T(8,128)(2,1)} %param.4), channel_id=1, source_target_pairs={{0,4},{4,0},{8,12},{12,8},{16,20},{20,16},{24,28},{28,24},{1,5},{5... | collective-permute-start | bytes 3145736 | tf_op jit(solution)/shard_map/ppermute | solution.py:135
  58.9 22.8 %copy-start.7 = (bf16[512,1024]{1,0:T(8,128)(2,1)S(1)}, bf16[512,1024]{1,0:T(8,128)(2,1)}, u32[]{:S(2)}) copy-start(bf16[512,1024]{1,0:T(8,128)(2,1)} %param.5) | copy-start | bytes 3145732
  81.7 1.2 copy-start.4
  81.7 1.2 copy-start.8
  82.3 3.4 %copy-start = (bf16[2048,1024]{1,0:T(8,128)(2,1)}, bf16[2048,1024]{1,0:T(8,128)(2,1)S(1)}, u32[]{:S(2)}) copy-start(bf16[2048,1024]{1,0:T(8,128)(2,1)S(1)} %pad_maximum_fusion) | copy-start | bytes 12582916
  83.0 2.7 %copy-start.5 = (bf16[512,1024]{1,0:T(8,128)(2,1)}, bf16[512,1024]{1,0:T(8,128)(2,1)S(1)}, u32[]{:S(2)}) copy-start(bf16[512,1024]{1,0:T(8,128)(2,1)S(1)} %collective-permute-done) | copy-start | bytes 3145732
  85.7 4.5 %collective-permute-start.8 = (f32[1024,512]{1,0:T(8,128)}, f32[1024,512]{1,0:T(8,128)}, u32[]{:S(2)}, u32[]{:S(2)}) collective-permute-start(f32[1024,512]{1,0:T(8,128)} %fusion.10), channel_id=1, source_target_pairs={{0,1},{1,0},{2,3},{3,2},{4,5},{5,4},{6,7},{7,6},{8,9},{9,8},{10,11... | collective-permute-start | bytes 6291464 | tf_op jit(solution)/shard_map/ppermute | solution.py:152
  89.5 9.1 %collective-permute-start.7 = (f32[1024,512]{1,0:T(8,128)}, f32[1024,512]{1,0:T(8,128)S(1)}, u32[]{:S(2)}, u32[]{:S(2)}) collective-permute-start(f32[1024,512]{1,0:T(8,128)} %fusion.13), channel_id=1, source_target_pairs={{0,1},{1,0},{2,3},{3,2},{4,5},{5,4},{6,7},{7,6},{8,9},{9,8},{10,11... | collective-permute-start | bytes 6291464 | tf_op jit(solution)/shard_map/ppermute | solution.py:152
  94.8 25.5 %collective-permute-start.9 = (bf16[1024,512]{1,0:T(8,128)(2,1)}, bf16[1024,512]{1,0:T(8,128)(2,1)}, u32[]{:S(2)}, u32[]{:S(2)}) collective-permute-start(bf16[1024,512]{1,0:T(8,128)(2,1)} %add_convert_fusion), channel_id=1, source_target_pairs={{0,2},{1,3},{2,0},{3,1},{4,6},{5,7},{6,4},{7,5},{8,10},{9,11},{10,... | collective-permute-start | bytes 3145736 | tf_op jit(solution)/shard_map/ppermute | solution.py:155
  98.6 1.4 copy-start.3
  124.0 24.7 %collective-permute-start.10 = (f32[512,512]{1,0:T(8,128)}, f32[512,512]{1,0:T(8,128)}, u32[]{:S(2)}, u32[]{:S(2)}) collective-permute-start(f32[512,512]{1,0:T(8,128)} %slice.19), channel_id=1, source_target_pairs={{0,4},{4,0},{8,12},{12,8},{16,20},{20,16},{24,28},{28,24},{1,5},{5... | collective-permute-start | bytes 3145736 | tf_op jit(solution)/shard_map/ppermute | solution.py:159
  130.9 19.2 %copy-start.2 = (f32[512,2,512]{2,0,1:T(8,128)S(1)}, f32[512,2,512]{2,0,1:T(8,128)}, u32[]{:S(2)}) copy-start(f32[512,2,512]{2,0,1:T(8,128)} %copy.6) | copy-start | bytes 6291460
  150.8 12.3 %collective-permute-start.11 = (bf16[512,512]{1,0:T(8,128)(2,1)S(1)}, bf16[512,512]{1,0:T(8,128)(2,1)S(1)}, u32[]{:S(2)}, u32[]{:S(2)}) collective-permute-start(bf16[512,512]{1,0:T(8,128)(2,1)S(1)} %get-tuple-element.8), channel_id=1, source_target_pairs={{0,4},{4,0},{8,12},{12,8},{16,20},{20,16},{24,28},{28,24},{1,5},{5... | collective-permute-start | bytes 1572872 | tf_op jit(solution)/shard_map/ppermute | solution.py:165
  164.1 22.7 %collective-permute-start.12 = (bf16[1024,512]{1,0:T(8,128)(2,1)}, bf16[1024,512]{1,0:T(8,128)(2,1)S(1)}, u32[]{:S(2)}, u32[]{:S(2)}) collective-permute-start(bf16[1024,512]{1,0:T(8,128)(2,1)} %pad_maximum_fusion.2), channel_id=1, source_target_pairs={{0,2},{1,3},{2,0},{3,1},{4,6},{5,7},{6,4},{7,5},{8,10},{9,11},{10,... | collective-permute-start | bytes 3145736 | tf_op jit(solution)/shard_map/ppermute | solution.py:169
  165.1 25.7 %collective-permute-start.13 = (bf16[1024,512]{1,0:T(8,128)(2,1)}, bf16[1024,512]{1,0:T(8,128)(2,1)}, u32[]{:S(2)}, u32[]{:S(2)}) collective-permute-start(bf16[1024,512]{1,0:T(8,128)(2,1)} %pad_maximum_fusion.2), channel_id=1, source_target_pairs={{0,1},{1,0},{2,3},{3,2},{4,5},{5,4},{6,7},{7,6},{8,9},{9,8},{10,11... | collective-permute-start | bytes 3145736 | tf_op jit(solution)/shard_map/ppermute | solution.py:170
  186.9 6.5 %collective-permute-start.14 = (bf16[1024,512]{1,0:T(8,128)(2,1)S(1)}, bf16[1024,512]{1,0:T(8,128)(2,1)}, u32[]{:S(2)}, u32[]{:S(2)}) collective-permute-start(bf16[1024,512]{1,0:T(8,128)(2,1)S(1)} %collective-permute-done.12), channel_id=1, source_target_pairs={{0,1},{1,0},{2,3},{3,2},{4,5},{5,4},{6,7},{7,6},{8,9},{9,8},{10,11... | collective-permute-start | bytes 3145736 | tf_op jit(solution)/shard_map/ppermute | solution.py:170
  186.9 2.6 %copy-start.1 = (bf16[2048,1024]{1,0:T(8,128)(2,1)S(1)}, bf16[2048,1024]{1,0:T(8,128)(2,1)}, u32[]{:S(2)}) copy-start(bf16[2048,1024]{1,0:T(8,128)(2,1)} %copy-done) | copy-start | bytes 12582916
  190.8 2.6 %copy-start.6 = (bf16[512,1024]{1,0:T(8,128)(2,1)S(1)}, bf16[512,1024]{1,0:T(8,128)(2,1)}, u32[]{:S(2)}) copy-start(bf16[512,1024]{1,0:T(8,128)(2,1)} %copy-done.5) | copy-start | bytes 3145732
  196.3 3.7 %collective-permute-start.15 = (f32[1024]{0:T(1024)S(1)}, f32[1024]{0:T(1024)S(1)}, u32[]{:S(2)}, u32[]{:S(2)}) collective-permute-start(f32[1024]{0:T(1024)S(1)} %fusion.1), channel_id=1, source_target_pairs={{0,4},{4,0},{8,12},{12,8},{16,20},{20,16},{24,28},{28,24},{1,5},{5... | collective-permute-start | bytes 12296 | tf_op jit(solution)/shard_map/ppermute | solution.py:84
  200.0 3.6 %collective-permute-start.16 = (f32[1024]{0:T(1024)S(1)}, f32[1024]{0:T(1024)S(1)}, u32[]{:S(2)}, u32[]{:S(2)}) collective-permute-start(f32[1024]{0:T(1024)S(1)} %add.160), channel_id=1, source_target_pairs={{0,8},{4,12},{8,0},{12,4},{16,24},{20,28},{24,16},{28,20},{1,9},{5... | collective-permute-start | bytes 12296 | tf_op jit(solution)/shard_map/ppermute | solution.py:84
  203.6 4.7 %collective-permute-start.17 = (f32[1024]{0:T(1024)S(1)}, f32[1024]{0:T(1024)S(1)}, u32[]{:S(2)}, u32[]{:S(2)}) collective-permute-start(f32[1024]{0:T(1024)S(1)} %add.161), channel_id=1, source_target_pairs={{0,16},{4,20},{8,24},{12,28},{16,0},{20,4},{24,8},{28,12},{1,17},{... | collective-permute-start | bytes 12296 | tf_op jit(solution)/shard_map/ppermute | solution.py:84

commit v16 on v8

--- a/solution.py
+++ b/solution.py
@@ -104,8 +104,8 @@
     def chip_perm(k):
         return [(g * 2 + p, ((g + k) % m) * 2 + p) for g in range(m) for p in range(2)]
 
-    scaled = (forward_voxel_field.astype(jnp.float32) * voxel_input_vector[None, :]).astype(
-        jnp.bfloat16
+    scaled = lax.optimization_barrier(
+        (forward_voxel_field.astype(jnp.float32) * voxel_input_vector[None, :]).astype(jnp.bfloat16)
     )
     weight = measurement_weight.reshape(sl, t, ds)
     if grid is not None and grid[0] == t:

time: 208 us -> 210 us (level)
  other arithmetic: 10.9 us -> 13.7 us
  transfers between devices with their start and end apart: 29 -> 29, of which waited for: 15 -> 15; matrix products, arithmetic and copies ran while one was open for 15% -> 17% of each run, Pallas kernels for 0% -> 0%
where the time goes in v16:
time: 210 us; the launch traced here: 209 us
  waiting for transfers between devices  129 us (61%)
  starting transfers between devices  33 us (16%)
  matrix products  22.3 us (11%)
  other arithmetic  13.7 us (7%)
  local copies, waits for them, and re-layouts  9.95 us (5%)
    ppermute x12, waiting for transfers between devices, _gather_src(): cur = lax.ppermute(cur, 'src', pairs)  48.1 us
    ppermute x2, waiting for transfers between devices, _gather_src(): other = lax.ppermute(col, 'src', swap)  28.9 us
    ppermute x2, waiting for transfers between devices, per_device(): got.append((2 * ((q - k) % m) + par, lax.ppermute(wt, 'vox', chip_perm(k))))  22.9 us
    ppermute x12, starting transfers between devices, _gather_src(): cur = lax.ppermute(cur, 'src', pairs)  22.9 us
    ppermute x2, waiting for transfers between devices, per_device(): lax.ppermute(halves[k].astype(jnp.bfloat16), 'vox', chip_perm(k))  20.1 us
    dot_general x8, matrix products, pblock(): lax.dot_general(scaled, _rows(adj, rel(blk), n), (((1,), (1,)), ((), ()))...  16 us
    ppermute x3, waiting for transfers between devices, _sum_over_src(): v = v + lax.ppermute(v, 'src', [(i, i ^ b) for i in range(n)])  8.7 us
    another operation x8, other arithmetic, _gather_src(): col = jnp.stack(col)  6.98 us
  transfers between devices with their start and end apart: 29, of which 15 were waited for; matrix products, arithmetic and copies ran while one was open for 17% of the time, Pallas kernels for 0%

profile of v16, /device:TPU:0, one launch (start us, length us, event | category | flops | bytes accessed | tf_op | source)
XLA Modules:
  0.0 208.8 jit_solution(13793853305523347621)
XLA Ops:
  0.0 2.3 %slice_bitcast_fusion = (bf16[1,256,1024]{2,1,0:T(8,128)(2,1)S(1)}, bf16[1,256,1024]{2,1,0:T(8,128)(2,1)S(1)}, bf16[256,1024]{1,0:T(8,128)(2,1)S(1)}, bf16[256,1024]{1,0:T(8,128)(2,1)}) fusion(bf16[512,1024]{1,0:T(8,128)(2,1)} %param.5), kind=kLoop, calls=%fused_computation.73 | loop fusion | bytes 3145728 | tf_op jit(solution)/shard_map/stack | solution.py:71
  2.3 1.3 collective-permute-start.7
  3.6 5.6 %collective-permute-start.8 = (bf16[256,1024]{1,0:T(8,128)(2,1)S(1)}, bf16[256,1024]{1,0:T(8,128)(2,1)S(1)}, u32[]{:S(2)}, u32[]{:S(2)}) collective-permute-start(bf16[256,1024]{1,0:T(8,128)(2,1)S(1)} %get-tuple-element.23), channel_id=1, source_target_pairs={{0,8},{4,12},{8,16},{12,20},{16,24},{20,28},{1,9},{5,13},{9,17},{1... | collective-permute-start | bytes 1572872 | tf_op jit(solution)/shard_map/ppermute | solution.py:66
  9.2 10.0 %collective-permute-done.7 = bf16[256,1024]{1,0:T(8,128)(2,1)S(1)} collective-permute-done((bf16[256,1024]{1,0:T(8,128)(2,1)S(1)}, bf16[256,1024]{1,0:T(8,128)(2,1)S(1)}, u32[]{:S(2)}, u32[]{:S(2)}) %collective-permute-start.7) | collective-permute-done | bytes 524320 | tf_op jit(solution)/shard_map/ppermute | solution.py:66
  19.1 1.3 collective-permute-start.11
  20.4 1.5 collective-permute-start.9
  21.9 12.2 %collective-permute-done.11 = bf16[256,1024]{1,0:T(8,128)(2,1)S(1)} collective-permute-done((bf16[256,1024]{1,0:T(8,128)(2,1)S(1)}, bf16[256,1024]{1,0:T(8,128)(2,1)S(1)}, u32[]{:S(2)}, u32[]{:S(2)}) %collective-permute-start.11) | collective-permute-done | bytes 524320 | tf_op jit(solution)/shard_map/ppermute | solution.py:66
  34.1 1.3 collective-permute-start.12
  36.2 12.1 %collective-permute-done.12 = bf16[256,1024]{1,0:T(8,128)(2,1)} collective-permute-done((bf16[256,1024]{1,0:T(8,128)(2,1)S(1)}, bf16[256,1024]{1,0:T(8,128)(2,1)}, u32[]{:S(2)}, u32[]{:S(2)}) %collective-permute-start.12) | collective-permute-done | bytes 524320 | tf_op jit(solution)/shard_map/ppermute | solution.py:66
  48.3 1.1 select_bitcast_fusion.4
  49.5 1.6 pad_maximum_fusion.3
  51.1 1.0 collective-permute-start.13
  52.2 1.3 collective-permute-start
  53.4 5.4 %collective-permute-start.1 = (bf16[256,1024]{1,0:T(8,128)(2,1)S(1)}, bf16[256,1024]{1,0:T(8,128)(2,1)}, u32[]{:S(2)}, u32[]{:S(2)}) collective-permute-start(bf16[256,1024]{1,0:T(8,128)(2,1)S(1)} %copy-done.23), channel_id=1, source_target_pairs={{0,8},{4,12},{8,16},{12,20},{16,24},{20,28},{1,9},{5,13},{9,17},{1... | collective-permute-start | bytes 1572872 | tf_op jit(solution)/shard_map/ppermute | solution.py:66
  58.8 6.0 %collective-permute-done = bf16[256,1024]{1,0:T(8,128)(2,1)} collective-permute-done((bf16[256,1024]{1,0:T(8,128)(2,1)S(1)}, bf16[256,1024]{1,0:T(8,128)(2,1)}, u32[]{:S(2)}, u32[]{:S(2)}) %collective-permute-start) | collective-permute-done | bytes 524320 | tf_op jit(solution)/shard_map/ppermute | solution.py:66
  64.8 1.3 collective-permute-start.4
  66.1 1.5 collective-permute-start.2
  67.6 1.5 fusion
  69.1 7.8 %collective-permute-done.4 = bf16[256,1024]{1,0:T(8,128)(2,1)} collective-permute-done((bf16[256,1024]{1,0:T(8,128)(2,1)}, bf16[256,1024]{1,0:T(8,128)(2,1)}, u32[]{:S(2)}, u32[]{:S(2)}) %collective-permute-start.4) | collective-permute-done | bytes 524320 | tf_op jit(solution)/shard_map/ppermute | solution.py:66
  76.9 1.3 collective-permute-start.5
  78.9 1.1 select_bitcast_fusion.8
  80.0 16.4 %collective-permute-done.13 = bf16[4,256,1024]{2,1,0:T(8,128)(2,1)} collective-permute-done((bf16[4,256,1024]{2,1,0:T(8,128)(2,1)}, bf16[4,256,1024]{2,1,0:T(8,128)(2,1)}, u32[]{:S(2)}, u32[]{:S(2)}) %collective-permute-start.13) | collective-permute-done | bytes 2097184 | tf_op jit(solution)/shard_map/ppermute | solution.py:72
  96.4 1.9 select_bitcast_fusion.1
  99.1 2.2 %fusion.31 = f32[512,512]{1,0:T(8,128)} fusion(bf16[512,1024]{1,0:T(8,128)(2,1)S(1)} %fusion, bf16[2048,1024]{1,0:T(8,128)(2,1)S(1)} %bitcast.48, s32[]{:T(128)S(6)} %select_n.207), kind=kOutput, calls=%fused_computation.45 | convolution fusion | flops 536870912 | bytes 3145732 | tf_op jit(solution)/shard_map/dot_general | solution.py:131
  101.5 1.3 select_bitcast_fusion.9
  102.8 1.6 pad_maximum_fusion.2
  105.2 1.7 fusion.34
  107.1 2.8 %fusion.6 = bf16[512,512]{1,0:T(8,128)(2,1)} fusion(f32[512,512]{1,0:T(8,128)S(1)} %collective-permute-done.15, bf16[512,1024]{1,0:T(8,128)(2,1)S(1)} %fusion, bf16[2048,1024]{1,0:T(8,128)(2,1)} %bitcast.50, s32[]{:T(128)S(6)} %select_n.205), kind=kOutput, calls=%fused_computation.20 | convolution fusion | flops 537395200 | bytes 3670020 | tf_op jit(solution)/shard_map/dot_general | solution.py:131
  109.9 1.5 collective-permute-start.16
  111.4 3.0 %reshape.17 = f32[512,2,512]{2,1,0:T(2,128)S(1)} reshape(f32[512,1024]{1,0:T(8,128)} %param.7) | data formatting | bytes 4194304 | tf_op jit(solution)/shard_map/reshape | solution.py:110
  114.4 1.7 fusion.53
  116.2 8.2 %collective-permute-done.16 = bf16[512,512]{1,0:T(8,128)(2,1)} collective-permute-done((bf16[512,512]{1,0:T(8,128)(2,1)}, bf16[512,512]{1,0:T(8,128)(2,1)}, u32[]{:S(2)}, u32[]{:S(2)}) %collective-permute-start.16) | collective-permute-done | bytes 524320 | tf_op jit(solution)/shard_map/ppermute | solution.py:141
  124.3 2.6 %fusion.9 = bf16[512,512]{1,0:T(8,128)(2,1)S(1)} fusion(f32[512,512]{1,0:T(8,128)S(1)} %bitcast.66, f32[512,512]{1,0:T(8,128)} %collective-permute-done.14, bf16[512,1024]{1,0:T(8,128)(2,1)S(1)} %fusion, bf16[512,512]{1,0:T(8,128)(2,1)} %collective-permute-done.16, bf16[2048,1024]{1,0:T(8,128)(2,1)} %bitcast.51, s32[]{:T(128)S(6)} %select_n.200), kind=kOutput, calls=%fused_computation.23 | convolution fusion | flops 538181632 | bytes 5242884 | tf_op jit(solution)/shard_map/dot_general | solution.py:131
  126.9 1.5 collective-permute-start.17
  128.5 11.8 %collective-permute-done.17 = bf16[512,512]{1,0:T(8,128)(2,1)S(1)} collective-permute-done((bf16[512,512]{1,0:T(8,128)(2,1)S(1)}, bf16[512,512]{1,0:T(8,128)(2,1)S(1)}, u32[]{:S(2)}, u32[]{:S(2)}) %collective-permute-start.17) | collective-permute-done | bytes 524320 | tf_op jit(solution)/shard_map/ppermute | solution.py:150
  140.3 12.5 %collective-permute-done.6 = bf16[4,256,1024]{2,1,0:T(8,128)(2,1)} collective-permute-done((bf16[4,256,1024]{2,1,0:T(8,128)(2,1)}, bf16[4,256,1024]{2,1,0:T(8,128)(2,1)}, u32[]{:S(2)}, u32[]{:S(2)}) %collective-permute-start.6) | collective-permute-done | bytes 2097184 | tf_op jit(solution)/shard_map/ppermute | solution.py:72
  152.8 2.0 select_bitcast_fusion.3
  156.1 1.7 fusion.17
  158.2 2.1 %fusion.20 = f32[512,512]{1,0:T(8,128)S(1)} fusion(bf16[512,1024]{1,0:T(8,128)(2,1)S(1)} %fusion, bf16[2048,1024]{1,0:T(8,128)(2,1)} %bitcast.57, s32[]{:T(128)S(6)} %select_n.202), kind=kOutput, calls=%fused_computation.34 | convolution fusion | flops 536870912 | bytes 3145732 | tf_op jit(solution)/shard_map/dot_general | solution.py:131
  161.6 1.1 copy-done.3
  162.7 2.0 fusion.7
  166.9 12.0 %collective-permute-done.22 = bf16[512,512]{1,0:T(8,128)(2,1)S(1)} collective-permute-done((bf16[512,512]{1,0:T(8,128)(2,1)S(1)}, bf16[512,512]{1,0:T(8,128)(2,1)S(1)}, u32[]{:S(2)}, u32[]{:S(2)}) %collective-permute-start.22) | collective-permute-done | bytes 524320 | tf_op jit(solution)/shard_map/ppermute | solution.py:141
  182.1 11.1 %collective-permute-done.23 = bf16[512,512]{1,0:T(8,128)(2,1)S(1)} collective-permute-done((bf16[512,512]{1,0:T(8,128)(2,1)S(1)}, bf16[512,512]{1,0:T(8,128)(2,1)S(1)}, u32[]{:S(2)}, u32[]{:S(2)}) %collective-permute-start.23) | collective-permute-done | bytes 524320 | tf_op jit(solution)/shard_map/ppermute | solution.py:150
  195.2 1.2 fusion.1
  197.2 2.9 %collective-permute-done.26 = f32[1024]{0:T(1024)S(1)} collective-permute-done((f32[1024]{0:T(1024)S(1)}, f32[1024]{0:T(1024)S(1)}, u32[]{:S(2)}, u32[]{:S(2)}) %collective-permute-start.26) | collective-permute-done | bytes 4128 | tf_op jit(solution)/shard_map/ppermute | solution.py:84
  200.1 3.6 %collective-permute-done.27 = f32[1024]{0:T(1024)S(1)} collective-permute-done((f32[1024]{0:T(1024)S(1)}, f32[1024]{0:T(1024)S(1)}, u32[]{:S(2)}, u32[]{:S(2)}) %collective-permute-start.27) | collective-permute-done | bytes 4128 | tf_op jit(solution)/shard_map/ppermute | solution.py:84
  203.7 2.3 %collective-permute-start.28 = (f32[1024]{0:T(1024)S(1)}, f32[1024]{0:T(1024)S(1)}, u32[]{:S(2)}, u32[]{:S(2)}) collective-permute-start(f32[1024]{0:T(1024)S(1)} %add.221), channel_id=1, source_target_pairs={{0,16},{4,20},{8,24},{12,28},{16,0},{20,4},{24,8},{28,12},{1,17},{... | collective-permute-start | bytes 12296 | tf_op jit(solution)/shard_map/ppermute | solution.py:84
  206.0 2.2 %collective-permute-done.28 = f32[1024]{0:T(1024)S(1)} collective-permute-done((f32[1024]{0:T(1024)S(1)}, f32[1024]{0:T(1024)S(1)}, u32[]{:S(2)}, u32[]{:S(2)}) %collective-permute-start.28) | collective-permute-done | bytes 4128 | tf_op jit(solution)/shard_map/ppermute | solution.py:84
  (98 shorter events, 15.0 us)
Async XLA Ops:
  2.3 47.2 %copy-start.12 = (bf16[1,256,1024]{2,1,0:T(8,128)(2,1)}, bf16[1,256,1024]{2,1,0:T(8,128)(2,1)S(1)}, u32[]{:S(2)}) copy-start(bf16[1,256,1024]{2,1,0:T(8,128)(2,1)S(1)} %get-tuple-element.21) | copy-start | bytes 1572868
  2.3 100.5 %copy-start.10 = (bf16[1,256,1024]{2,1,0:T(8,128)(2,1)}, bf16[1,256,1024]{2,1,0:T(8,128)(2,1)S(1)}, u32[]{:S(2)}) copy-start(bf16[1,256,1024]{2,1,0:T(8,128)(2,1)S(1)} %get-tuple-element.22) | copy-start | bytes 1572868
  2.3 16.8 %collective-permute-start.7 = (bf16[256,1024]{1,0:T(8,128)(2,1)S(1)}, bf16[256,1024]{1,0:T(8,128)(2,1)S(1)}, u32[]{:S(2)}, u32[]{:S(2)}) collective-permute-start(bf16[256,1024]{1,0:T(8,128)(2,1)S(1)} %get-tuple-element.23), channel_id=1, source_target_pairs={{8,0},{12,4},{16,8},{20,12},{24,16},{28,20},{9,1},{13,5},{17,9},{2... | collective-permute-start | bytes 1572872 | tf_op jit(solution)/shard_map/ppermute | solution.py:66
  3.6 16.8 %collective-permute-start.8 = (bf16[256,1024]{1,0:T(8,128)(2,1)S(1)}, bf16[256,1024]{1,0:T(8,128)(2,1)S(1)}, u32[]{:S(2)}, u32[]{:S(2)}) collective-permute-start(bf16[256,1024]{1,0:T(8,128)(2,1)S(1)} %get-tuple-element.23), channel_id=1, source_target_pairs={{0,8},{4,12},{8,16},{12,20},{16,24},{20,28},{1,9},{5,13},{9,17},{1... | collective-permute-start | bytes 1572872 | tf_op jit(solution)/shard_map/ppermute | solution.py:66
  19.1 15.0 %collective-permute-start.11 = (bf16[256,1024]{1,0:T(8,128)(2,1)S(1)}, bf16[256,1024]{1,0:T(8,128)(2,1)S(1)}, u32[]{:S(2)}, u32[]{:S(2)}) collective-permute-start(bf16[256,1024]{1,0:T(8,128)(2,1)S(1)} %collective-permute-done.7), channel_id=1, source_target_pairs={{8,0},{12,4},{16,8},{20,12},{9,1},{13,5},{17,9},{21,13},{10,2},{14... | collective-permute-start | bytes 1572872 | tf_op jit(solution)/shard_map/ppermute | solution.py:66
  20.4 15.0 %collective-permute-start.9 = (bf16[256,1024]{1,0:T(8,128)(2,1)S(1)}, bf16[256,1024]{1,0:T(8,128)(2,1)}, u32[]{:S(2)}, u32[]{:S(2)}) collective-permute-start(bf16[256,1024]{1,0:T(8,128)(2,1)S(1)} %collective-permute-done.8), channel_id=1, source_target_pairs={{8,16},{12,20},{16,24},{20,28},{9,17},{13,21},{17,25},{21,29},{10,... | collective-permute-start | bytes 1572872 | tf_op jit(solution)/shard_map/ppermute | solution.py:66
  34.1 14.2 %collective-permute-start.12 = (bf16[256,1024]{1,0:T(8,128)(2,1)S(1)}, bf16[256,1024]{1,0:T(8,128)(2,1)}, u32[]{:S(2)}, u32[]{:S(2)}) collective-permute-start(bf16[256,1024]{1,0:T(8,128)(2,1)S(1)} %collective-permute-done.11), channel_id=1, source_target_pairs={{8,0},{12,4},{9,1},{13,5},{10,2},{14,6},{11,3},{15,7}} | collective-permute-start | bytes 1572872 | tf_op jit(solution)/shard_map/ppermute | solution.py:66
  35.4 14.0 %collective-permute-start.10 = (bf16[256,1024]{1,0:T(8,128)(2,1)}, bf16[256,1024]{1,0:T(8,128)(2,1)S(1)}, u32[]{:S(2)}, u32[]{:S(2)}) collective-permute-start(bf16[256,1024]{1,0:T(8,128)(2,1)} %collective-permute-done.9), channel_id=1, source_target_pairs={{16,24},{20,28},{17,25},{21,29},{18,26},{22,30},{19,27},{23,31}} | collective-permute-start | bytes 1572872 | tf_op jit(solution)/shard_map/ppermute | solution.py:66
  49.5 2.7 %copy-start.23 = (bf16[256,1024]{1,0:T(8,128)(2,1)S(1)}, bf16[256,1024]{1,0:T(8,128)(2,1)}, u32[]{:S(2)}) copy-start(bf16[256,1024]{1,0:T(8,128)(2,1)} %get-tuple-element.24) | copy-start | bytes 1572868
  49.5 18.1 %copy-start.24 = (f32[1024]{0:T(1024)S(1)}, f32[1024]{0:T(1024)}, u32[]{:S(2)}) copy-start(f32[1024]{0:T(1024)} %param.6) | copy-start | bytes 12292
  51.1 45.3 %collective-permute-start.13 = (bf16[4,256,1024]{2,1,0:T(8,128)(2,1)}, bf16[4,256,1024]{2,1,0:T(8,128)(2,1)}, u32[]{:S(2)}, u32[]{:S(2)}) collective-permute-start(bf16[4,256,1024]{2,1,0:T(8,128)(2,1)} %pad_maximum_fusion.3), channel_id=1, source_target_pairs={{0,4},{4,0},{8,12},{12,8},{16,20},{20,16},{24,28},{28,24},{1,5},{5... | collective-permute-start | bytes 6291464 | tf_op jit(solution)/shard_map/ppermute | solution.py:72
  52.2 12.7 %collective-permute-start = (bf16[256,1024]{1,0:T(8,128)(2,1)S(1)}, bf16[256,1024]{1,0:T(8,128)(2,1)}, u32[]{:S(2)}, u32[]{:S(2)}) collective-permute-start(bf16[256,1024]{1,0:T(8,128)(2,1)S(1)} %copy-done.23), channel_id=1, source_target_pairs={{8,0},{12,4},{16,8},{20,12},{24,16},{28,20},{9,1},{13,5},{17,9},{2... | collective-permute-start | bytes 1572872 | tf_op jit(solution)/shard_map/ppermute | solution.py:66
  53.4 12.7 %collective-permute-start.1 = (bf16[256,1024]{1,0:T(8,128)(2,1)S(1)}, bf16[256,1024]{1,0:T(8,128)(2,1)}, u32[]{:S(2)}, u32[]{:S(2)}) collective-permute-start(bf16[256,1024]{1,0:T(8,128)(2,1)S(1)} %copy-done.23), channel_id=1, source_target_pairs={{0,8},{4,12},{8,16},{12,20},{16,24},{20,28},{1,9},{5,13},{9,17},{1... | collective-permute-start | bytes 1572872 | tf_op jit(solution)/shard_map/ppermute | solution.py:66
  64.8 12.1 %collective-permute-start.4 = (bf16[256,1024]{1,0:T(8,128)(2,1)}, bf16[256,1024]{1,0:T(8,128)(2,1)}, u32[]{:S(2)}, u32[]{:S(2)}) collective-permute-start(bf16[256,1024]{1,0:T(8,128)(2,1)} %collective-permute-done), channel_id=1, source_target_pairs={{8,0},{12,4},{16,8},{20,12},{9,1},{13,5},{17,9},{21,13},{10,2},{14... | collective-permute-start | bytes 1572872 | tf_op jit(solution)/shard_map/ppermute | solution.py:66
  66.1 12.1 %collective-permute-start.2 = (bf16[256,1024]{1,0:T(8,128)(2,1)}, bf16[256,1024]{1,0:T(8,128)(2,1)}, u32[]{:S(2)}, u32[]{:S(2)}) collective-permute-start(bf16[256,1024]{1,0:T(8,128)(2,1)} %collective-permute-done.1), channel_id=1, source_target_pairs={{8,16},{12,20},{16,24},{20,28},{9,17},{13,21},{17,25},{21,29},{10,... | collective-permute-start | bytes 1572872 | tf_op jit(solution)/shard_map/ppermute | solution.py:66
  76.9 24.4 %collective-permute-start.5 = (bf16[256,1024]{1,0:T(8,128)(2,1)}, bf16[256,1024]{1,0:T(8,128)(2,1)S(1)}, u32[]{:S(2)}, u32[]{:S(2)}) collective-permute-start(bf16[256,1024]{1,0:T(8,128)(2,1)} %collective-permute-done.4), channel_id=1, source_target_pairs={{8,0},{12,4},{9,1},{13,5},{10,2},{14,6},{11,3},{15,7}} | collective-permute-start | bytes 1572872 | tf_op jit(solution)/shard_map/ppermute | solution.py:66
  78.2 23.2 %collective-permute-start.3 = (bf16[256,1024]{1,0:T(8,128)(2,1)}, bf16[256,1024]{1,0:T(8,128)(2,1)S(1)}, u32[]{:S(2)}, u32[]{:S(2)}) collective-permute-start(bf16[256,1024]{1,0:T(8,128)(2,1)} %collective-permute-done.2), channel_id=1, source_target_pairs={{16,24},{20,28},{17,25},{21,29},{18,26},{22,30},{19,27},{23,31}} | collective-permute-start | bytes 1572872 | tf_op jit(solution)/shard_map/ppermute | solution.py:66
  80.0 22.8 %copy-start.4 = (bf16[1,256,1024]{2,1,0:T(8,128)(2,1)}, bf16[1,256,1024]{2,1,0:T(8,128)(2,1)S(1)}, u32[]{:S(2)}) copy-start(bf16[1,256,1024]{2,1,0:T(8,128)(2,1)S(1)} %select_bitcast_fusion.8) | copy-start | bytes 1572868
  99.1 6.1 %copy-start = (bf16[4,2,256,1024]{3,2,1,0:T(8,128)(2,1)}, bf16[4,2,256,1024]{3,2,1,0:T(8,128)(2,1)S(1)}, u32[]{:S(2)}) copy-start(bf16[4,2,256,1024]{3,2,1,0:T(8,128)(2,1)S(1)} %copy.6) | copy-start | bytes 12582916
  101.3 5.8 %collective-permute-start.15 = (f32[512,512]{1,0:T(8,128)}, f32[512,512]{1,0:T(8,128)S(1)}, u32[]{:S(2)}, u32[]{:S(2)}) collective-permute-start(f32[512,512]{1,0:T(8,128)} %fusion.31), channel_id=1, source_target_pairs={{0,1},{1,0},{2,3},{3,2},{4,5},{5,4},{6,7},{7,6},{8,9},{9,8},{10,11... | collective-permute-start | bytes 3145736 | tf_op jit(solution)/shard_map/ppermute | solution.py:138
  101.4 3.0 %copy-start.6 = (bf16[1,256,1024]{2,1,0:T(8,128)(2,1)}, bf16[1,256,1024]{2,1,0:T(8,128)(2,1)S(1)}, u32[]{:S(2)}) copy-start(bf16[1,256,1024]{2,1,0:T(8,128)(2,1)S(1)} %select_bitcast_fusion.7) | copy-start | bytes 1572868
  104.4 48.4 %collective-permute-start.6 = (bf16[4,256,1024]{2,1,0:T(8,128)(2,1)}, bf16[4,256,1024]{2,1,0:T(8,128)(2,1)}, u32[]{:S(2)}, u32[]{:S(2)}) collective-permute-start(bf16[4,256,1024]{2,1,0:T(8,128)(2,1)} %pad_maximum_fusion.2), channel_id=1, source_target_pairs={{0,4},{4,0},{8,12},{12,8},{16,20},{20,16},{24,28},{28,24},{1,5},{5... | collective-permute-start | bytes 6291464 | tf_op jit(solution)/shard_map/ppermute | solution.py:72
  106.9 9.3 %collective-permute-start.14 = (f32[512,512]{1,0:T(8,128)}, f32[512,512]{1,0:T(8,128)}, u32[]{:S(2)}, u32[]{:S(2)}) collective-permute-start(f32[512,512]{1,0:T(8,128)} %fusion.34), channel_id=1, source_target_pairs={{0,1},{1,0},{2,3},{3,2},{4,5},{5,4},{6,7},{7,6},{8,9},{9,8},{10,11... | collective-permute-start | bytes 3145736 | tf_op jit(solution)/shard_map/ppermute | solution.py:138
  109.9 14.4 %collective-permute-start.16 = (bf16[512,512]{1,0:T(8,128)(2,1)}, bf16[512,512]{1,0:T(8,128)(2,1)}, u32[]{:S(2)}, u32[]{:S(2)}) collective-permute-start(bf16[512,512]{1,0:T(8,128)(2,1)} %fusion.6), channel_id=1, source_target_pairs={{0,2},{1,3},{2,0},{3,1},{4,6},{5,7},{6,4},{7,5},{8,10},{9,11},{10,... | collective-permute-start | bytes 1572872 | tf_op jit(solution)/shard_map/ppermute | solution.py:141
  124.3 28.5 %copy-start.5 = (bf16[1,256,1024]{2,1,0:T(8,128)(2,1)S(1)}, bf16[1,256,1024]{2,1,0:T(8,128)(2,1)}, u32[]{:S(2)}) copy-start(bf16[1,256,1024]{2,1,0:T(8,128)(2,1)} %copy-done.4) | copy-start | bytes 1572868
  124.3 28.5 %copy-start.7 = (bf16[1,256,1024]{2,1,0:T(8,128)(2,1)S(1)}, bf16[1,256,1024]{2,1,0:T(8,128)(2,1)}, u32[]{:S(2)}) copy-start(bf16[1,256,1024]{2,1,0:T(8,128)(2,1)} %copy-done.6) | copy-start | bytes 1572868
  124.3 28.5 %copy-start.9 = (bf16[1,256,1024]{2,1,0:T(8,128)(2,1)S(1)}, bf16[1,256,1024]{2,1,0:T(8,128)(2,1)}, u32[]{:S(2)}) copy-start(bf16[1,256,1024]{2,1,0:T(8,128)(2,1)} %copy-done.8) | copy-start | bytes 1572868
  124.3 28.5 %copy-start.11 = (bf16[1,256,1024]{2,1,0:T(8,128)(2,1)S(1)}, bf16[1,256,1024]{2,1,0:T(8,128)(2,1)}, u32[]{:S(2)}) copy-start(bf16[1,256,1024]{2,1,0:T(8,128)(2,1)} %copy-done.10) | copy-start | bytes 1572868
  126.9 27.9 %copy-start.15 = (bf16[512,512]{1,0:T(8,128)(2,1)}, bf16[512,512]{1,0:T(8,128)(2,1)S(1)}, u32[]{:S(2)}) copy-start(bf16[512,512]{1,0:T(8,128)(2,1)S(1)} %fusion.9) | copy-start | bytes 1572868
  126.9 13.4 %collective-permute-start.17 = (bf16[512,512]{1,0:T(8,128)(2,1)S(1)}, bf16[512,512]{1,0:T(8,128)(2,1)S(1)}, u32[]{:S(2)}, u32[]{:S(2)}) collective-permute-start(bf16[512,512]{1,0:T(8,128)(2,1)S(1)} %fusion.9), channel_id=1, source_target_pairs={{0,2},{1,3},{2,0},{3,1},{4,6},{5,7},{6,4},{7,5},{8,10},{9,11},{10,... | collective-permute-start | bytes 1572872 | tf_op jit(solution)/shard_map/ppermute | solution.py:150
  128.5 26.8 %collective-permute-start.18 = (bf16[512,512]{1,0:T(8,128)(2,1)S(1)}, bf16[512,512]{1,0:T(8,128)(2,1)S(1)}, u32[]{:S(2)}, u32[]{:S(2)}) collective-permute-start(bf16[512,512]{1,0:T(8,128)(2,1)S(1)} %fusion.9), channel_id=1, source_target_pairs={{0,1},{1,0},{2,3},{3,2},{4,5},{5,4},{6,7},{7,6},{8,9},{9,8},{10,11... | collective-permute-start | bytes 1572872 | tf_op jit(solution)/shard_map/ppermute | solution.py:151
  140.3 14.5 %copy-start.21 = (bf16[512,512]{1,0:T(8,128)(2,1)}, bf16[512,512]{1,0:T(8,128)(2,1)S(1)}, u32[]{:S(2)}) copy-start(bf16[512,512]{1,0:T(8,128)(2,1)S(1)} %collective-permute-done.17) | copy-start | bytes 1572868
  140.3 15.0 %collective-permute-start.19 = (bf16[512,512]{1,0:T(8,128)(2,1)S(1)}, bf16[512,512]{1,0:T(8,128)(2,1)S(1)}, u32[]{:S(2)}, u32[]{:S(2)}) collective-permute-start(bf16[512,512]{1,0:T(8,128)(2,1)S(1)} %collective-permute-done.17), channel_id=1, source_target_pairs={{0,1},{1,0},{2,3},{3,2},{4,5},{5,4},{6,7},{7,6},{8,9},{9,8},{10,11... | collective-permute-start | bytes 1572872 | tf_op jit(solution)/shard_map/ppermute | solution.py:151
  155.2 2.6 %copy-start.2 = (bf16[4,2,256,1024]{3,2,1,0:T(8,128)(2,1)}, bf16[4,2,256,1024]{3,2,1,0:T(8,128)(2,1)S(1)}, u32[]{:S(2)}) copy-start(bf16[4,2,256,1024]{3,2,1,0:T(8,128)(2,1)S(1)} %pad_maximum_fusion) | copy-start | bytes 12582916
  156.1 2.0 copy-start.14
  157.9 3.7 %collective-permute-start.21 = (f32[512,512]{1,0:T(8,128)}, f32[512,512]{1,0:T(8,128)}, u32[]{:S(2)}, u32[]{:S(2)}) collective-permute-start(f32[512,512]{1,0:T(8,128)} %fusion.17), channel_id=1, source_target_pairs={{0,1},{1,0},{2,3},{3,2},{4,5},{5,4},{6,7},{7,6},{8,9},{9,8},{10,11... | collective-permute-start | bytes 3145736 | tf_op jit(solution)/shard_map/ppermute | solution.py:138
  158.2 2.5 %copy-start.1 = (bf16[4,2,256,1024]{3,2,1,0:T(8,128)(2,1)S(1)}, bf16[4,2,256,1024]{3,2,1,0:T(8,128)(2,1)}, u32[]{:S(2)}) copy-start(bf16[4,2,256,1024]{3,2,1,0:T(8,128)(2,1)} %copy-done) | copy-start | bytes 12582916
  158.2 2.6 %copy-start.22 = (bf16[512,512]{1,0:T(8,128)(2,1)S(1)}, bf16[512,512]{1,0:T(8,128)(2,1)}, u32[]{:S(2)}) copy-start(bf16[512,512]{1,0:T(8,128)(2,1)} %copy-done.21) | copy-start | bytes 1572868
  160.4 2.3 %copy-start.3 = (bf16[4,2,256,1024]{3,2,1,0:T(8,128)(2,1)S(1)}, bf16[4,2,256,1024]{3,2,1,0:T(8,128)(2,1)}, u32[]{:S(2)}) copy-start(bf16[4,2,256,1024]{3,2,1,0:T(8,128)(2,1)} %copy-done.2) | copy-start | bytes 12582916
  160.4 6.5 %collective-permute-start.20 = (f32[512,512]{1,0:T(8,128)S(1)}, f32[512,512]{1,0:T(8,128)S(1)}, u32[]{:S(2)}, u32[]{:S(2)}) collective-permute-start(f32[512,512]{1,0:T(8,128)S(1)} %fusion.20), channel_id=1, source_target_pairs={{0,1},{1,0},{2,3},{3,2},{4,5},{5,4},{6,7},{7,6},{8,9},{9,8},{10,11... | collective-permute-start | bytes 3145736 | tf_op jit(solution)/shard_map/ppermute | solution.py:138
  161.6 3.9 %copy-start.16 = (bf16[512,512]{1,0:T(8,128)(2,1)S(1)}, bf16[512,512]{1,0:T(8,128)(2,1)}, u32[]{:S(2)}) copy-start(bf16[512,512]{1,0:T(8,128)(2,1)} %copy-done.15) | copy-start | bytes 1572868
  164.7 14.2 %collective-permute-start.22 = (bf16[512,512]{1,0:T(8,128)(2,1)S(1)}, bf16[512,512]{1,0:T(8,128)(2,1)S(1)}, u32[]{:S(2)}, u32[]{:S(2)}) collective-permute-start(bf16[512,512]{1,0:T(8,128)(2,1)S(1)} %fusion.7), channel_id=1, source_target_pairs={{0,2},{1,3},{2,0},{3,1},{4,6},{5,7},{6,4},{7,5},{8,10},{9,11},{10,... | collective-permute-start | bytes 1572872 | tf_op jit(solution)/shard_map/ppermute | solution.py:141
  179.8 13.4 %collective-permute-start.23 = (bf16[512,512]{1,0:T(8,128)(2,1)S(1)}, bf16[512,512]{1,0:T(8,128)(2,1)S(1)}, u32[]{:S(2)}, u32[]{:S(2)}) collective-permute-start(bf16[512,512]{1,0:T(8,128)(2,1)S(1)} %fusion.8), channel_id=1, source_target_pairs={{0,2},{1,3},{2,0},{3,1},{4,6},{5,7},{6,4},{7,5},{8,10},{9,11},{10,... | collective-permute-start | bytes 1572872 | tf_op jit(solution)/shard_map/ppermute | solution.py:150
  181.3 12.7 %collective-permute-start.24 = (bf16[512,512]{1,0:T(8,128)(2,1)S(1)}, bf16[512,512]{1,0:T(8,128)(2,1)S(1)}, u32[]{:S(2)}, u32[]{:S(2)}) collective-permute-start(bf16[512,512]{1,0:T(8,128)(2,1)S(1)} %fusion.8), channel_id=1, source_target_pairs={{0,1},{1,0},{2,3},{3,2},{4,5},{5,4},{6,7},{7,6},{8,9},{9,8},{10,11... | collective-permute-start | bytes 1572872 | tf_op jit(solution)/shard_map/ppermute | solution.py:151
  193.2 1.9 collective-permute-start.25
  196.4 3.7 %collective-permute-start.26 = (f32[1024]{0:T(1024)S(1)}, f32[1024]{0:T(1024)S(1)}, u32[]{:S(2)}, u32[]{:S(2)}) collective-permute-start(f32[1024]{0:T(1024)S(1)} %fusion.1), channel_id=1, source_target_pairs={{0,4},{4,0},{8,12},{12,8},{16,20},{20,16},{24,28},{28,24},{1,5},{5... | collective-permute-start | bytes 12296 | tf_op jit(solution)/shard_map/ppermute | solution.py:84
  200.1 3.6 %collective-permute-start.27 = (f32[1024]{0:T(1024)S(1)}, f32[1024]{0:T(1024)S(1)}, u32[]{:S(2)}, u32[]{:S(2)}) collective-permute-start(f32[1024]{0:T(1024)S(1)} %add.220), channel_id=1, source_target_pairs={{0,8},{4,12},{8,0},{12,4},{16,24},{20,28},{24,16},{28,20},{1,9},{5... | collective-permute-start | bytes 12296 | tf_op jit(solution)/shard_map/ppermute | solution.py:84
  203.7 4.5 %collective-permute-start.28 = (f32[1024]{0:T(1024)S(1)}, f32[1024]{0:T(1024)S(1)}, u32[]{:S(2)}, u32[]{:S(2)}) collective-permute-start(f32[1024]{0:T(1024)S(1)} %add.221), channel_id=1, source_target_pairs={{0,16},{4,20},{8,24},{12,28},{16,0},{20,4},{24,8},{28,12},{1,17},{... | collective-permute-start | bytes 12296 | tf_op jit(solution)/shard_map/ppermute | solution.py:84
  (6 other events, 8.7 us)

commit v17 on v14

--- a/solution.py
+++ b/solution.py
@@ -134,7 +134,9 @@
     fwd = jnp.concatenate(
         [forward_voxel_field, lax.ppermute(forward_voxel_field, "src", swap)], axis=0
     )
-    scaled = (fwd.astype(jnp.float32) * voxel_input_vector[None, :]).astype(jnp.bfloat16)
+    scaled = lax.optimization_barrier(
+        (fwd.astype(jnp.float32) * voxel_input_vector[None, :]).astype(jnp.bfloat16)
+    )
     weight = measurement_weight.reshape(sl, 2, ds)
     back = jnp.zeros((2 * sl, vl), jnp.float32)
     nxt = _zline(adjoint_voxel_field[:r], na)
@@ -174,8 +176,11 @@
                 (_zline(adjoint_voxel_field[(c + 1) * r:(c + 2) * r], na), [w for _, w in got])
             )
             got = [(blk, w) for (blk, _), w in zip(got, ws)]
-        for blk, w in got:
-            back = back + jnp.dot(w, rows(col, blk), preferred_element_type=jnp.float32)
+        back = back + jnp.dot(
+            jnp.concatenate([w for _, w in got], axis=1),
+            jnp.concatenate([rows(col, blk) for blk, _ in got], axis=0),
+            preferred_element_type=jnp.float32,
+        )
 
     local_sum = jnp.sum(fwd.astype(jnp.float32) * back, axis=0)
     return _sum_over_src(local_sum)

time: 214 us -> 197 us (0.921)
  matrix products: 41.7 us -> 19.8 us
  local copies, waits for them, and re-layouts: 9 us -> 15.3 us
  starting transfers between devices: 40.8 us -> 34.7 us
  other arithmetic: 5.22 us -> 9.67 us
    dot_general x8 -> x2, matrix products: 18.9 us -> 7.52 us  [_fast(): jnp.dot(jnp.concatenate([w for _, w in got], axis=1), jnp.concatenate([ro...]
    dot_general x8, matrix products: 22.8 us -> 12.3 us  [pblock(): lax.dot_general(scaled, rows(col, blk), (((1,), (1,)), ((), ())), preferr...]
    ppermute x3, starting transfers between devices: 7.34 us -> 1.44 us  [_sum_over_src(): v = v + lax.ppermute(v, 'src', [(i, i ^ b) for i in range(n)])]
    ppermute x1, waiting for transfers between devices: 10.7 us -> 6.03 us  [_fast(): lax.ppermute(forward_voxel_field, 'src', swap)]
    unnamed x39, local copies, waits for them, and re-layouts: 4.86 us -> 8.84 us
    ppermute x3, waiting for transfers between devices: 7.22 us -> 10.4 us  [_sum_over_src(): v = v + lax.ppermute(v, 'src', [(i, i ^ b) for i in range(n)])]
    ppermute x12, starting transfers between devices: 21.5 us -> 18.7 us  [_zline(): cur = lax.ppermute(cur, 'src', pairs)]
    select_n x6, other arithmetic: 1.39 us -> 3.7 us  [_zline(): jnp.where(ia + k < na, got[-1, k], got[1, na - k])]
  transfers between devices with their start and end apart: 32 -> 32, of which waited for: 17 -> 20; matrix products, arithmetic and copies ran while one was open for 17% -> 14% of each run, Pallas kernels for 0% -> 0%
where the time goes in v17:
time: 197 us; the launch traced here: 196 us
  waiting for transfers between devices  116 us (59%)
  starting transfers between devices  34.7 us (18%)
  matrix products  19.8 us (10%)
  local copies, waits for them, and re-layouts  15.3 us (8%)
  other arithmetic  9.67 us (5%)
    ppermute x12, waiting for transfers between devices, _zline(): cur = lax.ppermute(cur, 'src', pairs)  41.8 us
    ppermute x2, waiting for transfers between devices, _fast(): lax.ppermute(halves[k].astype(jnp.bfloat16), 'vox', chip_perm(k))  22.7 us
    ppermute x12, starting transfers between devices, _zline(): cur = lax.ppermute(cur, 'src', pairs)  18.7 us
    ppermute x2, waiting for transfers between devices, _fast(): own, theirs = (share[:sl], lax.ppermute(share[sl:], 'src', swap))  12.6 us
    dot_general x8, matrix products, pblock(): lax.dot_general(scaled, rows(col, blk), (((1,), (1,)), ((), ())), preferr...  12.3 us
    ppermute x2, waiting for transfers between devices, _fast(): lax.ppermute(piece, 'vox', chip_perm(k))  10.9 us
    ppermute x3, waiting for transfers between devices, _sum_over_src(): v = v + lax.ppermute(v, 'src', [(i, i ^ b) for i in range(n)])  10.4 us
    ppermute x2, waiting for transfers between devices, _fast(): piece = jnp.concatenate([mine, lax.ppermute(other, 'src', swap)], axis=0)  9.43 us
  transfers between devices with their start and end apart: 32, of which 20 were waited for; matrix products, arithmetic and copies ran while one was open for 14% of the time, Pallas kernels for 0%

profile of v17, /device:TPU:0, one launch (start us, length us, event | category | flops | bytes accessed | tf_op | source)
XLA Modules:
  0.0 195.8 jit_solution(4766287099167804796)
XLA Ops:
  0.0 2.2 %fusion.67 = (bf16[256,1024]{1,0:T(8,128)(2,1)S(1)}, bf16[256,1024]{1,0:T(8,128)(2,1)}) fusion(bf16[512,1024]{1,0:T(8,128)(2,1)} %param.5), kind=kLoop, calls=%fused_computation.98 | loop fusion | bytes 2097152 | tf_op jit(solution)/shard_map/slice | solution.py:142
  2.2 4.9 %collective-permute-start.8 = (bf16[256,1024]{1,0:T(8,128)(2,1)S(1)}, bf16[256,1024]{1,0:T(8,128)(2,1)S(1)}, u32[]{:S(2)}, u32[]{:S(2)}) collective-permute-start(bf16[256,1024]{1,0:T(8,128)(2,1)S(1)} %get-tuple-element.29), channel_id=1, source_target_pairs={{0,8},{4,12},{8,16},{12,20},{16,24},{20,28},{1,9},{5,13},{9,17},{1... | collective-permute-start | bytes 1572872 | tf_op jit(solution)/shard_map/ppermute | solution.py:104
  7.1 1.6 collective-permute-start
  8.7 1.3 collective-permute-start.7
  10.0 8.2 %collective-permute-done.8 = bf16[256,1024]{1,0:T(8,128)(2,1)S(1)} collective-permute-done((bf16[256,1024]{1,0:T(8,128)(2,1)S(1)}, bf16[256,1024]{1,0:T(8,128)(2,1)S(1)}, u32[]{:S(2)}, u32[]{:S(2)}) %collective-permute-start.8) | collective-permute-done | bytes 524320 | tf_op jit(solution)/shard_map/ppermute | solution.py:104
  18.2 1.4 collective-permute-start.9
  19.7 4.1 %collective-permute-done.7 = bf16[256,1024]{1,0:T(8,128)(2,1)} collective-permute-done((bf16[256,1024]{1,0:T(8,128)(2,1)S(1)}, bf16[256,1024]{1,0:T(8,128)(2,1)}, u32[]{:S(2)}, u32[]{:S(2)}) %collective-permute-start.7) | collective-permute-done | bytes 524320 | tf_op jit(solution)/shard_map/ppermute | solution.py:104
  23.8 1.3 collective-permute-start.11
  25.9 6.0 %collective-permute-done = bf16[512,1024]{1,0:T(8,128)(2,1)} collective-permute-done((bf16[512,1024]{1,0:T(8,128)(2,1)S(1)}, bf16[512,1024]{1,0:T(8,128)(2,1)}, u32[]{:S(2)}, u32[]{:S(2)}) %collective-permute-start) | collective-permute-done | bytes 1048608 | tf_op jit(solution)/shard_map/ppermute | solution.py:135
  31.9 2.1 %fusion = bf16[1024,1024]{1,0:T(8,128)(2,1)S(1)} fusion(f32[1024]{0:T(1024)S(1)} %copy-done.11, bf16[512,1024]{1,0:T(8,128)(2,1)} %collective-permute-done, bf16[512,1024]{1,0:T(8,128)(2,1)} %param.4), kind=kLoop, calls=%fused_computation.2 | loop fusion | flops 6291456 | bytes 4198400 | tf_op jit(solution)/shard_map/convert_element_type | solution.py:138
  34.1 4.1 %collective-permute-done.11 = bf16[256,1024]{1,0:T(8,128)(2,1)} collective-permute-done((bf16[256,1024]{1,0:T(8,128)(2,1)}, bf16[256,1024]{1,0:T(8,128)(2,1)}, u32[]{:S(2)}, u32[]{:S(2)}) %collective-permute-start.11) | collective-permute-done | bytes 524320 | tf_op jit(solution)/shard_map/ppermute | solution.py:104
  38.2 1.3 collective-permute-start.12
  41.7 9.8 %collective-permute-done.12 = bf16[256,1024]{1,0:T(8,128)(2,1)S(1)} collective-permute-done((bf16[256,1024]{1,0:T(8,128)(2,1)}, bf16[256,1024]{1,0:T(8,128)(2,1)S(1)}, u32[]{:S(2)}, u32[]{:S(2)}) %collective-permute-start.12) | collective-permute-done | bytes 524320 | tf_op jit(solution)/shard_map/ppermute | solution.py:104
  51.8 1.7 fusion.50
  53.5 2.8 %fusion.53 = f32[1024,256]{1,0:T(8,128)} fusion(bf16[1024,1024]{1,0:T(8,128)(2,1)S(1)} %fusion, bf16[1024,1024]{1,0:T(8,128)(2,1)} %copy-done, s32[]{:T(128)S(6)} %select_n.229), kind=kOutput, calls=%fused_computation.66 | convolution fusion | flops 536870912 | bytes 3670020 | tf_op jit(solution)/shard_map/dot_general | solution.py:147
  56.8 2.6 %fusion.36 = bf16[1024,256]{1,0:T(8,128)(2,1)} fusion(f32[1024,256]{1,0:T(8,128)S(1)} %collective-permute-done.14, bf16[1024,1024]{1,0:T(8,128)(2,1)S(1)} %fusion, bf16[1024,1024]{1,0:T(8,128)(2,1)} %copy-done, s32[]{:T(128)S(6)} %select_n.232), kind=kOutput, calls=%fused_computation.45 | convolution fusion | flops 537395200 | bytes 4194308 | tf_op jit(solution)/shard_map/dot_general | solution.py:147
  59.4 1.5 collective-permute-start.15
  60.9 2.4 %collective-permute-start.2 = (bf16[256,1024]{1,0:T(8,128)(2,1)}, bf16[256,1024]{1,0:T(8,128)(2,1)}, u32[]{:S(2)}, u32[]{:S(2)}) collective-permute-start(bf16[256,1024]{1,0:T(8,128)(2,1)} %get-tuple-element.30), channel_id=1, source_target_pairs={{0,8},{4,12},{8,16},{12,20},{16,24},{20,28},{1,9},{5,13},{9,17},{1... | collective-permute-start | bytes 1572872 | tf_op jit(solution)/shard_map/ppermute | solution.py:104
  63.3 10.2 %collective-permute-done.15 = bf16[1024,256]{1,0:T(8,128)(2,1)S(1)} collective-permute-done((bf16[1024,256]{1,0:T(8,128)(2,1)}, bf16[1024,256]{1,0:T(8,128)(2,1)S(1)}, u32[]{:S(2)}, u32[]{:S(2)}) %collective-permute-start.15) | collective-permute-done | bytes 524320 | tf_op jit(solution)/shard_map/ppermute | solution.py:157
  73.5 2.1 %fusion.35 = f32[1024,256]{1,0:T(8,128)S(1)} fusion(f32[1024,256]{1,0:T(8,128)} %collective-permute-done.13, bf16[1024,1024]{1,0:T(8,128)(2,1)S(1)} %fusion, bf16[1024,256]{1,0:T(8,128)(2,1)S(1)} %collective-permute-done.15, bf16[1024,1024]{1,0:T(8,128)(2,1)} %copy-done, s32[]{:T(128)S(6)} %select_n.227), kind=kOutput, calls=%fused_computation.44 | convolution fusion | flops 537657344 | bytes 5242884 | tf_op jit(solution)/shard_map/dot_general | solution.py:147
  77.4 2.1 %collective-permute-start.16 = (f32[512,256]{1,0:T(8,128)}, f32[512,256]{1,0:T(8,128)}, u32[]{:S(2)}, u32[]{:S(2)}) collective-permute-start(f32[512,256]{1,0:T(8,128)} %slice.54), channel_id=1, source_target_pairs={{0,4},{4,0},{8,12},{12,8},{16,20},{20,16},{24,28},{28,24},{1,5},{5... | collective-permute-start | bytes 1572872 | tf_op jit(solution)/shard_map/ppermute | solution.py:161
  79.5 1.3 collective-permute-start.1
  80.8 2.9 %copy.5 = f32[512,1024]{0,1:T(8,128)} copy(f32[512,1024]{1,0:T(8,128)} %param.7) | data formatting | bytes 4194304 | tf_op args[3]
  83.8 3.1 %fusion.66 = (f32[512,2,256]{0,2,1:T(8,128)}, f32[512,2,256]{0,2,1:T(8,128)}) fusion(f32[512,2,512]{0,2,1:T(8,128)} %bitcast.25), kind=kLoop, calls=%fused_computation.97 | loop fusion | bytes 4194304 | tf_op jit(solution)/shard_map/slice | solution.py:163
  86.8 1.6 copy.8
  89.1 2.0 %collective-permute-done.16 = f32[512,256]{1,0:T(8,128)} collective-permute-done((f32[512,256]{1,0:T(8,128)}, f32[512,256]{1,0:T(8,128)}, u32[]{:S(2)}, u32[]{:S(2)}) %collective-permute-start.16) | collective-permute-done | bytes 524320 | tf_op jit(solution)/shard_map/ppermute | solution.py:161
  92.6 1.8 collective-permute-start.17
  94.4 1.3 collective-permute-start.5
  95.7 3.7 %collective-permute-done.17 = bf16[512,256]{1,0:T(8,128)(2,1)S(1)} collective-permute-done((bf16[512,256]{1,0:T(8,128)(2,1)S(1)}, bf16[512,256]{1,0:T(8,128)(2,1)S(1)}, u32[]{:S(2)}, u32[]{:S(2)}) %collective-permute-start.17) | collective-permute-done | bytes 262176 | tf_op jit(solution)/shard_map/ppermute | solution.py:167
  99.4 1.5 collective-permute-start.18
  101.7 6.7 %collective-permute-done.5 = bf16[256,1024]{1,0:T(8,128)(2,1)S(1)} collective-permute-done((bf16[256,1024]{1,0:T(8,128)(2,1)}, bf16[256,1024]{1,0:T(8,128)(2,1)S(1)}, u32[]{:S(2)}, u32[]{:S(2)}) %collective-permute-start.5) | collective-permute-done | bytes 524320 | tf_op jit(solution)/shard_map/ppermute | solution.py:104
  108.3 1.5 collective-permute-start.6
  110.9 1.3 broadcast_select_fusion.5
  112.2 8.8 %collective-permute-done.6 = bf16[256,1024]{1,0:T(8,128)(2,1)S(1)} collective-permute-done((bf16[256,1024]{1,0:T(8,128)(2,1)S(1)}, bf16[256,1024]{1,0:T(8,128)(2,1)S(1)}, u32[]{:S(2)}, u32[]{:S(2)}) %collective-permute-start.6) | collective-permute-done | bytes 524320 | tf_op jit(solution)/shard_map/ppermute | solution.py:104
  124.8 1.3 collective-permute-done.22
  126.9 1.5 collective-permute-start.23
  128.4 12.5 %collective-permute-done.23 = bf16[1024,256]{1,0:T(8,128)(2,1)S(1)} collective-permute-done((bf16[1024,256]{1,0:T(8,128)(2,1)S(1)}, bf16[1024,256]{1,0:T(8,128)(2,1)S(1)}, u32[]{:S(2)}, u32[]{:S(2)}) %collective-permute-start.23) | collective-permute-done | bytes 524320 | tf_op jit(solution)/shard_map/ppermute | solution.py:157
  142.7 1.6 copy.9
  144.4 10.6 %collective-permute-done.24 = f32[512,256]{1,0:T(8,128)S(1)} collective-permute-done((f32[512,256]{1,0:T(8,128)S(1)}, f32[512,256]{1,0:T(8,128)S(1)}, u32[]{:S(2)}, u32[]{:S(2)}) %collective-permute-start.24) | collective-permute-done | bytes 524320 | tf_op jit(solution)/shard_map/ppermute | solution.py:161
  156.2 5.8 %collective-permute-done.25 = bf16[512,256]{1,0:T(8,128)(2,1)S(1)} collective-permute-done((bf16[512,256]{1,0:T(8,128)(2,1)S(1)}, bf16[512,256]{1,0:T(8,128)(2,1)S(1)}, u32[]{:S(2)}, u32[]{:S(2)}) %collective-permute-start.25) | collective-permute-done | bytes 262176 | tf_op jit(solution)/shard_map/ppermute | solution.py:167
  162.0 1.5 collective-permute-start.26
  163.6 9.9 %collective-permute-done.26 = bf16[1024,256]{1,0:T(8,128)(2,1)} collective-permute-done((bf16[1024,256]{1,0:T(8,128)(2,1)S(1)}, bf16[1024,256]{1,0:T(8,128)(2,1)}, u32[]{:S(2)}, u32[]{:S(2)}) %collective-permute-start.26) | collective-permute-done | bytes 524320 | tf_op jit(solution)/shard_map/ppermute | solution.py:171
  173.7 1.4 copy-done.3
  175.8 3.8 %fusion.17 = f32[1024,1024]{1,0:T(8,128)S(1)} fusion(bf16[1024,256]{1,0:T(8,128)(2,1)} %collective-permute-done.28, bf16[1024,256]{1,0:T(8,128)(2,1)} %collective-permute-done.27, bf16[1024,256]{1,0:T(8,128)(2,1)} %collective-permute-done.26, bf16[512,256]{1,0:T(8,128)(2,1)S(1)} %collective-permute-done.25, bf16[512,256]{1,0:T(8,128)(2,1)S(1)} %get-tuple-element.31, ...), kind=kOutput, calls=%fused_computation.22 | convolution fusion | flops 2166358016 | bytes 8388608 | tf_op jit(solution)/shard_map/dot_general | solution.py:179
  179.7 3.7 %fusion.1 = f32[1024]{0:T(1024)S(1)} fusion(f32[1024,1024]{1,0:T(8,128)S(1)} %fusion.17, bf16[512,1024]{1,0:T(8,128)(2,1)} %collective-permute-done, bf16[512,1024]{1,0:T(8,128)(2,1)S(1)} %copy-done.8, bf16[256,1024]{1,0:T(8,128)(2,1)S(1)} %get-tuple-element.16, bf16[256,1024]{1,0:T(8,128)(2,1)S(1)} %get-tuple-element.17, ...), kind=kOutput, calls=%fused_computation.3 | convolution fusion | flops 2171599872 | bytes 10489856 | tf_op jit(solution)/shard_map/dot_general | solution.py:179
  184.2 2.8 %collective-permute-done.29 = f32[1024]{0:T(1024)S(1)} collective-permute-done((f32[1024]{0:T(1024)S(1)}, f32[1024]{0:T(1024)S(1)}, u32[]{:S(2)}, u32[]{:S(2)}) %collective-permute-start.29) | collective-permute-done | bytes 4128 | tf_op jit(solution)/shard_map/ppermute | solution.py:84
  187.6 3.0 %collective-permute-done.30 = f32[1024]{0:T(1024)S(1)} collective-permute-done((f32[1024]{0:T(1024)S(1)}, f32[1024]{0:T(1024)S(1)}, u32[]{:S(2)}, u32[]{:S(2)}) %collective-permute-start.30) | collective-permute-done | bytes 4128 | tf_op jit(solution)/shard_map/ppermute | solution.py:84
  190.7 4.5 %collective-permute-done.31 = f32[1024]{0:T(1024)S(1)} collective-permute-done((f32[1024]{0:T(1024)S(1)}, f32[1024]{0:T(1024)S(1)}, u32[]{:S(2)}, u32[]{:S(2)}) %collective-permute-start.31) | collective-permute-done | bytes 4128 | tf_op jit(solution)/shard_map/ppermute | solution.py:84
  (91 shorter events, 19.8 us)
Async XLA Ops:
  0.0 7.1 %copy-start.7 = (bf16[512,1024]{1,0:T(8,128)(2,1)S(1)}, bf16[512,1024]{1,0:T(8,128)(2,1)}, u32[]{:S(2)}) copy-start(bf16[512,1024]{1,0:T(8,128)(2,1)} %param.4) | copy-start | bytes 3145732
  0.0 31.9 %copy-start.11 = (f32[1024]{0:T(1024)S(1)}, f32[1024]{0:T(1024)}, u32[]{:S(2)}) copy-start(f32[1024]{0:T(1024)} %param.6) | copy-start | bytes 12292
  2.2 16.1 %collective-permute-start.8 = (bf16[256,1024]{1,0:T(8,128)(2,1)S(1)}, bf16[256,1024]{1,0:T(8,128)(2,1)S(1)}, u32[]{:S(2)}, u32[]{:S(2)}) collective-permute-start(bf16[256,1024]{1,0:T(8,128)(2,1)S(1)} %get-tuple-element.29), channel_id=1, source_target_pairs={{0,8},{4,12},{8,16},{12,20},{16,24},{20,28},{1,9},{5,13},{9,17},{1... | collective-permute-start | bytes 1572872 | tf_op jit(solution)/shard_map/ppermute | solution.py:104
  7.1 24.8 %collective-permute-start = (bf16[512,1024]{1,0:T(8,128)(2,1)S(1)}, bf16[512,1024]{1,0:T(8,128)(2,1)}, u32[]{:S(2)}, u32[]{:S(2)}) collective-permute-start(bf16[512,1024]{1,0:T(8,128)(2,1)S(1)} %copy-done.7), channel_id=1, source_target_pairs={{0,4},{4,0},{8,12},{12,8},{16,20},{20,16},{24,28},{28,24},{1,5},{5... | collective-permute-start | bytes 3145736 | tf_op jit(solution)/shard_map/ppermute | solution.py:135
  8.7 15.1 %collective-permute-start.7 = (bf16[256,1024]{1,0:T(8,128)(2,1)S(1)}, bf16[256,1024]{1,0:T(8,128)(2,1)}, u32[]{:S(2)}, u32[]{:S(2)}) collective-permute-start(bf16[256,1024]{1,0:T(8,128)(2,1)S(1)} %get-tuple-element.29), channel_id=1, source_target_pairs={{8,0},{12,4},{16,8},{20,12},{24,16},{28,20},{9,1},{13,5},{17,9},{2... | collective-permute-start | bytes 1572872 | tf_op jit(solution)/shard_map/ppermute | solution.py:104
  18.2 6.9 %collective-permute-start.9 = (bf16[256,1024]{1,0:T(8,128)(2,1)S(1)}, bf16[256,1024]{1,0:T(8,128)(2,1)}, u32[]{:S(2)}, u32[]{:S(2)}) collective-permute-start(bf16[256,1024]{1,0:T(8,128)(2,1)S(1)} %collective-permute-done.8), channel_id=1, source_target_pairs={{8,16},{12,20},{16,24},{20,28},{9,17},{13,21},{17,25},{21,29},{10,... | collective-permute-start | bytes 1572872 | tf_op jit(solution)/shard_map/ppermute | solution.py:104
  23.8 14.4 %collective-permute-start.11 = (bf16[256,1024]{1,0:T(8,128)(2,1)}, bf16[256,1024]{1,0:T(8,128)(2,1)}, u32[]{:S(2)}, u32[]{:S(2)}) collective-permute-start(bf16[256,1024]{1,0:T(8,128)(2,1)} %collective-permute-done.7), channel_id=1, source_target_pairs={{8,0},{12,4},{16,8},{20,12},{9,1},{13,5},{17,9},{21,13},{10,2},{14... | collective-permute-start | bytes 1572872 | tf_op jit(solution)/shard_map/ppermute | solution.py:104
  25.2 15.4 %collective-permute-start.10 = (bf16[256,1024]{1,0:T(8,128)(2,1)}, bf16[256,1024]{1,0:T(8,128)(2,1)S(1)}, u32[]{:S(2)}, u32[]{:S(2)}) collective-permute-start(bf16[256,1024]{1,0:T(8,128)(2,1)} %collective-permute-done.9), channel_id=1, source_target_pairs={{16,24},{20,28},{17,25},{21,29},{18,26},{22,30},{19,27},{23,31}} | collective-permute-start | bytes 1572872 | tf_op jit(solution)/shard_map/ppermute | solution.py:104
  38.2 13.3 %collective-permute-start.12 = (bf16[256,1024]{1,0:T(8,128)(2,1)}, bf16[256,1024]{1,0:T(8,128)(2,1)S(1)}, u32[]{:S(2)}, u32[]{:S(2)}) collective-permute-start(bf16[256,1024]{1,0:T(8,128)(2,1)} %collective-permute-done.11), channel_id=1, source_target_pairs={{8,0},{12,4},{9,1},{13,5},{10,2},{14,6},{11,3},{15,7}} | collective-permute-start | bytes 1572872 | tf_op jit(solution)/shard_map/ppermute | solution.py:104
  51.8 1.8 copy-start
  53.5 3.3 %collective-permute-start.14 = (f32[1024,256]{1,0:T(8,128)}, f32[1024,256]{1,0:T(8,128)S(1)}, u32[]{:S(2)}, u32[]{:S(2)}) collective-permute-start(f32[1024,256]{1,0:T(8,128)} %fusion.50), channel_id=1, source_target_pairs={{0,1},{1,0},{2,3},{3,2},{4,5},{5,4},{6,7},{7,6},{8,9},{9,8},{10,11... | collective-permute-start | bytes 3145736 | tf_op jit(solution)/shard_map/ppermute | solution.py:154
  56.3 7.0 %collective-permute-start.13 = (f32[1024,256]{1,0:T(8,128)}, f32[1024,256]{1,0:T(8,128)}, u32[]{:S(2)}, u32[]{:S(2)}) collective-permute-start(f32[1024,256]{1,0:T(8,128)} %fusion.53), channel_id=1, source_target_pairs={{0,1},{1,0},{2,3},{3,2},{4,5},{5,4},{6,7},{7,6},{8,9},{9,8},{10,11... | collective-permute-start | bytes 3145736 | tf_op jit(solution)/shard_map/ppermute | solution.py:154
  59.4 14.0 %collective-permute-start.15 = (bf16[1024,256]{1,0:T(8,128)(2,1)}, bf16[1024,256]{1,0:T(8,128)(2,1)S(1)}, u32[]{:S(2)}, u32[]{:S(2)}) collective-permute-start(bf16[1024,256]{1,0:T(8,128)(2,1)} %fusion.36), channel_id=1, source_target_pairs={{0,2},{1,3},{2,0},{3,1},{4,6},{5,7},{6,4},{7,5},{8,10},{9,11},{10,... | collective-permute-start | bytes 1572872 | tf_op jit(solution)/shard_map/ppermute | solution.py:157
  60.9 27.5 %collective-permute-start.2 = (bf16[256,1024]{1,0:T(8,128)(2,1)}, bf16[256,1024]{1,0:T(8,128)(2,1)}, u32[]{:S(2)}, u32[]{:S(2)}) collective-permute-start(bf16[256,1024]{1,0:T(8,128)(2,1)} %get-tuple-element.30), channel_id=1, source_target_pairs={{0,8},{4,12},{8,16},{12,20},{16,24},{20,28},{1,9},{5,13},{9,17},{1... | collective-permute-start | bytes 1572872 | tf_op jit(solution)/shard_map/ppermute | solution.py:104
  75.6 1.0 copy-start.4
  77.4 13.7 %collective-permute-start.16 = (f32[512,256]{1,0:T(8,128)}, f32[512,256]{1,0:T(8,128)}, u32[]{:S(2)}, u32[]{:S(2)}) collective-permute-start(f32[512,256]{1,0:T(8,128)} %slice.54), channel_id=1, source_target_pairs={{0,4},{4,0},{8,12},{12,8},{16,20},{20,16},{24,28},{28,24},{1,5},{5... | collective-permute-start | bytes 1572872 | tf_op jit(solution)/shard_map/ppermute | solution.py:161
  79.5 14.9 %collective-permute-start.1 = (bf16[256,1024]{1,0:T(8,128)(2,1)}, bf16[256,1024]{1,0:T(8,128)(2,1)}, u32[]{:S(2)}, u32[]{:S(2)}) collective-permute-start(bf16[256,1024]{1,0:T(8,128)(2,1)} %get-tuple-element.30), channel_id=1, source_target_pairs={{8,0},{12,4},{16,8},{20,12},{24,16},{28,20},{9,1},{13,5},{17,9},{2... | collective-permute-start | bytes 1572872 | tf_op jit(solution)/shard_map/ppermute | solution.py:104
  88.4 12.6 %collective-permute-start.3 = (bf16[256,1024]{1,0:T(8,128)(2,1)}, bf16[256,1024]{1,0:T(8,128)(2,1)S(1)}, u32[]{:S(2)}, u32[]{:S(2)}) collective-permute-start(bf16[256,1024]{1,0:T(8,128)(2,1)} %collective-permute-done.2), channel_id=1, source_target_pairs={{8,16},{12,20},{16,24},{20,28},{9,17},{13,21},{17,25},{21,29},{10,... | collective-permute-start | bytes 1572872 | tf_op jit(solution)/shard_map/ppermute | solution.py:104
  92.6 6.8 %collective-permute-start.17 = (bf16[512,256]{1,0:T(8,128)(2,1)S(1)}, bf16[512,256]{1,0:T(8,128)(2,1)S(1)}, u32[]{:S(2)}, u32[]{:S(2)}) collective-permute-start(bf16[512,256]{1,0:T(8,128)(2,1)S(1)} %get-tuple-element.34), channel_id=1, source_target_pairs={{0,4},{4,0},{8,12},{12,8},{16,20},{20,16},{24,28},{28,24},{1,5},{5... | collective-permute-start | bytes 786440 | tf_op jit(solution)/shard_map/ppermute | solution.py:167
  94.4 13.9 %collective-permute-start.5 = (bf16[256,1024]{1,0:T(8,128)(2,1)}, bf16[256,1024]{1,0:T(8,128)(2,1)S(1)}, u32[]{:S(2)}, u32[]{:S(2)}) collective-permute-start(bf16[256,1024]{1,0:T(8,128)(2,1)} %collective-permute-done.1), channel_id=1, source_target_pairs={{8,0},{12,4},{16,8},{20,12},{9,1},{13,5},{17,9},{21,13},{10,2},{14... | collective-permute-start | bytes 1572872 | tf_op jit(solution)/shard_map/ppermute | solution.py:104
  99.4 21.7 %copy-start.9 = (bf16[1024,256]{1,0:T(8,128)(2,1)}, bf16[1024,256]{1,0:T(8,128)(2,1)S(1)}, u32[]{:S(2)}) copy-start(bf16[1024,256]{1,0:T(8,128)(2,1)S(1)} %pad_maximum_fusion.3) | copy-start | bytes 1572868
  99.4 11.5 %collective-permute-start.18 = (bf16[1024,256]{1,0:T(8,128)(2,1)S(1)}, bf16[1024,256]{1,0:T(8,128)(2,1)S(1)}, u32[]{:S(2)}, u32[]{:S(2)}) collective-permute-start(bf16[1024,256]{1,0:T(8,128)(2,1)S(1)} %pad_maximum_fusion.3), channel_id=1, source_target_pairs={{0,2},{1,3},{2,0},{3,1},{4,6},{5,7},{6,4},{7,5},{8,10},{9,11},{10,... | collective-permute-start | bytes 1572872 | tf_op jit(solution)/shard_map/ppermute | solution.py:171
  101.0 10.0 %collective-permute-start.4 = (bf16[256,1024]{1,0:T(8,128)(2,1)S(1)}, bf16[256,1024]{1,0:T(8,128)(2,1)S(1)}, u32[]{:S(2)}, u32[]{:S(2)}) collective-permute-start(bf16[256,1024]{1,0:T(8,128)(2,1)S(1)} %collective-permute-done.3), channel_id=1, source_target_pairs={{16,24},{20,28},{17,25},{21,29},{18,26},{22,30},{19,27},{23,31}} | collective-permute-start | bytes 1572872 | tf_op jit(solution)/shard_map/ppermute | solution.py:104
  108.3 12.7 %collective-permute-start.6 = (bf16[256,1024]{1,0:T(8,128)(2,1)S(1)}, bf16[256,1024]{1,0:T(8,128)(2,1)S(1)}, u32[]{:S(2)}, u32[]{:S(2)}) collective-permute-start(bf16[256,1024]{1,0:T(8,128)(2,1)S(1)} %collective-permute-done.5), channel_id=1, source_target_pairs={{8,0},{12,4},{9,1},{13,5},{10,2},{14,6},{11,3},{15,7}} | collective-permute-start | bytes 1572872 | tf_op jit(solution)/shard_map/ppermute | solution.py:104
  109.9 12.5 %collective-permute-start.19 = (bf16[1024,256]{1,0:T(8,128)(2,1)S(1)}, bf16[1024,256]{1,0:T(8,128)(2,1)S(1)}, u32[]{:S(2)}, u32[]{:S(2)}) collective-permute-start(bf16[1024,256]{1,0:T(8,128)(2,1)S(1)} %pad_maximum_fusion.3), channel_id=1, source_target_pairs={{0,1},{1,0},{2,3},{3,2},{4,5},{5,4},{6,7},{7,6},{8,9},{9,8},{10,11... | collective-permute-start | bytes 1572872 | tf_op jit(solution)/shard_map/ppermute | solution.py:172
  110.9 11.4 %copy-start.12 = (bf16[1024,256]{1,0:T(8,128)(2,1)}, bf16[1024,256]{1,0:T(8,128)(2,1)S(1)}, u32[]{:S(2)}) copy-start(bf16[1024,256]{1,0:T(8,128)(2,1)S(1)} %collective-permute-done.18) | copy-start | bytes 1572868
  110.9 11.5 %collective-permute-start.20 = (bf16[1024,256]{1,0:T(8,128)(2,1)S(1)}, bf16[1024,256]{1,0:T(8,128)(2,1)S(1)}, u32[]{:S(2)}, u32[]{:S(2)}) collective-permute-start(bf16[1024,256]{1,0:T(8,128)(2,1)S(1)} %collective-permute-done.18), channel_id=1, source_target_pairs={{0,1},{1,0},{2,3},{3,2},{4,5},{5,4},{6,7},{7,6},{8,9},{9,8},{10,11... | collective-permute-start | bytes 1572872 | tf_op jit(solution)/shard_map/ppermute | solution.py:172
  122.4 18.6 %copy-start.2 = (bf16[1024,1024]{1,0:T(8,128)(2,1)}, bf16[1024,1024]{1,0:T(8,128)(2,1)S(1)}, u32[]{:S(2)}) copy-start(bf16[1024,1024]{1,0:T(8,128)(2,1)S(1)} %pad_maximum_fusion.1) | copy-start | bytes 6291460
  122.4 1.1 copy-start.16
  123.5 2.7 %collective-permute-start.22 = (f32[1024,256]{1,0:T(8,128)S(1)}, f32[1024,256]{1,0:T(8,128)S(1)}, u32[]{:S(2)}, u32[]{:S(2)}) collective-permute-start(f32[1024,256]{1,0:T(8,128)S(1)} %fusion.44), channel_id=1, source_target_pairs={{0,1},{1,0},{2,3},{3,2},{4,5},{5,4},{6,7},{7,6},{8,9},{9,8},{10,11... | collective-permute-start | bytes 3145736 | tf_op jit(solution)/shard_map/ppermute | solution.py:154
  124.2 4.2 %collective-permute-start.21 = (f32[1024,256]{1,0:T(8,128)S(1)}, f32[1024,256]{1,0:T(8,128)S(1)}, u32[]{:S(2)}, u32[]{:S(2)}) collective-permute-start(f32[1024,256]{1,0:T(8,128)S(1)} %fusion.47), channel_id=1, source_target_pairs={{0,1},{1,0},{2,3},{3,2},{4,5},{5,4},{6,7},{7,6},{8,9},{9,8},{10,11... | collective-permute-start | bytes 3145736 | tf_op jit(solution)/shard_map/ppermute | solution.py:154
  126.9 14.0 %collective-permute-start.23 = (bf16[1024,256]{1,0:T(8,128)(2,1)S(1)}, bf16[1024,256]{1,0:T(8,128)(2,1)S(1)}, u32[]{:S(2)}, u32[]{:S(2)}) collective-permute-start(bf16[1024,256]{1,0:T(8,128)(2,1)S(1)} %fusion.37), channel_id=1, source_target_pairs={{0,2},{1,3},{2,0},{3,1},{4,6},{5,7},{6,4},{7,5},{8,10},{9,11},{10,... | collective-permute-start | bytes 1572872 | tf_op jit(solution)/shard_map/ppermute | solution.py:157
  141.8 13.2 %collective-permute-start.24 = (f32[512,256]{1,0:T(8,128)S(1)}, f32[512,256]{1,0:T(8,128)S(1)}, u32[]{:S(2)}, u32[]{:S(2)}) collective-permute-start(f32[512,256]{1,0:T(8,128)S(1)} %slice.59), channel_id=1, source_target_pairs={{0,4},{4,0},{8,12},{12,8},{16,20},{20,16},{24,28},{28,24},{1,5},{5... | collective-permute-start | bytes 1572872 | tf_op jit(solution)/shard_map/ppermute | solution.py:161
  142.7 12.3 %copy-start.6 = (f32[1024,256]{1,0:T(8,128)S(1)}, f32[1024,256]{1,0:T(8,128)}, u32[]{:S(2)}) copy-start(f32[1024,256]{1,0:T(8,128)} %copy-done.5) | copy-start | bytes 3145732
  155.1 18.4 %copy-start.1 = (bf16[1024,1024]{1,0:T(8,128)(2,1)S(1)}, bf16[1024,1024]{1,0:T(8,128)(2,1)}, u32[]{:S(2)}) copy-start(bf16[1024,1024]{1,0:T(8,128)(2,1)} %copy-done) | copy-start | bytes 6291460
  155.3 6.7 %collective-permute-start.25 = (bf16[512,256]{1,0:T(8,128)(2,1)S(1)}, bf16[512,256]{1,0:T(8,128)(2,1)S(1)}, u32[]{:S(2)}, u32[]{:S(2)}) collective-permute-start(bf16[512,256]{1,0:T(8,128)(2,1)S(1)} %get-tuple-element.32), channel_id=1, source_target_pairs={{0,4},{4,0},{8,12},{12,8},{16,20},{20,16},{24,28},{28,24},{1,5},{5... | collective-permute-start | bytes 786440 | tf_op jit(solution)/shard_map/ppermute | solution.py:167
  162.0 11.5 %collective-permute-start.26 = (bf16[1024,256]{1,0:T(8,128)(2,1)S(1)}, bf16[1024,256]{1,0:T(8,128)(2,1)}, u32[]{:S(2)}, u32[]{:S(2)}) collective-permute-start(bf16[1024,256]{1,0:T(8,128)(2,1)S(1)} %pad_maximum_fusion.4), channel_id=1, source_target_pairs={{0,2},{1,3},{2,0},{3,1},{4,6},{5,7},{6,4},{7,5},{8,10},{9,11},{10,... | collective-permute-start | bytes 1572872 | tf_op jit(solution)/shard_map/ppermute | solution.py:171
  163.5 11.7 %collective-permute-start.27 = (bf16[1024,256]{1,0:T(8,128)(2,1)S(1)}, bf16[1024,256]{1,0:T(8,128)(2,1)}, u32[]{:S(2)}, u32[]{:S(2)}) collective-permute-start(bf16[1024,256]{1,0:T(8,128)(2,1)S(1)} %pad_maximum_fusion.4), channel_id=1, source_target_pairs={{0,1},{1,0},{2,3},{3,2},{4,5},{5,4},{6,7},{7,6},{8,9},{9,8},{10,11... | collective-permute-start | bytes 1572872 | tf_op jit(solution)/shard_map/ppermute | solution.py:172
  173.5 2.3 %collective-permute-start.28 = (bf16[1024,256]{1,0:T(8,128)(2,1)}, bf16[1024,256]{1,0:T(8,128)(2,1)}, u32[]{:S(2)}, u32[]{:S(2)}) collective-permute-start(bf16[1024,256]{1,0:T(8,128)(2,1)} %collective-permute-done.26), channel_id=1, source_target_pairs={{0,1},{1,0},{2,3},{3,2},{4,5},{5,4},{6,7},{7,6},{8,9},{9,8},{10,11... | collective-permute-start | bytes 1572872 | tf_op jit(solution)/shard_map/ppermute | solution.py:172
  173.5 1.6 copy-start.3
  175.8 3.9 %copy-start.8 = (bf16[512,1024]{1,0:T(8,128)(2,1)S(1)}, bf16[512,1024]{1,0:T(8,128)(2,1)}, u32[]{:S(2)}) copy-start(bf16[512,1024]{1,0:T(8,128)(2,1)} %param.4) | copy-start | bytes 3145732
  175.8 3.9 %copy-start.10 = (bf16[1024,256]{1,0:T(8,128)(2,1)S(1)}, bf16[1024,256]{1,0:T(8,128)(2,1)}, u32[]{:S(2)}) copy-start(bf16[1024,256]{1,0:T(8,128)(2,1)} %copy-done.9) | copy-start | bytes 1572868
  175.8 3.9 %copy-start.13 = (bf16[1024,256]{1,0:T(8,128)(2,1)S(1)}, bf16[1024,256]{1,0:T(8,128)(2,1)}, u32[]{:S(2)}) copy-start(bf16[1024,256]{1,0:T(8,128)(2,1)} %copy-done.12) | copy-start | bytes 1572868
  175.8 3.9 %copy-start.15 = (bf16[1024,256]{1,0:T(8,128)(2,1)S(1)}, bf16[1024,256]{1,0:T(8,128)(2,1)}, u32[]{:S(2)}) copy-start(bf16[1024,256]{1,0:T(8,128)(2,1)} %copy-done.14) | copy-start | bytes 1572868
  175.8 3.9 %copy-start.17 = (bf16[1024,256]{1,0:T(8,128)(2,1)S(1)}, bf16[1024,256]{1,0:T(8,128)(2,1)}, u32[]{:S(2)}) copy-start(bf16[1024,256]{1,0:T(8,128)(2,1)} %copy-done.16) | copy-start | bytes 1572868
  183.4 3.7 %collective-permute-start.29 = (f32[1024]{0:T(1024)S(1)}, f32[1024]{0:T(1024)S(1)}, u32[]{:S(2)}, u32[]{:S(2)}) collective-permute-start(f32[1024]{0:T(1024)S(1)} %fusion.1), channel_id=1, source_target_pairs={{0,4},{4,0},{8,12},{12,8},{16,20},{20,16},{24,28},{28,24},{1,5},{5... | collective-permute-start | bytes 12296 | tf_op jit(solution)/shard_map/ppermute | solution.py:84
  187.0 3.6 %collective-permute-start.30 = (f32[1024]{0:T(1024)S(1)}, f32[1024]{0:T(1024)S(1)}, u32[]{:S(2)}, u32[]{:S(2)}) collective-permute-start(f32[1024]{0:T(1024)S(1)} %add.195), channel_id=1, source_target_pairs={{0,8},{4,12},{8,0},{12,4},{16,24},{20,28},{24,16},{28,20},{1,9},{5... | collective-permute-start | bytes 12296 | tf_op jit(solution)/shard_map/ppermute | solution.py:84
  190.6 4.5 %collective-permute-start.31 = (f32[1024]{0:T(1024)S(1)}, f32[1024]{0:T(1024)S(1)}, u32[]{:S(2)}, u32[]{:S(2)}) collective-permute-start(f32[1024]{0:T(1024)S(1)} %add.196), channel_id=1, source_target_pairs={{0,16},{4,20},{8,24},{12,28},{16,0},{20,4},{24,8},{28,12},{1,17},{... | collective-permute-start | bytes 12296 | tf_op jit(solution)/shard_map/ppermute | solution.py:84
  (2 other events, 1.8 us)

commit v18 on v17

--- a/solution.py
+++ b/solution.py
@@ -158,7 +158,8 @@
                 halves[k].astype(jnp.bfloat16), "vox", chip_perm(k)
             ).astype(jnp.float32)
 
-        own, theirs = share[:sl], lax.ppermute(share[sl:], "src", swap)
+        own = share[:sl]
+        theirs = lax.ppermute(share[sl:].astype(jnp.bfloat16), "src", swap).astype(jnp.float32)
         pred = jnp.stack([jnp.where(first, own, theirs), jnp.where(first, theirs, own)], axis=1)
         w_c = weight[:, :, c * r:(c + 1) * r]
         wt = (w_c * pred).astype(jnp.bfloat16)

time: 197 us -> 185 us (0.939)
  waiting for transfers between devices: 116 us -> 106 us
  local copies, waits for them, and re-layouts: 15.3 us -> 13 us
    ppermute x2, waiting for transfers between devices: 12.6 us -> 7.06 us  [_fast(): lax.ppermute(share[sl:].astype(jnp.bfloat16), 'src', swap)]
    ppermute x2, waiting for transfers between devices: 22.7 us -> 18.4 us  [_fast(): lax.ppermute(halves[k].astype(jnp.bfloat16), 'vox', chip_perm(k))]
    unnamed x39 -> x41, local copies, waits for them, and re-layouts: 8.84 us -> 8.85 us
where the time goes in v18:
time: 185 us; the launch traced here: 184 us
  waiting for transfers between devices  106 us (57%)
  starting transfers between devices  34.9 us (19%)
  matrix products  19.9 us (11%)
  local copies, waits for them, and re-layouts  13 us (7%)
  other arithmetic  9.6 us (5%)
    ppermute x12, waiting for transfers between devices, _zline(): cur = lax.ppermute(cur, 'src', pairs)  41.7 us
    ppermute x12, starting transfers between devices, _zline(): cur = lax.ppermute(cur, 'src', pairs)  18.7 us
    ppermute x2, waiting for transfers between devices, _fast(): lax.ppermute(halves[k].astype(jnp.bfloat16), 'vox', chip_perm(k))  18.4 us
    dot_general x8, matrix products, pblock(): lax.dot_general(scaled, rows(col, blk), (((1,), (1,)), ((), ())), preferr...  12.4 us
    ppermute x2, waiting for transfers between devices, _fast(): lax.ppermute(piece, 'vox', chip_perm(k))  11.1 us
    ppermute x3, waiting for transfers between devices, _sum_over_src(): v = v + lax.ppermute(v, 'src', [(i, i ^ b) for i in range(n)])  10.3 us
    ppermute x2, waiting for transfers between devices, _fast(): piece = jnp.concatenate([mine, lax.ppermute(other, 'src', swap)], axis=0)  9.56 us
    unnamed x41, local copies, waits for them, and re-layouts  8.85 us
  transfers between devices with their start and end apart: 32, of which 20 were waited for; matrix products, arithmetic and copies ran while one was open for 14% of the time, Pallas kernels for 0%

profile of v18, /device:TPU:0, one launch (start us, length us, event | category | flops | bytes accessed | tf_op | source)
XLA Modules:
  0.0 183.9 jit_solution(5239784048418628657)
XLA Ops:
  0.0 2.2 %fusion.71 = (bf16[256,1024]{1,0:T(8,128)(2,1)S(1)}, bf16[256,1024]{1,0:T(8,128)(2,1)}) fusion(bf16[512,1024]{1,0:T(8,128)(2,1)} %param.5), kind=kLoop, calls=%fused_computation.104 | loop fusion | bytes 2097152 | tf_op jit(solution)/shard_map/slice | solution.py:142
  2.2 4.9 %collective-permute-start.8 = (bf16[256,1024]{1,0:T(8,128)(2,1)S(1)}, bf16[256,1024]{1,0:T(8,128)(2,1)S(1)}, u32[]{:S(2)}, u32[]{:S(2)}) collective-permute-start(bf16[256,1024]{1,0:T(8,128)(2,1)S(1)} %get-tuple-element.29), channel_id=1, source_target_pairs={{0,8},{4,12},{8,16},{12,20},{16,24},{20,28},{1,9},{5,13},{9,17},{1... | collective-permute-start | bytes 1572872 | tf_op jit(solution)/shard_map/ppermute | solution.py:104
  7.2 1.6 collective-permute-start
  8.8 1.3 collective-permute-start.7
  10.0 8.2 %collective-permute-done.8 = bf16[256,1024]{1,0:T(8,128)(2,1)S(1)} collective-permute-done((bf16[256,1024]{1,0:T(8,128)(2,1)S(1)}, bf16[256,1024]{1,0:T(8,128)(2,1)S(1)}, u32[]{:S(2)}, u32[]{:S(2)}) %collective-permute-start.8) | collective-permute-done | bytes 524320 | tf_op jit(solution)/shard_map/ppermute | solution.py:104
  18.3 1.4 collective-permute-start.9
  19.7 4.1 %collective-permute-done.7 = bf16[256,1024]{1,0:T(8,128)(2,1)} collective-permute-done((bf16[256,1024]{1,0:T(8,128)(2,1)S(1)}, bf16[256,1024]{1,0:T(8,128)(2,1)}, u32[]{:S(2)}, u32[]{:S(2)}) %collective-permute-start.7) | collective-permute-done | bytes 524320 | tf_op jit(solution)/shard_map/ppermute | solution.py:104
  23.8 1.3 collective-permute-start.11
  25.9 6.0 %collective-permute-done = bf16[512,1024]{1,0:T(8,128)(2,1)} collective-permute-done((bf16[512,1024]{1,0:T(8,128)(2,1)S(1)}, bf16[512,1024]{1,0:T(8,128)(2,1)}, u32[]{:S(2)}, u32[]{:S(2)}) %collective-permute-start) | collective-permute-done | bytes 1048608 | tf_op jit(solution)/shard_map/ppermute | solution.py:135
  32.0 2.1 %fusion = bf16[1024,1024]{1,0:T(8,128)(2,1)S(1)} fusion(f32[1024]{0:T(1024)S(1)} %copy-done.12, bf16[512,1024]{1,0:T(8,128)(2,1)} %collective-permute-done, bf16[512,1024]{1,0:T(8,128)(2,1)} %param.4), kind=kLoop, calls=%fused_computation.2 | loop fusion | flops 6291456 | bytes 4198400 | tf_op jit(solution)/shard_map/convert_element_type | solution.py:138
  34.1 4.1 %collective-permute-done.11 = bf16[256,1024]{1,0:T(8,128)(2,1)} collective-permute-done((bf16[256,1024]{1,0:T(8,128)(2,1)}, bf16[256,1024]{1,0:T(8,128)(2,1)}, u32[]{:S(2)}, u32[]{:S(2)}) %collective-permute-start.11) | collective-permute-done | bytes 524320 | tf_op jit(solution)/shard_map/ppermute | solution.py:104
  38.2 1.3 collective-permute-start.12
  41.8 9.8 %collective-permute-done.12 = bf16[256,1024]{1,0:T(8,128)(2,1)S(1)} collective-permute-done((bf16[256,1024]{1,0:T(8,128)(2,1)}, bf16[256,1024]{1,0:T(8,128)(2,1)S(1)}, u32[]{:S(2)}, u32[]{:S(2)}) %collective-permute-start.12) | collective-permute-done | bytes 524320 | tf_op jit(solution)/shard_map/ppermute | solution.py:104
  51.8 1.7 fusion.54
  53.6 2.8 %fusion.57 = f32[1024,256]{1,0:T(8,128)} fusion(bf16[1024,1024]{1,0:T(8,128)(2,1)S(1)} %fusion, bf16[1024,1024]{1,0:T(8,128)(2,1)} %copy-done, s32[]{:T(128)S(6)} %select_n.229), kind=kOutput, calls=%fused_computation.72 | convolution fusion | flops 536870912 | bytes 3670020 | tf_op jit(solution)/shard_map/dot_general | solution.py:147
  56.8 2.7 %fusion.36 = bf16[1024,256]{1,0:T(8,128)(2,1)} fusion(f32[1024,256]{1,0:T(8,128)S(1)} %collective-permute-done.14, bf16[1024,1024]{1,0:T(8,128)(2,1)S(1)} %fusion, bf16[1024,1024]{1,0:T(8,128)(2,1)} %copy-done, s32[]{:T(128)S(6)} %select_n.232), kind=kOutput, calls=%fused_computation.45 | convolution fusion | flops 537395200 | bytes 4194308 | tf_op jit(solution)/shard_map/dot_general | solution.py:147
  59.5 1.5 collective-permute-start.15
  61.0 2.3 %collective-permute-start.2 = (bf16[256,1024]{1,0:T(8,128)(2,1)}, bf16[256,1024]{1,0:T(8,128)(2,1)}, u32[]{:S(2)}, u32[]{:S(2)}) collective-permute-start(bf16[256,1024]{1,0:T(8,128)(2,1)} %get-tuple-element.30), channel_id=1, source_target_pairs={{0,8},{4,12},{8,16},{12,20},{16,24},{20,28},{1,9},{5,13},{9,17},{1... | collective-permute-start | bytes 1572872 | tf_op jit(solution)/shard_map/ppermute | solution.py:104
  63.3 1.3 collective-permute-start.1
  64.7 2.9 %copy.5 = f32[512,1024]{0,1:T(8,128)} copy(f32[512,1024]{1,0:T(8,128)} %param.7) | data formatting | bytes 4194304 | tf_op args[3]
  67.6 6.0 %collective-permute-done.15 = bf16[1024,256]{1,0:T(8,128)(2,1)S(1)} collective-permute-done((bf16[1024,256]{1,0:T(8,128)(2,1)}, bf16[1024,256]{1,0:T(8,128)(2,1)S(1)}, u32[]{:S(2)}, u32[]{:S(2)}) %collective-permute-start.15) | collective-permute-done | bytes 524320 | tf_op jit(solution)/shard_map/ppermute | solution.py:157
  73.5 2.1 %fusion.35 = f32[1024,256]{1,0:T(8,128)S(1)} fusion(f32[1024,256]{1,0:T(8,128)} %collective-permute-done.13, bf16[1024,1024]{1,0:T(8,128)(2,1)S(1)} %fusion, bf16[1024,256]{1,0:T(8,128)(2,1)S(1)} %collective-permute-done.15, bf16[1024,1024]{1,0:T(8,128)(2,1)} %copy-done, s32[]{:T(128)S(6)} %select_n.227), kind=kOutput, calls=%fused_computation.44 | convolution fusion | flops 537657344 | bytes 5242884 | tf_op jit(solution)/shard_map/dot_general | solution.py:147
  76.7 2.2 %collective-permute-start.16 = (bf16[512,256]{1,0:T(8,128)(2,1)S(1)}, bf16[512,256]{1,0:T(8,128)(2,1)}, u32[]{:S(2)}, u32[]{:S(2)}) collective-permute-start(bf16[512,256]{1,0:T(8,128)(2,1)S(1)} %slice.79), channel_id=1, source_target_pairs={{0,4},{4,0},{8,12},{12,8},{16,20},{20,16},{24,28},{28,24},{1,5},{5... | collective-permute-start | bytes 786440 | tf_op jit(solution)/shard_map/ppermute | solution.py:162
  78.9 1.5 fusion.70
  80.4 1.6 copy.8
  82.7 2.0 %collective-permute-done.16 = bf16[512,256]{1,0:T(8,128)(2,1)} collective-permute-done((bf16[512,256]{1,0:T(8,128)(2,1)S(1)}, bf16[512,256]{1,0:T(8,128)(2,1)}, u32[]{:S(2)}, u32[]{:S(2)}) %collective-permute-start.16) | collective-permute-done | bytes 262176 | tf_op jit(solution)/shard_map/ppermute | solution.py:162
  86.2 1.8 collective-permute-start.17
  88.0 1.3 collective-permute-start.5
  89.3 3.8 %collective-permute-done.17 = bf16[512,256]{1,0:T(8,128)(2,1)S(1)} collective-permute-done((bf16[512,256]{1,0:T(8,128)(2,1)S(1)}, bf16[512,256]{1,0:T(8,128)(2,1)S(1)}, u32[]{:S(2)}, u32[]{:S(2)}) %collective-permute-start.17) | collective-permute-done | bytes 262176 | tf_op jit(solution)/shard_map/ppermute | solution.py:168
  93.1 1.6 collective-permute-start.18
  95.4 6.6 %collective-permute-done.5 = bf16[256,1024]{1,0:T(8,128)(2,1)S(1)} collective-permute-done((bf16[256,1024]{1,0:T(8,128)(2,1)}, bf16[256,1024]{1,0:T(8,128)(2,1)S(1)}, u32[]{:S(2)}, u32[]{:S(2)}) %collective-permute-start.5) | collective-permute-done | bytes 524320 | tf_op jit(solution)/shard_map/ppermute | solution.py:104
  101.9 1.5 collective-permute-start.6
  104.7 1.3 broadcast_select_fusion.5
  106.0 8.8 %collective-permute-done.6 = bf16[256,1024]{1,0:T(8,128)(2,1)S(1)} collective-permute-done((bf16[256,1024]{1,0:T(8,128)(2,1)S(1)}, bf16[256,1024]{1,0:T(8,128)(2,1)S(1)}, u32[]{:S(2)}, u32[]{:S(2)}) %collective-permute-start.6) | collective-permute-done | bytes 524320 | tf_op jit(solution)/shard_map/ppermute | solution.py:104
  118.5 1.3 collective-permute-done.22
  120.6 1.6 collective-permute-start.23
  122.2 12.5 %collective-permute-done.23 = bf16[1024,256]{1,0:T(8,128)(2,1)S(1)} collective-permute-done((bf16[1024,256]{1,0:T(8,128)(2,1)S(1)}, bf16[1024,256]{1,0:T(8,128)(2,1)S(1)}, u32[]{:S(2)}, u32[]{:S(2)}) %collective-permute-start.23) | collective-permute-done | bytes 524320 | tf_op jit(solution)/shard_map/ppermute | solution.py:157
  136.5 1.6 copy.9
  138.1 5.0 %collective-permute-done.24 = bf16[512,256]{1,0:T(8,128)(2,1)S(1)} collective-permute-done((bf16[512,256]{1,0:T(8,128)(2,1)S(1)}, bf16[512,256]{1,0:T(8,128)(2,1)S(1)}, u32[]{:S(2)}, u32[]{:S(2)}) %collective-permute-start.24) | collective-permute-done | bytes 262176 | tf_op jit(solution)/shard_map/ppermute | solution.py:162
  144.3 5.8 %collective-permute-done.25 = bf16[512,256]{1,0:T(8,128)(2,1)S(1)} collective-permute-done((bf16[512,256]{1,0:T(8,128)(2,1)S(1)}, bf16[512,256]{1,0:T(8,128)(2,1)S(1)}, u32[]{:S(2)}, u32[]{:S(2)}) %collective-permute-start.25) | collective-permute-done | bytes 262176 | tf_op jit(solution)/shard_map/ppermute | solution.py:168
  150.1 1.6 collective-permute-start.26
  151.7 9.9 %collective-permute-done.26 = bf16[1024,256]{1,0:T(8,128)(2,1)} collective-permute-done((bf16[1024,256]{1,0:T(8,128)(2,1)S(1)}, bf16[1024,256]{1,0:T(8,128)(2,1)}, u32[]{:S(2)}, u32[]{:S(2)}) %collective-permute-start.26) | collective-permute-done | bytes 524320 | tf_op jit(solution)/shard_map/ppermute | solution.py:172
  161.8 1.4 copy-done.3
  163.9 3.8 %fusion.17 = f32[1024,1024]{1,0:T(8,128)S(1)} fusion(bf16[1024,256]{1,0:T(8,128)(2,1)} %collective-permute-done.28, bf16[1024,256]{1,0:T(8,128)(2,1)} %collective-permute-done.27, bf16[1024,256]{1,0:T(8,128)(2,1)} %collective-permute-done.26, bf16[512,256]{1,0:T(8,128)(2,1)S(1)} %collective-permute-done.25, bf16[512,256]{1,0:T(8,128)(2,1)S(1)} %get-tuple-element.31, ...), kind=kOutput, calls=%fused_computation.22 | convolution fusion | flops 2166358016 | bytes 8388608 | tf_op jit(solution)/shard_map/dot_general | solution.py:180
  167.8 3.7 %fusion.1 = f32[1024]{0:T(1024)S(1)} fusion(f32[1024,1024]{1,0:T(8,128)S(1)} %fusion.17, bf16[512,1024]{1,0:T(8,128)(2,1)} %collective-permute-done, bf16[512,1024]{1,0:T(8,128)(2,1)S(1)} %copy-done.9, bf16[256,1024]{1,0:T(8,128)(2,1)S(1)} %get-tuple-element.16, bf16[256,1024]{1,0:T(8,128)(2,1)S(1)} %get-tuple-element.17, ...), kind=kOutput, calls=%fused_computation.3 | convolution fusion | flops 2171599872 | bytes 10489856 | tf_op jit(solution)/shard_map/dot_general | solution.py:180
  172.4 2.8 %collective-permute-done.29 = f32[1024]{0:T(1024)S(1)} collective-permute-done((f32[1024]{0:T(1024)S(1)}, f32[1024]{0:T(1024)S(1)}, u32[]{:S(2)}, u32[]{:S(2)}) %collective-permute-start.29) | collective-permute-done | bytes 4128 | tf_op jit(solution)/shard_map/ppermute | solution.py:84
  175.7 3.0 %collective-permute-done.30 = f32[1024]{0:T(1024)S(1)} collective-permute-done((f32[1024]{0:T(1024)S(1)}, f32[1024]{0:T(1024)S(1)}, u32[]{:S(2)}, u32[]{:S(2)}) %collective-permute-start.30) | collective-permute-done | bytes 4128 | tf_op jit(solution)/shard_map/ppermute | solution.py:84
  178.8 4.5 %collective-permute-done.31 = f32[1024]{0:T(1024)S(1)} collective-permute-done((f32[1024]{0:T(1024)S(1)}, f32[1024]{0:T(1024)S(1)}, u32[]{:S(2)}, u32[]{:S(2)}) %collective-permute-start.31) | collective-permute-done | bytes 4128 | tf_op jit(solution)/shard_map/ppermute | solution.py:84
  (93 shorter events, 19.2 us)
Async XLA Ops:
  0.0 7.2 %copy-start.8 = (bf16[512,1024]{1,0:T(8,128)(2,1)S(1)}, bf16[512,1024]{1,0:T(8,128)(2,1)}, u32[]{:S(2)}) copy-start(bf16[512,1024]{1,0:T(8,128)(2,1)} %param.4) | copy-start | bytes 3145732
  0.0 32.0 %copy-start.12 = (f32[1024]{0:T(1024)S(1)}, f32[1024]{0:T(1024)}, u32[]{:S(2)}) copy-start(f32[1024]{0:T(1024)} %param.6) | copy-start | bytes 12292
  2.2 16.1 %collective-permute-start.8 = (bf16[256,1024]{1,0:T(8,128)(2,1)S(1)}, bf16[256,1024]{1,0:T(8,128)(2,1)S(1)}, u32[]{:S(2)}, u32[]{:S(2)}) collective-permute-start(bf16[256,1024]{1,0:T(8,128)(2,1)S(1)} %get-tuple-element.29), channel_id=1, source_target_pairs={{0,8},{4,12},{8,16},{12,20},{16,24},{20,28},{1,9},{5,13},{9,17},{1... | collective-permute-start | bytes 1572872 | tf_op jit(solution)/shard_map/ppermute | solution.py:104
  7.2 24.8 %collective-permute-start = (bf16[512,1024]{1,0:T(8,128)(2,1)S(1)}, bf16[512,1024]{1,0:T(8,128)(2,1)}, u32[]{:S(2)}, u32[]{:S(2)}) collective-permute-start(bf16[512,1024]{1,0:T(8,128)(2,1)S(1)} %copy-done.8), channel_id=1, source_target_pairs={{0,4},{4,0},{8,12},{12,8},{16,20},{20,16},{24,28},{28,24},{1,5},{5... | collective-permute-start | bytes 3145736 | tf_op jit(solution)/shard_map/ppermute | solution.py:135
  8.8 15.1 %collective-permute-start.7 = (bf16[256,1024]{1,0:T(8,128)(2,1)S(1)}, bf16[256,1024]{1,0:T(8,128)(2,1)}, u32[]{:S(2)}, u32[]{:S(2)}) collective-permute-start(bf16[256,1024]{1,0:T(8,128)(2,1)S(1)} %get-tuple-element.29), channel_id=1, source_target_pairs={{8,0},{12,4},{16,8},{20,12},{24,16},{28,20},{9,1},{13,5},{17,9},{2... | collective-permute-start | bytes 1572872 | tf_op jit(solution)/shard_map/ppermute | solution.py:104
  18.3 6.9 %collective-permute-start.9 = (bf16[256,1024]{1,0:T(8,128)(2,1)S(1)}, bf16[256,1024]{1,0:T(8,128)(2,1)}, u32[]{:S(2)}, u32[]{:S(2)}) collective-permute-start(bf16[256,1024]{1,0:T(8,128)(2,1)S(1)} %collective-permute-done.8), channel_id=1, source_target_pairs={{8,16},{12,20},{16,24},{20,28},{9,17},{13,21},{17,25},{21,29},{10,... | collective-permute-start | bytes 1572872 | tf_op jit(solution)/shard_map/ppermute | solution.py:104
  23.8 14.4 %collective-permute-start.11 = (bf16[256,1024]{1,0:T(8,128)(2,1)}, bf16[256,1024]{1,0:T(8,128)(2,1)}, u32[]{:S(2)}, u32[]{:S(2)}) collective-permute-start(bf16[256,1024]{1,0:T(8,128)(2,1)} %collective-permute-done.7), channel_id=1, source_target_pairs={{8,0},{12,4},{16,8},{20,12},{9,1},{13,5},{17,9},{21,13},{10,2},{14... | collective-permute-start | bytes 1572872 | tf_op jit(solution)/shard_map/ppermute | solution.py:104
  25.2 15.4 %collective-permute-start.10 = (bf16[256,1024]{1,0:T(8,128)(2,1)}, bf16[256,1024]{1,0:T(8,128)(2,1)S(1)}, u32[]{:S(2)}, u32[]{:S(2)}) collective-permute-start(bf16[256,1024]{1,0:T(8,128)(2,1)} %collective-permute-done.9), channel_id=1, source_target_pairs={{16,24},{20,28},{17,25},{21,29},{18,26},{22,30},{19,27},{23,31}} | collective-permute-start | bytes 1572872 | tf_op jit(solution)/shard_map/ppermute | solution.py:104
  38.2 13.3 %collective-permute-start.12 = (bf16[256,1024]{1,0:T(8,128)(2,1)}, bf16[256,1024]{1,0:T(8,128)(2,1)S(1)}, u32[]{:S(2)}, u32[]{:S(2)}) collective-permute-start(bf16[256,1024]{1,0:T(8,128)(2,1)} %collective-permute-done.11), channel_id=1, source_target_pairs={{8,0},{12,4},{9,1},{13,5},{10,2},{14,6},{11,3},{15,7}} | collective-permute-start | bytes 1572872 | tf_op jit(solution)/shard_map/ppermute | solution.py:104
  51.8 1.8 copy-start
  53.6 3.3 %collective-permute-start.14 = (f32[1024,256]{1,0:T(8,128)}, f32[1024,256]{1,0:T(8,128)S(1)}, u32[]{:S(2)}, u32[]{:S(2)}) collective-permute-start(f32[1024,256]{1,0:T(8,128)} %fusion.54), channel_id=1, source_target_pairs={{0,1},{1,0},{2,3},{3,2},{4,5},{5,4},{6,7},{7,6},{8,9},{9,8},{10,11... | collective-permute-start | bytes 3145736 | tf_op jit(solution)/shard_map/ppermute | solution.py:154
  56.3 11.3 %collective-permute-start.13 = (f32[1024,256]{1,0:T(8,128)}, f32[1024,256]{1,0:T(8,128)}, u32[]{:S(2)}, u32[]{:S(2)}) collective-permute-start(f32[1024,256]{1,0:T(8,128)} %fusion.57), channel_id=1, source_target_pairs={{0,1},{1,0},{2,3},{3,2},{4,5},{5,4},{6,7},{7,6},{8,9},{9,8},{10,11... | collective-permute-start | bytes 3145736 | tf_op jit(solution)/shard_map/ppermute | solution.py:154
  59.5 14.0 %collective-permute-start.15 = (bf16[1024,256]{1,0:T(8,128)(2,1)}, bf16[1024,256]{1,0:T(8,128)(2,1)S(1)}, u32[]{:S(2)}, u32[]{:S(2)}) collective-permute-start(bf16[1024,256]{1,0:T(8,128)(2,1)} %fusion.36), channel_id=1, source_target_pairs={{0,2},{1,3},{2,0},{3,1},{4,6},{5,7},{6,4},{7,5},{8,10},{9,11},{10,... | collective-permute-start | bytes 1572872 | tf_op jit(solution)/shard_map/ppermute | solution.py:157
  61.0 21.0 %collective-permute-start.2 = (bf16[256,1024]{1,0:T(8,128)(2,1)}, bf16[256,1024]{1,0:T(8,128)(2,1)}, u32[]{:S(2)}, u32[]{:S(2)}) collective-permute-start(bf16[256,1024]{1,0:T(8,128)(2,1)} %get-tuple-element.30), channel_id=1, source_target_pairs={{0,8},{4,12},{8,16},{12,20},{16,24},{20,28},{1,9},{5,13},{9,17},{1... | collective-permute-start | bytes 1572872 | tf_op jit(solution)/shard_map/ppermute | solution.py:104
  63.3 24.6 %collective-permute-start.1 = (bf16[256,1024]{1,0:T(8,128)(2,1)}, bf16[256,1024]{1,0:T(8,128)(2,1)}, u32[]{:S(2)}, u32[]{:S(2)}) collective-permute-start(bf16[256,1024]{1,0:T(8,128)(2,1)} %get-tuple-element.30), channel_id=1, source_target_pairs={{8,0},{12,4},{16,8},{20,12},{24,16},{28,20},{9,1},{13,5},{17,9},{2... | collective-permute-start | bytes 1572872 | tf_op jit(solution)/shard_map/ppermute | solution.py:104
  67.6 11.3 %copy-start.4 = (f32[512,1024]{0,1:T(8,128)S(1)}, f32[512,1024]{0,1:T(8,128)}, u32[]{:S(2)}) copy-start(f32[512,1024]{0,1:T(8,128)} %copy.5) | copy-start | bytes 6291460
  76.7 8.0 %collective-permute-start.16 = (bf16[512,256]{1,0:T(8,128)(2,1)S(1)}, bf16[512,256]{1,0:T(8,128)(2,1)}, u32[]{:S(2)}, u32[]{:S(2)}) collective-permute-start(bf16[512,256]{1,0:T(8,128)(2,1)S(1)} %slice.79), channel_id=1, source_target_pairs={{0,4},{4,0},{8,12},{12,8},{16,20},{20,16},{24,28},{28,24},{1,5},{5... | collective-permute-start | bytes 786440 | tf_op jit(solution)/shard_map/ppermute | solution.py:162
  82.0 12.7 %collective-permute-start.3 = (bf16[256,1024]{1,0:T(8,128)(2,1)}, bf16[256,1024]{1,0:T(8,128)(2,1)S(1)}, u32[]{:S(2)}, u32[]{:S(2)}) collective-permute-start(bf16[256,1024]{1,0:T(8,128)(2,1)} %collective-permute-done.2), channel_id=1, source_target_pairs={{8,16},{12,20},{16,24},{20,28},{9,17},{13,21},{17,25},{21,29},{10,... | collective-permute-start | bytes 1572872 | tf_op jit(solution)/shard_map/ppermute | solution.py:104
  86.2 6.9 %collective-permute-start.17 = (bf16[512,256]{1,0:T(8,128)(2,1)S(1)}, bf16[512,256]{1,0:T(8,128)(2,1)S(1)}, u32[]{:S(2)}, u32[]{:S(2)}) collective-permute-start(bf16[512,256]{1,0:T(8,128)(2,1)S(1)} %get-tuple-element.34), channel_id=1, source_target_pairs={{0,4},{4,0},{8,12},{12,8},{16,20},{20,16},{24,28},{28,24},{1,5},{5... | collective-permute-start | bytes 786440 | tf_op jit(solution)/shard_map/ppermute | solution.py:168
  88.0 14.0 %collective-permute-start.5 = (bf16[256,1024]{1,0:T(8,128)(2,1)}, bf16[256,1024]{1,0:T(8,128)(2,1)S(1)}, u32[]{:S(2)}, u32[]{:S(2)}) collective-permute-start(bf16[256,1024]{1,0:T(8,128)(2,1)} %collective-permute-done.1), channel_id=1, source_target_pairs={{8,0},{12,4},{16,8},{20,12},{9,1},{13,5},{17,9},{21,13},{10,2},{14... | collective-permute-start | bytes 1572872 | tf_op jit(solution)/shard_map/ppermute | solution.py:104
  93.1 21.8 %copy-start.10 = (bf16[1024,256]{1,0:T(8,128)(2,1)}, bf16[1024,256]{1,0:T(8,128)(2,1)S(1)}, u32[]{:S(2)}) copy-start(bf16[1024,256]{1,0:T(8,128)(2,1)S(1)} %pad_maximum_fusion.3) | copy-start | bytes 1572868
  93.1 11.6 %collective-permute-start.18 = (bf16[1024,256]{1,0:T(8,128)(2,1)S(1)}, bf16[1024,256]{1,0:T(8,128)(2,1)S(1)}, u32[]{:S(2)}, u32[]{:S(2)}) collective-permute-start(bf16[1024,256]{1,0:T(8,128)(2,1)S(1)} %pad_maximum_fusion.3), channel_id=1, source_target_pairs={{0,2},{1,3},{2,0},{3,1},{4,6},{5,7},{6,4},{7,5},{8,10},{9,11},{10,... | collective-permute-start | bytes 1572872 | tf_op jit(solution)/shard_map/ppermute | solution.py:172
  94.7 10.0 %collective-permute-start.4 = (bf16[256,1024]{1,0:T(8,128)(2,1)S(1)}, bf16[256,1024]{1,0:T(8,128)(2,1)S(1)}, u32[]{:S(2)}, u32[]{:S(2)}) collective-permute-start(bf16[256,1024]{1,0:T(8,128)(2,1)S(1)} %collective-permute-done.3), channel_id=1, source_target_pairs={{16,24},{20,28},{17,25},{21,29},{18,26},{22,30},{19,27},{23,31}} | collective-permute-start | bytes 1572872 | tf_op jit(solution)/shard_map/ppermute | solution.py:104
  101.9 12.8 %collective-permute-start.6 = (bf16[256,1024]{1,0:T(8,128)(2,1)S(1)}, bf16[256,1024]{1,0:T(8,128)(2,1)S(1)}, u32[]{:S(2)}, u32[]{:S(2)}) collective-permute-start(bf16[256,1024]{1,0:T(8,128)(2,1)S(1)} %collective-permute-done.5), channel_id=1, source_target_pairs={{8,0},{12,4},{9,1},{13,5},{10,2},{14,6},{11,3},{15,7}} | collective-permute-start | bytes 1572872 | tf_op jit(solution)/shard_map/ppermute | solution.py:104
  103.5 12.6 %collective-permute-start.19 = (bf16[1024,256]{1,0:T(8,128)(2,1)S(1)}, bf16[1024,256]{1,0:T(8,128)(2,1)S(1)}, u32[]{:S(2)}, u32[]{:S(2)}) collective-permute-start(bf16[1024,256]{1,0:T(8,128)(2,1)S(1)} %pad_maximum_fusion.3), channel_id=1, source_target_pairs={{0,1},{1,0},{2,3},{3,2},{4,5},{5,4},{6,7},{7,6},{8,9},{9,8},{10,11... | collective-permute-start | bytes 1572872 | tf_op jit(solution)/shard_map/ppermute | solution.py:173
  104.7 11.4 %copy-start.13 = (bf16[1024,256]{1,0:T(8,128)(2,1)}, bf16[1024,256]{1,0:T(8,128)(2,1)S(1)}, u32[]{:S(2)}) copy-start(bf16[1024,256]{1,0:T(8,128)(2,1)S(1)} %collective-permute-done.18) | copy-start | bytes 1572868
  104.7 11.4 %collective-permute-start.20 = (bf16[1024,256]{1,0:T(8,128)(2,1)S(1)}, bf16[1024,256]{1,0:T(8,128)(2,1)S(1)}, u32[]{:S(2)}, u32[]{:S(2)}) collective-permute-start(bf16[1024,256]{1,0:T(8,128)(2,1)S(1)} %collective-permute-done.18), channel_id=1, source_target_pairs={{0,1},{1,0},{2,3},{3,2},{4,5},{5,4},{6,7},{7,6},{8,9},{9,8},{10,11... | collective-permute-start | bytes 1572872 | tf_op jit(solution)/shard_map/ppermute | solution.py:173
  116.1 18.6 %copy-start.2 = (bf16[1024,1024]{1,0:T(8,128)(2,1)}, bf16[1024,1024]{1,0:T(8,128)(2,1)S(1)}, u32[]{:S(2)}) copy-start(bf16[1024,1024]{1,0:T(8,128)(2,1)S(1)} %pad_maximum_fusion.1) | copy-start | bytes 6291460
  116.1 1.1 copy-start.17
  117.2 2.7 %collective-permute-start.22 = (f32[1024,256]{1,0:T(8,128)S(1)}, f32[1024,256]{1,0:T(8,128)S(1)}, u32[]{:S(2)}, u32[]{:S(2)}) collective-permute-start(f32[1024,256]{1,0:T(8,128)S(1)} %fusion.48), channel_id=1, source_target_pairs={{0,1},{1,0},{2,3},{3,2},{4,5},{5,4},{6,7},{7,6},{8,9},{9,8},{10,11... | collective-permute-start | bytes 3145736 | tf_op jit(solution)/shard_map/ppermute | solution.py:154
  118.0 4.3 %collective-permute-start.21 = (f32[1024,256]{1,0:T(8,128)S(1)}, f32[1024,256]{1,0:T(8,128)S(1)}, u32[]{:S(2)}, u32[]{:S(2)}) collective-permute-start(f32[1024,256]{1,0:T(8,128)S(1)} %fusion.51), channel_id=1, source_target_pairs={{0,1},{1,0},{2,3},{3,2},{4,5},{5,4},{6,7},{7,6},{8,9},{9,8},{10,11... | collective-permute-start | bytes 3145736 | tf_op jit(solution)/shard_map/ppermute | solution.py:154
  120.6 14.0 %collective-permute-start.23 = (bf16[1024,256]{1,0:T(8,128)(2,1)S(1)}, bf16[1024,256]{1,0:T(8,128)(2,1)S(1)}, u32[]{:S(2)}, u32[]{:S(2)}) collective-permute-start(bf16[1024,256]{1,0:T(8,128)(2,1)S(1)} %fusion.37), channel_id=1, source_target_pairs={{0,2},{1,3},{2,0},{3,1},{4,6},{5,7},{6,4},{7,5},{8,10},{9,11},{10,... | collective-permute-start | bytes 1572872 | tf_op jit(solution)/shard_map/ppermute | solution.py:157
  135.5 7.6 %collective-permute-start.24 = (bf16[512,256]{1,0:T(8,128)(2,1)S(1)}, bf16[512,256]{1,0:T(8,128)(2,1)S(1)}, u32[]{:S(2)}, u32[]{:S(2)}) collective-permute-start(bf16[512,256]{1,0:T(8,128)(2,1)S(1)} %slice.78), channel_id=1, source_target_pairs={{0,4},{4,0},{8,12},{12,8},{16,20},{20,16},{24,28},{28,24},{1,5},{5... | collective-permute-start | bytes 786440 | tf_op jit(solution)/shard_map/ppermute | solution.py:162
  136.5 6.7 %copy-start.7 = (f32[1024,256]{1,0:T(8,128)S(1)}, f32[1024,256]{1,0:T(8,128)}, u32[]{:S(2)}) copy-start(f32[1024,256]{1,0:T(8,128)} %copy-done.6) | copy-start | bytes 3145732
  143.2 18.4 %copy-start.1 = (bf16[1024,1024]{1,0:T(8,128)(2,1)S(1)}, bf16[1024,1024]{1,0:T(8,128)(2,1)}, u32[]{:S(2)}) copy-start(bf16[1024,1024]{1,0:T(8,128)(2,1)} %copy-done) | copy-start | bytes 6291460
  143.4 6.7 %collective-permute-start.25 = (bf16[512,256]{1,0:T(8,128)(2,1)S(1)}, bf16[512,256]{1,0:T(8,128)(2,1)S(1)}, u32[]{:S(2)}, u32[]{:S(2)}) collective-permute-start(bf16[512,256]{1,0:T(8,128)(2,1)S(1)} %get-tuple-element.32), channel_id=1, source_target_pairs={{0,4},{4,0},{8,12},{12,8},{16,20},{20,16},{24,28},{28,24},{1,5},{5... | collective-permute-start | bytes 786440 | tf_op jit(solution)/shard_map/ppermute | solution.py:168
  150.1 11.5 %collective-permute-start.26 = (bf16[1024,256]{1,0:T(8,128)(2,1)S(1)}, bf16[1024,256]{1,0:T(8,128)(2,1)}, u32[]{:S(2)}, u32[]{:S(2)}) collective-permute-start(bf16[1024,256]{1,0:T(8,128)(2,1)S(1)} %pad_maximum_fusion.4), channel_id=1, source_target_pairs={{0,2},{1,3},{2,0},{3,1},{4,6},{5,7},{6,4},{7,5},{8,10},{9,11},{10,... | collective-permute-start | bytes 1572872 | tf_op jit(solution)/shard_map/ppermute | solution.py:172
  151.7 11.7 %collective-permute-start.27 = (bf16[1024,256]{1,0:T(8,128)(2,1)S(1)}, bf16[1024,256]{1,0:T(8,128)(2,1)}, u32[]{:S(2)}, u32[]{:S(2)}) collective-permute-start(bf16[1024,256]{1,0:T(8,128)(2,1)S(1)} %pad_maximum_fusion.4), channel_id=1, source_target_pairs={{0,1},{1,0},{2,3},{3,2},{4,5},{5,4},{6,7},{7,6},{8,9},{9,8},{10,11... | collective-permute-start | bytes 1572872 | tf_op jit(solution)/shard_map/ppermute | solution.py:173
  161.6 2.3 %collective-permute-start.28 = (bf16[1024,256]{1,0:T(8,128)(2,1)}, bf16[1024,256]{1,0:T(8,128)(2,1)}, u32[]{:S(2)}, u32[]{:S(2)}) collective-permute-start(bf16[1024,256]{1,0:T(8,128)(2,1)} %collective-permute-done.26), channel_id=1, source_target_pairs={{0,1},{1,0},{2,3},{3,2},{4,5},{5,4},{6,7},{7,6},{8,9},{9,8},{10,11... | collective-permute-start | bytes 1572872 | tf_op jit(solution)/shard_map/ppermute | solution.py:173
  161.6 1.6 copy-start.3
  163.9 3.9 %copy-start.9 = (bf16[512,1024]{1,0:T(8,128)(2,1)S(1)}, bf16[512,1024]{1,0:T(8,128)(2,1)}, u32[]{:S(2)}) copy-start(bf16[512,1024]{1,0:T(8,128)(2,1)} %param.4) | copy-start | bytes 3145732
  163.9 3.9 %copy-start.11 = (bf16[1024,256]{1,0:T(8,128)(2,1)S(1)}, bf16[1024,256]{1,0:T(8,128)(2,1)}, u32[]{:S(2)}) copy-start(bf16[1024,256]{1,0:T(8,128)(2,1)} %copy-done.10) | copy-start | bytes 1572868
  163.9 3.9 %copy-start.14 = (bf16[1024,256]{1,0:T(8,128)(2,1)S(1)}, bf16[1024,256]{1,0:T(8,128)(2,1)}, u32[]{:S(2)}) copy-start(bf16[1024,256]{1,0:T(8,128)(2,1)} %copy-done.13) | copy-start | bytes 1572868
  163.9 3.9 %copy-start.16 = (bf16[1024,256]{1,0:T(8,128)(2,1)S(1)}, bf16[1024,256]{1,0:T(8,128)(2,1)}, u32[]{:S(2)}) copy-start(bf16[1024,256]{1,0:T(8,128)(2,1)} %copy-done.15) | copy-start | bytes 1572868
  163.9 3.9 %copy-start.18 = (bf16[1024,256]{1,0:T(8,128)(2,1)S(1)}, bf16[1024,256]{1,0:T(8,128)(2,1)}, u32[]{:S(2)}) copy-start(bf16[1024,256]{1,0:T(8,128)(2,1)} %copy-done.17) | copy-start | bytes 1572868
  171.5 3.7 %collective-permute-start.29 = (f32[1024]{0:T(1024)S(1)}, f32[1024]{0:T(1024)S(1)}, u32[]{:S(2)}, u32[]{:S(2)}) collective-permute-start(f32[1024]{0:T(1024)S(1)} %fusion.1), channel_id=1, source_target_pairs={{0,4},{4,0},{8,12},{12,8},{16,20},{20,16},{24,28},{28,24},{1,5},{5... | collective-permute-start | bytes 12296 | tf_op jit(solution)/shard_map/ppermute | solution.py:84
  175.2 3.6 %collective-permute-start.30 = (f32[1024]{0:T(1024)S(1)}, f32[1024]{0:T(1024)S(1)}, u32[]{:S(2)}, u32[]{:S(2)}) collective-permute-start(f32[1024]{0:T(1024)S(1)} %add.195), channel_id=1, source_target_pairs={{0,8},{4,12},{8,0},{12,4},{16,24},{20,28},{24,16},{28,20},{1,9},{5... | collective-permute-start | bytes 12296 | tf_op jit(solution)/shard_map/ppermute | solution.py:84
  178.8 4.5 %collective-permute-start.31 = (f32[1024]{0:T(1024)S(1)}, f32[1024]{0:T(1024)S(1)}, u32[]{:S(2)}, u32[]{:S(2)}) collective-permute-start(f32[1024]{0:T(1024)S(1)} %add.196), channel_id=1, source_target_pairs={{0,16},{4,20},{8,24},{12,28},{16,0},{20,4},{24,8},{28,12},{1,17},{... | collective-permute-start | bytes 12296 | tf_op jit(solution)/shard_map/ppermute | solution.py:84
  (3 other events, 2.8 us)

commit v19 on v18

--- a/solution.py
+++ b/solution.py
@@ -5,7 +5,7 @@
 from jax import lax
 from jax.sharding import PartitionSpec as P
 
-CHUNKS = 2
+CHUNKS = 4
 
 
 def _rows(a, blk, n):

time: 185 us -> 218 us (1.18)
  starting transfers between devices: 34.9 us -> 65.1 us
  waiting for transfers between devices: 106 us -> 93.4 us
  matrix products: 19.9 us -> 25.4 us
  local copies, waits for them, and re-layouts: 13 us -> 18 us
  other arithmetic: 9.6 us -> 13.4 us
    ppermute x12 -> x24, starting transfers between devices: 18.7 us -> 42.8 us  [_zline(): cur = lax.ppermute(cur, 'src', pairs)]
    ppermute x2 -> x4, waiting for transfers between devices: 18.4 us -> 5.29 us  [_fast(): lax.ppermute(halves[k].astype(jnp.bfloat16), 'vox', chip_perm(k))]
    ppermute x2 -> x4, waiting for transfers between devices: 11.1 us -> 17.8 us  [_fast(): lax.ppermute(piece, 'vox', chip_perm(k))]
    dot_general x8 -> x16, matrix products: 12.4 us -> 18.6 us  [pblock(): lax.dot_general(scaled, rows(col, blk), (((1,), (1,)), ((), ())), preferr...]
    ppermute x2 -> x4, waiting for transfers between devices: 9.56 us -> 4.52 us  [_fast(): piece = jnp.concatenate([mine, lax.ppermute(other, 'src', swap)], axis=0)]
    ppermute x2 -> x4, waiting for transfers between devices: 7.06 us -> 3.56 us  [_fast(): lax.ppermute(share[sl:].astype(jnp.bfloat16), 'src', swap)]
    unnamed x41 -> x81, local copies, waits for them, and re-layouts: 8.85 us -> 11 us
    ppermute x12 -> x24, waiting for transfers between devices: 41.7 us -> 43 us  [_zline(): cur = lax.ppermute(cur, 'src', pairs)]
  transfers between devices with their start and end apart: 32 -> 60, of which waited for: 20 -> 31; matrix products, arithmetic and copies ran while one was open for 14% -> 19% of each run, Pallas kernels for 0% -> 0%
where the time goes in v19:
time: 218 us; the launch traced here: 216 us
  waiting for transfers between devices  93.4 us (43%)
  starting transfers between devices  65.1 us (30%)
  matrix products  25.4 us (12%)
  local copies, waits for them, and re-layouts  18 us (8%)
  other arithmetic  13.4 us (6%)
    ppermute x24, waiting for transfers between devices, _zline(): cur = lax.ppermute(cur, 'src', pairs)  43 us
    ppermute x24, starting transfers between devices, _zline(): cur = lax.ppermute(cur, 'src', pairs)  42.8 us
    dot_general x16, matrix products, pblock(): lax.dot_general(scaled, rows(col, blk), (((1,), (1,)), ((), ())), preferr...  18.6 us
    ppermute x4, waiting for transfers between devices, _fast(): lax.ppermute(piece, 'vox', chip_perm(k))  17.8 us
    unnamed x81, local copies, waits for them, and re-layouts  11 us
    ppermute x3, waiting for transfers between devices, _sum_over_src(): v = v + lax.ppermute(v, 'src', [(i, i ^ b) for i in range(n)])  8.65 us
    ppermute x1, waiting for transfers between devices, _fast(): lax.ppermute(forward_voxel_field, 'src', swap)  7.89 us
    dot_general x4, matrix products, _fast(): jnp.dot(jnp.concatenate([w for _, w in got], axis=1), jnp.concatenate([ro...  6.74 us
  transfers between devices with their start and end apart: 60, of which 31 were waited for; matrix products, arithmetic and copies ran while one was open for 19% of the time, Pallas kernels for 0%

profile of v19, /device:TPU:0, one launch (start us, length us, event | category | flops | bytes accessed | tf_op | source)
XLA Modules:
  0.0 216.4 jit_solution(13256714721344403733)
XLA Ops:
  0.0 2.2 fusion.128
  2.2 4.9 %collective-permute-start.8 = (bf16[128,1024]{1,0:T(8,128)(2,1)S(1)}, bf16[128,1024]{1,0:T(8,128)(2,1)S(1)}, u32[]{:S(2)}, u32[]{:S(2)}) collective-permute-start(bf16[128,1024]{1,0:T(8,128)(2,1)S(1)} %get-tuple-element.55), channel_id=1, source_target_pairs={{0,8},{4,12},{8,16},{12,20},{16,24},{20,28},{1,9},{5,13},{9,17},{1... | collective-permute-start | bytes 786440 | tf_op jit(solution)/shard_map/ppermute | solution.py:104
  8.4 4.2 %collective-permute-done.8 = bf16[128,1024]{1,0:T(8,128)(2,1)S(1)} collective-permute-done((bf16[128,1024]{1,0:T(8,128)(2,1)S(1)}, bf16[128,1024]{1,0:T(8,128)(2,1)S(1)}, u32[]{:S(2)}, u32[]{:S(2)}) %collective-permute-start.8) | collective-permute-done | bytes 262176 | tf_op jit(solution)/shard_map/ppermute | solution.py:104
  13.3 3.5 %collective-permute-done.7 = bf16[128,1024]{1,0:T(8,128)(2,1)S(1)} collective-permute-done((bf16[128,1024]{1,0:T(8,128)(2,1)S(1)}, bf16[128,1024]{1,0:T(8,128)(2,1)S(1)}, u32[]{:S(2)}, u32[]{:S(2)}) %collective-permute-start.7) | collective-permute-done | bytes 262176 | tf_op jit(solution)/shard_map/ppermute | solution.py:104
  18.1 1.6 collective-permute-start
  20.4 5.2 %collective-permute-done.11 = bf16[128,1024]{1,0:T(8,128)(2,1)S(1)} collective-permute-done((bf16[128,1024]{1,0:T(8,128)(2,1)S(1)}, bf16[128,1024]{1,0:T(8,128)(2,1)S(1)}, u32[]{:S(2)}, u32[]{:S(2)}) %collective-permute-start.11) | collective-permute-done | bytes 262176 | tf_op jit(solution)/shard_map/ppermute | solution.py:104
  27.0 6.9 %collective-permute-done.12 = bf16[128,1024]{1,0:T(8,128)(2,1)S(1)} collective-permute-done((bf16[128,1024]{1,0:T(8,128)(2,1)S(1)}, bf16[128,1024]{1,0:T(8,128)(2,1)S(1)}, u32[]{:S(2)}, u32[]{:S(2)}) %collective-permute-start.12) | collective-permute-done | bytes 262176 | tf_op jit(solution)/shard_map/ppermute | solution.py:104
  34.0 7.9 %collective-permute-done = bf16[512,1024]{1,0:T(8,128)(2,1)} collective-permute-done((bf16[512,1024]{1,0:T(8,128)(2,1)S(1)}, bf16[512,1024]{1,0:T(8,128)(2,1)}, u32[]{:S(2)}, u32[]{:S(2)}) %collective-permute-start) | collective-permute-done | bytes 1048608 | tf_op jit(solution)/shard_map/ppermute | solution.py:135
  41.9 1.8 fusion
  43.8 1.5 fusion.101
  45.3 1.5 fusion.104
  47.5 2.5 %fusion.6 = bf16[1024,128]{1,0:T(8,128)(2,1)} fusion(f32[1024,128]{1,0:T(8,128)} %collective-permute-done.14, bf16[1024,1024]{1,0:T(8,128)(2,1)S(1)} %fusion, bf16[512,1024]{1,0:T(8,128)(2,1)S(1)} %pad_maximum_fusion.2, s32[]{:T(128)S(6)} %select_n.370), kind=kOutput, calls=%fused_computation.17 | convolution fusion | flops 268697600 | bytes 3145732 | tf_op jit(solution)/shard_map/dot_general | solution.py:147
  50.0 1.5 collective-permute-start.15
  51.5 5.1 %collective-permute-start.2 = (bf16[128,1024]{1,0:T(8,128)(2,1)}, bf16[128,1024]{1,0:T(8,128)(2,1)}, u32[]{:S(2)}, u32[]{:S(2)}) collective-permute-start(bf16[128,1024]{1,0:T(8,128)(2,1)} %get-tuple-element.56), channel_id=1, source_target_pairs={{0,8},{4,12},{8,16},{12,20},{16,24},{20,28},{1,9},{5,13},{9,17},{1... | collective-permute-start | bytes 786440 | tf_op jit(solution)/shard_map/ppermute | solution.py:104
  57.9 2.9 %copy.5 = f32[512,1024]{0,1:T(8,128)} copy(f32[512,1024]{1,0:T(8,128)} %param.7) | data formatting | bytes 4194304 | tf_op args[3]
  60.9 2.0 fusion.5
  63.6 1.5 collective-permute-start.16
  69.8 1.6 collective-permute-start.17
  72.1 7.4 %collective-permute-done.5 = bf16[128,1024]{1,0:T(8,128)(2,1)S(1)} collective-permute-done((bf16[128,1024]{1,0:T(8,128)(2,1)}, bf16[128,1024]{1,0:T(8,128)(2,1)S(1)}, u32[]{:S(2)}, u32[]{:S(2)}) %collective-permute-start.5) | collective-permute-done | bytes 262176 | tf_op jit(solution)/shard_map/ppermute | solution.py:104
  82.5 4.7 %collective-permute-done.18 = bf16[1024,128]{1,0:T(8,128)(2,1)S(1)} collective-permute-done((bf16[1024,128]{1,0:T(8,128)(2,1)S(1)}, bf16[1024,128]{1,0:T(8,128)(2,1)S(1)}, u32[]{:S(2)}, u32[]{:S(2)}) %collective-permute-start.18) | collective-permute-done | bytes 262176 | tf_op jit(solution)/shard_map/ppermute | solution.py:172
  92.9 5.9 %collective-permute-start.22 = (bf16[128,1024]{1,0:T(8,128)(2,1)}, bf16[128,1024]{1,0:T(8,128)(2,1)}, u32[]{:S(2)}, u32[]{:S(2)}) collective-permute-start(bf16[128,1024]{1,0:T(8,128)(2,1)} %get-tuple-element.58), channel_id=1, source_target_pairs={{0,8},{4,12},{8,16},{12,20},{16,24},{20,28},{1,9},{5,13},{9,17},{1... | collective-permute-start | bytes 786440 | tf_op jit(solution)/shard_map/ppermute | solution.py:104
  103.4 2.0 copy.11
  106.1 2.9 %collective-permute-done.21 = bf16[128,1024]{1,0:T(8,128)(2,1)} collective-permute-done((bf16[128,1024]{1,0:T(8,128)(2,1)}, bf16[128,1024]{1,0:T(8,128)(2,1)}, u32[]{:S(2)}, u32[]{:S(2)}) %collective-permute-start.21) | collective-permute-done | bytes 262176 | tf_op jit(solution)/shard_map/ppermute | solution.py:104
  113.6 4.6 %collective-permute-done.25 = bf16[128,1024]{1,0:T(8,128)(2,1)S(1)} collective-permute-done((bf16[128,1024]{1,0:T(8,128)(2,1)}, bf16[128,1024]{1,0:T(8,128)(2,1)S(1)}, u32[]{:S(2)}, u32[]{:S(2)}) %collective-permute-start.25) | collective-permute-done | bytes 262176 | tf_op jit(solution)/shard_map/ppermute | solution.py:104
  118.2 1.5 collective-permute-start.26
  119.8 1.5 collective-permute-start.32
  122.4 3.8 %collective-permute-done.32 = bf16[1024,128]{1,0:T(8,128)(2,1)S(1)} collective-permute-done((bf16[1024,128]{1,0:T(8,128)(2,1)S(1)}, bf16[1024,128]{1,0:T(8,128)(2,1)S(1)}, u32[]{:S(2)}, u32[]{:S(2)}) %collective-permute-start.32) | collective-permute-done | bytes 262176 | tf_op jit(solution)/shard_map/ppermute | solution.py:172
  131.2 1.5 collective-permute-start.43
  132.7 6.0 %collective-permute-start.36 = (bf16[128,1024]{1,0:T(8,128)(2,1)S(1)}, bf16[128,1024]{1,0:T(8,128)(2,1)}, u32[]{:S(2)}, u32[]{:S(2)}) collective-permute-start(bf16[128,1024]{1,0:T(8,128)(2,1)S(1)} %get-tuple-element.57), channel_id=1, source_target_pairs={{0,8},{4,12},{8,16},{12,20},{16,24},{20,28},{1,9},{5,13},{9,17},{1... | collective-permute-start | bytes 786440 | tf_op jit(solution)/shard_map/ppermute | solution.py:104
  142.2 1.4 collective-permute-start.44
  143.6 2.0 copy.12
  146.3 2.3 %collective-permute-done.35 = bf16[128,1024]{1,0:T(8,128)(2,1)} collective-permute-done((bf16[128,1024]{1,0:T(8,128)(2,1)S(1)}, bf16[128,1024]{1,0:T(8,128)(2,1)}, u32[]{:S(2)}, u32[]{:S(2)}) %collective-permute-start.35) | collective-permute-done | bytes 262176 | tf_op jit(solution)/shard_map/ppermute | solution.py:104
  153.4 4.8 %collective-permute-done.39 = bf16[128,1024]{1,0:T(8,128)(2,1)S(1)} collective-permute-done((bf16[128,1024]{1,0:T(8,128)(2,1)}, bf16[128,1024]{1,0:T(8,128)(2,1)S(1)}, u32[]{:S(2)}, u32[]{:S(2)}) %collective-permute-start.39) | collective-permute-done | bytes 262176 | tf_op jit(solution)/shard_map/ppermute | solution.py:104
  161.3 4.9 %collective-permute-done.46 = bf16[1024,128]{1,0:T(8,128)(2,1)S(1)} collective-permute-done((bf16[1024,128]{1,0:T(8,128)(2,1)S(1)}, bf16[1024,128]{1,0:T(8,128)(2,1)S(1)}, u32[]{:S(2)}, u32[]{:S(2)}) %collective-permute-start.46) | collective-permute-done | bytes 262176 | tf_op jit(solution)/shard_map/ppermute | solution.py:172
  168.6 1.5 fusion.86
  170.5 1.4 fusion.9
  172.4 2.0 copy.13
  174.5 1.3 constant_dynamic-slice_fusion.15
  175.9 4.6 %collective-permute-done.51 = bf16[1024,128]{1,0:T(8,128)(2,1)S(1)} collective-permute-done((bf16[1024,128]{1,0:T(8,128)(2,1)}, bf16[1024,128]{1,0:T(8,128)(2,1)S(1)}, u32[]{:S(2)}, u32[]{:S(2)}) %collective-permute-start.51) | collective-permute-done | bytes 262176 | tf_op jit(solution)/shard_map/ppermute | solution.py:157
  180.5 1.8 fusion.2
  184.0 3.3 %collective-permute-done.52 = bf16[512,128]{1,0:T(8,128)(2,1)S(1)} collective-permute-done((bf16[512,128]{1,0:T(8,128)(2,1)S(1)}, bf16[512,128]{1,0:T(8,128)(2,1)S(1)}, u32[]{:S(2)}, u32[]{:S(2)}) %collective-permute-start.52) | collective-permute-done | bytes 131104 | tf_op jit(solution)/shard_map/ppermute | solution.py:162
  188.1 4.5 %collective-permute-done.53 = bf16[512,128]{1,0:T(8,128)(2,1)S(1)} collective-permute-done((bf16[512,128]{1,0:T(8,128)(2,1)S(1)}, bf16[512,128]{1,0:T(8,128)(2,1)S(1)}, u32[]{:S(2)}, u32[]{:S(2)}) %collective-permute-start.53) | collective-permute-done | bytes 131104 | tf_op jit(solution)/shard_map/ppermute | solution.py:168
  194.6 4.4 %collective-permute-done.54 = bf16[1024,128]{1,0:T(8,128)(2,1)S(1)} collective-permute-done((bf16[1024,128]{1,0:T(8,128)(2,1)S(1)}, bf16[1024,128]{1,0:T(8,128)(2,1)S(1)}, u32[]{:S(2)}, u32[]{:S(2)}) %collective-permute-start.54) | collective-permute-done | bytes 262176 | tf_op jit(solution)/shard_map/ppermute | solution.py:172
  200.6 3.0 %fusion.1 = f32[1024]{0:T(1024)S(1)} fusion(f32[1024,1024]{1,0:T(8,128)S(1)} %fusion.40, f32[1024,1024]{1,0:T(8,128)S(1)} %fusion.10, f32[1024,1024]{1,0:T(8,128)S(1)} %fusion.25, bf16[512,1024]{1,0:T(8,128)(2,1)} %collective-permute-done, bf16[512,1024]{1,0:T(8,128)(2,1)S(1)} %copy-done.12, bf16[1024,128]{1,0:T(8,128)(2,1)S(1)} %collective-permute-done.56, ...), kind=kOutput, calls=%fused_computation.3 | convolution fusion | flops 1092615168 | bytes 16781312 | tf_op jit(solution)/shard_map/dot_general | solution.py:180
  204.0 3.2 %collective-permute-done.57 = f32[1024]{0:T(1024)S(1)} collective-permute-done((f32[1024]{0:T(1024)S(1)}, f32[1024]{0:T(1024)S(1)}, u32[]{:S(2)}, u32[]{:S(2)}) %collective-permute-start.57) | collective-permute-done | bytes 4128 | tf_op jit(solution)/shard_map/ppermute | solution.py:84
  207.2 2.5 %collective-permute-start.58 = (f32[1024]{0:T(1024)S(1)}, f32[1024]{0:T(1024)S(1)}, u32[]{:S(2)}, u32[]{:S(2)}) collective-permute-start(f32[1024]{0:T(1024)S(1)} %add.289), channel_id=1, source_target_pairs={{0,8},{4,12},{8,0},{12,4},{16,24},{20,28},{24,16},{28,20},{1,9},{5... | collective-permute-start | bytes 12296 | tf_op jit(solution)/shard_map/ppermute | solution.py:84
  209.7 1.6 collective-permute-done.58
  212.0 3.8 %collective-permute-done.59 = f32[1024]{0:T(1024)S(1)} collective-permute-done((f32[1024]{0:T(1024)S(1)}, f32[1024]{0:T(1024)S(1)}, u32[]{:S(2)}, u32[]{:S(2)}) %collective-permute-start.59) | collective-permute-done | bytes 4128 | tf_op jit(solution)/shard_map/ppermute | solution.py:84
  (219 shorter events, 60.6 us)
Async XLA Ops:
  2.2 10.5 %collective-permute-start.8 = (bf16[128,1024]{1,0:T(8,128)(2,1)S(1)}, bf16[128,1024]{1,0:T(8,128)(2,1)S(1)}, u32[]{:S(2)}, u32[]{:S(2)}) collective-permute-start(bf16[128,1024]{1,0:T(8,128)(2,1)S(1)} %get-tuple-element.55), channel_id=1, source_target_pairs={{0,8},{4,12},{8,16},{12,20},{16,24},{20,28},{1,9},{5,13},{9,17},{1... | collective-permute-start | bytes 786440 | tf_op jit(solution)/shard_map/ppermute | solution.py:104
  7.1 9.7 %collective-permute-start.7 = (bf16[128,1024]{1,0:T(8,128)(2,1)S(1)}, bf16[128,1024]{1,0:T(8,128)(2,1)S(1)}, u32[]{:S(2)}, u32[]{:S(2)}) collective-permute-start(bf16[128,1024]{1,0:T(8,128)(2,1)S(1)} %get-tuple-element.55), channel_id=1, source_target_pairs={{8,0},{12,4},{16,8},{20,12},{24,16},{28,20},{9,1},{13,5},{17,9},{2... | collective-permute-start | bytes 786440 | tf_op jit(solution)/shard_map/ppermute | solution.py:104
  12.6 7.0 %collective-permute-start.9 = (bf16[128,1024]{1,0:T(8,128)(2,1)S(1)}, bf16[128,1024]{1,0:T(8,128)(2,1)S(1)}, u32[]{:S(2)}, u32[]{:S(2)}) collective-permute-start(bf16[128,1024]{1,0:T(8,128)(2,1)S(1)} %collective-permute-done.8), channel_id=1, source_target_pairs={{8,16},{12,20},{16,24},{20,28},{9,17},{13,21},{17,25},{21,29},{10,... | collective-permute-start | bytes 786440 | tf_op jit(solution)/shard_map/ppermute | solution.py:104
  16.8 8.9 %collective-permute-start.11 = (bf16[128,1024]{1,0:T(8,128)(2,1)S(1)}, bf16[128,1024]{1,0:T(8,128)(2,1)S(1)}, u32[]{:S(2)}, u32[]{:S(2)}) collective-permute-start(bf16[128,1024]{1,0:T(8,128)(2,1)S(1)} %collective-permute-done.7), channel_id=1, source_target_pairs={{8,0},{12,4},{16,8},{20,12},{9,1},{13,5},{17,9},{21,13},{10,2},{14... | collective-permute-start | bytes 786440 | tf_op jit(solution)/shard_map/ppermute | solution.py:104
  18.1 23.9 %collective-permute-start = (bf16[512,1024]{1,0:T(8,128)(2,1)S(1)}, bf16[512,1024]{1,0:T(8,128)(2,1)}, u32[]{:S(2)}, u32[]{:S(2)}) collective-permute-start(bf16[512,1024]{1,0:T(8,128)(2,1)S(1)} %copy-done.10), channel_id=1, source_target_pairs={{0,4},{4,0},{8,12},{12,8},{16,20},{20,16},{24,28},{28,24},{1,5},{5... | collective-permute-start | bytes 3145736 | tf_op jit(solution)/shard_map/ppermute | solution.py:135
  19.6 7.4 %collective-permute-start.10 = (bf16[128,1024]{1,0:T(8,128)(2,1)S(1)}, bf16[128,1024]{1,0:T(8,128)(2,1)S(1)}, u32[]{:S(2)}, u32[]{:S(2)}) collective-permute-start(bf16[128,1024]{1,0:T(8,128)(2,1)S(1)} %collective-permute-done.9), channel_id=1, source_target_pairs={{16,24},{20,28},{17,25},{21,29},{18,26},{22,30},{19,27},{23,31}} | collective-permute-start | bytes 786440 | tf_op jit(solution)/shard_map/ppermute | solution.py:104
  25.7 8.3 %collective-permute-start.12 = (bf16[128,1024]{1,0:T(8,128)(2,1)S(1)}, bf16[128,1024]{1,0:T(8,128)(2,1)S(1)}, u32[]{:S(2)}, u32[]{:S(2)}) collective-permute-start(bf16[128,1024]{1,0:T(8,128)(2,1)S(1)} %collective-permute-done.11), channel_id=1, source_target_pairs={{8,0},{12,4},{9,1},{13,5},{10,2},{14,6},{11,3},{15,7}} | collective-permute-start | bytes 786440 | tf_op jit(solution)/shard_map/ppermute | solution.py:104
  46.8 14.0 %collective-permute-start.13 = (f32[1024,128]{1,0:T(8,128)}, f32[1024,128]{1,0:T(8,128)}, u32[]{:S(2)}, u32[]{:S(2)}) collective-permute-start(f32[1024,128]{1,0:T(8,128)} %fusion.104), channel_id=1, source_target_pairs={{0,1},{1,0},{2,3},{3,2},{4,5},{5,4},{6,7},{7,6},{8,9},{9,8},{10,11... | collective-permute-start | bytes 1572872 | tf_op jit(solution)/shard_map/ppermute | solution.py:154
  50.0 10.8 %collective-permute-start.15 = (bf16[1024,128]{1,0:T(8,128)(2,1)}, bf16[1024,128]{1,0:T(8,128)(2,1)}, u32[]{:S(2)}, u32[]{:S(2)}) collective-permute-start(bf16[1024,128]{1,0:T(8,128)(2,1)} %fusion.6), channel_id=1, source_target_pairs={{0,2},{1,3},{2,0},{3,1},{4,6},{5,7},{6,4},{7,5},{8,10},{9,11},{10,... | collective-permute-start | bytes 786440 | tf_op jit(solution)/shard_map/ppermute | solution.py:157
  51.5 15.0 %collective-permute-start.2 = (bf16[128,1024]{1,0:T(8,128)(2,1)}, bf16[128,1024]{1,0:T(8,128)(2,1)}, u32[]{:S(2)}, u32[]{:S(2)}) collective-permute-start(bf16[128,1024]{1,0:T(8,128)(2,1)} %get-tuple-element.56), channel_id=1, source_target_pairs={{0,8},{4,12},{8,16},{12,20},{16,24},{20,28},{1,9},{5,13},{9,17},{1... | collective-permute-start | bytes 786440 | tf_op jit(solution)/shard_map/ppermute | solution.py:104
  56.6 10.6 %collective-permute-start.1 = (bf16[128,1024]{1,0:T(8,128)(2,1)}, bf16[128,1024]{1,0:T(8,128)(2,1)}, u32[]{:S(2)}, u32[]{:S(2)}) collective-permute-start(bf16[128,1024]{1,0:T(8,128)(2,1)} %get-tuple-element.56), channel_id=1, source_target_pairs={{8,0},{12,4},{16,8},{20,12},{24,16},{28,20},{9,1},{13,5},{17,9},{2... | collective-permute-start | bytes 786440 | tf_op jit(solution)/shard_map/ppermute | solution.py:104
  63.6 5.2 %collective-permute-start.16 = (bf16[512,128]{1,0:T(8,128)(2,1)}, bf16[512,128]{1,0:T(8,128)(2,1)S(1)}, u32[]{:S(2)}, u32[]{:S(2)}) collective-permute-start(bf16[512,128]{1,0:T(8,128)(2,1)} %slice.159), channel_id=1, source_target_pairs={{0,4},{4,0},{8,12},{12,8},{16,20},{20,16},{24,28},{28,24},{1,5},{5... | collective-permute-start | bytes 393224 | tf_op jit(solution)/shard_map/ppermute | solution.py:162
  67.2 12.3 %collective-permute-start.5 = (bf16[128,1024]{1,0:T(8,128)(2,1)}, bf16[128,1024]{1,0:T(8,128)(2,1)S(1)}, u32[]{:S(2)}, u32[]{:S(2)}) collective-permute-start(bf16[128,1024]{1,0:T(8,128)(2,1)} %collective-permute-done.1), channel_id=1, source_target_pairs={{8,0},{12,4},{16,8},{20,12},{9,1},{13,5},{17,9},{21,13},{10,2},{14... | collective-permute-start | bytes 786440 | tf_op jit(solution)/shard_map/ppermute | solution.py:104
  69.8 10.9 %collective-permute-start.17 = (bf16[512,128]{1,0:T(8,128)(2,1)S(1)}, bf16[512,128]{1,0:T(8,128)(2,1)S(1)}, u32[]{:S(2)}, u32[]{:S(2)}) collective-permute-start(bf16[512,128]{1,0:T(8,128)(2,1)S(1)} %get-tuple-element.74), channel_id=1, source_target_pairs={{0,4},{4,0},{8,12},{12,8},{16,20},{20,16},{24,28},{28,24},{1,5},{5... | collective-permute-start | bytes 393224 | tf_op jit(solution)/shard_map/ppermute | solution.py:168
  71.4 10.0 %collective-permute-start.4 = (bf16[128,1024]{1,0:T(8,128)(2,1)S(1)}, bf16[128,1024]{1,0:T(8,128)(2,1)S(1)}, u32[]{:S(2)}, u32[]{:S(2)}) collective-permute-start(bf16[128,1024]{1,0:T(8,128)(2,1)S(1)} %collective-permute-done.3), channel_id=1, source_target_pairs={{16,24},{20,28},{17,25},{21,29},{18,26},{22,30},{19,27},{23,31}} | collective-permute-start | bytes 786440 | tf_op jit(solution)/shard_map/ppermute | solution.py:104
  79.5 8.3 %collective-permute-start.6 = (bf16[128,1024]{1,0:T(8,128)(2,1)S(1)}, bf16[128,1024]{1,0:T(8,128)(2,1)S(1)}, u32[]{:S(2)}, u32[]{:S(2)}) collective-permute-start(bf16[128,1024]{1,0:T(8,128)(2,1)S(1)} %collective-permute-done.5), channel_id=1, source_target_pairs={{8,0},{12,4},{9,1},{13,5},{10,2},{14,6},{11,3},{15,7}} | collective-permute-start | bytes 786440 | tf_op jit(solution)/shard_map/ppermute | solution.py:104
  80.8 6.4 %collective-permute-start.18 = (bf16[1024,128]{1,0:T(8,128)(2,1)S(1)}, bf16[1024,128]{1,0:T(8,128)(2,1)S(1)}, u32[]{:S(2)}, u32[]{:S(2)}) collective-permute-start(bf16[1024,128]{1,0:T(8,128)(2,1)S(1)} %pad_maximum_fusion.5), channel_id=1, source_target_pairs={{0,2},{1,3},{2,0},{3,1},{4,6},{5,7},{6,4},{7,5},{8,10},{9,11},{10,... | collective-permute-start | bytes 786440 | tf_op jit(solution)/shard_map/ppermute | solution.py:172
  82.5 6.3 %collective-permute-start.19 = (bf16[1024,128]{1,0:T(8,128)(2,1)S(1)}, bf16[1024,128]{1,0:T(8,128)(2,1)S(1)}, u32[]{:S(2)}, u32[]{:S(2)}) collective-permute-start(bf16[1024,128]{1,0:T(8,128)(2,1)S(1)} %pad_maximum_fusion.5), channel_id=1, source_target_pairs={{0,1},{1,0},{2,3},{3,2},{4,5},{5,4},{6,7},{7,6},{8,9},{9,8},{10,11... | collective-permute-start | bytes 786440 | tf_op jit(solution)/shard_map/ppermute | solution.py:173
  90.5 9.6 %collective-permute-start.27 = (f32[1024,128]{1,0:T(8,128)S(1)}, f32[1024,128]{1,0:T(8,128)S(1)}, u32[]{:S(2)}, u32[]{:S(2)}) collective-permute-start(f32[1024,128]{1,0:T(8,128)S(1)} %fusion.98), channel_id=1, source_target_pairs={{0,1},{1,0},{2,3},{3,2},{4,5},{5,4},{6,7},{7,6},{8,9},{9,8},{10,11... | collective-permute-start | bytes 1572872 | tf_op jit(solution)/shard_map/ppermute | solution.py:154
  92.3 8.4 %collective-permute-start.29 = (bf16[1024,128]{1,0:T(8,128)(2,1)S(1)}, bf16[1024,128]{1,0:T(8,128)(2,1)S(1)}, u32[]{:S(2)}, u32[]{:S(2)}) collective-permute-start(bf16[1024,128]{1,0:T(8,128)(2,1)S(1)} %fusion.7), channel_id=1, source_target_pairs={{0,2},{1,3},{2,0},{3,1},{4,6},{5,7},{6,4},{7,5},{8,10},{9,11},{10,... | collective-permute-start | bytes 786440 | tf_op jit(solution)/shard_map/ppermute | solution.py:157
  92.9 12.5 %collective-permute-start.22 = (bf16[128,1024]{1,0:T(8,128)(2,1)}, bf16[128,1024]{1,0:T(8,128)(2,1)}, u32[]{:S(2)}, u32[]{:S(2)}) collective-permute-start(bf16[128,1024]{1,0:T(8,128)(2,1)} %get-tuple-element.58), channel_id=1, source_target_pairs={{0,8},{4,12},{8,16},{12,20},{16,24},{20,28},{1,9},{5,13},{9,17},{1... | collective-permute-start | bytes 786440 | tf_op jit(solution)/shard_map/ppermute | solution.py:104
  98.8 10.2 %collective-permute-start.21 = (bf16[128,1024]{1,0:T(8,128)(2,1)}, bf16[128,1024]{1,0:T(8,128)(2,1)}, u32[]{:S(2)}, u32[]{:S(2)}) collective-permute-start(bf16[128,1024]{1,0:T(8,128)(2,1)} %get-tuple-element.58), channel_id=1, source_target_pairs={{8,0},{12,4},{16,8},{20,12},{24,16},{28,20},{9,1},{13,5},{17,9},{2... | collective-permute-start | bytes 786440 | tf_op jit(solution)/shard_map/ppermute | solution.py:104
  102.9 7.4 %collective-permute-start.30 = (bf16[512,128]{1,0:T(8,128)(2,1)}, bf16[512,128]{1,0:T(8,128)(2,1)S(1)}, u32[]{:S(2)}, u32[]{:S(2)}) collective-permute-start(bf16[512,128]{1,0:T(8,128)(2,1)} %slice.158), channel_id=1, source_target_pairs={{0,4},{4,0},{8,12},{12,8},{16,20},{20,16},{24,28},{28,24},{1,5},{5... | collective-permute-start | bytes 393224 | tf_op jit(solution)/shard_map/ppermute | solution.py:162
  105.4 7.5 %collective-permute-start.23 = (bf16[128,1024]{1,0:T(8,128)(2,1)}, bf16[128,1024]{1,0:T(8,128)(2,1)S(1)}, u32[]{:S(2)}, u32[]{:S(2)}) collective-permute-start(bf16[128,1024]{1,0:T(8,128)(2,1)} %collective-permute-done.22), channel_id=1, source_target_pairs={{8,16},{12,20},{16,24},{20,28},{9,17},{13,21},{17,25},{21,29},{10,... | collective-permute-start | bytes 786440 | tf_op jit(solution)/shard_map/ppermute | solution.py:104
  109.0 9.3 %collective-permute-start.25 = (bf16[128,1024]{1,0:T(8,128)(2,1)}, bf16[128,1024]{1,0:T(8,128)(2,1)S(1)}, u32[]{:S(2)}, u32[]{:S(2)}) collective-permute-start(bf16[128,1024]{1,0:T(8,128)(2,1)} %collective-permute-done.21), channel_id=1, source_target_pairs={{8,0},{12,4},{16,8},{20,12},{9,1},{13,5},{17,9},{21,13},{10,2},{14... | collective-permute-start | bytes 786440 | tf_op jit(solution)/shard_map/ppermute | solution.py:104
  112.4 7.3 %collective-permute-start.31 = (bf16[512,128]{1,0:T(8,128)(2,1)S(1)}, bf16[512,128]{1,0:T(8,128)(2,1)S(1)}, u32[]{:S(2)}, u32[]{:S(2)}) collective-permute-start(bf16[512,128]{1,0:T(8,128)(2,1)S(1)} %get-tuple-element.72), channel_id=1, source_target_pairs={{0,4},{4,0},{8,12},{12,8},{16,20},{20,16},{24,28},{28,24},{1,5},{5... | collective-permute-start | bytes 393224 | tf_op jit(solution)/shard_map/ppermute | solution.py:168
  113.0 8.3 %collective-permute-start.24 = (bf16[128,1024]{1,0:T(8,128)(2,1)S(1)}, bf16[128,1024]{1,0:T(8,128)(2,1)S(1)}, u32[]{:S(2)}, u32[]{:S(2)}) collective-permute-start(bf16[128,1024]{1,0:T(8,128)(2,1)S(1)} %collective-permute-done.23), channel_id=1, source_target_pairs={{16,24},{20,28},{17,25},{21,29},{18,26},{22,30},{19,27},{23,31}} | collective-permute-start | bytes 786440 | tf_op jit(solution)/shard_map/ppermute | solution.py:104
  118.2 8.3 %collective-permute-start.26 = (bf16[128,1024]{1,0:T(8,128)(2,1)S(1)}, bf16[128,1024]{1,0:T(8,128)(2,1)S(1)}, u32[]{:S(2)}, u32[]{:S(2)}) collective-permute-start(bf16[128,1024]{1,0:T(8,128)(2,1)S(1)} %collective-permute-done.25), channel_id=1, source_target_pairs={{8,0},{12,4},{9,1},{13,5},{10,2},{14,6},{11,3},{15,7}} | collective-permute-start | bytes 786440 | tf_op jit(solution)/shard_map/ppermute | solution.py:104
  119.8 6.4 %collective-permute-start.32 = (bf16[1024,128]{1,0:T(8,128)(2,1)S(1)}, bf16[1024,128]{1,0:T(8,128)(2,1)S(1)}, u32[]{:S(2)}, u32[]{:S(2)}) collective-permute-start(bf16[1024,128]{1,0:T(8,128)(2,1)S(1)} %pad_maximum_fusion.6), channel_id=1, source_target_pairs={{0,2},{1,3},{2,0},{3,1},{4,6},{5,7},{6,4},{7,5},{8,10},{9,11},{10,... | collective-permute-start | bytes 786440 | tf_op jit(solution)/shard_map/ppermute | solution.py:172
  122.3 5.3 %collective-permute-start.33 = (bf16[1024,128]{1,0:T(8,128)(2,1)S(1)}, bf16[1024,128]{1,0:T(8,128)(2,1)S(1)}, u32[]{:S(2)}, u32[]{:S(2)}) collective-permute-start(bf16[1024,128]{1,0:T(8,128)(2,1)S(1)} %pad_maximum_fusion.6), channel_id=1, source_target_pairs={{0,1},{1,0},{2,3},{3,2},{4,5},{5,4},{6,7},{7,6},{8,9},{9,8},{10,11... | collective-permute-start | bytes 786440 | tf_op jit(solution)/shard_map/ppermute | solution.py:173
  129.4 10.5 %collective-permute-start.41 = (f32[1024,128]{1,0:T(8,128)S(1)}, f32[1024,128]{1,0:T(8,128)S(1)}, u32[]{:S(2)}, u32[]{:S(2)}) collective-permute-start(f32[1024,128]{1,0:T(8,128)S(1)} %fusion.92), channel_id=1, source_target_pairs={{0,1},{1,0},{2,3},{3,2},{4,5},{5,4},{6,7},{7,6},{8,9},{9,8},{10,11... | collective-permute-start | bytes 1572872 | tf_op jit(solution)/shard_map/ppermute | solution.py:154
  131.2 8.8 %collective-permute-start.43 = (bf16[1024,128]{1,0:T(8,128)(2,1)S(1)}, bf16[1024,128]{1,0:T(8,128)(2,1)S(1)}, u32[]{:S(2)}, u32[]{:S(2)}) collective-permute-start(bf16[1024,128]{1,0:T(8,128)(2,1)S(1)} %fusion.8), channel_id=1, source_target_pairs={{0,2},{1,3},{2,0},{3,1},{4,6},{5,7},{6,4},{7,5},{8,10},{9,11},{10,... | collective-permute-start | bytes 786440 | tf_op jit(solution)/shard_map/ppermute | solution.py:157
  132.7 13.0 %collective-permute-start.36 = (bf16[128,1024]{1,0:T(8,128)(2,1)S(1)}, bf16[128,1024]{1,0:T(8,128)(2,1)}, u32[]{:S(2)}, u32[]{:S(2)}) collective-permute-start(bf16[128,1024]{1,0:T(8,128)(2,1)S(1)} %get-tuple-element.57), channel_id=1, source_target_pairs={{0,8},{4,12},{8,16},{12,20},{16,24},{20,28},{1,9},{5,13},{9,17},{1... | collective-permute-start | bytes 786440 | tf_op jit(solution)/shard_map/ppermute | solution.py:104
  138.6 10.0 %collective-permute-start.35 = (bf16[128,1024]{1,0:T(8,128)(2,1)S(1)}, bf16[128,1024]{1,0:T(8,128)(2,1)}, u32[]{:S(2)}, u32[]{:S(2)}) collective-permute-start(bf16[128,1024]{1,0:T(8,128)(2,1)S(1)} %get-tuple-element.57), channel_id=1, source_target_pairs={{8,0},{12,4},{16,8},{20,12},{24,16},{28,20},{9,1},{13,5},{17,9},{2... | collective-permute-start | bytes 786440 | tf_op jit(solution)/shard_map/ppermute | solution.py:104
  142.2 7.8 %collective-permute-start.44 = (bf16[512,128]{1,0:T(8,128)(2,1)}, bf16[512,128]{1,0:T(8,128)(2,1)S(1)}, u32[]{:S(2)}, u32[]{:S(2)}) collective-permute-start(bf16[512,128]{1,0:T(8,128)(2,1)} %slice.157), channel_id=1, source_target_pairs={{0,4},{4,0},{8,12},{12,8},{16,20},{20,16},{24,28},{28,24},{1,5},{5... | collective-permute-start | bytes 393224 | tf_op jit(solution)/shard_map/ppermute | solution.py:162
  145.6 7.1 %collective-permute-start.37 = (bf16[128,1024]{1,0:T(8,128)(2,1)}, bf16[128,1024]{1,0:T(8,128)(2,1)S(1)}, u32[]{:S(2)}, u32[]{:S(2)}) collective-permute-start(bf16[128,1024]{1,0:T(8,128)(2,1)} %collective-permute-done.36), channel_id=1, source_target_pairs={{8,16},{12,20},{16,24},{20,28},{9,17},{13,21},{17,25},{21,29},{10,... | collective-permute-start | bytes 786440 | tf_op jit(solution)/shard_map/ppermute | solution.py:104
  148.6 9.6 %collective-permute-start.39 = (bf16[128,1024]{1,0:T(8,128)(2,1)}, bf16[128,1024]{1,0:T(8,128)(2,1)S(1)}, u32[]{:S(2)}, u32[]{:S(2)}) collective-permute-start(bf16[128,1024]{1,0:T(8,128)(2,1)} %collective-permute-done.35), channel_id=1, source_target_pairs={{8,0},{12,4},{16,8},{20,12},{9,1},{13,5},{17,9},{21,13},{10,2},{14... | collective-permute-start | bytes 786440 | tf_op jit(solution)/shard_map/ppermute | solution.py:104
  152.0 7.4 %collective-permute-start.45 = (bf16[512,128]{1,0:T(8,128)(2,1)S(1)}, bf16[512,128]{1,0:T(8,128)(2,1)S(1)}, u32[]{:S(2)}, u32[]{:S(2)}) collective-permute-start(bf16[512,128]{1,0:T(8,128)(2,1)S(1)} %get-tuple-element.70), channel_id=1, source_target_pairs={{0,4},{4,0},{8,12},{12,8},{16,20},{20,16},{24,28},{28,24},{1,5},{5... | collective-permute-start | bytes 393224 | tf_op jit(solution)/shard_map/ppermute | solution.py:168
  152.7 7.4 %collective-permute-start.38 = (bf16[128,1024]{1,0:T(8,128)(2,1)S(1)}, bf16[128,1024]{1,0:T(8,128)(2,1)S(1)}, u32[]{:S(2)}, u32[]{:S(2)}) collective-permute-start(bf16[128,1024]{1,0:T(8,128)(2,1)S(1)} %collective-permute-done.37), channel_id=1, source_target_pairs={{16,24},{20,28},{17,25},{21,29},{18,26},{22,30},{19,27},{23,31}} | collective-permute-start | bytes 786440 | tf_op jit(solution)/shard_map/ppermute | solution.py:104
  158.2 8.4 %collective-permute-start.40 = (bf16[128,1024]{1,0:T(8,128)(2,1)S(1)}, bf16[128,1024]{1,0:T(8,128)(2,1)S(1)}, u32[]{:S(2)}, u32[]{:S(2)}) collective-permute-start(bf16[128,1024]{1,0:T(8,128)(2,1)S(1)} %collective-permute-done.39), channel_id=1, source_target_pairs={{8,0},{12,4},{9,1},{13,5},{10,2},{14,6},{11,3},{15,7}} | collective-permute-start | bytes 786440 | tf_op jit(solution)/shard_map/ppermute | solution.py:104
  159.5 6.6 %collective-permute-start.46 = (bf16[1024,128]{1,0:T(8,128)(2,1)S(1)}, bf16[1024,128]{1,0:T(8,128)(2,1)S(1)}, u32[]{:S(2)}, u32[]{:S(2)}) collective-permute-start(bf16[1024,128]{1,0:T(8,128)(2,1)S(1)} %pad_maximum_fusion.7), channel_id=1, source_target_pairs={{0,2},{1,3},{2,0},{3,1},{4,6},{5,7},{6,4},{7,5},{8,10},{9,11},{10,... | collective-permute-start | bytes 786440 | tf_op jit(solution)/shard_map/ppermute | solution.py:172
  161.2 5.6 %collective-permute-start.47 = (bf16[1024,128]{1,0:T(8,128)(2,1)S(1)}, bf16[1024,128]{1,0:T(8,128)(2,1)S(1)}, u32[]{:S(2)}, u32[]{:S(2)}) collective-permute-start(bf16[1024,128]{1,0:T(8,128)(2,1)S(1)} %pad_maximum_fusion.7), channel_id=1, source_target_pairs={{0,1},{1,0},{2,3},{3,2},{4,5},{5,4},{6,7},{7,6},{8,9},{9,8},{10,11... | collective-permute-start | bytes 786440 | tf_op jit(solution)/shard_map/ppermute | solution.py:173
  170.1 5.7 %collective-permute-start.49 = (f32[1024,128]{1,0:T(8,128)}, f32[1024,128]{1,0:T(8,128)}, u32[]{:S(2)}, u32[]{:S(2)}) collective-permute-start(f32[1024,128]{1,0:T(8,128)} %fusion.86), channel_id=1, source_target_pairs={{0,1},{1,0},{2,3},{3,2},{4,5},{5,4},{6,7},{7,6},{8,9},{9,8},{10,11... | collective-permute-start | bytes 1572872 | tf_op jit(solution)/shard_map/ppermute | solution.py:154
  172.0 8.6 %collective-permute-start.51 = (bf16[1024,128]{1,0:T(8,128)(2,1)}, bf16[1024,128]{1,0:T(8,128)(2,1)S(1)}, u32[]{:S(2)}, u32[]{:S(2)}) collective-permute-start(bf16[1024,128]{1,0:T(8,128)(2,1)} %fusion.9), channel_id=1, source_target_pairs={{0,2},{1,3},{2,0},{3,1},{4,6},{5,7},{6,4},{7,5},{8,10},{9,11},{10,... | collective-permute-start | bytes 786440 | tf_op jit(solution)/shard_map/ppermute | solution.py:157
  182.3 5.0 %collective-permute-start.52 = (bf16[512,128]{1,0:T(8,128)(2,1)S(1)}, bf16[512,128]{1,0:T(8,128)(2,1)S(1)}, u32[]{:S(2)}, u32[]{:S(2)}) collective-permute-start(bf16[512,128]{1,0:T(8,128)(2,1)S(1)} %slice.156), channel_id=1, source_target_pairs={{0,4},{4,0},{8,12},{12,8},{16,20},{20,16},{24,28},{28,24},{1,5},{5... | collective-permute-start | bytes 393224 | tf_op jit(solution)/shard_map/ppermute | solution.py:162
  187.6 5.0 %collective-permute-start.53 = (bf16[512,128]{1,0:T(8,128)(2,1)S(1)}, bf16[512,128]{1,0:T(8,128)(2,1)S(1)}, u32[]{:S(2)}, u32[]{:S(2)}) collective-permute-start(bf16[512,128]{1,0:T(8,128)(2,1)S(1)} %get-tuple-element.68), channel_id=1, source_target_pairs={{0,4},{4,0},{8,12},{12,8},{16,20},{20,16},{24,28},{28,24},{1,5},{5... | collective-permute-start | bytes 393224 | tf_op jit(solution)/shard_map/ppermute | solution.py:168
  192.6 6.4 %collective-permute-start.54 = (bf16[1024,128]{1,0:T(8,128)(2,1)S(1)}, bf16[1024,128]{1,0:T(8,128)(2,1)S(1)}, u32[]{:S(2)}, u32[]{:S(2)}) collective-permute-start(bf16[1024,128]{1,0:T(8,128)(2,1)S(1)} %pad_maximum_fusion.8), channel_id=1, source_target_pairs={{0,2},{1,3},{2,0},{3,1},{4,6},{5,7},{6,4},{7,5},{8,10},{9,11},{10,... | collective-permute-start | bytes 786440 | tf_op jit(solution)/shard_map/ppermute | solution.py:172
  194.6 5.9 %collective-permute-start.55 = (bf16[1024,128]{1,0:T(8,128)(2,1)S(1)}, bf16[1024,128]{1,0:T(8,128)(2,1)S(1)}, u32[]{:S(2)}, u32[]{:S(2)}) collective-permute-start(bf16[1024,128]{1,0:T(8,128)(2,1)S(1)} %pad_maximum_fusion.8), channel_id=1, source_target_pairs={{0,1},{1,0},{2,3},{3,2},{4,5},{5,4},{6,7},{7,6},{8,9},{9,8},{10,11... | collective-permute-start | bytes 786440 | tf_op jit(solution)/shard_map/ppermute | solution.py:173
  (50 other events, 273.1 us)

commit v20 on v17

--- a/solution.py
+++ b/solution.py
@@ -138,6 +138,9 @@
         (fwd.astype(jnp.float32) * voxel_input_vector[None, :]).astype(jnp.bfloat16)
     )
     weight = measurement_weight.reshape(sl, 2, ds)
+    w_mine = jnp.where(first, weight[:, 0], weight[:, 1])
+    w_other = jnp.where(first, weight[:, 1], weight[:, 0])
+    weight = jnp.concatenate([w_mine, lax.ppermute(w_other, "src", swap)], axis=0)
     back = jnp.zeros((2 * sl, vl), jnp.float32)
     nxt = _zline(adjoint_voxel_field[:r], na)
     for c in range(chunks):
@@ -158,13 +161,7 @@
                 halves[k].astype(jnp.bfloat16), "vox", chip_perm(k)
             ).astype(jnp.float32)
 
-        own, theirs = share[:sl], lax.ppermute(share[sl:], "src", swap)
-        pred = jnp.stack([jnp.where(first, own, theirs), jnp.where(first, theirs, own)], axis=1)
-        w_c = weight[:, :, c * r:(c + 1) * r]
-        wt = (w_c * pred).astype(jnp.bfloat16)
-        mine = jnp.where(first, wt[:, 0], wt[:, 1])
-        other = jnp.where(first, wt[:, 1], wt[:, 0])
-        piece = jnp.concatenate([mine, lax.ppermute(other, "src", swap)], axis=0)
+        piece = (weight[:, c * r:(c + 1) * r] * share).astype(jnp.bfloat16)
 
         got = [(me, piece)]
         for k in range(1, m):

time: 197 us -> 171 us (0.87)
  waiting for transfers between devices: 116 us -> 86.1 us
  starting transfers between devices: 34.7 us -> 38.8 us
  local copies, waits for them, and re-layouts: 15.3 us -> 12.7 us
  matrix products: 19.8 us -> 22.1 us
    ppermute x4 -> x1, waiting for transfers between devices: 22.1 us -> 2.59 us  [_fast(): lax.ppermute(w_other, 'src', swap)]
    ppermute x2, waiting for transfers between devices: 22.7 us -> 15 us  [_fast(): lax.ppermute(halves[k].astype(jnp.bfloat16), 'vox', chip_perm(k))]
    ppermute x1, waiting for transfers between devices: 6.03 us -> 0.01 us  [_fast(): lax.ppermute(forward_voxel_field, 'src', swap)]
    ppermute x4 -> x1, starting transfers between devices: 5.74 us -> 1.04 us  [_fast(): lax.ppermute(w_other, 'src', swap)]
    ppermute x3, starting transfers between devices: 1.44 us -> 5.82 us  [_sum_over_src(): v = v + lax.ppermute(v, 'src', [(i, i ^ b) for i in range(n)])]
    ppermute x2, waiting for transfers between devices: 10.9 us -> 15 us  [_fast(): lax.ppermute(piece, 'vox', chip_perm(k))]
    ppermute x3, waiting for transfers between devices: 10.4 us -> 6.36 us  [_sum_over_src(): v = v + lax.ppermute(v, 'src', [(i, i ^ b) for i in range(n)])]
    ppermute x12, waiting for transfers between devices: 41.8 us -> 45.7 us  [_zline(): cur = lax.ppermute(cur, 'src', pairs)]
  transfers between devices with their start and end apart: 32 -> 29, of which waited for: 20 -> 16; matrix products, arithmetic and copies ran while one was open for 14% -> 16% of each run, Pallas kernels for 0% -> 0%
where the time goes in v20:
time: 171 us
  waiting for transfers between devices  86.1 us (50%)
  starting transfers between devices  38.8 us (23%)
  matrix products  22.1 us (13%)
  local copies, waits for them, and re-layouts  12.7 us (7%)
  other arithmetic  10.4 us (6%)
    ppermute x12, waiting for transfers between devices, _zline(): cur = lax.ppermute(cur, 'src', pairs)  45.7 us
    ppermute x12, starting transfers between devices, _zline(): cur = lax.ppermute(cur, 'src', pairs)  22.1 us
    ppermute x2, waiting for transfers between devices, _fast(): lax.ppermute(piece, 'vox', chip_perm(k))  15 us
    ppermute x2, waiting for transfers between devices, _fast(): lax.ppermute(halves[k].astype(jnp.bfloat16), 'vox', chip_perm(k))  15 us
    dot_general x8, matrix products, pblock(): lax.dot_general(scaled, rows(col, blk), (((1,), (1,)), ((), ())), preferr...  14.9 us
    unnamed x33, local copies, waits for them, and re-layouts  7.32 us
    dot_general x2, matrix products, _fast(): jnp.dot(jnp.concatenate([w for _, w in got], axis=1), jnp.concatenate([ro...  7.2 us
    ppermute x3, waiting for transfers between devices, _sum_over_src(): v = v + lax.ppermute(v, 'src', [(i, i ^ b) for i in range(n)])  6.36 us
  transfers between devices with their start and end apart: 29, of which 16 were waited for; matrix products, arithmetic and copies ran while one was open for 16% of the time, Pallas kernels for 0%

profile of v20, /device:TPU:0, one launch (start us, length us, event | category | flops | bytes accessed | tf_op | source)
XLA Modules:
  0.0 170.5 jit_solution(13890366769781052804)
XLA Ops:
  0.0 2.2 %fusion.68 = (bf16[256,1024]{1,0:T(8,128)(2,1)S(1)}, bf16[256,1024]{1,0:T(8,128)(2,1)}) fusion(bf16[512,1024]{1,0:T(8,128)(2,1)} %param.5), kind=kLoop, calls=%fused_computation.92 | loop fusion | bytes 2097152 | tf_op jit(solution)/shard_map/slice | solution.py:145
  2.2 1.3 collective-permute-start.8
  3.5 3.0 %collective-permute-start = (bf16[512,1024]{1,0:T(8,128)(2,1)}, bf16[512,1024]{1,0:T(8,128)(2,1)}, u32[]{:S(2)}, u32[]{:S(2)}) collective-permute-start(bf16[512,1024]{1,0:T(8,128)(2,1)} %param.4), channel_id=1, source_target_pairs={{0,4},{4,0},{8,12},{12,8},{16,20},{20,16},{24,28},{28,24},{1,5},{5... | collective-permute-start | bytes 3145736 | tf_op jit(solution)/shard_map/ppermute | solution.py:135
  6.5 5.3 %collective-permute-start.9 = (bf16[256,1024]{1,0:T(8,128)(2,1)S(1)}, bf16[256,1024]{1,0:T(8,128)(2,1)}, u32[]{:S(2)}, u32[]{:S(2)}) collective-permute-start(bf16[256,1024]{1,0:T(8,128)(2,1)S(1)} %get-tuple-element.27), channel_id=1, source_target_pairs={{0,8},{4,12},{8,16},{12,20},{16,24},{20,28},{1,9},{5,13},{9,17},{1... | collective-permute-start | bytes 1572872 | tf_op jit(solution)/shard_map/ppermute | solution.py:104
  11.9 7.2 %collective-permute-done.8 = bf16[256,1024]{1,0:T(8,128)(2,1)S(1)} collective-permute-done((bf16[256,1024]{1,0:T(8,128)(2,1)S(1)}, bf16[256,1024]{1,0:T(8,128)(2,1)S(1)}, u32[]{:S(2)}, u32[]{:S(2)}) %collective-permute-start.8) | collective-permute-done | bytes 524320 | tf_op jit(solution)/shard_map/ppermute | solution.py:104
  19.1 1.3 collective-permute-start.12
  20.3 1.3 collective-permute-done.9
  21.7 1.5 collective-permute-start.10
  23.2 1.8 %copy.6 = f32[512,1024]{0,1:T(8,128)} copy(f32[512,1024]{1,0:T(8,128)S(1)} %copy-done.4) | data formatting | bytes 4194304 | tf_op args[3]
  25.0 9.3 %collective-permute-done.12 = bf16[256,1024]{1,0:T(8,128)(2,1)} collective-permute-done((bf16[256,1024]{1,0:T(8,128)(2,1)S(1)}, bf16[256,1024]{1,0:T(8,128)(2,1)}, u32[]{:S(2)}, u32[]{:S(2)}) %collective-permute-start.12) | collective-permute-done | bytes 524320 | tf_op jit(solution)/shard_map/ppermute | solution.py:104
  34.3 1.3 collective-permute-start.13
  35.6 2.1 %fusion = bf16[1024,1024]{1,0:T(8,128)(2,1)S(1)} fusion(f32[1024]{0:T(1024)S(1)} %copy-done.8, bf16[512,1024]{1,0:T(8,128)(2,1)} %collective-permute-done, bf16[512,1024]{1,0:T(8,128)(2,1)} %param.4), kind=kLoop, calls=%fused_computation.2 | loop fusion | flops 6291456 | bytes 4198400 | tf_op jit(solution)/shard_map/convert_element_type | solution.py:138
  39.5 9.1 %collective-permute-done.13 = bf16[256,1024]{1,0:T(8,128)(2,1)S(1)} collective-permute-done((bf16[256,1024]{1,0:T(8,128)(2,1)}, bf16[256,1024]{1,0:T(8,128)(2,1)S(1)}, u32[]{:S(2)}, u32[]{:S(2)}) %collective-permute-start.13) | collective-permute-done | bytes 524320 | tf_op jit(solution)/shard_map/ppermute | solution.py:104
  49.0 1.8 %fusion.51 = f32[1024,256]{1,0:T(8,128)} fusion(bf16[1024,1024]{1,0:T(8,128)(2,1)S(1)} %fusion, bf16[1024,1024]{1,0:T(8,128)(2,1)S(1)} %pad_maximum_fusion.2, s32[]{:T(128)S(6)} %select_n.203), kind=kOutput, calls=%fused_computation.61 | convolution fusion | flops 536870912 | bytes 3670020 | tf_op jit(solution)/shard_map/dot_general | solution.py:150
  51.7 1.2 fusion.67
  52.9 2.5 %copy.11 = f32[512,1,512]{2,0,1:T(8,128)} copy(f32[512,1,512]{0,2,1:T(8,128)} %get-tuple-element.25) | data formatting | bytes 2097152
  55.4 1.3 copy.12
  56.7 2.8 %select_bitcast_fusion.1 = (f32[512,512]{1,0:T(8,128)S(1)}, f32[512,512]{1,0:T(8,128)}) fusion(f32[512,1,512]{2,0,1:T(8,128)} %copy.11, f32[512,1,512]{2,0,1:T(8,128)} %copy.12, pred[]{:T(512)S(6)} %eq.32), kind=kLoop, calls=%fused_computation.54 | loop fusion | flops 524288 | bytes 4194305 | tf_op jit(solution)/shard_map/jit(_where)/select_n | solution.py:141
  60.5 2.8 %fusion.54 = f32[1024,256]{1,0:T(8,128)} fusion(bf16[1024,1024]{1,0:T(8,128)(2,1)S(1)} %fusion, bf16[1024,1024]{1,0:T(8,128)(2,1)} %copy-done, s32[]{:T(128)S(6)} %select_n.198), kind=kOutput, calls=%fused_computation.64 | convolution fusion | flops 536870912 | bytes 3670020 | tf_op jit(solution)/shard_map/dot_general | solution.py:150
  63.3 1.3 collective-permute-start.1
  64.6 5.3 %collective-permute-start.2 = (bf16[256,1024]{1,0:T(8,128)(2,1)}, bf16[256,1024]{1,0:T(8,128)(2,1)}, u32[]{:S(2)}, u32[]{:S(2)}) collective-permute-start(bf16[256,1024]{1,0:T(8,128)(2,1)} %get-tuple-element.28), channel_id=1, source_target_pairs={{0,8},{4,12},{8,16},{12,20},{16,24},{20,28},{1,9},{5,13},{9,17},{1... | collective-permute-start | bytes 1572872 | tf_op jit(solution)/shard_map/ppermute | solution.py:104
  69.9 3.0 %fusion.34 = bf16[1024,256]{1,0:T(8,128)(2,1)} fusion(f32[1024,256]{1,0:T(8,128)} %collective-permute-done.15, bf16[1024,1024]{1,0:T(8,128)(2,1)S(1)} %fusion, bf16[1024,1024]{1,0:T(8,128)(2,1)} %copy-done, s32[]{:T(128)S(6)} %select_n.201), kind=kOutput, calls=%fused_computation.45 | convolution fusion | flops 537395200 | bytes 4194308 | tf_op jit(solution)/shard_map/dot_general | solution.py:150
  72.9 1.5 collective-permute-start.16
  74.4 5.4 %collective-permute-done.1 = bf16[256,1024]{1,0:T(8,128)(2,1)} collective-permute-done((bf16[256,1024]{1,0:T(8,128)(2,1)}, bf16[256,1024]{1,0:T(8,128)(2,1)}, u32[]{:S(2)}, u32[]{:S(2)}) %collective-permute-start.1) | collective-permute-done | bytes 524320 | tf_op jit(solution)/shard_map/ppermute | solution.py:104
  79.8 1.3 collective-permute-start.5
  81.9 2.6 %collective-permute-done.7 = f32[512,512]{1,0:T(8,128)} collective-permute-done((f32[512,512]{1,0:T(8,128)}, f32[512,512]{1,0:T(8,128)}, u32[]{:S(2)}, u32[]{:S(2)}) %collective-permute-start.7) | collective-permute-done | bytes 1048608 | tf_op jit(solution)/shard_map/ppermute | solution.py:143
  84.4 2.5 %collective-permute-done.16 = bf16[1024,256]{1,0:T(8,128)(2,1)} collective-permute-done((bf16[1024,256]{1,0:T(8,128)(2,1)}, bf16[1024,256]{1,0:T(8,128)(2,1)}, u32[]{:S(2)}, u32[]{:S(2)}) %collective-permute-start.16) | collective-permute-done | bytes 524320 | tf_op jit(solution)/shard_map/ppermute | solution.py:160
  87.0 2.5 %fusion.38 = bf16[1024,256]{1,0:T(8,128)(2,1)S(1)} fusion(f32[512,512]{1,0:T(8,128)S(1)} %get-tuple-element.23, f32[512,512]{1,0:T(8,128)} %collective-permute-done.7, bf16[1024,256]{1,0:T(8,128)(2,1)} %collective-permute-done.16, f32[1024,256]{1,0:T(8,128)} %collective-permute-done.14, bf16[1024,1024]{1,0:T(8,128)(2,1)S(1)} %fusion, ...), kind=kOutput, calls=%fused_computation.49 | convolution fusion | flops 538443776 | bytes 6815748 | tf_op jit(solution)/shard_map/dot_general | solution.py:150
  89.4 1.6 collective-permute-start.17
  91.0 4.9 %collective-permute-done.5 = bf16[256,1024]{1,0:T(8,128)(2,1)} collective-permute-done((bf16[256,1024]{1,0:T(8,128)(2,1)}, bf16[256,1024]{1,0:T(8,128)(2,1)}, u32[]{:S(2)}, u32[]{:S(2)}) %collective-permute-start.5) | collective-permute-done | bytes 524320 | tf_op jit(solution)/shard_map/ppermute | solution.py:104
  95.9 1.3 collective-permute-start.6
  99.2 3.2 %collective-permute-done.17 = bf16[1024,256]{1,0:T(8,128)(2,1)S(1)} collective-permute-done((bf16[1024,256]{1,0:T(8,128)(2,1)S(1)}, bf16[1024,256]{1,0:T(8,128)(2,1)S(1)}, u32[]{:S(2)}, u32[]{:S(2)}) %collective-permute-start.17) | collective-permute-done | bytes 524320 | tf_op jit(solution)/shard_map/ppermute | solution.py:168
  102.4 8.5 %collective-permute-done.6 = bf16[256,1024]{1,0:T(8,128)(2,1)S(1)} collective-permute-done((bf16[256,1024]{1,0:T(8,128)(2,1)}, bf16[256,1024]{1,0:T(8,128)(2,1)S(1)}, u32[]{:S(2)}, u32[]{:S(2)}) %collective-permute-start.6) | collective-permute-done | bytes 524320 | tf_op jit(solution)/shard_map/ppermute | solution.py:104
  112.1 1.2 pad_maximum_fusion.1
  115.8 1.3 collective-permute-done.21
  117.9 1.6 collective-permute-start.22
  119.5 12.5 %collective-permute-done.22 = bf16[1024,256]{1,0:T(8,128)(2,1)S(1)} collective-permute-done((bf16[1024,256]{1,0:T(8,128)(2,1)S(1)}, bf16[1024,256]{1,0:T(8,128)(2,1)S(1)}, u32[]{:S(2)}, u32[]{:S(2)}) %collective-permute-start.22) | collective-permute-done | bytes 524320 | tf_op jit(solution)/shard_map/ppermute | solution.py:160
  132.0 2.7 %fusion.40 = bf16[1024,256]{1,0:T(8,128)(2,1)} fusion(f32[512,512]{1,0:T(8,128)} %collective-permute-done.7, f32[512,512]{1,0:T(8,128)S(1)} %get-tuple-element.23, bf16[1024,256]{1,0:T(8,128)(2,1)S(1)} %collective-permute-done.22, f32[1024,256]{1,0:T(8,128)S(1)} %collective-permute-done.20, bf16[1024,1024]{1,0:T(8,128)(2,1)S(1)} %fusion, ...), kind=kOutput, calls=%fused_computation.52 | convolution fusion | flops 538443776 | bytes 6815748 | tf_op jit(solution)/shard_map/dot_general | solution.py:150
  134.7 1.5 collective-permute-start.23
  136.1 11.9 %collective-permute-done.23 = bf16[1024,256]{1,0:T(8,128)(2,1)S(1)} collective-permute-done((bf16[1024,256]{1,0:T(8,128)(2,1)}, bf16[1024,256]{1,0:T(8,128)(2,1)S(1)}, u32[]{:S(2)}, u32[]{:S(2)}) %collective-permute-start.23) | collective-permute-done | bytes 524320 | tf_op jit(solution)/shard_map/ppermute | solution.py:168
  148.0 1.9 %constant_dynamic-slice_fusion.7 = (bf16[256,1024]{1,0:T(8,128)(2,1)S(1)}, bf16[256,1024]{1,0:T(8,128)(2,1)S(1)}, bf16[256,1024]{1,0:T(8,128)(2,1)S(1)}, bf16[256,1024]{1,0:T(8,128)(2,1)S(1)}) fusion(bf16[1024,1024]{1,0:T(8,128)(2,1)} %copy-done, s32[]{:T(128)S(6)} %select_n.205, s32[]{:T(128)S(6)} %select_n.212, s32[]{:T(128)S(6)} %select_n.210, ...), kind=kLoop, calls=%fused_computation.84 | loop fusion | bytes 4194320 | tf_op jit(solution)/shard_map/dynamic_slice | solution.py:132
  150.5 3.5 %fusion.17 = f32[1024,1024]{1,0:T(8,128)S(1)} fusion(bf16[1024,256]{1,0:T(8,128)(2,1)S(1)} %collective-permute-done.25, bf16[1024,256]{1,0:T(8,128)(2,1)S(1)} %collective-permute-done.24, bf16[1024,256]{1,0:T(8,128)(2,1)S(1)} %collective-permute-done.23, bf16[1024,256]{1,0:T(8,128)(2,1)} %fusion.40, bf16[256,1024]{1,0:T(8,128)(2,1)S(1)} %get-tuple-element.20, ...), kind=kOutput, calls=%fused_computation.24 | convolution fusion | flops 2164260864 | bytes 8388608 | tf_op jit(solution)/shard_map/dot_general | solution.py:176
  154.1 3.7 %fusion.1 = f32[1024]{0:T(1024)S(1)} fusion(f32[1024,1024]{1,0:T(8,128)S(1)} %fusion.17, bf16[512,1024]{1,0:T(8,128)(2,1)} %collective-permute-done, bf16[512,1024]{1,0:T(8,128)(2,1)S(1)} %copy-done.5, bf16[256,1024]{1,0:T(8,128)(2,1)S(1)} %get-tuple-element.16, bf16[256,1024]{1,0:T(8,128)(2,1)S(1)} %get-tuple-element.17, ...), kind=kOutput, calls=%fused_computation.3 | convolution fusion | flops 2171599872 | bytes 10489856 | tf_op jit(solution)/shard_map/dot_general | solution.py:176
  157.7 1.8 %collective-permute-start.26 = (f32[1024]{0:T(1024)S(1)}, f32[1024]{0:T(1024)S(1)}, u32[]{:S(2)}, u32[]{:S(2)}) collective-permute-start(f32[1024]{0:T(1024)S(1)} %fusion.1), channel_id=1, source_target_pairs={{0,4},{4,0},{8,12},{12,8},{16,20},{20,16},{24,28},{28,24},{1,5},{5... | collective-permute-start | bytes 12296 | tf_op jit(solution)/shard_map/ppermute | solution.py:84
  159.6 1.9 %collective-permute-done.26 = f32[1024]{0:T(1024)S(1)} collective-permute-done((f32[1024]{0:T(1024)S(1)}, f32[1024]{0:T(1024)S(1)}, u32[]{:S(2)}, u32[]{:S(2)}) %collective-permute-start.26) | collective-permute-done | bytes 4128 | tf_op jit(solution)/shard_map/ppermute | solution.py:84
  162.1 2.9 %collective-permute-done.27 = f32[1024]{0:T(1024)S(1)} collective-permute-done((f32[1024]{0:T(1024)S(1)}, f32[1024]{0:T(1024)S(1)}, u32[]{:S(2)}, u32[]{:S(2)}) %collective-permute-start.27) | collective-permute-done | bytes 4128 | tf_op jit(solution)/shard_map/ppermute | solution.py:84
  165.0 3.3 %collective-permute-start.28 = (f32[1024]{0:T(1024)S(1)}, f32[1024]{0:T(1024)S(1)}, u32[]{:S(2)}, u32[]{:S(2)}) collective-permute-start(f32[1024]{0:T(1024)S(1)} %add.196), channel_id=1, source_target_pairs={{0,16},{4,20},{8,24},{12,28},{16,0},{20,4},{24,8},{28,12},{1,17},{... | collective-permute-start | bytes 12296 | tf_op jit(solution)/shard_map/ppermute | solution.py:84
  168.3 1.6 collective-permute-done.28
  (70 shorter events, 13.1 us)
Async XLA Ops:
  0.0 23.2 %copy-start.4 = (f32[512,1024]{1,0:T(8,128)S(1)}, f32[512,1024]{1,0:T(8,128)}, u32[]{:S(2)}) copy-start(f32[512,1024]{1,0:T(8,128)} %param.7) | copy-start | bytes 6291460
  2.2 16.8 %collective-permute-start.8 = (bf16[256,1024]{1,0:T(8,128)(2,1)S(1)}, bf16[256,1024]{1,0:T(8,128)(2,1)S(1)}, u32[]{:S(2)}, u32[]{:S(2)}) collective-permute-start(bf16[256,1024]{1,0:T(8,128)(2,1)S(1)} %get-tuple-element.27), channel_id=1, source_target_pairs={{8,0},{12,4},{16,8},{20,12},{24,16},{28,20},{9,1},{13,5},{17,9},{2... | collective-permute-start | bytes 1572872 | tf_op jit(solution)/shard_map/ppermute | solution.py:104
  3.5 32.0 %collective-permute-start = (bf16[512,1024]{1,0:T(8,128)(2,1)}, bf16[512,1024]{1,0:T(8,128)(2,1)}, u32[]{:S(2)}, u32[]{:S(2)}) collective-permute-start(bf16[512,1024]{1,0:T(8,128)(2,1)} %param.4), channel_id=1, source_target_pairs={{0,4},{4,0},{8,12},{12,8},{16,20},{20,16},{24,28},{28,24},{1,5},{5... | collective-permute-start | bytes 3145736 | tf_op jit(solution)/shard_map/ppermute | solution.py:135
  6.5 15.1 %collective-permute-start.9 = (bf16[256,1024]{1,0:T(8,128)(2,1)S(1)}, bf16[256,1024]{1,0:T(8,128)(2,1)}, u32[]{:S(2)}, u32[]{:S(2)}) collective-permute-start(bf16[256,1024]{1,0:T(8,128)(2,1)S(1)} %get-tuple-element.27), channel_id=1, source_target_pairs={{0,8},{4,12},{8,16},{12,20},{16,24},{20,28},{1,9},{5,13},{9,17},{1... | collective-permute-start | bytes 1572872 | tf_op jit(solution)/shard_map/ppermute | solution.py:104
  19.1 15.2 %collective-permute-start.12 = (bf16[256,1024]{1,0:T(8,128)(2,1)S(1)}, bf16[256,1024]{1,0:T(8,128)(2,1)}, u32[]{:S(2)}, u32[]{:S(2)}) collective-permute-start(bf16[256,1024]{1,0:T(8,128)(2,1)S(1)} %collective-permute-done.8), channel_id=1, source_target_pairs={{8,0},{12,4},{16,8},{20,12},{9,1},{13,5},{17,9},{21,13},{10,2},{14... | collective-permute-start | bytes 1572872 | tf_op jit(solution)/shard_map/ppermute | solution.py:104
  21.7 16.0 %collective-permute-start.10 = (bf16[256,1024]{1,0:T(8,128)(2,1)}, bf16[256,1024]{1,0:T(8,128)(2,1)}, u32[]{:S(2)}, u32[]{:S(2)}) collective-permute-start(bf16[256,1024]{1,0:T(8,128)(2,1)} %collective-permute-done.9), channel_id=1, source_target_pairs={{8,16},{12,20},{16,24},{20,28},{9,17},{13,21},{17,25},{21,29},{10,... | collective-permute-start | bytes 1572872 | tf_op jit(solution)/shard_map/ppermute | solution.py:104
  23.2 12.4 %copy-start.8 = (f32[1024]{0:T(1024)S(1)}, f32[1024]{0:T(1024)}, u32[]{:S(2)}) copy-start(f32[1024]{0:T(1024)} %param.6) | copy-start | bytes 12292
  34.3 14.4 %collective-permute-start.13 = (bf16[256,1024]{1,0:T(8,128)(2,1)}, bf16[256,1024]{1,0:T(8,128)(2,1)S(1)}, u32[]{:S(2)}, u32[]{:S(2)}) collective-permute-start(bf16[256,1024]{1,0:T(8,128)(2,1)} %collective-permute-done.12), channel_id=1, source_target_pairs={{8,0},{12,4},{9,1},{13,5},{10,2},{14,6},{11,3},{15,7}} | collective-permute-start | bytes 1572872 | tf_op jit(solution)/shard_map/ppermute | solution.py:104
  37.7 11.0 %collective-permute-start.11 = (bf16[256,1024]{1,0:T(8,128)(2,1)}, bf16[256,1024]{1,0:T(8,128)(2,1)S(1)}, u32[]{:S(2)}, u32[]{:S(2)}) collective-permute-start(bf16[256,1024]{1,0:T(8,128)(2,1)} %collective-permute-done.10), channel_id=1, source_target_pairs={{16,24},{20,28},{17,25},{21,29},{18,26},{22,30},{19,27},{23,31}} | collective-permute-start | bytes 1572872 | tf_op jit(solution)/shard_map/ppermute | solution.py:104
  49.0 1.8 %copy-start = (bf16[1024,1024]{1,0:T(8,128)(2,1)}, bf16[1024,1024]{1,0:T(8,128)(2,1)S(1)}, u32[]{:S(2)}) copy-start(bf16[1024,1024]{1,0:T(8,128)(2,1)S(1)} %pad_maximum_fusion.2) | copy-start | bytes 6291460
  49.0 2.7 %copy-start.3 = (f32[512,1024]{0,1:T(8,128)S(1)}, f32[512,1024]{0,1:T(8,128)}, u32[]{:S(2)}) copy-start(f32[512,1024]{0,1:T(8,128)} %copy.6) | copy-start | bytes 6291460
  50.8 19.1 %collective-permute-start.15 = (f32[1024,256]{1,0:T(8,128)}, f32[1024,256]{1,0:T(8,128)}, u32[]{:S(2)}, u32[]{:S(2)}) collective-permute-start(f32[1024,256]{1,0:T(8,128)} %fusion.51), channel_id=1, source_target_pairs={{0,1},{1,0},{2,3},{3,2},{4,5},{5,4},{6,7},{7,6},{8,9},{9,8},{10,11... | collective-permute-start | bytes 3145736 | tf_op jit(solution)/shard_map/ppermute | solution.py:157
  59.5 25.0 %collective-permute-start.7 = (f32[512,512]{1,0:T(8,128)}, f32[512,512]{1,0:T(8,128)}, u32[]{:S(2)}, u32[]{:S(2)}) collective-permute-start(f32[512,512]{1,0:T(8,128)} %get-tuple-element.24), channel_id=1, source_target_pairs={{0,4},{4,0},{8,12},{12,8},{16,20},{20,16},{24,28},{28,24},{1,5},{5... | collective-permute-start | bytes 3145736 | tf_op jit(solution)/shard_map/ppermute | solution.py:143
  63.3 21.2 %collective-permute-start.14 = (f32[1024,256]{1,0:T(8,128)}, f32[1024,256]{1,0:T(8,128)}, u32[]{:S(2)}, u32[]{:S(2)}) collective-permute-start(f32[1024,256]{1,0:T(8,128)} %fusion.54), channel_id=1, source_target_pairs={{0,1},{1,0},{2,3},{3,2},{4,5},{5,4},{6,7},{7,6},{8,9},{9,8},{10,11... | collective-permute-start | bytes 3145736 | tf_op jit(solution)/shard_map/ppermute | solution.py:157
  63.3 16.5 %collective-permute-start.1 = (bf16[256,1024]{1,0:T(8,128)(2,1)}, bf16[256,1024]{1,0:T(8,128)(2,1)}, u32[]{:S(2)}, u32[]{:S(2)}) collective-permute-start(bf16[256,1024]{1,0:T(8,128)(2,1)} %get-tuple-element.28), channel_id=1, source_target_pairs={{8,0},{12,4},{16,8},{20,12},{24,16},{28,20},{9,1},{13,5},{17,9},{2... | collective-permute-start | bytes 1572872 | tf_op jit(solution)/shard_map/ppermute | solution.py:104
  64.6 16.6 %collective-permute-start.2 = (bf16[256,1024]{1,0:T(8,128)(2,1)}, bf16[256,1024]{1,0:T(8,128)(2,1)}, u32[]{:S(2)}, u32[]{:S(2)}) collective-permute-start(bf16[256,1024]{1,0:T(8,128)(2,1)} %get-tuple-element.28), channel_id=1, source_target_pairs={{0,8},{4,12},{8,16},{12,20},{16,24},{20,28},{1,9},{5,13},{9,17},{1... | collective-permute-start | bytes 1572872 | tf_op jit(solution)/shard_map/ppermute | solution.py:104
  72.9 14.1 %collective-permute-start.16 = (bf16[1024,256]{1,0:T(8,128)(2,1)}, bf16[1024,256]{1,0:T(8,128)(2,1)}, u32[]{:S(2)}, u32[]{:S(2)}) collective-permute-start(bf16[1024,256]{1,0:T(8,128)(2,1)} %fusion.34), channel_id=1, source_target_pairs={{0,2},{1,3},{2,0},{3,1},{4,6},{5,7},{6,4},{7,5},{8,10},{9,11},{10,... | collective-permute-start | bytes 1572872 | tf_op jit(solution)/shard_map/ppermute | solution.py:160
  79.8 16.0 %collective-permute-start.5 = (bf16[256,1024]{1,0:T(8,128)(2,1)}, bf16[256,1024]{1,0:T(8,128)(2,1)}, u32[]{:S(2)}, u32[]{:S(2)}) collective-permute-start(bf16[256,1024]{1,0:T(8,128)(2,1)} %collective-permute-done.1), channel_id=1, source_target_pairs={{8,0},{12,4},{16,8},{20,12},{9,1},{13,5},{17,9},{21,13},{10,2},{14... | collective-permute-start | bytes 1572872 | tf_op jit(solution)/shard_map/ppermute | solution.py:104
  81.1 16.0 %collective-permute-start.3 = (bf16[256,1024]{1,0:T(8,128)(2,1)}, bf16[256,1024]{1,0:T(8,128)(2,1)S(1)}, u32[]{:S(2)}, u32[]{:S(2)}) collective-permute-start(bf16[256,1024]{1,0:T(8,128)(2,1)} %collective-permute-done.2), channel_id=1, source_target_pairs={{8,16},{12,20},{16,24},{20,28},{9,17},{13,21},{17,25},{21,29},{10,... | collective-permute-start | bytes 1572872 | tf_op jit(solution)/shard_map/ppermute | solution.py:104
  89.4 22.7 %copy-start.6 = (bf16[1024,256]{1,0:T(8,128)(2,1)}, bf16[1024,256]{1,0:T(8,128)(2,1)S(1)}, u32[]{:S(2)}) copy-start(bf16[1024,256]{1,0:T(8,128)(2,1)S(1)} %fusion.38) | copy-start | bytes 1572868
  89.4 13.0 %collective-permute-start.17 = (bf16[1024,256]{1,0:T(8,128)(2,1)S(1)}, bf16[1024,256]{1,0:T(8,128)(2,1)S(1)}, u32[]{:S(2)}, u32[]{:S(2)}) collective-permute-start(bf16[1024,256]{1,0:T(8,128)(2,1)S(1)} %fusion.38), channel_id=1, source_target_pairs={{0,2},{1,3},{2,0},{3,1},{4,6},{5,7},{6,4},{7,5},{8,10},{9,11},{10,... | collective-permute-start | bytes 1572872 | tf_op jit(solution)/shard_map/ppermute | solution.py:168
  95.9 15.1 %collective-permute-start.6 = (bf16[256,1024]{1,0:T(8,128)(2,1)}, bf16[256,1024]{1,0:T(8,128)(2,1)S(1)}, u32[]{:S(2)}, u32[]{:S(2)}) collective-permute-start(bf16[256,1024]{1,0:T(8,128)(2,1)} %collective-permute-done.5), channel_id=1, source_target_pairs={{8,0},{12,4},{9,1},{13,5},{10,2},{14,6},{11,3},{15,7}} | collective-permute-start | bytes 1572872 | tf_op jit(solution)/shard_map/ppermute | solution.py:104
  97.2 13.8 %collective-permute-start.4 = (bf16[256,1024]{1,0:T(8,128)(2,1)S(1)}, bf16[256,1024]{1,0:T(8,128)(2,1)S(1)}, u32[]{:S(2)}, u32[]{:S(2)}) collective-permute-start(bf16[256,1024]{1,0:T(8,128)(2,1)S(1)} %collective-permute-done.3), channel_id=1, source_target_pairs={{16,24},{20,28},{17,25},{21,29},{18,26},{22,30},{19,27},{23,31}} | collective-permute-start | bytes 1572872 | tf_op jit(solution)/shard_map/ppermute | solution.py:104
  99.2 14.2 %collective-permute-start.18 = (bf16[1024,256]{1,0:T(8,128)(2,1)S(1)}, bf16[1024,256]{1,0:T(8,128)(2,1)S(1)}, u32[]{:S(2)}, u32[]{:S(2)}) collective-permute-start(bf16[1024,256]{1,0:T(8,128)(2,1)S(1)} %fusion.38), channel_id=1, source_target_pairs={{0,1},{1,0},{2,3},{3,2},{4,5},{5,4},{6,7},{7,6},{8,9},{9,8},{10,11... | collective-permute-start | bytes 1572872 | tf_op jit(solution)/shard_map/ppermute | solution.py:169
  102.4 10.9 %copy-start.9 = (bf16[1024,256]{1,0:T(8,128)(2,1)}, bf16[1024,256]{1,0:T(8,128)(2,1)S(1)}, u32[]{:S(2)}) copy-start(bf16[1024,256]{1,0:T(8,128)(2,1)S(1)} %collective-permute-done.17) | copy-start | bytes 1572868
  102.4 11.0 %collective-permute-start.19 = (bf16[1024,256]{1,0:T(8,128)(2,1)S(1)}, bf16[1024,256]{1,0:T(8,128)(2,1)S(1)}, u32[]{:S(2)}, u32[]{:S(2)}) collective-permute-start(bf16[1024,256]{1,0:T(8,128)(2,1)S(1)} %collective-permute-done.17), channel_id=1, source_target_pairs={{0,1},{1,0},{2,3},{3,2},{4,5},{5,4},{6,7},{7,6},{8,9},{9,8},{10,11... | collective-permute-start | bytes 1572872 | tf_op jit(solution)/shard_map/ppermute | solution.py:169
  113.4 18.6 %copy-start.1 = (bf16[1024,1024]{1,0:T(8,128)(2,1)}, bf16[1024,1024]{1,0:T(8,128)(2,1)S(1)}, u32[]{:S(2)}) copy-start(bf16[1024,1024]{1,0:T(8,128)(2,1)S(1)} %pad_maximum_fusion.1) | copy-start | bytes 6291460
  113.4 0.9 copy-start.11
  113.4 1.1 copy-start.13
  114.5 2.7 %collective-permute-start.21 = (f32[1024,256]{1,0:T(8,128)S(1)}, f32[1024,256]{1,0:T(8,128)S(1)}, u32[]{:S(2)}, u32[]{:S(2)}) collective-permute-start(f32[1024,256]{1,0:T(8,128)S(1)} %fusion.45), channel_id=1, source_target_pairs={{0,1},{1,0},{2,3},{3,2},{4,5},{5,4},{6,7},{7,6},{8,9},{9,8},{10,11... | collective-permute-start | bytes 3145736 | tf_op jit(solution)/shard_map/ppermute | solution.py:157
  115.2 4.2 %collective-permute-start.20 = (f32[1024,256]{1,0:T(8,128)S(1)}, f32[1024,256]{1,0:T(8,128)S(1)}, u32[]{:S(2)}, u32[]{:S(2)}) collective-permute-start(f32[1024,256]{1,0:T(8,128)S(1)} %fusion.48), channel_id=1, source_target_pairs={{0,1},{1,0},{2,3},{3,2},{4,5},{5,4},{6,7},{7,6},{8,9},{9,8},{10,11... | collective-permute-start | bytes 3145736 | tf_op jit(solution)/shard_map/ppermute | solution.py:157
  117.9 14.0 %collective-permute-start.22 = (bf16[1024,256]{1,0:T(8,128)(2,1)S(1)}, bf16[1024,256]{1,0:T(8,128)(2,1)S(1)}, u32[]{:S(2)}, u32[]{:S(2)}) collective-permute-start(bf16[1024,256]{1,0:T(8,128)(2,1)S(1)} %fusion.35), channel_id=1, source_target_pairs={{0,2},{1,3},{2,0},{3,1},{4,6},{5,7},{6,4},{7,5},{8,10},{9,11},{10,... | collective-permute-start | bytes 1572872 | tf_op jit(solution)/shard_map/ppermute | solution.py:160
  134.7 13.3 %collective-permute-start.23 = (bf16[1024,256]{1,0:T(8,128)(2,1)}, bf16[1024,256]{1,0:T(8,128)(2,1)S(1)}, u32[]{:S(2)}, u32[]{:S(2)}) collective-permute-start(bf16[1024,256]{1,0:T(8,128)(2,1)} %fusion.40), channel_id=1, source_target_pairs={{0,2},{1,3},{2,0},{3,1},{4,6},{5,7},{6,4},{7,5},{8,10},{9,11},{10,... | collective-permute-start | bytes 1572872 | tf_op jit(solution)/shard_map/ppermute | solution.py:168
  136.1 14.3 %collective-permute-start.24 = (bf16[1024,256]{1,0:T(8,128)(2,1)}, bf16[1024,256]{1,0:T(8,128)(2,1)S(1)}, u32[]{:S(2)}, u32[]{:S(2)}) collective-permute-start(bf16[1024,256]{1,0:T(8,128)(2,1)} %fusion.40), channel_id=1, source_target_pairs={{0,1},{1,0},{2,3},{3,2},{4,5},{5,4},{6,7},{7,6},{8,9},{9,8},{10,11... | collective-permute-start | bytes 1572872 | tf_op jit(solution)/shard_map/ppermute | solution.py:169
  148.0 2.4 %collective-permute-start.25 = (bf16[1024,256]{1,0:T(8,128)(2,1)S(1)}, bf16[1024,256]{1,0:T(8,128)(2,1)S(1)}, u32[]{:S(2)}, u32[]{:S(2)}) collective-permute-start(bf16[1024,256]{1,0:T(8,128)(2,1)S(1)} %collective-permute-done.23), channel_id=1, source_target_pairs={{0,1},{1,0},{2,3},{3,2},{4,5},{5,4},{6,7},{7,6},{8,9},{9,8},{10,11... | collective-permute-start | bytes 1572872 | tf_op jit(solution)/shard_map/ppermute | solution.py:169
  148.0 2.2 %copy-start.2 = (bf16[1024,1024]{1,0:T(8,128)(2,1)S(1)}, bf16[1024,1024]{1,0:T(8,128)(2,1)}, u32[]{:S(2)}) copy-start(bf16[1024,1024]{1,0:T(8,128)(2,1)} %copy-done.1) | copy-start | bytes 6291460
  150.4 3.6 %copy-start.5 = (bf16[512,1024]{1,0:T(8,128)(2,1)S(1)}, bf16[512,1024]{1,0:T(8,128)(2,1)}, u32[]{:S(2)}) copy-start(bf16[512,1024]{1,0:T(8,128)(2,1)} %param.4) | copy-start | bytes 3145732
  150.4 3.6 %copy-start.7 = (bf16[1024,256]{1,0:T(8,128)(2,1)S(1)}, bf16[1024,256]{1,0:T(8,128)(2,1)}, u32[]{:S(2)}) copy-start(bf16[1024,256]{1,0:T(8,128)(2,1)} %copy-done.6) | copy-start | bytes 1572868
  150.4 3.6 %copy-start.10 = (bf16[1024,256]{1,0:T(8,128)(2,1)S(1)}, bf16[1024,256]{1,0:T(8,128)(2,1)}, u32[]{:S(2)}) copy-start(bf16[1024,256]{1,0:T(8,128)(2,1)} %copy-done.9) | copy-start | bytes 1572868
  150.5 3.6 %copy-start.12 = (bf16[1024,256]{1,0:T(8,128)(2,1)S(1)}, bf16[1024,256]{1,0:T(8,128)(2,1)}, u32[]{:S(2)}) copy-start(bf16[1024,256]{1,0:T(8,128)(2,1)} %copy-done.11) | copy-start | bytes 1572868
  150.5 3.6 %copy-start.14 = (bf16[1024,256]{1,0:T(8,128)(2,1)S(1)}, bf16[1024,256]{1,0:T(8,128)(2,1)}, u32[]{:S(2)}) copy-start(bf16[1024,256]{1,0:T(8,128)(2,1)} %copy-done.13) | copy-start | bytes 1572868
  157.7 3.7 %collective-permute-start.26 = (f32[1024]{0:T(1024)S(1)}, f32[1024]{0:T(1024)S(1)}, u32[]{:S(2)}, u32[]{:S(2)}) collective-permute-start(f32[1024]{0:T(1024)S(1)} %fusion.1), channel_id=1, source_target_pairs={{0,4},{4,0},{8,12},{12,8},{16,20},{20,16},{24,28},{28,24},{1,5},{5... | collective-permute-start | bytes 12296 | tf_op jit(solution)/shard_map/ppermute | solution.py:84
  161.4 3.6 %collective-permute-start.27 = (f32[1024]{0:T(1024)S(1)}, f32[1024]{0:T(1024)S(1)}, u32[]{:S(2)}, u32[]{:S(2)}) collective-permute-start(f32[1024]{0:T(1024)S(1)} %add.195), channel_id=1, source_target_pairs={{0,8},{4,12},{8,0},{12,4},{16,24},{20,28},{24,16},{28,20},{1,9},{5... | collective-permute-start | bytes 12296 | tf_op jit(solution)/shard_map/ppermute | solution.py:84
  165.0 4.9 %collective-permute-start.28 = (f32[1024]{0:T(1024)S(1)}, f32[1024]{0:T(1024)S(1)}, u32[]{:S(2)}, u32[]{:S(2)}) collective-permute-start(f32[1024]{0:T(1024)S(1)} %add.196), channel_id=1, source_target_pairs={{0,16},{4,20},{8,24},{12,28},{16,0},{20,4},{24,8},{28,12},{1,17},{... | collective-permute-start | bytes 12296 | tf_op jit(solution)/shard_map/ppermute | solution.py:84

commit v21 on v20

--- a/solution.py
+++ b/solution.py
@@ -5,7 +5,7 @@
 from jax import lax
 from jax.sharding import PartitionSpec as P
 
-CHUNKS = 2
+CHUNKS = 1
 
 
 def _rows(a, blk, n):

time: 171 us -> 178 us (1.041)
  waiting for transfers between devices: 86.1 us -> 116 us
  starting transfers between devices: 38.8 us -> 23.5 us
  local copies, waits for them, and re-layouts: 12.7 us -> 6.59 us
  other arithmetic: 10.4 us -> 8.17 us
    ppermute x12 -> x6, waiting for transfers between devices: 45.7 us -> 61.7 us  [_zline(): cur = lax.ppermute(cur, 'src', pairs)]
    ppermute x1, waiting for transfers between devices: 2.59 us -> 17.8 us  [_fast(): lax.ppermute(w_other, 'src', swap)]
    ppermute x12 -> x6, starting transfers between devices: 22.1 us -> 12.8 us  [_zline(): cur = lax.ppermute(cur, 'src', pairs)]
    ppermute x2 -> x1, waiting for transfers between devices: 15 us -> 5.77 us  [_fast(): lax.ppermute(halves[k].astype(jnp.bfloat16), 'vox', chip_perm(k))]
    ppermute x2 -> x1, waiting for transfers between devices: 15 us -> 22.6 us  [_fast(): lax.ppermute(piece, 'vox', chip_perm(k))]
    unnamed x33 -> x19, local copies, waits for them, and re-layouts: 7.32 us -> 3.89 us
    slice x2 -> x0, local copies, waits for them, and re-layouts: 3.37 us -> none  [the longest x1 2.21 us: _fast(): nxt = _zline(adjoint_voxel_field[:r], na)]
    dot_general x8 -> x4, matrix products: 14.9 us -> 16.7 us  [pblock(): lax.dot_general(scaled, rows(col, blk), (((1,), (1,)), ((), ())), preferr...]
  transfers between devices with their start and end apart: 29 -> 17, of which waited for: 16 -> 10; matrix products, arithmetic and copies ran while one was open for 16% -> 12% of each run, Pallas kernels for 0% -> 0%
where the time goes in v21:
time: 178 us; the launch traced here: 177 us
  waiting for transfers between devices  116 us (65%)
  starting transfers between devices  23.5 us (13%)
  matrix products  23 us (13%)
  other arithmetic  8.17 us (5%)
  local copies, waits for them, and re-layouts  6.59 us (4%)
    ppermute x6, waiting for transfers between devices, _zline(): cur = lax.ppermute(cur, 'src', pairs)  61.7 us
    ppermute x1, waiting for transfers between devices, _fast(): lax.ppermute(piece, 'vox', chip_perm(k))  22.6 us
    ppermute x1, waiting for transfers between devices, _fast(): lax.ppermute(w_other, 'src', swap)  17.8 us
    dot_general x4, matrix products, pblock(): lax.dot_general(scaled, rows(col, blk), (((1,), (1,)), ((), ())), preferr...  16.7 us
    ppermute x6, starting transfers between devices, _zline(): cur = lax.ppermute(cur, 'src', pairs)  12.8 us
    ppermute x3, waiting for transfers between devices, _sum_over_src(): v = v + lax.ppermute(v, 'src', [(i, i ^ b) for i in range(n)])  7.81 us
    dot_general x1, matrix products, _fast(): jnp.dot(jnp.concatenate([w for _, w in got], axis=1), jnp.concatenate([ro...  6.25 us
    ppermute x1, waiting for transfers between devices, _fast(): lax.ppermute(halves[k].astype(jnp.bfloat16), 'vox', chip_perm(k))  5.77 us
  transfers between devices with their start and end apart: 17, of which 10 were waited for; matrix products, arithmetic and copies ran while one was open for 12% of the time, Pallas kernels for 0%

profile of v21, /device:TPU:0, one launch (start us, length us, event | category | flops | bytes accessed | tf_op | source)
XLA Modules:
  0.0 177.3 jit_solution(8483284854347091492)
XLA Ops:
  0.0 1.3 collective-permute-start.2
  1.3 5.6 %collective-permute-start.3 = (bf16[512,1024]{1,0:T(8,128)(2,1)}, bf16[512,1024]{1,0:T(8,128)(2,1)S(1)}, u32[]{:S(2)}, u32[]{:S(2)}) collective-permute-start(bf16[512,1024]{1,0:T(8,128)(2,1)} %param.5), channel_id=1, source_target_pairs={{0,8},{4,12},{8,16},{12,20},{16,24},{20,28},{1,9},{5,13},{9,17},{1... | collective-permute-start | bytes 3145736 | tf_op jit(solution)/shard_map/ppermute | solution.py:104
  6.9 21.4 %collective-permute-done.2 = bf16[512,1024]{1,0:T(8,128)(2,1)S(1)} collective-permute-done((bf16[512,1024]{1,0:T(8,128)(2,1)}, bf16[512,1024]{1,0:T(8,128)(2,1)S(1)}, u32[]{:S(2)}, u32[]{:S(2)}) %collective-permute-start.2) | collective-permute-done | bytes 1048608 | tf_op jit(solution)/shard_map/ppermute | solution.py:104
  28.3 1.3 collective-permute-start.6
  29.6 0.0 collective-permute-done.3
  29.6 1.6 collective-permute-start.4
  31.2 1.7 collective-permute-start
  32.9 21.7 %collective-permute-done.6 = bf16[512,1024]{1,0:T(8,128)(2,1)} collective-permute-done((bf16[512,1024]{1,0:T(8,128)(2,1)S(1)}, bf16[512,1024]{1,0:T(8,128)(2,1)}, u32[]{:S(2)}, u32[]{:S(2)}) %collective-permute-start.6) | collective-permute-done | bytes 1048608 | tf_op jit(solution)/shard_map/ppermute | solution.py:104
  54.6 1.3 collective-permute-start.7
  55.9 0.0 collective-permute-done.4
  55.9 1.7 collective-permute-start.5
  57.6 0.0 collective-permute-done
  57.6 1.8 %fusion = bf16[1024,1024]{1,0:T(8,128)(2,1)S(1)} fusion(f32[1024]{0:T(1024)} %param.6, bf16[512,1024]{1,0:T(8,128)(2,1)S(1)} %collective-permute-done, bf16[512,1024]{1,0:T(8,128)(2,1)} %param.4), kind=kLoop, calls=%fused_computation.2 | loop fusion | flops 6291456 | bytes 4198400 | tf_op jit(solution)/shard_map/convert_element_type | solution.py:138
  59.4 0.0 copy-start.8
  59.5 2.1 %broadcast_select_fusion.1 = bf16[512,1024]{1,0:T(8,128)(2,1)S(1)} fusion(bf16[512,1024]{1,0:T(8,128)(2,1)} %collective-permute-done.6, bf16[512,1024]{1,0:T(8,128)(2,1)} %collective-permute-done.4, pred[]{:T(512)S(6)} %lt.93), kind=kLoop, calls=%fused_computation.33 | loop fusion | flops 524288 | bytes 3145729 | tf_op jit(solution)/shard_map/jit(_where)/select_n | solution.py:107
  61.6 18.7 %collective-permute-done.7 = bf16[512,1024]{1,0:T(8,128)(2,1)} collective-permute-done((bf16[512,1024]{1,0:T(8,128)(2,1)}, bf16[512,1024]{1,0:T(8,128)(2,1)}, u32[]{:S(2)}, u32[]{:S(2)}) %collective-permute-start.7) | collective-permute-done | bytes 1048608 | tf_op jit(solution)/shard_map/ppermute | solution.py:104
  80.2 1.4 broadcast_select_fusion
  81.6 0.0 collective-permute-done.5
  81.6 0.1 broadcast_select_fusion.2
  81.8 0.5 pad_maximum_fusion
  82.3 1.9 %copy-done = bf16[2048,1024]{1,0:T(8,128)(2,1)} copy-done((bf16[2048,1024]{1,0:T(8,128)(2,1)}, bf16[2048,1024]{1,0:T(8,128)(2,1)S(1)}, u32[]{:S(2)}) %copy-start) | copy-done | bytes 4194328
  84.3 2.6 %fusion.18 = f32[1024,512]{0,1:T(8,128)} fusion(bf16[1024,1024]{1,0:T(8,128)(2,1)S(1)} %fusion, bf16[2048,1024]{1,0:T(8,128)(2,1)S(1)} %pad_maximum_fusion, s32[]{:T(128)S(6)} %select_n.153), kind=kOutput, calls=%fused_computation.24 | convolution fusion | flops 1073741824 | bytes 5242884 | tf_op jit(solution)/shard_map/dot_general | solution.py:150
  86.9 0.0 collective-permute-start.9
  86.9 3.9 %fusion.21 = f32[1024,512]{0,1:T(8,128)} fusion(bf16[1024,1024]{1,0:T(8,128)(2,1)S(1)} %fusion, bf16[2048,1024]{1,0:T(8,128)(2,1)} %copy-done, s32[]{:T(128)S(6)} %select_n.148), kind=kOutput, calls=%fused_computation.27 | convolution fusion | flops 1073741824 | bytes 5242884 | tf_op jit(solution)/shard_map/dot_general | solution.py:150
  90.8 0.5 collective-permute-start.8
  91.3 1.9 %copy.5 = f32[512,1024]{0,1:T(8,128)S(1)} copy(f32[512,1024]{1,0:T(8,128)} %param.7) | data formatting | bytes 4194304 | tf_op args[3]
  93.2 1.6 select_bitcast_fusion.1
  94.8 1.0 collective-permute-start.1
  95.8 0.0 collective-permute-done.9
  95.8 5.0 %add_convert_fusion = bf16[1024,512]{0,1:T(8,128)(2,1)} fusion(f32[1024,512]{0,1:T(8,128)} %collective-permute-done.9, bf16[1024,1024]{1,0:T(8,128)(2,1)} %copy-done.1, bf16[2048,1024]{1,0:T(8,128)(2,1)} %copy-done, s32[]{:T(128)S(6)} %select_n.151), kind=kOutput, calls=%fused_computation.23 | convolution fusion | flops 1074790400 | bytes 6291460 | tf_op jit(solution)/shard_map/dot_general | solution.py:150
  100.9 1.5 collective-permute-start.10
  102.4 17.8 %collective-permute-done.1 = f32[512,512]{0,1:T(8,128)} collective-permute-done((f32[512,512]{0,1:T(8,128)}, f32[512,512]{0,1:T(8,128)}, u32[]{:S(2)}, u32[]{:S(2)}) %collective-permute-start.1) | collective-permute-done | bytes 1048608 | tf_op jit(solution)/shard_map/ppermute | solution.py:143
  120.2 0.0 collective-permute-done.8
  120.2 5.8 %collective-permute-done.10 = bf16[1024,512]{0,1:T(8,128)(2,1)} collective-permute-done((bf16[1024,512]{0,1:T(8,128)(2,1)}, bf16[1024,512]{0,1:T(8,128)(2,1)}, u32[]{:S(2)}, u32[]{:S(2)}) %collective-permute-start.10) | collective-permute-done | bytes 1048608 | tf_op jit(solution)/shard_map/ppermute | solution.py:160
  126.0 5.2 %fusion.17 = bf16[1024,512]{0,1:T(8,128)(2,1)} fusion(f32[512,512]{0,1:T(8,128)} %collective-permute-done.1, f32[512,512]{0,1:T(8,128)} %get-tuple-element.9, bf16[1024,512]{0,1:T(8,128)(2,1)} %collective-permute-done.10, f32[1024,512]{0,1:T(8,128)} %collective-permute-done.8, bf16[1024,1024]{1,0:T(8,128)(2,1)S(1)} %copy-done.2, ...), kind=kOutput, calls=%fused_computation.22 | convolution fusion | flops 1076887552 | bytes 9437188 | tf_op jit(solution)/shard_map/dot_general | solution.py:150
  131.2 1.5 collective-permute-start.11
  132.7 0.0 collective-permute-start.12
  132.7 22.6 %collective-permute-done.11 = bf16[1024,512]{0,1:T(8,128)(2,1)S(1)} collective-permute-done((bf16[1024,512]{0,1:T(8,128)(2,1)}, bf16[1024,512]{0,1:T(8,128)(2,1)S(1)}, u32[]{:S(2)}, u32[]{:S(2)}) %collective-permute-start.11) | collective-permute-done | bytes 1048608 | tf_op jit(solution)/shard_map/ppermute | solution.py:168
  155.3 0.0 collective-permute-start.13
  155.3 2.7 %constant_dynamic-slice_fusion.3 = (bf16[512,1024]{1,0:T(8,128)(2,1)S(1)}, bf16[512,1024]{1,0:T(8,128)(2,1)S(1)}, bf16[512,1024]{1,0:T(8,128)(2,1)S(1)}, bf16[512,1024]{1,0:T(8,128)(2,1)S(1)}) fusion(bf16[2048,1024]{1,0:T(8,128)(2,1)} %copy-done, s32[]{:T(128)S(6)} %select_n.155, s32[]{:T(128)S(6)} %select_n.162, s32[]{:T(128)S(6)} %select_n.160, ...), kind=kLoop, calls=%fused_computation.38 | loop fusion | bytes 8388624 | tf_op jit(solution)/shard_map/dynamic_slice | solution.py:132
  158.0 0.1 collective-permute-done.13
  158.1 6.3 %fusion.1 = f32[1024]{0:T(1024)S(1)} fusion(bf16[512,1024]{1,0:T(8,128)(2,1)S(1)} %collective-permute-done, bf16[512,1024]{1,0:T(8,128)(2,1)S(1)} %copy-done.3, bf16[512,1024]{1,0:T(8,128)(2,1)S(1)} %get-tuple-element.6, bf16[512,1024]{1,0:T(8,128)(2,1)S(1)} %get-tuple-element.7, bf16[512,1024]{1,0:T(8,128)(2,1)S(1)} %get-tuple-element.8, ...), kind=kOutput, calls=%fused_computation.3 | convolution fusion | flops 4334812160 | bytes 10489856 | tf_op jit(solution)/shard_map/dot_general | solution.py:176
  164.4 1.0 collective-permute-start.14
  165.4 2.6 %collective-permute-done.14 = f32[1024]{0:T(1024)S(1)} collective-permute-done((f32[1024]{0:T(1024)S(1)}, f32[1024]{0:T(1024)S(1)}, u32[]{:S(2)}, u32[]{:S(2)}) %collective-permute-start.14) | collective-permute-done | bytes 4128 | tf_op jit(solution)/shard_map/ppermute | solution.py:84
  168.0 3.6 %collective-permute-done.15 = f32[1024]{0:T(1024)S(1)} collective-permute-done((f32[1024]{0:T(1024)S(1)}, f32[1024]{0:T(1024)S(1)}, u32[]{:S(2)}, u32[]{:S(2)}) %collective-permute-start.15) | collective-permute-done | bytes 4128 | tf_op jit(solution)/shard_map/ppermute | solution.py:84
  171.7 3.5 %collective-permute-start.16 = (f32[1024]{0:T(1024)S(1)}, f32[1024]{0:T(1024)S(1)}, u32[]{:S(2)}, u32[]{:S(2)}) collective-permute-start(f32[1024]{0:T(1024)S(1)} %add.149), channel_id=1, source_target_pairs={{0,16},{4,20},{8,24},{12,28},{16,0},{20,4},{24,8},{28,12},{1,17},{... | collective-permute-start | bytes 12296 | tf_op jit(solution)/shard_map/ppermute | solution.py:84
  175.1 1.6 collective-permute-done.16
  176.7 0.6 add.150
  (20 shorter events, 0.0 us)
Async XLA Ops:
  0.0 28.3 %collective-permute-start.2 = (bf16[512,1024]{1,0:T(8,128)(2,1)}, bf16[512,1024]{1,0:T(8,128)(2,1)S(1)}, u32[]{:S(2)}, u32[]{:S(2)}) collective-permute-start(bf16[512,1024]{1,0:T(8,128)(2,1)} %param.5), channel_id=1, source_target_pairs={{8,0},{12,4},{16,8},{20,12},{24,16},{28,20},{9,1},{13,5},{17,9},{2... | collective-permute-start | bytes 3145736 | tf_op jit(solution)/shard_map/ppermute | solution.py:104
  1.3 28.3 %collective-permute-start.3 = (bf16[512,1024]{1,0:T(8,128)(2,1)}, bf16[512,1024]{1,0:T(8,128)(2,1)S(1)}, u32[]{:S(2)}, u32[]{:S(2)}) collective-permute-start(bf16[512,1024]{1,0:T(8,128)(2,1)} %param.5), channel_id=1, source_target_pairs={{0,8},{4,12},{8,16},{12,20},{16,24},{20,28},{1,9},{5,13},{9,17},{1... | collective-permute-start | bytes 3145736 | tf_op jit(solution)/shard_map/ppermute | solution.py:104
  28.3 1.3 copy-start.4
  28.3 26.3 %collective-permute-start.6 = (bf16[512,1024]{1,0:T(8,128)(2,1)S(1)}, bf16[512,1024]{1,0:T(8,128)(2,1)}, u32[]{:S(2)}, u32[]{:S(2)}) collective-permute-start(bf16[512,1024]{1,0:T(8,128)(2,1)S(1)} %collective-permute-done.2), channel_id=1, source_target_pairs={{8,0},{12,4},{16,8},{20,12},{9,1},{13,5},{17,9},{21,13},{10,2},{14... | collective-permute-start | bytes 3145736 | tf_op jit(solution)/shard_map/ppermute | solution.py:104
  29.6 25.0 %copy-start.6 = (bf16[512,1024]{1,0:T(8,128)(2,1)}, bf16[512,1024]{1,0:T(8,128)(2,1)S(1)}, u32[]{:S(2)}) copy-start(bf16[512,1024]{1,0:T(8,128)(2,1)S(1)} %collective-permute-done.3) | copy-start | bytes 3145732
  29.6 26.3 %collective-permute-start.4 = (bf16[512,1024]{1,0:T(8,128)(2,1)S(1)}, bf16[512,1024]{1,0:T(8,128)(2,1)}, u32[]{:S(2)}, u32[]{:S(2)}) collective-permute-start(bf16[512,1024]{1,0:T(8,128)(2,1)S(1)} %collective-permute-done.3), channel_id=1, source_target_pairs={{8,16},{12,20},{16,24},{20,28},{9,17},{13,21},{17,25},{21,29},{10,... | collective-permute-start | bytes 3145736 | tf_op jit(solution)/shard_map/ppermute | solution.py:104
  31.2 26.3 %collective-permute-start = (bf16[512,1024]{1,0:T(8,128)(2,1)}, bf16[512,1024]{1,0:T(8,128)(2,1)S(1)}, u32[]{:S(2)}, u32[]{:S(2)}) collective-permute-start(bf16[512,1024]{1,0:T(8,128)(2,1)} %param.4), channel_id=1, source_target_pairs={{0,4},{4,0},{8,12},{12,8},{16,20},{20,16},{24,28},{28,24},{1,5},{5... | collective-permute-start | bytes 3145736 | tf_op jit(solution)/shard_map/ppermute | solution.py:135
  54.6 25.6 %collective-permute-start.7 = (bf16[512,1024]{1,0:T(8,128)(2,1)}, bf16[512,1024]{1,0:T(8,128)(2,1)}, u32[]{:S(2)}, u32[]{:S(2)}) collective-permute-start(bf16[512,1024]{1,0:T(8,128)(2,1)} %collective-permute-done.6), channel_id=1, source_target_pairs={{8,0},{12,4},{9,1},{13,5},{10,2},{14,6},{11,3},{15,7}} | collective-permute-start | bytes 3145736 | tf_op jit(solution)/shard_map/ppermute | solution.py:104
  55.9 25.7 %collective-permute-start.5 = (bf16[512,1024]{1,0:T(8,128)(2,1)}, bf16[512,1024]{1,0:T(8,128)(2,1)}, u32[]{:S(2)}, u32[]{:S(2)}) collective-permute-start(bf16[512,1024]{1,0:T(8,128)(2,1)} %collective-permute-done.4), channel_id=1, source_target_pairs={{16,24},{20,28},{17,25},{21,29},{18,26},{22,30},{19,27},{23,31}} | collective-permute-start | bytes 3145736 | tf_op jit(solution)/shard_map/ppermute | solution.py:104
  57.6 22.7 %copy-start.7 = (bf16[512,1024]{1,0:T(8,128)(2,1)S(1)}, bf16[512,1024]{1,0:T(8,128)(2,1)}, u32[]{:S(2)}) copy-start(bf16[512,1024]{1,0:T(8,128)(2,1)} %copy-done.6) | copy-start | bytes 3145732
  59.4 27.4 %copy-start.1 = (bf16[1024,1024]{1,0:T(8,128)(2,1)}, bf16[1024,1024]{1,0:T(8,128)(2,1)S(1)}, u32[]{:S(2)}) copy-start(bf16[1024,1024]{1,0:T(8,128)(2,1)S(1)} %fusion) | copy-start | bytes 6291460
  59.4 22.2 %copy-start.5 = (bf16[512,1024]{1,0:T(8,128)(2,1)S(1)}, bf16[512,1024]{1,0:T(8,128)(2,1)}, u32[]{:S(2)}) copy-start(bf16[512,1024]{1,0:T(8,128)(2,1)} %copy-done.4) | copy-start | bytes 3145732
  59.4 22.3 %copy-start.8 = (bf16[512,1024]{1,0:T(8,128)(2,1)S(1)}, bf16[512,1024]{1,0:T(8,128)(2,1)}, u32[]{:S(2)}) copy-start(bf16[512,1024]{1,0:T(8,128)(2,1)} %param.5) | copy-start | bytes 3145732
  82.3 1.9 %copy-start = (bf16[2048,1024]{1,0:T(8,128)(2,1)}, bf16[2048,1024]{1,0:T(8,128)(2,1)S(1)}, u32[]{:S(2)}) copy-start(bf16[2048,1024]{1,0:T(8,128)(2,1)S(1)} %pad_maximum_fusion) | copy-start | bytes 12582916
  86.9 9.0 %collective-permute-start.9 = (f32[1024,512]{0,1:T(8,128)}, f32[1024,512]{0,1:T(8,128)}, u32[]{:S(2)}, u32[]{:S(2)}) collective-permute-start(f32[1024,512]{0,1:T(8,128)} %fusion.18), channel_id=1, source_target_pairs={{0,1},{1,0},{2,3},{3,2},{4,5},{5,4},{6,7},{7,6},{8,9},{9,8},{10,11... | collective-permute-start | bytes 6291464 | tf_op jit(solution)/shard_map/ppermute | solution.py:157
  90.8 29.4 %collective-permute-start.8 = (f32[1024,512]{0,1:T(8,128)}, f32[1024,512]{0,1:T(8,128)}, u32[]{:S(2)}, u32[]{:S(2)}) collective-permute-start(f32[1024,512]{0,1:T(8,128)} %fusion.21), channel_id=1, source_target_pairs={{0,1},{1,0},{2,3},{3,2},{4,5},{5,4},{6,7},{7,6},{8,9},{9,8},{10,11... | collective-permute-start | bytes 6291464 | tf_op jit(solution)/shard_map/ppermute | solution.py:157
  94.8 25.4 %collective-permute-start.1 = (f32[512,512]{0,1:T(8,128)}, f32[512,512]{0,1:T(8,128)}, u32[]{:S(2)}, u32[]{:S(2)}) collective-permute-start(f32[512,512]{0,1:T(8,128)} %get-tuple-element.10), channel_id=1, source_target_pairs={{0,4},{4,0},{8,12},{12,8},{16,20},{20,16},{24,28},{28,24},{1,5},{5... | collective-permute-start | bytes 3145736 | tf_op jit(solution)/shard_map/ppermute | solution.py:143
  95.8 30.1 %copy-start.2 = (bf16[1024,1024]{1,0:T(8,128)(2,1)S(1)}, bf16[1024,1024]{1,0:T(8,128)(2,1)}, u32[]{:S(2)}) copy-start(bf16[1024,1024]{1,0:T(8,128)(2,1)} %copy-done.1) | copy-start | bytes 6291460
  100.9 25.1 %collective-permute-start.10 = (bf16[1024,512]{0,1:T(8,128)(2,1)}, bf16[1024,512]{0,1:T(8,128)(2,1)}, u32[]{:S(2)}, u32[]{:S(2)}) collective-permute-start(bf16[1024,512]{0,1:T(8,128)(2,1)} %add_convert_fusion), channel_id=1, source_target_pairs={{0,2},{1,3},{2,0},{3,1},{4,6},{5,7},{6,4},{7,5},{8,10},{9,11},{10,... | collective-permute-start | bytes 3145736 | tf_op jit(solution)/shard_map/ppermute | solution.py:160
  131.2 24.1 %collective-permute-start.11 = (bf16[1024,512]{0,1:T(8,128)(2,1)}, bf16[1024,512]{0,1:T(8,128)(2,1)S(1)}, u32[]{:S(2)}, u32[]{:S(2)}) collective-permute-start(bf16[1024,512]{0,1:T(8,128)(2,1)} %fusion.17), channel_id=1, source_target_pairs={{0,2},{1,3},{2,0},{3,1},{4,6},{5,7},{6,4},{7,5},{8,10},{9,11},{10,... | collective-permute-start | bytes 3145736 | tf_op jit(solution)/shard_map/ppermute | solution.py:168
  132.7 25.3 %collective-permute-start.12 = (bf16[1024,512]{0,1:T(8,128)(2,1)}, bf16[1024,512]{0,1:T(8,128)(2,1)S(1)}, u32[]{:S(2)}, u32[]{:S(2)}) collective-permute-start(bf16[1024,512]{0,1:T(8,128)(2,1)} %fusion.17), channel_id=1, source_target_pairs={{0,1},{1,0},{2,3},{3,2},{4,5},{5,4},{6,7},{7,6},{8,9},{9,8},{10,11... | collective-permute-start | bytes 3145736 | tf_op jit(solution)/shard_map/ppermute | solution.py:169
  155.3 2.8 %collective-permute-start.13 = (bf16[1024,512]{0,1:T(8,128)(2,1)S(1)}, bf16[1024,512]{0,1:T(8,128)(2,1)}, u32[]{:S(2)}, u32[]{:S(2)}) collective-permute-start(bf16[1024,512]{0,1:T(8,128)(2,1)S(1)} %collective-permute-done.11), channel_id=1, source_target_pairs={{0,1},{1,0},{2,3},{3,2},{4,5},{5,4},{6,7},{7,6},{8,9},{9,8},{10,11... | collective-permute-start | bytes 3145736 | tf_op jit(solution)/shard_map/ppermute | solution.py:169
  155.3 2.8 %copy-start.3 = (bf16[512,1024]{1,0:T(8,128)(2,1)S(1)}, bf16[512,1024]{1,0:T(8,128)(2,1)}, u32[]{:S(2)}) copy-start(bf16[512,1024]{1,0:T(8,128)(2,1)} %param.4) | copy-start | bytes 3145732
  164.4 3.7 %collective-permute-start.14 = (f32[1024]{0:T(1024)S(1)}, f32[1024]{0:T(1024)S(1)}, u32[]{:S(2)}, u32[]{:S(2)}) collective-permute-start(f32[1024]{0:T(1024)S(1)} %fusion.1), channel_id=1, source_target_pairs={{0,4},{4,0},{8,12},{12,8},{16,20},{20,16},{24,28},{28,24},{1,5},{5... | collective-permute-start | bytes 12296 | tf_op jit(solution)/shard_map/ppermute | solution.py:84
  168.0 3.6 %collective-permute-start.15 = (f32[1024]{0:T(1024)S(1)}, f32[1024]{0:T(1024)S(1)}, u32[]{:S(2)}, u32[]{:S(2)}) collective-permute-start(f32[1024]{0:T(1024)S(1)} %add.148), channel_id=1, source_target_pairs={{0,8},{4,12},{8,0},{12,4},{16,24},{20,28},{24,16},{28,20},{1,9},{5... | collective-permute-start | bytes 12296 | tf_op jit(solution)/shard_map/ppermute | solution.py:84
  171.7 5.1 %collective-permute-start.16 = (f32[1024]{0:T(1024)S(1)}, f32[1024]{0:T(1024)S(1)}, u32[]{:S(2)}, u32[]{:S(2)}) collective-permute-start(f32[1024]{0:T(1024)S(1)} %add.149), channel_id=1, source_target_pairs={{0,16},{4,20},{8,24},{12,28},{16,0},{20,4},{24,8},{28,12},{1,17},{... | collective-permute-start | bytes 12296 | tf_op jit(solution)/shard_map/ppermute | solution.py:84

commit v22 on v20

--- a/solution.py
+++ b/solution.py
@@ -129,7 +129,7 @@
         return [(g * 2 + p, ((g + k) % m) * 2 + p) for g in range(m) for p in range(2)]
 
     def rows(col, blk):
-        return lax.dynamic_slice_in_dim(col, ((blk - ia) % na) * r, r, axis=0)
+        return lax.dynamic_slice(col, (((blk - ia) % na) * ds + c * r, 0), (r, vl))
 
     fwd = jnp.concatenate(
         [forward_voxel_field, lax.ppermute(forward_voxel_field, "src", swap)], axis=0
@@ -142,9 +142,8 @@
     w_other = jnp.where(first, weight[:, 1], weight[:, 0])
     weight = jnp.concatenate([w_mine, lax.ppermute(w_other, "src", swap)], axis=0)
     back = jnp.zeros((2 * sl, vl), jnp.float32)
-    nxt = _zline(adjoint_voxel_field[:r], na)
+    col = _zline(adjoint_voxel_field, na)
     for c in range(chunks):
-        col = nxt
 
         def pblock(blk):
             return lax.dot_general(
@@ -168,11 +167,6 @@
             got.append((2 * ((q - k) % m) + par, lax.ppermute(piece, "vox", chip_perm(k))))
         mates = lax.ppermute(tuple(w for _, w in got), "vox", pair)
         got = got + [(blk ^ 1, w) for (blk, _), w in zip(got, mates)]
-        if c + 1 < chunks:
-            nxt, ws = lax.optimization_barrier(
-                (_zline(adjoint_voxel_field[(c + 1) * r:(c + 2) * r], na), [w for _, w in got])
-            )
-            got = [(blk, w) for (blk, _), w in zip(got, ws)]
         back = back + jnp.dot(
             jnp.concatenate([w for _, w in got], axis=1),
             jnp.concatenate([rows(col, blk) for blk, _ in got], axis=0),

time: 171 us -> 171 us (level)
  starting transfers between devices: 38.8 us -> 26.6 us
  waiting for transfers between devices: 86.1 us -> 97.5 us
  matrix products: 22.1 us -> 30.7 us
  local copies, waits for them, and re-layouts: 12.7 us -> 7.93 us
  other arithmetic: 10.4 us -> 7.51 us
    ppermute x12 -> x6, waiting for transfers between devices: 45.7 us -> 59.3 us  [_zline(): cur = lax.ppermute(cur, 'src', pairs)]
    ppermute x12 -> x6, starting transfers between devices: 22.1 us -> 13 us  [_zline(): cur = lax.ppermute(cur, 'src', pairs)]
    dot_general x8, matrix products: 14.9 us -> 22.7 us  [pblock(): lax.dot_general(scaled, rows(col, blk), (((1,), (1,)), ((), ())), preferr...]
    ppermute x2, waiting for transfers between devices: 15 us -> 9.79 us  [_fast(): lax.ppermute(halves[k].astype(jnp.bfloat16), 'vox', chip_perm(k))]
    ppermute x1, waiting for transfers between devices: 2.59 us -> 6.62 us  [_fast(): lax.ppermute(w_other, 'src', swap)]
    slice x2 -> x0, local copies, waits for them, and re-layouts: 3.37 us -> none  [the longest x1 2.21 us: _fast(): nxt = _zline(adjoint_voxel_field[:r], na)]
    unnamed x33 -> x21, local copies, waits for them, and re-layouts: 7.32 us -> 5.32 us
    select_n x6 -> x3, other arithmetic: 3.51 us -> 3.02 us  [_zline(): jnp.where(ia + k < na, got[-1, k], got[1, na - k])]
  transfers between devices with their start and end apart: 29 -> 23, of which waited for: 16 -> 11; matrix products, arithmetic and copies ran while one was open for 16% -> 21% of each run, Pallas kernels for 0% -> 0%
where the time goes in v22:
time: 171 us; the launch traced here: 170 us
  waiting for transfers between devices  97.5 us (57%)
  matrix products  30.7 us (18%)
  starting transfers between devices  26.6 us (16%)
  local copies, waits for them, and re-layouts  7.93 us (5%)
  other arithmetic  7.51 us (4%)
    ppermute x6, waiting for transfers between devices, _zline(): cur = lax.ppermute(cur, 'src', pairs)  59.3 us
    dot_general x8, matrix products, pblock(): lax.dot_general(scaled, rows(col, blk), (((1,), (1,)), ((), ())), preferr...  22.7 us
    ppermute x2, waiting for transfers between devices, _fast(): lax.ppermute(piece, 'vox', chip_perm(k))  14 us
    ppermute x6, starting transfers between devices, _zline(): cur = lax.ppermute(cur, 'src', pairs)  13 us
    ppermute x2, waiting for transfers between devices, _fast(): lax.ppermute(halves[k].astype(jnp.bfloat16), 'vox', chip_perm(k))  9.79 us
    dot_general x2, matrix products, _fast(): jnp.dot(jnp.concatenate([w for _, w in got], axis=1), jnp.concatenate([ro...  7.98 us
    ppermute x3, waiting for transfers between devices, _sum_over_src(): v = v + lax.ppermute(v, 'src', [(i, i ^ b) for i in range(n)])  7.81 us
    ppermute x1, waiting for transfers between devices, _fast(): lax.ppermute(w_other, 'src', swap)  6.62 us
  transfers between devices with their start and end apart: 23, of which 11 were waited for; matrix products, arithmetic and copies ran while one was open for 21% of the time, Pallas kernels for 0%

profile of v22, /device:TPU:0, one launch (start us, length us, event | category | flops | bytes accessed | tf_op | source)
XLA Modules:
  0.0 170.5 jit_solution(8829424014979509178)
XLA Ops:
  0.0 1.4 collective-permute-start.2
  1.4 5.6 %collective-permute-start.3 = (bf16[512,1024]{1,0:T(8,128)(2,1)}, bf16[512,1024]{1,0:T(8,128)(2,1)S(1)}, u32[]{:S(2)}, u32[]{:S(2)}) collective-permute-start(bf16[512,1024]{1,0:T(8,128)(2,1)} %param.5), channel_id=1, source_target_pairs={{0,8},{4,12},{8,16},{12,20},{16,24},{20,28},{1,9},{5,13},{9,17},{1... | collective-permute-start | bytes 3145736 | tf_op jit(solution)/shard_map/ppermute | solution.py:104
  7.1 21.4 %collective-permute-done.2 = bf16[512,1024]{1,0:T(8,128)(2,1)S(1)} collective-permute-done((bf16[512,1024]{1,0:T(8,128)(2,1)}, bf16[512,1024]{1,0:T(8,128)(2,1)S(1)}, u32[]{:S(2)}, u32[]{:S(2)}) %collective-permute-start.2) | collective-permute-done | bytes 1048608 | tf_op jit(solution)/shard_map/ppermute | solution.py:104
  28.4 1.0 copy-done.4
  29.4 1.3 collective-permute-start.6
  30.7 1.6 collective-permute-start.4
  32.4 1.7 collective-permute-start
  34.0 21.7 %collective-permute-done.6 = bf16[512,1024]{1,0:T(8,128)(2,1)} collective-permute-done((bf16[512,1024]{1,0:T(8,128)(2,1)S(1)}, bf16[512,1024]{1,0:T(8,128)(2,1)}, u32[]{:S(2)}, u32[]{:S(2)}) %collective-permute-start.6) | collective-permute-done | bytes 1048608 | tf_op jit(solution)/shard_map/ppermute | solution.py:104
  55.7 1.3 collective-permute-start.7
  57.0 1.7 %collective-permute-start.5 = (bf16[512,1024]{1,0:T(8,128)(2,1)}, bf16[512,1024]{1,0:T(8,128)(2,1)}, u32[]{:S(2)}, u32[]{:S(2)}) collective-permute-start(bf16[512,1024]{1,0:T(8,128)(2,1)} %collective-permute-done.4), channel_id=1, source_target_pairs={{16,24},{20,28},{17,25},{21,29},{18,26},{22,30},{19,27},{23,31}} | collective-permute-start | bytes 3145736 | tf_op jit(solution)/shard_map/ppermute | solution.py:104
  58.8 2.9 %copy.5 = f32[512,1024]{0,1:T(8,128)} copy(f32[512,1024]{1,0:T(8,128)} %param.7) | data formatting | bytes 4194304 | tf_op args[3]
  61.7 1.9 %fusion = bf16[1024,1024]{1,0:T(8,128)(2,1)S(1)} fusion(f32[1024]{0:T(1024)S(1)} %copy-done.9, bf16[512,1024]{1,0:T(8,128)(2,1)} %collective-permute-done, bf16[512,1024]{1,0:T(8,128)(2,1)S(1)} %copy-done.2), kind=kLoop, calls=%fused_computation.2 | loop fusion | flops 6291456 | bytes 4198400 | tf_op jit(solution)/shard_map/convert_element_type | solution.py:138
  63.7 1.5 broadcast_select_fusion.1
  65.2 16.2 %collective-permute-done.7 = bf16[512,1024]{1,0:T(8,128)(2,1)} collective-permute-done((bf16[512,1024]{1,0:T(8,128)(2,1)}, bf16[512,1024]{1,0:T(8,128)(2,1)}, u32[]{:S(2)}, u32[]{:S(2)}) %collective-permute-start.7) | collective-permute-done | bytes 1048608 | tf_op jit(solution)/shard_map/ppermute | solution.py:104
  81.4 1.4 broadcast_select_fusion
  82.8 0.2 broadcast_select_fusion.2
  82.9 0.7 pad_maximum_fusion
  83.7 1.7 %fusion.45 = f32[1024,256]{0,1:T(8,128)} fusion(bf16[1024,1024]{1,0:T(8,128)(2,1)S(1)} %fusion, bf16[2048,1024]{1,0:T(8,128)(2,1)S(1)} %pad_maximum_fusion, s32[]{:T(128)S(6)} %select_n.216), kind=kOutput, calls=%fused_computation.57 | convolution fusion | flops 536870912 | bytes 3670020 | tf_op jit(solution)/shard_map/dot_general | solution.py:149
  85.4 1.4 copy-done.1
  86.8 1.3 select_bitcast_fusion.1
  88.0 1.0 collective-permute-start.1
  89.1 2.8 %fusion.51 = f32[1024,256]{0,1:T(8,128)} fusion(bf16[1024,1024]{1,0:T(8,128)(2,1)S(1)} %fusion, bf16[2048,1024]{1,0:T(8,128)(2,1)} %copy-done, s32[]{:T(128)S(6)} %select_n.203), kind=kOutput, calls=%fused_computation.63 | convolution fusion | flops 536870912 | bytes 3670020 | tf_op jit(solution)/shard_map/dot_general | solution.py:149
  91.9 2.8 %fusion.48 = f32[1024,256]{0,1:T(8,128)} fusion(bf16[1024,1024]{1,0:T(8,128)(2,1)S(1)} %fusion, bf16[2048,1024]{1,0:T(8,128)(2,1)} %copy-done, s32[]{:T(128)S(6)} %select_n.214), kind=kOutput, calls=%fused_computation.60 | convolution fusion | flops 536870912 | bytes 3670020 | tf_op jit(solution)/shard_map/dot_general | solution.py:149
  94.7 0.5 collective-permute-start.14
  95.2 2.9 %fusion.54 = f32[1024,256]{0,1:T(8,128)} fusion(bf16[1024,1024]{1,0:T(8,128)(2,1)S(1)} %fusion, bf16[2048,1024]{1,0:T(8,128)(2,1)} %copy-done, s32[]{:T(128)S(6)} %select_n.198), kind=kOutput, calls=%fused_computation.66 | convolution fusion | flops 536870912 | bytes 3670020 | tf_op jit(solution)/shard_map/dot_general | solution.py:149
  98.0 2.9 %fusion.35 = bf16[1024,256]{0,1:T(8,128)(2,1)} fusion(f32[1024,256]{0,1:T(8,128)} %collective-permute-done.15, bf16[1024,1024]{1,0:T(8,128)(2,1)S(1)} %fusion, bf16[2048,1024]{1,0:T(8,128)(2,1)} %copy-done, s32[]{:T(128)S(6)} %select_n.215), kind=kOutput, calls=%fused_computation.45 | convolution fusion | flops 537395200 | bytes 4194308 | tf_op jit(solution)/shard_map/dot_general | solution.py:149
  100.9 1.5 collective-permute-start.16
  102.4 3.0 %fusion.34 = bf16[1024,256]{0,1:T(8,128)(2,1)} fusion(f32[1024,256]{0,1:T(8,128)} %collective-permute-done.9, bf16[1024,1024]{1,0:T(8,128)(2,1)S(1)} %fusion, bf16[2048,1024]{1,0:T(8,128)(2,1)} %copy-done, s32[]{:T(128)S(6)} %select_n.201), kind=kOutput, calls=%fused_computation.44 | convolution fusion | flops 537395200 | bytes 4194308 | tf_op jit(solution)/shard_map/dot_general | solution.py:149
  105.4 0.5 collective-permute-start.10
  105.9 6.6 %collective-permute-done.1 = f32[512,512]{0,1:T(8,128)} collective-permute-done((f32[512,512]{0,1:T(8,128)}, f32[512,512]{0,1:T(8,128)}, u32[]{:S(2)}, u32[]{:S(2)}) %collective-permute-start.1) | collective-permute-done | bytes 1048608 | tf_op jit(solution)/shard_map/ppermute | solution.py:143
  112.6 3.4 %collective-permute-done.16 = bf16[1024,256]{0,1:T(8,128)(2,1)} collective-permute-done((bf16[1024,256]{0,1:T(8,128)(2,1)}, bf16[1024,256]{0,1:T(8,128)(2,1)}, u32[]{:S(2)}, u32[]{:S(2)}) %collective-permute-start.16) | collective-permute-done | bytes 524320 | tf_op jit(solution)/shard_map/ppermute | solution.py:159
  116.0 3.4 %fusion.40 = bf16[1024,256]{0,1:T(8,128)(2,1)} fusion(f32[512,512]{0,1:T(8,128)} %collective-permute-done.1, f32[512,512]{0,1:T(8,128)S(1)} %get-tuple-element.13, bf16[1024,256]{0,1:T(8,128)(2,1)} %collective-permute-done.16, f32[1024,256]{0,1:T(8,128)} %collective-permute-done.14, bf16[1024,1024]{1,0:T(8,128)(2,1)S(1)} %fusion, ...), kind=kOutput, calls=%fused_computation.51 | convolution fusion | flops 538443776 | bytes 6815748 | tf_op jit(solution)/shard_map/dot_general | solution.py:149
  119.3 1.5 collective-permute-start.17
  120.8 6.4 %collective-permute-done.10 = bf16[1024,256]{0,1:T(8,128)(2,1)} collective-permute-done((bf16[1024,256]{0,1:T(8,128)(2,1)}, bf16[1024,256]{0,1:T(8,128)(2,1)}, u32[]{:S(2)}, u32[]{:S(2)}) %collective-permute-start.10) | collective-permute-done | bytes 524320 | tf_op jit(solution)/shard_map/ppermute | solution.py:159
  127.2 3.3 %fusion.38 = bf16[1024,256]{0,1:T(8,128)(2,1)} fusion(f32[512,512]{0,1:T(8,128)S(1)} %get-tuple-element.13, f32[512,512]{0,1:T(8,128)} %collective-permute-done.1, bf16[1024,256]{0,1:T(8,128)(2,1)} %collective-permute-done.10, f32[1024,256]{0,1:T(8,128)} %collective-permute-done.8, bf16[1024,1024]{1,0:T(8,128)(2,1)S(1)} %fusion, ...), kind=kOutput, calls=%fused_computation.48 | convolution fusion | flops 538443776 | bytes 6815748 | tf_op jit(solution)/shard_map/dot_general | solution.py:149
  130.5 1.5 collective-permute-start.11
  132.0 6.4 %collective-permute-done.17 = bf16[1024,256]{0,1:T(8,128)(2,1)} collective-permute-done((bf16[1024,256]{0,1:T(8,128)(2,1)}, bf16[1024,256]{0,1:T(8,128)(2,1)}, u32[]{:S(2)}, u32[]{:S(2)}) %collective-permute-start.17) | collective-permute-done | bytes 524320 | tf_op jit(solution)/shard_map/ppermute | solution.py:167
  138.5 2.6 %constant_dynamic-slice_fusion.7 = (bf16[256,1024]{1,0:T(8,128)(2,1)S(1)}, bf16[256,1024]{1,0:T(8,128)(2,1)S(1)}, bf16[256,1024]{1,0:T(8,128)(2,1)S(1)}, bf16[25...) fusion(bf16[2048,1024]{1,0:T(8,128)(2,1)} %copy-done, ...), kind=kLoop, calls=%fused_computation.80 | loop fusion | bytes 8388640 | tf_op jit(solution)/shard_map/dynamic_slice | solution.py:132
  141.1 0.6 collective-permute-start.12
  141.6 7.6 %collective-permute-done.11 = bf16[1024,256]{0,1:T(8,128)(2,1)S(1)} collective-permute-done((bf16[1024,256]{0,1:T(8,128)(2,1)}, bf16[1024,256]{0,1:T(8,128)(2,1)S(1)}, u32[]{:S(2)}, u32[]{:S(2)}) %collective-permute-start.11) | collective-permute-done | bytes 524320 | tf_op jit(solution)/shard_map/ppermute | solution.py:167
  149.2 3.7 %fusion.17 = f32[1024,1024]{1,0:T(8,128)S(1)} fusion(bf16[1024,256]{0,1:T(8,128)(2,1)S(1)} %collective-permute-done.19, bf16[1024,256]{0,1:T(8,128)(2,1)S(1)} %collective-permute-done.18, bf16[1024,256]{0,1:T(8,128)(2,1)} %collective-permute-done.17, bf16[1024,256]{0,1:T(8,128)(2,1)} %fusion.40, bf16[256,1024]{1,0:T(8,128)(2,1)S(1)} %get-tuple-element.6, ...), kind=kOutput, calls=%fused_computation.23 | convolution fusion | flops 2164260864 | bytes 8388608 | tf_op jit(solution)/shard_map/dot_general | solution.py:170
  153.0 4.3 %fusion.1 = f32[1024]{0:T(1024)S(1)} fusion(f32[1024,1024]{1,0:T(8,128)S(1)} %fusion.17, bf16[512,1024]{1,0:T(8,128)(2,1)} %collective-permute-done, bf16[512,1024]{1,0:T(8,128)(2,1)S(1)} %copy-done.3, bf16[256,1024]{1,0:T(8,128)(2,1)S(1)} %get-tuple-element.10, bf16[256,1024]{1,0:T(8,128)(2,1)S(1)} %get-tuple-element.11, ...), kind=kOutput, calls=%fused_computation.3 | convolution fusion | flops 2171599872 | bytes 10489856 | tf_op jit(solution)/shard_map/dot_general | solution.py:170
  157.2 1.1 collective-permute-start.20
  158.3 2.6 %collective-permute-done.20 = f32[1024]{0:T(1024)S(1)} collective-permute-done((f32[1024]{0:T(1024)S(1)}, f32[1024]{0:T(1024)S(1)}, u32[]{:S(2)}, u32[]{:S(2)}) %collective-permute-start.20) | collective-permute-done | bytes 4128 | tf_op jit(solution)/shard_map/ppermute | solution.py:84
  160.9 3.6 %collective-permute-done.21 = f32[1024]{0:T(1024)S(1)} collective-permute-done((f32[1024]{0:T(1024)S(1)}, f32[1024]{0:T(1024)S(1)}, u32[]{:S(2)}, u32[]{:S(2)}) %collective-permute-start.21) | collective-permute-done | bytes 4128 | tf_op jit(solution)/shard_map/ppermute | solution.py:84
  164.5 3.7 %collective-permute-start.22 = (f32[1024]{0:T(1024)S(1)}, f32[1024]{0:T(1024)S(1)}, u32[]{:S(2)}, u32[]{:S(2)}) collective-permute-start(f32[1024]{0:T(1024)S(1)} %add.265), channel_id=1, source_target_pairs={{0,16},{4,20},{8,24},{12,28},{16,0},{20,4},{24,8},{28,12},{1,17},{... | collective-permute-start | bytes 12296 | tf_op jit(solution)/shard_map/ppermute | solution.py:84
  168.3 1.6 collective-permute-done.22
  169.9 0.6 add.266
  (39 shorter events, 0.1 us)
Async XLA Ops:
  0.0 61.7 %copy-start.2 = (bf16[512,1024]{1,0:T(8,128)(2,1)S(1)}, bf16[512,1024]{1,0:T(8,128)(2,1)}, u32[]{:S(2)}) copy-start(bf16[512,1024]{1,0:T(8,128)(2,1)} %param.4) | copy-start | bytes 3145732
  0.0 61.7 %copy-start.9 = (f32[1024]{0:T(1024)S(1)}, f32[1024]{0:T(1024)}, u32[]{:S(2)}) copy-start(f32[1024]{0:T(1024)} %param.6) | copy-start | bytes 12292
  0.0 28.4 %collective-permute-start.2 = (bf16[512,1024]{1,0:T(8,128)(2,1)}, bf16[512,1024]{1,0:T(8,128)(2,1)S(1)}, u32[]{:S(2)}, u32[]{:S(2)}) collective-permute-start(bf16[512,1024]{1,0:T(8,128)(2,1)} %param.5), channel_id=1, source_target_pairs={{8,0},{12,4},{16,8},{20,12},{24,16},{28,20},{9,1},{13,5},{17,9},{2... | collective-permute-start | bytes 3145736 | tf_op jit(solution)/shard_map/ppermute | solution.py:104
  1.4 29.3 %collective-permute-start.3 = (bf16[512,1024]{1,0:T(8,128)(2,1)}, bf16[512,1024]{1,0:T(8,128)(2,1)S(1)}, u32[]{:S(2)}, u32[]{:S(2)}) collective-permute-start(bf16[512,1024]{1,0:T(8,128)(2,1)} %param.5), channel_id=1, source_target_pairs={{0,8},{4,12},{8,16},{12,20},{16,24},{20,28},{1,9},{5,13},{9,17},{1... | collective-permute-start | bytes 3145736 | tf_op jit(solution)/shard_map/ppermute | solution.py:104
  28.4 1.0 copy-start.4
  29.4 26.3 %collective-permute-start.6 = (bf16[512,1024]{1,0:T(8,128)(2,1)S(1)}, bf16[512,1024]{1,0:T(8,128)(2,1)}, u32[]{:S(2)}, u32[]{:S(2)}) collective-permute-start(bf16[512,1024]{1,0:T(8,128)(2,1)S(1)} %collective-permute-done.2), channel_id=1, source_target_pairs={{8,0},{12,4},{16,8},{20,12},{9,1},{13,5},{17,9},{21,13},{10,2},{14... | collective-permute-start | bytes 3145736 | tf_op jit(solution)/shard_map/ppermute | solution.py:104
  30.7 25.0 %copy-start.6 = (bf16[512,1024]{1,0:T(8,128)(2,1)}, bf16[512,1024]{1,0:T(8,128)(2,1)S(1)}, u32[]{:S(2)}) copy-start(bf16[512,1024]{1,0:T(8,128)(2,1)S(1)} %collective-permute-done.3) | copy-start | bytes 3145732
  30.7 26.3 %collective-permute-start.4 = (bf16[512,1024]{1,0:T(8,128)(2,1)S(1)}, bf16[512,1024]{1,0:T(8,128)(2,1)}, u32[]{:S(2)}, u32[]{:S(2)}) collective-permute-start(bf16[512,1024]{1,0:T(8,128)(2,1)S(1)} %collective-permute-done.3), channel_id=1, source_target_pairs={{8,16},{12,20},{16,24},{20,28},{9,17},{13,21},{17,25},{21,29},{10,... | collective-permute-start | bytes 3145736 | tf_op jit(solution)/shard_map/ppermute | solution.py:104
  32.4 29.4 %collective-permute-start = (bf16[512,1024]{1,0:T(8,128)(2,1)}, bf16[512,1024]{1,0:T(8,128)(2,1)}, u32[]{:S(2)}, u32[]{:S(2)}) collective-permute-start(bf16[512,1024]{1,0:T(8,128)(2,1)} %param.4), channel_id=1, source_target_pairs={{0,4},{4,0},{8,12},{12,8},{16,20},{20,16},{24,28},{28,24},{1,5},{5... | collective-permute-start | bytes 3145736 | tf_op jit(solution)/shard_map/ppermute | solution.py:135
  55.7 25.6 %collective-permute-start.7 = (bf16[512,1024]{1,0:T(8,128)(2,1)}, bf16[512,1024]{1,0:T(8,128)(2,1)}, u32[]{:S(2)}, u32[]{:S(2)}) collective-permute-start(bf16[512,1024]{1,0:T(8,128)(2,1)} %collective-permute-done.6), channel_id=1, source_target_pairs={{8,0},{12,4},{9,1},{13,5},{10,2},{14,6},{11,3},{15,7}} | collective-permute-start | bytes 3145736 | tf_op jit(solution)/shard_map/ppermute | solution.py:104
  57.0 25.7 %collective-permute-start.5 = (bf16[512,1024]{1,0:T(8,128)(2,1)}, bf16[512,1024]{1,0:T(8,128)(2,1)}, u32[]{:S(2)}, u32[]{:S(2)}) collective-permute-start(bf16[512,1024]{1,0:T(8,128)(2,1)} %collective-permute-done.4), channel_id=1, source_target_pairs={{16,24},{20,28},{17,25},{21,29},{18,26},{22,30},{19,27},{23,31}} | collective-permute-start | bytes 3145736 | tf_op jit(solution)/shard_map/ppermute | solution.py:104
  61.7 19.7 %copy-start.7 = (bf16[512,1024]{1,0:T(8,128)(2,1)S(1)}, bf16[512,1024]{1,0:T(8,128)(2,1)}, u32[]{:S(2)}) copy-start(bf16[512,1024]{1,0:T(8,128)(2,1)} %copy-done.6) | copy-start | bytes 3145732
  63.6 19.1 %copy-start.5 = (bf16[512,1024]{1,0:T(8,128)(2,1)S(1)}, bf16[512,1024]{1,0:T(8,128)(2,1)}, u32[]{:S(2)}) copy-start(bf16[512,1024]{1,0:T(8,128)(2,1)} %copy-done.4) | copy-start | bytes 3145732
  63.7 19.3 %copy-start.8 = (bf16[512,1024]{1,0:T(8,128)(2,1)S(1)}, bf16[512,1024]{1,0:T(8,128)(2,1)}, u32[]{:S(2)}) copy-start(bf16[512,1024]{1,0:T(8,128)(2,1)} %param.5) | copy-start | bytes 3145732
  83.6 4.4 %copy-start = (bf16[2048,1024]{1,0:T(8,128)(2,1)}, bf16[2048,1024]{1,0:T(8,128)(2,1)S(1)}, u32[]{:S(2)}) copy-start(bf16[2048,1024]{1,0:T(8,128)(2,1)S(1)} %pad_maximum_fusion) | copy-start | bytes 12582916
  83.6 3.1 %copy-start.1 = (f32[512,1024]{0,1:T(8,128)S(1)}, f32[512,1024]{0,1:T(8,128)}, u32[]{:S(2)}) copy-start(f32[512,1024]{0,1:T(8,128)} %copy.5) | copy-start | bytes 6291460
  85.4 12.6 %collective-permute-start.15 = (f32[1024,256]{0,1:T(8,128)}, f32[1024,256]{0,1:T(8,128)}, u32[]{:S(2)}, u32[]{:S(2)}) collective-permute-start(f32[1024,256]{0,1:T(8,128)} %fusion.45), channel_id=1, source_target_pairs={{0,1},{1,0},{2,3},{3,2},{4,5},{5,4},{6,7},{7,6},{8,9},{9,8},{10,11... | collective-permute-start | bytes 3145736 | tf_op jit(solution)/shard_map/ppermute | solution.py:156
  88.0 24.5 %collective-permute-start.1 = (f32[512,512]{0,1:T(8,128)}, f32[512,512]{0,1:T(8,128)}, u32[]{:S(2)}, u32[]{:S(2)}) collective-permute-start(f32[512,512]{0,1:T(8,128)} %get-tuple-element.14), channel_id=1, source_target_pairs={{0,4},{4,0},{8,12},{12,8},{16,20},{20,16},{24,28},{28,24},{1,5},{5... | collective-permute-start | bytes 3145736 | tf_op jit(solution)/shard_map/ppermute | solution.py:143
  91.9 10.6 %collective-permute-start.9 = (f32[1024,256]{0,1:T(8,128)}, f32[1024,256]{0,1:T(8,128)}, u32[]{:S(2)}, u32[]{:S(2)}) collective-permute-start(f32[1024,256]{0,1:T(8,128)} %fusion.51), channel_id=1, source_target_pairs={{0,1},{1,0},{2,3},{3,2},{4,5},{5,4},{6,7},{7,6},{8,9},{9,8},{10,11... | collective-permute-start | bytes 3145736 | tf_op jit(solution)/shard_map/ppermute | solution.py:156
  94.7 17.9 %collective-permute-start.14 = (f32[1024,256]{0,1:T(8,128)}, f32[1024,256]{0,1:T(8,128)}, u32[]{:S(2)}, u32[]{:S(2)}) collective-permute-start(f32[1024,256]{0,1:T(8,128)} %fusion.48), channel_id=1, source_target_pairs={{0,1},{1,0},{2,3},{3,2},{4,5},{5,4},{6,7},{7,6},{8,9},{9,8},{10,11... | collective-permute-start | bytes 3145736 | tf_op jit(solution)/shard_map/ppermute | solution.py:156
  98.0 22.8 %collective-permute-start.8 = (f32[1024,256]{0,1:T(8,128)}, f32[1024,256]{0,1:T(8,128)}, u32[]{:S(2)}, u32[]{:S(2)}) collective-permute-start(f32[1024,256]{0,1:T(8,128)} %fusion.54), channel_id=1, source_target_pairs={{0,1},{1,0},{2,3},{3,2},{4,5},{5,4},{6,7},{7,6},{8,9},{9,8},{10,11... | collective-permute-start | bytes 3145736 | tf_op jit(solution)/shard_map/ppermute | solution.py:156
  100.9 15.0 %collective-permute-start.16 = (bf16[1024,256]{0,1:T(8,128)(2,1)}, bf16[1024,256]{0,1:T(8,128)(2,1)}, u32[]{:S(2)}, u32[]{:S(2)}) collective-permute-start(bf16[1024,256]{0,1:T(8,128)(2,1)} %fusion.35), channel_id=1, source_target_pairs={{0,2},{1,3},{2,0},{3,1},{4,6},{5,7},{6,4},{7,5},{8,10},{9,11},{10,... | collective-permute-start | bytes 1572872 | tf_op jit(solution)/shard_map/ppermute | solution.py:159
  105.4 21.8 %collective-permute-start.10 = (bf16[1024,256]{0,1:T(8,128)(2,1)}, bf16[1024,256]{0,1:T(8,128)(2,1)}, u32[]{:S(2)}, u32[]{:S(2)}) collective-permute-start(bf16[1024,256]{0,1:T(8,128)(2,1)} %fusion.34), channel_id=1, source_target_pairs={{0,2},{1,3},{2,0},{3,1},{4,6},{5,7},{6,4},{7,5},{8,10},{9,11},{10,... | collective-permute-start | bytes 1572872 | tf_op jit(solution)/shard_map/ppermute | solution.py:159
  119.3 19.1 %collective-permute-start.17 = (bf16[1024,256]{0,1:T(8,128)(2,1)}, bf16[1024,256]{0,1:T(8,128)(2,1)}, u32[]{:S(2)}, u32[]{:S(2)}) collective-permute-start(bf16[1024,256]{0,1:T(8,128)(2,1)} %fusion.40), channel_id=1, source_target_pairs={{0,2},{1,3},{2,0},{3,1},{4,6},{5,7},{6,4},{7,5},{8,10},{9,11},{10,... | collective-permute-start | bytes 1572872 | tf_op jit(solution)/shard_map/ppermute | solution.py:167
  130.5 18.7 %collective-permute-start.11 = (bf16[1024,256]{0,1:T(8,128)(2,1)}, bf16[1024,256]{0,1:T(8,128)(2,1)S(1)}, u32[]{:S(2)}, u32[]{:S(2)}) collective-permute-start(bf16[1024,256]{0,1:T(8,128)(2,1)} %fusion.38), channel_id=1, source_target_pairs={{0,2},{1,3},{2,0},{3,1},{4,6},{5,7},{6,4},{7,5},{8,10},{9,11},{10,... | collective-permute-start | bytes 1572872 | tf_op jit(solution)/shard_map/ppermute | solution.py:167
  132.0 17.2 %collective-permute-start.18 = (bf16[1024,256]{0,1:T(8,128)(2,1)}, bf16[1024,256]{0,1:T(8,128)(2,1)S(1)}, u32[]{:S(2)}, u32[]{:S(2)}) collective-permute-start(bf16[1024,256]{0,1:T(8,128)(2,1)} %fusion.40), channel_id=1, source_target_pairs={{0,1},{1,0},{2,3},{3,2},{4,5},{5,4},{6,7},{7,6},{8,9},{9,8},{10,11... | collective-permute-start | bytes 1572872 | tf_op jit(solution)/shard_map/ppermute | solution.py:168
  138.4 10.8 %collective-permute-start.19 = (bf16[1024,256]{0,1:T(8,128)(2,1)}, bf16[1024,256]{0,1:T(8,128)(2,1)S(1)}, u32[]{:S(2)}, u32[]{:S(2)}) collective-permute-start(bf16[1024,256]{0,1:T(8,128)(2,1)} %collective-permute-done.17), channel_id=1, source_target_pairs={{0,1},{1,0},{2,3},{3,2},{4,5},{5,4},{6,7},{7,6},{8,9},{9,8},{10,11... | collective-permute-start | bytes 1572872 | tf_op jit(solution)/shard_map/ppermute | solution.py:168
  141.1 11.9 %collective-permute-start.12 = (bf16[1024,256]{0,1:T(8,128)(2,1)}, bf16[1024,256]{0,1:T(8,128)(2,1)S(1)}, u32[]{:S(2)}, u32[]{:S(2)}) collective-permute-start(bf16[1024,256]{0,1:T(8,128)(2,1)} %fusion.38), channel_id=1, source_target_pairs={{0,1},{1,0},{2,3},{3,2},{4,5},{5,4},{6,7},{7,6},{8,9},{9,8},{10,11... | collective-permute-start | bytes 1572872 | tf_op jit(solution)/shard_map/ppermute | solution.py:168
  149.2 3.8 %collective-permute-start.13 = (bf16[1024,256]{0,1:T(8,128)(2,1)S(1)}, bf16[1024,256]{0,1:T(8,128)(2,1)S(1)}, u32[]{:S(2)}, u32[]{:S(2)}) collective-permute-start(bf16[1024,256]{0,1:T(8,128)(2,1)S(1)} %collective-permute-done.11), channel_id=1, source_target_pairs={{0,1},{1,0},{2,3},{3,2},{4,5},{5,4},{6,7},{7,6},{8,9},{9,8},{10,11... | collective-permute-start | bytes 1572872 | tf_op jit(solution)/shard_map/ppermute | solution.py:168
  149.2 3.8 %copy-start.3 = (bf16[512,1024]{1,0:T(8,128)(2,1)S(1)}, bf16[512,1024]{1,0:T(8,128)(2,1)}, u32[]{:S(2)}) copy-start(bf16[512,1024]{1,0:T(8,128)(2,1)} %param.4) | copy-start | bytes 3145732
  157.2 3.7 %collective-permute-start.20 = (f32[1024]{0:T(1024)S(1)}, f32[1024]{0:T(1024)S(1)}, u32[]{:S(2)}, u32[]{:S(2)}) collective-permute-start(f32[1024]{0:T(1024)S(1)} %fusion.1), channel_id=1, source_target_pairs={{0,4},{4,0},{8,12},{12,8},{16,20},{20,16},{24,28},{28,24},{1,5},{5... | collective-permute-start | bytes 12296 | tf_op jit(solution)/shard_map/ppermute | solution.py:84
  160.9 3.6 %collective-permute-start.21 = (f32[1024]{0:T(1024)S(1)}, f32[1024]{0:T(1024)S(1)}, u32[]{:S(2)}, u32[]{:S(2)}) collective-permute-start(f32[1024]{0:T(1024)S(1)} %add.264), channel_id=1, source_target_pairs={{0,8},{4,12},{8,0},{12,4},{16,24},{20,28},{24,16},{28,20},{1,9},{5... | collective-permute-start | bytes 12296 | tf_op jit(solution)/shard_map/ppermute | solution.py:84
  164.5 5.3 %collective-permute-start.22 = (f32[1024]{0:T(1024)S(1)}, f32[1024]{0:T(1024)S(1)}, u32[]{:S(2)}, u32[]{:S(2)}) collective-permute-start(f32[1024]{0:T(1024)S(1)} %add.265), channel_id=1, source_target_pairs={{0,16},{4,20},{8,24},{12,28},{16,0},{20,4},{24,8},{28,12},{1,17},{... | collective-permute-start | bytes 12296 | tf_op jit(solution)/shard_map/ppermute | solution.py:84

commit v23 on v22

--- a/solution.py
+++ b/solution.py
@@ -5,7 +5,7 @@
 from jax import lax
 from jax.sharding import PartitionSpec as P
 
-CHUNKS = 2
+CHUNKS = 4
 
 
 def _rows(a, blk, n):

time: 171 us -> 166 us (0.971)
  matrix products: 30.7 us -> 20.4 us
  waiting for transfers between devices: 97.5 us -> 102 us
  starting transfers between devices: 26.6 us -> 30.9 us
  local copies, waits for them, and re-layouts: 7.93 us -> 4.62 us
    dot_general x8 -> x16, matrix products: 22.7 us -> 13.3 us  [pblock(): lax.dot_general(scaled, rows(col, blk), (((1,), (1,)), ((), ())), preferr...]
    ppermute x1, waiting for transfers between devices: 6.62 us -> 0.01 us  [_fast(): lax.ppermute(w_other, 'src', swap)]
    ppermute x2 -> x4, waiting for transfers between devices: 9.79 us -> 16 us  [_fast(): lax.ppermute(halves[k].astype(jnp.bfloat16), 'vox', chip_perm(k))]
    ppermute x2 -> x4, waiting for transfers between devices: 14 us -> 20.2 us  [_fast(): lax.ppermute(piece, 'vox', chip_perm(k))]
    ppermute x2 -> x4, starting transfers between devices: 2.02 us -> 4.18 us  [_fast(): lax.ppermute(halves[k].astype(jnp.bfloat16), 'vox', chip_perm(k))]
    dynamic_slice x1, local copies, waits for them, and re-layouts: 2.61 us -> 0.62 us  [rows(): return lax.dynamic_slice(col, ((blk - ia) % na * ds + c * r, 0), (r, vl))]
    unnamed x21 -> x15, local copies, waits for them, and re-layouts: 5.32 us -> 4 us
    ppermute x2 -> x4, starting transfers between devices: 2.99 us -> 4.1 us  [_fast(): lax.ppermute(piece, 'vox', chip_perm(k))]
  transfers between devices with their start and end apart: 23 -> 35, of which waited for: 11 -> 13; matrix products, arithmetic and copies ran while one was open for 21% -> 16% of each run, Pallas kernels for 0% -> 0%
where the time goes in v23:
time: 166 us
  waiting for transfers between devices  102 us (61%)
  starting transfers between devices  30.9 us (19%)
  matrix products  20.4 us (12%)
  other arithmetic  7.55 us (5%)
  local copies, waits for them, and re-layouts  4.62 us (3%)
    ppermute x6, waiting for transfers between devices, _zline(): cur = lax.ppermute(cur, 'src', pairs)  57.6 us
    ppermute x4, waiting for transfers between devices, _fast(): lax.ppermute(piece, 'vox', chip_perm(k))  20.2 us
    ppermute x4, waiting for transfers between devices, _fast(): lax.ppermute(halves[k].astype(jnp.bfloat16), 'vox', chip_perm(k))  16 us
    dot_general x16, matrix products, pblock(): lax.dot_general(scaled, rows(col, blk), (((1,), (1,)), ((), ())), preferr...  13.3 us
    ppermute x6, starting transfers between devices, _zline(): cur = lax.ppermute(cur, 'src', pairs)  12.8 us
    ppermute x3, waiting for transfers between devices, _sum_over_src(): v = v + lax.ppermute(v, 'src', [(i, i ^ b) for i in range(n)])  8.4 us
    dot_general x4, matrix products, _fast(): jnp.dot(jnp.concatenate([w for _, w in got], axis=1), jnp.concatenate([ro...  7.08 us
    ppermute x4, starting transfers between devices, _fast(): lax.ppermute(halves[k].astype(jnp.bfloat16), 'vox', chip_perm(k))  4.18 us
  transfers between devices with their start and end apart: 35, of which 13 were waited for; matrix products, arithmetic and copies ran while one was open for 16% of the time, Pallas kernels for 0%

profile of v23, /device:TPU:0, one launch (start us, length us, event | category | flops | bytes accessed | tf_op | source)
XLA Modules:
  0.0 166.1 jit_solution(11996456686758087626)
XLA Ops:
  0.0 1.3 collective-permute-start.2
  1.3 5.6 %collective-permute-start.3 = (bf16[512,1024]{1,0:T(8,128)(2,1)}, bf16[512,1024]{1,0:T(8,128)(2,1)S(1)}, u32[]{:S(2)}, u32[]{:S(2)}) collective-permute-start(bf16[512,1024]{1,0:T(8,128)(2,1)} %param.5), channel_id=1, source_target_pairs={{0,8},{4,12},{8,16},{12,20},{16,24},{20,28},{1,9},{5,13},{9,17},{1... | collective-permute-start | bytes 3145736 | tf_op jit(solution)/shard_map/ppermute | solution.py:104
  6.9 21.4 %collective-permute-done.2 = bf16[512,1024]{1,0:T(8,128)(2,1)S(1)} collective-permute-done((bf16[512,1024]{1,0:T(8,128)(2,1)}, bf16[512,1024]{1,0:T(8,128)(2,1)S(1)}, u32[]{:S(2)}, u32[]{:S(2)}) %collective-permute-start.2) | collective-permute-done | bytes 1048608 | tf_op jit(solution)/shard_map/ppermute | solution.py:104
  28.3 1.0 copy-done.1
  29.3 1.3 collective-permute-start.6
  30.6 1.7 collective-permute-start.4
  32.2 1.7 %collective-permute-start = (bf16[512,1024]{1,0:T(8,128)(2,1)}, bf16[512,1024]{1,0:T(8,128)(2,1)}, u32[]{:S(2)}, u32[]{:S(2)}) collective-permute-start(bf16[512,1024]{1,0:T(8,128)(2,1)} %param.4), channel_id=1, source_target_pairs={{0,4},{4,0},{8,12},{12,8},{16,20},{20,16},{24,28},{28,24},{1,5},{5... | collective-permute-start | bytes 3145736 | tf_op jit(solution)/shard_map/ppermute | solution.py:135
  33.9 21.7 %collective-permute-done.6 = bf16[512,1024]{1,0:T(8,128)(2,1)} collective-permute-done((bf16[512,1024]{1,0:T(8,128)(2,1)S(1)}, bf16[512,1024]{1,0:T(8,128)(2,1)}, u32[]{:S(2)}, u32[]{:S(2)}) %collective-permute-start.6) | collective-permute-done | bytes 1048608 | tf_op jit(solution)/shard_map/ppermute | solution.py:104
  55.6 1.3 collective-permute-start.7
  56.9 1.9 %copy.5 = f32[512,1024]{0,1:T(8,128)S(1)} copy(f32[512,1024]{1,0:T(8,128)} %param.7) | data formatting | bytes 4194304 | tf_op args[3]
  58.9 1.6 collective-permute-start.5
  60.5 1.2 select_bitcast_fusion
  61.7 1.4 collective-permute-start.1
  63.1 2.1 %fusion = bf16[1024,1024]{1,0:T(8,128)(2,1)S(1)} fusion(f32[1024]{0:T(1024)S(1)} %copy-done.6, bf16[512,1024]{1,0:T(8,128)(2,1)} %collective-permute-done, bf16[512,1024]{1,0:T(8,128)(2,1)} %param.4), kind=kLoop, calls=%fused_computation.2 | loop fusion | flops 6291456 | bytes 4198400 | tf_op jit(solution)/shard_map/convert_element_type | solution.py:138
  65.3 1.4 broadcast_select_fusion.1
  66.7 14.5 %collective-permute-done.7 = bf16[512,1024]{1,0:T(8,128)(2,1)} collective-permute-done((bf16[512,1024]{1,0:T(8,128)(2,1)}, bf16[512,1024]{1,0:T(8,128)(2,1)}, u32[]{:S(2)}, u32[]{:S(2)}) %collective-permute-start.7) | collective-permute-done | bytes 1048608 | tf_op jit(solution)/shard_map/ppermute | solution.py:104
  81.2 1.3 broadcast_select_fusion
  82.7 1.1 copy-done.5
  86.2 0.8 fusion.89
  87.8 0.8 fusion.95
  96.4 1.1 collective-permute-start.22
  98.5 1.0 collective-permute-start.10
  99.5 6.0 %collective-permute-done.22 = bf16[1024,128]{0,1:T(8,128)(2,1)S(1)} collective-permute-done((bf16[1024,128]{0,1:T(8,128)(2,1)S(1)}, bf16[1024,128]{0,1:T(8,128)(2,1)S(1)}, u32[]{:S(2)}, u32[]{:S(2)}) %collective-permute-start.22) | collective-permute-done | bytes 262176 | tf_op jit(solution)/shard_map/ppermute | solution.py:159
  105.5 1.0 collective-permute-start.16
  106.5 0.8 fusion.74
  107.4 1.1 collective-permute-start.28
  108.5 2.7 %collective-permute-done.10 = bf16[1024,128]{0,1:T(8,128)(2,1)S(1)} collective-permute-done((bf16[1024,128]{0,1:T(8,128)(2,1)S(1)}, bf16[1024,128]{0,1:T(8,128)(2,1)S(1)}, u32[]{:S(2)}, u32[]{:S(2)}) %collective-permute-start.10) | collective-permute-done | bytes 262176 | tf_op jit(solution)/shard_map/ppermute | solution.py:159
  111.1 0.8 fusion.77
  112.0 1.1 collective-permute-start.23
  113.1 3.7 %collective-permute-done.16 = bf16[1024,128]{0,1:T(8,128)(2,1)S(1)} collective-permute-done((bf16[1024,128]{0,1:T(8,128)(2,1)S(1)}, bf16[1024,128]{0,1:T(8,128)(2,1)S(1)}, u32[]{:S(2)}, u32[]{:S(2)}) %collective-permute-start.16) | collective-permute-done | bytes 262176 | tf_op jit(solution)/shard_map/ppermute | solution.py:159
  116.8 1.0 collective-permute-start.11
  117.8 0.8 fusion.80
  118.7 3.7 %collective-permute-done.28 = bf16[1024,128]{0,1:T(8,128)(2,1)S(1)} collective-permute-done((bf16[1024,128]{0,1:T(8,128)(2,1)S(1)}, bf16[1024,128]{0,1:T(8,128)(2,1)S(1)}, u32[]{:S(2)}, u32[]{:S(2)}) %collective-permute-start.28) | collective-permute-done | bytes 262176 | tf_op jit(solution)/shard_map/ppermute | solution.py:159
  122.4 1.0 collective-permute-start.17
  123.4 10.2 %collective-permute-done.11 = bf16[1024,128]{0,1:T(8,128)(2,1)S(1)} collective-permute-done((bf16[1024,128]{0,1:T(8,128)(2,1)S(1)}, bf16[1024,128]{0,1:T(8,128)(2,1)S(1)}, u32[]{:S(2)}, u32[]{:S(2)}) %collective-permute-start.11) | collective-permute-done | bytes 262176 | tf_op jit(solution)/shard_map/ppermute | solution.py:167
  133.6 0.8 fusion.82
  134.5 4.3 %collective-permute-done.17 = bf16[1024,128]{0,1:T(8,128)(2,1)S(1)} collective-permute-done((bf16[1024,128]{0,1:T(8,128)(2,1)S(1)}, bf16[1024,128]{0,1:T(8,128)(2,1)S(1)}, u32[]{:S(2)}, u32[]{:S(2)}) %collective-permute-start.17) | collective-permute-done | bytes 262176 | tf_op jit(solution)/shard_map/ppermute | solution.py:167
  138.8 1.0 collective-permute-start.29
  140.0 1.5 fusion.10
  141.9 5.6 %collective-permute-done.29 = bf16[1024,128]{0,1:T(8,128)(2,1)S(1)} collective-permute-done((bf16[1024,128]{0,1:T(8,128)(2,1)S(1)}, bf16[1024,128]{0,1:T(8,128)(2,1)S(1)}, u32[]{:S(2)}, u32[]{:S(2)}) %collective-permute-start.29) | collective-permute-done | bytes 262176 | tf_op jit(solution)/shard_map/ppermute | solution.py:167
  148.0 1.3 fusion.25
  149.3 1.3 fusion.40
  150.7 3.0 %fusion.1 = f32[1024]{0:T(1024)S(1)} fusion(f32[1024,1024]{1,0:T(8,128)S(1)} %fusion.40, f32[1024,1024]{1,0:T(8,128)S(1)} %fusion.10, f32[1024,1024]{1,0:T(8,128)S(1)} %fusion.25, bf16[512,1024]{1,0:T(8,128)(2,1)} %collective-permute-done, bf16[512,1024]{1,0:T(8,128)(2,1)S(1)} %copy-done, bf16[1024,128]{0,1:T(8,128)(2,1)S(1)} %collective-permute-done.31, ...), kind=kOutput, calls=%fused_computation.3 | convolution fusion | flops 1091566592 | bytes 16781312 | tf_op jit(solution)/shard_map/dot_general | solution.py:170
  153.7 1.1 collective-permute-start.32
  154.8 2.6 %collective-permute-done.32 = f32[1024]{0:T(1024)S(1)} collective-permute-done((f32[1024]{0:T(1024)S(1)}, f32[1024]{0:T(1024)S(1)}, u32[]{:S(2)}, u32[]{:S(2)}) %collective-permute-start.32) | collective-permute-done | bytes 4128 | tf_op jit(solution)/shard_map/ppermute | solution.py:84
  157.4 3.6 %collective-permute-done.33 = f32[1024]{0:T(1024)S(1)} collective-permute-done((f32[1024]{0:T(1024)S(1)}, f32[1024]{0:T(1024)S(1)}, u32[]{:S(2)}, u32[]{:S(2)}) %collective-permute-start.33) | collective-permute-done | bytes 4128 | tf_op jit(solution)/shard_map/ppermute | solution.py:84
  161.0 2.3 %collective-permute-start.34 = (f32[1024]{0:T(1024)S(1)}, f32[1024]{0:T(1024)S(1)}, u32[]{:S(2)}, u32[]{:S(2)}) collective-permute-start(f32[1024]{0:T(1024)S(1)} %add.497), channel_id=1, source_target_pairs={{0,16},{4,20},{8,24},{12,28},{16,0},{20,4},{24,8},{28,12},{1,17},{... | collective-permute-start | bytes 12296 | tf_op jit(solution)/shard_map/ppermute | solution.py:84
  163.3 2.2 %collective-permute-done.34 = f32[1024]{0:T(1024)S(1)} collective-permute-done((f32[1024]{0:T(1024)S(1)}, f32[1024]{0:T(1024)S(1)}, u32[]{:S(2)}, u32[]{:S(2)}) %collective-permute-start.34) | collective-permute-done | bytes 4128 | tf_op jit(solution)/shard_map/ppermute | solution.py:84
  (67 shorter events, 13.8 us)
Async XLA Ops:
  0.0 28.3 %collective-permute-start.2 = (bf16[512,1024]{1,0:T(8,128)(2,1)}, bf16[512,1024]{1,0:T(8,128)(2,1)S(1)}, u32[]{:S(2)}, u32[]{:S(2)}) collective-permute-start(bf16[512,1024]{1,0:T(8,128)(2,1)} %param.5), channel_id=1, source_target_pairs={{8,0},{12,4},{16,8},{20,12},{24,16},{28,20},{9,1},{13,5},{17,9},{2... | collective-permute-start | bytes 3145736 | tf_op jit(solution)/shard_map/ppermute | solution.py:104
  1.3 29.3 %collective-permute-start.3 = (bf16[512,1024]{1,0:T(8,128)(2,1)}, bf16[512,1024]{1,0:T(8,128)(2,1)S(1)}, u32[]{:S(2)}, u32[]{:S(2)}) collective-permute-start(bf16[512,1024]{1,0:T(8,128)(2,1)} %param.5), channel_id=1, source_target_pairs={{0,8},{4,12},{8,16},{12,20},{16,24},{20,28},{1,9},{5,13},{9,17},{1... | collective-permute-start | bytes 3145736 | tf_op jit(solution)/shard_map/ppermute | solution.py:104
  28.3 1.0 copy-start.1
  29.3 26.3 %collective-permute-start.6 = (bf16[512,1024]{1,0:T(8,128)(2,1)S(1)}, bf16[512,1024]{1,0:T(8,128)(2,1)}, u32[]{:S(2)}, u32[]{:S(2)}) collective-permute-start(bf16[512,1024]{1,0:T(8,128)(2,1)S(1)} %collective-permute-done.2), channel_id=1, source_target_pairs={{8,0},{12,4},{16,8},{20,12},{9,1},{13,5},{17,9},{21,13},{10,2},{14... | collective-permute-start | bytes 3145736 | tf_op jit(solution)/shard_map/ppermute | solution.py:104
  30.6 28.3 %copy-start.3 = (bf16[512,1024]{1,0:T(8,128)(2,1)}, bf16[512,1024]{1,0:T(8,128)(2,1)S(1)}, u32[]{:S(2)}) copy-start(bf16[512,1024]{1,0:T(8,128)(2,1)S(1)} %collective-permute-done.3) | copy-start | bytes 3145732
  30.6 28.3 %collective-permute-start.4 = (bf16[512,1024]{1,0:T(8,128)(2,1)S(1)}, bf16[512,1024]{1,0:T(8,128)(2,1)}, u32[]{:S(2)}, u32[]{:S(2)}) collective-permute-start(bf16[512,1024]{1,0:T(8,128)(2,1)S(1)} %collective-permute-done.3), channel_id=1, source_target_pairs={{8,16},{12,20},{16,24},{20,28},{9,17},{13,21},{17,25},{21,29},{10,... | collective-permute-start | bytes 3145736 | tf_op jit(solution)/shard_map/ppermute | solution.py:104
  32.2 30.9 %collective-permute-start = (bf16[512,1024]{1,0:T(8,128)(2,1)}, bf16[512,1024]{1,0:T(8,128)(2,1)}, u32[]{:S(2)}, u32[]{:S(2)}) collective-permute-start(bf16[512,1024]{1,0:T(8,128)(2,1)} %param.4), channel_id=1, source_target_pairs={{0,4},{4,0},{8,12},{12,8},{16,20},{20,16},{24,28},{28,24},{1,5},{5... | collective-permute-start | bytes 3145736 | tf_op jit(solution)/shard_map/ppermute | solution.py:135
  55.6 25.6 %collective-permute-start.7 = (bf16[512,1024]{1,0:T(8,128)(2,1)}, bf16[512,1024]{1,0:T(8,128)(2,1)}, u32[]{:S(2)}, u32[]{:S(2)}) collective-permute-start(bf16[512,1024]{1,0:T(8,128)(2,1)} %collective-permute-done.6), channel_id=1, source_target_pairs={{8,0},{12,4},{9,1},{13,5},{10,2},{14,6},{11,3},{15,7}} | collective-permute-start | bytes 3145736 | tf_op jit(solution)/shard_map/ppermute | solution.py:104
  58.9 23.7 %collective-permute-start.5 = (bf16[512,1024]{1,0:T(8,128)(2,1)}, bf16[512,1024]{1,0:T(8,128)(2,1)}, u32[]{:S(2)}, u32[]{:S(2)}) collective-permute-start(bf16[512,1024]{1,0:T(8,128)(2,1)} %collective-permute-done.4), channel_id=1, source_target_pairs={{16,24},{20,28},{17,25},{21,29},{18,26},{22,30},{19,27},{23,31}} | collective-permute-start | bytes 3145736 | tf_op jit(solution)/shard_map/ppermute | solution.py:104
  60.5 2.6 %copy-start.6 = (f32[1024]{0:T(1024)S(1)}, f32[1024]{0:T(1024)}, u32[]{:S(2)}) copy-start(f32[1024]{0:T(1024)} %param.6) | copy-start | bytes 12292
  61.7 36.5 %collective-permute-start.1 = (f32[512,512]{0,1:T(8,128)}, f32[512,512]{0,1:T(8,128)S(1)}, u32[]{:S(2)}, u32[]{:S(2)}) collective-permute-start(f32[512,512]{0,1:T(8,128)} %get-tuple-element.21), channel_id=1, source_target_pairs={{0,4},{4,0},{8,12},{12,8},{16,20},{20,16},{24,28},{28,24},{1,5},{5... | collective-permute-start | bytes 3145736 | tf_op jit(solution)/shard_map/ppermute | solution.py:143
  65.3 16.0 %copy-start.4 = (bf16[512,1024]{1,0:T(8,128)(2,1)S(1)}, bf16[512,1024]{1,0:T(8,128)(2,1)}, u32[]{:S(2)}) copy-start(bf16[512,1024]{1,0:T(8,128)(2,1)} %copy-done.3) | copy-start | bytes 3145732
  66.7 15.9 %copy-start.2 = (bf16[512,1024]{1,0:T(8,128)(2,1)S(1)}, bf16[512,1024]{1,0:T(8,128)(2,1)}, u32[]{:S(2)}) copy-start(bf16[512,1024]{1,0:T(8,128)(2,1)} %copy-done.1) | copy-start | bytes 3145732
  82.6 1.2 copy-start.5
  89.5 3.5 %collective-permute-start.9 = (f32[1024,128]{0,1:T(8,128)S(1)}, f32[1024,128]{0,1:T(8,128)S(1)}, u32[]{:S(2)}, u32[]{:S(2)}) collective-permute-start(f32[1024,128]{0,1:T(8,128)S(1)} %fusion.101), channel_id=1, source_target_pairs={{0,1},{1,0},{2,3},{3,2},{4,5},{5,4},{6,7},{7,6},{8,9},{9,8},{10,11... | collective-permute-start | bytes 1572872 | tf_op jit(solution)/shard_map/ppermute | solution.py:156
  90.4 3.6 %collective-permute-start.15 = (f32[1024,128]{0,1:T(8,128)S(1)}, f32[1024,128]{0,1:T(8,128)S(1)}, u32[]{:S(2)}, u32[]{:S(2)}) collective-permute-start(f32[1024,128]{0,1:T(8,128)S(1)} %fusion.95), channel_id=1, source_target_pairs={{0,1},{1,0},{2,3},{3,2},{4,5},{5,4},{6,7},{7,6},{8,9},{9,8},{10,11... | collective-permute-start | bytes 1572872 | tf_op jit(solution)/shard_map/ppermute | solution.py:156
  91.8 15.6 %collective-permute-start.8 = (f32[1024,128]{0,1:T(8,128)S(1)}, f32[1024,128]{0,1:T(8,128)S(1)}, u32[]{:S(2)}, u32[]{:S(2)}) collective-permute-start(f32[1024,128]{0,1:T(8,128)S(1)} %fusion.104), channel_id=1, source_target_pairs={{0,1},{1,0},{2,3},{3,2},{4,5},{5,4},{6,7},{7,6},{8,9},{9,8},{10,11... | collective-permute-start | bytes 1572872 | tf_op jit(solution)/shard_map/ppermute | solution.py:156
  91.9 20.1 %collective-permute-start.14 = (f32[1024,128]{0,1:T(8,128)S(1)}, f32[1024,128]{0,1:T(8,128)S(1)}, u32[]{:S(2)}, u32[]{:S(2)}) collective-permute-start(f32[1024,128]{0,1:T(8,128)S(1)} %fusion.98), channel_id=1, source_target_pairs={{0,1},{1,0},{2,3},{3,2},{4,5},{5,4},{6,7},{7,6},{8,9},{9,8},{10,11... | collective-permute-start | bytes 1572872 | tf_op jit(solution)/shard_map/ppermute | solution.py:156
  93.0 2.3 %collective-permute-start.21 = (f32[1024,128]{0,1:T(8,128)S(1)}, f32[1024,128]{0,1:T(8,128)S(1)}, u32[]{:S(2)}, u32[]{:S(2)}) collective-permute-start(f32[1024,128]{0,1:T(8,128)S(1)} %fusion.89), channel_id=1, source_target_pairs={{0,1},{1,0},{2,3},{3,2},{4,5},{5,4},{6,7},{7,6},{8,9},{9,8},{10,11... | collective-permute-start | bytes 1572872 | tf_op jit(solution)/shard_map/ppermute | solution.py:156
  94.0 2.3 %collective-permute-start.27 = (f32[1024,128]{0,1:T(8,128)S(1)}, f32[1024,128]{0,1:T(8,128)S(1)}, u32[]{:S(2)}, u32[]{:S(2)}) collective-permute-start(f32[1024,128]{0,1:T(8,128)S(1)} %fusion.83), channel_id=1, source_target_pairs={{0,1},{1,0},{2,3},{3,2},{4,5},{5,4},{6,7},{7,6},{8,9},{9,8},{10,11... | collective-permute-start | bytes 1572872 | tf_op jit(solution)/shard_map/ppermute | solution.py:156
  95.4 3.1 %collective-permute-start.20 = (f32[1024,128]{0,1:T(8,128)S(1)}, f32[1024,128]{0,1:T(8,128)S(1)}, u32[]{:S(2)}, u32[]{:S(2)}) collective-permute-start(f32[1024,128]{0,1:T(8,128)S(1)} %fusion.92), channel_id=1, source_target_pairs={{0,1},{1,0},{2,3},{3,2},{4,5},{5,4},{6,7},{7,6},{8,9},{9,8},{10,11... | collective-permute-start | bytes 1572872 | tf_op jit(solution)/shard_map/ppermute | solution.py:156
  96.4 9.2 %collective-permute-start.22 = (bf16[1024,128]{0,1:T(8,128)(2,1)S(1)}, bf16[1024,128]{0,1:T(8,128)(2,1)S(1)}, u32[]{:S(2)}, u32[]{:S(2)}) collective-permute-start(bf16[1024,128]{0,1:T(8,128)(2,1)S(1)} %fusion.8), channel_id=1, source_target_pairs={{0,2},{1,3},{2,0},{3,1},{4,6},{5,7},{6,4},{7,5},{8,10},{9,11},{10,... | collective-permute-start | bytes 786440 | tf_op jit(solution)/shard_map/ppermute | solution.py:159
  98.3 20.4 %collective-permute-start.26 = (f32[1024,128]{0,1:T(8,128)S(1)}, f32[1024,128]{0,1:T(8,128)S(1)}, u32[]{:S(2)}, u32[]{:S(2)}) collective-permute-start(f32[1024,128]{0,1:T(8,128)S(1)} %fusion.86), channel_id=1, source_target_pairs={{0,1},{1,0},{2,3},{3,2},{4,5},{5,4},{6,7},{7,6},{8,9},{9,8},{10,11... | collective-permute-start | bytes 1572872 | tf_op jit(solution)/shard_map/ppermute | solution.py:156
  98.5 12.6 %collective-permute-start.10 = (bf16[1024,128]{0,1:T(8,128)(2,1)S(1)}, bf16[1024,128]{0,1:T(8,128)(2,1)S(1)}, u32[]{:S(2)}, u32[]{:S(2)}) collective-permute-start(bf16[1024,128]{0,1:T(8,128)(2,1)S(1)} %fusion.6), channel_id=1, source_target_pairs={{0,2},{1,3},{2,0},{3,1},{4,6},{5,7},{6,4},{7,5},{8,10},{9,11},{10,... | collective-permute-start | bytes 786440 | tf_op jit(solution)/shard_map/ppermute | solution.py:159
  105.5 11.2 %collective-permute-start.16 = (bf16[1024,128]{0,1:T(8,128)(2,1)S(1)}, bf16[1024,128]{0,1:T(8,128)(2,1)S(1)}, u32[]{:S(2)}, u32[]{:S(2)}) collective-permute-start(bf16[1024,128]{0,1:T(8,128)(2,1)S(1)} %fusion.7), channel_id=1, source_target_pairs={{0,2},{1,3},{2,0},{3,1},{4,6},{5,7},{6,4},{7,5},{8,10},{9,11},{10,... | collective-permute-start | bytes 786440 | tf_op jit(solution)/shard_map/ppermute | solution.py:159
  107.4 15.0 %collective-permute-start.28 = (bf16[1024,128]{0,1:T(8,128)(2,1)S(1)}, bf16[1024,128]{0,1:T(8,128)(2,1)S(1)}, u32[]{:S(2)}, u32[]{:S(2)}) collective-permute-start(bf16[1024,128]{0,1:T(8,128)(2,1)S(1)} %fusion.9), channel_id=1, source_target_pairs={{0,2},{1,3},{2,0},{3,1},{4,6},{5,7},{6,4},{7,5},{8,10},{9,11},{10,... | collective-permute-start | bytes 786440 | tf_op jit(solution)/shard_map/ppermute | solution.py:159
  111.1 38.2 %collective-permute-start.24 = (bf16[1024,128]{0,1:T(8,128)(2,1)S(1)}, bf16[1024,128]{0,1:T(8,128)(2,1)S(1)}, u32[]{:S(2)}, u32[]{:S(2)}) collective-permute-start(bf16[1024,128]{0,1:T(8,128)(2,1)S(1)} %fusion.74), channel_id=1, source_target_pairs={{0,1},{1,0},{2,3},{3,2},{4,5},{5,4},{6,7},{7,6},{8,9},{9,8},{10,11... | collective-permute-start | bytes 786440 | tf_op jit(solution)/shard_map/ppermute | solution.py:168
  112.0 29.5 %collective-permute-start.23 = (bf16[1024,128]{0,1:T(8,128)(2,1)S(1)}, bf16[1024,128]{0,1:T(8,128)(2,1)S(1)}, u32[]{:S(2)}, u32[]{:S(2)}) collective-permute-start(bf16[1024,128]{0,1:T(8,128)(2,1)S(1)} %fusion.74), channel_id=1, source_target_pairs={{0,2},{1,3},{2,0},{3,1},{4,6},{5,7},{6,4},{7,5},{8,10},{9,11},{10,... | collective-permute-start | bytes 786440 | tf_op jit(solution)/shard_map/ppermute | solution.py:167
  116.8 16.9 %collective-permute-start.11 = (bf16[1024,128]{0,1:T(8,128)(2,1)S(1)}, bf16[1024,128]{0,1:T(8,128)(2,1)S(1)}, u32[]{:S(2)}, u32[]{:S(2)}) collective-permute-start(bf16[1024,128]{0,1:T(8,128)(2,1)S(1)} %fusion.77), channel_id=1, source_target_pairs={{0,2},{1,3},{2,0},{3,1},{4,6},{5,7},{6,4},{7,5},{8,10},{9,11},{10,... | collective-permute-start | bytes 786440 | tf_op jit(solution)/shard_map/ppermute | solution.py:167
  118.6 20.2 %collective-permute-start.12 = (bf16[1024,128]{0,1:T(8,128)(2,1)S(1)}, bf16[1024,128]{0,1:T(8,128)(2,1)S(1)}, u32[]{:S(2)}, u32[]{:S(2)}) collective-permute-start(bf16[1024,128]{0,1:T(8,128)(2,1)S(1)} %fusion.77), channel_id=1, source_target_pairs={{0,1},{1,0},{2,3},{3,2},{4,5},{5,4},{6,7},{7,6},{8,9},{9,8},{10,11... | collective-permute-start | bytes 786440 | tf_op jit(solution)/shard_map/ppermute | solution.py:168
  122.4 16.4 %collective-permute-start.17 = (bf16[1024,128]{0,1:T(8,128)(2,1)S(1)}, bf16[1024,128]{0,1:T(8,128)(2,1)S(1)}, u32[]{:S(2)}, u32[]{:S(2)}) collective-permute-start(bf16[1024,128]{0,1:T(8,128)(2,1)S(1)} %fusion.80), channel_id=1, source_target_pairs={{0,2},{1,3},{2,0},{3,1},{4,6},{5,7},{6,4},{7,5},{8,10},{9,11},{10,... | collective-permute-start | bytes 786440 | tf_op jit(solution)/shard_map/ppermute | solution.py:167
  133.6 6.2 %collective-permute-start.13 = (bf16[1024,128]{0,1:T(8,128)(2,1)S(1)}, bf16[1024,128]{0,1:T(8,128)(2,1)S(1)}, u32[]{:S(2)}, u32[]{:S(2)}) collective-permute-start(bf16[1024,128]{0,1:T(8,128)(2,1)S(1)} %collective-permute-done.11), channel_id=1, source_target_pairs={{0,1},{1,0},{2,3},{3,2},{4,5},{5,4},{6,7},{7,6},{8,9},{9,8},{10,11... | collective-permute-start | bytes 786440 | tf_op jit(solution)/shard_map/ppermute | solution.py:168
  138.8 8.7 %collective-permute-start.18 = (bf16[1024,128]{0,1:T(8,128)(2,1)S(1)}, bf16[1024,128]{0,1:T(8,128)(2,1)S(1)}, u32[]{:S(2)}, u32[]{:S(2)}) collective-permute-start(bf16[1024,128]{0,1:T(8,128)(2,1)S(1)} %fusion.80), channel_id=1, source_target_pairs={{0,1},{1,0},{2,3},{3,2},{4,5},{5,4},{6,7},{7,6},{8,9},{9,8},{10,11... | collective-permute-start | bytes 786440 | tf_op jit(solution)/shard_map/ppermute | solution.py:168
  138.8 8.7 %collective-permute-start.29 = (bf16[1024,128]{0,1:T(8,128)(2,1)S(1)}, bf16[1024,128]{0,1:T(8,128)(2,1)S(1)}, u32[]{:S(2)}, u32[]{:S(2)}) collective-permute-start(bf16[1024,128]{0,1:T(8,128)(2,1)S(1)} %fusion.82), channel_id=1, source_target_pairs={{0,2},{1,3},{2,0},{3,1},{4,6},{5,7},{6,4},{7,5},{8,10},{9,11},{10,... | collective-permute-start | bytes 786440 | tf_op jit(solution)/shard_map/ppermute | solution.py:167
  139.8 8.2 %collective-permute-start.19 = (bf16[1024,128]{0,1:T(8,128)(2,1)S(1)}, bf16[1024,128]{0,1:T(8,128)(2,1)S(1)}, u32[]{:S(2)}, u32[]{:S(2)}) collective-permute-start(bf16[1024,128]{0,1:T(8,128)(2,1)S(1)} %collective-permute-done.17), channel_id=1, source_target_pairs={{0,1},{1,0},{2,3},{3,2},{4,5},{5,4},{6,7},{7,6},{8,9},{9,8},{10,11... | collective-permute-start | bytes 786440 | tf_op jit(solution)/shard_map/ppermute | solution.py:168
  141.5 9.1 %collective-permute-start.30 = (bf16[1024,128]{0,1:T(8,128)(2,1)S(1)}, bf16[1024,128]{0,1:T(8,128)(2,1)S(1)}, u32[]{:S(2)}, u32[]{:S(2)}) collective-permute-start(bf16[1024,128]{0,1:T(8,128)(2,1)S(1)} %fusion.82), channel_id=1, source_target_pairs={{0,1},{1,0},{2,3},{3,2},{4,5},{5,4},{6,7},{7,6},{8,9},{9,8},{10,11... | collective-permute-start | bytes 786440 | tf_op jit(solution)/shard_map/ppermute | solution.py:168
  147.5 1.8 %collective-permute-start.25 = (bf16[1024,128]{0,1:T(8,128)(2,1)S(1)}, bf16[1024,128]{0,1:T(8,128)(2,1)S(1)}, u32[]{:S(2)}, u32[]{:S(2)}) collective-permute-start(bf16[1024,128]{0,1:T(8,128)(2,1)S(1)} %collective-permute-done.23), channel_id=1, source_target_pairs={{0,1},{1,0},{2,3},{3,2},{4,5},{5,4},{6,7},{7,6},{8,9},{9,8},{10,11... | collective-permute-start | bytes 786440 | tf_op jit(solution)/shard_map/ppermute | solution.py:168
  147.5 3.1 %collective-permute-start.31 = (bf16[1024,128]{0,1:T(8,128)(2,1)S(1)}, bf16[1024,128]{0,1:T(8,128)(2,1)S(1)}, u32[]{:S(2)}, u32[]{:S(2)}) collective-permute-start(bf16[1024,128]{0,1:T(8,128)(2,1)S(1)} %collective-permute-done.29), channel_id=1, source_target_pairs={{0,1},{1,0},{2,3},{3,2},{4,5},{5,4},{6,7},{7,6},{8,9},{9,8},{10,11... | collective-permute-start | bytes 786440 | tf_op jit(solution)/shard_map/ppermute | solution.py:168
  149.3 1.3 copy-start
  153.7 3.7 %collective-permute-start.32 = (f32[1024]{0:T(1024)S(1)}, f32[1024]{0:T(1024)S(1)}, u32[]{:S(2)}, u32[]{:S(2)}) collective-permute-start(f32[1024]{0:T(1024)S(1)} %fusion.1), channel_id=1, source_target_pairs={{0,4},{4,0},{8,12},{12,8},{16,20},{20,16},{24,28},{28,24},{1,5},{5... | collective-permute-start | bytes 12296 | tf_op jit(solution)/shard_map/ppermute | solution.py:84
  157.4 3.6 %collective-permute-start.33 = (f32[1024]{0:T(1024)S(1)}, f32[1024]{0:T(1024)S(1)}, u32[]{:S(2)}, u32[]{:S(2)}) collective-permute-start(f32[1024]{0:T(1024)S(1)} %add.496), channel_id=1, source_target_pairs={{0,8},{4,12},{8,0},{12,4},{16,24},{20,28},{24,16},{28,20},{1,9},{5... | collective-permute-start | bytes 12296 | tf_op jit(solution)/shard_map/ppermute | solution.py:84
  161.0 4.5 %collective-permute-start.34 = (f32[1024]{0:T(1024)S(1)}, f32[1024]{0:T(1024)S(1)}, u32[]{:S(2)}, u32[]{:S(2)}) collective-permute-start(f32[1024]{0:T(1024)S(1)} %add.497), channel_id=1, source_target_pairs={{0,16},{4,20},{8,24},{12,28},{16,0},{20,4},{24,8},{28,12},{1,17},{... | collective-permute-start | bytes 12296 | tf_op jit(solution)/shard_map/ppermute | solution.py:84

commit v24 on v23

--- a/solution.py
+++ b/solution.py
@@ -6,6 +6,7 @@
 from jax.sharding import PartitionSpec as P
 
 CHUNKS = 4
+FAST_CHUNKS = 8
 
 
 def _rows(a, blk, n):
@@ -120,7 +121,7 @@
     first = si % 2 == 0
     sl, vl = forward_voxel_field.shape
     ds = adjoint_voxel_field.shape[0]
-    chunks = CHUNKS if ds % (CHUNKS * 8) == 0 else 1
+    chunks = FAST_CHUNKS if ds % (FAST_CHUNKS * 8) == 0 else 1
     r = ds // chunks
     swap = [(i, i ^ 1) for i in range(2 * na)]
     pair = [(j, j ^ 1) for j in range(vox)]

time: 166 us -> 207 us (1.25)
  matrix products: 20.4 us -> 45.3 us
  starting transfers between devices: 30.9 us -> 45.2 us
    dot_general x4 -> x8, matrix products: 7.08 us -> 20.7 us  [_fast(): jnp.dot(jnp.concatenate([w for _, w in got], axis=1), jnp.concatenate([ro...]
    dot_general x16 -> x32, matrix products: 13.3 us -> 24.6 us  [pblock(): lax.dot_general(scaled, rows(col, blk), (((1,), (1,)), ((), ())), preferr...]
    ppermute x4 -> x8, starting transfers between devices: 4.1 us -> 8.23 us  [_fast(): lax.ppermute(piece, 'vox', chip_perm(k))]
    ppermute x4 -> x8, starting transfers between devices: 4.18 us -> 8.23 us  [_fast(): lax.ppermute(halves[k].astype(jnp.bfloat16), 'vox', chip_perm(k))]
    ppermute x3, starting transfers between devices: 3.39 us -> 6.48 us  [_sum_over_src(): v = v + lax.ppermute(v, 'src', [(i, i ^ b) for i in range(n)])]
    ppermute x6, waiting for transfers between devices: 57.6 us -> 55 us  [_zline(): cur = lax.ppermute(cur, 'src', pairs)]
    ppermute x8 -> x16, waiting for transfers between devices: 0.02 us -> 2.23 us  [_fast(): lax.ppermute(tuple(sends), 'vox', pair)]
    ppermute x8 -> x16, starting transfers between devices: 2.22 us -> 4.37 us  [_fast(): lax.ppermute(tuple(sends), 'vox', pair)]
  transfers between devices with their start and end apart: 35 -> 59, of which waited for: 13 -> 25; matrix products, arithmetic and copies ran while one was open for 16% -> 25% of each run, Pallas kernels for 0% -> 0%
where the time goes in v24:
time: 207 us; the launch traced here: 206 us
  waiting for transfers between devices  102 us (49%)
  matrix products  45.3 us (22%)
  starting transfers between devices  45.2 us (22%)
  other arithmetic  8.99 us (4%)
  local copies, waits for them, and re-layouts  4.24 us (2%)
    ppermute x6, waiting for transfers between devices, _zline(): cur = lax.ppermute(cur, 'src', pairs)  55 us
    dot_general x32, matrix products, pblock(): lax.dot_general(scaled, rows(col, blk), (((1,), (1,)), ((), ())), preferr...  24.6 us
    ppermute x8, waiting for transfers between devices, _fast(): lax.ppermute(piece, 'vox', chip_perm(k))  21.8 us
    dot_general x8, matrix products, _fast(): jnp.dot(jnp.concatenate([w for _, w in got], axis=1), jnp.concatenate([ro...  20.7 us
    ppermute x8, waiting for transfers between devices, _fast(): lax.ppermute(halves[k].astype(jnp.bfloat16), 'vox', chip_perm(k))  16.2 us
    ppermute x6, starting transfers between devices, _zline(): cur = lax.ppermute(cur, 'src', pairs)  12.8 us
    ppermute x8, starting transfers between devices, _fast(): lax.ppermute(halves[k].astype(jnp.bfloat16), 'vox', chip_perm(k))  8.23 us
    ppermute x8, starting transfers between devices, _fast(): lax.ppermute(piece, 'vox', chip_perm(k))  8.23 us
  transfers between devices with their start and end apart: 59, of which 25 were waited for; matrix products, arithmetic and copies ran while one was open for 25% of the time, Pallas kernels for 0%

profile of v24, /device:TPU:0, one launch (start us, length us, event | category | flops | bytes accessed | tf_op | source)
XLA Modules:
  0.0 206.2 jit_solution(4412386470164277167)
XLA Ops:
  0.0 1.3 collective-permute-start.2
  1.3 5.6 %collective-permute-start.3 = (bf16[512,1024]{1,0:T(8,128)(2,1)}, bf16[512,1024]{1,0:T(8,128)(2,1)S(1)}, u32[]{:S(2)}, u32[]{:S(2)}) collective-permute-start(bf16[512,1024]{1,0:T(8,128)(2,1)} %param.5), channel_id=1, source_target_pairs={{0,8},{4,12},{8,16},{12,20},{16,24},{20,28},{1,9},{5,13},{9,17},{1... | collective-permute-start | bytes 3145736 | tf_op jit(solution)/shard_map/ppermute | solution.py:105
  6.9 21.4 %collective-permute-done.2 = bf16[512,1024]{1,0:T(8,128)(2,1)S(1)} collective-permute-done((bf16[512,1024]{1,0:T(8,128)(2,1)}, bf16[512,1024]{1,0:T(8,128)(2,1)S(1)}, u32[]{:S(2)}, u32[]{:S(2)}) %collective-permute-start.2) | collective-permute-done | bytes 1048608 | tf_op jit(solution)/shard_map/ppermute | solution.py:105
  28.3 1.3 collective-permute-start.6
  29.6 1.7 collective-permute-start.4
  31.3 1.7 collective-permute-start
  33.0 21.7 %collective-permute-done.6 = bf16[512,1024]{1,0:T(8,128)(2,1)} collective-permute-done((bf16[512,1024]{1,0:T(8,128)(2,1)S(1)}, bf16[512,1024]{1,0:T(8,128)(2,1)}, u32[]{:S(2)}, u32[]{:S(2)}) %collective-permute-start.6) | collective-permute-done | bytes 1048608 | tf_op jit(solution)/shard_map/ppermute | solution.py:105
  54.6 1.3 collective-permute-start.7
  55.9 3.0 %copy.5 = f32[512,1024]{0,1:T(8,128)} copy(f32[512,1024]{1,0:T(8,128)} %param.7) | data formatting | bytes 4194304 | tf_op args[3]
  58.9 1.7 collective-permute-start.5
  60.6 2.8 %select_bitcast_fusion = (f32[512,512]{0,1:T(8,128)}, f32[512,512]{0,1:T(8,128)S(1)}) fusion(f32[512,2,512]{0,2,1:T(8,128)} %bitcast.37, pred[]{:T(512)S(6)} %eq.110), kind=kLoop, calls=%fused_computation.52 | loop fusion | flops 524288 | bytes 4194305 | tf_op jit(solution)/shard_map/jit(_where)/select_n | solution.py:143
  63.5 1.4 collective-permute-start.1
  64.8 1.9 fusion
  66.8 1.5 broadcast_select_fusion.1
  68.3 12.0 %collective-permute-done.7 = bf16[512,1024]{1,0:T(8,128)(2,1)} collective-permute-done((bf16[512,1024]{1,0:T(8,128)(2,1)}, bf16[512,1024]{1,0:T(8,128)(2,1)}, u32[]{:S(2)}, u32[]{:S(2)}) %collective-permute-start.7) | collective-permute-done | bytes 1048608 | tf_op jit(solution)/shard_map/ppermute | solution.py:105
  80.2 1.3 broadcast_select_fusion
  95.2 1.0 constant_dynamic-slice_fusion.3
  107.2 1.0 collective-permute-start.10
  109.6 3.4 %collective-permute-done.10 = bf16[1024,64]{0,1:T(8,128)(2,1)S(1)} collective-permute-done((bf16[1024,64]{0,1:T(8,128)(2,1)S(1)}, bf16[1024,64]{0,1:T(8,128)(2,1)S(1)}, u32[]{:S(2)}, u32[]{:S(2)}) %collective-permute-start.10) | collective-permute-done | bytes 131104 | tf_op jit(solution)/shard_map/ppermute | solution.py:160
  114.9 3.1 %collective-permute-done.16 = bf16[1024,64]{0,1:T(8,128)(2,1)S(1)} collective-permute-done((bf16[1024,64]{0,1:T(8,128)(2,1)S(1)}, bf16[1024,64]{0,1:T(8,128)(2,1)S(1)}, u32[]{:S(2)}, u32[]{:S(2)}) %collective-permute-start.16) | collective-permute-done | bytes 131104 | tf_op jit(solution)/shard_map/ppermute | solution.py:160
  119.8 3.1 %collective-permute-done.22 = bf16[1024,64]{0,1:T(8,128)(2,1)S(1)} collective-permute-done((bf16[1024,64]{0,1:T(8,128)(2,1)S(1)}, bf16[1024,64]{0,1:T(8,128)(2,1)S(1)}, u32[]{:S(2)}, u32[]{:S(2)}) %collective-permute-start.22) | collective-permute-done | bytes 131104 | tf_op jit(solution)/shard_map/ppermute | solution.py:160
  124.8 3.1 %collective-permute-done.28 = bf16[1024,64]{0,1:T(8,128)(2,1)S(1)} collective-permute-done((bf16[1024,64]{0,1:T(8,128)(2,1)S(1)}, bf16[1024,64]{0,1:T(8,128)(2,1)S(1)}, u32[]{:S(2)}, u32[]{:S(2)}) %collective-permute-start.28) | collective-permute-done | bytes 131104 | tf_op jit(solution)/shard_map/ppermute | solution.py:160
  129.7 1.1 collective-permute-start.34
  130.8 3.2 %collective-permute-done.46 = bf16[1024,64]{0,1:T(8,128)(2,1)S(1)} collective-permute-done((bf16[1024,64]{0,1:T(8,128)(2,1)S(1)}, bf16[1024,64]{0,1:T(8,128)(2,1)S(1)}, u32[]{:S(2)}, u32[]{:S(2)}) %collective-permute-start.46) | collective-permute-done | bytes 131104 | tf_op jit(solution)/shard_map/ppermute | solution.py:160
  135.8 1.1 collective-permute-start.52
  137.7 1.1 collective-permute-start.47
  140.9 1.1 collective-permute-start.17
  141.9 4.9 %collective-permute-done.11 = bf16[1024,64]{0,1:T(8,128)(2,1)S(1)} collective-permute-done((bf16[1024,64]{0,1:T(8,128)(2,1)S(1)}, bf16[1024,64]{0,1:T(8,128)(2,1)S(1)}, u32[]{:S(2)}, u32[]{:S(2)}) %collective-permute-start.11) | collective-permute-done | bytes 131104 | tf_op jit(solution)/shard_map/ppermute | solution.py:168
  147.6 1.6 collective-permute-done.17
  149.3 1.0 collective-permute-start.23
  151.3 3.9 %collective-permute-done.23 = bf16[1024,64]{0,1:T(8,128)(2,1)S(1)} collective-permute-done((bf16[1024,64]{0,1:T(8,128)(2,1)S(1)}, bf16[1024,64]{0,1:T(8,128)(2,1)S(1)}, u32[]{:S(2)}, u32[]{:S(2)}) %collective-permute-start.23) | collective-permute-done | bytes 131104 | tf_op jit(solution)/shard_map/ppermute | solution.py:168
  155.2 1.0 collective-permute-start.29
  157.2 3.9 %collective-permute-done.29 = bf16[1024,64]{0,1:T(8,128)(2,1)S(1)} collective-permute-done((bf16[1024,64]{0,1:T(8,128)(2,1)S(1)}, bf16[1024,64]{0,1:T(8,128)(2,1)S(1)}, u32[]{:S(2)}, u32[]{:S(2)}) %collective-permute-start.29) | collective-permute-done | bytes 131104 | tf_op jit(solution)/shard_map/ppermute | solution.py:168
  161.1 1.0 collective-permute-start.35
  163.1 3.9 %collective-permute-done.35 = bf16[1024,64]{0,1:T(8,128)(2,1)S(1)} collective-permute-done((bf16[1024,64]{0,1:T(8,128)(2,1)S(1)}, bf16[1024,64]{0,1:T(8,128)(2,1)S(1)}, u32[]{:S(2)}, u32[]{:S(2)}) %collective-permute-start.35) | collective-permute-done | bytes 131104 | tf_op jit(solution)/shard_map/ppermute | solution.py:168
  167.0 1.0 collective-permute-start.41
  168.3 2.7 %fusion.63 = f32[1024,1024]{1,0:T(8,128)} fusion(bf16[1024,64]{0,1:T(8,128)(2,1)S(1)} %collective-permute-done.31, bf16[1024,64]{0,1:T(8,128)(2,1)S(1)} %collective-permute-done.30, bf16[1024,64]{0,1:T(8,128)(2,1)S(1)} %collective-permute-done.29, bf16[1024,64]{0,1:T(8,128)(2,1)S(1)} %fusion.154, bf16[64,1024]{1,0:T(8,128)(2,1)S(1)} %get-tuple-element.21, ...), kind=kOutput, calls=%fused_computation.102 | convolution fusion | flops 541065216 | bytes 5242880 | tf_op jit(solution)/shard_map/dot_general | solution.py:171
  171.0 2.0 collective-permute-done.41
  174.2 2.8 %fusion.78 = f32[1024,1024]{1,0:T(8,128)} fusion(bf16[1024,64]{0,1:T(8,128)(2,1)S(1)} %collective-permute-done.37, bf16[1024,64]{0,1:T(8,128)(2,1)S(1)} %collective-permute-done.36, bf16[1024,64]{0,1:T(8,128)(2,1)S(1)} %collective-permute-done.35, bf16[1024,64]{0,1:T(8,128)(2,1)S(1)} %fusion.157, bf16[64,1024]{1,0:T(8,128)(2,1)S(1)} %get-tuple-element.17, ...), kind=kOutput, calls=%fused_computation.117 | convolution fusion | flops 541065216 | bytes 5242880 | tf_op jit(solution)/shard_map/dot_general | solution.py:171
  177.3 1.6 collective-permute-done.53
  179.4 2.8 %fusion.93 = f32[1024,1024]{1,0:T(8,128)} fusion(bf16[1024,64]{0,1:T(8,128)(2,1)S(1)} %collective-permute-done.43, bf16[1024,64]{0,1:T(8,128)(2,1)S(1)} %collective-permute-done.42, bf16[1024,64]{0,1:T(8,128)(2,1)S(1)} %collective-permute-done.41, bf16[1024,64]{0,1:T(8,128)(2,1)S(1)} %fusion.160, bf16[64,1024]{1,0:T(8,128)(2,1)S(1)} %get-tuple-element.13, ...), kind=kOutput, calls=%fused_computation.132 | convolution fusion | flops 541065216 | bytes 5242880 | tf_op jit(solution)/shard_map/dot_general | solution.py:171
  182.2 2.7 %fusion.108 = f32[1024,1024]{1,0:T(8,128)} fusion(bf16[1024,64]{0,1:T(8,128)(2,1)S(1)} %collective-permute-done.49, bf16[1024,64]{0,1:T(8,128)(2,1)S(1)} %collective-permute-done.48, bf16[1024,64]{0,1:T(8,128)(2,1)S(1)} %collective-permute-done.47, bf16[1024,64]{0,1:T(8,128)(2,1)S(1)} %fusion.142, bf16[64,1024]{1,0:T(8,128)(2,1)S(1)} %get-tuple-element.9, ...), kind=kOutput, calls=%fused_computation.147 | convolution fusion | flops 541065216 | bytes 5242880 | tf_op jit(solution)/shard_map/dot_general | solution.py:171
  184.9 7.4 %fusion.1 = f32[1024]{0:T(1024)S(1)} fusion(f32[1024,1024]{1,0:T(8,128)} %fusion.108, f32[1024,1024]{1,0:T(8,128)} %fusion.93, f32[1024,1024]{1,0:T(8,128)} %fusion.78, f32[1024,1024]{1,0:T(8,128)} %fusion.63, f32[1024,1024]{1,0:T(8,128)S(1)} %fusion.48, f32[1024,1024]{1,0:T(8,128)S(1)} %fusion.18, f32[1024,1024]{1,0:T(8,128)S(1)} %fusion.33, ...), kind=kOutput, calls=%fused_computation.17 | convolution fusion | flops 554695680 | bytes 32509952 | tf_op jit(solution)/shard_map/dot_general | solution.py:171
  192.3 2.5 %collective-permute-start.56 = (f32[1024]{0:T(1024)S(1)}, f32[1024]{0:T(1024)S(1)}, u32[]{:S(2)}, u32[]{:S(2)}) collective-permute-start(f32[1024]{0:T(1024)S(1)} %fusion.1), channel_id=1, source_target_pairs={{0,4},{4,0},{8,12},{12,8},{16,20},{20,16},{24,28},{28,24},{1,5},{5... | collective-permute-start | bytes 12296 | tf_op jit(solution)/shard_map/ppermute | solution.py:85
  194.8 1.6 collective-permute-done.56
  196.4 3.6 %collective-permute-done.57 = f32[1024]{0:T(1024)S(1)} collective-permute-done((f32[1024]{0:T(1024)S(1)}, f32[1024]{0:T(1024)S(1)}, u32[]{:S(2)}, u32[]{:S(2)}) %collective-permute-start.57) | collective-permute-done | bytes 4128 | tf_op jit(solution)/shard_map/ppermute | solution.py:85
  200.0 4.0 %collective-permute-start.58 = (f32[1024]{0:T(1024)S(1)}, f32[1024]{0:T(1024)S(1)}, u32[]{:S(2)}, u32[]{:S(2)}) collective-permute-start(f32[1024]{0:T(1024)S(1)} %add.961), channel_id=1, source_target_pairs={{0,16},{4,20},{8,24},{12,28},{16,0},{20,4},{24,8},{28,12},{1,17},{... | collective-permute-start | bytes 12296 | tf_op jit(solution)/shard_map/ppermute | solution.py:85
  204.0 1.6 collective-permute-done.58
  (140 shorter events, 44.5 us)
Async XLA Ops:
  0.0 28.3 %collective-permute-start.2 = (bf16[512,1024]{1,0:T(8,128)(2,1)}, bf16[512,1024]{1,0:T(8,128)(2,1)S(1)}, u32[]{:S(2)}, u32[]{:S(2)}) collective-permute-start(bf16[512,1024]{1,0:T(8,128)(2,1)} %param.5), channel_id=1, source_target_pairs={{8,0},{12,4},{16,8},{20,12},{24,16},{28,20},{9,1},{13,5},{17,9},{2... | collective-permute-start | bytes 3145736 | tf_op jit(solution)/shard_map/ppermute | solution.py:105
  1.3 28.3 %collective-permute-start.3 = (bf16[512,1024]{1,0:T(8,128)(2,1)}, bf16[512,1024]{1,0:T(8,128)(2,1)S(1)}, u32[]{:S(2)}, u32[]{:S(2)}) collective-permute-start(bf16[512,1024]{1,0:T(8,128)(2,1)} %param.5), channel_id=1, source_target_pairs={{0,8},{4,12},{8,16},{12,20},{16,24},{20,28},{1,9},{5,13},{9,17},{1... | collective-permute-start | bytes 3145736 | tf_op jit(solution)/shard_map/ppermute | solution.py:105
  28.3 26.3 %collective-permute-start.6 = (bf16[512,1024]{1,0:T(8,128)(2,1)S(1)}, bf16[512,1024]{1,0:T(8,128)(2,1)}, u32[]{:S(2)}, u32[]{:S(2)}) collective-permute-start(bf16[512,1024]{1,0:T(8,128)(2,1)S(1)} %collective-permute-done.2), channel_id=1, source_target_pairs={{8,0},{12,4},{16,8},{20,12},{9,1},{13,5},{17,9},{21,13},{10,2},{14... | collective-permute-start | bytes 3145736 | tf_op jit(solution)/shard_map/ppermute | solution.py:105
  29.6 29.3 %collective-permute-start.4 = (bf16[512,1024]{1,0:T(8,128)(2,1)S(1)}, bf16[512,1024]{1,0:T(8,128)(2,1)}, u32[]{:S(2)}, u32[]{:S(2)}) collective-permute-start(bf16[512,1024]{1,0:T(8,128)(2,1)S(1)} %collective-permute-done.3), channel_id=1, source_target_pairs={{8,16},{12,20},{16,24},{20,28},{9,17},{13,21},{17,25},{21,29},{10,... | collective-permute-start | bytes 3145736 | tf_op jit(solution)/shard_map/ppermute | solution.py:105
  31.3 33.6 %collective-permute-start = (bf16[512,1024]{1,0:T(8,128)(2,1)}, bf16[512,1024]{1,0:T(8,128)(2,1)}, u32[]{:S(2)}, u32[]{:S(2)}) collective-permute-start(bf16[512,1024]{1,0:T(8,128)(2,1)} %param.4), channel_id=1, source_target_pairs={{0,4},{4,0},{8,12},{12,8},{16,20},{20,16},{24,28},{28,24},{1,5},{5... | collective-permute-start | bytes 3145736 | tf_op jit(solution)/shard_map/ppermute | solution.py:136
  54.6 25.6 %collective-permute-start.7 = (bf16[512,1024]{1,0:T(8,128)(2,1)}, bf16[512,1024]{1,0:T(8,128)(2,1)}, u32[]{:S(2)}, u32[]{:S(2)}) collective-permute-start(bf16[512,1024]{1,0:T(8,128)(2,1)} %collective-permute-done.6), channel_id=1, source_target_pairs={{8,0},{12,4},{9,1},{13,5},{10,2},{14,6},{11,3},{15,7}} | collective-permute-start | bytes 3145736 | tf_op jit(solution)/shard_map/ppermute | solution.py:105
  58.9 22.6 %collective-permute-start.5 = (bf16[512,1024]{1,0:T(8,128)(2,1)}, bf16[512,1024]{1,0:T(8,128)(2,1)}, u32[]{:S(2)}, u32[]{:S(2)}) collective-permute-start(bf16[512,1024]{1,0:T(8,128)(2,1)} %collective-permute-done.4), channel_id=1, source_target_pairs={{16,24},{20,28},{17,25},{21,29},{18,26},{22,30},{19,27},{23,31}} | collective-permute-start | bytes 3145736 | tf_op jit(solution)/shard_map/ppermute | solution.py:105
  63.5 45.5 %collective-permute-start.1 = (f32[512,512]{0,1:T(8,128)}, f32[512,512]{0,1:T(8,128)S(1)}, u32[]{:S(2)}, u32[]{:S(2)}) collective-permute-start(f32[512,512]{0,1:T(8,128)} %get-tuple-element.37), channel_id=1, source_target_pairs={{0,4},{4,0},{8,12},{12,8},{16,20},{20,16},{24,28},{28,24},{1,5},{5... | collective-permute-start | bytes 3145736 | tf_op jit(solution)/shard_map/ppermute | solution.py:144
  93.9 15.3 %collective-permute-start.8 = (f32[1024,64]{0,1:T(8,128)S(1)}, f32[1024,64]{0,1:T(8,128)S(1)}, u32[]{:S(2)}, u32[]{:S(2)}) collective-permute-start(f32[1024,64]{0,1:T(8,128)S(1)} %fusion.208), channel_id=1, source_target_pairs={{0,1},{1,0},{2,3},{3,2},{4,5},{5,4},{6,7},{7,6},{8,9},{9,8},{10,11... | collective-permute-start | bytes 786440 | tf_op jit(solution)/shard_map/ppermute | solution.py:157
  94.5 20.3 %collective-permute-start.14 = (f32[1024,64]{0,1:T(8,128)S(1)}, f32[1024,64]{0,1:T(8,128)S(1)}, u32[]{:S(2)}, u32[]{:S(2)}) collective-permute-start(f32[1024,64]{0,1:T(8,128)S(1)} %fusion.202), channel_id=1, source_target_pairs={{0,1},{1,0},{2,3},{3,2},{4,5},{5,4},{6,7},{7,6},{8,9},{9,8},{10,11... | collective-permute-start | bytes 786440 | tf_op jit(solution)/shard_map/ppermute | solution.py:157
  97.0 22.8 %collective-permute-start.20 = (f32[1024,64]{0,1:T(8,128)S(1)}, f32[1024,64]{0,1:T(8,128)S(1)}, u32[]{:S(2)}, u32[]{:S(2)}) collective-permute-start(f32[1024,64]{0,1:T(8,128)S(1)} %fusion.196), channel_id=1, source_target_pairs={{0,1},{1,0},{2,3},{3,2},{4,5},{5,4},{6,7},{7,6},{8,9},{9,8},{10,11... | collective-permute-start | bytes 786440 | tf_op jit(solution)/shard_map/ppermute | solution.py:157
  107.2 5.8 %collective-permute-start.10 = (bf16[1024,64]{0,1:T(8,128)(2,1)S(1)}, bf16[1024,64]{0,1:T(8,128)(2,1)S(1)}, u32[]{:S(2)}, u32[]{:S(2)}) collective-permute-start(bf16[1024,64]{0,1:T(8,128)(2,1)S(1)} %fusion.10), channel_id=1, source_target_pairs={{0,2},{1,3},{2,0},{3,1},{4,6},{5,7},{6,4},{7,5},{8,10},{9,11},{10,... | collective-permute-start | bytes 393224 | tf_op jit(solution)/shard_map/ppermute | solution.py:160
  109.0 15.7 %collective-permute-start.26 = (f32[1024,64]{0,1:T(8,128)S(1)}, f32[1024,64]{0,1:T(8,128)S(1)}, u32[]{:S(2)}, u32[]{:S(2)}) collective-permute-start(f32[1024,64]{0,1:T(8,128)S(1)} %fusion.190), channel_id=1, source_target_pairs={{0,1},{1,0},{2,3},{3,2},{4,5},{5,4},{6,7},{7,6},{8,9},{9,8},{10,11... | collective-permute-start | bytes 786440 | tf_op jit(solution)/shard_map/ppermute | solution.py:157
  109.2 26.6 %collective-permute-start.32 = (f32[1024,64]{0,1:T(8,128)S(1)}, f32[1024,64]{0,1:T(8,128)S(1)}, u32[]{:S(2)}, u32[]{:S(2)}) collective-permute-start(f32[1024,64]{0,1:T(8,128)S(1)} %fusion.184), channel_id=1, source_target_pairs={{0,1},{1,0},{2,3},{3,2},{4,5},{5,4},{6,7},{7,6},{8,9},{9,8},{10,11... | collective-permute-start | bytes 786440 | tf_op jit(solution)/shard_map/ppermute | solution.py:157
  113.0 5.0 %collective-permute-start.16 = (bf16[1024,64]{0,1:T(8,128)(2,1)S(1)}, bf16[1024,64]{0,1:T(8,128)(2,1)S(1)}, u32[]{:S(2)}, u32[]{:S(2)}) collective-permute-start(bf16[1024,64]{0,1:T(8,128)(2,1)S(1)} %fusion.11), channel_id=1, source_target_pairs={{0,2},{1,3},{2,0},{3,1},{4,6},{5,7},{6,4},{7,5},{8,10},{9,11},{10,... | collective-permute-start | bytes 393224 | tf_op jit(solution)/shard_map/ppermute | solution.py:160
  114.8 22.9 %collective-permute-start.38 = (f32[1024,64]{0,1:T(8,128)S(1)}, f32[1024,64]{0,1:T(8,128)S(1)}, u32[]{:S(2)}, u32[]{:S(2)}) collective-permute-start(f32[1024,64]{0,1:T(8,128)S(1)} %fusion.178), channel_id=1, source_target_pairs={{0,1},{1,0},{2,3},{3,2},{4,5},{5,4},{6,7},{7,6},{8,9},{9,8},{10,11... | collective-permute-start | bytes 786440 | tf_op jit(solution)/shard_map/ppermute | solution.py:157
  118.0 5.0 %collective-permute-start.22 = (bf16[1024,64]{0,1:T(8,128)(2,1)S(1)}, bf16[1024,64]{0,1:T(8,128)(2,1)S(1)}, u32[]{:S(2)}, u32[]{:S(2)}) collective-permute-start(bf16[1024,64]{0,1:T(8,128)(2,1)S(1)} %fusion.12), channel_id=1, source_target_pairs={{0,2},{1,3},{2,0},{3,1},{4,6},{5,7},{6,4},{7,5},{8,10},{9,11},{10,... | collective-permute-start | bytes 393224 | tf_op jit(solution)/shard_map/ppermute | solution.py:160
  119.8 9.9 %collective-permute-start.44 = (f32[1024,64]{0,1:T(8,128)S(1)}, f32[1024,64]{0,1:T(8,128)S(1)}, u32[]{:S(2)}, u32[]{:S(2)}) collective-permute-start(f32[1024,64]{0,1:T(8,128)S(1)} %fusion.172), channel_id=1, source_target_pairs={{0,1},{1,0},{2,3},{3,2},{4,5},{5,4},{6,7},{7,6},{8,9},{9,8},{10,11... | collective-permute-start | bytes 786440 | tf_op jit(solution)/shard_map/ppermute | solution.py:157
  122.9 5.0 %collective-permute-start.28 = (bf16[1024,64]{0,1:T(8,128)(2,1)S(1)}, bf16[1024,64]{0,1:T(8,128)(2,1)S(1)}, u32[]{:S(2)}, u32[]{:S(2)}) collective-permute-start(bf16[1024,64]{0,1:T(8,128)(2,1)S(1)} %fusion.13), channel_id=1, source_target_pairs={{0,2},{1,3},{2,0},{3,1},{4,6},{5,7},{6,4},{7,5},{8,10},{9,11},{10,... | collective-permute-start | bytes 393224 | tf_op jit(solution)/shard_map/ppermute | solution.py:160
  124.7 16.0 %collective-permute-start.50 = (f32[1024,64]{0,1:T(8,128)S(1)}, f32[1024,64]{0,1:T(8,128)S(1)}, u32[]{:S(2)}, u32[]{:S(2)}) collective-permute-start(f32[1024,64]{0,1:T(8,128)S(1)} %fusion.166), channel_id=1, source_target_pairs={{0,1},{1,0},{2,3},{3,2},{4,5},{5,4},{6,7},{7,6},{8,9},{9,8},{10,11... | collective-permute-start | bytes 786440 | tf_op jit(solution)/shard_map/ppermute | solution.py:157
  127.9 6.1 %collective-permute-start.46 = (bf16[1024,64]{0,1:T(8,128)(2,1)S(1)}, bf16[1024,64]{0,1:T(8,128)(2,1)S(1)}, u32[]{:S(2)}, u32[]{:S(2)}) collective-permute-start(bf16[1024,64]{0,1:T(8,128)(2,1)S(1)} %fusion.16), channel_id=1, source_target_pairs={{0,2},{1,3},{2,0},{3,1},{4,6},{5,7},{6,4},{7,5},{8,10},{9,11},{10,... | collective-permute-start | bytes 393224 | tf_op jit(solution)/shard_map/ppermute | solution.py:160
  129.7 7.2 %collective-permute-start.34 = (bf16[1024,64]{0,1:T(8,128)(2,1)S(1)}, bf16[1024,64]{0,1:T(8,128)(2,1)S(1)}, u32[]{:S(2)}, u32[]{:S(2)}) collective-permute-start(bf16[1024,64]{0,1:T(8,128)(2,1)S(1)} %fusion.14), channel_id=1, source_target_pairs={{0,2},{1,3},{2,0},{3,1},{4,6},{5,7},{6,4},{7,5},{8,10},{9,11},{10,... | collective-permute-start | bytes 393224 | tf_op jit(solution)/shard_map/ppermute | solution.py:160
  134.0 5.0 %collective-permute-start.40 = (bf16[1024,64]{0,1:T(8,128)(2,1)S(1)}, bf16[1024,64]{0,1:T(8,128)(2,1)S(1)}, u32[]{:S(2)}, u32[]{:S(2)}) collective-permute-start(bf16[1024,64]{0,1:T(8,128)(2,1)S(1)} %fusion.15), channel_id=1, source_target_pairs={{0,2},{1,3},{2,0},{3,1},{4,6},{5,7},{6,4},{7,5},{8,10},{9,11},{10,... | collective-permute-start | bytes 393224 | tf_op jit(solution)/shard_map/ppermute | solution.py:160
  135.8 5.0 %collective-permute-start.52 = (bf16[1024,64]{0,1:T(8,128)(2,1)S(1)}, bf16[1024,64]{0,1:T(8,128)(2,1)S(1)}, u32[]{:S(2)}, u32[]{:S(2)}) collective-permute-start(bf16[1024,64]{0,1:T(8,128)(2,1)S(1)} %fusion.17), channel_id=1, source_target_pairs={{0,2},{1,3},{2,0},{3,1},{4,6},{5,7},{6,4},{7,5},{8,10},{9,11},{10,... | collective-permute-start | bytes 393224 | tf_op jit(solution)/shard_map/ppermute | solution.py:160
  136.9 45.3 %collective-permute-start.48 = (bf16[1024,64]{0,1:T(8,128)(2,1)S(1)}, bf16[1024,64]{0,1:T(8,128)(2,1)S(1)}, u32[]{:S(2)}, u32[]{:S(2)}) collective-permute-start(bf16[1024,64]{0,1:T(8,128)(2,1)S(1)} %fusion.142), channel_id=1, source_target_pairs={{0,1},{1,0},{2,3},{3,2},{4,5},{5,4},{6,7},{7,6},{8,9},{9,8},{10,11... | collective-permute-start | bytes 393224 | tf_op jit(solution)/shard_map/ppermute | solution.py:169
  137.7 39.3 %collective-permute-start.47 = (bf16[1024,64]{0,1:T(8,128)(2,1)S(1)}, bf16[1024,64]{0,1:T(8,128)(2,1)S(1)}, u32[]{:S(2)}, u32[]{:S(2)}) collective-permute-start(bf16[1024,64]{0,1:T(8,128)(2,1)S(1)} %fusion.142), channel_id=1, source_target_pairs={{0,2},{1,3},{2,0},{3,1},{4,6},{5,7},{6,4},{7,5},{8,10},{9,11},{10,... | collective-permute-start | bytes 393224 | tf_op jit(solution)/shard_map/ppermute | solution.py:168
  139.0 7.9 %collective-permute-start.11 = (bf16[1024,64]{0,1:T(8,128)(2,1)S(1)}, bf16[1024,64]{0,1:T(8,128)(2,1)S(1)}, u32[]{:S(2)}, u32[]{:S(2)}) collective-permute-start(bf16[1024,64]{0,1:T(8,128)(2,1)S(1)} %fusion.145), channel_id=1, source_target_pairs={{0,2},{1,3},{2,0},{3,1},{4,6},{5,7},{6,4},{7,5},{8,10},{9,11},{10,... | collective-permute-start | bytes 393224 | tf_op jit(solution)/shard_map/ppermute | solution.py:168
  140.8 8.5 %collective-permute-start.12 = (bf16[1024,64]{0,1:T(8,128)(2,1)S(1)}, bf16[1024,64]{0,1:T(8,128)(2,1)S(1)}, u32[]{:S(2)}, u32[]{:S(2)}) collective-permute-start(bf16[1024,64]{0,1:T(8,128)(2,1)S(1)} %fusion.145), channel_id=1, source_target_pairs={{0,1},{1,0},{2,3},{3,2},{4,5},{5,4},{6,7},{7,6},{8,9},{9,8},{10,11... | collective-permute-start | bytes 393224 | tf_op jit(solution)/shard_map/ppermute | solution.py:169
  140.9 8.4 %collective-permute-start.17 = (bf16[1024,64]{0,1:T(8,128)(2,1)S(1)}, bf16[1024,64]{0,1:T(8,128)(2,1)S(1)}, u32[]{:S(2)}, u32[]{:S(2)}) collective-permute-start(bf16[1024,64]{0,1:T(8,128)(2,1)S(1)} %fusion.148), channel_id=1, source_target_pairs={{0,2},{1,3},{2,0},{3,1},{4,6},{5,7},{6,4},{7,5},{8,10},{9,11},{10,... | collective-permute-start | bytes 393224 | tf_op jit(solution)/shard_map/ppermute | solution.py:168
  149.3 5.9 %collective-permute-start.18 = (bf16[1024,64]{0,1:T(8,128)(2,1)S(1)}, bf16[1024,64]{0,1:T(8,128)(2,1)S(1)}, u32[]{:S(2)}, u32[]{:S(2)}) collective-permute-start(bf16[1024,64]{0,1:T(8,128)(2,1)S(1)} %fusion.148), channel_id=1, source_target_pairs={{0,1},{1,0},{2,3},{3,2},{4,5},{5,4},{6,7},{7,6},{8,9},{9,8},{10,11... | collective-permute-start | bytes 393224 | tf_op jit(solution)/shard_map/ppermute | solution.py:169
  149.3 5.9 %collective-permute-start.23 = (bf16[1024,64]{0,1:T(8,128)(2,1)S(1)}, bf16[1024,64]{0,1:T(8,128)(2,1)S(1)}, u32[]{:S(2)}, u32[]{:S(2)}) collective-permute-start(bf16[1024,64]{0,1:T(8,128)(2,1)S(1)} %fusion.151), channel_id=1, source_target_pairs={{0,2},{1,3},{2,0},{3,1},{4,6},{5,7},{6,4},{7,5},{8,10},{9,11},{10,... | collective-permute-start | bytes 393224 | tf_op jit(solution)/shard_map/ppermute | solution.py:168
  150.3 5.9 %collective-permute-start.19 = (bf16[1024,64]{0,1:T(8,128)(2,1)S(1)}, bf16[1024,64]{0,1:T(8,128)(2,1)S(1)}, u32[]{:S(2)}, u32[]{:S(2)}) collective-permute-start(bf16[1024,64]{0,1:T(8,128)(2,1)S(1)} %collective-permute-done.17), channel_id=1, source_target_pairs={{0,1},{1,0},{2,3},{3,2},{4,5},{5,4},{6,7},{7,6},{8,9},{9,8},{10,11... | collective-permute-start | bytes 393224 | tf_op jit(solution)/shard_map/ppermute | solution.py:169
  155.2 5.9 %collective-permute-start.24 = (bf16[1024,64]{0,1:T(8,128)(2,1)S(1)}, bf16[1024,64]{0,1:T(8,128)(2,1)S(1)}, u32[]{:S(2)}, u32[]{:S(2)}) collective-permute-start(bf16[1024,64]{0,1:T(8,128)(2,1)S(1)} %fusion.151), channel_id=1, source_target_pairs={{0,1},{1,0},{2,3},{3,2},{4,5},{5,4},{6,7},{7,6},{8,9},{9,8},{10,11... | collective-permute-start | bytes 393224 | tf_op jit(solution)/shard_map/ppermute | solution.py:169
  155.2 5.9 %collective-permute-start.29 = (bf16[1024,64]{0,1:T(8,128)(2,1)S(1)}, bf16[1024,64]{0,1:T(8,128)(2,1)S(1)}, u32[]{:S(2)}, u32[]{:S(2)}) collective-permute-start(bf16[1024,64]{0,1:T(8,128)(2,1)S(1)} %fusion.154), channel_id=1, source_target_pairs={{0,2},{1,3},{2,0},{3,1},{4,6},{5,7},{6,4},{7,5},{8,10},{9,11},{10,... | collective-permute-start | bytes 393224 | tf_op jit(solution)/shard_map/ppermute | solution.py:168
  156.2 5.9 %collective-permute-start.25 = (bf16[1024,64]{0,1:T(8,128)(2,1)S(1)}, bf16[1024,64]{0,1:T(8,128)(2,1)S(1)}, u32[]{:S(2)}, u32[]{:S(2)}) collective-permute-start(bf16[1024,64]{0,1:T(8,128)(2,1)S(1)} %collective-permute-done.23), channel_id=1, source_target_pairs={{0,1},{1,0},{2,3},{3,2},{4,5},{5,4},{6,7},{7,6},{8,9},{9,8},{10,11... | collective-permute-start | bytes 393224 | tf_op jit(solution)/shard_map/ppermute | solution.py:169
  161.1 5.9 %collective-permute-start.30 = (bf16[1024,64]{0,1:T(8,128)(2,1)S(1)}, bf16[1024,64]{0,1:T(8,128)(2,1)S(1)}, u32[]{:S(2)}, u32[]{:S(2)}) collective-permute-start(bf16[1024,64]{0,1:T(8,128)(2,1)S(1)} %fusion.154), channel_id=1, source_target_pairs={{0,1},{1,0},{2,3},{3,2},{4,5},{5,4},{6,7},{7,6},{8,9},{9,8},{10,11... | collective-permute-start | bytes 393224 | tf_op jit(solution)/shard_map/ppermute | solution.py:169
  161.1 5.9 %collective-permute-start.35 = (bf16[1024,64]{0,1:T(8,128)(2,1)S(1)}, bf16[1024,64]{0,1:T(8,128)(2,1)S(1)}, u32[]{:S(2)}, u32[]{:S(2)}) collective-permute-start(bf16[1024,64]{0,1:T(8,128)(2,1)S(1)} %fusion.157), channel_id=1, source_target_pairs={{0,2},{1,3},{2,0},{3,1},{4,6},{5,7},{6,4},{7,5},{8,10},{9,11},{10,... | collective-permute-start | bytes 393224 | tf_op jit(solution)/shard_map/ppermute | solution.py:168
  162.1 5.9 %collective-permute-start.31 = (bf16[1024,64]{0,1:T(8,128)(2,1)S(1)}, bf16[1024,64]{0,1:T(8,128)(2,1)S(1)}, u32[]{:S(2)}, u32[]{:S(2)}) collective-permute-start(bf16[1024,64]{0,1:T(8,128)(2,1)S(1)} %collective-permute-done.29), channel_id=1, source_target_pairs={{0,1},{1,0},{2,3},{3,2},{4,5},{5,4},{6,7},{7,6},{8,9},{9,8},{10,11... | collective-permute-start | bytes 393224 | tf_op jit(solution)/shard_map/ppermute | solution.py:169
  167.0 5.9 %collective-permute-start.36 = (bf16[1024,64]{0,1:T(8,128)(2,1)S(1)}, bf16[1024,64]{0,1:T(8,128)(2,1)S(1)}, u32[]{:S(2)}, u32[]{:S(2)}) collective-permute-start(bf16[1024,64]{0,1:T(8,128)(2,1)S(1)} %fusion.157), channel_id=1, source_target_pairs={{0,1},{1,0},{2,3},{3,2},{4,5},{5,4},{6,7},{7,6},{8,9},{9,8},{10,11... | collective-permute-start | bytes 393224 | tf_op jit(solution)/shard_map/ppermute | solution.py:169
  167.0 5.9 %collective-permute-start.41 = (bf16[1024,64]{0,1:T(8,128)(2,1)S(1)}, bf16[1024,64]{0,1:T(8,128)(2,1)S(1)}, u32[]{:S(2)}, u32[]{:S(2)}) collective-permute-start(bf16[1024,64]{0,1:T(8,128)(2,1)S(1)} %fusion.160), channel_id=1, source_target_pairs={{0,2},{1,3},{2,0},{3,1},{4,6},{5,7},{6,4},{7,5},{8,10},{9,11},{10,... | collective-permute-start | bytes 393224 | tf_op jit(solution)/shard_map/ppermute | solution.py:168
  168.0 5.9 %collective-permute-start.37 = (bf16[1024,64]{0,1:T(8,128)(2,1)S(1)}, bf16[1024,64]{0,1:T(8,128)(2,1)S(1)}, u32[]{:S(2)}, u32[]{:S(2)}) collective-permute-start(bf16[1024,64]{0,1:T(8,128)(2,1)S(1)} %collective-permute-done.35), channel_id=1, source_target_pairs={{0,1},{1,0},{2,3},{3,2},{4,5},{5,4},{6,7},{7,6},{8,9},{9,8},{10,11... | collective-permute-start | bytes 393224 | tf_op jit(solution)/shard_map/ppermute | solution.py:169
  172.9 5.9 %collective-permute-start.42 = (bf16[1024,64]{0,1:T(8,128)(2,1)S(1)}, bf16[1024,64]{0,1:T(8,128)(2,1)S(1)}, u32[]{:S(2)}, u32[]{:S(2)}) collective-permute-start(bf16[1024,64]{0,1:T(8,128)(2,1)S(1)} %fusion.160), channel_id=1, source_target_pairs={{0,1},{1,0},{2,3},{3,2},{4,5},{5,4},{6,7},{7,6},{8,9},{9,8},{10,11... | collective-permute-start | bytes 393224 | tf_op jit(solution)/shard_map/ppermute | solution.py:169
  172.9 5.9 %collective-permute-start.53 = (bf16[1024,64]{0,1:T(8,128)(2,1)S(1)}, bf16[1024,64]{0,1:T(8,128)(2,1)S(1)}, u32[]{:S(2)}, u32[]{:S(2)}) collective-permute-start(bf16[1024,64]{0,1:T(8,128)(2,1)S(1)} %fusion.162), channel_id=1, source_target_pairs={{0,2},{1,3},{2,0},{3,1},{4,6},{5,7},{6,4},{7,5},{8,10},{9,11},{10,... | collective-permute-start | bytes 393224 | tf_op jit(solution)/shard_map/ppermute | solution.py:168
  174.0 5.4 %collective-permute-start.43 = (bf16[1024,64]{0,1:T(8,128)(2,1)S(1)}, bf16[1024,64]{0,1:T(8,128)(2,1)S(1)}, u32[]{:S(2)}, u32[]{:S(2)}) collective-permute-start(bf16[1024,64]{0,1:T(8,128)(2,1)S(1)} %collective-permute-done.41), channel_id=1, source_target_pairs={{0,1},{1,0},{2,3},{3,2},{4,5},{5,4},{6,7},{7,6},{8,9},{9,8},{10,11... | collective-permute-start | bytes 393224 | tf_op jit(solution)/shard_map/ppermute | solution.py:169
  177.0 7.9 %collective-permute-start.54 = (bf16[1024,64]{0,1:T(8,128)(2,1)S(1)}, bf16[1024,64]{0,1:T(8,128)(2,1)S(1)}, u32[]{:S(2)}, u32[]{:S(2)}) collective-permute-start(bf16[1024,64]{0,1:T(8,128)(2,1)S(1)} %fusion.162), channel_id=1, source_target_pairs={{0,1},{1,0},{2,3},{3,2},{4,5},{5,4},{6,7},{7,6},{8,9},{9,8},{10,11... | collective-permute-start | bytes 393224 | tf_op jit(solution)/shard_map/ppermute | solution.py:169
  178.9 6.0 %collective-permute-start.55 = (bf16[1024,64]{0,1:T(8,128)(2,1)S(1)}, bf16[1024,64]{0,1:T(8,128)(2,1)S(1)}, u32[]{:S(2)}, u32[]{:S(2)}) collective-permute-start(bf16[1024,64]{0,1:T(8,128)(2,1)S(1)} %collective-permute-done.53), channel_id=1, source_target_pairs={{0,1},{1,0},{2,3},{3,2},{4,5},{5,4},{6,7},{7,6},{8,9},{9,8},{10,11... | collective-permute-start | bytes 393224 | tf_op jit(solution)/shard_map/ppermute | solution.py:169
  192.3 4.1 %collective-permute-start.56 = (f32[1024]{0:T(1024)S(1)}, f32[1024]{0:T(1024)S(1)}, u32[]{:S(2)}, u32[]{:S(2)}) collective-permute-start(f32[1024]{0:T(1024)S(1)} %fusion.1), channel_id=1, source_target_pairs={{0,4},{4,0},{8,12},{12,8},{16,20},{20,16},{24,28},{28,24},{1,5},{5... | collective-permute-start | bytes 12296 | tf_op jit(solution)/shard_map/ppermute | solution.py:85
  200.0 5.6 %collective-permute-start.58 = (f32[1024]{0:T(1024)S(1)}, f32[1024]{0:T(1024)S(1)}, u32[]{:S(2)}, u32[]{:S(2)}) collective-permute-start(f32[1024]{0:T(1024)S(1)} %add.961), channel_id=1, source_target_pairs={{0,16},{4,20},{8,24},{12,28},{16,0},{20,4},{24,8},{28,12},{1,17},{... | collective-permute-start | bytes 12296 | tf_op jit(solution)/shard_map/ppermute | solution.py:85
  (20 other events, 160.8 us)

commit v25 on v23

--- a/solution.py
+++ b/solution.py
@@ -6,6 +6,7 @@
 from jax.sharding import PartitionSpec as P
 
 CHUNKS = 4
+RELAYS = 2
 
 
 def _rows(a, blk, n):
@@ -128,8 +129,12 @@
     def chip_perm(k):
         return [(g * 2 + p, ((g + k) % m) * 2 + p) for g in range(m) for p in range(2)]
 
+    relays = RELAYS if chunks % RELAYS == 0 else 1
+    hr = ds // relays
+    per = chunks // relays
+
     def rows(col, blk):
-        return lax.dynamic_slice(col, (((blk - ia) % na) * ds + c * r, 0), (r, vl))
+        return lax.dynamic_slice(col, (((blk - ia) % na) * hr + (c % per) * r, 0), (r, vl))
 
     fwd = jnp.concatenate(
         [forward_voxel_field, lax.ppermute(forward_voxel_field, "src", swap)], axis=0
@@ -142,8 +147,9 @@
     w_other = jnp.where(first, weight[:, 1], weight[:, 0])
     weight = jnp.concatenate([w_mine, lax.ppermute(w_other, "src", swap)], axis=0)
     back = jnp.zeros((2 * sl, vl), jnp.float32)
-    col = _zline(adjoint_voxel_field, na)
+    cols = [_zline(adjoint_voxel_field[h * hr:(h + 1) * hr], na) for h in range(relays)]
     for c in range(chunks):
+        col = cols[c // per]
 
         def pblock(blk):
             return lax.dot_general(

time: 166 us -> 163 us (0.982)
  waiting for transfers between devices: 102 us -> 93 us
  starting transfers between devices: 30.9 us -> 38.4 us
  other arithmetic: 7.55 us -> 5.49 us
    ppermute x6 -> x12, waiting for transfers between devices: 57.6 us -> 47.1 us  [_zline(): cur = lax.ppermute(cur, 'src', pairs)]
    ppermute x6 -> x12, starting transfers between devices: 12.8 us -> 20.3 us  [_zline(): cur = lax.ppermute(cur, 'src', pairs)]
    ppermute x3, waiting for transfers between devices: 8.4 us -> 10.6 us  [_sum_over_src(): v = v + lax.ppermute(v, 'src', [(i, i ^ b) for i in range(n)])]
    ppermute x3, starting transfers between devices: 3.39 us -> 1.16 us  [_sum_over_src(): v = v + lax.ppermute(v, 'src', [(i, i ^ b) for i in range(n)])]
    ppermute x4, starting transfers between devices: 4.1 us -> 6.06 us  [_fast(): lax.ppermute(piece, 'vox', chip_perm(k))]
    unnamed x15 -> x5, local copies, waits for them, and re-layouts: 4 us -> 2.28 us
  transfers between devices with their start and end apart: 35 -> 41, of which waited for: 13 -> 20; matrix products, arithmetic and copies ran while one was open for 16% -> 16% of each run, Pallas kernels for 0% -> 0%
where the time goes in v25:
time: 163 us; the launch traced here: 162 us
  waiting for transfers between devices  93 us (57%)
  starting transfers between devices  38.4 us (24%)
  matrix products  20.5 us (13%)
  other arithmetic  5.49 us (3%)
  local copies, waits for them, and re-layouts  4.01 us (2%)
    ppermute x12, waiting for transfers between devices, _zline(): cur = lax.ppermute(cur, 'src', pairs)  47.1 us
    ppermute x12, starting transfers between devices, _zline(): cur = lax.ppermute(cur, 'src', pairs)  20.3 us
    ppermute x4, waiting for transfers between devices, _fast(): lax.ppermute(piece, 'vox', chip_perm(k))  19 us
    ppermute x4, waiting for transfers between devices, _fast(): lax.ppermute(halves[k].astype(jnp.bfloat16), 'vox', chip_perm(k))  15.1 us
    dot_general x16, matrix products, pblock(): lax.dot_general(scaled, rows(col, blk), (((1,), (1,)), ((), ())), preferr...  13.4 us
    ppermute x3, waiting for transfers between devices, _sum_over_src(): v = v + lax.ppermute(v, 'src', [(i, i ^ b) for i in range(n)])  10.6 us
    dot_general x4, matrix products, _fast(): jnp.dot(jnp.concatenate([w for _, w in got], axis=1), jnp.concatenate([ro...  7.13 us
    ppermute x4, starting transfers between devices, _fast(): lax.ppermute(piece, 'vox', chip_perm(k))  6.06 us
  transfers between devices with their start and end apart: 41, of which 20 were waited for; matrix products, arithmetic and copies ran while one was open for 16% of the time, Pallas kernels for 0%

profile of v25, /device:TPU:0, one launch (start us, length us, event | category | flops | bytes accessed | tf_op | source)
XLA Modules:
  0.0 162.3 jit_solution(11894357387684586493)
XLA Ops:
  0.0 3.0 %collective-permute-start = (bf16[512,1024]{1,0:T(8,128)(2,1)}, bf16[512,1024]{1,0:T(8,128)(2,1)}, u32[]{:S(2)}, u32[]{:S(2)}) collective-permute-start(bf16[512,1024]{1,0:T(8,128)(2,1)} %param.4), channel_id=1, source_target_pairs={{0,4},{4,0},{8,12},{12,8},{16,20},{20,16},{24,28},{28,24},{1,5},{5... | collective-permute-start | bytes 3145736 | tf_op jit(solution)/shard_map/ppermute | solution.py:140
  3.0 1.3 fusion.127
  4.2 4.3 %collective-permute-start.3 = (bf16[256,1024]{1,0:T(8,128)(2,1)S(1)}, bf16[256,1024]{1,0:T(8,128)(2,1)}, u32[]{:S(2)}, u32[]{:S(2)}) collective-permute-start(bf16[256,1024]{1,0:T(8,128)(2,1)S(1)} %get-tuple-element.23), channel_id=1, source_target_pairs={{0,8},{4,12},{8,16},{12,20},{16,24},{20,28},{1,9},{5,13},{9,17},{1... | collective-permute-start | bytes 1572872 | tf_op jit(solution)/shard_map/ppermute | solution.py:105
  8.5 1.3 collective-permute-start.2
  9.8 5.4 %collective-permute-start.21 = (bf16[256,1024]{1,0:T(8,128)(2,1)S(1)}, bf16[256,1024]{1,0:T(8,128)(2,1)}, u32[]{:S(2)}, u32[]{:S(2)}) collective-permute-start(bf16[256,1024]{1,0:T(8,128)(2,1)S(1)} %get-tuple-element.24), channel_id=1, source_target_pairs={{0,8},{4,12},{8,16},{12,20},{16,24},{20,28},{1,9},{5,13},{9,17},{1... | collective-permute-start | bytes 1572872 | tf_op jit(solution)/shard_map/ppermute | solution.py:105
  15.2 1.3 collective-permute-start.20
  16.8 1.9 %copy.5 = f32[512,1024]{0,1:T(8,128)S(1)} copy(f32[512,1024]{1,0:T(8,128)} %param.7) | data formatting | bytes 4194304 | tf_op args[3]
  18.8 1.3 collective-permute-done.3
  20.8 4.6 %collective-permute-done.2 = bf16[256,1024]{1,0:T(8,128)(2,1)} collective-permute-done((bf16[256,1024]{1,0:T(8,128)(2,1)S(1)}, bf16[256,1024]{1,0:T(8,128)(2,1)}, u32[]{:S(2)}, u32[]{:S(2)}) %collective-permute-start.2) | collective-permute-done | bytes 524320 | tf_op jit(solution)/shard_map/ppermute | solution.py:105
  25.4 1.3 collective-permute-start.6
  26.7 3.2 %collective-permute-done.21 = bf16[256,1024]{1,0:T(8,128)(2,1)} collective-permute-done((bf16[256,1024]{1,0:T(8,128)(2,1)S(1)}, bf16[256,1024]{1,0:T(8,128)(2,1)}, u32[]{:S(2)}, u32[]{:S(2)}) %collective-permute-start.21) | collective-permute-done | bytes 524320 | tf_op jit(solution)/shard_map/ppermute | solution.py:105
  30.5 6.1 %collective-permute-done.20 = bf16[256,1024]{1,0:T(8,128)(2,1)} collective-permute-done((bf16[256,1024]{1,0:T(8,128)(2,1)S(1)}, bf16[256,1024]{1,0:T(8,128)(2,1)}, u32[]{:S(2)}, u32[]{:S(2)}) %collective-permute-start.20) | collective-permute-done | bytes 524320 | tf_op jit(solution)/shard_map/ppermute | solution.py:105
  36.6 1.3 collective-permute-start.24
  39.1 1.8 %fusion = bf16[1024,1024]{1,0:T(8,128)(2,1)S(1)} fusion(f32[1024]{0:T(1024)S(1)} %copy-done.1, bf16[512,1024]{1,0:T(8,128)(2,1)} %collective-permute-done, bf16[512,1024]{1,0:T(8,128)(2,1)S(1)} %copy-done), kind=kLoop, calls=%fused_computation.2 | loop fusion | flops 6291456 | bytes 4198400 | tf_op jit(solution)/shard_map/convert_element_type | solution.py:143
  41.7 6.1 %collective-permute-done.6 = bf16[256,1024]{1,0:T(8,128)(2,1)S(1)} collective-permute-done((bf16[256,1024]{1,0:T(8,128)(2,1)}, bf16[256,1024]{1,0:T(8,128)(2,1)S(1)}, u32[]{:S(2)}, u32[]{:S(2)}) %collective-permute-start.6) | collective-permute-done | bytes 524320 | tf_op jit(solution)/shard_map/ppermute | solution.py:105
  47.8 1.3 collective-permute-start.7
  49.8 9.2 %collective-permute-done.24 = bf16[256,1024]{1,0:T(8,128)(2,1)S(1)} collective-permute-done((bf16[256,1024]{1,0:T(8,128)(2,1)}, bf16[256,1024]{1,0:T(8,128)(2,1)S(1)}, u32[]{:S(2)}, u32[]{:S(2)}) %collective-permute-start.24) | collective-permute-done | bytes 524320 | tf_op jit(solution)/shard_map/ppermute | solution.py:105
  59.0 1.5 collective-permute-start.25
  60.6 1.1 broadcast_select_fusion.5
  61.7 8.5 %collective-permute-done.7 = bf16[256,1024]{1,0:T(8,128)(2,1)S(1)} collective-permute-done((bf16[256,1024]{1,0:T(8,128)(2,1)S(1)}, bf16[256,1024]{1,0:T(8,128)(2,1)S(1)}, u32[]{:S(2)}, u32[]{:S(2)}) %collective-permute-start.7) | collective-permute-done | bytes 524320 | tf_op jit(solution)/shard_map/ppermute | solution.py:105
  70.5 1.1 broadcast_select_fusion.4
  71.6 8.1 %collective-permute-done.25 = bf16[256,1024]{1,0:T(8,128)(2,1)S(1)} collective-permute-done((bf16[256,1024]{1,0:T(8,128)(2,1)S(1)}, bf16[256,1024]{1,0:T(8,128)(2,1)S(1)}, u32[]{:S(2)}, u32[]{:S(2)}) %collective-permute-start.25) | collective-permute-done | bytes 524320 | tf_op jit(solution)/shard_map/ppermute | solution.py:105
  88.2 1.1 collective-permute-done.9
  89.4 0.8 fusion.6
  92.6 1.6 collective-permute-start.34
  95.7 6.1 %collective-permute-done.34 = bf16[1024,128]{0,1:T(8,128)(2,1)S(1)} collective-permute-done((bf16[1024,128]{0,1:T(8,128)(2,1)S(1)}, bf16[1024,128]{0,1:T(8,128)(2,1)S(1)}, u32[]{:S(2)}, u32[]{:S(2)}) %collective-permute-start.34) | collective-permute-done | bytes 262176 | tf_op jit(solution)/shard_map/ppermute | solution.py:165
  101.8 1.5 collective-permute-start.28
  103.3 0.9 fusion.82
  104.8 2.6 %collective-permute-done.10 = bf16[1024,128]{0,1:T(8,128)(2,1)S(1)} collective-permute-done((bf16[1024,128]{0,1:T(8,128)(2,1)S(1)}, bf16[1024,128]{0,1:T(8,128)(2,1)S(1)}, u32[]{:S(2)}, u32[]{:S(2)}) %collective-permute-start.10) | collective-permute-done | bytes 262176 | tf_op jit(solution)/shard_map/ppermute | solution.py:165
  107.4 0.9 fusion.77
  108.3 1.6 collective-permute-start.35
  109.9 3.2 %collective-permute-done.28 = bf16[1024,128]{0,1:T(8,128)(2,1)S(1)} collective-permute-done((bf16[1024,128]{0,1:T(8,128)(2,1)S(1)}, bf16[1024,128]{0,1:T(8,128)(2,1)S(1)}, u32[]{:S(2)}, u32[]{:S(2)}) %collective-permute-start.28) | collective-permute-done | bytes 262176 | tf_op jit(solution)/shard_map/ppermute | solution.py:165
  113.0 1.5 collective-permute-start.11
  114.5 0.9 fusion.74
  115.5 3.2 %collective-permute-done.16 = bf16[1024,128]{0,1:T(8,128)(2,1)S(1)} collective-permute-done((bf16[1024,128]{0,1:T(8,128)(2,1)S(1)}, bf16[1024,128]{0,1:T(8,128)(2,1)S(1)}, u32[]{:S(2)}, u32[]{:S(2)}) %collective-permute-start.16) | collective-permute-done | bytes 262176 | tf_op jit(solution)/shard_map/ppermute | solution.py:165
  118.7 1.5 collective-permute-start.29
  120.2 9.7 %collective-permute-done.11 = bf16[1024,128]{0,1:T(8,128)(2,1)S(1)} collective-permute-done((bf16[1024,128]{0,1:T(8,128)(2,1)S(1)}, bf16[1024,128]{0,1:T(8,128)(2,1)S(1)}, u32[]{:S(2)}, u32[]{:S(2)}) %collective-permute-start.11) | collective-permute-done | bytes 262176 | tf_op jit(solution)/shard_map/ppermute | solution.py:173
  129.9 0.9 fusion.80
  130.8 4.2 %collective-permute-done.29 = bf16[1024,128]{0,1:T(8,128)(2,1)S(1)} collective-permute-done((bf16[1024,128]{0,1:T(8,128)(2,1)S(1)}, bf16[1024,128]{0,1:T(8,128)(2,1)S(1)}, u32[]{:S(2)}, u32[]{:S(2)}) %collective-permute-start.29) | collective-permute-done | bytes 262176 | tf_op jit(solution)/shard_map/ppermute | solution.py:173
  135.0 1.5 collective-permute-start.17
  136.7 1.5 fusion.10
  138.6 5.1 %collective-permute-done.17 = bf16[1024,128]{0,1:T(8,128)(2,1)S(1)} collective-permute-done((bf16[1024,128]{0,1:T(8,128)(2,1)S(1)}, bf16[1024,128]{0,1:T(8,128)(2,1)S(1)}, u32[]{:S(2)}, u32[]{:S(2)}) %collective-permute-start.17) | collective-permute-done | bytes 262176 | tf_op jit(solution)/shard_map/ppermute | solution.py:173
  144.2 1.3 fusion.40
  145.6 1.3 fusion.25
  146.9 3.0 %fusion.1 = f32[1024]{0:T(1024)S(1)} fusion(f32[1024,1024]{1,0:T(8,128)S(1)} %fusion.40, f32[1024,1024]{1,0:T(8,128)S(1)} %fusion.10, f32[1024,1024]{1,0:T(8,128)S(1)} %fusion.25, bf16[512,1024]{1,0:T(8,128)(2,1)} %collective-permute-done, bf16[512,1024]{1,0:T(8,128)(2,1)S(1)} %copy-done, bf16[1024,128]{0,1:T(8,128)(2,1)S(1)} %collective-permute-done.37, ...), kind=kOutput, calls=%fused_computation.3 | convolution fusion | flops 1091566592 | bytes 16781312 | tf_op jit(solution)/shard_map/dot_general | solution.py:176
  150.5 3.1 %collective-permute-done.38 = f32[1024]{0:T(1024)S(1)} collective-permute-done((f32[1024]{0:T(1024)S(1)}, f32[1024]{0:T(1024)S(1)}, u32[]{:S(2)}, u32[]{:S(2)}) %collective-permute-start.38) | collective-permute-done | bytes 4128 | tf_op jit(solution)/shard_map/ppermute | solution.py:85
  154.2 3.0 %collective-permute-done.39 = f32[1024]{0:T(1024)S(1)} collective-permute-done((f32[1024]{0:T(1024)S(1)}, f32[1024]{0:T(1024)S(1)}, u32[]{:S(2)}, u32[]{:S(2)}) %collective-permute-start.39) | collective-permute-done | bytes 4128 | tf_op jit(solution)/shard_map/ppermute | solution.py:85
  157.2 4.5 %collective-permute-done.40 = f32[1024]{0:T(1024)S(1)} collective-permute-done((f32[1024]{0:T(1024)S(1)}, f32[1024]{0:T(1024)S(1)}, u32[]{:S(2)}, u32[]{:S(2)}) %collective-permute-start.40) | collective-permute-done | bytes 4128 | tf_op jit(solution)/shard_map/ppermute | solution.py:85
  (75 shorter events, 20.3 us)
Async XLA Ops:
  0.0 38.2 %collective-permute-start = (bf16[512,1024]{1,0:T(8,128)(2,1)}, bf16[512,1024]{1,0:T(8,128)(2,1)}, u32[]{:S(2)}, u32[]{:S(2)}) collective-permute-start(bf16[512,1024]{1,0:T(8,128)(2,1)} %param.4), channel_id=1, source_target_pairs={{0,4},{4,0},{8,12},{12,8},{16,20},{20,16},{24,28},{28,24},{1,5},{5... | collective-permute-start | bytes 3145736 | tf_op jit(solution)/shard_map/ppermute | solution.py:140
  4.2 15.8 %collective-permute-start.3 = (bf16[256,1024]{1,0:T(8,128)(2,1)S(1)}, bf16[256,1024]{1,0:T(8,128)(2,1)}, u32[]{:S(2)}, u32[]{:S(2)}) collective-permute-start(bf16[256,1024]{1,0:T(8,128)(2,1)S(1)} %get-tuple-element.23), channel_id=1, source_target_pairs={{0,8},{4,12},{8,16},{12,20},{16,24},{20,28},{1,9},{5,13},{9,17},{1... | collective-permute-start | bytes 1572872 | tf_op jit(solution)/shard_map/ppermute | solution.py:105
  8.5 16.9 %collective-permute-start.2 = (bf16[256,1024]{1,0:T(8,128)(2,1)S(1)}, bf16[256,1024]{1,0:T(8,128)(2,1)}, u32[]{:S(2)}, u32[]{:S(2)}) collective-permute-start(bf16[256,1024]{1,0:T(8,128)(2,1)S(1)} %get-tuple-element.23), channel_id=1, source_target_pairs={{8,0},{12,4},{16,8},{20,12},{24,16},{28,20},{9,1},{13,5},{17,9},{2... | collective-permute-start | bytes 1572872 | tf_op jit(solution)/shard_map/ppermute | solution.py:105
  9.8 20.0 %collective-permute-start.21 = (bf16[256,1024]{1,0:T(8,128)(2,1)S(1)}, bf16[256,1024]{1,0:T(8,128)(2,1)}, u32[]{:S(2)}, u32[]{:S(2)}) collective-permute-start(bf16[256,1024]{1,0:T(8,128)(2,1)S(1)} %get-tuple-element.24), channel_id=1, source_target_pairs={{0,8},{4,12},{8,16},{12,20},{16,24},{20,28},{1,9},{5,13},{9,17},{1... | collective-permute-start | bytes 1572872 | tf_op jit(solution)/shard_map/ppermute | solution.py:105
  15.2 21.4 %collective-permute-start.20 = (bf16[256,1024]{1,0:T(8,128)(2,1)S(1)}, bf16[256,1024]{1,0:T(8,128)(2,1)}, u32[]{:S(2)}, u32[]{:S(2)}) collective-permute-start(bf16[256,1024]{1,0:T(8,128)(2,1)S(1)} %get-tuple-element.24), channel_id=1, source_target_pairs={{8,0},{12,4},{16,8},{20,12},{24,16},{28,20},{9,1},{13,5},{17,9},{2... | collective-permute-start | bytes 1572872 | tf_op jit(solution)/shard_map/ppermute | solution.py:105
  20.1 20.9 %collective-permute-start.4 = (bf16[256,1024]{1,0:T(8,128)(2,1)}, bf16[256,1024]{1,0:T(8,128)(2,1)S(1)}, u32[]{:S(2)}, u32[]{:S(2)}) collective-permute-start(bf16[256,1024]{1,0:T(8,128)(2,1)} %collective-permute-done.3), channel_id=1, source_target_pairs={{8,16},{12,20},{16,24},{20,28},{9,17},{13,21},{17,25},{21,29},{10,... | collective-permute-start | bytes 1572872 | tf_op jit(solution)/shard_map/ppermute | solution.py:105
  25.4 22.4 %collective-permute-start.6 = (bf16[256,1024]{1,0:T(8,128)(2,1)}, bf16[256,1024]{1,0:T(8,128)(2,1)S(1)}, u32[]{:S(2)}, u32[]{:S(2)}) collective-permute-start(bf16[256,1024]{1,0:T(8,128)(2,1)} %collective-permute-done.2), channel_id=1, source_target_pairs={{8,0},{12,4},{16,8},{20,12},{9,1},{13,5},{17,9},{21,13},{10,2},{14... | collective-permute-start | bytes 1572872 | tf_op jit(solution)/shard_map/ppermute | solution.py:105
  29.8 19.2 %collective-permute-start.22 = (bf16[256,1024]{1,0:T(8,128)(2,1)}, bf16[256,1024]{1,0:T(8,128)(2,1)S(1)}, u32[]{:S(2)}, u32[]{:S(2)}) collective-permute-start(bf16[256,1024]{1,0:T(8,128)(2,1)} %collective-permute-done.21), channel_id=1, source_target_pairs={{8,16},{12,20},{16,24},{20,28},{9,17},{13,21},{17,25},{21,29},{10,... | collective-permute-start | bytes 1572872 | tf_op jit(solution)/shard_map/ppermute | solution.py:105
  36.6 22.4 %collective-permute-start.24 = (bf16[256,1024]{1,0:T(8,128)(2,1)}, bf16[256,1024]{1,0:T(8,128)(2,1)S(1)}, u32[]{:S(2)}, u32[]{:S(2)}) collective-permute-start(bf16[256,1024]{1,0:T(8,128)(2,1)} %collective-permute-done.20), channel_id=1, source_target_pairs={{8,0},{12,4},{16,8},{20,12},{9,1},{13,5},{17,9},{21,13},{10,2},{14... | collective-permute-start | bytes 1572872 | tf_op jit(solution)/shard_map/ppermute | solution.py:105
  37.9 1.2 copy-start
  37.9 1.2 copy-start.1
  38.2 56.8 %collective-permute-start.1 = (f32[512,512]{0,1:T(8,128)S(1)}, f32[512,512]{0,1:T(8,128)S(1)}, u32[]{:S(2)}, u32[]{:S(2)}) collective-permute-start(f32[512,512]{0,1:T(8,128)S(1)} %get-tuple-element.21), channel_id=1, source_target_pairs={{0,4},{4,0},{8,12},{12,8},{16,20},{20,16},{24,28},{28,24},{1,5},{5... | collective-permute-start | bytes 3145736 | tf_op jit(solution)/shard_map/ppermute | solution.py:148
  41.0 19.6 %collective-permute-start.5 = (bf16[256,1024]{1,0:T(8,128)(2,1)S(1)}, bf16[256,1024]{1,0:T(8,128)(2,1)S(1)}, u32[]{:S(2)}, u32[]{:S(2)}) collective-permute-start(bf16[256,1024]{1,0:T(8,128)(2,1)S(1)} %collective-permute-done.4), channel_id=1, source_target_pairs={{16,24},{20,28},{17,25},{21,29},{18,26},{22,30},{19,27},{23,31}} | collective-permute-start | bytes 1572872 | tf_op jit(solution)/shard_map/ppermute | solution.py:105
  47.8 22.5 %collective-permute-start.7 = (bf16[256,1024]{1,0:T(8,128)(2,1)S(1)}, bf16[256,1024]{1,0:T(8,128)(2,1)S(1)}, u32[]{:S(2)}, u32[]{:S(2)}) collective-permute-start(bf16[256,1024]{1,0:T(8,128)(2,1)S(1)} %collective-permute-done.6), channel_id=1, source_target_pairs={{8,0},{12,4},{9,1},{13,5},{10,2},{14,6},{11,3},{15,7}} | collective-permute-start | bytes 1572872 | tf_op jit(solution)/shard_map/ppermute | solution.py:105
  49.1 21.4 %collective-permute-start.23 = (bf16[256,1024]{1,0:T(8,128)(2,1)S(1)}, bf16[256,1024]{1,0:T(8,128)(2,1)S(1)}, u32[]{:S(2)}, u32[]{:S(2)}) collective-permute-start(bf16[256,1024]{1,0:T(8,128)(2,1)S(1)} %collective-permute-done.22), channel_id=1, source_target_pairs={{16,24},{20,28},{17,25},{21,29},{18,26},{22,30},{19,27},{23,31}} | collective-permute-start | bytes 1572872 | tf_op jit(solution)/shard_map/ppermute | solution.py:105
  59.0 20.7 %collective-permute-start.25 = (bf16[256,1024]{1,0:T(8,128)(2,1)S(1)}, bf16[256,1024]{1,0:T(8,128)(2,1)S(1)}, u32[]{:S(2)}, u32[]{:S(2)}) collective-permute-start(bf16[256,1024]{1,0:T(8,128)(2,1)S(1)} %collective-permute-done.24), channel_id=1, source_target_pairs={{8,0},{12,4},{9,1},{13,5},{10,2},{14,6},{11,3},{15,7}} | collective-permute-start | bytes 1572872 | tf_op jit(solution)/shard_map/ppermute | solution.py:105
  85.8 18.4 %collective-permute-start.8 = (f32[1024,128]{0,1:T(8,128)S(1)}, f32[1024,128]{0,1:T(8,128)S(1)}, u32[]{:S(2)}, u32[]{:S(2)}) collective-permute-start(f32[1024,128]{0,1:T(8,128)S(1)} %fusion.104), channel_id=1, source_target_pairs={{0,1},{1,0},{2,3},{3,2},{4,5},{5,4},{6,7},{7,6},{8,9},{9,8},{10,11... | collective-permute-start | bytes 1572872 | tf_op jit(solution)/shard_map/ppermute | solution.py:162
  85.9 22.4 %collective-permute-start.26 = (f32[1024,128]{0,1:T(8,128)S(1)}, f32[1024,128]{0,1:T(8,128)S(1)}, u32[]{:S(2)}, u32[]{:S(2)}) collective-permute-start(f32[1024,128]{0,1:T(8,128)S(1)} %fusion.92), channel_id=1, source_target_pairs={{0,1},{1,0},{2,3},{3,2},{4,5},{5,4},{6,7},{7,6},{8,9},{9,8},{10,11... | collective-permute-start | bytes 1572872 | tf_op jit(solution)/shard_map/ppermute | solution.py:162
  86.4 2.9 %collective-permute-start.9 = (f32[1024,128]{0,1:T(8,128)S(1)}, f32[1024,128]{0,1:T(8,128)S(1)}, u32[]{:S(2)}, u32[]{:S(2)}) collective-permute-start(f32[1024,128]{0,1:T(8,128)S(1)} %fusion.101), channel_id=1, source_target_pairs={{0,1},{1,0},{2,3},{3,2},{4,5},{5,4},{6,7},{7,6},{8,9},{9,8},{10,11... | collective-permute-start | bytes 1572872 | tf_op jit(solution)/shard_map/ppermute | solution.py:162
  86.5 3.8 %collective-permute-start.27 = (f32[1024,128]{0,1:T(8,128)S(1)}, f32[1024,128]{0,1:T(8,128)S(1)}, u32[]{:S(2)}, u32[]{:S(2)}) collective-permute-start(f32[1024,128]{0,1:T(8,128)S(1)} %fusion.89), channel_id=1, source_target_pairs={{0,1},{1,0},{2,3},{3,2},{4,5},{5,4},{6,7},{7,6},{8,9},{9,8},{10,11... | collective-permute-start | bytes 1572872 | tf_op jit(solution)/shard_map/ppermute | solution.py:162
  89.3 2.3 %collective-permute-start.33 = (f32[1024,128]{0,1:T(8,128)S(1)}, f32[1024,128]{0,1:T(8,128)S(1)}, u32[]{:S(2)}, u32[]{:S(2)}) collective-permute-start(f32[1024,128]{0,1:T(8,128)S(1)} %fusion.83), channel_id=1, source_target_pairs={{0,1},{1,0},{2,3},{3,2},{4,5},{5,4},{6,7},{7,6},{8,9},{9,8},{10,11... | collective-permute-start | bytes 1572872 | tf_op jit(solution)/shard_map/ppermute | solution.py:162
  90.3 2.3 %collective-permute-start.15 = (f32[1024,128]{0,1:T(8,128)S(1)}, f32[1024,128]{0,1:T(8,128)S(1)}, u32[]{:S(2)}, u32[]{:S(2)}) collective-permute-start(f32[1024,128]{0,1:T(8,128)S(1)} %fusion.95), channel_id=1, source_target_pairs={{0,1},{1,0},{2,3},{3,2},{4,5},{5,4},{6,7},{7,6},{8,9},{9,8},{10,11... | collective-permute-start | bytes 1572872 | tf_op jit(solution)/shard_map/ppermute | solution.py:162
  91.6 3.6 %collective-permute-start.32 = (f32[1024,128]{0,1:T(8,128)S(1)}, f32[1024,128]{0,1:T(8,128)S(1)}, u32[]{:S(2)}, u32[]{:S(2)}) collective-permute-start(f32[1024,128]{0,1:T(8,128)S(1)} %fusion.86), channel_id=1, source_target_pairs={{0,1},{1,0},{2,3},{3,2},{4,5},{5,4},{6,7},{7,6},{8,9},{9,8},{10,11... | collective-permute-start | bytes 1572872 | tf_op jit(solution)/shard_map/ppermute | solution.py:162
  92.6 9.2 %collective-permute-start.34 = (bf16[1024,128]{0,1:T(8,128)(2,1)S(1)}, bf16[1024,128]{0,1:T(8,128)(2,1)S(1)}, u32[]{:S(2)}, u32[]{:S(2)}) collective-permute-start(bf16[1024,128]{0,1:T(8,128)(2,1)S(1)} %fusion.9), channel_id=1, source_target_pairs={{0,2},{1,3},{2,0},{3,1},{4,6},{5,7},{6,4},{7,5},{8,10},{9,11},{10,... | collective-permute-start | bytes 786440 | tf_op jit(solution)/shard_map/ppermute | solution.py:165
  95.0 20.4 %collective-permute-start.14 = (f32[1024,128]{0,1:T(8,128)S(1)}, f32[1024,128]{0,1:T(8,128)S(1)}, u32[]{:S(2)}, u32[]{:S(2)}) collective-permute-start(f32[1024,128]{0,1:T(8,128)S(1)} %fusion.98), channel_id=1, source_target_pairs={{0,1},{1,0},{2,3},{3,2},{4,5},{5,4},{6,7},{7,6},{8,9},{9,8},{10,11... | collective-permute-start | bytes 1572872 | tf_op jit(solution)/shard_map/ppermute | solution.py:162
  95.2 12.3 %collective-permute-start.10 = (bf16[1024,128]{0,1:T(8,128)(2,1)S(1)}, bf16[1024,128]{0,1:T(8,128)(2,1)S(1)}, u32[]{:S(2)}, u32[]{:S(2)}) collective-permute-start(bf16[1024,128]{0,1:T(8,128)(2,1)S(1)} %fusion.6), channel_id=1, source_target_pairs={{0,2},{1,3},{2,0},{3,1},{4,6},{5,7},{6,4},{7,5},{8,10},{9,11},{10,... | collective-permute-start | bytes 786440 | tf_op jit(solution)/shard_map/ppermute | solution.py:165
  101.8 11.2 %collective-permute-start.28 = (bf16[1024,128]{0,1:T(8,128)(2,1)S(1)}, bf16[1024,128]{0,1:T(8,128)(2,1)S(1)}, u32[]{:S(2)}, u32[]{:S(2)}) collective-permute-start(bf16[1024,128]{0,1:T(8,128)(2,1)S(1)} %fusion.8), channel_id=1, source_target_pairs={{0,2},{1,3},{2,0},{3,1},{4,6},{5,7},{6,4},{7,5},{8,10},{9,11},{10,... | collective-permute-start | bytes 786440 | tf_op jit(solution)/shard_map/ppermute | solution.py:165
  104.2 14.5 %collective-permute-start.16 = (bf16[1024,128]{0,1:T(8,128)(2,1)S(1)}, bf16[1024,128]{0,1:T(8,128)(2,1)S(1)}, u32[]{:S(2)}, u32[]{:S(2)}) collective-permute-start(bf16[1024,128]{0,1:T(8,128)(2,1)S(1)} %fusion.7), channel_id=1, source_target_pairs={{0,2},{1,3},{2,0},{3,1},{4,6},{5,7},{6,4},{7,5},{8,10},{9,11},{10,... | collective-permute-start | bytes 786440 | tf_op jit(solution)/shard_map/ppermute | solution.py:165
  107.4 39.5 %collective-permute-start.36 = (bf16[1024,128]{0,1:T(8,128)(2,1)S(1)}, bf16[1024,128]{0,1:T(8,128)(2,1)S(1)}, u32[]{:S(2)}, u32[]{:S(2)}) collective-permute-start(bf16[1024,128]{0,1:T(8,128)(2,1)S(1)} %fusion.82), channel_id=1, source_target_pairs={{0,1},{1,0},{2,3},{3,2},{4,5},{5,4},{6,7},{7,6},{8,9},{9,8},{10,11... | collective-permute-start | bytes 786440 | tf_op jit(solution)/shard_map/ppermute | solution.py:174
  108.3 29.9 %collective-permute-start.35 = (bf16[1024,128]{0,1:T(8,128)(2,1)S(1)}, bf16[1024,128]{0,1:T(8,128)(2,1)S(1)}, u32[]{:S(2)}, u32[]{:S(2)}) collective-permute-start(bf16[1024,128]{0,1:T(8,128)(2,1)S(1)} %fusion.82), channel_id=1, source_target_pairs={{0,2},{1,3},{2,0},{3,1},{4,6},{5,7},{6,4},{7,5},{8,10},{9,11},{10,... | collective-permute-start | bytes 786440 | tf_op jit(solution)/shard_map/ppermute | solution.py:173
  113.0 16.9 %collective-permute-start.11 = (bf16[1024,128]{0,1:T(8,128)(2,1)S(1)}, bf16[1024,128]{0,1:T(8,128)(2,1)S(1)}, u32[]{:S(2)}, u32[]{:S(2)}) collective-permute-start(bf16[1024,128]{0,1:T(8,128)(2,1)S(1)} %fusion.77), channel_id=1, source_target_pairs={{0,2},{1,3},{2,0},{3,1},{4,6},{5,7},{6,4},{7,5},{8,10},{9,11},{10,... | collective-permute-start | bytes 786440 | tf_op jit(solution)/shard_map/ppermute | solution.py:173
  115.4 19.5 %collective-permute-start.12 = (bf16[1024,128]{0,1:T(8,128)(2,1)S(1)}, bf16[1024,128]{0,1:T(8,128)(2,1)S(1)}, u32[]{:S(2)}, u32[]{:S(2)}) collective-permute-start(bf16[1024,128]{0,1:T(8,128)(2,1)S(1)} %fusion.77), channel_id=1, source_target_pairs={{0,1},{1,0},{2,3},{3,2},{4,5},{5,4},{6,7},{7,6},{8,9},{9,8},{10,11... | collective-permute-start | bytes 786440 | tf_op jit(solution)/shard_map/ppermute | solution.py:174
  118.7 16.3 %collective-permute-start.29 = (bf16[1024,128]{0,1:T(8,128)(2,1)S(1)}, bf16[1024,128]{0,1:T(8,128)(2,1)S(1)}, u32[]{:S(2)}, u32[]{:S(2)}) collective-permute-start(bf16[1024,128]{0,1:T(8,128)(2,1)S(1)} %fusion.74), channel_id=1, source_target_pairs={{0,2},{1,3},{2,0},{3,1},{4,6},{5,7},{6,4},{7,5},{8,10},{9,11},{10,... | collective-permute-start | bytes 786440 | tf_op jit(solution)/shard_map/ppermute | solution.py:173
  129.9 6.6 %collective-permute-start.13 = (bf16[1024,128]{0,1:T(8,128)(2,1)S(1)}, bf16[1024,128]{0,1:T(8,128)(2,1)S(1)}, u32[]{:S(2)}, u32[]{:S(2)}) collective-permute-start(bf16[1024,128]{0,1:T(8,128)(2,1)S(1)} %collective-permute-done.11), channel_id=1, source_target_pairs={{0,1},{1,0},{2,3},{3,2},{4,5},{5,4},{6,7},{7,6},{8,9},{9,8},{10,11... | collective-permute-start | bytes 786440 | tf_op jit(solution)/shard_map/ppermute | solution.py:174
  135.0 8.7 %collective-permute-start.30 = (bf16[1024,128]{0,1:T(8,128)(2,1)S(1)}, bf16[1024,128]{0,1:T(8,128)(2,1)S(1)}, u32[]{:S(2)}, u32[]{:S(2)}) collective-permute-start(bf16[1024,128]{0,1:T(8,128)(2,1)S(1)} %fusion.74), channel_id=1, source_target_pairs={{0,1},{1,0},{2,3},{3,2},{4,5},{5,4},{6,7},{7,6},{8,9},{9,8},{10,11... | collective-permute-start | bytes 786440 | tf_op jit(solution)/shard_map/ppermute | solution.py:174
  135.0 8.7 %collective-permute-start.17 = (bf16[1024,128]{0,1:T(8,128)(2,1)S(1)}, bf16[1024,128]{0,1:T(8,128)(2,1)S(1)}, u32[]{:S(2)}, u32[]{:S(2)}) collective-permute-start(bf16[1024,128]{0,1:T(8,128)(2,1)S(1)} %fusion.80), channel_id=1, source_target_pairs={{0,2},{1,3},{2,0},{3,1},{4,6},{5,7},{6,4},{7,5},{8,10},{9,11},{10,... | collective-permute-start | bytes 786440 | tf_op jit(solution)/shard_map/ppermute | solution.py:173
  136.5 7.7 %collective-permute-start.31 = (bf16[1024,128]{0,1:T(8,128)(2,1)S(1)}, bf16[1024,128]{0,1:T(8,128)(2,1)S(1)}, u32[]{:S(2)}, u32[]{:S(2)}) collective-permute-start(bf16[1024,128]{0,1:T(8,128)(2,1)S(1)} %collective-permute-done.29), channel_id=1, source_target_pairs={{0,1},{1,0},{2,3},{3,2},{4,5},{5,4},{6,7},{7,6},{8,9},{9,8},{10,11... | collective-permute-start | bytes 786440 | tf_op jit(solution)/shard_map/ppermute | solution.py:174
  138.3 7.3 %collective-permute-start.18 = (bf16[1024,128]{0,1:T(8,128)(2,1)S(1)}, bf16[1024,128]{0,1:T(8,128)(2,1)S(1)}, u32[]{:S(2)}, u32[]{:S(2)}) collective-permute-start(bf16[1024,128]{0,1:T(8,128)(2,1)S(1)} %fusion.80), channel_id=1, source_target_pairs={{0,1},{1,0},{2,3},{3,2},{4,5},{5,4},{6,7},{7,6},{8,9},{9,8},{10,11... | collective-permute-start | bytes 786440 | tf_op jit(solution)/shard_map/ppermute | solution.py:174
  143.7 3.2 %collective-permute-start.37 = (bf16[1024,128]{0,1:T(8,128)(2,1)S(1)}, bf16[1024,128]{0,1:T(8,128)(2,1)S(1)}, u32[]{:S(2)}, u32[]{:S(2)}) collective-permute-start(bf16[1024,128]{0,1:T(8,128)(2,1)S(1)} %collective-permute-done.35), channel_id=1, source_target_pairs={{0,1},{1,0},{2,3},{3,2},{4,5},{5,4},{6,7},{7,6},{8,9},{9,8},{10,11... | collective-permute-start | bytes 786440 | tf_op jit(solution)/shard_map/ppermute | solution.py:174
  143.7 1.9 %collective-permute-start.19 = (bf16[1024,128]{0,1:T(8,128)(2,1)S(1)}, bf16[1024,128]{0,1:T(8,128)(2,1)S(1)}, u32[]{:S(2)}, u32[]{:S(2)}) collective-permute-start(bf16[1024,128]{0,1:T(8,128)(2,1)S(1)} %collective-permute-done.17), channel_id=1, source_target_pairs={{0,1},{1,0},{2,3},{3,2},{4,5},{5,4},{6,7},{7,6},{8,9},{9,8},{10,11... | collective-permute-start | bytes 786440 | tf_op jit(solution)/shard_map/ppermute | solution.py:174
  149.9 3.7 %collective-permute-start.38 = (f32[1024]{0:T(1024)S(1)}, f32[1024]{0:T(1024)S(1)}, u32[]{:S(2)}, u32[]{:S(2)}) collective-permute-start(f32[1024]{0:T(1024)S(1)} %fusion.1), channel_id=1, source_target_pairs={{0,4},{4,0},{8,12},{12,8},{16,20},{20,16},{24,28},{28,24},{1,5},{5... | collective-permute-start | bytes 12296 | tf_op jit(solution)/shard_map/ppermute | solution.py:85
  153.6 3.6 %collective-permute-start.39 = (f32[1024]{0:T(1024)S(1)}, f32[1024]{0:T(1024)S(1)}, u32[]{:S(2)}, u32[]{:S(2)}) collective-permute-start(f32[1024]{0:T(1024)S(1)} %add.363), channel_id=1, source_target_pairs={{0,8},{4,12},{8,0},{12,4},{16,24},{20,28},{24,16},{28,20},{1,9},{5... | collective-permute-start | bytes 12296 | tf_op jit(solution)/shard_map/ppermute | solution.py:85
  157.2 4.5 %collective-permute-start.40 = (f32[1024]{0:T(1024)S(1)}, f32[1024]{0:T(1024)S(1)}, u32[]{:S(2)}, u32[]{:S(2)}) collective-permute-start(f32[1024]{0:T(1024)S(1)} %add.364), channel_id=1, source_target_pairs={{0,16},{4,20},{8,24},{12,28},{16,0},{20,4},{24,8},{28,12},{1,17},{... | collective-permute-start | bytes 12296 | tf_op jit(solution)/shard_map/ppermute | solution.py:85

commit v26 on v25

--- a/solution.py
+++ b/solution.py
@@ -6,7 +6,7 @@
 from jax.sharding import PartitionSpec as P
 
 CHUNKS = 4
-RELAYS = 2
+RELAYS = 4
 
 
 def _rows(a, blk, n):

time: 163 us -> 181 us (1.11)
  starting transfers between devices: 38.4 us -> 60.5 us
  waiting for transfers between devices: 93 us -> 85.3 us
  other arithmetic: 5.49 us -> 9 us
    ppermute x12 -> x24, starting transfers between devices: 20.3 us -> 43.2 us  [_zline(): cur = lax.ppermute(cur, 'src', pairs)]
    ppermute x12 -> x24, waiting for transfers between devices: 47.1 us -> 39.3 us  [_zline(): cur = lax.ppermute(cur, 'src', pairs)]
    select_n x6 -> x12, other arithmetic: 2.45 us -> 5.22 us  [_zline(): jnp.where(ia + k < na, got[-1, k], got[1, na - k])]
  transfers between devices with their start and end apart: 41 -> 53, of which waited for: 20 -> 19; matrix products, arithmetic and copies ran while one was open for 16% -> 16% of each run, Pallas kernels for 0% -> 0%
where the time goes in v26:
time: 181 us; the launch traced here: 180 us
  waiting for transfers between devices  85.3 us (47%)
  starting transfers between devices  60.5 us (33%)
  matrix products  19.6 us (11%)
  other arithmetic  9 us (5%)
  local copies, waits for them, and re-layouts  5.29 us (3%)
    ppermute x24, starting transfers between devices, _zline(): cur = lax.ppermute(cur, 'src', pairs)  43.2 us
    ppermute x24, waiting for transfers between devices, _zline(): cur = lax.ppermute(cur, 'src', pairs)  39.3 us
    ppermute x4, waiting for transfers between devices, _fast(): lax.ppermute(piece, 'vox', chip_perm(k))  19 us
    ppermute x4, waiting for transfers between devices, _fast(): lax.ppermute(halves[k].astype(jnp.bfloat16), 'vox', chip_perm(k))  15.1 us
    dot_general x16, matrix products, pblock(): lax.dot_general(scaled, rows(col, blk), (((1,), (1,)), ((), ())), preferr...  13.4 us
    ppermute x3, waiting for transfers between devices, _sum_over_src(): v = v + lax.ppermute(v, 'src', [(i, i ^ b) for i in range(n)])  11.1 us
    dot_general x4, matrix products, _fast(): jnp.dot(jnp.concatenate([w for _, w in got], axis=1), jnp.concatenate([ro...  6.21 us
    ppermute x4, starting transfers between devices, _fast(): lax.ppermute(piece, 'vox', chip_perm(k))  6.02 us
  transfers between devices with their start and end apart: 53, of which 19 were waited for; matrix products, arithmetic and copies ran while one was open for 16% of the time, Pallas kernels for 0%

profile of v26, /device:TPU:0, one launch (start us, length us, event | category | flops | bytes accessed | tf_op | source)
XLA Modules:
  0.0 180.4 jit_solution(8426088726290459678)
XLA Ops:
  0.0 2.0 %fusion.127 = (bf16[128,1024]{1,0:T(8,128)(2,1)S(1)}, bf16[128,1024]{1,0:T(8,128)(2,1)S(1)}, bf16[128,1024]{1,0:T(8,128)(2,1)S(1)}, bf16[128,1024]{1,0:T(8,128)(2,1)}) fusion(bf16[512,1024]{1,0:T(8,128)(2,1)} %param.5), kind=kLoop, calls=%fused_computation.177 | loop fusion | bytes 2097152 | tf_op jit(solution)/shard_map/slice | solution.py:150
  2.0 5.6 %collective-permute-start.39 = (bf16[128,1024]{1,0:T(8,128)(2,1)S(1)}, bf16[128,1024]{1,0:T(8,128)(2,1)}, u32[]{:S(2)}, u32[]{:S(2)}) collective-permute-start(bf16[128,1024]{1,0:T(8,128)(2,1)S(1)} %get-tuple-element.11), channel_id=1, source_target_pairs={{0,8},{4,12},{8,16},{12,20},{16,24},{20,28},{1,9},{5,13},{9,17},{1... | collective-permute-start | bytes 786440 | tf_op jit(solution)/shard_map/ppermute | solution.py:105
  8.9 4.6 %collective-permute-start.15 = (bf16[128,1024]{1,0:T(8,128)(2,1)S(1)}, bf16[128,1024]{1,0:T(8,128)(2,1)S(1)}, u32[]{:S(2)}, u32[]{:S(2)}) collective-permute-start(bf16[128,1024]{1,0:T(8,128)(2,1)S(1)} %get-tuple-element.12), channel_id=1, source_target_pairs={{0,8},{4,12},{8,16},{12,20},{16,24},{20,28},{1,9},{5,13},{9,17},{1... | collective-permute-start | bytes 786440 | tf_op jit(solution)/shard_map/ppermute | solution.py:105
  13.5 1.3 collective-permute-start.14
  14.8 5.3 %collective-permute-start.3 = (bf16[128,1024]{1,0:T(8,128)(2,1)S(1)}, bf16[128,1024]{1,0:T(8,128)(2,1)}, u32[]{:S(2)}, u32[]{:S(2)}) collective-permute-start(bf16[128,1024]{1,0:T(8,128)(2,1)S(1)} %get-tuple-element.13), channel_id=1, source_target_pairs={{0,8},{4,12},{8,16},{12,20},{16,24},{20,28},{1,9},{5,13},{9,17},{1... | collective-permute-start | bytes 786440 | tf_op jit(solution)/shard_map/ppermute | solution.py:105
  20.1 1.3 collective-permute-start.2
  21.4 5.2 %collective-permute-start.27 = (bf16[128,1024]{1,0:T(8,128)(2,1)}, bf16[128,1024]{1,0:T(8,128)(2,1)}, u32[]{:S(2)}, u32[]{:S(2)}) collective-permute-start(bf16[128,1024]{1,0:T(8,128)(2,1)} %get-tuple-element.14), channel_id=1, source_target_pairs={{0,8},{4,12},{8,16},{12,20},{16,24},{20,28},{1,9},{5,13},{9,17},{1... | collective-permute-start | bytes 786440 | tf_op jit(solution)/shard_map/ppermute | solution.py:105
  26.6 1.9 %copy.5 = f32[512,1024]{0,1:T(8,128)S(1)} copy(f32[512,1024]{1,0:T(8,128)} %param.7) | data formatting | bytes 4194304 | tf_op args[3]
  28.6 1.3 collective-permute-start.26
  29.9 1.4 collective-permute-start.40
  31.3 1.3 collective-permute-start.42
  32.6 1.4 collective-permute-start.4
  34.0 1.3 collective-permute-start.6
  37.2 5.5 %collective-permute-done.42 = bf16[128,1024]{1,0:T(8,128)(2,1)} collective-permute-done((bf16[128,1024]{1,0:T(8,128)(2,1)}, bf16[128,1024]{1,0:T(8,128)(2,1)}, u32[]{:S(2)}, u32[]{:S(2)}) %collective-permute-start.42) | collective-permute-done | bytes 262176 | tf_op jit(solution)/shard_map/ppermute | solution.py:105
  42.8 1.3 collective-permute-start.18
  45.1 1.6 collective-permute-start
  47.3 2.1 %collective-permute-done.6 = bf16[128,1024]{1,0:T(8,128)(2,1)} collective-permute-done((bf16[128,1024]{1,0:T(8,128)(2,1)}, bf16[128,1024]{1,0:T(8,128)(2,1)}, u32[]{:S(2)}, u32[]{:S(2)}) %collective-permute-start.6) | collective-permute-done | bytes 262176 | tf_op jit(solution)/shard_map/ppermute | solution.py:105
  51.7 1.6 collective-permute-start.1
  53.3 3.9 %collective-permute-done.18 = bf16[128,1024]{1,0:T(8,128)(2,1)S(1)} collective-permute-done((bf16[128,1024]{1,0:T(8,128)(2,1)}, bf16[128,1024]{1,0:T(8,128)(2,1)S(1)}, u32[]{:S(2)}, u32[]{:S(2)}) %collective-permute-start.18) | collective-permute-done | bytes 262176 | tf_op jit(solution)/shard_map/ppermute | solution.py:105
  58.6 7.3 %collective-permute-done.30 = bf16[128,1024]{1,0:T(8,128)(2,1)S(1)} collective-permute-done((bf16[128,1024]{1,0:T(8,128)(2,1)}, bf16[128,1024]{1,0:T(8,128)(2,1)S(1)}, u32[]{:S(2)}, u32[]{:S(2)}) %collective-permute-start.30) | collective-permute-done | bytes 262176 | tf_op jit(solution)/shard_map/ppermute | solution.py:105
  65.9 1.3 collective-permute-start.7
  68.9 6.6 %collective-permute-done.7 = bf16[128,1024]{1,0:T(8,128)(2,1)S(1)} collective-permute-done((bf16[128,1024]{1,0:T(8,128)(2,1)}, bf16[128,1024]{1,0:T(8,128)(2,1)S(1)}, u32[]{:S(2)}, u32[]{:S(2)}) %collective-permute-start.7) | collective-permute-done | bytes 262176 | tf_op jit(solution)/shard_map/ppermute | solution.py:105
  75.5 1.3 collective-permute-start.31
  78.7 7.2 %collective-permute-done.31 = bf16[128,1024]{1,0:T(8,128)(2,1)S(1)} collective-permute-done((bf16[128,1024]{1,0:T(8,128)(2,1)S(1)}, bf16[128,1024]{1,0:T(8,128)(2,1)S(1)}, u32[]{:S(2)}, u32[]{:S(2)}) %collective-permute-start.31) | collective-permute-done | bytes 262176 | tf_op jit(solution)/shard_map/ppermute | solution.py:105
  85.9 1.3 collective-permute-start.19
  88.4 1.6 collective-permute-start.43
  90.1 4.0 %collective-permute-done.19 = bf16[128,1024]{1,0:T(8,128)(2,1)S(1)} collective-permute-done((bf16[128,1024]{1,0:T(8,128)(2,1)S(1)}, bf16[128,1024]{1,0:T(8,128)(2,1)S(1)}, u32[]{:S(2)}, u32[]{:S(2)}) %collective-permute-start.19) | collective-permute-done | bytes 262176 | tf_op jit(solution)/shard_map/ppermute | solution.py:105
  95.4 2.5 %collective-permute-done.43 = bf16[128,1024]{1,0:T(8,128)(2,1)S(1)} collective-permute-done((bf16[128,1024]{1,0:T(8,128)(2,1)}, bf16[128,1024]{1,0:T(8,128)(2,1)S(1)}, u32[]{:S(2)}, u32[]{:S(2)}) %collective-permute-start.43) | collective-permute-done | bytes 262176 | tf_op jit(solution)/shard_map/ppermute | solution.py:105
  111.7 1.6 collective-permute-start.34
  114.8 6.1 %collective-permute-done.34 = bf16[1024,128]{0,1:T(8,128)(2,1)S(1)} collective-permute-done((bf16[1024,128]{0,1:T(8,128)(2,1)S(1)}, bf16[1024,128]{0,1:T(8,128)(2,1)S(1)}, u32[]{:S(2)}, u32[]{:S(2)}) %collective-permute-start.34) | collective-permute-done | bytes 262176 | tf_op jit(solution)/shard_map/ppermute | solution.py:165
  120.9 1.5 collective-permute-start.22
  123.9 2.7 %collective-permute-done.10 = bf16[1024,128]{0,1:T(8,128)(2,1)S(1)} collective-permute-done((bf16[1024,128]{0,1:T(8,128)(2,1)S(1)}, bf16[1024,128]{0,1:T(8,128)(2,1)S(1)}, u32[]{:S(2)}, u32[]{:S(2)}) %collective-permute-start.10) | collective-permute-done | bytes 262176 | tf_op jit(solution)/shard_map/ppermute | solution.py:165
  127.4 1.6 collective-permute-start.35
  128.9 3.2 %collective-permute-done.22 = bf16[1024,128]{0,1:T(8,128)(2,1)S(1)} collective-permute-done((bf16[1024,128]{0,1:T(8,128)(2,1)S(1)}, bf16[1024,128]{0,1:T(8,128)(2,1)S(1)}, u32[]{:S(2)}, u32[]{:S(2)}) %collective-permute-start.22) | collective-permute-done | bytes 262176 | tf_op jit(solution)/shard_map/ppermute | solution.py:165
  132.1 1.5 collective-permute-start.11
  134.6 3.2 %collective-permute-done.46 = bf16[1024,128]{0,1:T(8,128)(2,1)S(1)} collective-permute-done((bf16[1024,128]{0,1:T(8,128)(2,1)S(1)}, bf16[1024,128]{0,1:T(8,128)(2,1)S(1)}, u32[]{:S(2)}, u32[]{:S(2)}) %collective-permute-start.46) | collective-permute-done | bytes 262176 | tf_op jit(solution)/shard_map/ppermute | solution.py:165
  137.7 1.5 collective-permute-start.23
  139.2 9.7 %collective-permute-done.11 = bf16[1024,128]{0,1:T(8,128)(2,1)S(1)} collective-permute-done((bf16[1024,128]{0,1:T(8,128)(2,1)S(1)}, bf16[1024,128]{0,1:T(8,128)(2,1)S(1)}, u32[]{:S(2)}, u32[]{:S(2)}) %collective-permute-start.11) | collective-permute-done | bytes 262176 | tf_op jit(solution)/shard_map/ppermute | solution.py:173
  149.8 4.2 %collective-permute-done.23 = bf16[1024,128]{0,1:T(8,128)(2,1)S(1)} collective-permute-done((bf16[1024,128]{0,1:T(8,128)(2,1)S(1)}, bf16[1024,128]{0,1:T(8,128)(2,1)S(1)}, u32[]{:S(2)}, u32[]{:S(2)}) %collective-permute-start.23) | collective-permute-done | bytes 262176 | tf_op jit(solution)/shard_map/ppermute | solution.py:173
  154.1 1.5 collective-permute-start.47
  155.8 1.5 fusion.10
  157.7 5.1 %collective-permute-done.47 = bf16[1024,128]{0,1:T(8,128)(2,1)S(1)} collective-permute-done((bf16[1024,128]{0,1:T(8,128)(2,1)S(1)}, bf16[1024,128]{0,1:T(8,128)(2,1)S(1)}, u32[]{:S(2)}, u32[]{:S(2)}) %collective-permute-start.47) | collective-permute-done | bytes 262176 | tf_op jit(solution)/shard_map/ppermute | solution.py:173
  163.3 1.3 fusion.25
  164.6 1.3 fusion.40
  165.9 2.1 %fusion.1 = f32[1024]{0:T(1024)S(1)} fusion(f32[1024,1024]{1,0:T(8,128)S(1)} %fusion.40, f32[1024,1024]{1,0:T(8,128)S(1)} %fusion.10, f32[1024,1024]{1,0:T(8,128)S(1)} %fusion.25, bf16[512,1024]{1,0:T(8,128)(2,1)S(1)} %collective-permute-done, bf16[512,1024]{1,0:T(8,128)(2,1)S(1)} %copy-done, bf16[1024,128]{0,1:T(8,128)(2,1)S(1)} %collective-permute-done.49, ...), kind=kOutput, calls=%fused_computation.3 | convolution fusion | flops 1091566592 | bytes 16781312 | tf_op jit(solution)/shard_map/dot_general | solution.py:176
  168.1 3.6 %collective-permute-done.50 = f32[1024]{0:T(1024)S(1)} collective-permute-done((f32[1024]{0:T(1024)S(1)}, f32[1024]{0:T(1024)S(1)}, u32[]{:S(2)}, u32[]{:S(2)}) %collective-permute-start.50) | collective-permute-done | bytes 4128 | tf_op jit(solution)/shard_map/ppermute | solution.py:85
  172.3 3.0 %collective-permute-done.51 = f32[1024]{0:T(1024)S(1)} collective-permute-done((f32[1024]{0:T(1024)S(1)}, f32[1024]{0:T(1024)S(1)}, u32[]{:S(2)}, u32[]{:S(2)}) %collective-permute-start.51) | collective-permute-done | bytes 4128 | tf_op jit(solution)/shard_map/ppermute | solution.py:85
  175.3 4.5 %collective-permute-done.52 = f32[1024]{0:T(1024)S(1)} collective-permute-done((f32[1024]{0:T(1024)S(1)}, f32[1024]{0:T(1024)S(1)}, u32[]{:S(2)}, u32[]{:S(2)}) %collective-permute-start.52) | collective-permute-done | bytes 4128 | tf_op jit(solution)/shard_map/ppermute | solution.py:85
  (125 shorter events, 36.2 us)
Async XLA Ops:
  2.0 18.1 %collective-permute-start.39 = (bf16[128,1024]{1,0:T(8,128)(2,1)S(1)}, bf16[128,1024]{1,0:T(8,128)(2,1)}, u32[]{:S(2)}, u32[]{:S(2)}) collective-permute-start(bf16[128,1024]{1,0:T(8,128)(2,1)S(1)} %get-tuple-element.11), channel_id=1, source_target_pairs={{0,8},{4,12},{8,16},{12,20},{16,24},{20,28},{1,9},{5,13},{9,17},{1... | collective-permute-start | bytes 786440 | tf_op jit(solution)/shard_map/ppermute | solution.py:105
  7.6 13.7 %collective-permute-start.38 = (bf16[128,1024]{1,0:T(8,128)(2,1)S(1)}, bf16[128,1024]{1,0:T(8,128)(2,1)}, u32[]{:S(2)}, u32[]{:S(2)}) collective-permute-start(bf16[128,1024]{1,0:T(8,128)(2,1)S(1)} %get-tuple-element.11), channel_id=1, source_target_pairs={{8,0},{12,4},{16,8},{20,12},{24,16},{28,20},{9,1},{13,5},{17,9},{2... | collective-permute-start | bytes 786440 | tf_op jit(solution)/shard_map/ppermute | solution.py:105
  8.9 19.6 %collective-permute-start.15 = (bf16[128,1024]{1,0:T(8,128)(2,1)S(1)}, bf16[128,1024]{1,0:T(8,128)(2,1)S(1)}, u32[]{:S(2)}, u32[]{:S(2)}) collective-permute-start(bf16[128,1024]{1,0:T(8,128)(2,1)S(1)} %get-tuple-element.12), channel_id=1, source_target_pairs={{0,8},{4,12},{8,16},{12,20},{16,24},{20,28},{1,9},{5,13},{9,17},{1... | collective-permute-start | bytes 786440 | tf_op jit(solution)/shard_map/ppermute | solution.py:105
  13.5 16.4 %collective-permute-start.14 = (bf16[128,1024]{1,0:T(8,128)(2,1)S(1)}, bf16[128,1024]{1,0:T(8,128)(2,1)S(1)}, u32[]{:S(2)}, u32[]{:S(2)}) collective-permute-start(bf16[128,1024]{1,0:T(8,128)(2,1)S(1)} %get-tuple-element.12), channel_id=1, source_target_pairs={{8,0},{12,4},{16,8},{20,12},{24,16},{28,20},{9,1},{13,5},{17,9},{2... | collective-permute-start | bytes 786440 | tf_op jit(solution)/shard_map/ppermute | solution.py:105
  14.8 16.5 %collective-permute-start.3 = (bf16[128,1024]{1,0:T(8,128)(2,1)S(1)}, bf16[128,1024]{1,0:T(8,128)(2,1)}, u32[]{:S(2)}, u32[]{:S(2)}) collective-permute-start(bf16[128,1024]{1,0:T(8,128)(2,1)S(1)} %get-tuple-element.13), channel_id=1, source_target_pairs={{0,8},{4,12},{8,16},{12,20},{16,24},{20,28},{1,9},{5,13},{9,17},{1... | collective-permute-start | bytes 786440 | tf_op jit(solution)/shard_map/ppermute | solution.py:105
  20.1 12.5 %collective-permute-start.2 = (bf16[128,1024]{1,0:T(8,128)(2,1)S(1)}, bf16[128,1024]{1,0:T(8,128)(2,1)}, u32[]{:S(2)}, u32[]{:S(2)}) collective-permute-start(bf16[128,1024]{1,0:T(8,128)(2,1)S(1)} %get-tuple-element.13), channel_id=1, source_target_pairs={{8,0},{12,4},{16,8},{20,12},{24,16},{28,20},{9,1},{13,5},{17,9},{2... | collective-permute-start | bytes 786440 | tf_op jit(solution)/shard_map/ppermute | solution.py:105
  21.4 12.6 %collective-permute-start.27 = (bf16[128,1024]{1,0:T(8,128)(2,1)}, bf16[128,1024]{1,0:T(8,128)(2,1)}, u32[]{:S(2)}, u32[]{:S(2)}) collective-permute-start(bf16[128,1024]{1,0:T(8,128)(2,1)} %get-tuple-element.14), channel_id=1, source_target_pairs={{0,8},{4,12},{8,16},{12,20},{16,24},{20,28},{1,9},{5,13},{9,17},{1... | collective-permute-start | bytes 786440 | tf_op jit(solution)/shard_map/ppermute | solution.py:105
  28.6 16.5 %collective-permute-start.26 = (bf16[128,1024]{1,0:T(8,128)(2,1)}, bf16[128,1024]{1,0:T(8,128)(2,1)}, u32[]{:S(2)}, u32[]{:S(2)}) collective-permute-start(bf16[128,1024]{1,0:T(8,128)(2,1)} %get-tuple-element.14), channel_id=1, source_target_pairs={{8,0},{12,4},{16,8},{20,12},{24,16},{28,20},{9,1},{13,5},{17,9},{2... | collective-permute-start | bytes 786440 | tf_op jit(solution)/shard_map/ppermute | solution.py:105
  29.9 6.7 %collective-permute-start.40 = (bf16[128,1024]{1,0:T(8,128)(2,1)}, bf16[128,1024]{1,0:T(8,128)(2,1)}, u32[]{:S(2)}, u32[]{:S(2)}) collective-permute-start(bf16[128,1024]{1,0:T(8,128)(2,1)} %collective-permute-done.39), channel_id=1, source_target_pairs={{8,16},{12,20},{16,24},{20,28},{9,17},{13,21},{17,25},{21,29},{10,... | collective-permute-start | bytes 786440 | tf_op jit(solution)/shard_map/ppermute | solution.py:105
  31.3 11.5 %collective-permute-start.42 = (bf16[128,1024]{1,0:T(8,128)(2,1)}, bf16[128,1024]{1,0:T(8,128)(2,1)}, u32[]{:S(2)}, u32[]{:S(2)}) collective-permute-start(bf16[128,1024]{1,0:T(8,128)(2,1)} %collective-permute-done.38), channel_id=1, source_target_pairs={{8,0},{12,4},{16,8},{20,12},{9,1},{13,5},{17,9},{21,13},{10,2},{14... | collective-permute-start | bytes 786440 | tf_op jit(solution)/shard_map/ppermute | solution.py:105
  32.6 14.1 %collective-permute-start.4 = (bf16[128,1024]{1,0:T(8,128)(2,1)}, bf16[128,1024]{1,0:T(8,128)(2,1)}, u32[]{:S(2)}, u32[]{:S(2)}) collective-permute-start(bf16[128,1024]{1,0:T(8,128)(2,1)} %collective-permute-done.3), channel_id=1, source_target_pairs={{8,16},{12,20},{16,24},{20,28},{9,17},{13,21},{17,25},{21,29},{10,... | collective-permute-start | bytes 786440 | tf_op jit(solution)/shard_map/ppermute | solution.py:105
  34.0 15.5 %collective-permute-start.6 = (bf16[128,1024]{1,0:T(8,128)(2,1)}, bf16[128,1024]{1,0:T(8,128)(2,1)}, u32[]{:S(2)}, u32[]{:S(2)}) collective-permute-start(bf16[128,1024]{1,0:T(8,128)(2,1)} %collective-permute-done.2), channel_id=1, source_target_pairs={{8,0},{12,4},{16,8},{20,12},{9,1},{13,5},{17,9},{21,13},{10,2},{14... | collective-permute-start | bytes 786440 | tf_op jit(solution)/shard_map/ppermute | solution.py:105
  36.6 15.2 %collective-permute-start.16 = (bf16[128,1024]{1,0:T(8,128)(2,1)}, bf16[128,1024]{1,0:T(8,128)(2,1)S(1)}, u32[]{:S(2)}, u32[]{:S(2)}) collective-permute-start(bf16[128,1024]{1,0:T(8,128)(2,1)} %copy-done.5), channel_id=1, source_target_pairs={{8,16},{12,20},{16,24},{20,28},{9,17},{13,21},{17,25},{21,29},{10,... | collective-permute-start | bytes 786440 | tf_op jit(solution)/shard_map/ppermute | solution.py:105
  42.8 14.4 %collective-permute-start.18 = (bf16[128,1024]{1,0:T(8,128)(2,1)}, bf16[128,1024]{1,0:T(8,128)(2,1)S(1)}, u32[]{:S(2)}, u32[]{:S(2)}) collective-permute-start(bf16[128,1024]{1,0:T(8,128)(2,1)} %copy-done.7), channel_id=1, source_target_pairs={{8,0},{12,4},{16,8},{20,12},{9,1},{13,5},{17,9},{21,13},{10,2},{14... | collective-permute-start | bytes 786440 | tf_op jit(solution)/shard_map/ppermute | solution.py:105
  45.1 53.1 %collective-permute-start = (bf16[512,1024]{1,0:T(8,128)(2,1)}, bf16[512,1024]{1,0:T(8,128)(2,1)S(1)}, u32[]{:S(2)}, u32[]{:S(2)}) collective-permute-start(bf16[512,1024]{1,0:T(8,128)(2,1)} %param.4), channel_id=1, source_target_pairs={{0,4},{4,0},{8,12},{12,8},{16,20},{20,16},{24,28},{28,24},{1,5},{5... | collective-permute-start | bytes 3145736 | tf_op jit(solution)/shard_map/ppermute | solution.py:140
  46.7 11.3 %collective-permute-start.28 = (bf16[128,1024]{1,0:T(8,128)(2,1)}, bf16[128,1024]{1,0:T(8,128)(2,1)S(1)}, u32[]{:S(2)}, u32[]{:S(2)}) collective-permute-start(bf16[128,1024]{1,0:T(8,128)(2,1)} %collective-permute-done.27), channel_id=1, source_target_pairs={{8,16},{12,20},{16,24},{20,28},{9,17},{13,21},{17,25},{21,29},{10,... | collective-permute-start | bytes 786440 | tf_op jit(solution)/shard_map/ppermute | solution.py:105
  49.4 16.5 %collective-permute-start.30 = (bf16[128,1024]{1,0:T(8,128)(2,1)}, bf16[128,1024]{1,0:T(8,128)(2,1)S(1)}, u32[]{:S(2)}, u32[]{:S(2)}) collective-permute-start(bf16[128,1024]{1,0:T(8,128)(2,1)} %collective-permute-done.26), channel_id=1, source_target_pairs={{8,0},{12,4},{16,8},{20,12},{9,1},{13,5},{17,9},{21,13},{10,2},{14... | collective-permute-start | bytes 786440 | tf_op jit(solution)/shard_map/ppermute | solution.py:105
  51.7 62.4 %collective-permute-start.1 = (f32[512,512]{0,1:T(8,128)}, f32[512,512]{0,1:T(8,128)S(1)}, u32[]{:S(2)}, u32[]{:S(2)}) collective-permute-start(f32[512,512]{0,1:T(8,128)} %get-tuple-element.5), channel_id=1, source_target_pairs={{0,4},{4,0},{8,12},{12,8},{16,20},{20,16},{24,28},{28,24},{1,5},{5... | collective-permute-start | bytes 3145736 | tf_op jit(solution)/shard_map/ppermute | solution.py:148
  57.2 10.0 %collective-permute-start.5 = (bf16[128,1024]{1,0:T(8,128)(2,1)}, bf16[128,1024]{1,0:T(8,128)(2,1)S(1)}, u32[]{:S(2)}, u32[]{:S(2)}) collective-permute-start(bf16[128,1024]{1,0:T(8,128)(2,1)} %collective-permute-done.4), channel_id=1, source_target_pairs={{16,24},{20,28},{17,25},{21,29},{18,26},{22,30},{19,27},{23,31}} | collective-permute-start | bytes 786440 | tf_op jit(solution)/shard_map/ppermute | solution.py:105
  57.9 36.5 %collective-permute-start.41 = (bf16[128,1024]{1,0:T(8,128)(2,1)}, bf16[128,1024]{1,0:T(8,128)(2,1)S(1)}, u32[]{:S(2)}, u32[]{:S(2)}) collective-permute-start(bf16[128,1024]{1,0:T(8,128)(2,1)} %collective-permute-done.40), channel_id=1, source_target_pairs={{16,24},{20,28},{17,25},{21,29},{18,26},{22,30},{19,27},{23,31}} | collective-permute-start | bytes 786440 | tf_op jit(solution)/shard_map/ppermute | solution.py:105
  65.9 9.6 %collective-permute-start.7 = (bf16[128,1024]{1,0:T(8,128)(2,1)}, bf16[128,1024]{1,0:T(8,128)(2,1)S(1)}, u32[]{:S(2)}, u32[]{:S(2)}) collective-permute-start(bf16[128,1024]{1,0:T(8,128)(2,1)} %collective-permute-done.6), channel_id=1, source_target_pairs={{8,0},{12,4},{9,1},{13,5},{10,2},{14,6},{11,3},{15,7}} | collective-permute-start | bytes 786440 | tf_op jit(solution)/shard_map/ppermute | solution.py:105
  67.2 9.7 %collective-permute-start.29 = (bf16[128,1024]{1,0:T(8,128)(2,1)S(1)}, bf16[128,1024]{1,0:T(8,128)(2,1)S(1)}, u32[]{:S(2)}, u32[]{:S(2)}) collective-permute-start(bf16[128,1024]{1,0:T(8,128)(2,1)S(1)} %collective-permute-done.28), channel_id=1, source_target_pairs={{16,24},{20,28},{17,25},{21,29},{18,26},{22,30},{19,27},{23,31}} | collective-permute-start | bytes 786440 | tf_op jit(solution)/shard_map/ppermute | solution.py:105
  75.5 10.3 %collective-permute-start.31 = (bf16[128,1024]{1,0:T(8,128)(2,1)S(1)}, bf16[128,1024]{1,0:T(8,128)(2,1)S(1)}, u32[]{:S(2)}, u32[]{:S(2)}) collective-permute-start(bf16[128,1024]{1,0:T(8,128)(2,1)S(1)} %collective-permute-done.30), channel_id=1, source_target_pairs={{8,0},{12,4},{9,1},{13,5},{10,2},{14,6},{11,3},{15,7}} | collective-permute-start | bytes 786440 | tf_op jit(solution)/shard_map/ppermute | solution.py:105
  77.0 11.4 %collective-permute-start.17 = (bf16[128,1024]{1,0:T(8,128)(2,1)S(1)}, bf16[128,1024]{1,0:T(8,128)(2,1)S(1)}, u32[]{:S(2)}, u32[]{:S(2)}) collective-permute-start(bf16[128,1024]{1,0:T(8,128)(2,1)S(1)} %collective-permute-done.16), channel_id=1, source_target_pairs={{16,24},{20,28},{17,25},{21,29},{18,26},{22,30},{19,27},{23,31}} | collective-permute-start | bytes 786440 | tf_op jit(solution)/shard_map/ppermute | solution.py:105
  85.9 8.3 %collective-permute-start.19 = (bf16[128,1024]{1,0:T(8,128)(2,1)S(1)}, bf16[128,1024]{1,0:T(8,128)(2,1)S(1)}, u32[]{:S(2)}, u32[]{:S(2)}) collective-permute-start(bf16[128,1024]{1,0:T(8,128)(2,1)S(1)} %collective-permute-done.18), channel_id=1, source_target_pairs={{8,0},{12,4},{9,1},{13,5},{10,2},{14,6},{11,3},{15,7}} | collective-permute-start | bytes 786440 | tf_op jit(solution)/shard_map/ppermute | solution.py:105
  88.4 9.6 %collective-permute-start.43 = (bf16[128,1024]{1,0:T(8,128)(2,1)}, bf16[128,1024]{1,0:T(8,128)(2,1)S(1)}, u32[]{:S(2)}, u32[]{:S(2)}) collective-permute-start(bf16[128,1024]{1,0:T(8,128)(2,1)} %collective-permute-done.42), channel_id=1, source_target_pairs={{8,0},{12,4},{9,1},{13,5},{10,2},{14,6},{11,3},{15,7}} | collective-permute-start | bytes 786440 | tf_op jit(solution)/shard_map/ppermute | solution.py:105
  104.9 18.4 %collective-permute-start.8 = (f32[1024,128]{0,1:T(8,128)S(1)}, f32[1024,128]{0,1:T(8,128)S(1)}, u32[]{:S(2)}, u32[]{:S(2)}) collective-permute-start(f32[1024,128]{0,1:T(8,128)S(1)} %fusion.104), channel_id=1, source_target_pairs={{0,1},{1,0},{2,3},{3,2},{4,5},{5,4},{6,7},{7,6},{8,9},{9,8},{10,11... | collective-permute-start | bytes 1572872 | tf_op jit(solution)/shard_map/ppermute | solution.py:162
  105.0 22.4 %collective-permute-start.20 = (f32[1024,128]{0,1:T(8,128)S(1)}, f32[1024,128]{0,1:T(8,128)S(1)}, u32[]{:S(2)}, u32[]{:S(2)}) collective-permute-start(f32[1024,128]{0,1:T(8,128)S(1)} %fusion.98), channel_id=1, source_target_pairs={{0,1},{1,0},{2,3},{3,2},{4,5},{5,4},{6,7},{7,6},{8,9},{9,8},{10,11... | collective-permute-start | bytes 1572872 | tf_op jit(solution)/shard_map/ppermute | solution.py:162
  105.5 3.8 %collective-permute-start.21 = (f32[1024,128]{0,1:T(8,128)S(1)}, f32[1024,128]{0,1:T(8,128)S(1)}, u32[]{:S(2)}, u32[]{:S(2)}) collective-permute-start(f32[1024,128]{0,1:T(8,128)S(1)} %fusion.95), channel_id=1, source_target_pairs={{0,1},{1,0},{2,3},{3,2},{4,5},{5,4},{6,7},{7,6},{8,9},{9,8},{10,11... | collective-permute-start | bytes 1572872 | tf_op jit(solution)/shard_map/ppermute | solution.py:162
  110.6 3.6 %collective-permute-start.32 = (f32[1024,128]{0,1:T(8,128)S(1)}, f32[1024,128]{0,1:T(8,128)S(1)}, u32[]{:S(2)}, u32[]{:S(2)}) collective-permute-start(f32[1024,128]{0,1:T(8,128)S(1)} %fusion.92), channel_id=1, source_target_pairs={{0,1},{1,0},{2,3},{3,2},{4,5},{5,4},{6,7},{7,6},{8,9},{9,8},{10,11... | collective-permute-start | bytes 1572872 | tf_op jit(solution)/shard_map/ppermute | solution.py:162
  111.7 9.2 %collective-permute-start.34 = (bf16[1024,128]{0,1:T(8,128)(2,1)S(1)}, bf16[1024,128]{0,1:T(8,128)(2,1)S(1)}, u32[]{:S(2)}, u32[]{:S(2)}) collective-permute-start(bf16[1024,128]{0,1:T(8,128)(2,1)S(1)} %fusion.8), channel_id=1, source_target_pairs={{0,2},{1,3},{2,0},{3,1},{4,6},{5,7},{6,4},{7,5},{8,10},{9,11},{10,... | collective-permute-start | bytes 786440 | tf_op jit(solution)/shard_map/ppermute | solution.py:165
  114.1 20.4 %collective-permute-start.44 = (f32[1024,128]{0,1:T(8,128)S(1)}, f32[1024,128]{0,1:T(8,128)S(1)}, u32[]{:S(2)}, u32[]{:S(2)}) collective-permute-start(f32[1024,128]{0,1:T(8,128)S(1)} %fusion.86), channel_id=1, source_target_pairs={{0,1},{1,0},{2,3},{3,2},{4,5},{5,4},{6,7},{7,6},{8,9},{9,8},{10,11... | collective-permute-start | bytes 1572872 | tf_op jit(solution)/shard_map/ppermute | solution.py:162
  114.3 12.3 %collective-permute-start.10 = (bf16[1024,128]{0,1:T(8,128)(2,1)S(1)}, bf16[1024,128]{0,1:T(8,128)(2,1)S(1)}, u32[]{:S(2)}, u32[]{:S(2)}) collective-permute-start(bf16[1024,128]{0,1:T(8,128)(2,1)S(1)} %fusion.6), channel_id=1, source_target_pairs={{0,2},{1,3},{2,0},{3,1},{4,6},{5,7},{6,4},{7,5},{8,10},{9,11},{10,... | collective-permute-start | bytes 786440 | tf_op jit(solution)/shard_map/ppermute | solution.py:165
  120.9 11.2 %collective-permute-start.22 = (bf16[1024,128]{0,1:T(8,128)(2,1)S(1)}, bf16[1024,128]{0,1:T(8,128)(2,1)S(1)}, u32[]{:S(2)}, u32[]{:S(2)}) collective-permute-start(bf16[1024,128]{0,1:T(8,128)(2,1)S(1)} %fusion.7), channel_id=1, source_target_pairs={{0,2},{1,3},{2,0},{3,1},{4,6},{5,7},{6,4},{7,5},{8,10},{9,11},{10,... | collective-permute-start | bytes 786440 | tf_op jit(solution)/shard_map/ppermute | solution.py:165
  123.3 14.5 %collective-permute-start.46 = (bf16[1024,128]{0,1:T(8,128)(2,1)S(1)}, bf16[1024,128]{0,1:T(8,128)(2,1)S(1)}, u32[]{:S(2)}, u32[]{:S(2)}) collective-permute-start(bf16[1024,128]{0,1:T(8,128)(2,1)S(1)} %fusion.9), channel_id=1, source_target_pairs={{0,2},{1,3},{2,0},{3,1},{4,6},{5,7},{6,4},{7,5},{8,10},{9,11},{10,... | collective-permute-start | bytes 786440 | tf_op jit(solution)/shard_map/ppermute | solution.py:165
  126.5 38.1 %collective-permute-start.36 = (bf16[1024,128]{0,1:T(8,128)(2,1)S(1)}, bf16[1024,128]{0,1:T(8,128)(2,1)S(1)}, u32[]{:S(2)}, u32[]{:S(2)}) collective-permute-start(bf16[1024,128]{0,1:T(8,128)(2,1)S(1)} %fusion.74), channel_id=1, source_target_pairs={{0,1},{1,0},{2,3},{3,2},{4,5},{5,4},{6,7},{7,6},{8,9},{9,8},{10,11... | collective-permute-start | bytes 786440 | tf_op jit(solution)/shard_map/ppermute | solution.py:174
  127.4 29.9 %collective-permute-start.35 = (bf16[1024,128]{0,1:T(8,128)(2,1)S(1)}, bf16[1024,128]{0,1:T(8,128)(2,1)S(1)}, u32[]{:S(2)}, u32[]{:S(2)}) collective-permute-start(bf16[1024,128]{0,1:T(8,128)(2,1)S(1)} %fusion.74), channel_id=1, source_target_pairs={{0,2},{1,3},{2,0},{3,1},{4,6},{5,7},{6,4},{7,5},{8,10},{9,11},{10,... | collective-permute-start | bytes 786440 | tf_op jit(solution)/shard_map/ppermute | solution.py:173
  132.1 16.9 %collective-permute-start.11 = (bf16[1024,128]{0,1:T(8,128)(2,1)S(1)}, bf16[1024,128]{0,1:T(8,128)(2,1)S(1)}, u32[]{:S(2)}, u32[]{:S(2)}) collective-permute-start(bf16[1024,128]{0,1:T(8,128)(2,1)S(1)} %fusion.77), channel_id=1, source_target_pairs={{0,2},{1,3},{2,0},{3,1},{4,6},{5,7},{6,4},{7,5},{8,10},{9,11},{10,... | collective-permute-start | bytes 786440 | tf_op jit(solution)/shard_map/ppermute | solution.py:173
  134.5 19.6 %collective-permute-start.12 = (bf16[1024,128]{0,1:T(8,128)(2,1)S(1)}, bf16[1024,128]{0,1:T(8,128)(2,1)S(1)}, u32[]{:S(2)}, u32[]{:S(2)}) collective-permute-start(bf16[1024,128]{0,1:T(8,128)(2,1)S(1)} %fusion.77), channel_id=1, source_target_pairs={{0,1},{1,0},{2,3},{3,2},{4,5},{5,4},{6,7},{7,6},{8,9},{9,8},{10,11... | collective-permute-start | bytes 786440 | tf_op jit(solution)/shard_map/ppermute | solution.py:174
  137.7 16.3 %collective-permute-start.23 = (bf16[1024,128]{0,1:T(8,128)(2,1)S(1)}, bf16[1024,128]{0,1:T(8,128)(2,1)S(1)}, u32[]{:S(2)}, u32[]{:S(2)}) collective-permute-start(bf16[1024,128]{0,1:T(8,128)(2,1)S(1)} %fusion.80), channel_id=1, source_target_pairs={{0,2},{1,3},{2,0},{3,1},{4,6},{5,7},{6,4},{7,5},{8,10},{9,11},{10,... | collective-permute-start | bytes 786440 | tf_op jit(solution)/shard_map/ppermute | solution.py:173
  149.0 6.6 %collective-permute-start.13 = (bf16[1024,128]{0,1:T(8,128)(2,1)S(1)}, bf16[1024,128]{0,1:T(8,128)(2,1)S(1)}, u32[]{:S(2)}, u32[]{:S(2)}) collective-permute-start(bf16[1024,128]{0,1:T(8,128)(2,1)S(1)} %collective-permute-done.11), channel_id=1, source_target_pairs={{0,1},{1,0},{2,3},{3,2},{4,5},{5,4},{6,7},{7,6},{8,9},{9,8},{10,11... | collective-permute-start | bytes 786440 | tf_op jit(solution)/shard_map/ppermute | solution.py:174
  154.0 8.7 %collective-permute-start.24 = (bf16[1024,128]{0,1:T(8,128)(2,1)S(1)}, bf16[1024,128]{0,1:T(8,128)(2,1)S(1)}, u32[]{:S(2)}, u32[]{:S(2)}) collective-permute-start(bf16[1024,128]{0,1:T(8,128)(2,1)S(1)} %fusion.80), channel_id=1, source_target_pairs={{0,1},{1,0},{2,3},{3,2},{4,5},{5,4},{6,7},{7,6},{8,9},{9,8},{10,11... | collective-permute-start | bytes 786440 | tf_op jit(solution)/shard_map/ppermute | solution.py:174
  154.1 8.7 %collective-permute-start.47 = (bf16[1024,128]{0,1:T(8,128)(2,1)S(1)}, bf16[1024,128]{0,1:T(8,128)(2,1)S(1)}, u32[]{:S(2)}, u32[]{:S(2)}) collective-permute-start(bf16[1024,128]{0,1:T(8,128)(2,1)S(1)} %fusion.82), channel_id=1, source_target_pairs={{0,2},{1,3},{2,0},{3,1},{4,6},{5,7},{6,4},{7,5},{8,10},{9,11},{10,... | collective-permute-start | bytes 786440 | tf_op jit(solution)/shard_map/ppermute | solution.py:173
  155.5 7.7 %collective-permute-start.25 = (bf16[1024,128]{0,1:T(8,128)(2,1)S(1)}, bf16[1024,128]{0,1:T(8,128)(2,1)S(1)}, u32[]{:S(2)}, u32[]{:S(2)}) collective-permute-start(bf16[1024,128]{0,1:T(8,128)(2,1)S(1)} %collective-permute-done.23), channel_id=1, source_target_pairs={{0,1},{1,0},{2,3},{3,2},{4,5},{5,4},{6,7},{7,6},{8,9},{9,8},{10,11... | collective-permute-start | bytes 786440 | tf_op jit(solution)/shard_map/ppermute | solution.py:174
  157.3 8.6 %collective-permute-start.48 = (bf16[1024,128]{0,1:T(8,128)(2,1)S(1)}, bf16[1024,128]{0,1:T(8,128)(2,1)S(1)}, u32[]{:S(2)}, u32[]{:S(2)}) collective-permute-start(bf16[1024,128]{0,1:T(8,128)(2,1)S(1)} %fusion.82), channel_id=1, source_target_pairs={{0,1},{1,0},{2,3},{3,2},{4,5},{5,4},{6,7},{7,6},{8,9},{9,8},{10,11... | collective-permute-start | bytes 786440 | tf_op jit(solution)/shard_map/ppermute | solution.py:174
  168.0 3.7 %collective-permute-start.50 = (f32[1024]{0:T(1024)S(1)}, f32[1024]{0:T(1024)S(1)}, u32[]{:S(2)}, u32[]{:S(2)}) collective-permute-start(f32[1024]{0:T(1024)S(1)} %fusion.1), channel_id=1, source_target_pairs={{0,4},{4,0},{8,12},{12,8},{16,20},{20,16},{24,28},{28,24},{1,5},{5... | collective-permute-start | bytes 12296 | tf_op jit(solution)/shard_map/ppermute | solution.py:85
  171.7 3.6 %collective-permute-start.51 = (f32[1024]{0:T(1024)S(1)}, f32[1024]{0:T(1024)S(1)}, u32[]{:S(2)}, u32[]{:S(2)}) collective-permute-start(f32[1024]{0:T(1024)S(1)} %add.289), channel_id=1, source_target_pairs={{0,8},{4,12},{8,0},{12,4},{16,24},{20,28},{24,16},{28,20},{1,9},{5... | collective-permute-start | bytes 12296 | tf_op jit(solution)/shard_map/ppermute | solution.py:85
  175.3 4.5 %collective-permute-start.52 = (f32[1024]{0:T(1024)S(1)}, f32[1024]{0:T(1024)S(1)}, u32[]{:S(2)}, u32[]{:S(2)}) collective-permute-start(f32[1024]{0:T(1024)S(1)} %add.290), channel_id=1, source_target_pairs={{0,16},{4,20},{8,24},{12,28},{16,0},{20,4},{24,8},{28,12},{1,17},{... | collective-permute-start | bytes 12296 | tf_op jit(solution)/shard_map/ppermute | solution.py:85
  (15 other events, 127.5 us)

commit v27 on v23

--- a/solution.py
+++ b/solution.py
@@ -6,6 +6,7 @@
 from jax.sharding import PartitionSpec as P
 
 CHUNKS = 4
+RELAY_SPLIT = (1, 3)
 
 
 def _rows(a, blk, n):
@@ -128,8 +129,15 @@
     def chip_perm(k):
         return [(g * 2 + p, ((g + k) % m) * 2 + p) for g in range(m) for p in range(2)]
 
+    split = RELAY_SPLIT if sum(RELAY_SPLIT) == chunks else (chunks,)
+    starts = [sum(split[:h]) for h in range(len(split))]
+    part = [h for h, k in enumerate(split) for _ in range(k)]
+
     def rows(col, blk):
-        return lax.dynamic_slice(col, (((blk - ia) % na) * ds + c * r, 0), (r, vl))
+        h = part[c]
+        return lax.dynamic_slice(
+            col, (((blk - ia) % na) * split[h] * r + (c - starts[h]) * r, 0), (r, vl)
+        )
 
     fwd = jnp.concatenate(
         [forward_voxel_field, lax.ppermute(forward_voxel_field, "src", swap)], axis=0
@@ -142,8 +150,11 @@
     w_other = jnp.where(first, weight[:, 1], weight[:, 0])
     weight = jnp.concatenate([w_mine, lax.ppermute(w_other, "src", swap)], axis=0)
     back = jnp.zeros((2 * sl, vl), jnp.float32)
-    col = _zline(adjoint_voxel_field, na)
+    cols = [
+        _zline(adjoint_voxel_field[s0 * r:(s0 + k) * r], na) for s0, k in zip(starts, split)
+    ]
     for c in range(chunks):
+        col = cols[part[c]]
 
         def pblock(blk):
             return lax.dot_general(

time: 166 us -> 177 us (1.066)
  waiting for transfers between devices: 102 us -> 89.5 us
  starting transfers between devices: 30.9 us -> 42 us
  matrix products: 20.4 us -> 28.7 us
  local copies, waits for them, and re-layouts: 4.62 us -> 6.7 us
    ppermute x6 -> x12, starting transfers between devices: 12.8 us -> 24.5 us  [_zline(): cur = lax.ppermute(cur, 'src', pairs)]
    dot_general x16, matrix products: 13.3 us -> 21.4 us  [pblock(): lax.dot_general(scaled, rows(col, blk), (((1,), (1,)), ((), ())), preferr...]
    ppermute x6 -> x12, waiting for transfers between devices: 57.6 us -> 50.3 us  [_zline(): cur = lax.ppermute(cur, 'src', pairs)]
    ppermute x4, waiting for transfers between devices: 16 us -> 11.8 us  [_fast(): lax.ppermute(halves[k].astype(jnp.bfloat16), 'vox', chip_perm(k))]
    ppermute x4, waiting for transfers between devices: 20.2 us -> 16.6 us  [_fast(): lax.ppermute(piece, 'vox', chip_perm(k))]
    slice x0 -> x2, local copies, waits for them, and re-layouts: none -> 3.2 us  [_fast(): adjoint_voxel_field[s0 * r:(s0 + k) * r]]
    unnamed x15 -> x13, local copies, waits for them, and re-layouts: 4 us -> 1.87 us
    ppermute x3, starting transfers between devices: 3.39 us -> 1.35 us  [_sum_over_src(): v = v + lax.ppermute(v, 'src', [(i, i ^ b) for i in range(n)])]
  transfers between devices with their start and end apart: 35 -> 41, of which waited for: 13 -> 16; matrix products, arithmetic and copies ran while one was open for 16% -> 22% of each run, Pallas kernels for 0% -> 0%
where the time goes in v27:
time: 177 us; the launch traced here: 176 us
  waiting for transfers between devices  89.5 us (51%)
  starting transfers between devices  42 us (24%)
  matrix products  28.7 us (16%)
  other arithmetic  8.29 us (5%)
  local copies, waits for them, and re-layouts  6.7 us (4%)
    ppermute x12, waiting for transfers between devices, _zline(): cur = lax.ppermute(cur, 'src', pairs)  50.3 us
    ppermute x12, starting transfers between devices, _zline(): cur = lax.ppermute(cur, 'src', pairs)  24.5 us
    dot_general x16, matrix products, pblock(): lax.dot_general(scaled, rows(col, blk), (((1,), (1,)), ((), ())), preferr...  21.4 us
    ppermute x4, waiting for transfers between devices, _fast(): lax.ppermute(piece, 'vox', chip_perm(k))  16.6 us
    ppermute x4, waiting for transfers between devices, _fast(): lax.ppermute(halves[k].astype(jnp.bfloat16), 'vox', chip_perm(k))  11.8 us
    ppermute x3, waiting for transfers between devices, _sum_over_src(): v = v + lax.ppermute(v, 'src', [(i, i ^ b) for i in range(n)])  10.4 us
    dot_general x4, matrix products, _fast(): jnp.dot(jnp.concatenate([w for _, w in got], axis=1), jnp.concatenate([ro...  7.27 us
    ppermute x4, starting transfers between devices, _fast(): lax.ppermute(piece, 'vox', chip_perm(k))  5.2 us
  transfers between devices with their start and end apart: 41, of which 16 were waited for; matrix products, arithmetic and copies ran while one was open for 22% of the time, Pallas kernels for 0%

profile of v27, /device:TPU:0, one launch (start us, length us, event | category | flops | bytes accessed | tf_op | source)
XLA Modules:
  0.0 175.8 jit_solution(497088070492153384)
XLA Ops:
  1.1 4.9 %collective-permute-start.3 = (bf16[128,1024]{1,0:T(8,128)(2,1)S(1)}, bf16[128,1024]{1,0:T(8,128)(2,1)S(1)}, u32[]{:S(2)}, u32[]{:S(2)}) collective-permute-start(bf16[128,1024]{1,0:T(8,128)(2,1)S(1)} %slice.29), channel_id=1, source_target_pairs={{0,8},{4,12},{8,16},{12,20},{16,24},{20,28},{1,9},{5,13},{9,17},{1... | collective-permute-start | bytes 786440 | tf_op jit(solution)/shard_map/ppermute | solution.py:105
  6.1 1.3 collective-permute-start.2
  7.4 4.2 %collective-permute-done.3 = bf16[128,1024]{1,0:T(8,128)(2,1)S(1)} collective-permute-done((bf16[128,1024]{1,0:T(8,128)(2,1)S(1)}, bf16[128,1024]{1,0:T(8,128)(2,1)S(1)}, u32[]{:S(2)}, u32[]{:S(2)}) %collective-permute-start.3) | collective-permute-done | bytes 262176 | tf_op jit(solution)/shard_map/ppermute | solution.py:105
  12.3 3.5 %collective-permute-done.2 = bf16[128,1024]{1,0:T(8,128)(2,1)S(1)} collective-permute-done((bf16[128,1024]{1,0:T(8,128)(2,1)S(1)}, bf16[128,1024]{1,0:T(8,128)(2,1)S(1)}, u32[]{:S(2)}, u32[]{:S(2)}) %collective-permute-start.2) | collective-permute-done | bytes 262176 | tf_op jit(solution)/shard_map/ppermute | solution.py:105
  15.7 1.3 collective-permute-start.6
  17.0 1.6 collective-permute-start
  18.6 1.4 collective-permute-start.5
  20.0 2.1 %slice.31 = bf16[384,1024]{1,0:T(8,128)(2,1)} slice(bf16[512,1024]{1,0:T(8,128)(2,1)} %param.5), slice={[128:512], [0:1024]} | slice | bytes 1572864 | tf_op jit(solution)/shard_map/slice | solution.py:154
  22.1 6.4 %collective-permute-start.15 = (bf16[384,1024]{1,0:T(8,128)(2,1)}, bf16[384,1024]{1,0:T(8,128)(2,1)}, u32[]{:S(2)}, u32[]{:S(2)}) collective-permute-start(bf16[384,1024]{1,0:T(8,128)(2,1)} %slice.31), channel_id=1, source_target_pairs={{0,8},{4,12},{8,16},{12,20},{16,24},{20,28},{1,9},{5,13},{9,17},{1... | collective-permute-start | bytes 2359304 | tf_op jit(solution)/shard_map/ppermute | solution.py:105
  28.5 1.3 collective-permute-start.14
  29.9 1.8 %copy.5 = f32[512,1024]{0,1:T(8,128)} copy(f32[512,1024]{1,0:T(8,128)S(1)} %copy-done.2) | data formatting | bytes 4194304 | tf_op args[3]
  31.7 1.4 collective-permute-start.7
  33.2 22.7 %collective-permute-done.7 = bf16[128,1024]{1,0:T(8,128)(2,1)S(1)} collective-permute-done((bf16[128,1024]{1,0:T(8,128)(2,1)S(1)}, bf16[128,1024]{1,0:T(8,128)(2,1)S(1)}, u32[]{:S(2)}, u32[]{:S(2)}) %collective-permute-start.7) | collective-permute-done | bytes 262176 | tf_op jit(solution)/shard_map/ppermute | solution.py:105
  56.1 2.2 %fusion = bf16[1024,1024]{1,0:T(8,128)(2,1)S(1)} fusion(f32[1024]{0:T(1024)S(1)} %copy-done.5, bf16[512,1024]{1,0:T(8,128)(2,1)} %collective-permute-done, bf16[512,1024]{1,0:T(8,128)(2,1)S(1)} %copy-done.3), kind=kLoop, calls=%fused_computation.2 | loop fusion | flops 6291456 | bytes 4198400 | tf_op jit(solution)/shard_map/convert_element_type | solution.py:146
  58.3 1.7 fusion.101
  61.2 1.5 collective-permute-start.1
  62.7 1.6 collective-permute-start.16
  64.4 1.3 collective-permute-start.18
  65.7 2.6 %fusion.104 = f32[1024,128]{0,1:T(8,128)} fusion(bf16[1024,1024]{1,0:T(8,128)(2,1)S(1)} %fusion, bf16[512,1024]{1,0:T(8,128)(2,1)} %copy-done, s32[]{:T(128)S(6)} %select_n.319), kind=kOutput, calls=%fused_computation.127 | convolution fusion | flops 268435456 | bytes 2883588 | tf_op jit(solution)/shard_map/dot_general | solution.py:160
  68.5 2.0 %fusion.6 = bf16[1024,128]{0,1:T(8,128)(2,1)S(1)} fusion(f32[1024,128]{0,1:T(8,128)} %collective-permute-done.9, bf16[1024,1024]{1,0:T(8,128)(2,1)S(1)} %fusion, bf16[512,1024]{1,0:T(8,128)(2,1)} %copy-done, s32[]{:T(128)S(6)} %select_n.322), kind=kOutput, calls=%fused_computation.24 | convolution fusion | flops 268697600 | bytes 3145732 | tf_op jit(solution)/shard_map/dot_general | solution.py:160
  70.5 1.6 collective-permute-start.10
  72.0 1.6 collective-permute-start.17
  74.9 11.3 %collective-permute-done.18 = bf16[384,1024]{1,0:T(8,128)(2,1)} collective-permute-done((bf16[384,1024]{1,0:T(8,128)(2,1)}, bf16[384,1024]{1,0:T(8,128)(2,1)}, u32[]{:S(2)}, u32[]{:S(2)}) %collective-permute-start.18) | collective-permute-done | bytes 786464 | tf_op jit(solution)/shard_map/ppermute | solution.py:105
  86.2 1.3 collective-permute-start.19
  87.6 2.1 %fusion.77 = bf16[1024,128]{0,1:T(8,128)(2,1)S(1)} fusion(f32[512,512]{0,1:T(8,128)S(1)} %get-tuple-element.18, f32[512,512]{0,1:T(8,128)} %collective-permute-done.1, bf16[1024,128]{0,1:T(8,128)(2,1)} %collective-permute-done.10, f32[1024,128]{0,1:T(8,128)} %collective-permute-done.8, bf16[1024,1024]{1,0:T(8,128)(2,1)S(1)} %fusion, ...), kind=kOutput, calls=%fused_computation.99 | convolution fusion | flops 269221888 | bytes 5505028 | tf_op jit(solution)/shard_map/dot_general | solution.py:160
  89.7 1.6 collective-permute-start.11
  92.6 4.8 %collective-permute-done.11 = bf16[1024,128]{0,1:T(8,128)(2,1)S(1)} collective-permute-done((bf16[1024,128]{0,1:T(8,128)(2,1)S(1)}, bf16[1024,128]{0,1:T(8,128)(2,1)S(1)}, u32[]{:S(2)}, u32[]{:S(2)}) %collective-permute-start.11) | collective-permute-done | bytes 262176 | tf_op jit(solution)/shard_map/ppermute | solution.py:178
  98.6 8.6 %collective-permute-done.19 = bf16[384,1024]{1,0:T(8,128)(2,1)S(1)} collective-permute-done((bf16[384,1024]{1,0:T(8,128)(2,1)}, bf16[384,1024]{1,0:T(8,128)(2,1)S(1)}, u32[]{:S(2)}, u32[]{:S(2)}) %collective-permute-start.19) | collective-permute-done | bytes 786464 | tf_op jit(solution)/shard_map/ppermute | solution.py:105
  107.3 1.6 pad_maximum_fusion
  117.3 1.6 collective-permute-start.22
  119.8 5.9 %collective-permute-done.22 = bf16[1024,128]{0,1:T(8,128)(2,1)S(1)} collective-permute-done((bf16[1024,128]{0,1:T(8,128)(2,1)S(1)}, bf16[1024,128]{0,1:T(8,128)(2,1)S(1)}, u32[]{:S(2)}, u32[]{:S(2)}) %collective-permute-start.22) | collective-permute-done | bytes 262176 | tf_op jit(solution)/shard_map/ppermute | solution.py:170
  125.7 1.5 collective-permute-start.28
  127.2 1.8 %fusion.80 = bf16[1024,128]{0,1:T(8,128)(2,1)S(1)} fusion(f32[512,512]{0,1:T(8,128)S(1)} %get-tuple-element.18, f32[512,512]{0,1:T(8,128)} %collective-permute-done.1, bf16[1024,128]{0,1:T(8,128)(2,1)S(1)} %collective-permute-done.22, f32[1024,128]{0,1:T(8,128)S(1)} %collective-permute-done.20, bf16[1024,1024]{1,0:T(8,128)(2,1)S(1)} %fusion, ...), kind=kOutput, calls=%fused_computation.102 | convolution fusion | flops 269221888 | bytes 5505028 | tf_op jit(solution)/shard_map/dot_general | solution.py:160
  129.6 5.3 %collective-permute-done.28 = bf16[1024,128]{0,1:T(8,128)(2,1)S(1)} collective-permute-done((bf16[1024,128]{0,1:T(8,128)(2,1)S(1)}, bf16[1024,128]{0,1:T(8,128)(2,1)S(1)}, u32[]{:S(2)}, u32[]{:S(2)}) %collective-permute-start.28) | collective-permute-done | bytes 262176 | tf_op jit(solution)/shard_map/ppermute | solution.py:170
  135.0 1.8 %fusion.74 = bf16[1024,128]{0,1:T(8,128)(2,1)S(1)} fusion(f32[512,512]{0,1:T(8,128)S(1)} %get-tuple-element.18, f32[512,512]{0,1:T(8,128)} %collective-permute-done.1, bf16[1024,128]{0,1:T(8,128)(2,1)S(1)} %collective-permute-done.28, f32[1024,128]{0,1:T(8,128)S(1)} %collective-permute-done.26, bf16[1024,1024]{1,0:T(8,128)(2,1)S(1)} %fusion, ...), kind=kOutput, calls=%fused_computation.96 | convolution fusion | flops 269221888 | bytes 5505028 | tf_op jit(solution)/shard_map/dot_general | solution.py:160
  136.8 1.6 collective-permute-start.23
  138.9 1.5 collective-permute-start.29
  140.3 1.8 %fusion.82 = bf16[1024,128]{0,1:T(8,128)(2,1)S(1)} fusion(f32[512,512]{0,1:T(8,128)} %collective-permute-done.1, f32[512,512]{0,1:T(8,128)S(1)} %get-tuple-element.18, bf16[1024,128]{0,1:T(8,128)(2,1)S(1)} %collective-permute-done.34, f32[1024,128]{0,1:T(8,128)S(1)} %collective-permute-done.32, bf16[1024,1024]{1,0:T(8,128)(2,1)S(1)} %fusion, ...), kind=kOutput, calls=%fused_computation.105 | convolution fusion | flops 269221888 | bytes 5505028 | tf_op jit(solution)/shard_map/dot_general | solution.py:160
  142.8 3.2 %collective-permute-done.23 = bf16[1024,128]{0,1:T(8,128)(2,1)S(1)} collective-permute-done((bf16[1024,128]{0,1:T(8,128)(2,1)S(1)}, bf16[1024,128]{0,1:T(8,128)(2,1)S(1)}, u32[]{:S(2)}, u32[]{:S(2)}) %collective-permute-start.23) | collective-permute-done | bytes 262176 | tf_op jit(solution)/shard_map/ppermute | solution.py:178
  146.0 1.3 fusion.10
  148.2 3.4 %collective-permute-done.29 = bf16[1024,128]{0,1:T(8,128)(2,1)S(1)} collective-permute-done((bf16[1024,128]{0,1:T(8,128)(2,1)S(1)}, bf16[1024,128]{0,1:T(8,128)(2,1)S(1)}, u32[]{:S(2)}, u32[]{:S(2)}) %collective-permute-start.29) | collective-permute-done | bytes 262176 | tf_op jit(solution)/shard_map/ppermute | solution.py:178
  151.6 5.2 %collective-permute-done.35 = bf16[1024,128]{0,1:T(8,128)(2,1)S(1)} collective-permute-done((bf16[1024,128]{0,1:T(8,128)(2,1)S(1)}, bf16[1024,128]{0,1:T(8,128)(2,1)S(1)}, u32[]{:S(2)}, u32[]{:S(2)}) %collective-permute-start.35) | collective-permute-done | bytes 262176 | tf_op jit(solution)/shard_map/ppermute | solution.py:178
  157.3 1.3 fusion.25
  158.7 1.3 fusion.40
  160.0 3.3 %fusion.1 = f32[1024]{0:T(1024)S(1)} fusion(f32[1024,1024]{1,0:T(8,128)S(1)} %fusion.40, f32[1024,1024]{1,0:T(8,128)S(1)} %fusion.10, f32[1024,1024]{1,0:T(8,128)S(1)} %fusion.25, bf16[512,1024]{1,0:T(8,128)(2,1)} %collective-permute-done, bf16[512,1024]{1,0:T(8,128)(2,1)S(1)} %copy-done.4, bf16[1024,128]{0,1:T(8,128)(2,1)S(1)} %collective-permute-done.37, ...), kind=kOutput, calls=%fused_computation.3 | convolution fusion | flops 1091566592 | bytes 16781312 | tf_op jit(solution)/shard_map/dot_general | solution.py:181
  164.0 3.1 %collective-permute-done.38 = f32[1024]{0:T(1024)S(1)} collective-permute-done((f32[1024]{0:T(1024)S(1)}, f32[1024]{0:T(1024)S(1)}, u32[]{:S(2)}, u32[]{:S(2)}) %collective-permute-start.38) | collective-permute-done | bytes 4128 | tf_op jit(solution)/shard_map/ppermute | solution.py:85
  167.8 2.8 %collective-permute-done.39 = f32[1024]{0:T(1024)S(1)} collective-permute-done((f32[1024]{0:T(1024)S(1)}, f32[1024]{0:T(1024)S(1)}, u32[]{:S(2)}, u32[]{:S(2)}) %collective-permute-start.39) | collective-permute-done | bytes 4128 | tf_op jit(solution)/shard_map/ppermute | solution.py:85
  170.7 4.5 %collective-permute-done.40 = f32[1024]{0:T(1024)S(1)} collective-permute-done((f32[1024]{0:T(1024)S(1)}, f32[1024]{0:T(1024)S(1)}, u32[]{:S(2)}, u32[]{:S(2)}) %collective-permute-start.40) | collective-permute-done | bytes 4128 | tf_op jit(solution)/shard_map/ppermute | solution.py:85
  (84 shorter events, 21.7 us)
Async XLA Ops:
  0.0 29.9 %copy-start.2 = (f32[512,1024]{1,0:T(8,128)S(1)}, f32[512,1024]{1,0:T(8,128)}, u32[]{:S(2)}) copy-start(f32[512,1024]{1,0:T(8,128)} %param.7) | copy-start | bytes 6291460
  1.1 10.5 %collective-permute-start.3 = (bf16[128,1024]{1,0:T(8,128)(2,1)S(1)}, bf16[128,1024]{1,0:T(8,128)(2,1)S(1)}, u32[]{:S(2)}, u32[]{:S(2)}) collective-permute-start(bf16[128,1024]{1,0:T(8,128)(2,1)S(1)} %slice.29), channel_id=1, source_target_pairs={{0,8},{4,12},{8,16},{12,20},{16,24},{20,28},{1,9},{5,13},{9,17},{1... | collective-permute-start | bytes 786440 | tf_op jit(solution)/shard_map/ppermute | solution.py:105
  6.1 9.7 %collective-permute-start.2 = (bf16[128,1024]{1,0:T(8,128)(2,1)S(1)}, bf16[128,1024]{1,0:T(8,128)(2,1)S(1)}, u32[]{:S(2)}, u32[]{:S(2)}) collective-permute-start(bf16[128,1024]{1,0:T(8,128)(2,1)S(1)} %slice.29), channel_id=1, source_target_pairs={{8,0},{12,4},{16,8},{20,12},{24,16},{28,20},{9,1},{13,5},{17,9},{2... | collective-permute-start | bytes 786440 | tf_op jit(solution)/shard_map/ppermute | solution.py:105
  11.6 7.0 %collective-permute-start.4 = (bf16[128,1024]{1,0:T(8,128)(2,1)S(1)}, bf16[128,1024]{1,0:T(8,128)(2,1)S(1)}, u32[]{:S(2)}, u32[]{:S(2)}) collective-permute-start(bf16[128,1024]{1,0:T(8,128)(2,1)S(1)} %collective-permute-done.3), channel_id=1, source_target_pairs={{8,16},{12,20},{16,24},{20,28},{9,17},{13,21},{17,25},{21,29},{10,... | collective-permute-start | bytes 786440 | tf_op jit(solution)/shard_map/ppermute | solution.py:105
  15.7 16.0 %collective-permute-start.6 = (bf16[128,1024]{1,0:T(8,128)(2,1)S(1)}, bf16[128,1024]{1,0:T(8,128)(2,1)S(1)}, u32[]{:S(2)}, u32[]{:S(2)}) collective-permute-start(bf16[128,1024]{1,0:T(8,128)(2,1)S(1)} %collective-permute-done.2), channel_id=1, source_target_pairs={{8,0},{12,4},{16,8},{20,12},{9,1},{13,5},{17,9},{21,13},{10,2},{14... | collective-permute-start | bytes 786440 | tf_op jit(solution)/shard_map/ppermute | solution.py:105
  17.0 39.0 %collective-permute-start = (bf16[512,1024]{1,0:T(8,128)(2,1)}, bf16[512,1024]{1,0:T(8,128)(2,1)}, u32[]{:S(2)}, u32[]{:S(2)}) collective-permute-start(bf16[512,1024]{1,0:T(8,128)(2,1)} %param.4), channel_id=1, source_target_pairs={{0,4},{4,0},{8,12},{12,8},{16,20},{20,16},{24,28},{28,24},{1,5},{5... | collective-permute-start | bytes 3145736 | tf_op jit(solution)/shard_map/ppermute | solution.py:143
  18.6 14.6 %collective-permute-start.5 = (bf16[128,1024]{1,0:T(8,128)(2,1)S(1)}, bf16[128,1024]{1,0:T(8,128)(2,1)}, u32[]{:S(2)}, u32[]{:S(2)}) collective-permute-start(bf16[128,1024]{1,0:T(8,128)(2,1)S(1)} %collective-permute-done.4), channel_id=1, source_target_pairs={{16,24},{20,28},{17,25},{21,29},{18,26},{22,30},{19,27},{23,31}} | collective-permute-start | bytes 786440 | tf_op jit(solution)/shard_map/ppermute | solution.py:105
  22.1 40.7 %collective-permute-start.15 = (bf16[384,1024]{1,0:T(8,128)(2,1)}, bf16[384,1024]{1,0:T(8,128)(2,1)}, u32[]{:S(2)}, u32[]{:S(2)}) collective-permute-start(bf16[384,1024]{1,0:T(8,128)(2,1)} %slice.31), channel_id=1, source_target_pairs={{0,8},{4,12},{8,16},{12,20},{16,24},{20,28},{1,9},{5,13},{9,17},{1... | collective-permute-start | bytes 2359304 | tf_op jit(solution)/shard_map/ppermute | solution.py:105
  28.5 35.9 %collective-permute-start.14 = (bf16[384,1024]{1,0:T(8,128)(2,1)}, bf16[384,1024]{1,0:T(8,128)(2,1)}, u32[]{:S(2)}, u32[]{:S(2)}) collective-permute-start(bf16[384,1024]{1,0:T(8,128)(2,1)} %slice.31), channel_id=1, source_target_pairs={{8,0},{12,4},{16,8},{20,12},{24,16},{28,20},{9,1},{13,5},{17,9},{2... | collective-permute-start | bytes 2359304 | tf_op jit(solution)/shard_map/ppermute | solution.py:105
  31.7 24.4 %copy-start.3 = (bf16[512,1024]{1,0:T(8,128)(2,1)S(1)}, bf16[512,1024]{1,0:T(8,128)(2,1)}, u32[]{:S(2)}) copy-start(bf16[512,1024]{1,0:T(8,128)(2,1)} %param.4) | copy-start | bytes 3145732
  31.7 24.4 %copy-start.5 = (f32[1024]{0:T(1024)S(1)}, f32[1024]{0:T(1024)}, u32[]{:S(2)}) copy-start(f32[1024]{0:T(1024)} %param.6) | copy-start | bytes 12292
  31.7 24.2 %collective-permute-start.7 = (bf16[128,1024]{1,0:T(8,128)(2,1)S(1)}, bf16[128,1024]{1,0:T(8,128)(2,1)S(1)}, u32[]{:S(2)}, u32[]{:S(2)}) collective-permute-start(bf16[128,1024]{1,0:T(8,128)(2,1)S(1)} %collective-permute-done.6), channel_id=1, source_target_pairs={{8,0},{12,4},{9,1},{13,5},{10,2},{14,6},{11,3},{15,7}} | collective-permute-start | bytes 786440 | tf_op jit(solution)/shard_map/ppermute | solution.py:105
  56.0 2.2 %copy-start = (bf16[512,1024]{1,0:T(8,128)(2,1)}, bf16[512,1024]{1,0:T(8,128)(2,1)S(1)}, u32[]{:S(2)}) copy-start(bf16[512,1024]{1,0:T(8,128)(2,1)S(1)} %pad_maximum_fusion.2) | copy-start | bytes 3145732
  58.3 1.7 copy-start.1
  60.0 8.5 %collective-permute-start.9 = (f32[1024,128]{0,1:T(8,128)}, f32[1024,128]{0,1:T(8,128)}, u32[]{:S(2)}, u32[]{:S(2)}) collective-permute-start(f32[1024,128]{0,1:T(8,128)} %fusion.101), channel_id=1, source_target_pairs={{0,1},{1,0},{2,3},{3,2},{4,5},{5,4},{6,7},{7,6},{8,9},{9,8},{10,11... | collective-permute-start | bytes 1572872 | tf_op jit(solution)/shard_map/ppermute | solution.py:167
  61.2 26.3 %collective-permute-start.1 = (f32[512,512]{0,1:T(8,128)}, f32[512,512]{0,1:T(8,128)}, u32[]{:S(2)}, u32[]{:S(2)}) collective-permute-start(f32[512,512]{0,1:T(8,128)} %get-tuple-element.17), channel_id=1, source_target_pairs={{0,4},{4,0},{8,12},{12,8},{16,20},{20,16},{24,28},{28,24},{1,5},{5... | collective-permute-start | bytes 3145736 | tf_op jit(solution)/shard_map/ppermute | solution.py:151
  62.7 9.3 %collective-permute-start.16 = (bf16[384,1024]{1,0:T(8,128)(2,1)}, bf16[384,1024]{1,0:T(8,128)(2,1)}, u32[]{:S(2)}, u32[]{:S(2)}) collective-permute-start(bf16[384,1024]{1,0:T(8,128)(2,1)} %collective-permute-done.15), channel_id=1, source_target_pairs={{8,16},{12,20},{16,24},{20,28},{9,17},{13,21},{17,25},{21,29},{10,... | collective-permute-start | bytes 2359304 | tf_op jit(solution)/shard_map/ppermute | solution.py:105
  64.4 21.9 %collective-permute-start.18 = (bf16[384,1024]{1,0:T(8,128)(2,1)}, bf16[384,1024]{1,0:T(8,128)(2,1)}, u32[]{:S(2)}, u32[]{:S(2)}) collective-permute-start(bf16[384,1024]{1,0:T(8,128)(2,1)} %collective-permute-done.14), channel_id=1, source_target_pairs={{8,0},{12,4},{16,8},{20,12},{9,1},{13,5},{17,9},{21,13},{10,2},{14... | collective-permute-start | bytes 2359304 | tf_op jit(solution)/shard_map/ppermute | solution.py:105
  68.3 19.3 %collective-permute-start.8 = (f32[1024,128]{0,1:T(8,128)}, f32[1024,128]{0,1:T(8,128)}, u32[]{:S(2)}, u32[]{:S(2)}) collective-permute-start(f32[1024,128]{0,1:T(8,128)} %fusion.104), channel_id=1, source_target_pairs={{0,1},{1,0},{2,3},{3,2},{4,5},{5,4},{6,7},{7,6},{8,9},{9,8},{10,11... | collective-permute-start | bytes 1572872 | tf_op jit(solution)/shard_map/ppermute | solution.py:167
  70.5 17.1 %collective-permute-start.10 = (bf16[1024,128]{0,1:T(8,128)(2,1)S(1)}, bf16[1024,128]{0,1:T(8,128)(2,1)}, u32[]{:S(2)}, u32[]{:S(2)}) collective-permute-start(bf16[1024,128]{0,1:T(8,128)(2,1)S(1)} %fusion.6), channel_id=1, source_target_pairs={{0,2},{1,3},{2,0},{3,1},{4,6},{5,7},{6,4},{7,5},{8,10},{9,11},{10,... | collective-permute-start | bytes 786440 | tf_op jit(solution)/shard_map/ppermute | solution.py:170
  72.0 25.4 %collective-permute-start.17 = (bf16[384,1024]{1,0:T(8,128)(2,1)}, bf16[384,1024]{1,0:T(8,128)(2,1)}, u32[]{:S(2)}, u32[]{:S(2)}) collective-permute-start(bf16[384,1024]{1,0:T(8,128)(2,1)} %collective-permute-done.16), channel_id=1, source_target_pairs={{16,24},{20,28},{17,25},{21,29},{18,26},{22,30},{19,27},{23,31}} | collective-permute-start | bytes 2359304 | tf_op jit(solution)/shard_map/ppermute | solution.py:105
  86.2 20.9 %collective-permute-start.19 = (bf16[384,1024]{1,0:T(8,128)(2,1)}, bf16[384,1024]{1,0:T(8,128)(2,1)S(1)}, u32[]{:S(2)}, u32[]{:S(2)}) collective-permute-start(bf16[384,1024]{1,0:T(8,128)(2,1)} %collective-permute-done.18), channel_id=1, source_target_pairs={{8,0},{12,4},{9,1},{13,5},{10,2},{14,6},{11,3},{15,7}} | collective-permute-start | bytes 2359304 | tf_op jit(solution)/shard_map/ppermute | solution.py:105
  89.7 7.7 %collective-permute-start.11 = (bf16[1024,128]{0,1:T(8,128)(2,1)S(1)}, bf16[1024,128]{0,1:T(8,128)(2,1)S(1)}, u32[]{:S(2)}, u32[]{:S(2)}) collective-permute-start(bf16[1024,128]{0,1:T(8,128)(2,1)S(1)} %fusion.77), channel_id=1, source_target_pairs={{0,2},{1,3},{2,0},{3,1},{4,6},{5,7},{6,4},{7,5},{8,10},{9,11},{10,... | collective-permute-start | bytes 786440 | tf_op jit(solution)/shard_map/ppermute | solution.py:178
  92.5 49.7 %collective-permute-start.12 = (bf16[1024,128]{0,1:T(8,128)(2,1)S(1)}, bf16[1024,128]{0,1:T(8,128)(2,1)S(1)}, u32[]{:S(2)}, u32[]{:S(2)}) collective-permute-start(bf16[1024,128]{0,1:T(8,128)(2,1)S(1)} %fusion.77), channel_id=1, source_target_pairs={{0,1},{1,0},{2,3},{3,2},{4,5},{5,4},{6,7},{7,6},{8,9},{9,8},{10,11... | collective-permute-start | bytes 786440 | tf_op jit(solution)/shard_map/ppermute | solution.py:179
  97.4 48.6 %collective-permute-start.13 = (bf16[1024,128]{0,1:T(8,128)(2,1)S(1)}, bf16[1024,128]{0,1:T(8,128)(2,1)S(1)}, u32[]{:S(2)}, u32[]{:S(2)}) collective-permute-start(bf16[1024,128]{0,1:T(8,128)(2,1)S(1)} %collective-permute-done.11), channel_id=1, source_target_pairs={{0,1},{1,0},{2,3},{3,2},{4,5},{5,4},{6,7},{7,6},{8,9},{9,8},{10,11... | collective-permute-start | bytes 786440 | tf_op jit(solution)/shard_map/ppermute | solution.py:179
  112.3 7.4 %collective-permute-start.20 = (f32[1024,128]{0,1:T(8,128)S(1)}, f32[1024,128]{0,1:T(8,128)S(1)}, u32[]{:S(2)}, u32[]{:S(2)}) collective-permute-start(f32[1024,128]{0,1:T(8,128)S(1)} %fusion.98), channel_id=1, source_target_pairs={{0,1},{1,0},{2,3},{3,2},{4,5},{5,4},{6,7},{7,6},{8,9},{9,8},{10,11... | collective-permute-start | bytes 1572872 | tf_op jit(solution)/shard_map/ppermute | solution.py:167
  112.4 2.6 %collective-permute-start.21 = (f32[1024,128]{0,1:T(8,128)S(1)}, f32[1024,128]{0,1:T(8,128)S(1)}, u32[]{:S(2)}, u32[]{:S(2)}) collective-permute-start(f32[1024,128]{0,1:T(8,128)S(1)} %fusion.95), channel_id=1, source_target_pairs={{0,1},{1,0},{2,3},{3,2},{4,5},{5,4},{6,7},{7,6},{8,9},{9,8},{10,11... | collective-permute-start | bytes 1572872 | tf_op jit(solution)/shard_map/ppermute | solution.py:167
  112.9 3.1 %collective-permute-start.27 = (f32[1024,128]{0,1:T(8,128)S(1)}, f32[1024,128]{0,1:T(8,128)S(1)}, u32[]{:S(2)}, u32[]{:S(2)}) collective-permute-start(f32[1024,128]{0,1:T(8,128)S(1)} %fusion.89), channel_id=1, source_target_pairs={{0,1},{1,0},{2,3},{3,2},{4,5},{5,4},{6,7},{7,6},{8,9},{9,8},{10,11... | collective-permute-start | bytes 1572872 | tf_op jit(solution)/shard_map/ppermute | solution.py:167
  115.0 2.3 %collective-permute-start.33 = (f32[1024,128]{0,1:T(8,128)S(1)}, f32[1024,128]{0,1:T(8,128)S(1)}, u32[]{:S(2)}, u32[]{:S(2)}) collective-permute-start(f32[1024,128]{0,1:T(8,128)S(1)} %fusion.83), channel_id=1, source_target_pairs={{0,1},{1,0},{2,3},{3,2},{4,5},{5,4},{6,7},{7,6},{8,9},{9,8},{10,11... | collective-permute-start | bytes 1572872 | tf_op jit(solution)/shard_map/ppermute | solution.py:167
  116.0 13.0 %collective-permute-start.26 = (f32[1024,128]{0,1:T(8,128)S(1)}, f32[1024,128]{0,1:T(8,128)S(1)}, u32[]{:S(2)}, u32[]{:S(2)}) collective-permute-start(f32[1024,128]{0,1:T(8,128)S(1)} %fusion.92), channel_id=1, source_target_pairs={{0,1},{1,0},{2,3},{3,2},{4,5},{5,4},{6,7},{7,6},{8,9},{9,8},{10,11... | collective-permute-start | bytes 1572872 | tf_op jit(solution)/shard_map/ppermute | solution.py:167
  117.3 8.4 %collective-permute-start.22 = (bf16[1024,128]{0,1:T(8,128)(2,1)S(1)}, bf16[1024,128]{0,1:T(8,128)(2,1)S(1)}, u32[]{:S(2)}, u32[]{:S(2)}) collective-permute-start(bf16[1024,128]{0,1:T(8,128)(2,1)S(1)} %fusion.7), channel_id=1, source_target_pairs={{0,2},{1,3},{2,0},{3,1},{4,6},{5,7},{6,4},{7,5},{8,10},{9,11},{10,... | collective-permute-start | bytes 786440 | tf_op jit(solution)/shard_map/ppermute | solution.py:170
  119.7 17.1 %collective-permute-start.32 = (f32[1024,128]{0,1:T(8,128)S(1)}, f32[1024,128]{0,1:T(8,128)S(1)}, u32[]{:S(2)}, u32[]{:S(2)}) collective-permute-start(f32[1024,128]{0,1:T(8,128)S(1)} %fusion.86), channel_id=1, source_target_pairs={{0,1},{1,0},{2,3},{3,2},{4,5},{5,4},{6,7},{7,6},{8,9},{9,8},{10,11... | collective-permute-start | bytes 1572872 | tf_op jit(solution)/shard_map/ppermute | solution.py:167
  125.7 9.2 %collective-permute-start.28 = (bf16[1024,128]{0,1:T(8,128)(2,1)S(1)}, bf16[1024,128]{0,1:T(8,128)(2,1)S(1)}, u32[]{:S(2)}, u32[]{:S(2)}) collective-permute-start(bf16[1024,128]{0,1:T(8,128)(2,1)S(1)} %fusion.8), channel_id=1, source_target_pairs={{0,2},{1,3},{2,0},{3,1},{4,6},{5,7},{6,4},{7,5},{8,10},{9,11},{10,... | collective-permute-start | bytes 786440 | tf_op jit(solution)/shard_map/ppermute | solution.py:170
  129.0 9.8 %collective-permute-start.34 = (bf16[1024,128]{0,1:T(8,128)(2,1)S(1)}, bf16[1024,128]{0,1:T(8,128)(2,1)S(1)}, u32[]{:S(2)}, u32[]{:S(2)}) collective-permute-start(bf16[1024,128]{0,1:T(8,128)(2,1)S(1)} %fusion.9), channel_id=1, source_target_pairs={{0,2},{1,3},{2,0},{3,1},{4,6},{5,7},{6,4},{7,5},{8,10},{9,11},{10,... | collective-permute-start | bytes 786440 | tf_op jit(solution)/shard_map/ppermute | solution.py:170
  135.0 21.9 %collective-permute-start.24 = (bf16[1024,128]{0,1:T(8,128)(2,1)S(1)}, bf16[1024,128]{0,1:T(8,128)(2,1)S(1)}, u32[]{:S(2)}, u32[]{:S(2)}) collective-permute-start(bf16[1024,128]{0,1:T(8,128)(2,1)S(1)} %fusion.80), channel_id=1, source_target_pairs={{0,1},{1,0},{2,3},{3,2},{4,5},{5,4},{6,7},{7,6},{8,9},{9,8},{10,11... | collective-permute-start | bytes 786440 | tf_op jit(solution)/shard_map/ppermute | solution.py:179
  136.8 9.2 %collective-permute-start.23 = (bf16[1024,128]{0,1:T(8,128)(2,1)S(1)}, bf16[1024,128]{0,1:T(8,128)(2,1)S(1)}, u32[]{:S(2)}, u32[]{:S(2)}) collective-permute-start(bf16[1024,128]{0,1:T(8,128)(2,1)S(1)} %fusion.80), channel_id=1, source_target_pairs={{0,2},{1,3},{2,0},{3,1},{4,6},{5,7},{6,4},{7,5},{8,10},{9,11},{10,... | collective-permute-start | bytes 786440 | tf_op jit(solution)/shard_map/ppermute | solution.py:178
  138.9 12.7 %collective-permute-start.29 = (bf16[1024,128]{0,1:T(8,128)(2,1)S(1)}, bf16[1024,128]{0,1:T(8,128)(2,1)S(1)}, u32[]{:S(2)}, u32[]{:S(2)}) collective-permute-start(bf16[1024,128]{0,1:T(8,128)(2,1)S(1)} %fusion.74), channel_id=1, source_target_pairs={{0,2},{1,3},{2,0},{3,1},{4,6},{5,7},{6,4},{7,5},{8,10},{9,11},{10,... | collective-permute-start | bytes 786440 | tf_op jit(solution)/shard_map/ppermute | solution.py:178
  142.2 14.6 %collective-permute-start.35 = (bf16[1024,128]{0,1:T(8,128)(2,1)S(1)}, bf16[1024,128]{0,1:T(8,128)(2,1)S(1)}, u32[]{:S(2)}, u32[]{:S(2)}) collective-permute-start(bf16[1024,128]{0,1:T(8,128)(2,1)S(1)} %fusion.82), channel_id=1, source_target_pairs={{0,2},{1,3},{2,0},{3,1},{4,6},{5,7},{6,4},{7,5},{8,10},{9,11},{10,... | collective-permute-start | bytes 786440 | tf_op jit(solution)/shard_map/ppermute | solution.py:178
  146.0 11.4 %collective-permute-start.25 = (bf16[1024,128]{0,1:T(8,128)(2,1)S(1)}, bf16[1024,128]{0,1:T(8,128)(2,1)S(1)}, u32[]{:S(2)}, u32[]{:S(2)}) collective-permute-start(bf16[1024,128]{0,1:T(8,128)(2,1)S(1)} %collective-permute-done.23), channel_id=1, source_target_pairs={{0,1},{1,0},{2,3},{3,2},{4,5},{5,4},{6,7},{7,6},{8,9},{9,8},{10,11... | collective-permute-start | bytes 786440 | tf_op jit(solution)/shard_map/ppermute | solution.py:179
  147.6 11.0 %collective-permute-start.30 = (bf16[1024,128]{0,1:T(8,128)(2,1)S(1)}, bf16[1024,128]{0,1:T(8,128)(2,1)S(1)}, u32[]{:S(2)}, u32[]{:S(2)}) collective-permute-start(bf16[1024,128]{0,1:T(8,128)(2,1)S(1)} %fusion.74), channel_id=1, source_target_pairs={{0,1},{1,0},{2,3},{3,2},{4,5},{5,4},{6,7},{7,6},{8,9},{9,8},{10,11... | collective-permute-start | bytes 786440 | tf_op jit(solution)/shard_map/ppermute | solution.py:179
  151.6 8.4 %collective-permute-start.36 = (bf16[1024,128]{0,1:T(8,128)(2,1)S(1)}, bf16[1024,128]{0,1:T(8,128)(2,1)S(1)}, u32[]{:S(2)}, u32[]{:S(2)}) collective-permute-start(bf16[1024,128]{0,1:T(8,128)(2,1)S(1)} %fusion.82), channel_id=1, source_target_pairs={{0,1},{1,0},{2,3},{3,2},{4,5},{5,4},{6,7},{7,6},{8,9},{9,8},{10,11... | collective-permute-start | bytes 786440 | tf_op jit(solution)/shard_map/ppermute | solution.py:179
  156.8 1.9 %collective-permute-start.31 = (bf16[1024,128]{0,1:T(8,128)(2,1)S(1)}, bf16[1024,128]{0,1:T(8,128)(2,1)S(1)}, u32[]{:S(2)}, u32[]{:S(2)}) collective-permute-start(bf16[1024,128]{0,1:T(8,128)(2,1)S(1)} %collective-permute-done.29), channel_id=1, source_target_pairs={{0,1},{1,0},{2,3},{3,2},{4,5},{5,4},{6,7},{7,6},{8,9},{9,8},{10,11... | collective-permute-start | bytes 786440 | tf_op jit(solution)/shard_map/ppermute | solution.py:179
  156.8 3.2 %collective-permute-start.37 = (bf16[1024,128]{0,1:T(8,128)(2,1)S(1)}, bf16[1024,128]{0,1:T(8,128)(2,1)S(1)}, u32[]{:S(2)}, u32[]{:S(2)}) collective-permute-start(bf16[1024,128]{0,1:T(8,128)(2,1)S(1)} %collective-permute-done.35), channel_id=1, source_target_pairs={{0,1},{1,0},{2,3},{3,2},{4,5},{5,4},{6,7},{7,6},{8,9},{9,8},{10,11... | collective-permute-start | bytes 786440 | tf_op jit(solution)/shard_map/ppermute | solution.py:179
  158.7 1.4 copy-start.4
  163.4 3.7 %collective-permute-start.38 = (f32[1024]{0:T(1024)S(1)}, f32[1024]{0:T(1024)S(1)}, u32[]{:S(2)}, u32[]{:S(2)}) collective-permute-start(f32[1024]{0:T(1024)S(1)} %fusion.1), channel_id=1, source_target_pairs={{0,4},{4,0},{8,12},{12,8},{16,20},{20,16},{24,28},{28,24},{1,5},{5... | collective-permute-start | bytes 12296 | tf_op jit(solution)/shard_map/ppermute | solution.py:85
  167.1 3.6 %collective-permute-start.39 = (f32[1024]{0:T(1024)S(1)}, f32[1024]{0:T(1024)S(1)}, u32[]{:S(2)}, u32[]{:S(2)}) collective-permute-start(f32[1024]{0:T(1024)S(1)} %add.451), channel_id=1, source_target_pairs={{0,8},{4,12},{8,0},{12,4},{16,24},{20,28},{24,16},{28,20},{1,9},{5... | collective-permute-start | bytes 12296 | tf_op jit(solution)/shard_map/ppermute | solution.py:85
  170.7 4.5 %collective-permute-start.40 = (f32[1024]{0:T(1024)S(1)}, f32[1024]{0:T(1024)S(1)}, u32[]{:S(2)}, u32[]{:S(2)}) collective-permute-start(f32[1024]{0:T(1024)S(1)} %add.452), channel_id=1, source_target_pairs={{0,16},{4,20},{8,24},{12,28},{16,0},{20,4},{24,8},{28,12},{1,17},{... | collective-permute-start | bytes 12296 | tf_op jit(solution)/shard_map/ppermute | solution.py:85

commit v28 on v25

--- a/solution.py
+++ b/solution.py
@@ -159,7 +159,10 @@
 
         keeps = [pblock(2 * ((q + k) % m) + par) for k in range(m)]
         sends = [pblock(2 * ((q + k) % m) + 1 - par) for k in range(m)]
-        halves = [a + b for a, b in zip(keeps, lax.ppermute(tuple(sends), "vox", pair))]
+        sends = tuple(x.astype(jnp.bfloat16) for x in sends)
+        halves = [
+            a + b.astype(jnp.float32) for a, b in zip(keeps, lax.ppermute(sends, "vox", pair))
+        ]
         share = halves[0]
         for k in range(1, m):
             share = share + lax.ppermute(

time: 163 us -> 163 us (level)
  transfers between devices with their start and end apart: 41 -> 41, of which waited for: 20 -> 22; matrix products, arithmetic and copies ran while one was open for 16% -> 16% of each run, Pallas kernels for 0% -> 0%
where the time goes in v28:
time: 163 us; the launch traced here: 162 us
  waiting for transfers between devices  93.1 us (57%)
  starting transfers between devices  38.5 us (24%)
  matrix products  20.5 us (13%)
  other arithmetic  5.49 us (3%)
  local copies, waits for them, and re-layouts  3.94 us (2%)
    ppermute x12, waiting for transfers between devices, _zline(): cur = lax.ppermute(cur, 'src', pairs)  47.1 us
    ppermute x12, starting transfers between devices, _zline(): cur = lax.ppermute(cur, 'src', pairs)  20.3 us
    ppermute x4, waiting for transfers between devices, _fast(): lax.ppermute(piece, 'vox', chip_perm(k))  19 us
    ppermute x4, waiting for transfers between devices, _fast(): lax.ppermute(halves[k].astype(jnp.bfloat16), 'vox', chip_perm(k))  15.1 us
    dot_general x16, matrix products, pblock(): lax.dot_general(scaled, rows(col, blk), (((1,), (1,)), ((), ())), preferr...  13.4 us
    ppermute x3, waiting for transfers between devices, _sum_over_src(): v = v + lax.ppermute(v, 'src', [(i, i ^ b) for i in range(n)])  10.6 us
    dot_general x4, matrix products, _fast(): jnp.dot(jnp.concatenate([w for _, w in got], axis=1), jnp.concatenate([ro...  7.09 us
    ppermute x4, starting transfers between devices, _fast(): lax.ppermute(piece, 'vox', chip_perm(k))  6.02 us
  transfers between devices with their start and end apart: 41, of which 22 were waited for; matrix products, arithmetic and copies ran while one was open for 16% of the time, Pallas kernels for 0%

profile of v28, /device:TPU:0, one launch (start us, length us, event | category | flops | bytes accessed | tf_op | source)
XLA Modules:
  0.0 162.3 jit_solution(16339072196143594116)
XLA Ops:
  0.0 3.0 %collective-permute-start = (bf16[512,1024]{1,0:T(8,128)(2,1)}, bf16[512,1024]{1,0:T(8,128)(2,1)}, u32[]{:S(2)}, u32[]{:S(2)}) collective-permute-start(bf16[512,1024]{1,0:T(8,128)(2,1)} %param.4), channel_id=1, source_target_pairs={{0,4},{4,0},{8,12},{12,8},{16,20},{20,16},{24,28},{28,24},{1,5},{5... | collective-permute-start | bytes 3145736 | tf_op jit(solution)/shard_map/ppermute | solution.py:140
  3.0 1.3 fusion.119
  4.2 4.3 %collective-permute-start.3 = (bf16[256,1024]{1,0:T(8,128)(2,1)S(1)}, bf16[256,1024]{1,0:T(8,128)(2,1)}, u32[]{:S(2)}, u32[]{:S(2)}) collective-permute-start(bf16[256,1024]{1,0:T(8,128)(2,1)S(1)} %get-tuple-element.23), channel_id=1, source_target_pairs={{0,8},{4,12},{8,16},{12,20},{16,24},{20,28},{1,9},{5,13},{9,17},{1... | collective-permute-start | bytes 1572872 | tf_op jit(solution)/shard_map/ppermute | solution.py:105
  8.5 1.3 collective-permute-start.2
  9.8 5.4 %collective-permute-start.21 = (bf16[256,1024]{1,0:T(8,128)(2,1)S(1)}, bf16[256,1024]{1,0:T(8,128)(2,1)}, u32[]{:S(2)}, u32[]{:S(2)}) collective-permute-start(bf16[256,1024]{1,0:T(8,128)(2,1)S(1)} %get-tuple-element.24), channel_id=1, source_target_pairs={{0,8},{4,12},{8,16},{12,20},{16,24},{20,28},{1,9},{5,13},{9,17},{1... | collective-permute-start | bytes 1572872 | tf_op jit(solution)/shard_map/ppermute | solution.py:105
  15.2 1.3 collective-permute-start.20
  16.8 1.9 %copy.5 = f32[512,1024]{0,1:T(8,128)S(1)} copy(f32[512,1024]{1,0:T(8,128)} %param.7) | data formatting | bytes 4194304 | tf_op args[3]
  18.8 1.3 collective-permute-done.3
  20.8 4.6 %collective-permute-done.2 = bf16[256,1024]{1,0:T(8,128)(2,1)} collective-permute-done((bf16[256,1024]{1,0:T(8,128)(2,1)S(1)}, bf16[256,1024]{1,0:T(8,128)(2,1)}, u32[]{:S(2)}, u32[]{:S(2)}) %collective-permute-start.2) | collective-permute-done | bytes 524320 | tf_op jit(solution)/shard_map/ppermute | solution.py:105
  25.4 1.3 collective-permute-start.6
  26.7 3.2 %collective-permute-done.21 = bf16[256,1024]{1,0:T(8,128)(2,1)} collective-permute-done((bf16[256,1024]{1,0:T(8,128)(2,1)S(1)}, bf16[256,1024]{1,0:T(8,128)(2,1)}, u32[]{:S(2)}, u32[]{:S(2)}) %collective-permute-start.21) | collective-permute-done | bytes 524320 | tf_op jit(solution)/shard_map/ppermute | solution.py:105
  30.5 6.1 %collective-permute-done.20 = bf16[256,1024]{1,0:T(8,128)(2,1)} collective-permute-done((bf16[256,1024]{1,0:T(8,128)(2,1)S(1)}, bf16[256,1024]{1,0:T(8,128)(2,1)}, u32[]{:S(2)}, u32[]{:S(2)}) %collective-permute-start.20) | collective-permute-done | bytes 524320 | tf_op jit(solution)/shard_map/ppermute | solution.py:105
  36.6 1.3 collective-permute-start.24
  39.1 1.8 %fusion = bf16[1024,1024]{1,0:T(8,128)(2,1)S(1)} fusion(f32[1024]{0:T(1024)S(1)} %copy-done.1, bf16[512,1024]{1,0:T(8,128)(2,1)} %collective-permute-done, bf16[512,1024]{1,0:T(8,128)(2,1)S(1)} %copy-done), kind=kLoop, calls=%fused_computation.2 | loop fusion | flops 6291456 | bytes 4198400 | tf_op jit(solution)/shard_map/convert_element_type | solution.py:143
  41.7 6.1 %collective-permute-done.6 = bf16[256,1024]{1,0:T(8,128)(2,1)S(1)} collective-permute-done((bf16[256,1024]{1,0:T(8,128)(2,1)}, bf16[256,1024]{1,0:T(8,128)(2,1)S(1)}, u32[]{:S(2)}, u32[]{:S(2)}) %collective-permute-start.6) | collective-permute-done | bytes 524320 | tf_op jit(solution)/shard_map/ppermute | solution.py:105
  47.8 1.3 collective-permute-start.7
  49.8 9.2 %collective-permute-done.24 = bf16[256,1024]{1,0:T(8,128)(2,1)S(1)} collective-permute-done((bf16[256,1024]{1,0:T(8,128)(2,1)}, bf16[256,1024]{1,0:T(8,128)(2,1)S(1)}, u32[]{:S(2)}, u32[]{:S(2)}) %collective-permute-start.24) | collective-permute-done | bytes 524320 | tf_op jit(solution)/shard_map/ppermute | solution.py:105
  59.0 1.5 collective-permute-start.25
  60.6 1.1 broadcast_select_fusion.5
  61.7 8.5 %collective-permute-done.7 = bf16[256,1024]{1,0:T(8,128)(2,1)S(1)} collective-permute-done((bf16[256,1024]{1,0:T(8,128)(2,1)S(1)}, bf16[256,1024]{1,0:T(8,128)(2,1)S(1)}, u32[]{:S(2)}, u32[]{:S(2)}) %collective-permute-start.7) | collective-permute-done | bytes 524320 | tf_op jit(solution)/shard_map/ppermute | solution.py:105
  70.5 1.1 broadcast_select_fusion.4
  71.6 8.1 %collective-permute-done.25 = bf16[256,1024]{1,0:T(8,128)(2,1)S(1)} collective-permute-done((bf16[256,1024]{1,0:T(8,128)(2,1)S(1)}, bf16[256,1024]{1,0:T(8,128)(2,1)S(1)}, u32[]{:S(2)}, u32[]{:S(2)}) %collective-permute-start.25) | collective-permute-done | bytes 524320 | tf_op jit(solution)/shard_map/ppermute | solution.py:105
  80.8 0.8 convolution_convert_fusion.4
  85.4 0.8 convolution_convert_fusion.1
  92.7 1.5 collective-permute-start.34
  95.7 6.1 %collective-permute-done.34 = bf16[1024,128]{0,1:T(8,128)(2,1)S(1)} collective-permute-done((bf16[1024,128]{0,1:T(8,128)(2,1)S(1)}, bf16[1024,128]{0,1:T(8,128)(2,1)S(1)}, u32[]{:S(2)}, u32[]{:S(2)}) %collective-permute-start.34) | collective-permute-done | bytes 262176 | tf_op jit(solution)/shard_map/ppermute | solution.py:168
  101.8 1.5 collective-permute-start.28
  103.3 0.9 fusion.82
  104.8 2.6 %collective-permute-done.10 = bf16[1024,128]{0,1:T(8,128)(2,1)S(1)} collective-permute-done((bf16[1024,128]{0,1:T(8,128)(2,1)S(1)}, bf16[1024,128]{0,1:T(8,128)(2,1)S(1)}, u32[]{:S(2)}, u32[]{:S(2)}) %collective-permute-start.10) | collective-permute-done | bytes 262176 | tf_op jit(solution)/shard_map/ppermute | solution.py:168
  107.5 0.9 fusion.77
  108.3 1.6 collective-permute-start.35
  109.9 3.2 %collective-permute-done.28 = bf16[1024,128]{0,1:T(8,128)(2,1)S(1)} collective-permute-done((bf16[1024,128]{0,1:T(8,128)(2,1)S(1)}, bf16[1024,128]{0,1:T(8,128)(2,1)S(1)}, u32[]{:S(2)}, u32[]{:S(2)}) %collective-permute-start.28) | collective-permute-done | bytes 262176 | tf_op jit(solution)/shard_map/ppermute | solution.py:168
  113.1 1.5 collective-permute-start.11
  114.6 0.9 fusion.74
  115.5 3.2 %collective-permute-done.16 = bf16[1024,128]{0,1:T(8,128)(2,1)S(1)} collective-permute-done((bf16[1024,128]{0,1:T(8,128)(2,1)S(1)}, bf16[1024,128]{0,1:T(8,128)(2,1)S(1)}, u32[]{:S(2)}, u32[]{:S(2)}) %collective-permute-start.16) | collective-permute-done | bytes 262176 | tf_op jit(solution)/shard_map/ppermute | solution.py:168
  118.7 1.5 collective-permute-start.29
  120.2 9.7 %collective-permute-done.11 = bf16[1024,128]{0,1:T(8,128)(2,1)S(1)} collective-permute-done((bf16[1024,128]{0,1:T(8,128)(2,1)S(1)}, bf16[1024,128]{0,1:T(8,128)(2,1)S(1)}, u32[]{:S(2)}, u32[]{:S(2)}) %collective-permute-start.11) | collective-permute-done | bytes 262176 | tf_op jit(solution)/shard_map/ppermute | solution.py:176
  129.9 0.9 fusion.80
  130.8 4.2 %collective-permute-done.29 = bf16[1024,128]{0,1:T(8,128)(2,1)S(1)} collective-permute-done((bf16[1024,128]{0,1:T(8,128)(2,1)S(1)}, bf16[1024,128]{0,1:T(8,128)(2,1)S(1)}, u32[]{:S(2)}, u32[]{:S(2)}) %collective-permute-start.29) | collective-permute-done | bytes 262176 | tf_op jit(solution)/shard_map/ppermute | solution.py:176
  135.0 1.5 collective-permute-start.17
  136.7 1.5 fusion.10
  138.6 5.1 %collective-permute-done.17 = bf16[1024,128]{0,1:T(8,128)(2,1)S(1)} collective-permute-done((bf16[1024,128]{0,1:T(8,128)(2,1)S(1)}, bf16[1024,128]{0,1:T(8,128)(2,1)S(1)}, u32[]{:S(2)}, u32[]{:S(2)}) %collective-permute-start.17) | collective-permute-done | bytes 262176 | tf_op jit(solution)/shard_map/ppermute | solution.py:176
  144.2 1.3 fusion.40
  145.6 1.3 fusion.25
  147.0 3.0 %fusion.1 = f32[1024]{0:T(1024)S(1)} fusion(f32[1024,1024]{1,0:T(8,128)S(1)} %fusion.40, f32[1024,1024]{1,0:T(8,128)S(1)} %fusion.10, f32[1024,1024]{1,0:T(8,128)S(1)} %fusion.25, bf16[512,1024]{1,0:T(8,128)(2,1)} %collective-permute-done, bf16[512,1024]{1,0:T(8,128)(2,1)S(1)} %copy-done, bf16[1024,128]{0,1:T(8,128)(2,1)S(1)} %collective-permute-done.37, ...), kind=kOutput, calls=%fused_computation.3 | convolution fusion | flops 1091566592 | bytes 16781312 | tf_op jit(solution)/shard_map/dot_general | solution.py:179
  150.5 3.1 %collective-permute-done.38 = f32[1024]{0:T(1024)S(1)} collective-permute-done((f32[1024]{0:T(1024)S(1)}, f32[1024]{0:T(1024)S(1)}, u32[]{:S(2)}, u32[]{:S(2)}) %collective-permute-start.38) | collective-permute-done | bytes 4128 | tf_op jit(solution)/shard_map/ppermute | solution.py:85
  154.2 3.0 %collective-permute-done.39 = f32[1024]{0:T(1024)S(1)} collective-permute-done((f32[1024]{0:T(1024)S(1)}, f32[1024]{0:T(1024)S(1)}, u32[]{:S(2)}, u32[]{:S(2)}) %collective-permute-start.39) | collective-permute-done | bytes 4128 | tf_op jit(solution)/shard_map/ppermute | solution.py:85
  157.2 4.5 %collective-permute-done.40 = f32[1024]{0:T(1024)S(1)} collective-permute-done((f32[1024]{0:T(1024)S(1)}, f32[1024]{0:T(1024)S(1)}, u32[]{:S(2)}, u32[]{:S(2)}) %collective-permute-start.40) | collective-permute-done | bytes 4128 | tf_op jit(solution)/shard_map/ppermute | solution.py:85
  (75 shorter events, 20.7 us)
Async XLA Ops:
  0.0 38.2 %collective-permute-start = (bf16[512,1024]{1,0:T(8,128)(2,1)}, bf16[512,1024]{1,0:T(8,128)(2,1)}, u32[]{:S(2)}, u32[]{:S(2)}) collective-permute-start(bf16[512,1024]{1,0:T(8,128)(2,1)} %param.4), channel_id=1, source_target_pairs={{0,4},{4,0},{8,12},{12,8},{16,20},{20,16},{24,28},{28,24},{1,5},{5... | collective-permute-start | bytes 3145736 | tf_op jit(solution)/shard_map/ppermute | solution.py:140
  4.2 15.8 %collective-permute-start.3 = (bf16[256,1024]{1,0:T(8,128)(2,1)S(1)}, bf16[256,1024]{1,0:T(8,128)(2,1)}, u32[]{:S(2)}, u32[]{:S(2)}) collective-permute-start(bf16[256,1024]{1,0:T(8,128)(2,1)S(1)} %get-tuple-element.23), channel_id=1, source_target_pairs={{0,8},{4,12},{8,16},{12,20},{16,24},{20,28},{1,9},{5,13},{9,17},{1... | collective-permute-start | bytes 1572872 | tf_op jit(solution)/shard_map/ppermute | solution.py:105
  8.5 16.9 %collective-permute-start.2 = (bf16[256,1024]{1,0:T(8,128)(2,1)S(1)}, bf16[256,1024]{1,0:T(8,128)(2,1)}, u32[]{:S(2)}, u32[]{:S(2)}) collective-permute-start(bf16[256,1024]{1,0:T(8,128)(2,1)S(1)} %get-tuple-element.23), channel_id=1, source_target_pairs={{8,0},{12,4},{16,8},{20,12},{24,16},{28,20},{9,1},{13,5},{17,9},{2... | collective-permute-start | bytes 1572872 | tf_op jit(solution)/shard_map/ppermute | solution.py:105
  9.8 20.0 %collective-permute-start.21 = (bf16[256,1024]{1,0:T(8,128)(2,1)S(1)}, bf16[256,1024]{1,0:T(8,128)(2,1)}, u32[]{:S(2)}, u32[]{:S(2)}) collective-permute-start(bf16[256,1024]{1,0:T(8,128)(2,1)S(1)} %get-tuple-element.24), channel_id=1, source_target_pairs={{0,8},{4,12},{8,16},{12,20},{16,24},{20,28},{1,9},{5,13},{9,17},{1... | collective-permute-start | bytes 1572872 | tf_op jit(solution)/shard_map/ppermute | solution.py:105
  15.2 21.4 %collective-permute-start.20 = (bf16[256,1024]{1,0:T(8,128)(2,1)S(1)}, bf16[256,1024]{1,0:T(8,128)(2,1)}, u32[]{:S(2)}, u32[]{:S(2)}) collective-permute-start(bf16[256,1024]{1,0:T(8,128)(2,1)S(1)} %get-tuple-element.24), channel_id=1, source_target_pairs={{8,0},{12,4},{16,8},{20,12},{24,16},{28,20},{9,1},{13,5},{17,9},{2... | collective-permute-start | bytes 1572872 | tf_op jit(solution)/shard_map/ppermute | solution.py:105
  20.1 20.9 %collective-permute-start.4 = (bf16[256,1024]{1,0:T(8,128)(2,1)}, bf16[256,1024]{1,0:T(8,128)(2,1)S(1)}, u32[]{:S(2)}, u32[]{:S(2)}) collective-permute-start(bf16[256,1024]{1,0:T(8,128)(2,1)} %collective-permute-done.3), channel_id=1, source_target_pairs={{8,16},{12,20},{16,24},{20,28},{9,17},{13,21},{17,25},{21,29},{10,... | collective-permute-start | bytes 1572872 | tf_op jit(solution)/shard_map/ppermute | solution.py:105
  25.4 22.4 %collective-permute-start.6 = (bf16[256,1024]{1,0:T(8,128)(2,1)}, bf16[256,1024]{1,0:T(8,128)(2,1)S(1)}, u32[]{:S(2)}, u32[]{:S(2)}) collective-permute-start(bf16[256,1024]{1,0:T(8,128)(2,1)} %collective-permute-done.2), channel_id=1, source_target_pairs={{8,0},{12,4},{16,8},{20,12},{9,1},{13,5},{17,9},{21,13},{10,2},{14... | collective-permute-start | bytes 1572872 | tf_op jit(solution)/shard_map/ppermute | solution.py:105
  29.8 19.2 %collective-permute-start.22 = (bf16[256,1024]{1,0:T(8,128)(2,1)}, bf16[256,1024]{1,0:T(8,128)(2,1)S(1)}, u32[]{:S(2)}, u32[]{:S(2)}) collective-permute-start(bf16[256,1024]{1,0:T(8,128)(2,1)} %collective-permute-done.21), channel_id=1, source_target_pairs={{8,16},{12,20},{16,24},{20,28},{9,17},{13,21},{17,25},{21,29},{10,... | collective-permute-start | bytes 1572872 | tf_op jit(solution)/shard_map/ppermute | solution.py:105
  36.6 22.4 %collective-permute-start.24 = (bf16[256,1024]{1,0:T(8,128)(2,1)}, bf16[256,1024]{1,0:T(8,128)(2,1)S(1)}, u32[]{:S(2)}, u32[]{:S(2)}) collective-permute-start(bf16[256,1024]{1,0:T(8,128)(2,1)} %collective-permute-done.20), channel_id=1, source_target_pairs={{8,0},{12,4},{16,8},{20,12},{9,1},{13,5},{17,9},{21,13},{10,2},{14... | collective-permute-start | bytes 1572872 | tf_op jit(solution)/shard_map/ppermute | solution.py:105
  37.9 1.2 copy-start
  37.9 1.2 copy-start.1
  38.2 56.8 %collective-permute-start.1 = (f32[512,512]{0,1:T(8,128)S(1)}, f32[512,512]{0,1:T(8,128)S(1)}, u32[]{:S(2)}, u32[]{:S(2)}) collective-permute-start(f32[512,512]{0,1:T(8,128)S(1)} %get-tuple-element.21), channel_id=1, source_target_pairs={{0,4},{4,0},{8,12},{12,8},{16,20},{20,16},{24,28},{28,24},{1,5},{5... | collective-permute-start | bytes 3145736 | tf_op jit(solution)/shard_map/ppermute | solution.py:148
  41.0 19.6 %collective-permute-start.5 = (bf16[256,1024]{1,0:T(8,128)(2,1)S(1)}, bf16[256,1024]{1,0:T(8,128)(2,1)S(1)}, u32[]{:S(2)}, u32[]{:S(2)}) collective-permute-start(bf16[256,1024]{1,0:T(8,128)(2,1)S(1)} %collective-permute-done.4), channel_id=1, source_target_pairs={{16,24},{20,28},{17,25},{21,29},{18,26},{22,30},{19,27},{23,31}} | collective-permute-start | bytes 1572872 | tf_op jit(solution)/shard_map/ppermute | solution.py:105
  47.8 22.5 %collective-permute-start.7 = (bf16[256,1024]{1,0:T(8,128)(2,1)S(1)}, bf16[256,1024]{1,0:T(8,128)(2,1)S(1)}, u32[]{:S(2)}, u32[]{:S(2)}) collective-permute-start(bf16[256,1024]{1,0:T(8,128)(2,1)S(1)} %collective-permute-done.6), channel_id=1, source_target_pairs={{8,0},{12,4},{9,1},{13,5},{10,2},{14,6},{11,3},{15,7}} | collective-permute-start | bytes 1572872 | tf_op jit(solution)/shard_map/ppermute | solution.py:105
  49.1 21.4 %collective-permute-start.23 = (bf16[256,1024]{1,0:T(8,128)(2,1)S(1)}, bf16[256,1024]{1,0:T(8,128)(2,1)S(1)}, u32[]{:S(2)}, u32[]{:S(2)}) collective-permute-start(bf16[256,1024]{1,0:T(8,128)(2,1)S(1)} %collective-permute-done.22), channel_id=1, source_target_pairs={{16,24},{20,28},{17,25},{21,29},{18,26},{22,30},{19,27},{23,31}} | collective-permute-start | bytes 1572872 | tf_op jit(solution)/shard_map/ppermute | solution.py:105
  59.0 20.7 %collective-permute-start.25 = (bf16[256,1024]{1,0:T(8,128)(2,1)S(1)}, bf16[256,1024]{1,0:T(8,128)(2,1)S(1)}, u32[]{:S(2)}, u32[]{:S(2)}) collective-permute-start(bf16[256,1024]{1,0:T(8,128)(2,1)S(1)} %collective-permute-done.24), channel_id=1, source_target_pairs={{8,0},{12,4},{9,1},{13,5},{10,2},{14,6},{11,3},{15,7}} | collective-permute-start | bytes 1572872 | tf_op jit(solution)/shard_map/ppermute | solution.py:105
  86.2 18.0 %collective-permute-start.8 = (bf16[1024,128]{0,1:T(8,128)(2,1)S(1)}, bf16[1024,128]{0,1:T(8,128)(2,1)S(1)}, u32[]{:S(2)}, u32[]{:S(2)}) collective-permute-start(bf16[1024,128]{0,1:T(8,128)(2,1)S(1)} %convolution_convert_fusion.7), channel_id=1, source_target_pairs={{0,1},{1,0},{2,3},{3,2},{4,5},{5,4},{6,7},{7,6},{8,9},{9,8},{10,11... | collective-permute-start | bytes 786440 | tf_op jit(solution)/shard_map/ppermute | solution.py:164
  86.3 22.0 %collective-permute-start.26 = (bf16[1024,128]{0,1:T(8,128)(2,1)S(1)}, bf16[1024,128]{0,1:T(8,128)(2,1)S(1)}, u32[]{:S(2)}, u32[]{:S(2)}) collective-permute-start(bf16[1024,128]{0,1:T(8,128)(2,1)S(1)} %convolution_convert_fusion.3), channel_id=1, source_target_pairs={{0,1},{1,0},{2,3},{3,2},{4,5},{5,4},{6,7},{7,6},{8,9},{9,8},{10,11... | collective-permute-start | bytes 786440 | tf_op jit(solution)/shard_map/ppermute | solution.py:164
  86.8 1.8 %collective-permute-start.9 = (bf16[1024,128]{0,1:T(8,128)(2,1)S(1)}, bf16[1024,128]{0,1:T(8,128)(2,1)S(1)}, u32[]{:S(2)}, u32[]{:S(2)}) collective-permute-start(bf16[1024,128]{0,1:T(8,128)(2,1)S(1)} %convolution_convert_fusion.6), channel_id=1, source_target_pairs={{0,1},{1,0},{2,3},{3,2},{4,5},{5,4},{6,7},{7,6},{8,9},{9,8},{10,11... | collective-permute-start | bytes 786440 | tf_op jit(solution)/shard_map/ppermute | solution.py:164
  86.9 2.7 %collective-permute-start.27 = (bf16[1024,128]{0,1:T(8,128)(2,1)S(1)}, bf16[1024,128]{0,1:T(8,128)(2,1)S(1)}, u32[]{:S(2)}, u32[]{:S(2)}) collective-permute-start(bf16[1024,128]{0,1:T(8,128)(2,1)S(1)} %convolution_convert_fusion.2), channel_id=1, source_target_pairs={{0,1},{1,0},{2,3},{3,2},{4,5},{5,4},{6,7},{7,6},{8,9},{9,8},{10,11... | collective-permute-start | bytes 786440 | tf_op jit(solution)/shard_map/ppermute | solution.py:164
  88.6 6.6 %collective-permute-start.32 = (bf16[1024,128]{0,1:T(8,128)(2,1)S(1)}, bf16[1024,128]{0,1:T(8,128)(2,1)S(1)}, u32[]{:S(2)}, u32[]{:S(2)}) collective-permute-start(bf16[1024,128]{0,1:T(8,128)(2,1)S(1)} %convolution_convert_fusion.1), channel_id=1, source_target_pairs={{0,1},{1,0},{2,3},{3,2},{4,5},{5,4},{6,7},{7,6},{8,9},{9,8},{10,11... | collective-permute-start | bytes 786440 | tf_op jit(solution)/shard_map/ppermute | solution.py:164
  89.6 1.6 collective-permute-start.33
  91.2 1.5 collective-permute-start.15
  92.7 9.1 %collective-permute-start.34 = (bf16[1024,128]{0,1:T(8,128)(2,1)S(1)}, bf16[1024,128]{0,1:T(8,128)(2,1)S(1)}, u32[]{:S(2)}, u32[]{:S(2)}) collective-permute-start(bf16[1024,128]{0,1:T(8,128)(2,1)S(1)} %fusion.9), channel_id=1, source_target_pairs={{0,2},{1,3},{2,0},{3,1},{4,6},{5,7},{6,4},{7,5},{8,10},{9,11},{10,... | collective-permute-start | bytes 786440 | tf_op jit(solution)/shard_map/ppermute | solution.py:168
  95.0 20.4 %collective-permute-start.14 = (bf16[1024,128]{0,1:T(8,128)(2,1)S(1)}, bf16[1024,128]{0,1:T(8,128)(2,1)S(1)}, u32[]{:S(2)}, u32[]{:S(2)}) collective-permute-start(bf16[1024,128]{0,1:T(8,128)(2,1)S(1)} %convolution_convert_fusion.5), channel_id=1, source_target_pairs={{0,1},{1,0},{2,3},{3,2},{4,5},{5,4},{6,7},{7,6},{8,9},{9,8},{10,11... | collective-permute-start | bytes 786440 | tf_op jit(solution)/shard_map/ppermute | solution.py:164
  95.2 12.3 %collective-permute-start.10 = (bf16[1024,128]{0,1:T(8,128)(2,1)S(1)}, bf16[1024,128]{0,1:T(8,128)(2,1)S(1)}, u32[]{:S(2)}, u32[]{:S(2)}) collective-permute-start(bf16[1024,128]{0,1:T(8,128)(2,1)S(1)} %fusion.6), channel_id=1, source_target_pairs={{0,2},{1,3},{2,0},{3,1},{4,6},{5,7},{6,4},{7,5},{8,10},{9,11},{10,... | collective-permute-start | bytes 786440 | tf_op jit(solution)/shard_map/ppermute | solution.py:168
  101.8 11.2 %collective-permute-start.28 = (bf16[1024,128]{0,1:T(8,128)(2,1)S(1)}, bf16[1024,128]{0,1:T(8,128)(2,1)S(1)}, u32[]{:S(2)}, u32[]{:S(2)}) collective-permute-start(bf16[1024,128]{0,1:T(8,128)(2,1)S(1)} %fusion.8), channel_id=1, source_target_pairs={{0,2},{1,3},{2,0},{3,1},{4,6},{5,7},{6,4},{7,5},{8,10},{9,11},{10,... | collective-permute-start | bytes 786440 | tf_op jit(solution)/shard_map/ppermute | solution.py:168
  104.2 14.5 %collective-permute-start.16 = (bf16[1024,128]{0,1:T(8,128)(2,1)S(1)}, bf16[1024,128]{0,1:T(8,128)(2,1)S(1)}, u32[]{:S(2)}, u32[]{:S(2)}) collective-permute-start(bf16[1024,128]{0,1:T(8,128)(2,1)S(1)} %fusion.7), channel_id=1, source_target_pairs={{0,2},{1,3},{2,0},{3,1},{4,6},{5,7},{6,4},{7,5},{8,10},{9,11},{10,... | collective-permute-start | bytes 786440 | tf_op jit(solution)/shard_map/ppermute | solution.py:168
  107.5 39.5 %collective-permute-start.36 = (bf16[1024,128]{0,1:T(8,128)(2,1)S(1)}, bf16[1024,128]{0,1:T(8,128)(2,1)S(1)}, u32[]{:S(2)}, u32[]{:S(2)}) collective-permute-start(bf16[1024,128]{0,1:T(8,128)(2,1)S(1)} %fusion.82), channel_id=1, source_target_pairs={{0,1},{1,0},{2,3},{3,2},{4,5},{5,4},{6,7},{7,6},{8,9},{9,8},{10,11... | collective-permute-start | bytes 786440 | tf_op jit(solution)/shard_map/ppermute | solution.py:177
  108.3 29.9 %collective-permute-start.35 = (bf16[1024,128]{0,1:T(8,128)(2,1)S(1)}, bf16[1024,128]{0,1:T(8,128)(2,1)S(1)}, u32[]{:S(2)}, u32[]{:S(2)}) collective-permute-start(bf16[1024,128]{0,1:T(8,128)(2,1)S(1)} %fusion.82), channel_id=1, source_target_pairs={{0,2},{1,3},{2,0},{3,1},{4,6},{5,7},{6,4},{7,5},{8,10},{9,11},{10,... | collective-permute-start | bytes 786440 | tf_op jit(solution)/shard_map/ppermute | solution.py:176
  113.1 16.9 %collective-permute-start.11 = (bf16[1024,128]{0,1:T(8,128)(2,1)S(1)}, bf16[1024,128]{0,1:T(8,128)(2,1)S(1)}, u32[]{:S(2)}, u32[]{:S(2)}) collective-permute-start(bf16[1024,128]{0,1:T(8,128)(2,1)S(1)} %fusion.77), channel_id=1, source_target_pairs={{0,2},{1,3},{2,0},{3,1},{4,6},{5,7},{6,4},{7,5},{8,10},{9,11},{10,... | collective-permute-start | bytes 786440 | tf_op jit(solution)/shard_map/ppermute | solution.py:176
  115.4 19.6 %collective-permute-start.12 = (bf16[1024,128]{0,1:T(8,128)(2,1)S(1)}, bf16[1024,128]{0,1:T(8,128)(2,1)S(1)}, u32[]{:S(2)}, u32[]{:S(2)}) collective-permute-start(bf16[1024,128]{0,1:T(8,128)(2,1)S(1)} %fusion.77), channel_id=1, source_target_pairs={{0,1},{1,0},{2,3},{3,2},{4,5},{5,4},{6,7},{7,6},{8,9},{9,8},{10,11... | collective-permute-start | bytes 786440 | tf_op jit(solution)/shard_map/ppermute | solution.py:177
  118.7 16.3 %collective-permute-start.29 = (bf16[1024,128]{0,1:T(8,128)(2,1)S(1)}, bf16[1024,128]{0,1:T(8,128)(2,1)S(1)}, u32[]{:S(2)}, u32[]{:S(2)}) collective-permute-start(bf16[1024,128]{0,1:T(8,128)(2,1)S(1)} %fusion.74), channel_id=1, source_target_pairs={{0,2},{1,3},{2,0},{3,1},{4,6},{5,7},{6,4},{7,5},{8,10},{9,11},{10,... | collective-permute-start | bytes 786440 | tf_op jit(solution)/shard_map/ppermute | solution.py:176
  129.9 6.6 %collective-permute-start.13 = (bf16[1024,128]{0,1:T(8,128)(2,1)S(1)}, bf16[1024,128]{0,1:T(8,128)(2,1)S(1)}, u32[]{:S(2)}, u32[]{:S(2)}) collective-permute-start(bf16[1024,128]{0,1:T(8,128)(2,1)S(1)} %collective-permute-done.11), channel_id=1, source_target_pairs={{0,1},{1,0},{2,3},{3,2},{4,5},{5,4},{6,7},{7,6},{8,9},{9,8},{10,11... | collective-permute-start | bytes 786440 | tf_op jit(solution)/shard_map/ppermute | solution.py:177
  135.0 8.7 %collective-permute-start.30 = (bf16[1024,128]{0,1:T(8,128)(2,1)S(1)}, bf16[1024,128]{0,1:T(8,128)(2,1)S(1)}, u32[]{:S(2)}, u32[]{:S(2)}) collective-permute-start(bf16[1024,128]{0,1:T(8,128)(2,1)S(1)} %fusion.74), channel_id=1, source_target_pairs={{0,1},{1,0},{2,3},{3,2},{4,5},{5,4},{6,7},{7,6},{8,9},{9,8},{10,11... | collective-permute-start | bytes 786440 | tf_op jit(solution)/shard_map/ppermute | solution.py:177
  135.0 8.7 %collective-permute-start.17 = (bf16[1024,128]{0,1:T(8,128)(2,1)S(1)}, bf16[1024,128]{0,1:T(8,128)(2,1)S(1)}, u32[]{:S(2)}, u32[]{:S(2)}) collective-permute-start(bf16[1024,128]{0,1:T(8,128)(2,1)S(1)} %fusion.80), channel_id=1, source_target_pairs={{0,2},{1,3},{2,0},{3,1},{4,6},{5,7},{6,4},{7,5},{8,10},{9,11},{10,... | collective-permute-start | bytes 786440 | tf_op jit(solution)/shard_map/ppermute | solution.py:176
  136.5 7.7 %collective-permute-start.31 = (bf16[1024,128]{0,1:T(8,128)(2,1)S(1)}, bf16[1024,128]{0,1:T(8,128)(2,1)S(1)}, u32[]{:S(2)}, u32[]{:S(2)}) collective-permute-start(bf16[1024,128]{0,1:T(8,128)(2,1)S(1)} %collective-permute-done.29), channel_id=1, source_target_pairs={{0,1},{1,0},{2,3},{3,2},{4,5},{5,4},{6,7},{7,6},{8,9},{9,8},{10,11... | collective-permute-start | bytes 786440 | tf_op jit(solution)/shard_map/ppermute | solution.py:177
  138.3 7.3 %collective-permute-start.18 = (bf16[1024,128]{0,1:T(8,128)(2,1)S(1)}, bf16[1024,128]{0,1:T(8,128)(2,1)S(1)}, u32[]{:S(2)}, u32[]{:S(2)}) collective-permute-start(bf16[1024,128]{0,1:T(8,128)(2,1)S(1)} %fusion.80), channel_id=1, source_target_pairs={{0,1},{1,0},{2,3},{3,2},{4,5},{5,4},{6,7},{7,6},{8,9},{9,8},{10,11... | collective-permute-start | bytes 786440 | tf_op jit(solution)/shard_map/ppermute | solution.py:177
  143.7 3.2 %collective-permute-start.37 = (bf16[1024,128]{0,1:T(8,128)(2,1)S(1)}, bf16[1024,128]{0,1:T(8,128)(2,1)S(1)}, u32[]{:S(2)}, u32[]{:S(2)}) collective-permute-start(bf16[1024,128]{0,1:T(8,128)(2,1)S(1)} %collective-permute-done.35), channel_id=1, source_target_pairs={{0,1},{1,0},{2,3},{3,2},{4,5},{5,4},{6,7},{7,6},{8,9},{9,8},{10,11... | collective-permute-start | bytes 786440 | tf_op jit(solution)/shard_map/ppermute | solution.py:177
  143.7 1.9 %collective-permute-start.19 = (bf16[1024,128]{0,1:T(8,128)(2,1)S(1)}, bf16[1024,128]{0,1:T(8,128)(2,1)S(1)}, u32[]{:S(2)}, u32[]{:S(2)}) collective-permute-start(bf16[1024,128]{0,1:T(8,128)(2,1)S(1)} %collective-permute-done.17), channel_id=1, source_target_pairs={{0,1},{1,0},{2,3},{3,2},{4,5},{5,4},{6,7},{7,6},{8,9},{9,8},{10,11... | collective-permute-start | bytes 786440 | tf_op jit(solution)/shard_map/ppermute | solution.py:177
  149.9 3.7 %collective-permute-start.38 = (f32[1024]{0:T(1024)S(1)}, f32[1024]{0:T(1024)S(1)}, u32[]{:S(2)}, u32[]{:S(2)}) collective-permute-start(f32[1024]{0:T(1024)S(1)} %fusion.1), channel_id=1, source_target_pairs={{0,4},{4,0},{8,12},{12,8},{16,20},{20,16},{24,28},{28,24},{1,5},{5... | collective-permute-start | bytes 12296 | tf_op jit(solution)/shard_map/ppermute | solution.py:85
  153.6 3.6 %collective-permute-start.39 = (f32[1024]{0:T(1024)S(1)}, f32[1024]{0:T(1024)S(1)}, u32[]{:S(2)}, u32[]{:S(2)}) collective-permute-start(f32[1024]{0:T(1024)S(1)} %add.363), channel_id=1, source_target_pairs={{0,8},{4,12},{8,0},{12,4},{16,24},{20,28},{24,16},{28,20},{1,9},{5... | collective-permute-start | bytes 12296 | tf_op jit(solution)/shard_map/ppermute | solution.py:85
  157.2 4.5 %collective-permute-start.40 = (f32[1024]{0:T(1024)S(1)}, f32[1024]{0:T(1024)S(1)}, u32[]{:S(2)}, u32[]{:S(2)}) collective-permute-start(f32[1024]{0:T(1024)S(1)} %add.364), channel_id=1, source_target_pairs={{0,16},{4,20},{8,24},{12,28},{16,0},{20,4},{24,8},{28,12},{1,17},{... | collective-permute-start | bytes 12296 | tf_op jit(solution)/shard_map/ppermute | solution.py:85

commit v29 on v25

--- a/solution.py
+++ b/solution.py
@@ -171,8 +171,8 @@
         got = [(me, piece)]
         for k in range(1, m):
             got.append((2 * ((q - k) % m) + par, lax.ppermute(piece, "vox", chip_perm(k))))
-        mates = lax.ppermute(tuple(w for _, w in got), "vox", pair)
-        got = got + [(blk ^ 1, w) for (blk, _), w in zip(got, mates)]
+        mates = lax.ppermute(jnp.stack([w for _, w in got]), "vox", pair)
+        got = got + [(blk ^ 1, mates[i]) for i, (blk, _) in enumerate(got)]
         back = back + jnp.dot(
             jnp.concatenate([w for _, w in got], axis=1),
             jnp.concatenate([rows(col, blk) for blk, _ in got], axis=0),

time: 163 us -> 162 us (level)
  starting transfers between devices: 38.4 us -> 35.8 us
    ppermute x4, waiting for transfers between devices: 15.1 us -> 17 us  [_fast(): lax.ppermute(halves[k].astype(jnp.bfloat16), 'vox', chip_perm(k))]
    ppermute x4, starting transfers between devices: 6.06 us -> 4.25 us  [_fast(): lax.ppermute(piece, 'vox', chip_perm(k))]
    ppermute x8 -> x4, waiting for transfers between devices: 0.08 us -> 1.74 us  [_fast(): mates = lax.ppermute(jnp.stack([w for _, w in got]), 'vox', pair)]
  transfers between devices with their start and end apart: 41 -> 37, of which waited for: 20 -> 20; matrix products, arithmetic and copies ran while one was open for 16% -> 14% of each run, Pallas kernels for 0% -> 0%
where the time goes in v29:
time: 162 us; the launch traced here: 161 us
  waiting for transfers between devices  94.3 us (58%)
  starting transfers between devices  35.8 us (22%)
  matrix products  20.5 us (13%)
  other arithmetic  5.69 us (4%)
  local copies, waits for them, and re-layouts  4.1 us (3%)
    ppermute x12, waiting for transfers between devices, _zline(): cur = lax.ppermute(cur, 'src', pairs)  47.1 us
    ppermute x12, starting transfers between devices, _zline(): cur = lax.ppermute(cur, 'src', pairs)  20.3 us
    ppermute x4, waiting for transfers between devices, _fast(): lax.ppermute(piece, 'vox', chip_perm(k))  17.4 us
    ppermute x4, waiting for transfers between devices, _fast(): lax.ppermute(halves[k].astype(jnp.bfloat16), 'vox', chip_perm(k))  17 us
    dot_general x16, matrix products, pblock(): lax.dot_general(scaled, rows(col, blk), (((1,), (1,)), ((), ())), preferr...  13.4 us
    ppermute x3, waiting for transfers between devices, _sum_over_src(): v = v + lax.ppermute(v, 'src', [(i, i ^ b) for i in range(n)])  10.7 us
    dot_general x4, matrix products, _fast(): jnp.dot(jnp.concatenate([w for _, w in got], axis=1), jnp.concatenate([ro...  7.09 us
    ppermute x4, starting transfers between devices, _fast(): lax.ppermute(piece, 'vox', chip_perm(k))  4.25 us
  transfers between devices with their start and end apart: 37, of which 20 were waited for; matrix products, arithmetic and copies ran while one was open for 14% of the time, Pallas kernels for 0%

profile of v29, /device:TPU:0, one launch (start us, length us, event | category | flops | bytes accessed | tf_op | source)
XLA Modules:
  0.0 161.3 jit_solution(17795334521598125291)
XLA Ops:
  0.0 3.0 %collective-permute-start = (bf16[512,1024]{1,0:T(8,128)(2,1)}, bf16[512,1024]{1,0:T(8,128)(2,1)}, u32[]{:S(2)}, u32[]{:S(2)}) collective-permute-start(bf16[512,1024]{1,0:T(8,128)(2,1)} %param.4), channel_id=1, source_target_pairs={{0,4},{4,0},{8,12},{12,8},{16,20},{20,16},{24,28},{28,24},{1,5},{5... | collective-permute-start | bytes 3145736 | tf_op jit(solution)/shard_map/ppermute | solution.py:140
  3.0 1.3 fusion.124
  4.2 4.3 %collective-permute-start.3 = (bf16[256,1024]{1,0:T(8,128)(2,1)S(1)}, bf16[256,1024]{1,0:T(8,128)(2,1)}, u32[]{:S(2)}, u32[]{:S(2)}) collective-permute-start(bf16[256,1024]{1,0:T(8,128)(2,1)S(1)} %get-tuple-element.23), channel_id=1, source_target_pairs={{0,8},{4,12},{8,16},{12,20},{16,24},{20,28},{1,9},{5,13},{9,17},{1... | collective-permute-start | bytes 1572872 | tf_op jit(solution)/shard_map/ppermute | solution.py:105
  8.5 1.3 collective-permute-start.2
  9.8 5.4 %collective-permute-start.19 = (bf16[256,1024]{1,0:T(8,128)(2,1)S(1)}, bf16[256,1024]{1,0:T(8,128)(2,1)}, u32[]{:S(2)}, u32[]{:S(2)}) collective-permute-start(bf16[256,1024]{1,0:T(8,128)(2,1)S(1)} %get-tuple-element.24), channel_id=1, source_target_pairs={{0,8},{4,12},{8,16},{12,20},{16,24},{20,28},{1,9},{5,13},{9,17},{1... | collective-permute-start | bytes 1572872 | tf_op jit(solution)/shard_map/ppermute | solution.py:105
  15.2 1.3 collective-permute-start.18
  16.8 1.9 %copy.5 = f32[512,1024]{0,1:T(8,128)S(1)} copy(f32[512,1024]{1,0:T(8,128)} %param.7) | data formatting | bytes 4194304 | tf_op args[3]
  18.8 1.3 collective-permute-done.3
  20.8 4.6 %collective-permute-done.2 = bf16[256,1024]{1,0:T(8,128)(2,1)} collective-permute-done((bf16[256,1024]{1,0:T(8,128)(2,1)S(1)}, bf16[256,1024]{1,0:T(8,128)(2,1)}, u32[]{:S(2)}, u32[]{:S(2)}) %collective-permute-start.2) | collective-permute-done | bytes 524320 | tf_op jit(solution)/shard_map/ppermute | solution.py:105
  25.4 1.3 collective-permute-start.6
  26.7 3.2 %collective-permute-done.19 = bf16[256,1024]{1,0:T(8,128)(2,1)} collective-permute-done((bf16[256,1024]{1,0:T(8,128)(2,1)S(1)}, bf16[256,1024]{1,0:T(8,128)(2,1)}, u32[]{:S(2)}, u32[]{:S(2)}) %collective-permute-start.19) | collective-permute-done | bytes 524320 | tf_op jit(solution)/shard_map/ppermute | solution.py:105
  30.5 6.1 %collective-permute-done.18 = bf16[256,1024]{1,0:T(8,128)(2,1)} collective-permute-done((bf16[256,1024]{1,0:T(8,128)(2,1)S(1)}, bf16[256,1024]{1,0:T(8,128)(2,1)}, u32[]{:S(2)}, u32[]{:S(2)}) %collective-permute-start.18) | collective-permute-done | bytes 524320 | tf_op jit(solution)/shard_map/ppermute | solution.py:105
  36.6 1.3 collective-permute-start.22
  39.1 1.8 %fusion = bf16[1024,1024]{1,0:T(8,128)(2,1)S(1)} fusion(f32[1024]{0:T(1024)S(1)} %copy-done.1, bf16[512,1024]{1,0:T(8,128)(2,1)} %collective-permute-done, bf16[512,1024]{1,0:T(8,128)(2,1)S(1)} %copy-done), kind=kLoop, calls=%fused_computation.2 | loop fusion | flops 6291456 | bytes 4198400 | tf_op jit(solution)/shard_map/convert_element_type | solution.py:143
  41.7 6.1 %collective-permute-done.6 = bf16[256,1024]{1,0:T(8,128)(2,1)S(1)} collective-permute-done((bf16[256,1024]{1,0:T(8,128)(2,1)}, bf16[256,1024]{1,0:T(8,128)(2,1)S(1)}, u32[]{:S(2)}, u32[]{:S(2)}) %collective-permute-start.6) | collective-permute-done | bytes 524320 | tf_op jit(solution)/shard_map/ppermute | solution.py:105
  47.8 1.3 collective-permute-start.7
  49.8 9.2 %collective-permute-done.22 = bf16[256,1024]{1,0:T(8,128)(2,1)S(1)} collective-permute-done((bf16[256,1024]{1,0:T(8,128)(2,1)}, bf16[256,1024]{1,0:T(8,128)(2,1)S(1)}, u32[]{:S(2)}, u32[]{:S(2)}) %collective-permute-start.22) | collective-permute-done | bytes 524320 | tf_op jit(solution)/shard_map/ppermute | solution.py:105
  59.0 1.5 collective-permute-start.23
  60.6 1.1 broadcast_select_fusion.5
  61.7 8.5 %collective-permute-done.7 = bf16[256,1024]{1,0:T(8,128)(2,1)S(1)} collective-permute-done((bf16[256,1024]{1,0:T(8,128)(2,1)S(1)}, bf16[256,1024]{1,0:T(8,128)(2,1)S(1)}, u32[]{:S(2)}, u32[]{:S(2)}) %collective-permute-start.7) | collective-permute-done | bytes 524320 | tf_op jit(solution)/shard_map/ppermute | solution.py:105
  70.5 1.1 broadcast_select_fusion.4
  71.6 8.1 %collective-permute-done.23 = bf16[256,1024]{1,0:T(8,128)(2,1)S(1)} collective-permute-done((bf16[256,1024]{1,0:T(8,128)(2,1)S(1)}, bf16[256,1024]{1,0:T(8,128)(2,1)S(1)}, u32[]{:S(2)}, u32[]{:S(2)}) %collective-permute-start.23) | collective-permute-done | bytes 524320 | tf_op jit(solution)/shard_map/ppermute | solution.py:105
  80.8 0.8 fusion.92
  82.5 0.8 fusion.95
  84.1 0.8 fusion.98
  91.7 1.6 collective-permute-start.31
  94.8 6.1 %collective-permute-done.31 = bf16[1024,128]{0,1:T(8,128)(2,1)S(1)} collective-permute-done((bf16[1024,128]{0,1:T(8,128)(2,1)S(1)}, bf16[1024,128]{0,1:T(8,128)(2,1)S(1)}, u32[]{:S(2)}, u32[]{:S(2)}) %collective-permute-start.31) | collective-permute-done | bytes 262176 | tf_op jit(solution)/shard_map/ppermute | solution.py:165
  100.9 1.5 collective-permute-start.15
  102.4 0.9 fusion.79
  103.9 8.3 %collective-permute-done.15 = bf16[1024,128]{0,1:T(8,128)(2,1)S(1)} collective-permute-done((bf16[1024,128]{0,1:T(8,128)(2,1)S(1)}, bf16[1024,128]{0,1:T(8,128)(2,1)S(1)}, u32[]{:S(2)}, u32[]{:S(2)}) %collective-permute-start.15) | collective-permute-done | bytes 262176 | tf_op jit(solution)/shard_map/ppermute | solution.py:165
  112.2 1.5 collective-permute-start.32
  113.7 0.9 fusion.77
  115.1 2.6 %collective-permute-done.26 = bf16[1024,128]{0,1:T(8,128)(2,1)S(1)} collective-permute-done((bf16[1024,128]{0,1:T(8,128)(2,1)S(1)}, bf16[1024,128]{0,1:T(8,128)(2,1)S(1)}, u32[]{:S(2)}, u32[]{:S(2)}) %collective-permute-start.26) | collective-permute-done | bytes 262176 | tf_op jit(solution)/shard_map/ppermute | solution.py:165
  117.8 0.9 fusion.71
  118.7 1.6 collective-permute-start.27
  120.2 0.9 fusion.74
  121.7 1.7 %collective-permute-done.32 = bf16[1024,128]{0,1:T(8,128)(2,1)S(1)} collective-permute-done((bf16[1024,128]{0,1:T(8,128)(2,1)S(1)}, bf16[1024,128]{0,1:T(8,128)(2,1)S(1)}, u32[]{:S(2)}, u32[]{:S(2)}) %collective-permute-start.32) | collective-permute-done | bytes 262176 | tf_op jit(solution)/shard_map/ppermute | solution.py:173
  123.5 5.5 %collective-permute-done.16 = bf16[1024,128]{0,1:T(8,128)(2,1)S(1)} collective-permute-done((bf16[1024,128]{0,1:T(8,128)(2,1)S(1)}, bf16[1024,128]{0,1:T(8,128)(2,1)S(1)}, u32[]{:S(2)}, u32[]{:S(2)}) %collective-permute-start.16) | collective-permute-done | bytes 262176 | tf_op jit(solution)/shard_map/ppermute | solution.py:173
  129.4 5.3 %collective-permute-done.27 = bf16[1024,128]{0,1:T(8,128)(2,1)S(1)} collective-permute-done((bf16[1024,128]{0,1:T(8,128)(2,1)S(1)}, bf16[1024,128]{0,1:T(8,128)(2,1)S(1)}, u32[]{:S(2)}, u32[]{:S(2)}) %collective-permute-start.27) | collective-permute-done | bytes 262176 | tf_op jit(solution)/shard_map/ppermute | solution.py:173
  134.8 4.9 %collective-permute-done.11 = bf16[1024,128]{0,1:T(8,128)(2,1)S(1)} collective-permute-done((bf16[1024,128]{0,1:T(8,128)(2,1)S(1)}, bf16[1024,128]{0,1:T(8,128)(2,1)S(1)}, u32[]{:S(2)}, u32[]{:S(2)}) %collective-permute-start.11) | collective-permute-done | bytes 262176 | tf_op jit(solution)/shard_map/ppermute | solution.py:173
  140.0 1.7 %collective-permute-done.12 = bf16[2,1024,128]{1,2,0:T(8,128)(2,1)S(1)} collective-permute-done((bf16[2,1024,128]{1,2,0:T(8,128)(2,1)S(1)}, bf16[2,1024,128]{1,2,0:T(8,128)(2,1)S(1)}, u32[]{:S(2)}, u32[]{:S(2)}) %collective-permute-start.12) | collective-permute-done | bytes 524320 | tf_op jit(solution)/shard_map/ppermute | solution.py:174
  141.8 1.5 fusion.10
  143.3 1.3 fusion.40
  144.6 1.3 fusion.25
  145.9 3.0 %fusion.1 = f32[1024]{0:T(1024)S(1)} fusion(f32[1024,1024]{1,0:T(8,128)S(1)} %fusion.40, f32[1024,1024]{1,0:T(8,128)S(1)} %fusion.10, f32[1024,1024]{1,0:T(8,128)S(1)} %fusion.25, bf16[512,1024]{1,0:T(8,128)(2,1)} %collective-permute-done, bf16[512,1024]{1,0:T(8,128)(2,1)S(1)} %copy-done, bf16[1024,128]{0,1:T(8,128)(2,1)S(1)} %get-tuple-element.26, ...), kind=kOutput, calls=%fused_computation.3 | convolution fusion | flops 1091566592 | bytes 16781312 | tf_op jit(solution)/shard_map/dot_general | solution.py:176
  149.4 3.1 %collective-permute-done.34 = f32[1024]{0:T(1024)S(1)} collective-permute-done((f32[1024]{0:T(1024)S(1)}, f32[1024]{0:T(1024)S(1)}, u32[]{:S(2)}, u32[]{:S(2)}) %collective-permute-start.34) | collective-permute-done | bytes 4128 | tf_op jit(solution)/shard_map/ppermute | solution.py:85
  153.1 3.0 %collective-permute-done.35 = f32[1024]{0:T(1024)S(1)} collective-permute-done((f32[1024]{0:T(1024)S(1)}, f32[1024]{0:T(1024)S(1)}, u32[]{:S(2)}, u32[]{:S(2)}) %collective-permute-start.35) | collective-permute-done | bytes 4128 | tf_op jit(solution)/shard_map/ppermute | solution.py:85
  156.2 4.5 %collective-permute-done.36 = f32[1024]{0:T(1024)S(1)} collective-permute-done((f32[1024]{0:T(1024)S(1)}, f32[1024]{0:T(1024)S(1)}, u32[]{:S(2)}, u32[]{:S(2)}) %collective-permute-start.36) | collective-permute-done | bytes 4128 | tf_op jit(solution)/shard_map/ppermute | solution.py:85
  (75 shorter events, 19.6 us)
Async XLA Ops:
  0.0 38.2 %collective-permute-start = (bf16[512,1024]{1,0:T(8,128)(2,1)}, bf16[512,1024]{1,0:T(8,128)(2,1)}, u32[]{:S(2)}, u32[]{:S(2)}) collective-permute-start(bf16[512,1024]{1,0:T(8,128)(2,1)} %param.4), channel_id=1, source_target_pairs={{0,4},{4,0},{8,12},{12,8},{16,20},{20,16},{24,28},{28,24},{1,5},{5... | collective-permute-start | bytes 3145736 | tf_op jit(solution)/shard_map/ppermute | solution.py:140
  4.2 15.8 %collective-permute-start.3 = (bf16[256,1024]{1,0:T(8,128)(2,1)S(1)}, bf16[256,1024]{1,0:T(8,128)(2,1)}, u32[]{:S(2)}, u32[]{:S(2)}) collective-permute-start(bf16[256,1024]{1,0:T(8,128)(2,1)S(1)} %get-tuple-element.23), channel_id=1, source_target_pairs={{0,8},{4,12},{8,16},{12,20},{16,24},{20,28},{1,9},{5,13},{9,17},{1... | collective-permute-start | bytes 1572872 | tf_op jit(solution)/shard_map/ppermute | solution.py:105
  8.5 16.9 %collective-permute-start.2 = (bf16[256,1024]{1,0:T(8,128)(2,1)S(1)}, bf16[256,1024]{1,0:T(8,128)(2,1)}, u32[]{:S(2)}, u32[]{:S(2)}) collective-permute-start(bf16[256,1024]{1,0:T(8,128)(2,1)S(1)} %get-tuple-element.23), channel_id=1, source_target_pairs={{8,0},{12,4},{16,8},{20,12},{24,16},{28,20},{9,1},{13,5},{17,9},{2... | collective-permute-start | bytes 1572872 | tf_op jit(solution)/shard_map/ppermute | solution.py:105
  9.8 20.0 %collective-permute-start.19 = (bf16[256,1024]{1,0:T(8,128)(2,1)S(1)}, bf16[256,1024]{1,0:T(8,128)(2,1)}, u32[]{:S(2)}, u32[]{:S(2)}) collective-permute-start(bf16[256,1024]{1,0:T(8,128)(2,1)S(1)} %get-tuple-element.24), channel_id=1, source_target_pairs={{0,8},{4,12},{8,16},{12,20},{16,24},{20,28},{1,9},{5,13},{9,17},{1... | collective-permute-start | bytes 1572872 | tf_op jit(solution)/shard_map/ppermute | solution.py:105
  15.2 21.4 %collective-permute-start.18 = (bf16[256,1024]{1,0:T(8,128)(2,1)S(1)}, bf16[256,1024]{1,0:T(8,128)(2,1)}, u32[]{:S(2)}, u32[]{:S(2)}) collective-permute-start(bf16[256,1024]{1,0:T(8,128)(2,1)S(1)} %get-tuple-element.24), channel_id=1, source_target_pairs={{8,0},{12,4},{16,8},{20,12},{24,16},{28,20},{9,1},{13,5},{17,9},{2... | collective-permute-start | bytes 1572872 | tf_op jit(solution)/shard_map/ppermute | solution.py:105
  20.1 20.9 %collective-permute-start.4 = (bf16[256,1024]{1,0:T(8,128)(2,1)}, bf16[256,1024]{1,0:T(8,128)(2,1)S(1)}, u32[]{:S(2)}, u32[]{:S(2)}) collective-permute-start(bf16[256,1024]{1,0:T(8,128)(2,1)} %collective-permute-done.3), channel_id=1, source_target_pairs={{8,16},{12,20},{16,24},{20,28},{9,17},{13,21},{17,25},{21,29},{10,... | collective-permute-start | bytes 1572872 | tf_op jit(solution)/shard_map/ppermute | solution.py:105
  25.4 22.4 %collective-permute-start.6 = (bf16[256,1024]{1,0:T(8,128)(2,1)}, bf16[256,1024]{1,0:T(8,128)(2,1)S(1)}, u32[]{:S(2)}, u32[]{:S(2)}) collective-permute-start(bf16[256,1024]{1,0:T(8,128)(2,1)} %collective-permute-done.2), channel_id=1, source_target_pairs={{8,0},{12,4},{16,8},{20,12},{9,1},{13,5},{17,9},{21,13},{10,2},{14... | collective-permute-start | bytes 1572872 | tf_op jit(solution)/shard_map/ppermute | solution.py:105
  29.8 19.2 %collective-permute-start.20 = (bf16[256,1024]{1,0:T(8,128)(2,1)}, bf16[256,1024]{1,0:T(8,128)(2,1)S(1)}, u32[]{:S(2)}, u32[]{:S(2)}) collective-permute-start(bf16[256,1024]{1,0:T(8,128)(2,1)} %collective-permute-done.19), channel_id=1, source_target_pairs={{8,16},{12,20},{16,24},{20,28},{9,17},{13,21},{17,25},{21,29},{10,... | collective-permute-start | bytes 1572872 | tf_op jit(solution)/shard_map/ppermute | solution.py:105
  36.6 22.4 %collective-permute-start.22 = (bf16[256,1024]{1,0:T(8,128)(2,1)}, bf16[256,1024]{1,0:T(8,128)(2,1)S(1)}, u32[]{:S(2)}, u32[]{:S(2)}) collective-permute-start(bf16[256,1024]{1,0:T(8,128)(2,1)} %collective-permute-done.18), channel_id=1, source_target_pairs={{8,0},{12,4},{16,8},{20,12},{9,1},{13,5},{17,9},{21,13},{10,2},{14... | collective-permute-start | bytes 1572872 | tf_op jit(solution)/shard_map/ppermute | solution.py:105
  37.9 1.2 copy-start
  37.9 1.2 copy-start.1
  38.2 55.9 %collective-permute-start.1 = (f32[512,512]{0,1:T(8,128)S(1)}, f32[512,512]{0,1:T(8,128)S(1)}, u32[]{:S(2)}, u32[]{:S(2)}) collective-permute-start(f32[512,512]{0,1:T(8,128)S(1)} %get-tuple-element.21), channel_id=1, source_target_pairs={{0,4},{4,0},{8,12},{12,8},{16,20},{20,16},{24,28},{28,24},{1,5},{5... | collective-permute-start | bytes 3145736 | tf_op jit(solution)/shard_map/ppermute | solution.py:148
  41.0 19.6 %collective-permute-start.5 = (bf16[256,1024]{1,0:T(8,128)(2,1)S(1)}, bf16[256,1024]{1,0:T(8,128)(2,1)S(1)}, u32[]{:S(2)}, u32[]{:S(2)}) collective-permute-start(bf16[256,1024]{1,0:T(8,128)(2,1)S(1)} %collective-permute-done.4), channel_id=1, source_target_pairs={{16,24},{20,28},{17,25},{21,29},{18,26},{22,30},{19,27},{23,31}} | collective-permute-start | bytes 1572872 | tf_op jit(solution)/shard_map/ppermute | solution.py:105
  47.8 22.5 %collective-permute-start.7 = (bf16[256,1024]{1,0:T(8,128)(2,1)S(1)}, bf16[256,1024]{1,0:T(8,128)(2,1)S(1)}, u32[]{:S(2)}, u32[]{:S(2)}) collective-permute-start(bf16[256,1024]{1,0:T(8,128)(2,1)S(1)} %collective-permute-done.6), channel_id=1, source_target_pairs={{8,0},{12,4},{9,1},{13,5},{10,2},{14,6},{11,3},{15,7}} | collective-permute-start | bytes 1572872 | tf_op jit(solution)/shard_map/ppermute | solution.py:105
  49.1 21.4 %collective-permute-start.21 = (bf16[256,1024]{1,0:T(8,128)(2,1)S(1)}, bf16[256,1024]{1,0:T(8,128)(2,1)S(1)}, u32[]{:S(2)}, u32[]{:S(2)}) collective-permute-start(bf16[256,1024]{1,0:T(8,128)(2,1)S(1)} %collective-permute-done.20), channel_id=1, source_target_pairs={{16,24},{20,28},{17,25},{21,29},{18,26},{22,30},{19,27},{23,31}} | collective-permute-start | bytes 1572872 | tf_op jit(solution)/shard_map/ppermute | solution.py:105
  59.0 20.7 %collective-permute-start.23 = (bf16[256,1024]{1,0:T(8,128)(2,1)S(1)}, bf16[256,1024]{1,0:T(8,128)(2,1)S(1)}, u32[]{:S(2)}, u32[]{:S(2)}) collective-permute-start(bf16[256,1024]{1,0:T(8,128)(2,1)S(1)} %collective-permute-done.22), channel_id=1, source_target_pairs={{8,0},{12,4},{9,1},{13,5},{10,2},{14,6},{11,3},{15,7}} | collective-permute-start | bytes 1572872 | tf_op jit(solution)/shard_map/ppermute | solution.py:105
  85.0 3.1 %collective-permute-start.9 = (f32[1024,128]{0,1:T(8,128)S(1)}, f32[1024,128]{0,1:T(8,128)S(1)}, u32[]{:S(2)}, u32[]{:S(2)}) collective-permute-start(f32[1024,128]{0,1:T(8,128)S(1)} %fusion.98), channel_id=1, source_target_pairs={{0,1},{1,0},{2,3},{3,2},{4,5},{5,4},{6,7},{7,6},{8,9},{9,8},{10,11... | collective-permute-start | bytes 1572872 | tf_op jit(solution)/shard_map/ppermute | solution.py:162
  85.9 3.2 %collective-permute-start.25 = (f32[1024,128]{0,1:T(8,128)S(1)}, f32[1024,128]{0,1:T(8,128)S(1)}, u32[]{:S(2)}, u32[]{:S(2)}) collective-permute-start(f32[1024,128]{0,1:T(8,128)S(1)} %fusion.86), channel_id=1, source_target_pairs={{0,1},{1,0},{2,3},{3,2},{4,5},{5,4},{6,7},{7,6},{8,9},{9,8},{10,11... | collective-permute-start | bytes 1572872 | tf_op jit(solution)/shard_map/ppermute | solution.py:162
  87.3 32.9 %collective-permute-start.8 = (f32[1024,128]{0,1:T(8,128)S(1)}, f32[1024,128]{0,1:T(8,128)S(1)}, u32[]{:S(2)}, u32[]{:S(2)}) collective-permute-start(f32[1024,128]{0,1:T(8,128)S(1)} %fusion.101), channel_id=1, source_target_pairs={{0,1},{1,0},{2,3},{3,2},{4,5},{5,4},{6,7},{7,6},{8,9},{9,8},{10,11... | collective-permute-start | bytes 1572872 | tf_op jit(solution)/shard_map/ppermute | solution.py:162
  87.4 15.9 %collective-permute-start.13 = (f32[1024,128]{0,1:T(8,128)S(1)}, f32[1024,128]{0,1:T(8,128)S(1)}, u32[]{:S(2)}, u32[]{:S(2)}) collective-permute-start(f32[1024,128]{0,1:T(8,128)S(1)} %fusion.95), channel_id=1, source_target_pairs={{0,1},{1,0},{2,3},{3,2},{4,5},{5,4},{6,7},{7,6},{8,9},{9,8},{10,11... | collective-permute-start | bytes 1572872 | tf_op jit(solution)/shard_map/ppermute | solution.py:162
  88.1 2.7 %collective-permute-start.30 = (f32[1024,128]{0,1:T(8,128)S(1)}, f32[1024,128]{0,1:T(8,128)S(1)}, u32[]{:S(2)}, u32[]{:S(2)}) collective-permute-start(f32[1024,128]{0,1:T(8,128)S(1)} %fusion.80), channel_id=1, source_target_pairs={{0,1},{1,0},{2,3},{3,2},{4,5},{5,4},{6,7},{7,6},{8,9},{9,8},{10,11... | collective-permute-start | bytes 1572872 | tf_op jit(solution)/shard_map/ppermute | solution.py:162
  89.1 2.7 %collective-permute-start.14 = (f32[1024,128]{0,1:T(8,128)S(1)}, f32[1024,128]{0,1:T(8,128)S(1)}, u32[]{:S(2)}, u32[]{:S(2)}) collective-permute-start(f32[1024,128]{0,1:T(8,128)S(1)} %fusion.92), channel_id=1, source_target_pairs={{0,1},{1,0},{2,3},{3,2},{4,5},{5,4},{6,7},{7,6},{8,9},{9,8},{10,11... | collective-permute-start | bytes 1572872 | tf_op jit(solution)/shard_map/ppermute | solution.py:162
  90.8 3.5 %collective-permute-start.29 = (f32[1024,128]{0,1:T(8,128)S(1)}, f32[1024,128]{0,1:T(8,128)S(1)}, u32[]{:S(2)}, u32[]{:S(2)}) collective-permute-start(f32[1024,128]{0,1:T(8,128)S(1)} %fusion.83), channel_id=1, source_target_pairs={{0,1},{1,0},{2,3},{3,2},{4,5},{5,4},{6,7},{7,6},{8,9},{9,8},{10,11... | collective-permute-start | bytes 1572872 | tf_op jit(solution)/shard_map/ppermute | solution.py:162
  91.7 9.2 %collective-permute-start.31 = (bf16[1024,128]{0,1:T(8,128)(2,1)S(1)}, bf16[1024,128]{0,1:T(8,128)(2,1)S(1)}, u32[]{:S(2)}, u32[]{:S(2)}) collective-permute-start(bf16[1024,128]{0,1:T(8,128)(2,1)S(1)} %fusion.9), channel_id=1, source_target_pairs={{0,2},{1,3},{2,0},{3,1},{4,6},{5,7},{6,4},{7,5},{8,10},{9,11},{10,... | collective-permute-start | bytes 786440 | tf_op jit(solution)/shard_map/ppermute | solution.py:165
  94.1 20.4 %collective-permute-start.24 = (f32[1024,128]{0,1:T(8,128)S(1)}, f32[1024,128]{0,1:T(8,128)S(1)}, u32[]{:S(2)}, u32[]{:S(2)}) collective-permute-start(f32[1024,128]{0,1:T(8,128)S(1)} %fusion.89), channel_id=1, source_target_pairs={{0,1},{1,0},{2,3},{3,2},{4,5},{5,4},{6,7},{7,6},{8,9},{9,8},{10,11... | collective-permute-start | bytes 1572872 | tf_op jit(solution)/shard_map/ppermute | solution.py:162
  94.3 25.9 %collective-permute-start.10 = (bf16[1024,128]{0,1:T(8,128)(2,1)S(1)}, bf16[1024,128]{0,1:T(8,128)(2,1)S(1)}, u32[]{:S(2)}, u32[]{:S(2)}) collective-permute-start(bf16[1024,128]{0,1:T(8,128)(2,1)S(1)} %fusion.6), channel_id=1, source_target_pairs={{0,2},{1,3},{2,0},{3,1},{4,6},{5,7},{6,4},{7,5},{8,10},{9,11},{10,... | collective-permute-start | bytes 786440 | tf_op jit(solution)/shard_map/ppermute | solution.py:165
  100.9 11.2 %collective-permute-start.15 = (bf16[1024,128]{0,1:T(8,128)(2,1)S(1)}, bf16[1024,128]{0,1:T(8,128)(2,1)S(1)}, u32[]{:S(2)}, u32[]{:S(2)}) collective-permute-start(bf16[1024,128]{0,1:T(8,128)(2,1)S(1)} %fusion.7), channel_id=1, source_target_pairs={{0,2},{1,3},{2,0},{3,1},{4,6},{5,7},{6,4},{7,5},{8,10},{9,11},{10,... | collective-permute-start | bytes 786440 | tf_op jit(solution)/shard_map/ppermute | solution.py:165
  103.3 14.5 %collective-permute-start.26 = (bf16[1024,128]{0,1:T(8,128)(2,1)S(1)}, bf16[1024,128]{0,1:T(8,128)(2,1)S(1)}, u32[]{:S(2)}, u32[]{:S(2)}) collective-permute-start(bf16[1024,128]{0,1:T(8,128)(2,1)S(1)} %fusion.8), channel_id=1, source_target_pairs={{0,2},{1,3},{2,0},{3,1},{4,6},{5,7},{6,4},{7,5},{8,10},{9,11},{10,... | collective-permute-start | bytes 786440 | tf_op jit(solution)/shard_map/ppermute | solution.py:165
  112.2 11.2 %collective-permute-start.32 = (bf16[1024,128]{0,1:T(8,128)(2,1)S(1)}, bf16[1024,128]{0,1:T(8,128)(2,1)S(1)}, u32[]{:S(2)}, u32[]{:S(2)}) collective-permute-start(bf16[1024,128]{0,1:T(8,128)(2,1)S(1)} %fusion.79), channel_id=1, source_target_pairs={{0,2},{1,3},{2,0},{3,1},{4,6},{5,7},{6,4},{7,5},{8,10},{9,11},{10,... | collective-permute-start | bytes 786440 | tf_op jit(solution)/shard_map/ppermute | solution.py:173
  114.5 14.5 %collective-permute-start.16 = (bf16[1024,128]{0,1:T(8,128)(2,1)S(1)}, bf16[1024,128]{0,1:T(8,128)(2,1)S(1)}, u32[]{:S(2)}, u32[]{:S(2)}) collective-permute-start(bf16[1024,128]{0,1:T(8,128)(2,1)S(1)} %fusion.77), channel_id=1, source_target_pairs={{0,2},{1,3},{2,0},{3,1},{4,6},{5,7},{6,4},{7,5},{8,10},{9,11},{10,... | collective-permute-start | bytes 786440 | tf_op jit(solution)/shard_map/ppermute | solution.py:173
  118.7 16.0 %collective-permute-start.27 = (bf16[1024,128]{0,1:T(8,128)(2,1)S(1)}, bf16[1024,128]{0,1:T(8,128)(2,1)S(1)}, u32[]{:S(2)}, u32[]{:S(2)}) collective-permute-start(bf16[1024,128]{0,1:T(8,128)(2,1)S(1)} %fusion.71), channel_id=1, source_target_pairs={{0,2},{1,3},{2,0},{3,1},{4,6},{5,7},{6,4},{7,5},{8,10},{9,11},{10,... | collective-permute-start | bytes 786440 | tf_op jit(solution)/shard_map/ppermute | solution.py:173
  121.1 18.6 %collective-permute-start.11 = (bf16[1024,128]{0,1:T(8,128)(2,1)S(1)}, bf16[1024,128]{0,1:T(8,128)(2,1)S(1)}, u32[]{:S(2)}, u32[]{:S(2)}) collective-permute-start(bf16[1024,128]{0,1:T(8,128)(2,1)S(1)} %fusion.74), channel_id=1, source_target_pairs={{0,2},{1,3},{2,0},{3,1},{4,6},{5,7},{6,4},{7,5},{8,10},{9,11},{10,... | collective-permute-start | bytes 786440 | tf_op jit(solution)/shard_map/ppermute | solution.py:173
  123.5 16.4 %collective-permute-start.33 = (bf16[2,1024,128]{1,2,0:T(8,128)(2,1)S(1)}, bf16[2,1024,128]{1,2,0:T(8,128)(2,1)S(1)}, u32[]{:S(2)}, u32[]{:S(2)}) collective-permute-start(bf16[2,1024,128]{1,2,0:T(8,128)(2,1)S(1)} %pad_maximum_fusion.7), channel_id=1, source_target_pairs={{0,1},{1,0},{2,3},{3,2},{4,5},{5,4},{6,7},{7,6},{8,9},{9,8},{10,11... | collective-permute-start | bytes 1572872 | tf_op jit(solution)/shard_map/ppermute | solution.py:174
  129.1 10.8 %collective-permute-start.17 = (bf16[2,1024,128]{1,2,0:T(8,128)(2,1)S(1)}, bf16[2,1024,128]{1,2,0:T(8,128)(2,1)S(1)}, u32[]{:S(2)}, u32[]{:S(2)}) collective-permute-start(bf16[2,1024,128]{1,2,0:T(8,128)(2,1)S(1)} %pad_maximum_fusion.5), channel_id=1, source_target_pairs={{0,1},{1,0},{2,3},{3,2},{4,5},{5,4},{6,7},{7,6},{8,9},{9,8},{10,11... | collective-permute-start | bytes 1572872 | tf_op jit(solution)/shard_map/ppermute | solution.py:174
  134.7 5.3 %collective-permute-start.28 = (bf16[2,1024,128]{1,2,0:T(8,128)(2,1)S(1)}, bf16[2,1024,128]{1,2,0:T(8,128)(2,1)S(1)}, u32[]{:S(2)}, u32[]{:S(2)}) collective-permute-start(bf16[2,1024,128]{1,2,0:T(8,128)(2,1)S(1)} %pad_maximum_fusion.6), channel_id=1, source_target_pairs={{0,1},{1,0},{2,3},{3,2},{4,5},{5,4},{6,7},{7,6},{8,9},{9,8},{10,11... | collective-permute-start | bytes 1572872 | tf_op jit(solution)/shard_map/ppermute | solution.py:174
  139.8 2.0 %collective-permute-start.12 = (bf16[2,1024,128]{1,2,0:T(8,128)(2,1)S(1)}, bf16[2,1024,128]{1,2,0:T(8,128)(2,1)S(1)}, u32[]{:S(2)}, u32[]{:S(2)}) collective-permute-start(bf16[2,1024,128]{1,2,0:T(8,128)(2,1)S(1)} %pad_maximum_fusion.4), channel_id=1, source_target_pairs={{0,1},{1,0},{2,3},{3,2},{4,5},{5,4},{6,7},{7,6},{8,9},{9,8},{10,11... | collective-permute-start | bytes 1572872 | tf_op jit(solution)/shard_map/ppermute | solution.py:174
  148.9 3.7 %collective-permute-start.34 = (f32[1024]{0:T(1024)S(1)}, f32[1024]{0:T(1024)S(1)}, u32[]{:S(2)}, u32[]{:S(2)}) collective-permute-start(f32[1024]{0:T(1024)S(1)} %fusion.1), channel_id=1, source_target_pairs={{0,4},{4,0},{8,12},{12,8},{16,20},{20,16},{24,28},{28,24},{1,5},{5... | collective-permute-start | bytes 12296 | tf_op jit(solution)/shard_map/ppermute | solution.py:85
  152.6 3.6 %collective-permute-start.35 = (f32[1024]{0:T(1024)S(1)}, f32[1024]{0:T(1024)S(1)}, u32[]{:S(2)}, u32[]{:S(2)}) collective-permute-start(f32[1024]{0:T(1024)S(1)} %add.363), channel_id=1, source_target_pairs={{0,8},{4,12},{8,0},{12,4},{16,24},{20,28},{24,16},{28,20},{1,9},{5... | collective-permute-start | bytes 12296 | tf_op jit(solution)/shard_map/ppermute | solution.py:85
  156.2 4.5 %collective-permute-start.36 = (f32[1024]{0:T(1024)S(1)}, f32[1024]{0:T(1024)S(1)}, u32[]{:S(2)}, u32[]{:S(2)}) collective-permute-start(f32[1024]{0:T(1024)S(1)} %add.364), channel_id=1, source_target_pairs={{0,16},{4,20},{8,24},{12,28},{16,0},{20,4},{24,8},{28,12},{1,17},{... | collective-permute-start | bytes 12296 | tf_op jit(solution)/shard_map/ppermute | solution.py:85
